TPU v7x, 32 devices: a whole 2x2x4 slice. The times are simulated.
32 devices in a mesh: group: 2 (over y), seq: 4 (over z), batch: 2 (over x), chan: 2 (over core).
Axes of the slice: x: 2, y: 2, z: 4, core: 2. Of those that a mesh axis runs over, the one named last changes fastest.
Arguments:
- seq_in: bfloat16 [4, 4096, 768], P(('group', 'batch'), 'seq', 'chan'), parts along dimension 0, may hold values from -6 to 6
- conv_weight: bfloat16 [3, 768, 768], P(None, 'chan'), may hold values from -0.125 to 0.125
- cotangent: bfloat16 [4, 2048, 768], P(('group', 'batch'), 'seq', 'chan'), parts along dimension 0, may hold values from -0.59765625 to 0.59765625
Outputs:
- block_out: bfloat16 [4, 2048, 768], P(('group', 'batch'), 'seq', 'chan'), parts along dimension 0
- input_grad: bfloat16 [4, 4096, 768], P(('group', 'batch'), 'seq', 'chan'), parts along dimension 0
- weight_grad: float32 [6, 768, 768], P('group', 'chan', 'batch'), parts along dimension 0
There are 2 independent parts, one for each index of `group`. A program takes and returns all parts, laid end to end along the dimension named above; an argument that names none is the same for every part. Nothing has to cross between parts.
All inputs are finite; a program needn't handle non-finite values.
Results may differ from a plain program's by a relative error of at most 0.0031.
Values may be sent and summed in bfloat16 or wider, within the bound.
No kernel may reach another device: no remote copies, remote signals or barrier semaphores. Data moves between devices by JAX's collectives and lax.ppermute only.
A program may use at most 64 MiB of HBM per device.

v0:
```python
import jax
import jax.numpy as jnp
from jax import lax
from jax.sharding import PartitionSpec as P


def from_behind(block, axis, distance):
    devices = range(lax.axis_size(axis))
    route = [(i - distance, i) for i in devices if i - distance in devices]
    return lax.ppermute(block, axis, route)


def place_rows(act_rows, cot_rows, arrived, offset):
    row_count = act_rows.shape[0]
    if offset > 0:
        return (
            jnp.concatenate([act_rows[offset:], arrived[0]], 0),
            jnp.concatenate([cot_rows[offset:], arrived[1]], 0),
        )
    return (
        jnp.concatenate([arrived[0], act_rows[: row_count + offset]], 0),
        jnp.concatenate([arrived[1], cot_rows[: row_count + offset]], 0),
    )


def outgoing_rows(act_rows, cot_rows, offset):
    row_count = act_rows.shape[0]
    if offset > 0:
        return (jnp.stack([act_rows[:offset], cot_rows[:offset]]), -1)
    return (jnp.stack([act_rows[row_count + offset :], cot_rows[row_count + offset :]]), 1)


def reach_rows(act_full, cot_full, offset):
    outgoing, direction = outgoing_rows(act_full, cot_full, offset)
    arrived = from_behind(outgoing, "seq", direction)
    return place_rows(act_full, cot_full, arrived, offset)


def shards(seq_in, conv_weight, cotangent):
    local_in = seq_in[0]
    local_cot = cotangent[0]
    pooled_rows = local_in.shape[0] // 2
    half_width = local_in.shape[1]
    full_width = conv_weight.shape[2]
    spread = pooled_rows // 2
    pooled = 0.5 * jnp.sum(local_in.astype(jnp.float32).reshape(pooled_rows, 2, half_width), axis=1)
    activation_block = jax.nn.gelu(pooled).astype(jnp.bfloat16)
    col_start = lax.axis_index("chan") * half_width
    act_full, cot_full, weight_full = (
        lax.all_gather(activation_block, "chan", axis=1, tiled=True),
        lax.all_gather(local_cot, "chan", axis=1, tiled=True),
        lax.all_gather(conv_weight, "chan", axis=1, tiled=True),
    )
    activation_later, cotangent_later = reach_rows(act_full, cot_full, spread)
    activation_earlier, cotangent_earlier = reach_rows(act_full, cot_full, -spread)
    act_taps = jnp.stack([activation_earlier, act_full, activation_later], 1)
    weight_cols = lax.dynamic_slice_in_dim(weight_full, col_start, half_width, 2)
    conv_out = jnp.dot(
        act_taps.reshape(pooled_rows, 3 * full_width),
        weight_cols.reshape(3 * full_width, half_width),
        preferred_element_type=jnp.float32,
    )
    cot_taps = jnp.stack([cotangent_later, cot_full, cotangent_earlier], 1)
    act_own = lax.dynamic_slice_in_dim(act_taps, col_start, half_width, 2)
    block_out = (pooled + conv_out).astype(jnp.bfloat16)
    activ_grad = jnp.einsum(
        "tkc,khc->th", cot_taps, conv_weight, preferred_element_type=jnp.float32
    )
    unused, gelu_back = jax.vjp(jax.nn.gelu, pooled)
    pooled_grad = local_cot.astype(jnp.float32) + gelu_back(activ_grad)[0]
    input_grad = jnp.repeat(0.5 * pooled_grad, 2, axis=0).astype(jnp.bfloat16)
    partial_grad = jnp.einsum("tkh,tc->khc", act_own, cot_full, preferred_element_type=jnp.float32)
    seq_count = lax.axis_size("seq")
    batch_count = lax.axis_size("batch")
    narrow = full_width // (seq_count * batch_count)
    reordered = partial_grad.reshape(3, half_width, batch_count, seq_count, narrow)
    reordered = jnp.transpose(reordered, (0, 1, 3, 2, 4)).reshape(3, half_width, full_width)
    grad_piece = lax.psum_scatter(reordered, ("seq", "batch"), scatter_dimension=2, tiled=True)
    weight_grad = lax.all_gather(grad_piece, "seq", axis=2, tiled=True)
    return (block_out[None], input_grad[None], weight_grad)


def solution(mesh):
    in_specs = (
        P(("group", "batch"), "seq", "chan"),
        P(None, "chan", None),
        P(("group", "batch"), "seq", "chan"),
    )
    out_specs = (
        P(("group", "batch"), "seq", "chan"),
        P(("group", "batch"), "seq", "chan"),
        P("group", "chan", "batch"),
    )
    return jax.shard_map(shards, mesh=mesh, in_specs=in_specs, out_specs=out_specs, check_vma=False)
```

profile of v0, /device:TPU:0, one launch (start us, length us, event | category | flops | bytes accessed | tf_op | source)
XLA Modules:
  0.0 184.6 jit_solution(14534622430438306470)
XLA Ops:
  8.0 0.0 reduce-scatter.2.cloned.1.call-start
  8.0 2.7 %all-gather = bf16[1,512,768]{2,1,0:T(8,128)(2,1)S(1)} all-gather(bf16[1,512,384]{2,1,0:T(8,128)(2,1)} %param.5), channel_id=2, replica_groups=mesh['group'=2,'seq'=4,'batch'=2,'chan'=2] {'chan'}, dimensions={2}, use_global_device_ids=true | all-gather | bytes 1179648 | tf_op jit(solution)/shard_map/all_gather | solution.py:51
  10.7 2.2 %reshape.32 = f32[512,2,384]{2,1,0:T(2,128)S(1)} reshape(bf16[1,1024,384]{2,1,0:T(8,128)(2,1)} %param.3) | data formatting | bytes 2359296 | tf_op jit(solution)/shard_map/convert_element_type | solution.py:46
  12.9 1.9 %reduce_sum.9 = f32[512,384]{1,0:T(8,128)S(1)} reduce(f32[512,2,384]{2,1,0:T(2,128)S(1)} %reshape.32, f32[]{:T(128)} %constant.2.clone.1), dimensions={1}, to_apply=%region_0.0 | reduce | flops 196608 | bytes 2359300 | tf_op jit(solution)/shard_map/reduce_sum | solution.py:46
  14.8 0.0 copy-start
  14.8 0.9 copy-done
  15.7 0.3 multiply_convert_fusion
  16.0 2.4 %all_gather.12 = bf16[512,768]{1,0:T(8,128)(2,1)S(1)} all-gather(bf16[512,384]{1,0:T(8,128)(2,1)S(1)} %multiply_convert_fusion), channel_id=1, replica_groups=mesh['group'=2,'seq'=4,'batch'=2,'chan'=2] {'chan'}, dimensions={1}, use_global_device_ids=true | all-gather | bytes 1179648 | tf_op jit(solution)/shard_map/all_gather | solution.py:50
  18.3 0.9 slice_bitcast_fusion.7
  19.2 0.8 slice_bitcast_fusion.6
  20.0 1.0 pad_maximum_fusion.1
  21.0 5.8 %collective-permute-start = (bf16[2,256,768]{2,1,0:T(8,128)(2,1)}, bf16[2,256,768]{2,1,0:T(8,128)(2,1)}, u32[]{:S(2)}, u32[]{:S(2)}) collective-permute-start(bf16[2,256,768]{2,1,0:T(8,128)(2,1)} %pad_maximum_fusion.1), channel_id=1, source_target_pairs={{0,4},{4,8},{8,12},{1,5},{5,9},{9,13},{2,6},{6,10},{10,14},{3,7},{... | collective-permute-start | bytes 2359304 | tf_op jit(solution)/shard_map/ppermute | solution.py:10
  26.8 0.9 pad_maximum_fusion.2
  27.7 1.3 collective-permute-start.1
  29.0 0.0 copy-start.5
  29.0 14.2 %collective-permute-done = bf16[2,256,768]{2,1,0:T(8,128)(2,1)} collective-permute-done((bf16[2,256,768]{2,1,0:T(8,128)(2,1)}, bf16[2,256,768]{2,1,0:T(8,128)(2,1)}, u32[]{:S(2)}, u32[]{:S(2)}) %collective-permute-start) | collective-permute-done | bytes 786464 | tf_op jit(solution)/shard_map/ppermute | solution.py:10
  43.2 1.9 %slice_bitcast_fusion = (bf16[256,768]{1,0:T(8,128)(2,1)}, bf16[256,768]{1,0:T(8,128)(2,1)S(1)}) fusion(bf16[2,256,768]{2,1,0:T(8,128)(2,1)} %collective-permute-done), kind=kLoop, calls=%fused_computation.35 | loop fusion | bytes 1572864 | tf_op jit(solution)/shard_map/squeeze | solution.py:22
  45.1 0.1 maximum_bitcast_fusion
  45.2 4.0 %collective-permute-done.1 = bf16[2,256,768]{2,1,0:T(8,128)(2,1)} collective-permute-done((bf16[2,256,768]{2,1,0:T(8,128)(2,1)}, bf16[2,256,768]{2,1,0:T(8,128)(2,1)}, u32[]{:S(2)}, u32[]{:S(2)}) %collective-permute-start.1) | collective-permute-done | bytes 786464 | tf_op jit(solution)/shard_map/ppermute | solution.py:10
  49.2 2.0 %slice_bitcast_fusion.1 = (bf16[256,768]{1,0:T(8,128)(2,1)}, bf16[256,768]{1,0:T(8,128)(2,1)S(1)}) fusion(bf16[2,256,768]{2,1,0:T(8,128)(2,1)} %collective-permute-done.1), kind=kLoop, calls=%fused_computation.36 | loop fusion | bytes 1572864 | tf_op jit(solution)/shard_map/squeeze | solution.py:18
  51.2 0.0 copy-done.5
  51.2 0.1 maximum_bitcast_fusion.1
  51.2 0.0 copy-start.2
  51.2 0.3 pad_maximum_fusion
  51.5 0.6 copy-done.2
  52.1 1.3 fusion.23
  53.4 2.1 %copy.10 = f32[3,384,4,2,96]{1,4,3,2,0:T(8,128)} copy(f32[3,384,4,2,96]{1,4,2,3,0:T(8,128)S(1)} %bitcast.53) | data formatting | bytes 7077888 | tf_op jit(solution)/shard_map/transpose | solution.py:77
  55.5 0.0 reduce-scatter.2.cloned.1.call-update
  55.5 0.0 copy-start.1
  55.5 0.0 all-gather.4.cloned.1.call-start
  55.5 0.5 all-gather.4.cloned.1.call-update
  56.1 0.0 all-gather.6.cloned.1.call-start
  56.1 78.3 %reduce-scatter.2.cloned.1.call-done = f32[3,384,96]{1,2,0:T(8,128)} async-done(((f32[3,384,768]{1,2,0:T(8,128)}), f32[3,384,96]{1,2,0:T(8,128)}) %reduce-scatter.2.cloned.1.call-update) | async-done | bytes 442384 | tf_op jit(solution)/shard_map/reduce_scatter | solution.py:78
  134.4 0.0 all-gather.6.cloned.1.call-update
  134.4 0.0 copy-start.4
  134.4 0.0 copy-start.6
  134.5 1.3 maximum_bitcast_fusion.3
  135.8 1.0 maximum_bitcast_fusion.2
  136.8 0.0 copy-done.1
  136.8 0.0 copy-done.4
  136.9 1.8 fusion.33
  138.7 0.0 copy-start.3
  138.7 1.3 broadcast_in_dim.8
  140.0 3.0 %convert_element_type.40 = bf16[1,1024,384]{2,1,0:T(8,128)(2,1)} reshape(bf16[512,2,384]{2,1,0:T(2,128)(2,1)} %broadcast_in_dim.8) | data formatting | bytes 1572864 | tf_op jit(solution)/shard_map/convert_element_type | solution.py:71
  143.0 0.0 copy-done.3
  143.0 3.6 %fusion.20 = bf16[1,512,384]{2,1,0:T(8,128)(2,1)} fusion(bf16[3,768,768]{2,1,0:T(8,128)(2,1)} %all-gather.4.cloned.1.call-done, s32[]{:T(128)S(6)} %select_n.4, f32[512,384]{1,0:T(8,128)S(1)} %copy-done.1, bf16[512,1,768]{2,0,1:T(8,128)(2,1)S(1)} %copy-done.3, bf16[512,1,768]{2,0,1:T(8,128)(2,1)S(1)} %bitcast.55, ...), kind=kOutput, calls=%fused_computation.13 | convolution fusion | flops 908918784 | bytes 5308420 | tf_op jit(solution)/shard_map/dot_general | solution.py:58
  146.6 27.6 %all-gather.6.cloned.1.call-done = f32[3,384,384]{1,2,0:T(8,128)} async-done(((f32[3,384,96]{1,2,0:T(8,128)}), f32[3,384,384]{1,2,0:T(8,128)}) %all-gather.6.cloned.1.call-update) | async-done | bytes 1769488 | tf_op jit(solution)/shard_map/all_gather | solution.py:79
  174.3 2.8 %copy.11 = f32[3,384,384]{2,1,0:T(8,128)} copy(f32[3,384,384]{1,2,0:T(8,128)} %all-gather.6.cloned.1.call-done) | data formatting | bytes 3538944
  (2 shorter events, 0.0 us)
Async XLA Ops:
  8.0 126.4 %reduce-scatter.2.cloned.1.call-start = ((), (), s32[]{:S(2)}) async-start(), calls=%async_computation.2 | async-start | bytes 3981312 | tf_op jit(solution)/shard_map/reduce_scatter | solution.py:78
  14.8 0.9 copy-start
  21.0 22.2 %collective-permute-start = (bf16[2,256,768]{2,1,0:T(8,128)(2,1)}, bf16[2,256,768]{2,1,0:T(8,128)(2,1)}, u32[]{:S(2)}, u32[]{:S(2)}) collective-permute-start(bf16[2,256,768]{2,1,0:T(8,128)(2,1)} %pad_maximum_fusion.1), channel_id=1, source_target_pairs={{0,4},{4,8},{8,12},{1,5},{5,9},{9,13},{2,6},{6,10},{10,14},{3,7},{... | collective-permute-start | bytes 2359304 | tf_op jit(solution)/shard_map/ppermute | solution.py:10
  27.7 21.5 %collective-permute-start.1 = (bf16[2,256,768]{2,1,0:T(8,128)(2,1)}, bf16[2,256,768]{2,1,0:T(8,128)(2,1)}, u32[]{:S(2)}, u32[]{:S(2)}) collective-permute-start(bf16[2,256,768]{2,1,0:T(8,128)(2,1)} %pad_maximum_fusion.2), channel_id=1, source_target_pairs={{4,0},{8,4},{12,8},{5,1},{9,5},{13,9},{6,2},{10,6},{14,10},{7,3},{... | collective-permute-start | bytes 2359304 | tf_op jit(solution)/shard_map/ppermute | solution.py:10
  29.0 22.2 %copy-start.5 = (bf16[256,768]{1,0:T(8,128)(2,1)S(1)}, bf16[256,768]{1,0:T(8,128)(2,1)}, u32[]{:S(2)}) copy-start(bf16[256,768]{1,0:T(8,128)(2,1)} %get-tuple-element.17) | copy-start | bytes 1179652
  51.2 0.9 copy-start.2
  55.5 81.4 %copy-start.1 = (f32[512,384]{1,0:T(8,128)S(1)}, f32[512,384]{1,0:T(8,128)}, u32[]{:S(2)}) copy-start(f32[512,384]{1,0:T(8,128)} %copy-done) | copy-start | bytes 2359300
  55.5 87.5 %all-gather.4.cloned.1.call-start = ((), (), s32[]{:S(2)}) async-start(), calls=%async_computation.1 | async-start | bytes 5308416 | tf_op jit(solution)/shard_map/all_gather | solution.py:52
  56.1 118.2 %all-gather.6.cloned.1.call-start = ((), (), s32[]{:S(2)}) async-start(), calls=%async_computation.3 | async-start | bytes 2211840 | tf_op jit(solution)/shard_map/all_gather | solution.py:79
  134.4 2.4 %copy-start.4 = (bf16[3,384,768]{2,1,0:T(8,128)(2,1)S(1)}, bf16[3,384,768]{2,1,0:T(8,128)(2,1)}, u32[]{:S(2)}) copy-start(bf16[3,384,768]{2,1,0:T(8,128)(2,1)} %param.4) | copy-start | bytes 5308420
  134.4 2.4 %copy-start.6 = (bf16[1,512,384]{2,1,0:T(8,128)(2,1)S(1)}, bf16[1,512,384]{2,1,0:T(8,128)(2,1)}, u32[]{:S(2)}) copy-start(bf16[1,512,384]{2,1,0:T(8,128)(2,1)} %param.5) | copy-start | bytes 1179652
  138.7 4.3 %copy-start.3 = (bf16[512,1,768]{2,0,1:T(8,128)(2,1)S(1)}, bf16[512,1,768]{2,0,1:T(8,128)(2,1)}, u32[]{:S(2)}) copy-start(bf16[512,1,768]{2,0,1:T(8,128)(2,1)} %copy-done.2) | copy-start | bytes 2359300
Sparse Core Ops, SparseCore 0:
  55.6 78.7 reduce-scatter.1
Sparse Core Ops, SparseCore 1:
  57.5 11.9 all-gather.3
  134.5 39.7 all-gather.5
where the time goes:
time: 185 us
  waiting for transfers between devices  125 us (68%)
  local copies, waits for them, and re-layouts  18.5 us (10%)
  between operations  15.6 us (8%)
  starting transfers between devices  7.16 us (4%)
  other arithmetic  6.81 us (4%)
  matrix products  6.72 us (4%)
  blocking collectives  5.07 us (3%)
    reduce_scatter x1, waiting for transfers between devices, shards(): lax.psum_scatter(reordered, ('seq', 'batch'), scatter_dimension=2, tiled=...  78.3 us
    all_gather x1, waiting for transfers between devices, shards(): weight_grad = lax.all_gather(grad_piece, 'seq', axis=2, tiled=True)  27.6 us
    ppermute x2, waiting for transfers between devices, from_behind(): return lax.ppermute(block, axis, route)  18.2 us
    ppermute x2, starting transfers between devices, from_behind(): return lax.ppermute(block, axis, route)  7.03 us
    unnamed x15, local copies, waits for them, and re-layouts  4.36 us
    squeeze x2, local copies, waits for them, and re-layouts, place_rows(): arrived[1]  3.88 us
  transfers between devices with their start and end apart: 5, of which 4 were waited for; matrix products, arithmetic and copies ran while one was open for 8% of the time, Pallas kernels for 0%

commit v1 on v0

v1 whole, which is shorter than its diff:
```python
import jax
import jax.numpy as jnp
from jax import lax
from jax.sharding import PartitionSpec as P


def shift_from(block, axis, distance):
    size = lax.axis_size(axis)
    route = [(i - distance, i) for i in range(size) if 0 <= i - distance < size]
    return lax.ppermute(block, axis, route)


def half_of(array, index, axis):
    parts = 2
    shape = array.shape
    split = shape[:axis] + (parts, shape[axis] // parts) + shape[axis + 1 :]
    return lax.dynamic_index_in_dim(array.reshape(split), index, axis, keepdims=False)


def shards(seq_in, conv_weight, cotangent):
    local_in = seq_in[0]
    local_cot = cotangent[0]
    rows = local_in.shape[0] // 2
    width = local_in.shape[1]
    spread = rows // 2
    pooled = 0.5 * jnp.sum(local_in.astype(jnp.float32).reshape(rows, 2, width), axis=1)
    activation = jax.nn.gelu(pooled).astype(jnp.bfloat16)

    both = jnp.stack([activation, local_cot])
    from_prev = shift_from(both[:, rows - spread :], "seq", 1)
    from_next = shift_from(both[:, :spread], "seq", -1)
    own_ext = jnp.concatenate([from_prev, both, from_next], 1)
    full_ext = lax.all_gather(own_ext, "chan", axis=2, tiled=True)
    act_full, cot_full = full_ext[0], full_ext[1]

    weight_cols = lax.all_to_all(conv_weight, "chan", 2, 1, tiled=True)
    act_taps = jnp.stack([act_full[k * spread : k * spread + rows] for k in range(3)], 1)
    conv_out = jnp.dot(
        act_taps.reshape(rows, -1),
        weight_cols.reshape(-1, weight_cols.shape[2]),
        preferred_element_type=jnp.float32,
    )
    block_out = (pooled + conv_out).astype(jnp.bfloat16)

    cot_taps = jnp.stack([cot_full[(2 - k) * spread : (2 - k) * spread + rows] for k in range(3)], 1)
    activ_grad = jnp.einsum(
        "tko,kio->ti", cot_taps, conv_weight, preferred_element_type=jnp.float32
    )
    unused, gelu_back = jax.vjp(jax.nn.gelu, pooled)
    pooled_grad = local_cot.astype(jnp.float32) + gelu_back(activ_grad)[0]
    input_grad = jnp.repeat(0.5 * pooled_grad, 2, axis=0).astype(jnp.bfloat16)

    own_taps = jnp.stack([own_ext[0, k * spread : k * spread + rows] for k in range(3)], 1)
    cot_mid = cot_full[spread : spread + rows]
    batch_count = lax.axis_size("batch")
    if batch_count == 2:
        b = lax.axis_index("batch")
        send = jnp.einsum(
            "tki,to->kio", own_taps, half_of(cot_mid, 1 - b, 1), preferred_element_type=jnp.float32
        )
        keep = jnp.einsum(
            "tki,to->kio", own_taps, half_of(cot_mid, b, 1), preferred_element_type=jnp.float32
        )
        summed = keep + lax.ppermute(send, "batch", [(0, 1), (1, 0)])
    else:
        partial = jnp.einsum("tki,to->kio", own_taps, cot_mid, preferred_element_type=jnp.float32)
        summed = lax.psum_scatter(partial, "batch", scatter_dimension=2, tiled=True)
    weight_grad = lax.psum(summed, "seq")
    return (block_out[None], input_grad[None], weight_grad)


def solution(mesh):
    in_specs = (
        P(("group", "batch"), "seq", "chan"),
        P(None, "chan", None),
        P(("group", "batch"), "seq", "chan"),
    )
    out_specs = (
        P(("group", "batch"), "seq", "chan"),
        P(("group", "batch"), "seq", "chan"),
        P("group", "chan", "batch"),
    )
    return jax.shard_map(shards, mesh=mesh, in_specs=in_specs, out_specs=out_specs, check_vma=False)
```

time: 185 us -> 180 us (0.973)
  waiting for transfers between devices: 125 us -> 112 us
  matrix products: 6.72 us -> 11.3 us
  local copies, waits for them, and re-layouts: 18.5 us -> 21.9 us
    reduce_scatter x1 -> x0, waiting for transfers between devices: 78.3 us -> none  [shards(): lax.psum_scatter(reordered, ('seq', 'batch'), scatter_dimension=2, tiled=...]
    psum x0 -> x1, waiting for transfers between devices: none -> 50.3 us  [shards(): weight_grad = lax.psum(summed, 'seq')]
    ppermute x2 -> x3, waiting for transfers between devices: 18.2 us -> 50.2 us  [the longest x1 39.1 us: shards(): summed = keep + lax.ppermute(send, 'batch', [(0, 1), (1, 0)])]
    all_gather x2 -> x1, waiting for transfers between devices: 27.6 us -> 11.2 us  [shards(): full_ext = lax.all_gather(own_ext, 'chan', axis=2, tiled=True)]
    all_to_all x0 -> x1, blocking collectives: none -> 5.63 us  [shards(): weight_cols = lax.all_to_all(conv_weight, 'chan', 2, 1, tiled=True)]
    all_gather x2 -> x0, blocking collectives: 5.07 us -> none  [the longest x1 2.7 us: shards(): lax.all_gather(local_cot, 'chan', axis=1, tiled=True)]
    dot_general x3 -> x4, matrix products: 6.72 us -> 11.3 us  [the longest x1 4.4 us: shards(): jnp.dot(act_taps.reshape(rows, -1), weight_cols.reshape(-1, weight_cols.s...]
    squeeze x2 -> x0, local copies, waits for them, and re-layouts: 3.88 us -> none  [place_rows(): arrived[1]]
  transfers between devices with their start and end apart: 5 -> 5, of which waited for: 4 -> 5; matrix products, arithmetic and copies ran while one was open for 8% -> 12% of each run, Pallas kernels for 0% -> 0%
where the time goes in v1:
time: 180 us; the launch traced here: 179 us
  waiting for transfers between devices  112 us (62%)
  local copies, waits for them, and re-layouts  21.9 us (12%)
  between operations  14.2 us (8%)
  matrix products  11.3 us (6%)
  starting transfers between devices  8.15 us (5%)
  other arithmetic  6.57 us (4%)
  blocking collectives  5.63 us (3%)
    psum x1, waiting for transfers between devices, shards(): weight_grad = lax.psum(summed, 'seq')  50.3 us
    ppermute x1, waiting for transfers between devices, shards(): summed = keep + lax.ppermute(send, 'batch', [(0, 1), (1, 0)])  39.1 us
    all_gather x1, waiting for transfers between devices, shards(): full_ext = lax.all_gather(own_ext, 'chan', axis=2, tiled=True)  11.2 us
    ppermute x2, waiting for transfers between devices, shift_from(): return lax.ppermute(block, axis, route)  11.2 us
    unnamed x6, local copies, waits for them, and re-layouts  6.76 us
    ppermute x2, starting transfers between devices, shift_from(): return lax.ppermute(block, axis, route)  6.27 us
    all_to_all x1, blocking collectives, shards(): weight_cols = lax.all_to_all(conv_weight, 'chan', 2, 1, tiled=True)  5.63 us
    slice x1, local copies, waits for them, and re-layouts, shards(): cot_full[(2 - k) * spread:(2 - k) * spread + rows]  4.6 us
  transfers between devices with their start and end apart: 5, of which 5 were waited for; matrix products, arithmetic and copies ran while one was open for 12% of the time, Pallas kernels for 0%

profile of v1, /device:TPU:0, one launch (start us, length us, event | category | flops | bytes accessed | tf_op | source)
XLA Modules:
  0.0 179.5 jit_solution(5351627847527597983)
XLA Ops:
  7.2 0.0 all-gather.2.cloned.1.call-start
  7.2 2.2 %reshape.129 = f32[512,2,384]{2,1,0:T(2,128)S(1)} reshape(bf16[1,1024,384]{2,1,0:T(8,128)(2,1)} %param.3) | data formatting | bytes 2359296 | tf_op jit(solution)/shard_map/convert_element_type | solution.py:26
  9.4 0.0 copy-start
  9.4 1.9 %reduce_sum.9 = f32[512,384]{1,0:T(8,128)S(1)} reduce(f32[512,2,384]{2,1,0:T(2,128)S(1)} %reshape.129, f32[]{:T(128)} %constant.8.clone.1), dimensions={1}, to_apply=%region_0.0 | reduce | flops 196608 | bytes 2359300 | tf_op jit(solution)/shard_map/reduce_sum | solution.py:26
  11.3 0.3 fusion.27
  11.6 0.0 copy-done
  11.6 0.1 fusion.39
  11.7 5.0 %collective-permute-start = (bf16[2,256,384]{2,1,0:T(8,128)(2,1)S(1)}, bf16[2,256,384]{2,1,0:T(8,128)(2,1)S(1)}, u32[]{:S(2)}, u32[]{:S(2)}) collective-permute-start(bf16[2,256,384]{2,1,0:T(8,128)(2,1)S(1)} %get-tuple-element.14), channel_id=1, source_target_pairs={{0,4},{4,8},{8,12},{1,5},{5,9},{9,13},{2,6},{6,10},{10,14},{3,7},{... | collective-permute-start | bytes 1179656 | tf_op jit(solution)/shard_map/ppermute | solution.py:10
  16.7 1.3 collective-permute-start.1
  18.0 7.0 %collective-permute-done = bf16[2,256,384]{2,1,0:T(8,128)(2,1)S(1)} collective-permute-done((bf16[2,256,384]{2,1,0:T(8,128)(2,1)S(1)}, bf16[2,256,384]{2,1,0:T(8,128)(2,1)S(1)}, u32[]{:S(2)}, u32[]{:S(2)}) %collective-permute-start) | collective-permute-done | bytes 393248 | tf_op jit(solution)/shard_map/ppermute | solution.py:10
  25.0 4.1 %collective-permute-done.1 = bf16[2,256,384]{2,1,0:T(8,128)(2,1)S(1)} collective-permute-done((bf16[2,256,384]{2,1,0:T(8,128)(2,1)S(1)}, bf16[2,256,384]{2,1,0:T(8,128)(2,1)S(1)}, u32[]{:S(2)}, u32[]{:S(2)}) %collective-permute-start.1) | collective-permute-done | bytes 393248 | tf_op jit(solution)/shard_map/ppermute | solution.py:10
  29.1 1.3 pad_maximum_fusion.1
  30.4 0.0 all-gather.2.cloned.1.call-update
  30.5 0.0 all-reduce.2.cloned.1.call-start
  30.5 1.0 fusion.35
  31.6 0.1 fusion.41
  31.6 11.2 %all-gather.2.cloned.1.call-done = bf16[2,1024,768]{2,1,0:T(8,128)(2,1)} async-done(((bf16[2,1024,384]{2,1,0:T(8,128)(2,1)}), bf16[2,1024,768]{2,1,0:T(8,128)(2,1)}) %all-gather.2.cloned.1.call-update) | async-done | bytes 3145744 | tf_op jit(solution)/shard_map/all_gather | solution.py:33
  42.8 4.6 %fusion.45 = (bf16[1,512,768]{2,1,0:T(8,128)(2,1)S(1)}, bf16[512,1,768]{2,0,1:T(8,128)(2,1)}, bf16[512,1,768]{2,0,1:T(8,128)(2,1)}, bf16[512,1,768]{2,0,1:T(8,12...) fusion(bf16[2,1024,768]{2,1,0:T(8,128)(2,1)} %all-gather.2.cloned.1.call-done), kind=kLoop, calls=%fused_computation.67 | loop fusion | bytes 10223616 | tf_op jit(solution)/shard_map/slice | solution.py:45
  47.4 0.2 reshape.128
  47.6 0.0 copy-start.1
  47.6 1.6 constant_dynamic-slice_fusion.1
  49.3 0.0 copy-done.1
  49.3 0.8 fusion.38
  50.1 1.8 %collective-permute-start.2 = (f32[3,384,384]{2,1,0:T(8,128)S(1)}, f32[3,384,384]{2,1,0:T(8,128)S(1)}, u32[]{:S(2)}, u32[]{:S(2)}) collective-permute-start(f32[3,384,384]{2,1,0:T(8,128)S(1)} %fusion.38), channel_id=1, source_target_pairs={{0,2},{2,0},{1,3},{3,1},{4,6},{6,4},{5,7},{7,5},{8,10},{10,8},{9,1... | collective-permute-start | bytes 5308424 | tf_op jit(solution)/shard_map/ppermute | solution.py:64
  51.9 39.1 %collective-permute-done.2 = f32[3,384,384]{2,1,0:T(8,128)S(1)} collective-permute-done((f32[3,384,384]{2,1,0:T(8,128)S(1)}, f32[3,384,384]{2,1,0:T(8,128)S(1)}, u32[]{:S(2)}, u32[]{:S(2)}) %collective-permute-start.2) | collective-permute-done | bytes 1769504 | tf_op jit(solution)/shard_map/ppermute | solution.py:64
  91.0 2.0 %convolution_add_fusion = f32[3,384,384]{2,1,0:T(8,128)} fusion(f32[3,384,384]{2,1,0:T(8,128)S(1)} %collective-permute-done.2, bf16[512,1,384]{2,0,1:T(8,128)(2,1)S(1)} %get-tuple-element.13, bf16[512,1,384]{2,0,1:T(8,128)(2,1)S(1)} %copy-done.1, bf16[512,1,384]{2,0,1:T(8,128)(2,1)S(1)} %get-tuple-element.12, bf16[512,1,384]{2,1,0:T(2,128)(2,1)S(1)} %get-tuple-element.10), kind=kOutput, calls=%fused_computation.8 | convolution fusion | flops 454606848 | bytes 5111808 | tf_op jit(solution)/shard_map/tki,to->kio/dot_general | solution.py:61
  93.0 0.0 all-reduce.2.cloned.1.call-update
  93.0 4.0 %copy.21 = bf16[3,384,768]{1,0,2:T(4,128)(2,1)S(1)} copy(bf16[3,384,768]{2,1,0:T(8,128)(2,1)} %param.4) | data formatting | bytes 3538944 | tf_op args[1]
  97.0 5.6 %all_to_all.15 = bf16[3,384,768]{1,0,2:T(4,128)(2,1)S(1)} all-to-all(bf16[3,384,768]{1,0,2:T(4,128)(2,1)S(1)} %copy.21), channel_id=1, replica_groups=mesh['group'=2,'seq'=4,'batch'=2,'chan'=2] {'chan'}, dimensions={2} | all-to-all | bytes 3538944 | tf_op jit(solution)/shard_map/all_to_all | solution.py:36
  102.6 0.2 copy.22
  102.9 2.3 %copy.23 = bf16[3,2,384,384]{3,2,1,0:T(8,128)(2,1)} copy(bf16[3,2,384,384]{2,3,1,0:T(8,128)(2,1)S(1)} %bitcast.46) | data formatting | bytes 3538944 | tf_op jit(solution)/shard_map/all_to_all | solution.py:36
  105.1 4.0 %fusion.19 = bf16[512,384]{1,0:T(8,128)(2,1)S(1)} fusion(bf16[3,384,768]{2,1,0:T(8,128)(2,1)} %param.4, bf16[512,1,768]{2,0,1:T(8,128)(2,1)} %get-tuple-element.5, bf16[512,1,768]{2,0,1:T(8,128)(2,1)} %get-tuple-element.4, bf16[512,1,768]{2,0,1:T(8,128)(2,1)} %get-tuple-element.6, f32[512,384]{1,0:T(8,128)S(1)} %reduce_sum.9, ...), kind=kOutput, calls=%fused_computation.26 | convolution fusion | flops 913047552 | bytes 5701632 | tf_op jit(solution)/shard_map/tko,kio->ti/dot_general | solution.py:46
  109.2 0.4 broadcast_in_dim.8
  109.6 1.2 convert_element_type.60
  110.8 1.9 %pad_maximum_fusion = bf16[512,3,768]{2,0,1:T(8,128)(2,1)S(1)} fusion(bf16[512,1,768]{2,0,1:T(8,128)(2,1)} %get-tuple-element.7, bf16[512,1,768]{2,0,1:T(8,128)(2,1)} %get-tuple-element.8, bf16[512,1,768]{2,0,1:T(8,128)(2,1)} %get-tuple-element.9), kind=kLoop, calls=%fused_computation | loop fusion | flops 2359296 | bytes 4718592 | tf_op jit(solution)/shard_map/stack | solution.py:37
  112.7 2.5 %copy.20 = bf16[512,3,768]{0,2,1:T(8,128)(2,1)} copy(bf16[512,3,768]{2,0,1:T(8,128)(2,1)S(1)} %pad_maximum_fusion) | data formatting | bytes 4718592 | tf_op jit(solution)/shard_map/stack | solution.py:37
  115.2 4.4 %fusion.10 = bf16[1,512,384]{2,1,0:T(8,128)(2,1)} fusion(bf16[512,2304]{0,1:T(8,128)(2,1)} %bitcast.45, bf16[2304,384]{1,0:T(8,128)(2,1)} %bitcast.47, f32[512,384]{1,0:T(8,128)S(1)} %reduce_sum.9), kind=kOutput, calls=%fused_computation.12 | convolution fusion | flops 906559488 | bytes 5308416 | tf_op jit(solution)/shard_map/dot_general | solution.py:38
  119.6 50.3 %all-reduce.2.cloned.1.call-done = f32[3,384,384]{2,1,0:T(8,128)} async-done(((f32[3,384,384]{2,1,0:T(8,128)}), f32[3,384,384]{2,1,0:T(8,128)}) %all-reduce.2.cloned.1.call-update) | async-done | bytes 1769488 | tf_op jit(solution)/shard_map/psum | solution.py:68
  169.8 2.8 %copy.37 = f32[3,384,384]{2,1,0:T(8,128)} copy(f32[3,384,384]{2,1,0:T(8,128)} %all-reduce.2.cloned.1.call-done) | data formatting | bytes 3538944
Async XLA Ops:
  7.2 35.7 %all-gather.2.cloned.1.call-start = ((), (), s32[]{:S(2)}) async-start(), calls=%async_computation.1 | async-start | bytes 4718592 | tf_op jit(solution)/shard_map/all_gather | solution.py:33
  9.4 2.2 %copy-start = (bf16[1,512,384]{2,1,0:T(8,128)(2,1)S(1)}, bf16[1,512,384]{2,1,0:T(8,128)(2,1)}, u32[]{:S(2)}) copy-start(bf16[1,512,384]{2,1,0:T(8,128)(2,1)} %param.5) | copy-start | bytes 1179652
  11.7 13.3 %collective-permute-start = (bf16[2,256,384]{2,1,0:T(8,128)(2,1)S(1)}, bf16[2,256,384]{2,1,0:T(8,128)(2,1)S(1)}, u32[]{:S(2)}, u32[]{:S(2)}) collective-permute-start(bf16[2,256,384]{2,1,0:T(8,128)(2,1)S(1)} %get-tuple-element.14), channel_id=1, source_target_pairs={{0,4},{4,8},{8,12},{1,5},{5,9},{9,13},{2,6},{6,10},{10,14},{3,7},{... | collective-permute-start | bytes 1179656 | tf_op jit(solution)/shard_map/ppermute | solution.py:10
  16.7 12.5 %collective-permute-start.1 = (bf16[2,256,384]{2,1,0:T(8,128)(2,1)S(1)}, bf16[2,256,384]{2,1,0:T(8,128)(2,1)S(1)}, u32[]{:S(2)}, u32[]{:S(2)}) collective-permute-start(bf16[2,256,384]{2,1,0:T(8,128)(2,1)S(1)} %get-tuple-element.15), channel_id=1, source_target_pairs={{4,0},{8,4},{12,8},{5,1},{9,5},{13,9},{6,2},{10,6},{14,10},{7,3},{... | collective-permute-start | bytes 1179656 | tf_op jit(solution)/shard_map/ppermute | solution.py:10
  30.5 139.4 %all-reduce.2.cloned.1.call-start = ((), (), s32[]{:S(2)}) async-start(), calls=%async_computation.2 | async-start | bytes 3538944 | tf_op jit(solution)/shard_map/psum | solution.py:68
  47.6 1.6 copy-start.1
  50.1 40.9 %collective-permute-start.2 = (f32[3,384,384]{2,1,0:T(8,128)S(1)}, f32[3,384,384]{2,1,0:T(8,128)S(1)}, u32[]{:S(2)}, u32[]{:S(2)}) collective-permute-start(f32[3,384,384]{2,1,0:T(8,128)S(1)} %fusion.38), channel_id=1, source_target_pairs={{0,2},{2,0},{1,3},{3,1},{4,6},{6,4},{5,7},{7,5},{8,10},{10,8},{9,1... | collective-permute-start | bytes 5308424 | tf_op jit(solution)/shard_map/ppermute | solution.py:64
Sparse Core Ops, SparseCore 0:
  30.6 12.2 all-gather.1
  93.2 76.6 all-reduce.1

commit v2 on v1

v2 whole, which is shorter than its diff:
```python
import jax
import jax.numpy as jnp
from jax import lax
from jax.sharding import PartitionSpec as P

SWAP = [(0, 1), (1, 0)]


def shift_from(block, axis, distance):
    size = lax.axis_size(axis)
    route = [(i - distance, i) for i in range(size) if 0 <= i - distance < size]
    return lax.ppermute(block, axis, route)


def half_of(array, index, axis):
    shape = array.shape
    split = shape[:axis] + (2, shape[axis] // 2) + shape[axis + 1 :]
    return lax.dynamic_index_in_dim(array.reshape(split), index, axis, keepdims=False)


def tap_stack(ext, rows, spread, order):
    return jnp.stack([ext[k * spread : k * spread + rows] for k in order], 1)


def line_total(pieces):
    inner = lax.axis_index("seq")
    inner = (inner == 1) | (inner == 2)
    totals = []
    for piece in pieces:
        pair = piece + lax.ppermute(piece, "seq", [(0, 1), (3, 2)])
        whole = pair + lax.ppermute(pair, "seq", [(1, 2), (2, 1)])
        sent = lax.ppermute(whole, "seq", [(1, 0), (2, 3)])
        totals.append(jnp.where(inner, whole, sent))
    return totals


def shards(seq_in, conv_weight, cotangent):
    local_in = seq_in[0]
    local_cot = cotangent[0]
    rows = local_in.shape[0] // 2
    width = local_in.shape[1]
    spread = rows // 2
    c = lax.axis_index("chan")
    pooled = 0.5 * jnp.sum(local_in.astype(jnp.float32).reshape(rows, 2, width), axis=1)
    activation = jax.nn.gelu(pooled).astype(jnp.bfloat16)

    both = jnp.stack([activation, local_cot])
    par_mid = lax.ppermute(both, "chan", SWAP)
    from_prev = shift_from(both[:, rows - spread :], "seq", 1)
    from_next = shift_from(both[:, :spread], "seq", -1)
    par_halo = lax.ppermute(jnp.stack([from_prev, from_next]), "chan", SWAP)
    own_ext = jnp.concatenate([from_prev, both, from_next], 1)
    par_ext = jnp.concatenate([par_halo[0], par_mid, par_halo[1]], 1)

    w_own = half_of(conv_weight, c, 2)
    w_other = half_of(conv_weight, 1 - c, 2)
    w_par = lax.ppermute(w_other, "chan", SWAP)

    conv_out = jnp.einsum(
        "tki,kio->to", tap_stack(own_ext[0], rows, spread, (0, 1, 2)), w_own,
        preferred_element_type=jnp.float32,
    ) + jnp.einsum(
        "tki,kio->to", tap_stack(par_ext[0], rows, spread, (0, 1, 2)), w_par,
        preferred_element_type=jnp.float32,
    )
    block_out = (pooled + conv_out).astype(jnp.bfloat16)

    activ_grad = jnp.einsum(
        "tko,kio->ti", tap_stack(own_ext[1], rows, spread, (2, 1, 0)), w_own,
        preferred_element_type=jnp.float32,
    ) + jnp.einsum(
        "tko,kio->ti", tap_stack(par_ext[1], rows, spread, (2, 1, 0)), w_other,
        preferred_element_type=jnp.float32,
    )
    unused, gelu_back = jax.vjp(jax.nn.gelu, pooled)
    pooled_grad = local_cot.astype(jnp.float32) + gelu_back(activ_grad)[0]
    input_grad = jnp.repeat(0.5 * pooled_grad, 2, axis=0).astype(jnp.bfloat16)

    own_taps = tap_stack(own_ext[0], rows, spread, (0, 1, 2))
    par_cot = par_mid[1]
    batch_count = lax.axis_size("batch")
    seq_count = lax.axis_size("seq")
    if batch_count == 2 and seq_count == 4:
        b = lax.axis_index("batch")
        cot_mine = jnp.where(b == c, local_cot, par_cot)
        cot_theirs = jnp.where(b == c, par_cot, local_cot)
        far_mid = lax.ppermute(jnp.stack([activation, cot_theirs]), "batch", SWAP)
        far_halo = lax.ppermute(jnp.stack([from_prev[0], from_next[0]]), "batch", SWAP)
        far_act = jnp.concatenate([far_halo[0], far_mid[0], far_halo[1]], 0)
        far_taps = tap_stack(far_act, rows, spread, (0, 1, 2))
        pieces = []
        for k in (1, 0, 2):
            grad_k = jnp.dot(
                own_taps[:, k].T, cot_mine, preferred_element_type=jnp.float32
            ) + jnp.dot(far_taps[:, k].T, far_mid[1], preferred_element_type=jnp.float32)
            pieces.extend(jnp.split(grad_k, 2, 0))
        totals = line_total(pieces)
        by_k = {k: jnp.concatenate(totals[2 * n : 2 * n + 2], 0) for n, k in enumerate((1, 0, 2))}
        weight_grad = jnp.stack([by_k[0], by_k[1], by_k[2]])
    else:
        lo = jnp.where(c == 0, local_cot, par_cot)
        hi = jnp.where(c == 0, par_cot, local_cot)
        cot_full = jnp.concatenate([lo, hi], 1)
        partial = jnp.einsum("tki,to->kio", own_taps, cot_full, preferred_element_type=jnp.float32)
        summed = lax.psum_scatter(partial, "batch", scatter_dimension=2, tiled=True)
        weight_grad = lax.psum(summed, "seq")
    return (block_out[None], input_grad[None], weight_grad)


def solution(mesh):
    in_specs = (
        P(("group", "batch"), "seq", "chan"),
        P(None, "chan", None),
        P(("group", "batch"), "seq", "chan"),
    )
    out_specs = (
        P(("group", "batch"), "seq", "chan"),
        P(("group", "batch"), "seq", "chan"),
        P("group", "chan", "batch"),
    )
    return jax.shard_map(shards, mesh=mesh, in_specs=in_specs, out_specs=out_specs, check_vma=False)
```

time: 180 us -> 157 us (0.87)
  waiting for transfers between devices: 112 us -> 79.7 us
  starting transfers between devices: 8.15 us -> 39.5 us
  between operations: 14.2 us -> 1.15 us
  local copies, waits for them, and re-layouts: 21.9 us -> 15.9 us
  blocking collectives: 5.63 us -> 0 us
  other arithmetic: 6.57 us -> 11.6 us
  matrix products: 11.3 us -> 8.24 us
    psum x1 -> x0, waiting for transfers between devices: 50.3 us -> none  [shards(): weight_grad = lax.psum(summed, 'seq')]
    ppermute x1 -> x23, starting transfers between devices: 1.8 us -> 33 us  [the longest x6 16.2 us: line_total(): pair = piece + lax.ppermute(piece, 'seq', [(0, 1), (3, 2)])]
    ppermute x1 -> x23, waiting for transfers between devices: 39.1 us -> 68.8 us  [the longest x6 29.7 us: line_total(): sent = lax.ppermute(whole, 'seq', [(1, 0), (2, 3)])]
    all_gather x1 -> x0, waiting for transfers between devices: 11.2 us -> none  [shards(): full_ext = lax.all_gather(own_ext, 'chan', axis=2, tiled=True)]
    all_to_all x1 -> x0, blocking collectives: 5.63 us -> none  [shards(): weight_cols = lax.all_to_all(conv_weight, 'chan', 2, 1, tiled=True)]
    slice x1 -> x2, local copies, waits for them, and re-layouts: 4.6 us -> 0.04 us  [the longest x1 0.02 us: shards(): from_next[0]]
    unnamed x6 -> x17, local copies, waits for them, and re-layouts: 6.76 us -> 2.23 us
    reshape x1, local copies, waits for them, and re-layouts: 0.18 us -> 3.66 us  [half_of(): array.reshape(split)]
  transfers between devices with their start and end apart: 5 -> 25, of which waited for: 5 -> 16; matrix products, arithmetic and copies ran while one was open for 12% -> 17% of each run, Pallas kernels for 0% -> 0%
where the time goes in v2:
time: 157 us; the launch traced here: 156 us
  waiting for transfers between devices  79.7 us (51%)
  starting transfers between devices  39.5 us (25%)
  local copies, waits for them, and re-layouts  15.9 us (10%)
  other arithmetic  11.6 us (7%)
  matrix products  8.24 us (5%)
    ppermute x6, waiting for transfers between devices, line_total(): sent = lax.ppermute(whole, 'seq', [(1, 0), (2, 3)])  29.7 us
    ppermute x6, waiting for transfers between devices, line_total(): pair = piece + lax.ppermute(piece, 'seq', [(0, 1), (3, 2)])  18.8 us
    ppermute x6, starting transfers between devices, line_total(): pair = piece + lax.ppermute(piece, 'seq', [(0, 1), (3, 2)])  16.2 us
    ppermute x1, waiting for transfers between devices, shards(): far_mid = lax.ppermute(jnp.stack([activation, cot_theirs]), 'batch', SWAP)  15 us
    ppermute x2, waiting for transfers between devices, shift_from(): return lax.ppermute(block, axis, route)  11 us
    ppermute x6, starting transfers between devices, line_total(): sent = lax.ppermute(whole, 'seq', [(1, 0), (2, 3)])  7.74 us
    ppermute x2, starting transfers between devices, shift_from(): return lax.ppermute(block, axis, route)  6.45 us
    ppermute x6, starting transfers between devices, line_total(): whole = pair + lax.ppermute(pair, 'seq', [(1, 2), (2, 1)])  6.35 us
  transfers between devices with their start and end apart: 25, of which 16 were waited for; matrix products, arithmetic and copies ran while one was open for 17% of the time, Pallas kernels for 0%

profile of v2, /device:TPU:0, one launch (start us, length us, event | category | flops | bytes accessed | tf_op | source)
XLA Modules:
  0.0 156.1 jit_solution(12806808459786301883)
XLA Ops:
  0.6 2.2 %reshape.122 = f32[512,2,384]{2,1,0:T(2,128)S(1)} reshape(bf16[1,1024,384]{2,1,0:T(8,128)(2,1)} %param.3) | data formatting | bytes 2359296 | tf_op jit(solution)/shard_map/convert_element_type | solution.py:44
  2.8 1.9 %reduce_sum.9 = f32[512,384]{1,0:T(8,128)S(1)} reduce(f32[512,2,384]{2,1,0:T(2,128)S(1)} %reshape.122, f32[]{:T(128)} %constant.11.clone.1), dimensions={1}, to_apply=%region_0.0 | reduce | flops 196608 | bytes 2359300 | tf_op jit(solution)/shard_map/reduce_sum | solution.py:44
  5.8 5.0 %collective-permute-start = (bf16[2,256,384]{2,1,0:T(8,128)(2,1)S(1)}, bf16[2,256,384]{2,1,0:T(8,128)(2,1)S(1)}, u32[]{:S(2)}, u32[]{:S(2)}) collective-permute-start(bf16[2,256,384]{2,1,0:T(8,128)(2,1)S(1)} %get-tuple-element.25), channel_id=1, source_target_pairs={{0,4},{4,8},{8,12},{1,5},{5,9},{9,13},{2,6},{6,10},{10,14},{3,7},{... | collective-permute-start | bytes 1179656 | tf_op jit(solution)/shard_map/ppermute | solution.py:12
  10.8 1.5 collective-permute-start.1
  12.2 6.9 %collective-permute-done = bf16[2,256,384]{2,1,0:T(8,128)(2,1)S(1)} collective-permute-done((bf16[2,256,384]{2,1,0:T(8,128)(2,1)S(1)}, bf16[2,256,384]{2,1,0:T(8,128)(2,1)S(1)}, u32[]{:S(2)}, u32[]{:S(2)}) %collective-permute-start) | collective-permute-done | bytes 393248 | tf_op jit(solution)/shard_map/ppermute | solution.py:12
  19.1 4.1 %collective-permute-done.1 = bf16[2,256,384]{2,1,0:T(8,128)(2,1)S(1)} collective-permute-done((bf16[2,256,384]{2,1,0:T(8,128)(2,1)S(1)}, bf16[2,256,384]{2,1,0:T(8,128)(2,1)S(1)}, u32[]{:S(2)}, u32[]{:S(2)}) %collective-permute-start.1) | collective-permute-done | bytes 393248 | tf_op jit(solution)/shard_map/ppermute | solution.py:12
  23.2 1.0 pad_maximum_fusion.3
  25.7 3.7 %reshape.121 = bf16[3,384,2,384]{3,2,1,0:T(2,128)(2,1)S(1)} reshape(bf16[3,384,768]{2,1,0:T(8,128)(2,1)} %param.4) | data formatting | bytes 3538944 | tf_op jit(solution)/shard_map/reshape | solution.py:18
  29.4 4.9 %constant_dynamic-slice_fusion = (bf16[3,384,1,384]{3,2,1,0:T(2,128)(2,1)S(1)}, bf16[3,384,1,384]{3,2,1,0:T(2,128)(2,1)}) fusion(bf16[3,384,2,384]{3,2,1,0:T(2,128)(2,1)S(1)} %reshape.121, s32[]{:T(128)S(6)} %select_n.54, s32[]{:T(128)S(6)} %select_n.53), kind=kLoop, calls=%fused_computation.124 | loop fusion | bytes 3538952 | tf_op jit(solution)/shard_map/jit(dynamic_index_in_dim)/dynamic_slice | solution.py:18
  35.6 1.6 collective-permute-start.5
  37.2 1.2 slice_bitcast_fusion.4
  38.4 1.7 %broadcast_select_fusion.1 = (bf16[1,512,384]{2,1,0:T(8,128)(2,1)S(1)}, bf16[1,512,384]{2,1,0:T(8,128)(2,1)S(1)}, bf16[512,1,384]{2,0,1:T(8,128)(2,1)S(1)}, bf16...) fusion(bf16[1,512,384]{2,1,0:T(8,128)(2,1)S(1)} %copy-done, ...), kind=kLoop, calls=%fused_computation.113 | loop fusion | flops 3538944 | bytes 5898241 | tf_op jit(solution)/shard_map/jit(_where)/select_n | solution.py:85
  42.5 5.2 %collective-permute-done.5 = bf16[2,256,384]{2,1,0:T(8,128)(2,1)S(1)} collective-permute-done((bf16[2,256,384]{2,1,0:T(8,128)(2,1)S(1)}, bf16[2,256,384]{2,1,0:T(8,128)(2,1)S(1)}, u32[]{:S(2)}, u32[]{:S(2)}) %collective-permute-start.5) | collective-permute-done | bytes 393248 | tf_op jit(solution)/shard_map/ppermute | solution.py:88
  48.5 15.0 %collective-permute-done.6 = bf16[2,512,384]{2,1,0:T(8,128)(2,1)S(1)} collective-permute-done((bf16[2,512,384]{2,1,0:T(8,128)(2,1)S(1)}, bf16[2,512,384]{2,1,0:T(8,128)(2,1)S(1)}, u32[]{:S(2)}, u32[]{:S(2)}) %collective-permute-start.6) | collective-permute-done | bytes 786464 | tf_op jit(solution)/shard_map/ppermute | solution.py:87
  64.5 3.5 %collective-permute-start.10 = (f32[192,384]{1,0:T(8,128)S(1)}, f32[192,384]{1,0:T(8,128)S(1)}, u32[]{:S(2)}, u32[]{:S(2)}) collective-permute-start(f32[192,384]{1,0:T(8,128)S(1)} %get-tuple-element.30), channel_id=1, source_target_pairs={{0,4},{12,8},{1,5},{13,9},{2,6},{14,10},{3,7},{15,11},{16,20},{28,... | collective-permute-start | bytes 884744 | tf_op jit(solution)/shard_map/ppermute | solution.py:30
  67.9 1.3 collective-permute-start.7
  70.3 1.3 collective-permute-start.13
  71.6 1.3 collective-permute-start.16
  73.7 1.6 %collective-permute-done.10 = f32[192,384]{1,0:T(8,128)S(1)} collective-permute-done((f32[192,384]{1,0:T(8,128)S(1)}, f32[192,384]{1,0:T(8,128)S(1)}, u32[]{:S(2)}, u32[]{:S(2)}) %collective-permute-start.10) | collective-permute-done | bytes 294944 | tf_op jit(solution)/shard_map/ppermute | solution.py:30
  75.3 4.4 %collective-permute-start.19 = (f32[192,384]{1,0:T(8,128)S(1)}, f32[192,384]{1,0:T(8,128)S(1)}, u32[]{:S(2)}, u32[]{:S(2)}) collective-permute-start(f32[192,384]{1,0:T(8,128)S(1)} %get-tuple-element.37), channel_id=1, source_target_pairs={{0,4},{12,8},{1,5},{13,9},{2,6},{14,10},{3,7},{15,11},{16,20},{28,... | collective-permute-start | bytes 884744 | tf_op jit(solution)/shard_map/ppermute | solution.py:30
  79.7 1.9 %collective-permute-done.7 = f32[192,384]{1,0:T(8,128)S(1)} collective-permute-done((f32[192,384]{1,0:T(8,128)S(1)}, f32[192,384]{1,0:T(8,128)S(1)}, u32[]{:S(2)}, u32[]{:S(2)}) %collective-permute-start.7) | collective-permute-done | bytes 294944 | tf_op jit(solution)/shard_map/ppermute | solution.py:30
  81.6 4.4 %collective-permute-start.22 = (f32[192,384]{1,0:T(8,128)S(1)}, f32[192,384]{1,0:T(8,128)S(1)}, u32[]{:S(2)}, u32[]{:S(2)}) collective-permute-start(f32[192,384]{1,0:T(8,128)S(1)} %get-tuple-element.38), channel_id=1, source_target_pairs={{0,4},{12,8},{1,5},{13,9},{2,6},{14,10},{3,7},{15,11},{16,20},{28,... | collective-permute-start | bytes 884744 | tf_op jit(solution)/shard_map/ppermute | solution.py:30
  86.1 1.8 %collective-permute-done.13 = f32[192,384]{1,0:T(8,128)S(1)} collective-permute-done((f32[192,384]{1,0:T(8,128)S(1)}, f32[192,384]{1,0:T(8,128)S(1)}, u32[]{:S(2)}, u32[]{:S(2)}) %collective-permute-start.13) | collective-permute-done | bytes 294944 | tf_op jit(solution)/shard_map/ppermute | solution.py:30
  88.6 5.6 %collective-permute-done.16 = f32[192,384]{1,0:T(8,128)S(1)} collective-permute-done((f32[192,384]{1,0:T(8,128)S(1)}, f32[192,384]{1,0:T(8,128)S(1)}, u32[]{:S(2)}, u32[]{:S(2)}) %collective-permute-start.16) | collective-permute-done | bytes 294944 | tf_op jit(solution)/shard_map/ppermute | solution.py:30
  95.0 5.6 %collective-permute-done.19 = f32[192,384]{1,0:T(8,128)S(1)} collective-permute-done((f32[192,384]{1,0:T(8,128)S(1)}, f32[192,384]{1,0:T(8,128)S(1)}, u32[]{:S(2)}, u32[]{:S(2)}) %collective-permute-start.19) | collective-permute-done | bytes 294944 | tf_op jit(solution)/shard_map/ppermute | solution.py:30
  101.5 1.3 fusion.33
  102.8 2.3 %collective-permute-done.22 = f32[192,384]{1,0:T(8,128)S(1)} collective-permute-done((f32[192,384]{1,0:T(8,128)S(1)}, f32[192,384]{1,0:T(8,128)S(1)}, u32[]{:S(2)}, u32[]{:S(2)}) %collective-permute-start.22) | collective-permute-done | bytes 294944 | tf_op jit(solution)/shard_map/ppermute | solution.py:30
  105.1 1.4 collective-permute-start.17
  106.6 1.4 collective-permute-start.20
  108.0 1.4 collective-permute-start.23
  109.4 1.3 collective-permute-start.9
  110.7 1.3 collective-permute-start.12
  112.1 2.8 %fusion.4 = bf16[1,512,384]{2,1,0:T(8,128)(2,1)} fusion(f32[512,384]{1,0:T(8,128)S(1)} %convolution_bitcast_fusion.3, bf16[3,384,384]{2,1,0:T(8,128)(2,1)} %collective-permute-done.4, bf16[512,1,384]{2,0,1:T(8,128)(2,1)S(1)} %get-tuple-element.16, bf16[512,1,384]{2,0,1:T(8,128)(2,1)S(1)} %get-tuple-element.18, ...), kind=kOutput, calls=%fused_computation.12 | convolution fusion | flops 454950912 | bytes 4030464 | tf_op jit(solution)/shard_map/tki,kio->to/dot_general | solution.py:62
  115.2 1.2 convert_element_type.62
  116.5 1.3 collective-permute-start.15
  117.8 1.0 add.129
  118.8 1.3 collective-permute-start.18
  120.1 1.0 add.132
  121.1 1.3 collective-permute-start.21
  122.4 1.0 add.134
  123.4 2.9 %collective-permute-done.9 = f32[192,384]{1,0:T(8,128)S(1)} collective-permute-done((f32[192,384]{1,0:T(8,128)S(1)}, f32[192,384]{1,0:T(8,128)S(1)}, u32[]{:S(2)}, u32[]{:S(2)}) %collective-permute-start.9) | collective-permute-done | bytes 294944 | tf_op jit(solution)/shard_map/ppermute | solution.py:32
  126.3 1.3 collective-permute-start.24
  127.6 5.0 %collective-permute-done.12 = f32[192,384]{1,0:T(8,128)S(1)} collective-permute-done((f32[192,384]{1,0:T(8,128)S(1)}, f32[192,384]{1,0:T(8,128)S(1)}, u32[]{:S(2)}, u32[]{:S(2)}) %collective-permute-start.12) | collective-permute-done | bytes 294944 | tf_op jit(solution)/shard_map/ppermute | solution.py:32
  132.6 6.3 %collective-permute-done.15 = f32[192,384]{1,0:T(8,128)S(1)} collective-permute-done((f32[192,384]{1,0:T(8,128)S(1)}, f32[192,384]{1,0:T(8,128)S(1)}, u32[]{:S(2)}, u32[]{:S(2)}) %collective-permute-start.15) | collective-permute-done | bytes 294944 | tf_op jit(solution)/shard_map/ppermute | solution.py:32
  138.9 6.3 %collective-permute-done.18 = f32[192,384]{1,0:T(8,128)S(1)} collective-permute-done((f32[192,384]{1,0:T(8,128)S(1)}, f32[192,384]{1,0:T(8,128)S(1)}, u32[]{:S(2)}, u32[]{:S(2)}) %collective-permute-start.18) | collective-permute-done | bytes 294944 | tf_op jit(solution)/shard_map/ppermute | solution.py:32
  145.4 6.1 %collective-permute-done.21 = f32[192,384]{1,0:T(8,128)S(1)} collective-permute-done((f32[192,384]{1,0:T(8,128)S(1)}, f32[192,384]{1,0:T(8,128)S(1)}, u32[]{:S(2)}, u32[]{:S(2)}) %collective-permute-start.21) | collective-permute-done | bytes 294944 | tf_op jit(solution)/shard_map/ppermute | solution.py:32
  151.5 3.1 %collective-permute-done.24 = f32[192,384]{1,0:T(8,128)S(1)} collective-permute-done((f32[192,384]{1,0:T(8,128)S(1)}, f32[192,384]{1,0:T(8,128)S(1)}, u32[]{:S(2)}, u32[]{:S(2)}) %collective-permute-start.24) | collective-permute-done | bytes 294944 | tf_op jit(solution)/shard_map/ppermute | solution.py:32
  154.7 1.4 pad_maximum_fusion
  (71 shorter events, 13.1 us)
Async XLA Ops:
  4.7 1.0 copy-start
  5.8 13.3 %collective-permute-start = (bf16[2,256,384]{2,1,0:T(8,128)(2,1)S(1)}, bf16[2,256,384]{2,1,0:T(8,128)(2,1)S(1)}, u32[]{:S(2)}, u32[]{:S(2)}) collective-permute-start(bf16[2,256,384]{2,1,0:T(8,128)(2,1)S(1)} %get-tuple-element.25), channel_id=1, source_target_pairs={{0,4},{4,8},{8,12},{1,5},{5,9},{9,13},{2,6},{6,10},{10,14},{3,7},{... | collective-permute-start | bytes 1179656 | tf_op jit(solution)/shard_map/ppermute | solution.py:12
  10.8 12.5 %collective-permute-start.1 = (bf16[2,256,384]{2,1,0:T(8,128)(2,1)S(1)}, bf16[2,256,384]{2,1,0:T(8,128)(2,1)S(1)}, u32[]{:S(2)}, u32[]{:S(2)}) collective-permute-start(bf16[2,256,384]{2,1,0:T(8,128)(2,1)S(1)} %get-tuple-element.26), channel_id=1, source_target_pairs={{4,0},{8,4},{12,8},{5,1},{9,5},{13,9},{6,2},{10,6},{14,10},{7,3},{... | collective-permute-start | bytes 1179656 | tf_op jit(solution)/shard_map/ppermute | solution.py:12
  19.1 6.1 %copy-start.3 = (bf16[2,256,384]{2,1,0:T(8,128)(2,1)}, bf16[2,256,384]{2,1,0:T(8,128)(2,1)S(1)}, u32[]{:S(2)}) copy-start(bf16[2,256,384]{2,1,0:T(8,128)(2,1)S(1)} %collective-permute-done) | copy-start | bytes 1179652
  23.2 2.0 %copy-start.1 = (bf16[2,256,384]{2,1,0:T(8,128)(2,1)}, bf16[2,256,384]{2,1,0:T(8,128)(2,1)S(1)}, u32[]{:S(2)}) copy-start(bf16[2,256,384]{2,1,0:T(8,128)(2,1)S(1)} %collective-permute-done.1) | copy-start | bytes 1179652
  24.2 12.9 %collective-permute-start.2 = (bf16[2,2,256,384]{3,2,1,0:T(8,128)(2,1)}, bf16[2,2,256,384]{3,2,1,0:T(8,128)(2,1)}, u32[]{:S(2)}, u32[]{:S(2)}) collective-permute-start(bf16[2,2,256,384]{3,2,1,0:T(8,128)(2,1)} %pad_maximum_fusion.3), channel_id=1, source_target_pairs={{0,1},{1,0},{2,3},{3,2},{4,5},{5,4},{6,7},{7,6},{8,9},{9,8},{10,11... | collective-permute-start | bytes 2359304 | tf_op jit(solution)/shard_map/ppermute | solution.py:51
  25.2 13.1 %collective-permute-start.3 = (bf16[2,512,384]{2,1,0:T(8,128)(2,1)}, bf16[2,512,384]{2,1,0:T(8,128)(2,1)}, u32[]{:S(2)}, u32[]{:S(2)}) collective-permute-start(bf16[2,512,384]{2,1,0:T(8,128)(2,1)} %pad_maximum_fusion.2), channel_id=1, source_target_pairs={{0,1},{1,0},{2,3},{3,2},{4,5},{5,4},{6,7},{7,6},{8,9},{9,8},{10,11... | collective-permute-start | bytes 2359304 | tf_op jit(solution)/shard_map/ppermute | solution.py:48
  34.4 1.0 copy-start.4
  34.4 1.1 copy-start.2
  34.4 75.0 %collective-permute-start.4 = (bf16[3,384,384]{2,1,0:T(8,128)(2,1)S(1)}, bf16[3,384,384]{2,1,0:T(8,128)(2,1)}, u32[]{:S(2)}, u32[]{:S(2)}) collective-permute-start(bf16[3,384,384]{2,1,0:T(8,128)(2,1)S(1)} %bitcast.99), channel_id=1, source_target_pairs={{0,1},{1,0},{2,3},{3,2},{4,5},{5,4},{6,7},{7,6},{8,9},{9,8},{10,11... | collective-permute-start | bytes 2654216 | tf_op jit(solution)/shard_map/ppermute | solution.py:57
  35.6 12.1 %collective-permute-start.5 = (bf16[2,256,384]{2,1,0:T(8,128)(2,1)S(1)}, bf16[2,256,384]{2,1,0:T(8,128)(2,1)S(1)}, u32[]{:S(2)}, u32[]{:S(2)}) collective-permute-start(bf16[2,256,384]{2,1,0:T(8,128)(2,1)S(1)} %pad_maximum_fusion.16), channel_id=1, source_target_pairs={{0,2},{2,0},{1,3},{3,1},{4,6},{6,4},{5,7},{7,5},{8,10},{10,8},{9,1... | collective-permute-start | bytes 1179656 | tf_op jit(solution)/shard_map/ppermute | solution.py:88
  40.2 1.5 copy-start.5
  40.2 23.4 %collective-permute-start.6 = (bf16[2,512,384]{2,1,0:T(8,128)(2,1)S(1)}, bf16[2,512,384]{2,1,0:T(8,128)(2,1)S(1)}, u32[]{:S(2)}, u32[]{:S(2)}) collective-permute-start(bf16[2,512,384]{2,1,0:T(8,128)(2,1)S(1)} %pad_maximum_fusion.1), channel_id=1, source_target_pairs={{0,2},{2,0},{1,3},{3,1},{4,6},{6,4},{5,7},{7,5},{8,10},{10,8},{9,1... | collective-permute-start | bytes 2359304 | tf_op jit(solution)/shard_map/ppermute | solution.py:87
  64.5 10.8 %collective-permute-start.10 = (f32[192,384]{1,0:T(8,128)S(1)}, f32[192,384]{1,0:T(8,128)S(1)}, u32[]{:S(2)}, u32[]{:S(2)}) collective-permute-start(f32[192,384]{1,0:T(8,128)S(1)} %get-tuple-element.30), channel_id=1, source_target_pairs={{0,4},{12,8},{1,5},{13,9},{2,6},{14,10},{3,7},{15,11},{16,20},{28,... | collective-permute-start | bytes 884744 | tf_op jit(solution)/shard_map/ppermute | solution.py:30
  67.9 13.7 %collective-permute-start.7 = (f32[192,384]{1,0:T(8,128)S(1)}, f32[192,384]{1,0:T(8,128)S(1)}, u32[]{:S(2)}, u32[]{:S(2)}) collective-permute-start(f32[192,384]{1,0:T(8,128)S(1)} %get-tuple-element.29), channel_id=1, source_target_pairs={{0,4},{12,8},{1,5},{13,9},{2,6},{14,10},{3,7},{15,11},{16,20},{28,... | collective-permute-start | bytes 884744 | tf_op jit(solution)/shard_map/ppermute | solution.py:30
  70.3 17.7 %collective-permute-start.13 = (f32[192,384]{1,0:T(8,128)S(1)}, f32[192,384]{1,0:T(8,128)S(1)}, u32[]{:S(2)}, u32[]{:S(2)}) collective-permute-start(f32[192,384]{1,0:T(8,128)S(1)} %get-tuple-element.33), channel_id=1, source_target_pairs={{0,4},{12,8},{1,5},{13,9},{2,6},{14,10},{3,7},{15,11},{16,20},{28,... | collective-permute-start | bytes 884744 | tf_op jit(solution)/shard_map/ppermute | solution.py:30
  71.6 22.7 %collective-permute-start.16 = (f32[192,384]{1,0:T(8,128)S(1)}, f32[192,384]{1,0:T(8,128)S(1)}, u32[]{:S(2)}, u32[]{:S(2)}) collective-permute-start(f32[192,384]{1,0:T(8,128)S(1)} %get-tuple-element.34), channel_id=1, source_target_pairs={{0,4},{12,8},{1,5},{13,9},{2,6},{14,10},{3,7},{15,11},{16,20},{28,... | collective-permute-start | bytes 884744 | tf_op jit(solution)/shard_map/ppermute | solution.py:30
  75.3 25.3 %collective-permute-start.19 = (f32[192,384]{1,0:T(8,128)S(1)}, f32[192,384]{1,0:T(8,128)S(1)}, u32[]{:S(2)}, u32[]{:S(2)}) collective-permute-start(f32[192,384]{1,0:T(8,128)S(1)} %get-tuple-element.37), channel_id=1, source_target_pairs={{0,4},{12,8},{1,5},{13,9},{2,6},{14,10},{3,7},{15,11},{16,20},{28,... | collective-permute-start | bytes 884744 | tf_op jit(solution)/shard_map/ppermute | solution.py:30
  81.6 23.5 %collective-permute-start.22 = (f32[192,384]{1,0:T(8,128)S(1)}, f32[192,384]{1,0:T(8,128)S(1)}, u32[]{:S(2)}, u32[]{:S(2)}) collective-permute-start(f32[192,384]{1,0:T(8,128)S(1)} %get-tuple-element.38), channel_id=1, source_target_pairs={{0,4},{12,8},{1,5},{13,9},{2,6},{14,10},{3,7},{15,11},{16,20},{28,... | collective-permute-start | bytes 884744 | tf_op jit(solution)/shard_map/ppermute | solution.py:30
  87.9 18.6 %collective-permute-start.8 = (f32[192,384]{1,0:T(8,128)S(1)}, f32[192,384]{1,0:T(8,128)S(1)}, u32[]{:S(2)}, u32[]{:S(2)}) collective-permute-start(f32[192,384]{1,0:T(8,128)S(1)} %get-tuple-element.27), channel_id=1, source_target_pairs={{4,8},{8,4},{5,9},{9,5},{6,10},{10,6},{7,11},{11,7},{20,24},{24,20... | collective-permute-start | bytes 884744 | tf_op jit(solution)/shard_map/ppermute | solution.py:31
  94.3 13.7 %collective-permute-start.11 = (f32[192,384]{1,0:T(8,128)S(1)}, f32[192,384]{1,0:T(8,128)S(1)}, u32[]{:S(2)}, u32[]{:S(2)}) collective-permute-start(f32[192,384]{1,0:T(8,128)S(1)} %get-tuple-element.28), channel_id=1, source_target_pairs={{4,8},{8,4},{5,9},{9,5},{6,10},{10,6},{7,11},{11,7},{20,24},{24,20... | collective-permute-start | bytes 884744 | tf_op jit(solution)/shard_map/ppermute | solution.py:31
  100.6 10.1 %collective-permute-start.14 = (f32[192,384]{1,0:T(8,128)S(1)}, f32[192,384]{1,0:T(8,128)S(1)}, u32[]{:S(2)}, u32[]{:S(2)}) collective-permute-start(f32[192,384]{1,0:T(8,128)S(1)} %get-tuple-element.31), channel_id=1, source_target_pairs={{4,8},{8,4},{5,9},{9,5},{6,10},{10,6},{7,11},{11,7},{20,24},{24,20... | collective-permute-start | bytes 884744 | tf_op jit(solution)/shard_map/ppermute | solution.py:31
  105.1 11.3 %collective-permute-start.17 = (f32[192,384]{1,0:T(8,128)S(1)}, f32[192,384]{1,0:T(8,128)}, u32[]{:S(2)}, u32[]{:S(2)}) collective-permute-start(f32[192,384]{1,0:T(8,128)S(1)} %get-tuple-element.32), channel_id=1, source_target_pairs={{4,8},{8,4},{5,9},{9,5},{6,10},{10,6},{7,11},{11,7},{20,24},{24,20... | collective-permute-start | bytes 884744 | tf_op jit(solution)/shard_map/ppermute | solution.py:31
  106.6 12.2 %collective-permute-start.20 = (f32[192,384]{1,0:T(8,128)S(1)}, f32[192,384]{1,0:T(8,128)}, u32[]{:S(2)}, u32[]{:S(2)}) collective-permute-start(f32[192,384]{1,0:T(8,128)S(1)} %get-tuple-element.35), channel_id=1, source_target_pairs={{4,8},{8,4},{5,9},{9,5},{6,10},{10,6},{7,11},{11,7},{20,24},{24,20... | collective-permute-start | bytes 884744 | tf_op jit(solution)/shard_map/ppermute | solution.py:31
  108.0 13.1 %collective-permute-start.23 = (f32[192,384]{1,0:T(8,128)S(1)}, f32[192,384]{1,0:T(8,128)}, u32[]{:S(2)}, u32[]{:S(2)}) collective-permute-start(f32[192,384]{1,0:T(8,128)S(1)} %get-tuple-element.36), channel_id=1, source_target_pairs={{4,8},{8,4},{5,9},{9,5},{6,10},{10,6},{7,11},{11,7},{20,24},{24,20... | collective-permute-start | bytes 884744 | tf_op jit(solution)/shard_map/ppermute | solution.py:31
  109.4 16.8 %collective-permute-start.9 = (f32[192,384]{1,0:T(8,128)S(1)}, f32[192,384]{1,0:T(8,128)S(1)}, u32[]{:S(2)}, u32[]{:S(2)}) collective-permute-start(f32[192,384]{1,0:T(8,128)S(1)} %add.122), channel_id=1, source_target_pairs={{4,0},{8,12},{5,1},{9,13},{6,2},{10,14},{7,3},{11,15},{20,16},{24,... | collective-permute-start | bytes 884744 | tf_op jit(solution)/shard_map/ppermute | solution.py:32
  110.7 1.3 copy-start.6
  110.7 21.8 %collective-permute-start.12 = (f32[192,384]{1,0:T(8,128)S(1)}, f32[192,384]{1,0:T(8,128)S(1)}, u32[]{:S(2)}, u32[]{:S(2)}) collective-permute-start(f32[192,384]{1,0:T(8,128)S(1)} %add.124), channel_id=1, source_target_pairs={{4,0},{8,12},{5,1},{9,13},{6,2},{10,14},{7,3},{11,15},{20,16},{24,... | collective-permute-start | bytes 884744 | tf_op jit(solution)/shard_map/ppermute | solution.py:32
  114.8 1.6 %copy-start.7 = (f32[192,384]{1,0:T(8,128)S(1)}, f32[192,384]{1,0:T(8,128)}, u32[]{:S(2)}) copy-start(f32[192,384]{1,0:T(8,128)} %copy-done.6) | copy-start | bytes 884740
  116.5 22.5 %collective-permute-start.15 = (f32[192,384]{1,0:T(8,128)S(1)}, f32[192,384]{1,0:T(8,128)S(1)}, u32[]{:S(2)}, u32[]{:S(2)}) collective-permute-start(f32[192,384]{1,0:T(8,128)S(1)} %add.127), channel_id=1, source_target_pairs={{4,0},{8,12},{5,1},{9,13},{6,2},{10,14},{7,3},{11,15},{20,16},{24,... | collective-permute-start | bytes 884744 | tf_op jit(solution)/shard_map/ppermute | solution.py:32
  118.8 26.5 %collective-permute-start.18 = (f32[192,384]{1,0:T(8,128)S(1)}, f32[192,384]{1,0:T(8,128)S(1)}, u32[]{:S(2)}, u32[]{:S(2)}) collective-permute-start(f32[192,384]{1,0:T(8,128)S(1)} %add.129), channel_id=1, source_target_pairs={{4,0},{8,12},{5,1},{9,13},{6,2},{10,14},{7,3},{11,15},{20,16},{24,... | collective-permute-start | bytes 884744 | tf_op jit(solution)/shard_map/ppermute | solution.py:32
  121.1 30.4 %collective-permute-start.21 = (f32[192,384]{1,0:T(8,128)S(1)}, f32[192,384]{1,0:T(8,128)S(1)}, u32[]{:S(2)}, u32[]{:S(2)}) collective-permute-start(f32[192,384]{1,0:T(8,128)S(1)} %add.132), channel_id=1, source_target_pairs={{4,0},{8,12},{5,1},{9,13},{6,2},{10,14},{7,3},{11,15},{20,16},{24,... | collective-permute-start | bytes 884744 | tf_op jit(solution)/shard_map/ppermute | solution.py:32
  126.3 28.4 %collective-permute-start.24 = (f32[192,384]{1,0:T(8,128)S(1)}, f32[192,384]{1,0:T(8,128)S(1)}, u32[]{:S(2)}, u32[]{:S(2)}) collective-permute-start(f32[192,384]{1,0:T(8,128)S(1)} %add.134), channel_id=1, source_target_pairs={{4,0},{8,12},{5,1},{9,13},{6,2},{10,14},{7,3},{11,15},{20,16},{24,... | collective-permute-start | bytes 884744 | tf_op jit(solution)/shard_map/ppermute | solution.py:32

commit v3 on v2

--- a/solution.py
+++ b/solution.py
@@ -13,9 +13,8 @@
 
 
 def half_of(array, index, axis):
-    shape = array.shape
-    split = shape[:axis] + (2, shape[axis] // 2) + shape[axis + 1 :]
-    return lax.dynamic_index_in_dim(array.reshape(split), index, axis, keepdims=False)
+    size = array.shape[axis] // 2
+    return lax.dynamic_slice_in_dim(array, index * size, size, axis)
 
 
 def tap_stack(ext, rows, spread, order):
@@ -23,15 +22,29 @@
 
 
 def line_total(pieces):
-    inner = lax.axis_index("seq")
-    inner = (inner == 1) | (inner == 2)
-    totals = []
-    for piece in pieces:
-        pair = piece + lax.ppermute(piece, "seq", [(0, 1), (3, 2)])
-        whole = pair + lax.ppermute(pair, "seq", [(1, 2), (2, 1)])
-        sent = lax.ppermute(whole, "seq", [(1, 0), (2, 3)])
-        totals.append(jnp.where(inner, whole, sent))
-    return totals
+    position = lax.axis_index("seq")
+    inner = (position == 1) | (position == 2)
+    inward, outward, middle = [(0, 1), (3, 2)], [(1, 0), (2, 3)], [(1, 2), (2, 1)]
+    count = len(pieces)
+    pairs, wholes, totals = {}, {}, {}
+    for step in range(count + 2):
+        going_in = step < count
+        going_out = step >= 2
+        if going_in and going_out:
+            sent = jnp.where(inner, wholes[step - 2], pieces[step])
+            got = lax.ppermute(sent, "seq", inward + outward)
+        elif going_in:
+            got = lax.ppermute(pieces[step], "seq", inward)
+        else:
+            got = lax.ppermute(wholes[step - 2], "seq", outward)
+        if going_in:
+            pairs[step] = pieces[step] + got
+        if going_out:
+            totals[step - 2] = jnp.where(inner, wholes[step - 2], got)
+        if 1 <= step <= count:
+            ready = pairs[step - 1]
+            wholes[step - 1] = ready + lax.ppermute(ready, "seq", middle)
+    return [totals[n] for n in range(count)]
 
 
 def shards(seq_in, conv_weight, cotangent):
@@ -41,7 +54,7 @@
     width = local_in.shape[1]
     spread = rows // 2
     c = lax.axis_index("chan")
-    pooled = 0.5 * jnp.sum(local_in.astype(jnp.float32).reshape(rows, 2, width), axis=1)
+    pooled = 0.5 * (local_in[0::2].astype(jnp.float32) + local_in[1::2].astype(jnp.float32))
     activation = jax.nn.gelu(pooled).astype(jnp.bfloat16)
 
     both = jnp.stack([activation, local_cot])

time: 157 us -> 158 us (level)
  waiting for transfers between devices: 79.7 us -> 64.4 us
  starting transfers between devices: 39.5 us -> 47.5 us
  other arithmetic: 11.6 us -> 16.3 us
  matrix products: 8.24 us -> 12.4 us
    ppermute x18 -> x14, waiting for transfers between devices: 48.5 us -> 33.7 us  [the longest x4 13.9 us: line_total(): got = lax.ppermute(sent, 'seq', inward + outward)]
    ppermute x18 -> x14, starting transfers between devices: 30.3 us -> 38.7 us  [the longest x4 26.3 us: line_total(): got = lax.ppermute(sent, 'seq', inward + outward)]
    slice x0 -> x2, local copies, waits for them, and re-layouts: none -> 8.11 us  [the longest x1 4.07 us: shards(): local_in[0::2].astype(jnp.float32) + local_in[1::2].astype(jnp.float32)]
    ppermute x1, waiting for transfers between devices: 5.18 us -> 0.86 us  [shards(): lax.ppermute(jnp.stack([from_prev[0], from_next[0]]), 'batch', SWAP)]
    dynamic_slice x1, local copies, waits for them, and re-layouts: 4.86 us -> 1 us  [half_of(): return lax.dynamic_slice_in_dim(array, index * size, size, axis)]
    reshape x1 -> x0, local copies, waits for them, and re-layouts: 3.66 us -> none  [half_of(): array.reshape(split)]
    dot_general x3, matrix products: 1.16 us -> 4.27 us  [shards(): jnp.dot(far_taps[:, k].T, far_mid[1], preferred_element_type=jnp.float32)]
    ppermute x1, waiting for transfers between devices: 15 us -> 17.6 us  [shards(): far_mid = lax.ppermute(jnp.stack([activation, cot_theirs]), 'batch', SWAP)]
  transfers between devices with their start and end apart: 25 -> 21, of which waited for: 16 -> 13; matrix products, arithmetic and copies ran while one was open for 17% -> 17% of each run, Pallas kernels for 0% -> 0%
where the time goes in v3:
time: 158 us; the launch traced here: 157 us
  waiting for transfers between devices  64.4 us (41%)
  starting transfers between devices  47.5 us (30%)
  other arithmetic  16.3 us (10%)
  local copies, waits for them, and re-layouts  15.4 us (10%)
  matrix products  12.4 us (8%)
    ppermute x4, starting transfers between devices, line_total(): got = lax.ppermute(sent, 'seq', inward + outward)  26.3 us
    ppermute x1, waiting for transfers between devices, shards(): far_mid = lax.ppermute(jnp.stack([activation, cot_theirs]), 'batch', SWAP)  17.6 us
    ppermute x4, waiting for transfers between devices, line_total(): got = lax.ppermute(sent, 'seq', inward + outward)  13.9 us
    ppermute x2, waiting for transfers between devices, line_total(): got = lax.ppermute(wholes[step - 2], 'seq', outward)  12.3 us
    ppermute x2, waiting for transfers between devices, shift_from(): return lax.ppermute(block, axis, route)  11.2 us
    ppermute x2, waiting for transfers between devices, line_total(): got = lax.ppermute(pieces[step], 'seq', inward)  7.48 us
    ppermute x2, starting transfers between devices, shift_from(): return lax.ppermute(block, axis, route)  6.26 us
    ppermute x6, starting transfers between devices, line_total(): wholes[step - 1] = ready + lax.ppermute(ready, 'seq', middle)  5.03 us
  transfers between devices with their start and end apart: 21, of which 13 were waited for; matrix products, arithmetic and copies ran while one was open for 17% of the time, Pallas kernels for 0%

profile of v3, /device:TPU:0, one launch (start us, length us, event | category | flops | bytes accessed | tf_op | source)
XLA Modules:
  0.0 157.3 jit_solution(4986343757774491483)
XLA Ops:
  0.6 4.0 %slice.128 = bf16[512,384]{1,0:T(8,128)(2,1)S(1)} slice(bf16[1024,384]{1,0:T(8,128)(2,1)} %bitcast.99), slice={[1:1024:2], [0:384:1]} | slice | bytes 786432 | tf_op jit(solution)/shard_map/slice | solution.py:57
  4.7 4.1 %slice.127 = bf16[512,384]{1,0:T(8,128)(2,1)S(1)} slice(bf16[1024,384]{1,0:T(8,128)(2,1)} %bitcast.100), slice={[0:1024:2], [0:384:1]} | slice | bytes 786432 | tf_op jit(solution)/shard_map/slice | solution.py:57
  9.6 5.0 %collective-permute-start = (bf16[2,256,384]{2,1,0:T(8,128)(2,1)S(1)}, bf16[2,256,384]{2,1,0:T(8,128)(2,1)S(1)}, u32[]{:S(2)}, u32[]{:S(2)}) collective-permute-start(bf16[2,256,384]{2,1,0:T(8,128)(2,1)S(1)} %get-tuple-element.31), channel_id=1, source_target_pairs={{0,4},{4,8},{8,12},{1,5},{5,9},{9,13},{2,6},{6,10},{10,14},{3,7},{... | collective-permute-start | bytes 1179656 | tf_op jit(solution)/shard_map/ppermute | solution.py:12
  14.5 1.3 collective-permute-start.1
  15.8 7.0 %collective-permute-done = bf16[2,256,384]{2,1,0:T(8,128)(2,1)S(1)} collective-permute-done((bf16[2,256,384]{2,1,0:T(8,128)(2,1)S(1)}, bf16[2,256,384]{2,1,0:T(8,128)(2,1)S(1)}, u32[]{:S(2)}, u32[]{:S(2)}) %collective-permute-start) | collective-permute-done | bytes 393248 | tf_op jit(solution)/shard_map/ppermute | solution.py:12
  22.9 4.1 %collective-permute-done.1 = bf16[2,256,384]{2,1,0:T(8,128)(2,1)S(1)} collective-permute-done((bf16[2,256,384]{2,1,0:T(8,128)(2,1)S(1)}, bf16[2,256,384]{2,1,0:T(8,128)(2,1)S(1)}, u32[]{:S(2)}, u32[]{:S(2)}) %collective-permute-start.1) | collective-permute-done | bytes 393248 | tf_op jit(solution)/shard_map/ppermute | solution.py:12
  27.0 1.0 pad_maximum_fusion.3
  28.0 1.0 pad_maximum_fusion.2
  29.5 1.1 collective-permute-done.2
  30.6 1.2 slice_bitcast_fusion.4
  31.8 2.9 %broadcast_select_fusion.1 = (bf16[1,512,384]{2,1,0:T(8,128)(2,1)S(1)}, bf16[1,512,384]{2,1,0:T(8,128)(2,1)S(1)}, bf16[512,1,384]{2,0,1:T(8,128)(2,1)}, bf16[512...) fusion(bf16[1,512,384]{2,1,0:T(8,128)(2,1)S(1)} %copy-done.1, ...), kind=kLoop, calls=%fused_computation.92 | loop fusion | flops 3538944 | bytes 5898241 | tf_op jit(solution)/shard_map/jit(_where)/select_n | solution.py:98
  34.7 1.0 pad_maximum_fusion.1
  35.7 1.5 collective-permute-start.6
  37.2 0.9 slice.161
  38.8 17.6 %collective-permute-done.6 = bf16[2,512,384]{2,1,0:T(8,128)(2,1)} collective-permute-done((bf16[2,512,384]{2,1,0:T(8,128)(2,1)}, bf16[2,512,384]{2,1,0:T(8,128)(2,1)}, u32[]{:S(2)}, u32[]{:S(2)}) %collective-permute-start.6) | collective-permute-done | bytes 786464 | tf_op jit(solution)/shard_map/ppermute | solution.py:100
  56.4 1.5 fusion.53
  58.4 3.5 %collective-permute-start.7 = (f32[192,384]{1,0:T(8,128)S(1)}, f32[192,384]{1,0:T(8,128)S(1)}, u32[]{:S(2)}, u32[]{:S(2)}) collective-permute-start(f32[192,384]{1,0:T(8,128)S(1)} %get-tuple-element.43), channel_id=1, source_target_pairs={{0,4},{12,8},{1,5},{13,9},{2,6},{14,10},{3,7},{15,11},{16,20},{28,... | collective-permute-start | bytes 884744 | tf_op jit(solution)/shard_map/ppermute | solution.py:37
  61.9 1.3 collective-permute-start.12
  63.2 0.9 collective-permute-done.5
  64.8 1.0 slice_bitcast_fusion.1
  65.8 3.4 %collective-permute-done.7 = f32[192,384]{1,0:T(8,128)S(1)} collective-permute-done((f32[192,384]{1,0:T(8,128)S(1)}, f32[192,384]{1,0:T(8,128)S(1)}, u32[]{:S(2)}, u32[]{:S(2)}) %collective-permute-start.7) | collective-permute-done | bytes 294944 | tf_op jit(solution)/shard_map/ppermute | solution.py:37
  69.2 4.1 %collective-permute-done.12 = f32[192,384]{1,0:T(8,128)S(1)} collective-permute-done((f32[192,384]{1,0:T(8,128)S(1)}, f32[192,384]{1,0:T(8,128)S(1)}, u32[]{:S(2)}, u32[]{:S(2)}) %collective-permute-start.12) | collective-permute-done | bytes 294944 | tf_op jit(solution)/shard_map/ppermute | solution.py:37
  73.4 0.8 collective-permute-start.8
  74.9 1.4 fusion.42
  76.7 1.1 slice_select_fusion.3
  77.8 14.3 %collective-permute-start.9 = (f32[192,384]{1,0:T(8,128)}, f32[192,384]{1,0:T(8,128)}, u32[]{:S(2)}, u32[]{:S(2)}) collective-permute-start(f32[192,384]{1,0:T(8,128)} %get-tuple-element.5), channel_id=1, source_target_pairs={{0,4},{12,8},{4,0},{8,12},{1,5},{13,9},{5,1},{9,13},{2,6},{14,10},... | collective-permute-start | bytes 884744 | tf_op jit(solution)/shard_map/ppermute | solution.py:35
  92.1 1.0 constant_dynamic-slice_fusion
  93.1 1.4 fusion.47
  94.5 5.2 %collective-permute-done.9 = f32[192,384]{1,0:T(8,128)} collective-permute-done((f32[192,384]{1,0:T(8,128)}, f32[192,384]{1,0:T(8,128)}, u32[]{:S(2)}, u32[]{:S(2)}) %collective-permute-start.9) | collective-permute-done | bytes 294944 | tf_op jit(solution)/shard_map/ppermute | solution.py:35
  99.7 3.2 %collective-permute-done.14 = f32[192,384]{1,0:T(8,128)} collective-permute-done((f32[192,384]{1,0:T(8,128)}, f32[192,384]{1,0:T(8,128)}, u32[]{:S(2)}, u32[]{:S(2)}) %collective-permute-start.14) | collective-permute-done | bytes 294944 | tf_op jit(solution)/shard_map/ppermute | solution.py:35
  102.9 2.1 %slice_add_fusion.3 = (f32[192,384]{1,0:T(8,128)S(1)}, f32[192,384]{1,0:T(8,128)S(1)}, f32[192,384]{1,0:T(8,128)}, f32[192,384]{1,0:T(8,128)}) fusion(f32[192,384]{1,0:T(8,128)} %collective-permute-done.9, f32[384,384]{1,0:T(8,128)S(1)} %convolution_add_fusion.2, f32[192,384]{1,0:T(8,128)} %collective-permute-done.14, f32[192,384]{1,0:T(8,128)S(1)} %copy-done.11, ...), kind=kLoop, calls=%fused_computation.101 | loop fusion | flops 294912 | bytes 2949121 | tf_op jit(solution)/shard_map/add | solution.py:41
  106.5 1.4 fusion.40
  108.4 11.9 %collective-permute-start.11 = (f32[192,384]{1,0:T(8,128)S(1)}, f32[192,384]{1,0:T(8,128)S(1)}, u32[]{:S(2)}, u32[]{:S(2)}) collective-permute-start(f32[192,384]{1,0:T(8,128)S(1)} %get-tuple-element.3), channel_id=1, source_target_pairs={{0,4},{12,8},{4,0},{8,12},{1,5},{13,9},{5,1},{9,13},{2,6},{14,10},... | collective-permute-start | bytes 884744 | tf_op jit(solution)/shard_map/ppermute | solution.py:35
  121.6 2.0 %convolution_bitcast_fusion = f32[512,384]{1,0:T(8,128)S(1)} fusion(bf16[3,384,384]{2,1,0:T(8,128)(2,1)} %constant_dynamic-slice_fusion, bf16[512,1,384]{2,0,1:T(8,128)(2,1)S(1)} %copy-done.21, bf16[512,1,384]{2,0,1:T(8,128)(2,1)S(1)} %copy-done.19, bf16[512,1,384]{2,0,1:T(8,128)(2,1)S(1)} %copy-done.20), kind=kOutput, calls=%fused_computation.1 | convolution fusion | flops 454164480 | bytes 2850816 | tf_op jit(solution)/shard_map/tko,kio->ti/dot_general | solution.py:84
  123.6 2.4 %collective-permute-done.11 = f32[192,384]{1,0:T(8,128)S(1)} collective-permute-done((f32[192,384]{1,0:T(8,128)S(1)}, f32[192,384]{1,0:T(8,128)S(1)}, u32[]{:S(2)}, u32[]{:S(2)}) %collective-permute-start.11) | collective-permute-done | bytes 294944 | tf_op jit(solution)/shard_map/ppermute | solution.py:35
  126.0 3.2 %collective-permute-done.16 = f32[192,384]{1,0:T(8,128)S(1)} collective-permute-done((f32[192,384]{1,0:T(8,128)S(1)}, f32[192,384]{1,0:T(8,128)S(1)}, u32[]{:S(2)}, u32[]{:S(2)}) %collective-permute-start.16) | collective-permute-done | bytes 294944 | tf_op jit(solution)/shard_map/ppermute | solution.py:35
  129.1 1.0 slice_add_fusion.2
  130.8 1.4 fusion.33
  132.3 1.4 collective-permute-start.19
  134.4 1.3 collective-permute-start.18
  135.7 2.8 %fusion.4 = bf16[1,512,384]{2,1,0:T(8,128)(2,1)} fusion(f32[512,384]{1,0:T(8,128)S(1)} %convolution_bitcast_fusion.3, bf16[3,384,384]{2,1,0:T(8,128)(2,1)} %collective-permute-done.4, bf16[512,1,384]{2,0,1:T(8,128)(2,1)S(1)} %copy-done.16, bf16[512,1,384]{2,0,1:T(8,128)(2,1)S(1)} %copy-done.17, bf16[512,1,384]{2,0,1:T(8,128)(2,1)S(1)} %copy-done.18, ...), kind=kOutput, calls=%fused_computation.12 | convolution fusion | flops 455540736 | bytes 4030464 | tf_op jit(solution)/shard_map/tki,kio->to/dot_general | solution.py:75
  138.9 1.2 convert_element_type.39
  140.2 1.0 add.98
  141.2 1.3 collective-permute-start.20
  142.6 8.0 %collective-permute-done.18 = f32[192,384]{1,0:T(8,128)} collective-permute-done((f32[192,384]{1,0:T(8,128)}, f32[192,384]{1,0:T(8,128)}, u32[]{:S(2)}, u32[]{:S(2)}) %collective-permute-start.18) | collective-permute-done | bytes 294944 | tf_op jit(solution)/shard_map/ppermute | solution.py:39
  150.6 1.0 broadcast_select_fusion.3
  151.6 4.3 %collective-permute-done.20 = f32[192,384]{1,0:T(8,128)S(1)} collective-permute-done((f32[192,384]{1,0:T(8,128)S(1)}, f32[192,384]{1,0:T(8,128)S(1)}, u32[]{:S(2)}, u32[]{:S(2)}) %collective-permute-start.20) | collective-permute-done | bytes 294944 | tf_op jit(solution)/shard_map/ppermute | solution.py:39
  156.0 1.4 pad_maximum_fusion
  (86 shorter events, 9.6 us)
Async XLA Ops:
  0.6 91.5 %copy-start = (bf16[3,384,768]{2,1,0:T(8,128)(2,1)S(1)}, bf16[3,384,768]{2,1,0:T(8,128)(2,1)}, u32[]{:S(2)}) copy-start(bf16[3,384,768]{2,1,0:T(8,128)(2,1)} %param.4) | copy-start | bytes 5308420
  4.7 4.6 %copy-start.6 = (bf16[512,384]{1,0:T(8,128)(2,1)}, bf16[512,384]{1,0:T(8,128)(2,1)S(1)}, u32[]{:S(2)}) copy-start(bf16[512,384]{1,0:T(8,128)(2,1)S(1)} %slice.128) | copy-start | bytes 1179652
  4.7 4.5 %copy-start.1 = (bf16[1,512,384]{2,1,0:T(8,128)(2,1)S(1)}, bf16[1,512,384]{2,1,0:T(8,128)(2,1)}, u32[]{:S(2)}) copy-start(bf16[1,512,384]{2,1,0:T(8,128)(2,1)} %param.5) | copy-start | bytes 1179652
  8.8 0.8 copy-start.8
  9.6 13.3 %collective-permute-start = (bf16[2,256,384]{2,1,0:T(8,128)(2,1)S(1)}, bf16[2,256,384]{2,1,0:T(8,128)(2,1)S(1)}, u32[]{:S(2)}, u32[]{:S(2)}) collective-permute-start(bf16[2,256,384]{2,1,0:T(8,128)(2,1)S(1)} %get-tuple-element.31), channel_id=1, source_target_pairs={{0,4},{4,8},{8,12},{1,5},{5,9},{9,13},{2,6},{6,10},{10,14},{3,7},{... | collective-permute-start | bytes 1179656 | tf_op jit(solution)/shard_map/ppermute | solution.py:12
  14.5 12.5 %collective-permute-start.1 = (bf16[2,256,384]{2,1,0:T(8,128)(2,1)S(1)}, bf16[2,256,384]{2,1,0:T(8,128)(2,1)S(1)}, u32[]{:S(2)}, u32[]{:S(2)}) collective-permute-start(bf16[2,256,384]{2,1,0:T(8,128)(2,1)S(1)} %get-tuple-element.32), channel_id=1, source_target_pairs={{4,0},{8,4},{12,8},{5,1},{9,5},{13,9},{6,2},{10,6},{14,10},{7,3},{... | collective-permute-start | bytes 1179656 | tf_op jit(solution)/shard_map/ppermute | solution.py:12
  22.9 6.1 %copy-start.4 = (bf16[2,256,384]{2,1,0:T(8,128)(2,1)}, bf16[2,256,384]{2,1,0:T(8,128)(2,1)S(1)}, u32[]{:S(2)}) copy-start(bf16[2,256,384]{2,1,0:T(8,128)(2,1)S(1)} %collective-permute-done) | copy-start | bytes 1179652
  27.0 11.2 %copy-start.2 = (bf16[2,256,384]{2,1,0:T(8,128)(2,1)}, bf16[2,256,384]{2,1,0:T(8,128)(2,1)S(1)}, u32[]{:S(2)}) copy-start(bf16[2,256,384]{2,1,0:T(8,128)(2,1)S(1)} %collective-permute-done.1) | copy-start | bytes 1179652
  28.0 2.6 %collective-permute-start.2 = (bf16[2,2,256,384]{3,2,1,0:T(8,128)(2,1)}, bf16[2,2,256,384]{3,2,1,0:T(8,128)(2,1)}, u32[]{:S(2)}, u32[]{:S(2)}) collective-permute-start(bf16[2,2,256,384]{3,2,1,0:T(8,128)(2,1)} %pad_maximum_fusion.3), channel_id=1, source_target_pairs={{0,1},{1,0},{2,3},{3,2},{4,5},{5,4},{6,7},{7,6},{8,9},{9,8},{10,11... | collective-permute-start | bytes 2359304 | tf_op jit(solution)/shard_map/ppermute | solution.py:64
  29.0 2.9 %collective-permute-start.3 = (bf16[2,512,384]{2,1,0:T(8,128)(2,1)}, bf16[2,512,384]{2,1,0:T(8,128)(2,1)}, u32[]{:S(2)}, u32[]{:S(2)}) collective-permute-start(bf16[2,512,384]{2,1,0:T(8,128)(2,1)} %pad_maximum_fusion.2), channel_id=1, source_target_pairs={{0,1},{1,0},{2,3},{3,2},{4,5},{5,4},{6,7},{7,6},{8,9},{9,8},{10,11... | collective-permute-start | bytes 2359304 | tf_op jit(solution)/shard_map/ppermute | solution.py:61
  35.7 20.7 %collective-permute-start.6 = (bf16[2,512,384]{2,1,0:T(8,128)(2,1)}, bf16[2,512,384]{2,1,0:T(8,128)(2,1)}, u32[]{:S(2)}, u32[]{:S(2)}) collective-permute-start(bf16[2,512,384]{2,1,0:T(8,128)(2,1)} %pad_maximum_fusion.1), channel_id=1, source_target_pairs={{0,2},{2,0},{1,3},{3,1},{4,6},{6,4},{5,7},{7,5},{8,10},{10,8},{9,1... | collective-permute-start | bytes 2359304 | tf_op jit(solution)/shard_map/ppermute | solution.py:100
  38.2 25.8 %collective-permute-start.5 = (bf16[2,256,384]{2,1,0:T(8,128)(2,1)S(1)}, bf16[2,256,384]{2,1,0:T(8,128)(2,1)S(1)}, u32[]{:S(2)}, u32[]{:S(2)}) collective-permute-start(bf16[2,256,384]{2,1,0:T(8,128)(2,1)S(1)} %pad_maximum_fusion.16), channel_id=1, source_target_pairs={{0,2},{2,0},{1,3},{3,1},{4,6},{6,4},{5,7},{7,5},{8,10},{10,8},{9,1... | collective-permute-start | bytes 1179656 | tf_op jit(solution)/shard_map/ppermute | solution.py:101
  58.4 10.9 %collective-permute-start.7 = (f32[192,384]{1,0:T(8,128)S(1)}, f32[192,384]{1,0:T(8,128)S(1)}, u32[]{:S(2)}, u32[]{:S(2)}) collective-permute-start(f32[192,384]{1,0:T(8,128)S(1)} %get-tuple-element.43), channel_id=1, source_target_pairs={{0,4},{12,8},{1,5},{13,9},{2,6},{14,10},{3,7},{15,11},{16,20},{28,... | collective-permute-start | bytes 884744 | tf_op jit(solution)/shard_map/ppermute | solution.py:37
  61.9 11.4 %collective-permute-start.12 = (f32[192,384]{1,0:T(8,128)S(1)}, f32[192,384]{1,0:T(8,128)S(1)}, u32[]{:S(2)}, u32[]{:S(2)}) collective-permute-start(f32[192,384]{1,0:T(8,128)S(1)} %get-tuple-element.44), channel_id=1, source_target_pairs={{0,4},{12,8},{1,5},{13,9},{2,6},{14,10},{3,7},{15,11},{16,20},{28,... | collective-permute-start | bytes 884744 | tf_op jit(solution)/shard_map/ppermute | solution.py:37
  65.8 10.5 %copy-start.22 = (bf16[512,384]{1,0:T(8,128)(2,1)}, bf16[512,384]{1,0:T(8,128)(2,1)S(1)}, u32[]{:S(2)}) copy-start(bf16[512,384]{1,0:T(8,128)(2,1)S(1)} %slice_bitcast_fusion.1) | copy-start | bytes 1179652
  73.4 2.9 %copy-start.5 = (bf16[2,256,384]{2,1,0:T(8,128)(2,1)S(1)}, bf16[2,256,384]{2,1,0:T(8,128)(2,1)}, u32[]{:S(2)}) copy-start(bf16[2,256,384]{2,1,0:T(8,128)(2,1)} %copy-done.4) | copy-start | bytes 1179652
  73.4 3.3 %collective-permute-start.8 = (f32[192,384]{1,0:T(8,128)S(1)}, f32[192,384]{1,0:T(8,128)S(1)}, u32[]{:S(2)}, u32[]{:S(2)}) collective-permute-start(f32[192,384]{1,0:T(8,128)S(1)} %get-tuple-element.41), channel_id=1, source_target_pairs={{4,8},{8,4},{5,9},{9,5},{6,10},{10,6},{7,11},{11,7},{20,24},{24,20... | collective-permute-start | bytes 884744 | tf_op jit(solution)/shard_map/ppermute | solution.py:46
  74.2 2.5 %collective-permute-start.13 = (f32[192,384]{1,0:T(8,128)S(1)}, f32[192,384]{1,0:T(8,128)S(1)}, u32[]{:S(2)}, u32[]{:S(2)}) collective-permute-start(f32[192,384]{1,0:T(8,128)S(1)} %get-tuple-element.42), channel_id=1, source_target_pairs={{4,8},{8,4},{5,9},{9,5},{6,10},{10,6},{7,11},{11,7},{20,24},{24,20... | collective-permute-start | bytes 884744 | tf_op jit(solution)/shard_map/ppermute | solution.py:46
  77.8 21.9 %collective-permute-start.9 = (f32[192,384]{1,0:T(8,128)}, f32[192,384]{1,0:T(8,128)}, u32[]{:S(2)}, u32[]{:S(2)}) collective-permute-start(f32[192,384]{1,0:T(8,128)} %get-tuple-element.5), channel_id=1, source_target_pairs={{0,4},{12,8},{4,0},{8,12},{1,5},{13,9},{5,1},{9,13},{2,6},{14,10},... | collective-permute-start | bytes 884744 | tf_op jit(solution)/shard_map/ppermute | solution.py:35
  92.1 10.8 %collective-permute-start.14 = (f32[192,384]{1,0:T(8,128)}, f32[192,384]{1,0:T(8,128)}, u32[]{:S(2)}, u32[]{:S(2)}) collective-permute-start(f32[192,384]{1,0:T(8,128)} %get-tuple-element.39), channel_id=1, source_target_pairs={{0,4},{12,8},{4,0},{8,12},{1,5},{13,9},{5,1},{9,13},{2,6},{14,10},... | collective-permute-start | bytes 884744 | tf_op jit(solution)/shard_map/ppermute | solution.py:35
  93.1 42.6 %collective-permute-start.4 = (bf16[3,384,384]{2,1,0:T(8,128)(2,1)}, bf16[3,384,384]{2,1,0:T(8,128)(2,1)}, u32[]{:S(2)}, u32[]{:S(2)}) collective-permute-start(bf16[3,384,384]{2,1,0:T(8,128)(2,1)} %constant_dynamic-slice_fusion), channel_id=1, source_target_pairs={{0,1},{1,0},{2,3},{3,2},{4,5},{5,4},{6,7},{7,6},{8,9},{9,8},{10,11... | collective-permute-start | bytes 2654216 | tf_op jit(solution)/shard_map/ppermute | solution.py:70
  93.1 9.8 %copy-start.10 = (f32[192,384]{1,0:T(8,128)S(1)}, f32[192,384]{1,0:T(8,128)}, u32[]{:S(2)}) copy-start(f32[192,384]{1,0:T(8,128)} %get-tuple-element.6) | copy-start | bytes 884740
  93.1 9.8 %copy-start.11 = (f32[192,384]{1,0:T(8,128)S(1)}, f32[192,384]{1,0:T(8,128)}, u32[]{:S(2)}) copy-start(f32[192,384]{1,0:T(8,128)} %get-tuple-element.40) | copy-start | bytes 884740
  102.9 3.6 %copy-start.23 = (bf16[512,384]{1,0:T(8,128)(2,1)S(1)}, bf16[512,384]{1,0:T(8,128)(2,1)}, u32[]{:S(2)}) copy-start(bf16[512,384]{1,0:T(8,128)(2,1)} %copy-done.22) | copy-start | bytes 1179652
  102.9 3.6 %copy-start.24 = (bf16[256,384]{1,0:T(8,128)(2,1)S(1)}, bf16[256,384]{1,0:T(8,128)(2,1)}, u32[]{:S(2)}) copy-start(bf16[256,384]{1,0:T(8,128)(2,1)} %get-tuple-element.46) | copy-start | bytes 589828
  105.0 2.9 %copy-start.3 = (bf16[2,256,384]{2,1,0:T(8,128)(2,1)S(1)}, bf16[2,256,384]{2,1,0:T(8,128)(2,1)}, u32[]{:S(2)}) copy-start(bf16[2,256,384]{2,1,0:T(8,128)(2,1)} %copy-done.2) | copy-start | bytes 1179652
  105.0 3.3 %collective-permute-start.10 = (f32[192,384]{1,0:T(8,128)S(1)}, f32[192,384]{1,0:T(8,128)S(1)}, u32[]{:S(2)}, u32[]{:S(2)}) collective-permute-start(f32[192,384]{1,0:T(8,128)S(1)} %get-tuple-element.37), channel_id=1, source_target_pairs={{4,8},{8,4},{5,9},{9,5},{6,10},{10,6},{7,11},{11,7},{20,24},{24,20... | collective-permute-start | bytes 884744 | tf_op jit(solution)/shard_map/ppermute | solution.py:46
  105.8 2.5 %collective-permute-start.15 = (f32[192,384]{1,0:T(8,128)S(1)}, f32[192,384]{1,0:T(8,128)S(1)}, u32[]{:S(2)}, u32[]{:S(2)}) collective-permute-start(f32[192,384]{1,0:T(8,128)S(1)} %get-tuple-element.38), channel_id=1, source_target_pairs={{4,8},{8,4},{5,9},{9,5},{6,10},{10,6},{7,11},{11,7},{20,24},{24,20... | collective-permute-start | bytes 884744 | tf_op jit(solution)/shard_map/ppermute | solution.py:46
  108.4 17.6 %collective-permute-start.11 = (f32[192,384]{1,0:T(8,128)S(1)}, f32[192,384]{1,0:T(8,128)S(1)}, u32[]{:S(2)}, u32[]{:S(2)}) collective-permute-start(f32[192,384]{1,0:T(8,128)S(1)} %get-tuple-element.3), channel_id=1, source_target_pairs={{0,4},{12,8},{4,0},{8,12},{1,5},{13,9},{5,1},{9,13},{2,6},{14,10},... | collective-permute-start | bytes 884744 | tf_op jit(solution)/shard_map/ppermute | solution.py:35
  120.3 8.8 %collective-permute-start.16 = (f32[192,384]{1,0:T(8,128)S(1)}, f32[192,384]{1,0:T(8,128)S(1)}, u32[]{:S(2)}, u32[]{:S(2)}) collective-permute-start(f32[192,384]{1,0:T(8,128)S(1)} %get-tuple-element.35), channel_id=1, source_target_pairs={{0,4},{12,8},{4,0},{8,12},{1,5},{13,9},{5,1},{9,13},{2,6},{14,10},... | collective-permute-start | bytes 884744 | tf_op jit(solution)/shard_map/ppermute | solution.py:35
  120.4 1.0 copy-start.19
  120.4 1.1 copy-start.20
  120.4 1.2 copy-start.21
  129.1 1.7 %copy-start.7 = (bf16[512,384]{1,0:T(8,128)(2,1)S(1)}, bf16[512,384]{1,0:T(8,128)(2,1)}, u32[]{:S(2)}) copy-start(bf16[512,384]{1,0:T(8,128)(2,1)} %copy-done.6) | copy-start | bytes 1179652
  129.1 1.7 %copy-start.9 = (bf16[512,384]{1,0:T(8,128)(2,1)S(1)}, bf16[512,384]{1,0:T(8,128)(2,1)}, u32[]{:S(2)}) copy-start(bf16[512,384]{1,0:T(8,128)(2,1)} %copy-done.8) | copy-start | bytes 1179652
  130.1 3.5 %collective-permute-start.17 = (f32[192,384]{1,0:T(8,128)S(1)}, f32[192,384]{1,0:T(8,128)S(1)}, u32[]{:S(2)}, u32[]{:S(2)}) collective-permute-start(f32[192,384]{1,0:T(8,128)S(1)} %get-tuple-element.33), channel_id=1, source_target_pairs={{4,8},{8,4},{5,9},{9,5},{6,10},{10,6},{7,11},{11,7},{20,24},{24,20... | collective-permute-start | bytes 884744 | tf_op jit(solution)/shard_map/ppermute | solution.py:46
  130.8 4.9 %copy-start.16 = (bf16[512,1,384]{2,0,1:T(8,128)(2,1)S(1)}, bf16[512,1,384]{2,0,1:T(8,128)(2,1)}, u32[]{:S(2)}) copy-start(bf16[512,1,384]{2,0,1:T(8,128)(2,1)} %get-tuple-element.22) | copy-start | bytes 1179652
  130.8 4.9 %copy-start.17 = (bf16[512,1,384]{2,0,1:T(8,128)(2,1)S(1)}, bf16[512,1,384]{2,0,1:T(8,128)(2,1)}, u32[]{:S(2)}) copy-start(bf16[512,1,384]{2,0,1:T(8,128)(2,1)} %get-tuple-element.24) | copy-start | bytes 1179652
  130.8 4.9 %copy-start.18 = (bf16[512,1,384]{2,0,1:T(8,128)(2,1)S(1)}, bf16[512,1,384]{2,0,1:T(8,128)(2,1)}, u32[]{:S(2)}) copy-start(bf16[512,1,384]{2,0,1:T(8,128)(2,1)} %get-tuple-element.25) | copy-start | bytes 1179652
  132.3 7.9 %collective-permute-start.19 = (f32[192,384]{1,0:T(8,128)S(1)}, f32[192,384]{1,0:T(8,128)}, u32[]{:S(2)}, u32[]{:S(2)}) collective-permute-start(f32[192,384]{1,0:T(8,128)S(1)} %get-tuple-element.34), channel_id=1, source_target_pairs={{4,8},{8,4},{5,9},{9,5},{6,10},{10,6},{7,11},{11,7},{20,24},{24,20... | collective-permute-start | bytes 884744 | tf_op jit(solution)/shard_map/ppermute | solution.py:46
  134.4 16.2 %collective-permute-start.18 = (f32[192,384]{1,0:T(8,128)}, f32[192,384]{1,0:T(8,128)}, u32[]{:S(2)}, u32[]{:S(2)}) collective-permute-start(f32[192,384]{1,0:T(8,128)} %add.96), channel_id=1, source_target_pairs={{4,0},{8,12},{5,1},{9,13},{6,2},{10,14},{7,3},{11,15},{20,16},{24,... | collective-permute-start | bytes 884744 | tf_op jit(solution)/shard_map/ppermute | solution.py:39
  138.5 1.6 %copy-start.12 = (f32[192,384]{1,0:T(8,128)S(1)}, f32[192,384]{1,0:T(8,128)}, u32[]{:S(2)}) copy-start(f32[192,384]{1,0:T(8,128)} %get-tuple-element.47) | copy-start | bytes 884740
  138.5 1.6 %copy-start.13 = (f32[192,384]{1,0:T(8,128)S(1)}, f32[192,384]{1,0:T(8,128)}, u32[]{:S(2)}) copy-start(f32[192,384]{1,0:T(8,128)} %get-tuple-element.50) | copy-start | bytes 884740
  140.1 2.4 %copy-start.14 = (f32[192,384]{1,0:T(8,128)S(1)}, f32[192,384]{1,0:T(8,128)}, u32[]{:S(2)}) copy-start(f32[192,384]{1,0:T(8,128)} %get-tuple-element.48) | copy-start | bytes 884740
  140.1 2.4 %copy-start.15 = (f32[192,384]{1,0:T(8,128)S(1)}, f32[192,384]{1,0:T(8,128)}, u32[]{:S(2)}) copy-start(f32[192,384]{1,0:T(8,128)} %get-tuple-element.49) | copy-start | bytes 884740
  141.2 14.7 %collective-permute-start.20 = (f32[192,384]{1,0:T(8,128)S(1)}, f32[192,384]{1,0:T(8,128)S(1)}, u32[]{:S(2)}, u32[]{:S(2)}) collective-permute-start(f32[192,384]{1,0:T(8,128)S(1)} %add.98), channel_id=1, source_target_pairs={{4,0},{8,12},{5,1},{9,13},{6,2},{10,14},{7,3},{11,15},{20,16},{24,... | collective-permute-start | bytes 884744 | tf_op jit(solution)/shard_map/ppermute | solution.py:39

commit v4 on v3

--- a/solution.py
+++ b/solution.py
@@ -54,7 +54,11 @@
     width = local_in.shape[1]
     spread = rows // 2
     c = lax.axis_index("chan")
-    pooled = 0.5 * (local_in[0::2].astype(jnp.float32) + local_in[1::2].astype(jnp.float32))
+    pairing = lax.broadcasted_iota(jnp.int32, (rows, 2 * rows), 1) // 2 == lax.broadcasted_iota(
+        jnp.int32, (rows, 2 * rows), 0
+    )
+    pairing = jnp.where(pairing, 0.5, 0.0).astype(jnp.bfloat16)
+    pooled = jnp.dot(pairing, local_in, preferred_element_type=jnp.float32)
     activation = jax.nn.gelu(pooled).astype(jnp.bfloat16)
 
     both = jnp.stack([activation, local_cot])
@@ -93,22 +97,26 @@
     par_cot = par_mid[1]
     batch_count = lax.axis_size("batch")
     seq_count = lax.axis_size("seq")
-    if batch_count == 2 and seq_count == 4:
+    if batch_count == 2:
         b = lax.axis_index("batch")
         cot_mine = jnp.where(b == c, local_cot, par_cot)
-        cot_theirs = jnp.where(b == c, par_cot, local_cot)
-        far_mid = lax.ppermute(jnp.stack([activation, cot_theirs]), "batch", SWAP)
+        same_core = lax.ppermute(local_cot, ("batch", "chan"), [(2, 0), (1, 3)])
+        cross_core = lax.ppermute(local_cot, ("batch", "chan"), [(2, 1), (1, 2)])
+        far_cot = jnp.where(b == c, same_core, cross_core)
+        far_mid = lax.ppermute(activation, "batch", SWAP)
         far_halo = lax.ppermute(jnp.stack([from_prev[0], from_next[0]]), "batch", SWAP)
-        far_act = jnp.concatenate([far_halo[0], far_mid[0], far_halo[1]], 0)
+        far_act = jnp.concatenate([far_halo[0], far_mid, far_halo[1]], 0)
         far_taps = tap_stack(far_act, rows, spread, (0, 1, 2))
-        pieces = []
+        by_k = {}
+        previous = None
         for k in (1, 0, 2):
             grad_k = jnp.dot(
                 own_taps[:, k].T, cot_mine, preferred_element_type=jnp.float32
-            ) + jnp.dot(far_taps[:, k].T, far_mid[1], preferred_element_type=jnp.float32)
-            pieces.extend(jnp.split(grad_k, 2, 0))
-        totals = line_total(pieces)
-        by_k = {k: jnp.concatenate(totals[2 * n : 2 * n + 2], 0) for n, k in enumerate((1, 0, 2))}
+            ) + jnp.dot(far_taps[:, k].T, far_cot, preferred_element_type=jnp.float32)
+            if previous is not None:
+                grad_k, previous = lax.optimization_barrier((grad_k, previous))
+            by_k[k] = lax.psum(grad_k, "seq")
+            previous = by_k[k]
         weight_grad = jnp.stack([by_k[0], by_k[1], by_k[2]])
     else:
         lo = jnp.where(c == 0, local_cot, par_cot)

time: 158 us -> 179 us (1.13)
  waiting for transfers between devices: 64.4 us -> 115 us
  starting transfers between devices: 47.5 us -> 16 us
  between operations: 1.18 us -> 14 us
  local copies, waits for them, and re-layouts: 15.4 us -> 3.84 us
  matrix products: 12.4 us -> 21.6 us
  other arithmetic: 16.3 us -> 7.89 us
    psum x0 -> x3, waiting for transfers between devices: none -> 104 us  [shards(): by_k[k] = lax.psum(grad_k, 'seq')]
    ppermute x15 -> x3, waiting for transfers between devices: 51.3 us -> 5.21 us  [the longest x1 5.2 us: shards(): far_mid = lax.ppermute(activation, 'batch', SWAP)]
    ppermute x15 -> x3, starting transfers between devices: 40.1 us -> 7.03 us  [the longest x1 4.33 us: shards(): far_mid = lax.ppermute(activation, 'batch', SWAP)]
    slice x2 -> x0, local copies, waits for them, and re-layouts: 8.11 us -> none  [the longest x1 4.07 us: shards(): local_in[0::2].astype(jnp.float32) + local_in[1::2].astype(jnp.float32)]
    ppermute x2, waiting for transfers between devices: 11.2 us -> 3.22 us  [shift_from(): return lax.ppermute(block, axis, route)]
    add x5 -> x0, other arithmetic: 4.87 us -> none  [the longest x3 3.09 us: line_total(): pairs[step] = pieces[step] + got]
    dot_general x3 -> x4, matrix products: 4.27 us -> 7.05 us  [the longest x3 4.12 us: shards(): jnp.dot(far_taps[:, k].T, far_cot, preferred_element_type=jnp.float32)]
    dot_general x3, matrix products: 1.19 us -> 3.67 us  [shards(): jnp.dot(own_taps[:, k].T, cot_mine, preferred_element_type=jnp.float32)]
  transfers between devices with their start and end apart: 21 -> 12, of which waited for: 13 -> 6; matrix products, arithmetic and copies ran while one was open for 17% -> 15% of each run, Pallas kernels for 0% -> 0%
where the time goes in v4:
time: 179 us
  waiting for transfers between devices  115 us (64%)
  matrix products  21.6 us (12%)
  starting transfers between devices  16 us (9%)
  between operations  14 us (8%)
  other arithmetic  7.89 us (4%)
  local copies, waits for them, and re-layouts  3.84 us (2%)
    psum x3, waiting for transfers between devices, shards(): by_k[k] = lax.psum(grad_k, 'seq')  104 us
    ppermute x2, starting transfers between devices, shift_from(): return lax.ppermute(block, axis, route)  6.26 us
    ppermute x1, waiting for transfers between devices, shards(): far_mid = lax.ppermute(activation, 'batch', SWAP)  5.2 us
    ppermute x1, starting transfers between devices, shards(): far_mid = lax.ppermute(activation, 'batch', SWAP)  4.33 us
    dot_general x3, matrix products, shards(): jnp.dot(far_taps[:, k].T, far_cot, preferred_element_type=jnp.float32)  4.12 us
    dot_general x3, matrix products, shards(): jnp.dot(own_taps[:, k].T, cot_mine, preferred_element_type=jnp.float32)  3.67 us
  transfers between devices with their start and end apart: 12, of which 6 were waited for; matrix products, arithmetic and copies ran while one was open for 15% of the time, Pallas kernels for 0%

profile of v4, /device:TPU:0, one launch (start us, length us, event | category | flops | bytes accessed | tf_op | source)
XLA Modules:
  0.0 178.7 jit_solution(5339654678908696308)
XLA Ops:
  7.2 0.0 copy-start
  7.2 0.0 all-reduce.4.cloned.1.call-start
  7.2 0.0 copy-start.1
  7.3 2.9 %multiply_convert_fusion = (bf16[512,384]{1,0:T(8,128)(2,1)S(1)}, f32[512,384]{1,0:T(8,128)}) fusion(bf16[1,1024,384]{2,1,0:T(8,128)(2,1)} %param.3, s32[1024]{0:T(1024)S(1)} %get-tuple-element.32, s32[1024]{0:T(1024)S(1)} %get-tuple-element.33, pred[1024]{0:T(1024)(128)(4,1)S(1)} %fusion.62), kind=kOutput, calls=%fused_computation.59 | convolution fusion | flops 406519808 | bytes 1975296 | tf_op jit(solution)/shard_map/dot_general | solution.py:61
  10.2 1.0 fusion.45
  11.2 5.0 %collective-permute-start = (bf16[2,256,384]{2,1,0:T(8,128)(2,1)}, bf16[2,256,384]{2,1,0:T(8,128)(2,1)S(1)}, u32[]{:S(2)}, u32[]{:S(2)}) collective-permute-start(bf16[2,256,384]{2,1,0:T(8,128)(2,1)} %get-tuple-element.26), channel_id=1, source_target_pairs={{0,4},{4,8},{8,12},{1,5},{5,9},{9,13},{2,6},{6,10},{10,14},{3,7},{... | collective-permute-start | bytes 1179656 | tf_op jit(solution)/shard_map/ppermute | solution.py:12
  16.1 1.3 collective-permute-start.1
  17.4 1.3 collective-permute-start.7
  18.7 1.4 collective-permute-start.8
  20.1 4.3 %collective-permute-start.6 = (bf16[512,384]{1,0:T(8,128)(2,1)S(1)}, bf16[512,384]{1,0:T(8,128)(2,1)}, u32[]{:S(2)}, u32[]{:S(2)}) collective-permute-start(bf16[512,384]{1,0:T(8,128)(2,1)S(1)} %get-tuple-element.30), channel_id=1, source_target_pairs={{0,2},{2,0},{1,3},{3,1},{4,6},{6,4},{5,7},{7,5},{8,10},{10,8},{9,1... | collective-permute-start | bytes 1179656 | tf_op jit(solution)/shard_map/ppermute | solution.py:106
  24.5 0.1 pad_maximum_fusion.1
  24.6 1.0 constant_dynamic-slice_fusion
  25.6 0.0 collective-permute-done
  25.6 3.2 %collective-permute-done.1 = bf16[2,256,384]{2,1,0:T(8,128)(2,1)S(1)} collective-permute-done((bf16[2,256,384]{2,1,0:T(8,128)(2,1)}, bf16[2,256,384]{2,1,0:T(8,128)(2,1)S(1)}, u32[]{:S(2)}, u32[]{:S(2)}) %collective-permute-start.1) | collective-permute-done | bytes 393248 | tf_op jit(solution)/shard_map/ppermute | solution.py:12
  28.8 0.1 pad_maximum_fusion.2
  28.9 0.1 collective-permute-start.2
  29.0 1.0 fusion.54
  30.0 1.7 convolution_bitcast_fusion.3
  31.8 0.8 pad_maximum_fusion.15
  32.6 0.0 collective-permute-done.7
  32.6 0.5 collective-permute-start.4
  33.1 2.0 %collective-permute-start.5 = (bf16[2,256,384]{2,1,0:T(8,128)(2,1)}, bf16[2,256,384]{2,1,0:T(8,128)(2,1)}, u32[]{:S(2)}, u32[]{:S(2)}) collective-permute-start(bf16[2,256,384]{2,1,0:T(8,128)(2,1)} %pad_maximum_fusion.15), channel_id=1, source_target_pairs={{0,2},{2,0},{1,3},{3,1},{4,6},{6,4},{5,7},{7,5},{8,10},{10,8},{9,1... | collective-permute-start | bytes 1179656 | tf_op jit(solution)/shard_map/ppermute | solution.py:107
  35.1 1.0 broadcast_select_fusion
  36.1 5.2 %collective-permute-done.6 = bf16[512,384]{1,0:T(8,128)(2,1)} collective-permute-done((bf16[512,384]{1,0:T(8,128)(2,1)S(1)}, bf16[512,384]{1,0:T(8,128)(2,1)}, u32[]{:S(2)}, u32[]{:S(2)}) %collective-permute-start.6) | collective-permute-done | bytes 393248 | tf_op jit(solution)/shard_map/ppermute | solution.py:106
  41.3 1.4 fusion.75
  42.7 0.1 slice_bitcast_fusion.2
  42.8 1.5 broadcast_select_fusion.1
  44.3 1.2 convolution_add_fusion.1
  45.5 0.0 all-reduce.4.cloned.1.call-update
  45.5 0.0 all-reduce.6.cloned.1.call-start
  45.6 2.7 %collective-permute-done.5 = bf16[2,256,384]{2,1,0:T(8,128)(2,1)} collective-permute-done((bf16[2,256,384]{2,1,0:T(8,128)(2,1)}, bf16[2,256,384]{2,1,0:T(8,128)(2,1)}, u32[]{:S(2)}, u32[]{:S(2)}) %collective-permute-start.5) | collective-permute-done | bytes 393248 | tf_op jit(solution)/shard_map/ppermute | solution.py:107
  48.3 1.1 slice_bitcast_fusion.5
  49.3 1.3 fusion.49
  50.7 1.2 convolution_add_fusion.2
  51.9 34.8 %all-reduce.4.cloned.1.call-done = f32[384,384]{1,0:T(8,128)} async-done(((f32[384,384]{1,0:T(8,128)}), f32[384,384]{1,0:T(8,128)}) %all-reduce.4.cloned.1.call-update) | async-done | bytes 589840 | tf_op jit(solution)/shard_map/psum | solution.py:118
  86.7 0.0 all-reduce.6.cloned.1.call-update
  86.8 0.0 all-reduce.8.cloned.1.call-start
  86.8 1.4 fusion.47
  88.3 2.9 %convolution_bitcast_fusion = f32[512,384]{1,0:T(8,128)} fusion(bf16[3,384,384]{2,1,0:T(8,128)(2,1)} %constant_dynamic-slice_fusion, bf16[512,1,384]{2,0,1:T(8,128)(2,1)S(1)} %copy-done.12, bf16[512,1,384]{2,0,1:T(8,128)(2,1)S(1)} %copy-done.10, bf16[512,1,384]{2,0,1:T(8,128)(2,1)S(1)} %copy-done.11), kind=kOutput, calls=%fused_computation.3 | convolution fusion | flops 454164480 | bytes 2850816 | tf_op jit(solution)/shard_map/tko,kio->ti/dot_general | solution.py:88
  91.2 1.2 convolution_add_fusion
  92.4 35.8 %all-reduce.6.cloned.1.call-done = f32[384,384]{1,0:T(8,128)} async-done(((f32[384,384]{1,0:T(8,128)}), f32[384,384]{1,0:T(8,128)}) %all-reduce.6.cloned.1.call-update) | async-done | bytes 589840 | tf_op jit(solution)/shard_map/psum | solution.py:118
  128.2 0.0 all-reduce.8.cloned.1.call-update
  128.3 2.8 %fusion.39 = bf16[512,384]{1,0:T(8,128)(2,1)S(1)} fusion(f32[512,384]{1,0:T(8,128)} %get-tuple-element.31, f32[512,384]{1,0:T(8,128)} %convolution_bitcast_fusion, bf16[512,1,384]{2,0,1:T(8,128)(2,1)} %get-tuple-element.23, bf16[512,1,384]{2,0,1:T(8,128)(2,1)S(1)} %bitcast.87, bf16[512,1,384]{2,0,1:T(8,128)(2,1)S(1)} %copy-done.8, ...), kind=kOutput, calls=%fused_computation.56 | convolution fusion | flops 458883072 | bytes 4423684 | tf_op jit(solution)/shard_map/tko,kio->ti/dot_general | solution.py:85
  131.1 0.4 broadcast_in_dim.18
  131.5 1.2 convert_element_type.31
  132.7 3.5 %fusion.4 = bf16[1,512,384]{2,1,0:T(8,128)(2,1)} fusion(f32[512,384]{1,0:T(8,128)} %get-tuple-element.31, f32[512,384]{1,0:T(8,128)} %convolution_bitcast_fusion.3, bf16[3,384,384]{2,1,0:T(8,128)(2,1)} %collective-permute-done.4, bf16[512,1,384]{2,0,1:T(8,128)(2,1)S(1)} %copy-done.9, bf16[512,1,384]{2,0,1:T(8,128)(2,1)} %get-tuple-element.19, ...), kind=kOutput, calls=%fused_computation.14 | convolution fusion | flops 454754304 | bytes 4030464 | tf_op jit(solution)/shard_map/tki,kio->to/dot_general | solution.py:79
  136.2 33.6 %all-reduce.8.cloned.1.call-done = f32[1,384,384]{2,1,0:T(8,128)} async-done(((f32[1,384,384]{2,1,0:T(8,128)}), f32[1,384,384]{2,1,0:T(8,128)}) %all-reduce.8.cloned.1.call-update) | async-done | bytes 589840 | tf_op jit(solution)/shard_map/psum | solution.py:118
  169.8 2.4 %pad_maximum_fusion = f32[3,384,384]{2,1,0:T(8,128)} fusion(f32[1,384,384]{2,1,0:T(8,128)} %all-reduce.8.cloned.1.call-done, f32[1,384,384]{2,1,0:T(8,128)S(1)} %bitcast.97, f32[1,384,384]{2,1,0:T(8,128)S(1)} %bitcast.98), kind=kLoop, calls=%fused_computation.2 | loop fusion | flops 884736 | bytes 3538944 | tf_op jit(solution)/shard_map/stack | solution.py:120
  (33 shorter events, 0.1 us)
Async XLA Ops:
  7.2 17.4 %copy-start = (bf16[3,384,768]{2,1,0:T(8,128)(2,1)S(1)}, bf16[3,384,768]{2,1,0:T(8,128)(2,1)}, u32[]{:S(2)}) copy-start(bf16[3,384,768]{2,1,0:T(8,128)(2,1)} %param.4) | copy-start | bytes 5308420
  7.2 79.6 %all-reduce.4.cloned.1.call-start = ((), (), s32[]{:S(2)}) async-start(), calls=%async_computation | async-start | bytes 1179648 | tf_op jit(solution)/shard_map/psum | solution.py:118
  7.2 2.9 %copy-start.1 = (bf16[1,512,384]{2,1,0:T(8,128)(2,1)S(1)}, bf16[1,512,384]{2,1,0:T(8,128)(2,1)}, u32[]{:S(2)}) copy-start(bf16[1,512,384]{2,1,0:T(8,128)(2,1)} %param.5) | copy-start | bytes 1179652
  11.2 14.4 %collective-permute-start = (bf16[2,256,384]{2,1,0:T(8,128)(2,1)}, bf16[2,256,384]{2,1,0:T(8,128)(2,1)S(1)}, u32[]{:S(2)}, u32[]{:S(2)}) collective-permute-start(bf16[2,256,384]{2,1,0:T(8,128)(2,1)} %get-tuple-element.26), channel_id=1, source_target_pairs={{0,4},{4,8},{8,12},{1,5},{5,9},{9,13},{2,6},{6,10},{10,14},{3,7},{... | collective-permute-start | bytes 1179656 | tf_op jit(solution)/shard_map/ppermute | solution.py:12
  16.1 12.7 %collective-permute-start.1 = (bf16[2,256,384]{2,1,0:T(8,128)(2,1)}, bf16[2,256,384]{2,1,0:T(8,128)(2,1)S(1)}, u32[]{:S(2)}, u32[]{:S(2)}) collective-permute-start(bf16[2,256,384]{2,1,0:T(8,128)(2,1)} %get-tuple-element.27), channel_id=1, source_target_pairs={{4,0},{8,4},{12,8},{5,1},{9,5},{13,9},{6,2},{10,6},{14,10},{7,3},{... | collective-permute-start | bytes 1179656 | tf_op jit(solution)/shard_map/ppermute | solution.py:12
  17.4 15.2 %collective-permute-start.7 = (bf16[512,384]{1,0:T(8,128)(2,1)S(1)}, bf16[512,384]{1,0:T(8,128)(2,1)}, u32[]{:S(2)}, u32[]{:S(2)}) collective-permute-start(bf16[512,384]{1,0:T(8,128)(2,1)S(1)} %bitcast.85), channel_id=1, source_target_pairs={{2,0},{1,3},{6,4},{5,7},{10,8},{9,11},{14,12},{13,15},{18,16},{17,... | collective-permute-start | bytes 1179656 | tf_op jit(solution)/shard_map/ppermute | solution.py:103
  18.7 14.4 %collective-permute-start.8 = (bf16[512,384]{1,0:T(8,128)(2,1)S(1)}, bf16[512,384]{1,0:T(8,128)(2,1)}, u32[]{:S(2)}, u32[]{:S(2)}) collective-permute-start(bf16[512,384]{1,0:T(8,128)(2,1)S(1)} %bitcast.86), channel_id=1, source_target_pairs={{2,1},{1,2},{6,5},{5,6},{10,9},{9,10},{14,13},{13,14},{18,17},{17,... | collective-permute-start | bytes 1179656 | tf_op jit(solution)/shard_map/ppermute | solution.py:104
  20.1 21.2 %collective-permute-start.6 = (bf16[512,384]{1,0:T(8,128)(2,1)S(1)}, bf16[512,384]{1,0:T(8,128)(2,1)}, u32[]{:S(2)}, u32[]{:S(2)}) collective-permute-start(bf16[512,384]{1,0:T(8,128)(2,1)S(1)} %get-tuple-element.30), channel_id=1, source_target_pairs={{0,2},{2,0},{1,3},{3,1},{4,6},{6,4},{5,7},{7,5},{8,10},{10,8},{9,1... | collective-permute-start | bytes 1179656 | tf_op jit(solution)/shard_map/ppermute | solution.py:106
  25.6 6.2 %copy-start.4 = (bf16[2,256,384]{2,1,0:T(8,128)(2,1)}, bf16[2,256,384]{2,1,0:T(8,128)(2,1)S(1)}, u32[]{:S(2)}) copy-start(bf16[2,256,384]{2,1,0:T(8,128)(2,1)S(1)} %collective-permute-done) | copy-start | bytes 1179652
  25.6 17.2 %collective-permute-start.3 = (bf16[2,512,384]{2,1,0:T(8,128)(2,1)S(1)}, bf16[2,512,384]{2,1,0:T(8,128)(2,1)S(1)}, u32[]{:S(2)}, u32[]{:S(2)}) collective-permute-start(bf16[2,512,384]{2,1,0:T(8,128)(2,1)S(1)} %pad_maximum_fusion.1), channel_id=1, source_target_pairs={{0,1},{1,0},{2,3},{3,2},{4,5},{5,4},{6,7},{7,6},{8,9},{9,8},{10,11... | collective-permute-start | bytes 2359304 | tf_op jit(solution)/shard_map/ppermute | solution.py:65
  28.8 3.0 %copy-start.2 = (bf16[2,256,384]{2,1,0:T(8,128)(2,1)}, bf16[2,256,384]{2,1,0:T(8,128)(2,1)S(1)}, u32[]{:S(2)}) copy-start(bf16[2,256,384]{2,1,0:T(8,128)(2,1)S(1)} %collective-permute-done.1) | copy-start | bytes 1179652
  28.9 13.8 %collective-permute-start.2 = (bf16[2,2,256,384]{3,2,1,0:T(8,128)(2,1)S(1)}, bf16[2,2,256,384]{3,2,1,0:T(8,128)(2,1)S(1)}, u32[]{:S(2)}, u32[]{:S(2)}) collective-permute-start(bf16[2,2,256,384]{3,2,1,0:T(8,128)(2,1)S(1)} %pad_maximum_fusion.2), channel_id=1, source_target_pairs={{0,1},{1,0},{2,3},{3,2},{4,5},{5,4},{6,7},{7,6},{8,9},{9,8},{10,11... | collective-permute-start | bytes 2359304 | tf_op jit(solution)/shard_map/ppermute | solution.py:68
  32.6 100.1 %collective-permute-start.4 = (bf16[3,384,384]{2,1,0:T(8,128)(2,1)}, bf16[3,384,384]{2,1,0:T(8,128)(2,1)}, u32[]{:S(2)}, u32[]{:S(2)}) collective-permute-start(bf16[3,384,384]{2,1,0:T(8,128)(2,1)} %constant_dynamic-slice_fusion), channel_id=1, source_target_pairs={{0,1},{1,0},{2,3},{3,2},{4,5},{5,4},{6,7},{7,6},{8,9},{9,8},{10,11... | collective-permute-start | bytes 2654216 | tf_op jit(solution)/shard_map/ppermute | solution.py:74
  33.1 15.2 %collective-permute-start.5 = (bf16[2,256,384]{2,1,0:T(8,128)(2,1)}, bf16[2,256,384]{2,1,0:T(8,128)(2,1)}, u32[]{:S(2)}, u32[]{:S(2)}) collective-permute-start(bf16[2,256,384]{2,1,0:T(8,128)(2,1)} %pad_maximum_fusion.15), channel_id=1, source_target_pairs={{0,2},{2,0},{1,3},{3,1},{4,6},{6,4},{5,7},{7,5},{8,10},{10,8},{9,1... | collective-permute-start | bytes 1179656 | tf_op jit(solution)/shard_map/ppermute | solution.py:107
  45.5 82.7 %all-reduce.6.cloned.1.call-start = ((), (), s32[]{:S(2)}) async-start(), calls=%async_computation.1 | async-start | bytes 1179648 | tf_op jit(solution)/shard_map/psum | solution.py:118
  45.6 5.1 %copy-start.5 = (bf16[2,256,384]{2,1,0:T(8,128)(2,1)S(1)}, bf16[2,256,384]{2,1,0:T(8,128)(2,1)}, u32[]{:S(2)}) copy-start(bf16[2,256,384]{2,1,0:T(8,128)(2,1)} %copy-done.4) | copy-start | bytes 1179652
  86.8 83.0 %all-reduce.8.cloned.1.call-start = ((), (), s32[]{:S(2)}) async-start(), calls=%async_computation.2 | async-start | bytes 1179648 | tf_op jit(solution)/shard_map/psum | solution.py:118
  86.8 1.4 copy-start.10
  86.8 1.4 copy-start.11
  86.8 1.4 copy-start.12
  88.3 2.9 %copy-start.3 = (bf16[2,256,384]{2,1,0:T(8,128)(2,1)S(1)}, bf16[2,256,384]{2,1,0:T(8,128)(2,1)}, u32[]{:S(2)}) copy-start(bf16[2,256,384]{2,1,0:T(8,128)(2,1)} %copy-done.2) | copy-start | bytes 1179652
  91.2 37.1 %copy-start.8 = (bf16[512,1,384]{2,0,1:T(8,128)(2,1)S(1)}, bf16[512,1,384]{2,0,1:T(8,128)(2,1)}, u32[]{:S(2)}) copy-start(bf16[512,1,384]{2,0,1:T(8,128)(2,1)} %get-tuple-element.7) | copy-start | bytes 1179652
  131.1 1.6 copy-start.9
  132.7 37.1 %copy-start.6 = (f32[384,384]{1,0:T(8,128)S(1)}, f32[384,384]{1,0:T(8,128)}, u32[]{:S(2)}) copy-start(f32[384,384]{1,0:T(8,128)} %all-reduce.4.cloned.1.call-done) | copy-start | bytes 1769476
  132.7 37.1 %copy-start.7 = (f32[384,384]{1,0:T(8,128)S(1)}, f32[384,384]{1,0:T(8,128)}, u32[]{:S(2)}) copy-start(f32[384,384]{1,0:T(8,128)} %all-reduce.6.cloned.1.call-done) | copy-start | bytes 1769476
Sparse Core Ops, SparseCore 0:
  45.7 41.0 all-reduce.3
  89.1 39.1 all-reduce.5
  130.6 39.1 all-reduce.7

commit v5 on v4

--- a/solution.py
+++ b/solution.py
@@ -45,6 +45,23 @@
             ready = pairs[step - 1]
             wholes[step - 1] = ready + lax.ppermute(ready, "seq", middle)
     return [totals[n] for n in range(count)]
+
+
+def seq_total(block):
+    count = lax.axis_size("seq")
+    s = lax.axis_index("seq")
+    rows = block.shape[1] // count
+    quarters = block.reshape(block.shape[0], count, rows, block.shape[2])
+    mine = lax.dynamic_index_in_dim(quarters, s, 1, keepdims=False)
+    for d in range(1, count):
+        going = lax.dynamic_index_in_dim(quarters, (s + d) % count, 1, keepdims=False)
+        mine = mine + lax.ppermute(going, "seq", [(j, (j + d) % count) for j in range(count)])
+    gathered = [mine] + [
+        lax.ppermute(mine, "seq", [(j, (j + d) % count) for j in range(count)]) for d in range(1, count)
+    ]
+    stacked = jnp.stack(gathered, 1)
+    order = (s - jnp.arange(count)) % count
+    return jnp.take(stacked, order, axis=1).reshape(block.shape)
 
 
 def shards(seq_in, conv_weight, cotangent):
@@ -107,17 +124,17 @@
         far_halo = lax.ppermute(jnp.stack([from_prev[0], from_next[0]]), "batch", SWAP)
         far_act = jnp.concatenate([far_halo[0], far_mid, far_halo[1]], 0)
         far_taps = tap_stack(far_act, rows, spread, (0, 1, 2))
-        by_k = {}
-        previous = None
+        grads = {}
         for k in (1, 0, 2):
-            grad_k = jnp.dot(
+            grads[k] = jnp.dot(
                 own_taps[:, k].T, cot_mine, preferred_element_type=jnp.float32
             ) + jnp.dot(far_taps[:, k].T, far_cot, preferred_element_type=jnp.float32)
-            if previous is not None:
-                grad_k, previous = lax.optimization_barrier((grad_k, previous))
-            by_k[k] = lax.psum(grad_k, "seq")
-            previous = by_k[k]
-        weight_grad = jnp.stack([by_k[0], by_k[1], by_k[2]])
+        if seq_count == 4:
+            middle = seq_total(grads[1][None])
+            sides = seq_total(jnp.stack([grads[0], grads[2]]))
+            weight_grad = jnp.concatenate([sides[:1], middle, sides[1:]], 0)
+        else:
+            weight_grad = lax.psum(jnp.stack([grads[0], grads[1], grads[2]]), "seq")
     else:
         lo = jnp.where(c == 0, local_cot, par_cot)
         hi = jnp.where(c == 0, par_cot, local_cot)

time: 179 us -> 132 us (0.74)
  the two profiles are of different devices: /device:TPU:0 before, /device:TPU:26 now
where the time goes in v5:
time: 132 us
  waiting for transfers between devices  51.9 us (39%)
  starting transfers between devices  45.6 us (35%)
  matrix products  12.5 us (9%)
  other arithmetic  11.8 us (9%)
  local copies, waits for them, and re-layouts  9 us (7%)
    ppermute x6, starting transfers between devices, seq_total(): lax.ppermute(mine, 'seq', [(j, (j + d) % count) for j in range(count)])  23.7 us
    ppermute x6, waiting for transfers between devices, seq_total(): lax.ppermute(mine, 'seq', [(j, (j + d) % count) for j in range(count)])  23.6 us
    ppermute x6, waiting for transfers between devices, seq_total(): lax.ppermute(going, 'seq', [(j, (j + d) % count) for j in range(count)])  12.7 us
    ppermute x6, starting transfers between devices, seq_total(): lax.ppermute(going, 'seq', [(j, (j + d) % count) for j in range(count)])  9.17 us
    ppermute x2, waiting for transfers between devices, shift_from(): return lax.ppermute(block, axis, route)  8.26 us
    ppermute x1, waiting for transfers between devices, shards(): lax.ppermute(jnp.stack([from_prev[0], from_next[0]]), 'batch', SWAP)  7.37 us
    ppermute x2, starting transfers between devices, shift_from(): return lax.ppermute(block, axis, route)  5.85 us
    dot_general x3, matrix products, shards(): jnp.dot(far_taps[:, k].T, far_cot, preferred_element_type=jnp.float32)  4.03 us
  transfers between devices with their start and end apart: 21, of which 8 were waited for; matrix products, arithmetic and copies ran while one was open for 20% of the time, Pallas kernels for 0%

profile of v5, /device:TPU:26, one launch (start us, length us, event | category | flops | bytes accessed | tf_op | source)
XLA Modules:
  0.0 131.9 jit_solution(13857962440496166380)
XLA Ops:
  0.6 3.3 %collective-permute-start.7 = (bf16[512,384]{1,0:T(8,128)(2,1)}, bf16[512,384]{1,0:T(8,128)(2,1)}, u32[]{:S(2)}, u32[]{:S(2)}) collective-permute-start(bf16[512,384]{1,0:T(8,128)(2,1)} %bitcast.136), channel_id=1, source_target_pairs={{2,0},{1,3},{6,4},{5,7},{10,8},{9,11},{14,12},{13,15},{18,16},{17,... | collective-permute-start | bytes 1179656 | tf_op jit(solution)/shard_map/ppermute | solution.py:120
  4.0 2.5 %collective-permute-start.8 = (bf16[512,384]{1,0:T(8,128)(2,1)}, bf16[512,384]{1,0:T(8,128)(2,1)}, u32[]{:S(2)}, u32[]{:S(2)}) collective-permute-start(bf16[512,384]{1,0:T(8,128)(2,1)} %bitcast.137), channel_id=1, source_target_pairs={{2,1},{1,2},{6,5},{5,6},{10,9},{9,10},{14,13},{13,14},{18,17},{17,... | collective-permute-start | bytes 1179656 | tf_op jit(solution)/shard_map/ppermute | solution.py:121
  6.6 2.8 %multiply_convert_fusion = (bf16[512,384]{1,0:T(8,128)(2,1)S(1)}, f32[512,384]{1,0:T(8,128)}) fusion(bf16[1,1024,384]{2,1,0:T(8,128)(2,1)} %param.3, s32[1024]{0:T(1024)S(1)} %get-tuple-element.36, s32[1024]{0:T(1024)S(1)} %get-tuple-element.37, pred[1024]{0:T(1024)(128)(4,1)S(1)} %fusion.75), kind=kOutput, calls=%fused_computation.71 | convolution fusion | flops 406519808 | bytes 1975296 | tf_op jit(solution)/shard_map/dot_general | solution.py:78
  9.4 1.0 fusion.45
  10.4 1.3 collective-permute-start
  11.6 4.6 %collective-permute-start.1 = (bf16[2,256,384]{2,1,0:T(8,128)(2,1)}, bf16[2,256,384]{2,1,0:T(8,128)(2,1)S(1)}, u32[]{:S(2)}, u32[]{:S(2)}) collective-permute-start(bf16[2,256,384]{2,1,0:T(8,128)(2,1)} %get-tuple-element.28), channel_id=1, source_target_pairs={{4,0},{8,4},{12,8},{5,1},{9,5},{13,9},{6,2},{10,6},{14,10},{7,3},{... | collective-permute-start | bytes 1179656 | tf_op jit(solution)/shard_map/ppermute | solution.py:12
  16.3 1.0 pad_maximum_fusion.2
  17.6 6.6 %collective-permute-done = bf16[2,256,384]{2,1,0:T(8,128)(2,1)S(1)} collective-permute-done((bf16[2,256,384]{2,1,0:T(8,128)(2,1)}, bf16[2,256,384]{2,1,0:T(8,128)(2,1)S(1)}, u32[]{:S(2)}, u32[]{:S(2)}) %collective-permute-start) | collective-permute-done | bytes 393248 | tf_op jit(solution)/shard_map/ppermute | solution.py:12
  24.3 1.6 %collective-permute-done.1 = bf16[2,256,384]{2,1,0:T(8,128)(2,1)S(1)} collective-permute-done((bf16[2,256,384]{2,1,0:T(8,128)(2,1)}, bf16[2,256,384]{2,1,0:T(8,128)(2,1)S(1)}, u32[]{:S(2)}, u32[]{:S(2)}) %collective-permute-start.1) | collective-permute-done | bytes 393248 | tf_op jit(solution)/shard_map/ppermute | solution.py:12
  26.2 0.5 collective-permute-start.2
  27.0 1.0 broadcast_select_fusion
  28.3 1.4 %fusion.92 = f32[384,384]{1,0:T(8,128)S(1)} fusion(bf16[512,384]{1,0:T(8,128)(2,1)} %collective-permute-done.6, bf16[512,384]{1,0:T(8,128)(2,1)S(1)} %broadcast_select_fusion), kind=kOutput, calls=%fused_computation.163 | convolution fusion | flops 150994944 | bytes 1376256 | tf_op jit(solution)/shard_map/dot_general | solution.py:131
  29.7 0.8 convolution_bitcast_fusion.3
  30.5 7.4 %collective-permute-done.5 = bf16[2,256,384]{2,1,0:T(8,128)(2,1)S(1)} collective-permute-done((bf16[2,256,384]{2,1,0:T(8,128)(2,1)S(1)}, bf16[2,256,384]{2,1,0:T(8,128)(2,1)S(1)}, u32[]{:S(2)}, u32[]{:S(2)}) %collective-permute-start.5) | collective-permute-done | bytes 393248 | tf_op jit(solution)/shard_map/ppermute | solution.py:124
  37.9 1.3 %fusion.47 = f32[384,384]{1,0:T(8,128)S(1)} fusion(bf16[512,384]{1,0:T(8,128)(2,1)S(1)} %broadcast_select_fusion, bf16[256,384]{1,0:T(8,128)(2,1)S(1)} %get-tuple-element.32, bf16[512,384]{1,0:T(8,128)(2,1)} %collective-permute-done.6), kind=kOutput, calls=%fused_computation.79 | convolution fusion | flops 151781376 | bytes 1572864 | tf_op jit(solution)/shard_map/dot_general | solution.py:131
  39.2 1.3 fusion.49
  41.4 0.8 dynamic-slice_bitcast_fusion.2
  42.2 2.2 %collective-permute-start.15 = (f32[1,96,384]{2,1,0:T(8,128)S(1)}, f32[1,96,384]{2,1,0:T(8,128)}, u32[]{:S(2)}, u32[]{:S(2)}) collective-permute-start(f32[1,96,384]{2,1,0:T(8,128)S(1)} %get-tuple-element.29), channel_id=1, source_target_pairs={{0,4},{4,8},{8,12},{12,0},{1,5},{5,9},{9,13},{13,1},{2,6},{6,10},{... | collective-permute-start | bytes 442376 | tf_op jit(solution)/shard_map/ppermute | solution.py:58
  44.4 1.7 %collective-permute-start.16 = (f32[1,96,384]{2,1,0:T(8,128)}, f32[1,96,384]{2,1,0:T(8,128)}, u32[]{:S(2)}, u32[]{:S(2)}) collective-permute-start(f32[1,96,384]{2,1,0:T(8,128)} %get-tuple-element.31), channel_id=1, source_target_pairs={{0,8},{4,12},{8,0},{12,4},{1,9},{5,13},{9,1},{13,5},{2,10},{6,14},... | collective-permute-start | bytes 442376 | tf_op jit(solution)/shard_map/ppermute | solution.py:58
  46.0 0.5 collective-permute-start.17
  46.9 0.4 convolution_add_fusion.2
  47.3 0.8 copy-done.2
  48.2 1.0 fusion.68
  49.1 1.0 collective-permute-start.10
  50.1 0.8 convolution_bitcast_fusion
  51.3 1.3 %fusion.39 = bf16[512,384]{1,0:T(8,128)(2,1)S(1)} fusion(f32[512,384]{1,0:T(8,128)S(1)} %copy-done.8, f32[512,384]{1,0:T(8,128)S(1)} %convolution_bitcast_fusion, bf16[512,1,384]{2,0,1:T(8,128)(2,1)S(1)} %get-tuple-element.24, bf16[512,1,384]{2,0,1:T(8,128)(2,1)S(1)} %bitcast.138, bf16[512,1,384]{2,0,1:T(8,128)(2,1)S(1)} %get-tuple-element.8, ...), kind=kOutput, calls=%fused_computation.68 | convolution fusion | flops 458883072 | bytes 4423684 | tf_op jit(solution)/shard_map/tko,kio->ti/dot_general | solution.py:102
  52.6 3.0 %collective-permute-start.11 = (f32[2,96,384]{2,1,0:T(8,128)}, f32[2,96,384]{2,1,0:T(8,128)}, u32[]{:S(2)}, u32[]{:S(2)}) collective-permute-start(f32[2,96,384]{2,1,0:T(8,128)} %get-tuple-element.7), channel_id=1, source_target_pairs={{0,12},{4,0},{8,4},{12,8},{1,13},{5,1},{9,5},{13,9},{2,14},{6,2},{... | collective-permute-start | bytes 884744 | tf_op jit(solution)/shard_map/ppermute | solution.py:58
  55.6 0.9 collective-permute-start.9
  56.5 1.6 %fusion.4 = bf16[1,512,384]{2,1,0:T(8,128)(2,1)} fusion(f32[512,384]{1,0:T(8,128)S(1)} %copy-done.8, f32[512,384]{1,0:T(8,128)S(1)} %convolution_bitcast_fusion.3, bf16[3,384,384]{2,1,0:T(8,128)(2,1)S(1)} %collective-permute-done.4, bf16[512,1,384]{2,0,1:T(8,128)(2,1)S(1)} %get-tuple-element.18, bf16[512,1,384]{2,0,1:T(8,128)(2,1)S(1)} %get-tuple-element.20, ...), kind=kOutput, calls=%fused_computation.24 | convolution fusion | flops 454754304 | bytes 4030464 | tf_op jit(solution)/shard_map/tki,kio->to/dot_general | solution.py:96
  58.0 1.3 broadcast_in_dim.42
  59.3 3.0 %convert_element_type.31 = bf16[1,1024,384]{2,1,0:T(8,128)(2,1)} reshape(bf16[512,2,384]{2,1,0:T(2,128)(2,1)} %broadcast_in_dim.42) | data formatting | bytes 1572864 | tf_op jit(solution)/shard_map/convert_element_type | solution.py:111
  62.3 10.5 %collective-permute-done.16 = f32[1,96,384]{2,1,0:T(8,128)} collective-permute-done((f32[1,96,384]{2,1,0:T(8,128)}, f32[1,96,384]{2,1,0:T(8,128)}, u32[]{:S(2)}, u32[]{:S(2)}) %collective-permute-start.16) | collective-permute-done | bytes 147488 | tf_op jit(solution)/shard_map/ppermute | solution.py:58
  72.9 1.2 fusion.72
  74.0 3.0 %collective-permute-start.18 = (f32[1,96,384]{2,1,0:T(8,128)S(1)}, f32[1,96,384]{2,1,0:T(8,128)S(1)}, u32[]{:S(2)}, u32[]{:S(2)}) collective-permute-start(f32[1,96,384]{2,1,0:T(8,128)S(1)} %fusion.72), channel_id=1, source_target_pairs={{0,4},{4,8},{8,12},{12,0},{1,5},{5,9},{9,13},{13,1},{2,6},{6,10},{... | collective-permute-start | bytes 442376 | tf_op jit(solution)/shard_map/ppermute | solution.py:60
  77.0 1.7 %collective-permute-start.19 = (f32[1,96,384]{2,1,0:T(8,128)S(1)}, f32[1,96,384]{2,1,0:T(8,128)S(1)}, u32[]{:S(2)}, u32[]{:S(2)}) collective-permute-start(f32[1,96,384]{2,1,0:T(8,128)S(1)} %fusion.72), channel_id=1, source_target_pairs={{0,8},{4,12},{8,0},{12,4},{1,9},{5,13},{9,1},{13,5},{2,10},{6,14},... | collective-permute-start | bytes 442376 | tf_op jit(solution)/shard_map/ppermute | solution.py:60
  78.7 1.9 %collective-permute-done.10 = f32[2,96,384]{2,1,0:T(8,128)S(1)} collective-permute-done((f32[2,96,384]{2,1,0:T(8,128)}, f32[2,96,384]{2,1,0:T(8,128)S(1)}, u32[]{:S(2)}, u32[]{:S(2)}) %collective-permute-start.10) | collective-permute-done | bytes 294944 | tf_op jit(solution)/shard_map/ppermute | solution.py:58
  80.6 1.4 %collective-permute-start.20 = (f32[1,96,384]{2,1,0:T(8,128)S(1)}, f32[1,96,384]{2,1,0:T(8,128)S(1)}, u32[]{:S(2)}, u32[]{:S(2)}) collective-permute-start(f32[1,96,384]{2,1,0:T(8,128)S(1)} %fusion.72), channel_id=1, source_target_pairs={{0,12},{4,0},{8,4},{12,8},{1,13},{5,1},{9,5},{13,9},{2,14},{6,2},{... | collective-permute-start | bytes 442376 | tf_op jit(solution)/shard_map/ppermute | solution.py:60
  82.3 1.8 %fusion.66 = f32[2,96,384]{2,1,0:T(8,128)} fusion(f32[2,96,384]{2,1,0:T(8,128)} %collective-permute-done.11, f32[2,96,384]{2,1,0:T(8,128)S(1)} %collective-permute-done.10, f32[2,96,384]{2,1,0:T(8,128)} %collective-permute-done.9, s32[]{:T(128)S(6)} %select_n.138, f32[1,4,96,384]{3,2,1,0:T(8,128)S(1)} %bitcast.148, f32[1,4,96,384]{3,2,1,0:T(8,128)S(1)} %bitcast.146), kind=kLoop, calls=%fused_computation.116 | loop fusion | flops 294912 | bytes 2359300 | tf_op jit(solution)/shard_map/add | solution.py:58
  84.1 2.8 %collective-permute-start.12 = (f32[2,96,384]{2,1,0:T(8,128)}, f32[2,96,384]{2,1,0:T(8,128)}, u32[]{:S(2)}, u32[]{:S(2)}) collective-permute-start(f32[2,96,384]{2,1,0:T(8,128)} %fusion.66), channel_id=1, source_target_pairs={{0,4},{4,8},{8,12},{12,0},{1,5},{5,9},{9,13},{13,1},{2,6},{6,10},{... | collective-permute-start | bytes 884744 | tf_op jit(solution)/shard_map/ppermute | solution.py:60
  86.9 12.8 %collective-permute-start.13 = (f32[2,96,384]{2,1,0:T(8,128)}, f32[2,96,384]{2,1,0:T(8,128)}, u32[]{:S(2)}, u32[]{:S(2)}) collective-permute-start(f32[2,96,384]{2,1,0:T(8,128)} %fusion.66), channel_id=1, source_target_pairs={{0,8},{4,12},{8,0},{12,4},{1,9},{5,13},{9,1},{13,5},{2,10},{6,14},... | collective-permute-start | bytes 884744 | tf_op jit(solution)/shard_map/ppermute | solution.py:60
  99.7 2.0 %collective-permute-start.14 = (f32[2,96,384]{2,1,0:T(8,128)}, f32[2,96,384]{2,1,0:T(8,128)}, u32[]{:S(2)}, u32[]{:S(2)}) collective-permute-start(f32[2,96,384]{2,1,0:T(8,128)} %fusion.66), channel_id=1, source_target_pairs={{0,12},{4,0},{8,4},{12,8},{1,13},{5,1},{9,5},{13,9},{2,14},{6,2},{... | collective-permute-start | bytes 884744 | tf_op jit(solution)/shard_map/ppermute | solution.py:60
  101.8 0.6 gather_fusion.1
  102.5 2.5 %collective-permute-done.12 = f32[2,96,384]{2,1,0:T(8,128)} collective-permute-done((f32[2,96,384]{2,1,0:T(8,128)}, f32[2,96,384]{2,1,0:T(8,128)}, u32[]{:S(2)}, u32[]{:S(2)}) %collective-permute-start.12) | collective-permute-done | bytes 294944 | tf_op jit(solution)/shard_map/ppermute | solution.py:60
  105.0 21.0 %collective-permute-done.13 = f32[2,96,384]{2,1,0:T(8,128)} collective-permute-done((f32[2,96,384]{2,1,0:T(8,128)}, f32[2,96,384]{2,1,0:T(8,128)}, u32[]{:S(2)}, u32[]{:S(2)}) %collective-permute-start.13) | collective-permute-done | bytes 294944 | tf_op jit(solution)/shard_map/ppermute | solution.py:60
  126.1 1.3 pad_maximum_fusion.1
  127.4 1.6 %gather_fusion = f32[4,2,96,384]{3,2,1,0:T(8,128)} fusion(f32[2,4,96,384]{3,2,1,0:T(8,128)S(1)} %pad_maximum_fusion.1, s32[1024]{0:T(1024)S(1)} %pad_clamp_fusion), kind=kCustom, calls=%fused_computation | custom fusion | bytes 2359312 | tf_op jit(solution)/shard_map/jit(_take)/gather | solution.py:64
  129.0 1.4 %select_bitcast_fusion = f32[2,4,96,384]{3,2,0,1:T(8,128)S(1)} fusion(f32[4,2,96,384]{3,2,1,0:T(8,128)} %gather_fusion, pred[4]{0:T(512)(128)(4,1)S(1)} %compare_and_fusion), kind=kLoop, calls=%fused_computation.46 | loop fusion | flops 294912 | bytes 2359300 | tf_op jit(solution)/shard_map/jit(_take)/select_n | solution.py:64
  130.5 1.4 %pad_maximum_fusion = f32[3,384,384]{2,1,0:T(8,128)} fusion(f32[1,384,384]{2,1,0:T(8,128)S(1)} %bitcast.152, f32[1,384,384]{2,1,0:T(8,128)S(1)} %bitcast_select_fusion, f32[1,384,384]{2,1,0:T(8,128)S(1)} %bitcast.151), kind=kLoop, calls=%fused_computation.12 | loop fusion | flops 884736 | bytes 3538944 | tf_op jit(solution)/shard_map/concatenate | solution.py:135
  (56 shorter events, 3.2 us)
Async XLA Ops:
  0.6 16.8 %copy-start = (bf16[3,384,768]{2,1,0:T(8,128)(2,1)S(1)}, bf16[3,384,768]{2,1,0:T(8,128)(2,1)}, u32[]{:S(2)}) copy-start(bf16[3,384,768]{2,1,0:T(8,128)(2,1)} %param.4) | copy-start | bytes 5308420
  0.6 25.6 %collective-permute-start.7 = (bf16[512,384]{1,0:T(8,128)(2,1)}, bf16[512,384]{1,0:T(8,128)(2,1)}, u32[]{:S(2)}, u32[]{:S(2)}) collective-permute-start(bf16[512,384]{1,0:T(8,128)(2,1)} %bitcast.136), channel_id=1, source_target_pairs={{2,0},{1,3},{6,4},{5,7},{10,8},{9,11},{14,12},{13,15},{18,16},{17,... | collective-permute-start | bytes 1179656 | tf_op jit(solution)/shard_map/ppermute | solution.py:120
  4.0 22.7 %collective-permute-start.8 = (bf16[512,384]{1,0:T(8,128)(2,1)}, bf16[512,384]{1,0:T(8,128)(2,1)}, u32[]{:S(2)}, u32[]{:S(2)}) collective-permute-start(bf16[512,384]{1,0:T(8,128)(2,1)} %bitcast.137), channel_id=1, source_target_pairs={{2,1},{1,2},{6,5},{5,6},{10,9},{9,10},{14,13},{13,14},{18,17},{17,... | collective-permute-start | bytes 1179656 | tf_op jit(solution)/shard_map/ppermute | solution.py:121
  6.6 2.8 %copy-start.1 = (bf16[1,512,384]{2,1,0:T(8,128)(2,1)S(1)}, bf16[1,512,384]{2,1,0:T(8,128)(2,1)}, u32[]{:S(2)}) copy-start(bf16[1,512,384]{2,1,0:T(8,128)(2,1)} %param.5) | copy-start | bytes 1179652
  9.4 18.9 %collective-permute-start.6 = (bf16[512,384]{1,0:T(8,128)(2,1)S(1)}, bf16[512,384]{1,0:T(8,128)(2,1)}, u32[]{:S(2)}, u32[]{:S(2)}) collective-permute-start(bf16[512,384]{1,0:T(8,128)(2,1)S(1)} %get-tuple-element.34), channel_id=1, source_target_pairs={{0,2},{2,0},{1,3},{3,1},{4,6},{6,4},{5,7},{7,5},{8,10},{10,8},{9,1... | collective-permute-start | bytes 1179656 | tf_op jit(solution)/shard_map/ppermute | solution.py:123
  10.4 13.8 %collective-permute-start = (bf16[2,256,384]{2,1,0:T(8,128)(2,1)}, bf16[2,256,384]{2,1,0:T(8,128)(2,1)S(1)}, u32[]{:S(2)}, u32[]{:S(2)}) collective-permute-start(bf16[2,256,384]{2,1,0:T(8,128)(2,1)} %get-tuple-element.27), channel_id=1, source_target_pairs={{0,4},{4,8},{8,12},{1,5},{5,9},{9,13},{2,6},{6,10},{10,14},{3,7},{... | collective-permute-start | bytes 1179656 | tf_op jit(solution)/shard_map/ppermute | solution.py:12
  11.6 14.3 %collective-permute-start.1 = (bf16[2,256,384]{2,1,0:T(8,128)(2,1)}, bf16[2,256,384]{2,1,0:T(8,128)(2,1)S(1)}, u32[]{:S(2)}, u32[]{:S(2)}) collective-permute-start(bf16[2,256,384]{2,1,0:T(8,128)(2,1)} %get-tuple-element.28), channel_id=1, source_target_pairs={{4,0},{8,4},{12,8},{5,1},{9,5},{13,9},{6,2},{10,6},{14,10},{7,3},{... | collective-permute-start | bytes 1179656 | tf_op jit(solution)/shard_map/ppermute | solution.py:12
  17.5 6.7 %copy-start.7 = (bf16[2,512,384]{2,1,0:T(8,128)(2,1)S(1)}, bf16[2,512,384]{2,1,0:T(8,128)(2,1)}, u32[]{:S(2)}) copy-start(bf16[2,512,384]{2,1,0:T(8,128)(2,1)} %pad_maximum_fusion.2) | copy-start | bytes 2359300
  24.2 16.4 %collective-permute-start.3 = (bf16[2,512,384]{2,1,0:T(8,128)(2,1)S(1)}, bf16[2,512,384]{2,1,0:T(8,128)(2,1)S(1)}, u32[]{:S(2)}, u32[]{:S(2)}) collective-permute-start(bf16[2,512,384]{2,1,0:T(8,128)(2,1)S(1)} %copy-done.7), channel_id=1, source_target_pairs={{0,1},{1,0},{2,3},{3,2},{4,5},{5,4},{6,7},{7,6},{8,9},{9,8},{10,11... | collective-permute-start | bytes 2359304 | tf_op jit(solution)/shard_map/ppermute | solution.py:82
  26.0 2.1 %copy-start.4 = (bf16[2,256,384]{2,1,0:T(8,128)(2,1)}, bf16[2,256,384]{2,1,0:T(8,128)(2,1)S(1)}, u32[]{:S(2)}) copy-start(bf16[2,256,384]{2,1,0:T(8,128)(2,1)S(1)} %collective-permute-done.1) | copy-start | bytes 1179652
  26.0 26.6 %collective-permute-start.4 = (bf16[3,384,384]{2,1,0:T(8,128)(2,1)S(1)}, bf16[3,384,384]{2,1,0:T(8,128)(2,1)S(1)}, u32[]{:S(2)}, u32[]{:S(2)}) collective-permute-start(bf16[3,384,384]{2,1,0:T(8,128)(2,1)S(1)} %constant_dynamic-slice_fusion), channel_id=1, source_target_pairs={{0,1},{1,0},{2,3},{3,2},{4,5},{5,4},{6,7},{7,6},{8,9},{9,8},{10,11... | collective-permute-start | bytes 2654216 | tf_op jit(solution)/shard_map/ppermute | solution.py:91
  26.2 14.3 %collective-permute-start.2 = (bf16[2,2,256,384]{3,2,1,0:T(8,128)(2,1)S(1)}, bf16[2,2,256,384]{3,2,1,0:T(8,128)(2,1)S(1)}, u32[]{:S(2)}, u32[]{:S(2)}) collective-permute-start(bf16[2,2,256,384]{3,2,1,0:T(8,128)(2,1)S(1)} %pad_maximum_fusion.3), channel_id=1, source_target_pairs={{0,1},{1,0},{2,3},{3,2},{4,5},{5,4},{6,7},{7,6},{8,9},{9,8},{10,11... | collective-permute-start | bytes 2359304 | tf_op jit(solution)/shard_map/ppermute | solution.py:85
  26.7 11.1 %collective-permute-start.5 = (bf16[2,256,384]{2,1,0:T(8,128)(2,1)S(1)}, bf16[2,256,384]{2,1,0:T(8,128)(2,1)S(1)}, u32[]{:S(2)}, u32[]{:S(2)}) collective-permute-start(bf16[2,256,384]{2,1,0:T(8,128)(2,1)S(1)} %pad_maximum_fusion.16), channel_id=1, source_target_pairs={{0,2},{2,0},{1,3},{3,1},{4,6},{6,4},{5,7},{7,5},{8,10},{10,8},{9,1... | collective-permute-start | bytes 1179656 | tf_op jit(solution)/shard_map/ppermute | solution.py:124
  41.0 5.5 %copy-start.5 = (bf16[2,256,384]{2,1,0:T(8,128)(2,1)S(1)}, bf16[2,256,384]{2,1,0:T(8,128)(2,1)}, u32[]{:S(2)}) copy-start(bf16[2,256,384]{2,1,0:T(8,128)(2,1)} %copy-done.4) | copy-start | bytes 1179652
  41.4 5.5 %copy-start.6 = (f32[384,384]{1,0:T(8,128)}, f32[384,384]{1,0:T(8,128)S(1)}, u32[]{:S(2)}) copy-start(f32[384,384]{1,0:T(8,128)S(1)} %convolution_add_fusion) | copy-start | bytes 1769476
  42.2 13.4 %collective-permute-start.15 = (f32[1,96,384]{2,1,0:T(8,128)S(1)}, f32[1,96,384]{2,1,0:T(8,128)}, u32[]{:S(2)}, u32[]{:S(2)}) collective-permute-start(f32[1,96,384]{2,1,0:T(8,128)S(1)} %get-tuple-element.29), channel_id=1, source_target_pairs={{0,4},{4,8},{8,12},{12,0},{1,5},{5,9},{9,13},{13,1},{2,6},{6,10},{... | collective-permute-start | bytes 442376 | tf_op jit(solution)/shard_map/ppermute | solution.py:58
  44.4 28.5 %collective-permute-start.16 = (f32[1,96,384]{2,1,0:T(8,128)}, f32[1,96,384]{2,1,0:T(8,128)}, u32[]{:S(2)}, u32[]{:S(2)}) collective-permute-start(f32[1,96,384]{2,1,0:T(8,128)} %get-tuple-element.31), channel_id=1, source_target_pairs={{0,8},{4,12},{8,0},{12,4},{1,9},{5,13},{9,1},{13,5},{2,10},{6,14},... | collective-permute-start | bytes 442376 | tf_op jit(solution)/shard_map/ppermute | solution.py:58
  46.0 26.8 %collective-permute-start.17 = (f32[1,96,384]{2,1,0:T(8,128)}, f32[1,96,384]{2,1,0:T(8,128)}, u32[]{:S(2)}, u32[]{:S(2)}) collective-permute-start(f32[1,96,384]{2,1,0:T(8,128)} %get-tuple-element.30), channel_id=1, source_target_pairs={{0,12},{4,0},{8,4},{12,8},{1,13},{5,1},{9,5},{13,9},{2,14},{6,2},{... | collective-permute-start | bytes 442376 | tf_op jit(solution)/shard_map/ppermute | solution.py:58
  47.3 0.8 copy-start.2
  49.1 31.5 %collective-permute-start.10 = (f32[2,96,384]{2,1,0:T(8,128)}, f32[2,96,384]{2,1,0:T(8,128)S(1)}, u32[]{:S(2)}, u32[]{:S(2)}) collective-permute-start(f32[2,96,384]{2,1,0:T(8,128)} %get-tuple-element.6), channel_id=1, source_target_pairs={{0,8},{4,12},{8,0},{12,4},{1,9},{5,13},{9,1},{13,5},{2,10},{6,14},... | collective-permute-start | bytes 884744 | tf_op jit(solution)/shard_map/ppermute | solution.py:58
  50.1 1.1 copy-start.8
  52.6 29.4 %collective-permute-start.11 = (f32[2,96,384]{2,1,0:T(8,128)}, f32[2,96,384]{2,1,0:T(8,128)}, u32[]{:S(2)}, u32[]{:S(2)}) collective-permute-start(f32[2,96,384]{2,1,0:T(8,128)} %get-tuple-element.7), channel_id=1, source_target_pairs={{0,12},{4,0},{8,4},{12,8},{1,13},{5,1},{9,5},{13,9},{2,14},{6,2},{... | collective-permute-start | bytes 884744 | tf_op jit(solution)/shard_map/ppermute | solution.py:58
  55.6 26.7 %collective-permute-start.9 = (f32[2,96,384]{2,1,0:T(8,128)}, f32[2,96,384]{2,1,0:T(8,128)}, u32[]{:S(2)}, u32[]{:S(2)}) collective-permute-start(f32[2,96,384]{2,1,0:T(8,128)} %get-tuple-element.5), channel_id=1, source_target_pairs={{0,4},{4,8},{8,12},{12,0},{1,5},{5,9},{9,13},{13,1},{2,6},{6,10},{... | collective-permute-start | bytes 884744 | tf_op jit(solution)/shard_map/ppermute | solution.py:58
  59.3 23.0 %copy-start.3 = (f32[384,384]{1,0:T(8,128)S(1)}, f32[384,384]{1,0:T(8,128)}, u32[]{:S(2)}) copy-start(f32[384,384]{1,0:T(8,128)} %copy-done.2) | copy-start | bytes 1769476
  74.0 25.7 %collective-permute-start.18 = (f32[1,96,384]{2,1,0:T(8,128)S(1)}, f32[1,96,384]{2,1,0:T(8,128)S(1)}, u32[]{:S(2)}, u32[]{:S(2)}) collective-permute-start(f32[1,96,384]{2,1,0:T(8,128)S(1)} %fusion.72), channel_id=1, source_target_pairs={{0,4},{4,8},{8,12},{12,0},{1,5},{5,9},{9,13},{13,1},{2,6},{6,10},{... | collective-permute-start | bytes 442376 | tf_op jit(solution)/shard_map/ppermute | solution.py:60
  77.0 24.7 %collective-permute-start.19 = (f32[1,96,384]{2,1,0:T(8,128)S(1)}, f32[1,96,384]{2,1,0:T(8,128)S(1)}, u32[]{:S(2)}, u32[]{:S(2)}) collective-permute-start(f32[1,96,384]{2,1,0:T(8,128)S(1)} %fusion.72), channel_id=1, source_target_pairs={{0,8},{4,12},{8,0},{12,4},{1,9},{5,13},{9,1},{13,5},{2,10},{6,14},... | collective-permute-start | bytes 442376 | tf_op jit(solution)/shard_map/ppermute | solution.py:60
  80.6 21.1 %collective-permute-start.20 = (f32[1,96,384]{2,1,0:T(8,128)S(1)}, f32[1,96,384]{2,1,0:T(8,128)S(1)}, u32[]{:S(2)}, u32[]{:S(2)}) collective-permute-start(f32[1,96,384]{2,1,0:T(8,128)S(1)} %fusion.72), channel_id=1, source_target_pairs={{0,12},{4,0},{8,4},{12,8},{1,13},{5,1},{9,5},{13,9},{2,14},{6,2},{... | collective-permute-start | bytes 442376 | tf_op jit(solution)/shard_map/ppermute | solution.py:60
  84.1 20.9 %collective-permute-start.12 = (f32[2,96,384]{2,1,0:T(8,128)}, f32[2,96,384]{2,1,0:T(8,128)}, u32[]{:S(2)}, u32[]{:S(2)}) collective-permute-start(f32[2,96,384]{2,1,0:T(8,128)} %fusion.66), channel_id=1, source_target_pairs={{0,4},{4,8},{8,12},{12,0},{1,5},{5,9},{9,13},{13,1},{2,6},{6,10},{... | collective-permute-start | bytes 884744 | tf_op jit(solution)/shard_map/ppermute | solution.py:60
  86.9 39.1 %collective-permute-start.13 = (f32[2,96,384]{2,1,0:T(8,128)}, f32[2,96,384]{2,1,0:T(8,128)}, u32[]{:S(2)}, u32[]{:S(2)}) collective-permute-start(f32[2,96,384]{2,1,0:T(8,128)} %fusion.66), channel_id=1, source_target_pairs={{0,8},{4,12},{8,0},{12,4},{1,9},{5,13},{9,1},{13,5},{2,10},{6,14},... | collective-permute-start | bytes 884744 | tf_op jit(solution)/shard_map/ppermute | solution.py:60
  99.7 26.4 %collective-permute-start.14 = (f32[2,96,384]{2,1,0:T(8,128)}, f32[2,96,384]{2,1,0:T(8,128)}, u32[]{:S(2)}, u32[]{:S(2)}) collective-permute-start(f32[2,96,384]{2,1,0:T(8,128)} %fusion.66), channel_id=1, source_target_pairs={{0,12},{4,0},{8,4},{12,8},{1,13},{5,1},{9,5},{13,9},{2,14},{6,2},{... | collective-permute-start | bytes 884744 | tf_op jit(solution)/shard_map/ppermute | solution.py:60

commit v6 on v5

--- a/solution.py
+++ b/solution.py
@@ -56,12 +56,13 @@
     for d in range(1, count):
         going = lax.dynamic_index_in_dim(quarters, (s + d) % count, 1, keepdims=False)
         mine = mine + lax.ppermute(going, "seq", [(j, (j + d) % count) for j in range(count)])
+    mine = mine.astype(jnp.bfloat16)
     gathered = [mine] + [
         lax.ppermute(mine, "seq", [(j, (j + d) % count) for j in range(count)]) for d in range(1, count)
     ]
     stacked = jnp.stack(gathered, 1)
     order = (s - jnp.arange(count)) % count
-    return jnp.take(stacked, order, axis=1).reshape(block.shape)
+    return jnp.take(stacked, order, axis=1).reshape(block.shape).astype(jnp.float32)
 
 
 def shards(seq_in, conv_weight, cotangent):

time: 132 us -> 114 us (0.86)
  the two profiles are of different devices: /device:TPU:26 before, /device:TPU:0 now
where the time goes in v6:
time: 114 us
  starting transfers between devices  45.3 us (40%)
  waiting for transfers between devices  39.5 us (35%)
  matrix products  12.5 us (11%)
  other arithmetic  8.54 us (7%)
  local copies, waits for them, and re-layouts  7.06 us (6%)
    ppermute x6, starting transfers between devices, seq_total(): lax.ppermute(going, 'seq', [(j, (j + d) % count) for j in range(count)])  18.6 us
    ppermute x6, waiting for transfers between devices, seq_total(): lax.ppermute(mine, 'seq', [(j, (j + d) % count) for j in range(count)])  16.6 us
    ppermute x6, starting transfers between devices, seq_total(): lax.ppermute(mine, 'seq', [(j, (j + d) % count) for j in range(count)])  10.7 us
    ppermute x2, waiting for transfers between devices, shift_from(): return lax.ppermute(block, axis, route)  9.64 us
    ppermute x6, waiting for transfers between devices, seq_total(): lax.ppermute(going, 'seq', [(j, (j + d) % count) for j in range(count)])  7.32 us
    ppermute x1, starting transfers between devices, shards(): far_mid = lax.ppermute(activation, 'batch', SWAP)  6.01 us
    ppermute x1, waiting for transfers between devices, shards(): lax.ppermute(jnp.stack([from_prev[0], from_next[0]]), 'batch', SWAP)  5.91 us
    ppermute x2, starting transfers between devices, shift_from(): return lax.ppermute(block, axis, route)  4.78 us
  transfers between devices with their start and end apart: 21, of which 7 were waited for; matrix products, arithmetic and copies ran while one was open for 21% of the time, Pallas kernels for 0%

profile of v6, /device:TPU:0, one launch (start us, length us, event | category | flops | bytes accessed | tf_op | source)
XLA Modules:
  0.0 114.0 jit_solution(5624810419598166834)
XLA Ops:
  0.6 1.4 %collective-permute-start.7 = (bf16[512,384]{1,0:T(8,128)(2,1)}, bf16[512,384]{1,0:T(8,128)(2,1)}, u32[]{:S(2)}, u32[]{:S(2)}) collective-permute-start(bf16[512,384]{1,0:T(8,128)(2,1)} %bitcast.143), channel_id=1, source_target_pairs={{2,0},{1,3},{6,4},{5,7},{10,8},{9,11},{14,12},{13,15},{18,16},{17,... | collective-permute-start | bytes 1179656 | tf_op jit(solution)/shard_map/ppermute | solution.py:121
  2.1 1.4 %collective-permute-start.8 = (bf16[512,384]{1,0:T(8,128)(2,1)}, bf16[512,384]{1,0:T(8,128)(2,1)}, u32[]{:S(2)}, u32[]{:S(2)}) collective-permute-start(bf16[512,384]{1,0:T(8,128)(2,1)} %bitcast.144), channel_id=1, source_target_pairs={{2,1},{1,2},{6,5},{5,6},{10,9},{9,10},{14,13},{13,14},{18,17},{17,... | collective-permute-start | bytes 1179656 | tf_op jit(solution)/shard_map/ppermute | solution.py:122
  3.5 2.8 %multiply_convert_fusion = (bf16[512,384]{1,0:T(8,128)(2,1)S(1)}, f32[512,384]{1,0:T(8,128)}) fusion(bf16[1,1024,384]{2,1,0:T(8,128)(2,1)} %param.3, s32[1024]{0:T(1024)S(1)} %get-tuple-element.36, s32[1024]{0:T(1024)S(1)} %get-tuple-element.37, pred[1024]{0:T(1024)(128)(4,1)S(1)} %fusion.79), kind=kOutput, calls=%fused_computation.69 | convolution fusion | flops 406519808 | bytes 1975296 | tf_op jit(solution)/shard_map/dot_general | solution.py:79
  6.3 6.0 %collective-permute-start.6 = (bf16[512,384]{1,0:T(8,128)(2,1)S(1)}, bf16[512,384]{1,0:T(8,128)(2,1)}, u32[]{:S(2)}, u32[]{:S(2)}) collective-permute-start(bf16[512,384]{1,0:T(8,128)(2,1)S(1)} %get-tuple-element.34), channel_id=1, source_target_pairs={{0,2},{2,0},{1,3},{3,1},{4,6},{6,4},{5,7},{7,5},{8,10},{10,8},{9,1... | collective-permute-start | bytes 1179656 | tf_op jit(solution)/shard_map/ppermute | solution.py:124
  12.4 1.0 fusion.46
  13.3 3.5 %collective-permute-start = (bf16[2,256,384]{2,1,0:T(8,128)(2,1)}, bf16[2,256,384]{2,1,0:T(8,128)(2,1)S(1)}, u32[]{:S(2)}, u32[]{:S(2)}) collective-permute-start(bf16[2,256,384]{2,1,0:T(8,128)(2,1)} %get-tuple-element.27), channel_id=1, source_target_pairs={{0,4},{4,8},{8,12},{1,5},{5,9},{9,13},{2,6},{6,10},{10,14},{3,7},{... | collective-permute-start | bytes 1179656 | tf_op jit(solution)/shard_map/ppermute | solution.py:12
  16.8 1.3 %collective-permute-start.1 = (bf16[2,256,384]{2,1,0:T(8,128)(2,1)}, bf16[2,256,384]{2,1,0:T(8,128)(2,1)S(1)}, u32[]{:S(2)}, u32[]{:S(2)}) collective-permute-start(bf16[2,256,384]{2,1,0:T(8,128)(2,1)} %get-tuple-element.28), channel_id=1, source_target_pairs={{4,0},{8,4},{12,8},{5,1},{9,5},{13,9},{6,2},{10,6},{14,10},{7,3},{... | collective-permute-start | bytes 1179656 | tf_op jit(solution)/shard_map/ppermute | solution.py:12
  18.2 1.0 pad_maximum_fusion.1
  19.5 5.6 %collective-permute-done = bf16[2,256,384]{2,1,0:T(8,128)(2,1)S(1)} collective-permute-done((bf16[2,256,384]{2,1,0:T(8,128)(2,1)}, bf16[2,256,384]{2,1,0:T(8,128)(2,1)S(1)}, u32[]{:S(2)}, u32[]{:S(2)}) %collective-permute-start) | collective-permute-done | bytes 393248 | tf_op jit(solution)/shard_map/ppermute | solution.py:12
  25.1 4.0 %collective-permute-done.1 = bf16[2,256,384]{2,1,0:T(8,128)(2,1)S(1)} collective-permute-done((bf16[2,256,384]{2,1,0:T(8,128)(2,1)}, bf16[2,256,384]{2,1,0:T(8,128)(2,1)S(1)}, u32[]{:S(2)}, u32[]{:S(2)}) %collective-permute-start.1) | collective-permute-done | bytes 393248 | tf_op jit(solution)/shard_map/ppermute | solution.py:12
  29.3 0.6 collective-permute-start.2
  29.9 1.7 %collective-permute-start.5 = (bf16[2,256,384]{2,1,0:T(8,128)(2,1)S(1)}, bf16[2,256,384]{2,1,0:T(8,128)(2,1)S(1)}, u32[]{:S(2)}, u32[]{:S(2)}) collective-permute-start(bf16[2,256,384]{2,1,0:T(8,128)(2,1)S(1)} %pad_maximum_fusion.16), channel_id=1, source_target_pairs={{0,2},{2,0},{1,3},{3,1},{4,6},{6,4},{5,7},{7,5},{8,10},{10,8},{9,1... | collective-permute-start | bytes 1179656 | tf_op jit(solution)/shard_map/ppermute | solution.py:125
  31.6 1.0 broadcast_select_fusion
  32.9 1.4 %fusion.96 = f32[384,384]{1,0:T(8,128)S(1)} fusion(bf16[512,384]{1,0:T(8,128)(2,1)} %collective-permute-done.6, bf16[512,384]{1,0:T(8,128)(2,1)S(1)} %broadcast_select_fusion), kind=kOutput, calls=%fused_computation.167 | convolution fusion | flops 150994944 | bytes 1376256 | tf_op jit(solution)/shard_map/dot_general | solution.py:132
  34.3 0.8 convolution_bitcast_fusion.3
  35.1 5.9 %collective-permute-done.5 = bf16[2,256,384]{2,1,0:T(8,128)(2,1)S(1)} collective-permute-done((bf16[2,256,384]{2,1,0:T(8,128)(2,1)S(1)}, bf16[2,256,384]{2,1,0:T(8,128)(2,1)S(1)}, u32[]{:S(2)}, u32[]{:S(2)}) %collective-permute-start.5) | collective-permute-done | bytes 393248 | tf_op jit(solution)/shard_map/ppermute | solution.py:125
  41.1 1.3 %fusion.48 = f32[384,384]{1,0:T(8,128)S(1)} fusion(bf16[512,384]{1,0:T(8,128)(2,1)S(1)} %broadcast_select_fusion, bf16[256,384]{1,0:T(8,128)(2,1)S(1)} %get-tuple-element.32, bf16[512,384]{1,0:T(8,128)(2,1)} %collective-permute-done.6), kind=kOutput, calls=%fused_computation.78 | convolution fusion | flops 151781376 | bytes 1572864 | tf_op jit(solution)/shard_map/dot_general | solution.py:132
  42.4 1.3 %fusion.50 = f32[384,384]{1,0:T(8,128)S(1)} fusion(bf16[512,384]{1,0:T(8,128)(2,1)S(1)} %broadcast_select_fusion, bf16[512,384]{1,0:T(8,128)(2,1)} %collective-permute-done.6, bf16[256,384]{1,0:T(8,128)(2,1)S(1)} %get-tuple-element.33), kind=kOutput, calls=%fused_computation.81 | convolution fusion | flops 151781376 | bytes 1572864 | tf_op jit(solution)/shard_map/dot_general | solution.py:132
  43.8 0.3 broadcast_select_fusion.1
  44.2 0.4 convolution_add_fusion
  44.6 1.6 %collective-permute-start.15 = (f32[1,96,384]{2,1,0:T(8,128)S(1)}, f32[1,96,384]{2,1,0:T(8,128)S(1)}, u32[]{:S(2)}, u32[]{:S(2)}) collective-permute-start(f32[1,96,384]{2,1,0:T(8,128)S(1)} %get-tuple-element.29), channel_id=1, source_target_pairs={{0,4},{4,8},{8,12},{12,0},{1,5},{5,9},{9,13},{13,1},{2,6},{6,10},{... | collective-permute-start | bytes 442376 | tf_op jit(solution)/shard_map/ppermute | solution.py:58
  46.2 1.1 collective-permute-start.16
  47.3 2.8 %collective-permute-start.17 = (f32[1,96,384]{2,1,0:T(8,128)S(1)}, f32[1,96,384]{2,1,0:T(8,128)S(1)}, u32[]{:S(2)}, u32[]{:S(2)}) collective-permute-start(f32[1,96,384]{2,1,0:T(8,128)S(1)} %get-tuple-element.30), channel_id=1, source_target_pairs={{0,12},{4,0},{8,4},{12,8},{1,13},{5,1},{9,5},{13,9},{2,14},{6,2},{... | collective-permute-start | bytes 442376 | tf_op jit(solution)/shard_map/ppermute | solution.py:58
  50.2 0.4 convolution_add_fusion.1
  50.6 0.4 convolution_add_fusion.2
  51.0 0.8 copy-done.2
  51.8 0.9 fusion.70
  52.8 0.4 collective-permute-start.10
  53.1 0.8 convolution_bitcast_fusion
  53.9 1.2 %collective-permute-start.11 = (f32[2,96,384]{2,1,0:T(8,128)}, f32[2,96,384]{2,1,0:T(8,128)}, u32[]{:S(2)}, u32[]{:S(2)}) collective-permute-start(f32[2,96,384]{2,1,0:T(8,128)} %get-tuple-element.7), channel_id=1, source_target_pairs={{0,12},{4,0},{8,4},{12,8},{1,13},{5,1},{9,5},{13,9},{2,14},{6,2},{... | collective-permute-start | bytes 884744 | tf_op jit(solution)/shard_map/ppermute | solution.py:58
  55.2 7.3 %collective-permute-done.16 = f32[1,96,384]{2,1,0:T(8,128)S(1)} collective-permute-done((f32[1,96,384]{2,1,0:T(8,128)S(1)}, f32[1,96,384]{2,1,0:T(8,128)S(1)}, u32[]{:S(2)}, u32[]{:S(2)}) %collective-permute-start.16) | collective-permute-done | bytes 147488 | tf_op jit(solution)/shard_map/ppermute | solution.py:58
  62.5 11.5 %collective-permute-start.9 = (f32[2,96,384]{2,1,0:T(8,128)}, f32[2,96,384]{2,1,0:T(8,128)}, u32[]{:S(2)}, u32[]{:S(2)}) collective-permute-start(f32[2,96,384]{2,1,0:T(8,128)} %get-tuple-element.5), channel_id=1, source_target_pairs={{0,4},{4,8},{8,12},{12,0},{1,5},{5,9},{9,13},{13,1},{2,6},{6,10},{... | collective-permute-start | bytes 884744 | tf_op jit(solution)/shard_map/ppermute | solution.py:58
  74.1 1.3 %fusion.39 = bf16[512,384]{1,0:T(8,128)(2,1)S(1)} fusion(f32[512,384]{1,0:T(8,128)S(1)} %copy-done.9, f32[512,384]{1,0:T(8,128)S(1)} %convolution_bitcast_fusion, bf16[512,1,384]{2,0,1:T(8,128)(2,1)S(1)} %get-tuple-element.24, bf16[512,1,384]{2,0,1:T(8,128)(2,1)S(1)} %bitcast.145, bf16[512,1,384]{2,0,1:T(8,128)(2,1)S(1)} %get-tuple-element.8, ...), kind=kOutput, calls=%fused_computation.66 | convolution fusion | flops 458883072 | bytes 4423684 | tf_op jit(solution)/shard_map/tko,kio->ti/dot_general | solution.py:103
  75.4 3.5 %collective-permute-start.19 = (bf16[1,96,384]{2,1,0:T(8,128)(2,1)S(1)}, bf16[1,96,384]{2,1,0:T(8,128)(2,1)}, u32[]{:S(2)}, u32[]{:S(2)}) collective-permute-start(bf16[1,96,384]{2,1,0:T(8,128)(2,1)S(1)} %fusion.76), channel_id=1, source_target_pairs={{0,8},{4,12},{8,0},{12,4},{1,9},{5,13},{9,1},{13,5},{2,10},{6,14},... | collective-permute-start | bytes 221192 | tf_op jit(solution)/shard_map/ppermute | solution.py:61
  78.9 7.8 %collective-permute-done.18 = bf16[1,96,384]{2,1,0:T(8,128)(2,1)S(1)} collective-permute-done((bf16[1,96,384]{2,1,0:T(8,128)(2,1)S(1)}, bf16[1,96,384]{2,1,0:T(8,128)(2,1)S(1)}, u32[]{:S(2)}, u32[]{:S(2)}) %collective-permute-start.18) | collective-permute-done | bytes 73760 | tf_op jit(solution)/shard_map/ppermute | solution.py:61
  86.7 2.7 %collective-permute-start.20 = (bf16[1,96,384]{2,1,0:T(8,128)(2,1)S(1)}, bf16[1,96,384]{2,1,0:T(8,128)(2,1)}, u32[]{:S(2)}, u32[]{:S(2)}) collective-permute-start(bf16[1,96,384]{2,1,0:T(8,128)(2,1)S(1)} %fusion.76), channel_id=1, source_target_pairs={{0,12},{4,0},{8,4},{12,8},{1,13},{5,1},{9,5},{13,9},{2,14},{6,2},{... | collective-permute-start | bytes 221192 | tf_op jit(solution)/shard_map/ppermute | solution.py:61
  89.5 1.6 %fusion.4 = bf16[1,512,384]{2,1,0:T(8,128)(2,1)} fusion(f32[512,384]{1,0:T(8,128)S(1)} %copy-done.9, f32[512,384]{1,0:T(8,128)S(1)} %convolution_bitcast_fusion.3, bf16[3,384,384]{2,1,0:T(8,128)(2,1)S(1)} %collective-permute-done.4, bf16[512,1,384]{2,0,1:T(8,128)(2,1)S(1)} %get-tuple-element.18, bf16[512,1,384]{2,0,1:T(8,128)(2,1)S(1)} %get-tuple-element.20, ...), kind=kOutput, calls=%fused_computation.24 | convolution fusion | flops 454754304 | bytes 4030464 | tf_op jit(solution)/shard_map/tki,kio->to/dot_general | solution.py:97
  91.0 1.3 %broadcast_in_dim.42 = bf16[512,2,384]{2,1,0:T(2,128)(2,1)} broadcast(bf16[512,384]{1,0:T(8,128)(2,1)S(1)} %fusion.39), dimensions={0,2} | broadcast | bytes 1179648 | tf_op jit(solution)/shard_map/broadcast_in_dim | solution.py:112
  92.3 3.0 %convert_element_type.51 = bf16[1,1024,384]{2,1,0:T(8,128)(2,1)} reshape(bf16[512,2,384]{2,1,0:T(2,128)(2,1)} %broadcast_in_dim.42) | data formatting | bytes 1572864 | tf_op jit(solution)/shard_map/convert_element_type | solution.py:112
  95.3 1.0 maximum_bitcast_fusion.2
  96.3 0.6 gather_fusion.1
  97.0 1.2 %fusion.68 = bf16[2,96,384]{2,1,0:T(8,128)(2,1)S(1)} fusion(f32[2,96,384]{2,1,0:T(8,128)} %collective-permute-done.11, f32[2,96,384]{2,1,0:T(8,128)} %collective-permute-done.10, f32[2,96,384]{2,1,0:T(8,128)} %collective-permute-done.9, s32[]{:T(128)S(6)} %select_n.140, f32[1,4,96,384]{3,2,1,0:T(8,128)S(1)} %bitcast.155, f32[1,4,96,384]{3,2,1,0:T(8,128)S(1)} %bitcast.153), kind=kLoop, calls=%fused_computation.116 | loop fusion | flops 368640 | bytes 2211844 | tf_op jit(solution)/shard_map/convert_element_type | solution.py:59
  98.2 3.5 %collective-permute-start.13 = (bf16[2,96,384]{2,1,0:T(8,128)(2,1)S(1)}, bf16[2,96,384]{2,1,0:T(8,128)(2,1)S(1)}, u32[]{:S(2)}, u32[]{:S(2)}) collective-permute-start(bf16[2,96,384]{2,1,0:T(8,128)(2,1)S(1)} %fusion.68), channel_id=1, source_target_pairs={{0,8},{4,12},{8,0},{12,4},{1,9},{5,13},{9,1},{13,5},{2,10},{6,14},... | collective-permute-start | bytes 442376 | tf_op jit(solution)/shard_map/ppermute | solution.py:61
  101.8 0.9 collective-permute-start.14
  102.8 4.0 %collective-permute-done.12 = bf16[2,96,384]{2,1,0:T(8,128)(2,1)S(1)} collective-permute-done((bf16[2,96,384]{2,1,0:T(8,128)(2,1)S(1)}, bf16[2,96,384]{2,1,0:T(8,128)(2,1)S(1)}, u32[]{:S(2)}, u32[]{:S(2)}) %collective-permute-start.12) | collective-permute-done | bytes 147488 | tf_op jit(solution)/shard_map/ppermute | solution.py:61
  106.8 4.8 %collective-permute-done.13 = bf16[2,96,384]{2,1,0:T(8,128)(2,1)S(1)} collective-permute-done((bf16[2,96,384]{2,1,0:T(8,128)(2,1)S(1)}, bf16[2,96,384]{2,1,0:T(8,128)(2,1)S(1)}, u32[]{:S(2)}, u32[]{:S(2)}) %collective-permute-start.13) | collective-permute-done | bytes 147488 | tf_op jit(solution)/shard_map/ppermute | solution.py:61
  111.7 0.7 gather_fusion
  112.7 1.4 %pad_maximum_fusion = f32[3,384,384]{2,1,0:T(8,128)} fusion(f32[1,384,384]{2,1,0:T(8,128)S(1)} %get-tuple-element.4, f32[1,384,384]{2,1,0:T(8,128)S(1)} %fusion.73, f32[1,384,384]{2,1,0:T(8,128)S(1)} %get-tuple-element.3), kind=kLoop, calls=%fused_computation.12 | loop fusion | flops 884736 | bytes 3538944 | tf_op jit(solution)/shard_map/concatenate | solution.py:136
  (59 shorter events, 1.6 us)
Async XLA Ops:
  0.6 18.7 %copy-start = (bf16[3,384,768]{2,1,0:T(8,128)(2,1)S(1)}, bf16[3,384,768]{2,1,0:T(8,128)(2,1)}, u32[]{:S(2)}) copy-start(bf16[3,384,768]{2,1,0:T(8,128)(2,1)} %param.4) | copy-start | bytes 5308420
  0.6 28.7 %collective-permute-start.7 = (bf16[512,384]{1,0:T(8,128)(2,1)}, bf16[512,384]{1,0:T(8,128)(2,1)}, u32[]{:S(2)}, u32[]{:S(2)}) collective-permute-start(bf16[512,384]{1,0:T(8,128)(2,1)} %bitcast.143), channel_id=1, source_target_pairs={{2,0},{1,3},{6,4},{5,7},{10,8},{9,11},{14,12},{13,15},{18,16},{17,... | collective-permute-start | bytes 1179656 | tf_op jit(solution)/shard_map/ppermute | solution.py:121
  2.1 27.8 %collective-permute-start.8 = (bf16[512,384]{1,0:T(8,128)(2,1)}, bf16[512,384]{1,0:T(8,128)(2,1)}, u32[]{:S(2)}, u32[]{:S(2)}) collective-permute-start(bf16[512,384]{1,0:T(8,128)(2,1)} %bitcast.144), channel_id=1, source_target_pairs={{2,1},{1,2},{6,5},{5,6},{10,9},{9,10},{14,13},{13,14},{18,17},{17,... | collective-permute-start | bytes 1179656 | tf_op jit(solution)/shard_map/ppermute | solution.py:122
  3.5 8.8 %copy-start.1 = (bf16[1,512,384]{2,1,0:T(8,128)(2,1)S(1)}, bf16[1,512,384]{2,1,0:T(8,128)(2,1)}, u32[]{:S(2)}) copy-start(bf16[1,512,384]{2,1,0:T(8,128)(2,1)} %param.5) | copy-start | bytes 1179652
  6.3 26.5 %collective-permute-start.6 = (bf16[512,384]{1,0:T(8,128)(2,1)S(1)}, bf16[512,384]{1,0:T(8,128)(2,1)}, u32[]{:S(2)}, u32[]{:S(2)}) collective-permute-start(bf16[512,384]{1,0:T(8,128)(2,1)S(1)} %get-tuple-element.34), channel_id=1, source_target_pairs={{0,2},{2,0},{1,3},{3,1},{4,6},{6,4},{5,7},{7,5},{8,10},{10,8},{9,1... | collective-permute-start | bytes 1179656 | tf_op jit(solution)/shard_map/ppermute | solution.py:124
  13.3 11.8 %collective-permute-start = (bf16[2,256,384]{2,1,0:T(8,128)(2,1)}, bf16[2,256,384]{2,1,0:T(8,128)(2,1)S(1)}, u32[]{:S(2)}, u32[]{:S(2)}) collective-permute-start(bf16[2,256,384]{2,1,0:T(8,128)(2,1)} %get-tuple-element.27), channel_id=1, source_target_pairs={{0,4},{4,8},{8,12},{1,5},{5,9},{9,13},{2,6},{6,10},{10,14},{3,7},{... | collective-permute-start | bytes 1179656 | tf_op jit(solution)/shard_map/ppermute | solution.py:12
  16.8 12.3 %collective-permute-start.1 = (bf16[2,256,384]{2,1,0:T(8,128)(2,1)}, bf16[2,256,384]{2,1,0:T(8,128)(2,1)S(1)}, u32[]{:S(2)}, u32[]{:S(2)}) collective-permute-start(bf16[2,256,384]{2,1,0:T(8,128)(2,1)} %get-tuple-element.28), channel_id=1, source_target_pairs={{4,0},{8,4},{12,8},{5,1},{9,5},{13,9},{6,2},{10,6},{14,10},{7,3},{... | collective-permute-start | bytes 1179656 | tf_op jit(solution)/shard_map/ppermute | solution.py:12
  19.4 5.7 %copy-start.6 = (bf16[2,512,384]{2,1,0:T(8,128)(2,1)S(1)}, bf16[2,512,384]{2,1,0:T(8,128)(2,1)}, u32[]{:S(2)}) copy-start(bf16[2,512,384]{2,1,0:T(8,128)(2,1)} %pad_maximum_fusion.1) | copy-start | bytes 2359300
  25.1 18.7 %collective-permute-start.3 = (bf16[2,512,384]{2,1,0:T(8,128)(2,1)S(1)}, bf16[2,512,384]{2,1,0:T(8,128)(2,1)S(1)}, u32[]{:S(2)}, u32[]{:S(2)}) collective-permute-start(bf16[2,512,384]{2,1,0:T(8,128)(2,1)S(1)} %copy-done.6), channel_id=1, source_target_pairs={{0,1},{1,0},{2,3},{3,2},{4,5},{5,4},{6,7},{7,6},{8,9},{9,8},{10,11... | collective-permute-start | bytes 2359304 | tf_op jit(solution)/shard_map/ppermute | solution.py:83
  29.1 3.6 %copy-start.4 = (bf16[2,256,384]{2,1,0:T(8,128)(2,1)}, bf16[2,256,384]{2,1,0:T(8,128)(2,1)S(1)}, u32[]{:S(2)}) copy-start(bf16[2,256,384]{2,1,0:T(8,128)(2,1)S(1)} %collective-permute-done.1) | copy-start | bytes 1179652
  29.1 46.3 %collective-permute-start.4 = (bf16[3,384,384]{2,1,0:T(8,128)(2,1)S(1)}, bf16[3,384,384]{2,1,0:T(8,128)(2,1)S(1)}, u32[]{:S(2)}, u32[]{:S(2)}) collective-permute-start(bf16[3,384,384]{2,1,0:T(8,128)(2,1)S(1)} %constant_dynamic-slice_fusion), channel_id=1, source_target_pairs={{0,1},{1,0},{2,3},{3,2},{4,5},{5,4},{6,7},{7,6},{8,9},{9,8},{10,11... | collective-permute-start | bytes 2654216 | tf_op jit(solution)/shard_map/ppermute | solution.py:92
  29.3 14.4 %collective-permute-start.2 = (bf16[2,2,256,384]{3,2,1,0:T(8,128)(2,1)S(1)}, bf16[2,2,256,384]{3,2,1,0:T(8,128)(2,1)S(1)}, u32[]{:S(2)}, u32[]{:S(2)}) collective-permute-start(bf16[2,2,256,384]{3,2,1,0:T(8,128)(2,1)S(1)} %pad_maximum_fusion.2), channel_id=1, source_target_pairs={{0,1},{1,0},{2,3},{3,2},{4,5},{5,4},{6,7},{7,6},{8,9},{9,8},{10,11... | collective-permute-start | bytes 2359304 | tf_op jit(solution)/shard_map/ppermute | solution.py:86
  29.9 11.1 %collective-permute-start.5 = (bf16[2,256,384]{2,1,0:T(8,128)(2,1)S(1)}, bf16[2,256,384]{2,1,0:T(8,128)(2,1)S(1)}, u32[]{:S(2)}, u32[]{:S(2)}) collective-permute-start(bf16[2,256,384]{2,1,0:T(8,128)(2,1)S(1)} %pad_maximum_fusion.16), channel_id=1, source_target_pairs={{0,2},{2,0},{1,3},{3,1},{4,6},{6,4},{5,7},{7,5},{8,10},{10,8},{9,1... | collective-permute-start | bytes 1179656 | tf_op jit(solution)/shard_map/ppermute | solution.py:125
  44.1 6.0 %copy-start.5 = (bf16[2,256,384]{2,1,0:T(8,128)(2,1)S(1)}, bf16[2,256,384]{2,1,0:T(8,128)(2,1)}, u32[]{:S(2)}) copy-start(bf16[2,256,384]{2,1,0:T(8,128)(2,1)} %copy-done.4) | copy-start | bytes 1179652
  44.6 9.3 %collective-permute-start.15 = (f32[1,96,384]{2,1,0:T(8,128)S(1)}, f32[1,96,384]{2,1,0:T(8,128)S(1)}, u32[]{:S(2)}, u32[]{:S(2)}) collective-permute-start(f32[1,96,384]{2,1,0:T(8,128)S(1)} %get-tuple-element.29), channel_id=1, source_target_pairs={{0,4},{4,8},{8,12},{12,0},{1,5},{5,9},{9,13},{13,1},{2,6},{6,10},{... | collective-permute-start | bytes 442376 | tf_op jit(solution)/shard_map/ppermute | solution.py:58
  46.2 16.3 %collective-permute-start.16 = (f32[1,96,384]{2,1,0:T(8,128)S(1)}, f32[1,96,384]{2,1,0:T(8,128)S(1)}, u32[]{:S(2)}, u32[]{:S(2)}) collective-permute-start(f32[1,96,384]{2,1,0:T(8,128)S(1)} %get-tuple-element.31), channel_id=1, source_target_pairs={{0,8},{4,12},{8,0},{12,4},{1,9},{5,13},{9,1},{13,5},{2,10},{6,14},... | collective-permute-start | bytes 442376 | tf_op jit(solution)/shard_map/ppermute | solution.py:58
  47.3 26.7 %collective-permute-start.17 = (f32[1,96,384]{2,1,0:T(8,128)S(1)}, f32[1,96,384]{2,1,0:T(8,128)S(1)}, u32[]{:S(2)}, u32[]{:S(2)}) collective-permute-start(f32[1,96,384]{2,1,0:T(8,128)S(1)} %get-tuple-element.30), channel_id=1, source_target_pairs={{0,12},{4,0},{8,4},{12,8},{1,13},{5,1},{9,5},{13,9},{2,14},{6,2},{... | collective-permute-start | bytes 442376 | tf_op jit(solution)/shard_map/ppermute | solution.py:58
  51.0 0.8 copy-start.2
  52.8 44.2 %collective-permute-start.10 = (f32[2,96,384]{2,1,0:T(8,128)}, f32[2,96,384]{2,1,0:T(8,128)}, u32[]{:S(2)}, u32[]{:S(2)}) collective-permute-start(f32[2,96,384]{2,1,0:T(8,128)} %get-tuple-element.6), channel_id=1, source_target_pairs={{0,8},{4,12},{8,0},{12,4},{1,9},{5,13},{9,1},{13,5},{2,10},{6,14},... | collective-permute-start | bytes 884744 | tf_op jit(solution)/shard_map/ppermute | solution.py:58
  53.1 21.0 %copy-start.9 = (f32[512,384]{1,0:T(8,128)S(1)}, f32[512,384]{1,0:T(8,128)}, u32[]{:S(2)}) copy-start(f32[512,384]{1,0:T(8,128)} %get-tuple-element.35) | copy-start | bytes 2359300
  53.9 43.0 %collective-permute-start.11 = (f32[2,96,384]{2,1,0:T(8,128)}, f32[2,96,384]{2,1,0:T(8,128)}, u32[]{:S(2)}, u32[]{:S(2)}) collective-permute-start(f32[2,96,384]{2,1,0:T(8,128)} %get-tuple-element.7), channel_id=1, source_target_pairs={{0,12},{4,0},{8,4},{12,8},{1,13},{5,1},{9,5},{13,9},{2,14},{6,2},{... | collective-permute-start | bytes 884744 | tf_op jit(solution)/shard_map/ppermute | solution.py:58
  62.5 34.5 %collective-permute-start.9 = (f32[2,96,384]{2,1,0:T(8,128)}, f32[2,96,384]{2,1,0:T(8,128)}, u32[]{:S(2)}, u32[]{:S(2)}) collective-permute-start(f32[2,96,384]{2,1,0:T(8,128)} %get-tuple-element.5), channel_id=1, source_target_pairs={{0,4},{4,8},{8,12},{12,0},{1,5},{5,9},{9,13},{13,1},{2,6},{6,10},{... | collective-permute-start | bytes 884744 | tf_op jit(solution)/shard_map/ppermute | solution.py:58
  74.0 12.7 %collective-permute-start.18 = (bf16[1,96,384]{2,1,0:T(8,128)(2,1)S(1)}, bf16[1,96,384]{2,1,0:T(8,128)(2,1)S(1)}, u32[]{:S(2)}, u32[]{:S(2)}) collective-permute-start(bf16[1,96,384]{2,1,0:T(8,128)(2,1)S(1)} %fusion.76), channel_id=1, source_target_pairs={{0,4},{4,8},{8,12},{12,0},{1,5},{5,9},{9,13},{13,1},{2,6},{6,10},{... | collective-permute-start | bytes 221192 | tf_op jit(solution)/shard_map/ppermute | solution.py:61
  75.4 19.9 %collective-permute-start.19 = (bf16[1,96,384]{2,1,0:T(8,128)(2,1)S(1)}, bf16[1,96,384]{2,1,0:T(8,128)(2,1)}, u32[]{:S(2)}, u32[]{:S(2)}) collective-permute-start(bf16[1,96,384]{2,1,0:T(8,128)(2,1)S(1)} %fusion.76), channel_id=1, source_target_pairs={{0,8},{4,12},{8,0},{12,4},{1,9},{5,13},{9,1},{13,5},{2,10},{6,14},... | collective-permute-start | bytes 221192 | tf_op jit(solution)/shard_map/ppermute | solution.py:61
  86.7 4.3 %copy-start.7 = (bf16[1,96,384]{2,1,0:T(8,128)(2,1)}, bf16[1,96,384]{2,1,0:T(8,128)(2,1)S(1)}, u32[]{:S(2)}) copy-start(bf16[1,96,384]{2,1,0:T(8,128)(2,1)S(1)} %collective-permute-done.18) | copy-start | bytes 221188
  86.7 8.6 %collective-permute-start.20 = (bf16[1,96,384]{2,1,0:T(8,128)(2,1)S(1)}, bf16[1,96,384]{2,1,0:T(8,128)(2,1)}, u32[]{:S(2)}, u32[]{:S(2)}) collective-permute-start(bf16[1,96,384]{2,1,0:T(8,128)(2,1)S(1)} %fusion.76), channel_id=1, source_target_pairs={{0,12},{4,0},{8,4},{12,8},{1,13},{5,1},{9,5},{13,9},{2,14},{6,2},{... | collective-permute-start | bytes 221192 | tf_op jit(solution)/shard_map/ppermute | solution.py:61
  92.3 3.0 %copy-start.8 = (bf16[1,96,384]{2,1,0:T(8,128)(2,1)S(1)}, bf16[1,96,384]{2,1,0:T(8,128)(2,1)}, u32[]{:S(2)}) copy-start(bf16[1,96,384]{2,1,0:T(8,128)(2,1)} %copy-done.7) | copy-start | bytes 221188
  92.3 4.7 %copy-start.3 = (f32[384,384]{1,0:T(8,128)S(1)}, f32[384,384]{1,0:T(8,128)}, u32[]{:S(2)}) copy-start(f32[384,384]{1,0:T(8,128)} %copy-done.2) | copy-start | bytes 1769476
  98.2 8.6 %collective-permute-start.12 = (bf16[2,96,384]{2,1,0:T(8,128)(2,1)S(1)}, bf16[2,96,384]{2,1,0:T(8,128)(2,1)S(1)}, u32[]{:S(2)}, u32[]{:S(2)}) collective-permute-start(bf16[2,96,384]{2,1,0:T(8,128)(2,1)S(1)} %fusion.68), channel_id=1, source_target_pairs={{0,4},{4,8},{8,12},{12,0},{1,5},{5,9},{9,13},{13,1},{2,6},{6,10},{... | collective-permute-start | bytes 442376 | tf_op jit(solution)/shard_map/ppermute | solution.py:61
  98.2 13.3 %collective-permute-start.13 = (bf16[2,96,384]{2,1,0:T(8,128)(2,1)S(1)}, bf16[2,96,384]{2,1,0:T(8,128)(2,1)S(1)}, u32[]{:S(2)}, u32[]{:S(2)}) collective-permute-start(bf16[2,96,384]{2,1,0:T(8,128)(2,1)S(1)} %fusion.68), channel_id=1, source_target_pairs={{0,8},{4,12},{8,0},{12,4},{1,9},{5,13},{9,1},{13,5},{2,10},{6,14},... | collective-permute-start | bytes 442376 | tf_op jit(solution)/shard_map/ppermute | solution.py:61
  101.8 9.8 %collective-permute-start.14 = (bf16[2,96,384]{2,1,0:T(8,128)(2,1)S(1)}, bf16[2,96,384]{2,1,0:T(8,128)(2,1)S(1)}, u32[]{:S(2)}, u32[]{:S(2)}) collective-permute-start(bf16[2,96,384]{2,1,0:T(8,128)(2,1)S(1)} %fusion.68), channel_id=1, source_target_pairs={{0,12},{4,0},{8,4},{12,8},{1,13},{5,1},{9,5},{13,9},{2,14},{6,2},{... | collective-permute-start | bytes 442376 | tf_op jit(solution)/shard_map/ppermute | solution.py:61

commit v7 on v6

--- a/solution.py
+++ b/solution.py
@@ -63,6 +63,28 @@
     stacked = jnp.stack(gathered, 1)
     order = (s - jnp.arange(count)) % count
     return jnp.take(stacked, order, axis=1).reshape(block.shape).astype(jnp.float32)
+
+
+def line_total(block):
+    s = lax.axis_index("seq")
+    odd = (s % 2) == 1
+    low = s < 2
+    rows = block.shape[0] // 4
+    quarters = block.reshape(2, 2, rows, block.shape[1])
+    even_set, odd_set = quarters[:, 0], quarters[:, 1]
+    pairs, across = [(0, 1), (1, 0), (2, 3), (3, 2)], [(0, 2), (2, 0), (1, 3), (3, 1)]
+    pair = jnp.where(odd, odd_set, even_set) + lax.ppermute(
+        jnp.where(odd, even_set, odd_set), "seq", pairs
+    )
+    keep = jnp.where(low, pair[0], pair[1])
+    give = jnp.where(low, pair[1], pair[0])
+    total = (keep + lax.ppermute(give, "seq", across)).astype(jnp.bfloat16)
+    other = lax.ppermute(total, "seq", across)
+    own_set = jnp.where(low, jnp.stack([total, other]), jnp.stack([other, total]))
+    far_set = lax.ppermute(own_set, "seq", pairs)
+    evens = jnp.where(odd, far_set, own_set)
+    odds = jnp.where(odd, own_set, far_set)
+    return jnp.stack([evens, odds], 1).reshape(block.shape).astype(jnp.float32)
 
 
 def shards(seq_in, conv_weight, cotangent):
@@ -131,9 +153,9 @@
                 own_taps[:, k].T, cot_mine, preferred_element_type=jnp.float32
             ) + jnp.dot(far_taps[:, k].T, far_cot, preferred_element_type=jnp.float32)
         if seq_count == 4:
-            middle = seq_total(grads[1][None])
-            sides = seq_total(jnp.stack([grads[0], grads[2]]))
-            weight_grad = jnp.concatenate([sides[:1], middle, sides[1:]], 0)
+            middle = line_total(grads[1])
+            sides = line_total(jnp.concatenate([grads[0], grads[2]], 0))
+            weight_grad = jnp.stack([sides[: middle.shape[0]], middle, sides[middle.shape[0] :]])
         else:
             weight_grad = lax.psum(jnp.stack([grads[0], grads[1], grads[2]]), "seq")
     else:

time: 114 us -> 107 us (0.939); the launches traced: 114 us -> 106 us
  starting transfers between devices: 45.3 us -> 28.1 us
  waiting for transfers between devices: 39.5 us -> 55.3 us
  local copies, waits for them, and re-layouts: 7.06 us -> 3 us
  other arithmetic: 8.54 us -> 5.72 us
    ppermute x12 -> x8, starting transfers between devices: 29.3 us -> 8.74 us  [the longest x2 3.54 us: line_total(): other = lax.ppermute(total, 'seq', across)]
    ppermute x12 -> x8, waiting for transfers between devices: 23.9 us -> 43.5 us  [the longest x2 13.6 us: line_total(): total = (keep + lax.ppermute(give, 'seq', across)).astype(jnp.bfloat16)]
    ppermute x2, waiting for transfers between devices: 9.64 us -> 2.2 us  [shift_from(): return lax.ppermute(block, axis, route)]
    ppermute x1, waiting for transfers between devices: 0.01 us -> 5.24 us  [shards(): far_mid = lax.ppermute(activation, 'batch', SWAP)]
    ppermute x1, starting transfers between devices: 1.74 us -> 5.5 us  [shards(): lax.ppermute(jnp.stack([from_prev[0], from_next[0]]), 'batch', SWAP)]
    convert_element_type x1, local copies, waits for them, and re-layouts: 3.02 us -> 1.17 us  [shards(): input_grad = jnp.repeat(0.5 * pooled_grad, 2, axis=0).astype(jnp.bfloat16)]
    ppermute x1, starting transfers between devices: 6.01 us -> 4.32 us  [shards(): far_mid = lax.ppermute(activation, 'batch', SWAP)]
    ppermute x1, waiting for transfers between devices: 5.91 us -> 4.42 us  [shards(): lax.ppermute(jnp.stack([from_prev[0], from_next[0]]), 'batch', SWAP)]
  transfers between devices with their start and end apart: 21 -> 17, of which waited for: 7 -> 9; matrix products, arithmetic and copies ran while one was open for 21% -> 14% of each run, Pallas kernels for 0% -> 0%
where the time goes in v7:
time: 107 us; the launch traced here: 106 us
  waiting for transfers between devices  55.3 us (52%)
  starting transfers between devices  28.1 us (26%)
  matrix products  12.7 us (12%)
  other arithmetic  5.72 us (5%)
  local copies, waits for them, and re-layouts  3 us (3%)
    ppermute x2, waiting for transfers between devices, line_total(): total = (keep + lax.ppermute(give, 'seq', across)).astype(jnp.bfloat16)  13.6 us
    ppermute x2, waiting for transfers between devices, line_total(): other = lax.ppermute(total, 'seq', across)  12.8 us
    ppermute x2, waiting for transfers between devices, line_total(): far_set = lax.ppermute(own_set, 'seq', pairs)  8.76 us
    ppermute x2, waiting for transfers between devices, line_total(): lax.ppermute(jnp.where(odd, even_set, odd_set), 'seq', pairs)  8.39 us
    ppermute x2, starting transfers between devices, shift_from(): return lax.ppermute(block, axis, route)  6.26 us
    ppermute x1, starting transfers between devices, shards(): lax.ppermute(jnp.stack([from_prev[0], from_next[0]]), 'batch', SWAP)  5.5 us
    ppermute x1, waiting for transfers between devices, shards(): far_mid = lax.ppermute(activation, 'batch', SWAP)  5.24 us
    ppermute x1, waiting for transfers between devices, shards(): lax.ppermute(jnp.stack([from_prev[0], from_next[0]]), 'batch', SWAP)  4.42 us
  transfers between devices with their start and end apart: 17, of which 9 were waited for; matrix products, arithmetic and copies ran while one was open for 14% of the time, Pallas kernels for 0%

profile of v7, /device:TPU:0, one launch (start us, length us, event | category | flops | bytes accessed | tf_op | source)
XLA Modules:
  0.0 105.8 jit_solution(12362794003083291576)
XLA Ops:
  0.7 2.9 %multiply_convert_fusion = (bf16[512,384]{1,0:T(8,128)(2,1)S(1)}, f32[512,384]{1,0:T(8,128)}) fusion(bf16[1,1024,384]{2,1,0:T(8,128)(2,1)} %param.3, s32[1024]{0:T(1024)S(1)} %get-tuple-element.34, s32[1024]{0:T(1024)S(1)} %get-tuple-element.35, pred[1024]{0:T(1024)(128)(4,1)S(1)} %fusion.68), kind=kOutput, calls=%fused_computation.60 | convolution fusion | flops 406519808 | bytes 1975296 | tf_op jit(solution)/shard_map/dot_general | solution.py:101
  3.6 1.0 fusion.47
  4.6 5.0 %collective-permute-start = (bf16[2,256,384]{2,1,0:T(8,128)(2,1)}, bf16[2,256,384]{2,1,0:T(8,128)(2,1)S(1)}, u32[]{:S(2)}, u32[]{:S(2)}) collective-permute-start(bf16[2,256,384]{2,1,0:T(8,128)(2,1)} %get-tuple-element.24), channel_id=1, source_target_pairs={{0,4},{4,8},{8,12},{1,5},{5,9},{9,13},{2,6},{6,10},{10,14},{3,7},{... | collective-permute-start | bytes 1179656 | tf_op jit(solution)/shard_map/ppermute | solution.py:12
  9.5 1.3 %collective-permute-start.1 = (bf16[2,256,384]{2,1,0:T(8,128)(2,1)}, bf16[2,256,384]{2,1,0:T(8,128)(2,1)S(1)}, u32[]{:S(2)}, u32[]{:S(2)}) collective-permute-start(bf16[2,256,384]{2,1,0:T(8,128)(2,1)} %get-tuple-element.25), channel_id=1, source_target_pairs={{4,0},{8,4},{12,8},{5,1},{9,5},{13,9},{6,2},{10,6},{14,10},{7,3},{... | collective-permute-start | bytes 1179656 | tf_op jit(solution)/shard_map/ppermute | solution.py:12
  10.8 1.3 %collective-permute-start.7 = (bf16[512,384]{1,0:T(8,128)(2,1)S(1)}, bf16[512,384]{1,0:T(8,128)(2,1)}, u32[]{:S(2)}, u32[]{:S(2)}) collective-permute-start(bf16[512,384]{1,0:T(8,128)(2,1)S(1)} %bitcast.147), channel_id=1, source_target_pairs={{2,0},{1,3},{6,4},{5,7},{10,8},{9,11},{14,12},{13,15},{18,16},{17,... | collective-permute-start | bytes 1179656 | tf_op jit(solution)/shard_map/ppermute | solution.py:143
  12.1 1.4 %collective-permute-start.8 = (bf16[512,384]{1,0:T(8,128)(2,1)S(1)}, bf16[512,384]{1,0:T(8,128)(2,1)}, u32[]{:S(2)}, u32[]{:S(2)}) collective-permute-start(bf16[512,384]{1,0:T(8,128)(2,1)S(1)} %bitcast.148), channel_id=1, source_target_pairs={{2,1},{1,2},{6,5},{5,6},{10,9},{9,10},{14,13},{13,14},{18,17},{17,... | collective-permute-start | bytes 1179656 | tf_op jit(solution)/shard_map/ppermute | solution.py:144
  13.6 4.3 %collective-permute-start.6 = (bf16[512,384]{1,0:T(8,128)(2,1)S(1)}, bf16[512,384]{1,0:T(8,128)(2,1)}, u32[]{:S(2)}, u32[]{:S(2)}) collective-permute-start(bf16[512,384]{1,0:T(8,128)(2,1)S(1)} %get-tuple-element.32), channel_id=1, source_target_pairs={{0,2},{2,0},{1,3},{3,1},{4,6},{6,4},{5,7},{7,5},{8,10},{10,8},{9,1... | collective-permute-start | bytes 1179656 | tf_op jit(solution)/shard_map/ppermute | solution.py:146
  17.9 1.0 pad_maximum_fusion.2
  18.9 0.1 constant_dynamic-slice_fusion
  19.0 1.0 copy-done.2
  20.0 2.2 %collective-permute-done.1 = bf16[2,256,384]{2,1,0:T(8,128)(2,1)S(1)} collective-permute-done((bf16[2,256,384]{2,1,0:T(8,128)(2,1)}, bf16[2,256,384]{2,1,0:T(8,128)(2,1)S(1)}, u32[]{:S(2)}, u32[]{:S(2)}) %collective-permute-start.1) | collective-permute-done | bytes 393248 | tf_op jit(solution)/shard_map/ppermute | solution.py:12
  22.3 0.1 pad_maximum_fusion.3
  22.4 0.6 collective-permute-start.2
  23.0 5.5 %collective-permute-start.5 = (bf16[2,256,384]{2,1,0:T(8,128)(2,1)S(1)}, bf16[2,256,384]{2,1,0:T(8,128)(2,1)S(1)}, u32[]{:S(2)}, u32[]{:S(2)}) collective-permute-start(bf16[2,256,384]{2,1,0:T(8,128)(2,1)S(1)} %pad_maximum_fusion.16), channel_id=1, source_target_pairs={{0,2},{2,0},{1,3},{3,1},{4,6},{6,4},{5,7},{7,5},{8,10},{10,8},{9,1... | collective-permute-start | bytes 1179656 | tf_op jit(solution)/shard_map/ppermute | solution.py:147
  28.5 1.0 broadcast_select_fusion
  29.5 0.2 fusion.56
  29.7 5.2 %collective-permute-done.6 = bf16[512,384]{1,0:T(8,128)(2,1)} collective-permute-done((bf16[512,384]{1,0:T(8,128)(2,1)S(1)}, bf16[512,384]{1,0:T(8,128)(2,1)}, u32[]{:S(2)}, u32[]{:S(2)}) %collective-permute-start.6) | collective-permute-done | bytes 393248 | tf_op jit(solution)/shard_map/ppermute | solution.py:146
  35.0 1.4 %fusion.82 = f32[384,384]{1,0:T(8,128)S(1)} fusion(bf16[512,384]{1,0:T(8,128)(2,1)} %collective-permute-done.6, bf16[512,384]{1,0:T(8,128)(2,1)S(1)} %broadcast_select_fusion), kind=kOutput, calls=%fused_computation.142 | convolution fusion | flops 150994944 | bytes 1376256 | tf_op jit(solution)/shard_map/dot_general | solution.py:154
  36.3 0.8 convolution_bitcast_fusion.3
  37.2 4.4 %collective-permute-done.5 = bf16[2,256,384]{2,1,0:T(8,128)(2,1)S(1)} collective-permute-done((bf16[2,256,384]{2,1,0:T(8,128)(2,1)S(1)}, bf16[2,256,384]{2,1,0:T(8,128)(2,1)S(1)}, u32[]{:S(2)}, u32[]{:S(2)}) %collective-permute-start.5) | collective-permute-done | bytes 393248 | tf_op jit(solution)/shard_map/ppermute | solution.py:147
  41.6 1.3 %fusion.51 = f32[384,384]{1,0:T(8,128)S(1)} fusion(bf16[512,384]{1,0:T(8,128)(2,1)S(1)} %broadcast_select_fusion, bf16[512,384]{1,0:T(8,128)(2,1)} %collective-permute-done.6, bf16[256,384]{1,0:T(8,128)(2,1)S(1)} %get-tuple-element.28), kind=kOutput, calls=%fused_computation.74 | convolution fusion | flops 151781376 | bytes 1572864 | tf_op jit(solution)/shard_map/dot_general | solution.py:154
  43.0 1.3 %fusion.49 = f32[384,384]{1,0:T(8,128)S(1)} fusion(bf16[512,384]{1,0:T(8,128)(2,1)S(1)} %broadcast_select_fusion, bf16[256,384]{1,0:T(8,128)(2,1)S(1)} %get-tuple-element.29, bf16[512,384]{1,0:T(8,128)(2,1)} %collective-permute-done.6), kind=kOutput, calls=%fused_computation.71 | convolution fusion | flops 151781376 | bytes 1572864 | tf_op jit(solution)/shard_map/dot_general | solution.py:154
  44.3 0.1 slice_bitcast_fusion.2
  44.4 0.3 broadcast_select_fusion.1
  44.7 0.4 convolution_add_fusion
  45.2 2.7 %collective-permute-start.13 = (f32[2,96,384]{2,1,0:T(8,128)S(1)}, f32[2,96,384]{2,1,0:T(8,128)S(1)}, u32[]{:S(2)}, u32[]{:S(2)}) collective-permute-start(f32[2,96,384]{2,1,0:T(8,128)S(1)} %select_bitcast_fusion.1), channel_id=1, source_target_pairs={{0,4},{4,0},{8,12},{12,8},{1,5},{5,1},{9,13},{13,9},{2,6},{6,2},{1... | collective-permute-start | bytes 884744 | tf_op jit(solution)/shard_map/ppermute | solution.py:76
  47.9 0.4 convolution_add_fusion.2
  48.3 0.4 convolution_add_fusion.1
  48.7 0.1 pad_maximum_fusion.1
  48.9 0.1 collective-permute-start.9
  48.9 8.4 %collective-permute-done.13 = f32[2,96,384]{2,1,0:T(8,128)S(1)} collective-permute-done((f32[2,96,384]{2,1,0:T(8,128)S(1)}, f32[2,96,384]{2,1,0:T(8,128)S(1)}, u32[]{:S(2)}, u32[]{:S(2)}) %collective-permute-start.13) | collective-permute-done | bytes 294944 | tf_op jit(solution)/shard_map/ppermute | solution.py:76
  57.4 2.2 %collective-permute-start.14 = (f32[96,384]{1,0:T(8,128)S(1)}, f32[96,384]{1,0:T(8,128)S(1)}, u32[]{:S(2)}, u32[]{:S(2)}) collective-permute-start(f32[96,384]{1,0:T(8,128)S(1)} %select_bitcast_fusion.7), channel_id=1, source_target_pairs={{0,8},{8,0},{4,12},{12,4},{1,9},{9,1},{5,13},{13,5},{2,10},{10,2},... | collective-permute-start | bytes 442376 | tf_op jit(solution)/shard_map/ppermute | solution.py:81
  59.6 0.8 convolution_bitcast_fusion
  60.4 8.1 %collective-permute-done.14 = f32[96,384]{1,0:T(8,128)S(1)} collective-permute-done((f32[96,384]{1,0:T(8,128)S(1)}, f32[96,384]{1,0:T(8,128)S(1)}, u32[]{:S(2)}, u32[]{:S(2)}) %collective-permute-start.14) | collective-permute-done | bytes 147488 | tf_op jit(solution)/shard_map/ppermute | solution.py:81
  68.6 3.5 %collective-permute-start.15 = (bf16[96,384]{1,0:T(8,128)(2,1)S(1)}, bf16[96,384]{1,0:T(8,128)(2,1)S(1)}, u32[]{:S(2)}, u32[]{:S(2)}) collective-permute-start(bf16[96,384]{1,0:T(8,128)(2,1)S(1)} %fusion.65), channel_id=1, source_target_pairs={{0,8},{8,0},{4,12},{12,4},{1,9},{9,1},{5,13},{13,5},{2,10},{10,2},... | collective-permute-start | bytes 221192 | tf_op jit(solution)/shard_map/ppermute | solution.py:82
  72.0 0.1 fusion.46
  72.2 0.1 collective-permute-start.10
  72.2 1.3 %fusion.39 = bf16[512,384]{1,0:T(8,128)(2,1)S(1)} fusion(f32[512,384]{1,0:T(8,128)S(1)} %copy-done.3, f32[512,384]{1,0:T(8,128)S(1)} %convolution_bitcast_fusion, bf16[512,1,384]{2,0,1:T(8,128)(2,1)S(1)} %get-tuple-element.21, bf16[512,1,384]{2,0,1:T(8,128)(2,1)S(1)} %bitcast.149, bf16[512,1,384]{2,0,1:T(8,128)(2,1)S(1)} %get-tuple-element.5, ...), kind=kOutput, calls=%fused_computation.57 | convolution fusion | flops 458883072 | bytes 4423684 | tf_op jit(solution)/shard_map/tko,kio->ti/dot_general | solution.py:125
  73.6 8.3 %collective-permute-done.15 = bf16[96,384]{1,0:T(8,128)(2,1)S(1)} collective-permute-done((bf16[96,384]{1,0:T(8,128)(2,1)S(1)}, bf16[96,384]{1,0:T(8,128)(2,1)S(1)}, u32[]{:S(2)}, u32[]{:S(2)}) %collective-permute-start.15) | collective-permute-done | bytes 73760 | tf_op jit(solution)/shard_map/ppermute | solution.py:82
  82.0 5.4 %collective-permute-done.10 = f32[192,384]{1,0:T(8,128)S(1)} collective-permute-done((f32[192,384]{1,0:T(8,128)S(1)}, f32[192,384]{1,0:T(8,128)S(1)}, u32[]{:S(2)}, u32[]{:S(2)}) %collective-permute-start.10) | collective-permute-done | bytes 294944 | tf_op jit(solution)/shard_map/ppermute | solution.py:81
  87.5 1.6 %fusion.4 = bf16[1,512,384]{2,1,0:T(8,128)(2,1)} fusion(f32[512,384]{1,0:T(8,128)S(1)} %copy-done.3, f32[512,384]{1,0:T(8,128)S(1)} %convolution_bitcast_fusion.3, bf16[3,384,384]{2,1,0:T(8,128)(2,1)S(1)} %collective-permute-done.4, bf16[512,1,384]{2,0,1:T(8,128)(2,1)S(1)} %get-tuple-element.15, bf16[512,1,384]{2,0,1:T(8,128)(2,1)S(1)} %get-tuple-element.17, ...), kind=kOutput, calls=%fused_computation.14 | convolution fusion | flops 454754304 | bytes 4030464 | tf_op jit(solution)/shard_map/tki,kio->to/dot_general | solution.py:119
  89.1 0.4 broadcast_in_dim.18
  89.5 1.2 %convert_element_type.54 = bf16[1,1024,384]{2,1,0:T(8,128)(2,1)} reshape(bf16[512,2,384]{2,1,0:T(2,128)(2,1)S(1)} %broadcast_in_dim.18) | data formatting | bytes 1572864 | tf_op jit(solution)/shard_map/convert_element_type | solution.py:134
  90.7 4.5 %collective-permute-done.11 = bf16[192,384]{1,0:T(8,128)(2,1)S(1)} collective-permute-done((bf16[192,384]{1,0:T(8,128)(2,1)S(1)}, bf16[192,384]{1,0:T(8,128)(2,1)S(1)}, u32[]{:S(2)}, u32[]{:S(2)}) %collective-permute-start.11) | collective-permute-done | bytes 147488 | tf_op jit(solution)/shard_map/ppermute | solution.py:82
  95.5 8.8 %collective-permute-done.12 = bf16[2,192,384]{2,1,0:T(8,128)(2,1)S(1)} collective-permute-done((bf16[2,192,384]{2,1,0:T(8,128)(2,1)S(1)}, bf16[2,192,384]{2,1,0:T(8,128)(2,1)S(1)}, u32[]{:S(2)}, u32[]{:S(2)}) %collective-permute-start.12) | collective-permute-done | bytes 294944 | tf_op jit(solution)/shard_map/ppermute | solution.py:84
  104.2 0.1 select_bitcast_fusion.3
  104.3 0.1 maximum_convert_fusion
  104.5 1.3 %pad_maximum_fusion = f32[3,384,384]{2,1,0:T(8,128)} fusion(f32[1,384,384]{2,1,0:T(8,128)S(1)} %bitcast.164, f32[1,384,384]{2,1,0:T(8,128)S(1)} %bitcast.162, f32[1,384,384]{2,1,0:T(8,128)S(1)} %bitcast.163), kind=kLoop, calls=%fused_computation.2 | loop fusion | flops 884736 | bytes 3538944 | tf_op jit(solution)/shard_map/stack | solution.py:158
  (39 shorter events, 1.0 us)
Async XLA Ops:
  0.6 18.2 %copy-start = (bf16[3,384,768]{2,1,0:T(8,128)(2,1)S(1)}, bf16[3,384,768]{2,1,0:T(8,128)(2,1)}, u32[]{:S(2)}) copy-start(bf16[3,384,768]{2,1,0:T(8,128)(2,1)} %param.4) | copy-start | bytes 5308420
  0.7 2.9 %copy-start.1 = (bf16[1,512,384]{2,1,0:T(8,128)(2,1)S(1)}, bf16[1,512,384]{2,1,0:T(8,128)(2,1)}, u32[]{:S(2)}) copy-start(bf16[1,512,384]{2,1,0:T(8,128)(2,1)} %param.5) | copy-start | bytes 1179652
  4.6 14.4 %collective-permute-start = (bf16[2,256,384]{2,1,0:T(8,128)(2,1)}, bf16[2,256,384]{2,1,0:T(8,128)(2,1)S(1)}, u32[]{:S(2)}, u32[]{:S(2)}) collective-permute-start(bf16[2,256,384]{2,1,0:T(8,128)(2,1)} %get-tuple-element.24), channel_id=1, source_target_pairs={{0,4},{4,8},{8,12},{1,5},{5,9},{9,13},{2,6},{6,10},{10,14},{3,7},{... | collective-permute-start | bytes 1179656 | tf_op jit(solution)/shard_map/ppermute | solution.py:12
  9.5 12.7 %collective-permute-start.1 = (bf16[2,256,384]{2,1,0:T(8,128)(2,1)}, bf16[2,256,384]{2,1,0:T(8,128)(2,1)S(1)}, u32[]{:S(2)}, u32[]{:S(2)}) collective-permute-start(bf16[2,256,384]{2,1,0:T(8,128)(2,1)} %get-tuple-element.25), channel_id=1, source_target_pairs={{4,0},{8,4},{12,8},{5,1},{9,5},{13,9},{6,2},{10,6},{14,10},{7,3},{... | collective-permute-start | bytes 1179656 | tf_op jit(solution)/shard_map/ppermute | solution.py:12
  10.8 11.6 %collective-permute-start.7 = (bf16[512,384]{1,0:T(8,128)(2,1)S(1)}, bf16[512,384]{1,0:T(8,128)(2,1)}, u32[]{:S(2)}, u32[]{:S(2)}) collective-permute-start(bf16[512,384]{1,0:T(8,128)(2,1)S(1)} %bitcast.147), channel_id=1, source_target_pairs={{2,0},{1,3},{6,4},{5,7},{10,8},{9,11},{14,12},{13,15},{18,16},{17,... | collective-permute-start | bytes 1179656 | tf_op jit(solution)/shard_map/ppermute | solution.py:143
  12.1 10.8 %collective-permute-start.8 = (bf16[512,384]{1,0:T(8,128)(2,1)S(1)}, bf16[512,384]{1,0:T(8,128)(2,1)}, u32[]{:S(2)}, u32[]{:S(2)}) collective-permute-start(bf16[512,384]{1,0:T(8,128)(2,1)S(1)} %bitcast.148), channel_id=1, source_target_pairs={{2,1},{1,2},{6,5},{5,6},{10,9},{9,10},{14,13},{13,14},{18,17},{17,... | collective-permute-start | bytes 1179656 | tf_op jit(solution)/shard_map/ppermute | solution.py:144
  13.6 21.4 %collective-permute-start.6 = (bf16[512,384]{1,0:T(8,128)(2,1)S(1)}, bf16[512,384]{1,0:T(8,128)(2,1)}, u32[]{:S(2)}, u32[]{:S(2)}) collective-permute-start(bf16[512,384]{1,0:T(8,128)(2,1)S(1)} %get-tuple-element.32), channel_id=1, source_target_pairs={{0,2},{2,0},{1,3},{3,1},{4,6},{6,4},{5,7},{7,5},{8,10},{10,8},{9,1... | collective-permute-start | bytes 1179656 | tf_op jit(solution)/shard_map/ppermute | solution.py:146
  18.9 1.1 %copy-start.2 = (bf16[2,512,384]{2,1,0:T(8,128)(2,1)S(1)}, bf16[2,512,384]{2,1,0:T(8,128)(2,1)}, u32[]{:S(2)}) copy-start(bf16[2,512,384]{2,1,0:T(8,128)(2,1)} %pad_maximum_fusion.2) | copy-start | bytes 2359300
  20.0 24.4 %collective-permute-start.3 = (bf16[2,512,384]{2,1,0:T(8,128)(2,1)S(1)}, bf16[2,512,384]{2,1,0:T(8,128)(2,1)S(1)}, u32[]{:S(2)}, u32[]{:S(2)}) collective-permute-start(bf16[2,512,384]{2,1,0:T(8,128)(2,1)S(1)} %copy-done.2), channel_id=1, source_target_pairs={{0,1},{1,0},{2,3},{3,2},{4,5},{5,4},{6,7},{7,6},{8,9},{9,8},{10,11... | collective-permute-start | bytes 2359304 | tf_op jit(solution)/shard_map/ppermute | solution.py:105
  22.2 65.3 %collective-permute-start.4 = (bf16[3,384,384]{2,1,0:T(8,128)(2,1)S(1)}, bf16[3,384,384]{2,1,0:T(8,128)(2,1)S(1)}, u32[]{:S(2)}, u32[]{:S(2)}) collective-permute-start(bf16[3,384,384]{2,1,0:T(8,128)(2,1)S(1)} %constant_dynamic-slice_fusion), channel_id=1, source_target_pairs={{0,1},{1,0},{2,3},{3,2},{4,5},{5,4},{6,7},{7,6},{8,9},{9,8},{10,11... | collective-permute-start | bytes 2654216 | tf_op jit(solution)/shard_map/ppermute | solution.py:114
  22.4 21.9 %collective-permute-start.2 = (bf16[2,2,256,384]{3,2,1,0:T(8,128)(2,1)S(1)}, bf16[2,2,256,384]{3,2,1,0:T(8,128)(2,1)S(1)}, u32[]{:S(2)}, u32[]{:S(2)}) collective-permute-start(bf16[2,2,256,384]{3,2,1,0:T(8,128)(2,1)S(1)} %pad_maximum_fusion.3), channel_id=1, source_target_pairs={{0,1},{1,0},{2,3},{3,2},{4,5},{5,4},{6,7},{7,6},{8,9},{9,8},{10,11... | collective-permute-start | bytes 2359304 | tf_op jit(solution)/shard_map/ppermute | solution.py:108
  23.0 18.6 %collective-permute-start.5 = (bf16[2,256,384]{2,1,0:T(8,128)(2,1)S(1)}, bf16[2,256,384]{2,1,0:T(8,128)(2,1)S(1)}, u32[]{:S(2)}, u32[]{:S(2)}) collective-permute-start(bf16[2,256,384]{2,1,0:T(8,128)(2,1)S(1)} %pad_maximum_fusion.16), channel_id=1, source_target_pairs={{0,2},{2,0},{1,3},{3,1},{4,6},{6,4},{5,7},{7,5},{8,10},{10,8},{9,1... | collective-permute-start | bytes 1179656 | tf_op jit(solution)/shard_map/ppermute | solution.py:147
  45.2 12.2 %collective-permute-start.13 = (f32[2,96,384]{2,1,0:T(8,128)S(1)}, f32[2,96,384]{2,1,0:T(8,128)S(1)}, u32[]{:S(2)}, u32[]{:S(2)}) collective-permute-start(f32[2,96,384]{2,1,0:T(8,128)S(1)} %select_bitcast_fusion.1), channel_id=1, source_target_pairs={{0,4},{4,0},{8,12},{12,8},{1,5},{5,1},{9,13},{13,9},{2,6},{6,2},{1... | collective-permute-start | bytes 884744 | tf_op jit(solution)/shard_map/ppermute | solution.py:76
  48.9 23.2 %collective-permute-start.9 = (f32[2,192,384]{2,1,0:T(8,128)S(1)}, f32[2,192,384]{2,1,0:T(8,128)S(1)}, u32[]{:S(2)}, u32[]{:S(2)}) collective-permute-start(f32[2,192,384]{2,1,0:T(8,128)S(1)} %select_bitcast_fusion), channel_id=1, source_target_pairs={{0,4},{4,0},{8,12},{12,8},{1,5},{5,1},{9,13},{13,9},{2,6},{6,2},{1... | collective-permute-start | bytes 1769480 | tf_op jit(solution)/shard_map/ppermute | solution.py:76
  57.4 11.1 %collective-permute-start.14 = (f32[96,384]{1,0:T(8,128)S(1)}, f32[96,384]{1,0:T(8,128)S(1)}, u32[]{:S(2)}, u32[]{:S(2)}) collective-permute-start(f32[96,384]{1,0:T(8,128)S(1)} %select_bitcast_fusion.7), channel_id=1, source_target_pairs={{0,8},{8,0},{4,12},{12,4},{1,9},{9,1},{5,13},{13,5},{2,10},{10,2},... | collective-permute-start | bytes 442376 | tf_op jit(solution)/shard_map/ppermute | solution.py:81
  68.5 3.7 %copy-start.3 = (f32[512,384]{1,0:T(8,128)S(1)}, f32[512,384]{1,0:T(8,128)}, u32[]{:S(2)}) copy-start(f32[512,384]{1,0:T(8,128)} %get-tuple-element.33) | copy-start | bytes 2359300
  68.6 13.3 %collective-permute-start.15 = (bf16[96,384]{1,0:T(8,128)(2,1)S(1)}, bf16[96,384]{1,0:T(8,128)(2,1)S(1)}, u32[]{:S(2)}, u32[]{:S(2)}) collective-permute-start(bf16[96,384]{1,0:T(8,128)(2,1)S(1)} %fusion.65), channel_id=1, source_target_pairs={{0,8},{8,0},{4,12},{12,4},{1,9},{9,1},{5,13},{13,5},{2,10},{10,2},... | collective-permute-start | bytes 221192 | tf_op jit(solution)/shard_map/ppermute | solution.py:82
  72.2 15.2 %collective-permute-start.10 = (f32[192,384]{1,0:T(8,128)S(1)}, f32[192,384]{1,0:T(8,128)S(1)}, u32[]{:S(2)}, u32[]{:S(2)}) collective-permute-start(f32[192,384]{1,0:T(8,128)S(1)} %select_bitcast_fusion.4), channel_id=1, source_target_pairs={{0,8},{8,0},{4,12},{12,4},{1,9},{9,1},{5,13},{13,5},{2,10},{10,2},... | collective-permute-start | bytes 884744 | tf_op jit(solution)/shard_map/ppermute | solution.py:81
  81.9 13.4 %collective-permute-start.16 = (bf16[2,96,384]{2,1,0:T(8,128)(2,1)S(1)}, bf16[2,96,384]{2,1,0:T(8,128)(2,1)S(1)}, u32[]{:S(2)}, u32[]{:S(2)}) collective-permute-start(bf16[2,96,384]{2,1,0:T(8,128)(2,1)S(1)} %maximum_select_fusion.1), channel_id=1, source_target_pairs={{0,4},{4,0},{8,12},{12,8},{1,5},{5,1},{9,13},{13,9},{2,6},{6,2},{1... | collective-permute-start | bytes 442376 | tf_op jit(solution)/shard_map/ppermute | solution.py:84
  87.4 7.7 %collective-permute-start.11 = (bf16[192,384]{1,0:T(8,128)(2,1)S(1)}, bf16[192,384]{1,0:T(8,128)(2,1)S(1)}, u32[]{:S(2)}, u32[]{:S(2)}) collective-permute-start(bf16[192,384]{1,0:T(8,128)(2,1)S(1)} %fusion.64), channel_id=1, source_target_pairs={{0,8},{8,0},{4,12},{12,4},{1,9},{9,1},{5,13},{13,5},{2,10},{10,2},... | collective-permute-start | bytes 442376 | tf_op jit(solution)/shard_map/ppermute | solution.py:82
  95.2 9.0 %collective-permute-start.12 = (bf16[2,192,384]{2,1,0:T(8,128)(2,1)S(1)}, bf16[2,192,384]{2,1,0:T(8,128)(2,1)S(1)}, u32[]{:S(2)}, u32[]{:S(2)}) collective-permute-start(bf16[2,192,384]{2,1,0:T(8,128)(2,1)S(1)} %maximum_select_fusion), channel_id=1, source_target_pairs={{0,4},{4,0},{8,12},{12,8},{1,5},{5,1},{9,13},{13,9},{2,6},{6,2},{1... | collective-permute-start | bytes 884744 | tf_op jit(solution)/shard_map/ppermute | solution.py:84

commit v8 on v7

--- a/solution.py
+++ b/solution.py
@@ -144,8 +144,17 @@
         cross_core = lax.ppermute(local_cot, ("batch", "chan"), [(2, 1), (1, 2)])
         far_cot = jnp.where(b == c, same_core, cross_core)
         far_mid = lax.ppermute(activation, "batch", SWAP)
-        far_halo = lax.ppermute(jnp.stack([from_prev[0], from_next[0]]), "batch", SWAP)
-        far_act = jnp.concatenate([far_halo[0], far_mid, far_halo[1]], 0)
+        far_prev = lax.ppermute(
+            activation[rows - spread :],
+            ("seq", "batch"),
+            [((j - 1) * 2 + 1 - h, j * 2 + h) for j in range(1, seq_count) for h in range(2)],
+        )
+        far_next = lax.ppermute(
+            activation[:spread],
+            ("seq", "batch"),
+            [((j + 1) * 2 + 1 - h, j * 2 + h) for j in range(seq_count - 1) for h in range(2)],
+        )
+        far_act = jnp.concatenate([far_prev, far_mid, far_next], 0)
         far_taps = tap_stack(far_act, rows, spread, (0, 1, 2))
         grads = {}
         for k in (1, 0, 2):
@@ -153,9 +162,8 @@
                 own_taps[:, k].T, cot_mine, preferred_element_type=jnp.float32
             ) + jnp.dot(far_taps[:, k].T, far_cot, preferred_element_type=jnp.float32)
         if seq_count == 4:
-            middle = line_total(grads[1])
-            sides = line_total(jnp.concatenate([grads[0], grads[2]], 0))
-            weight_grad = jnp.stack([sides[: middle.shape[0]], middle, sides[middle.shape[0] :]])
+            summed = line_total(jnp.concatenate([grads[0], grads[1], grads[2]], 0))
+            weight_grad = summed.reshape(3, -1, summed.shape[1])
         else:
             weight_grad = lax.psum(jnp.stack([grads[0], grads[1], grads[2]]), "seq")
     else:

time: 107 us -> 124 us (1.16)
  the two profiles are of different devices: /device:TPU:0 before, /device:TPU:2 now
where the time goes in v8:
time: 124 us; the launch traced here: 123 us
  waiting for transfers between devices  61.5 us (50%)
  starting transfers between devices  26.2 us (21%)
  matrix products  16.8 us (14%)
  other arithmetic  12 us (10%)
  local copies, waits for them, and re-layouts  5.95 us (5%)
    ppermute x1, waiting for transfers between devices, line_total(): lax.ppermute(jnp.where(odd, even_set, odd_set), 'seq', pairs)  20.2 us
    ppermute x1, waiting for transfers between devices, line_total(): total = (keep + lax.ppermute(give, 'seq', across)).astype(jnp.bfloat16)  15.7 us
    ppermute x1, waiting for transfers between devices, line_total(): other = lax.ppermute(total, 'seq', across)  9.73 us
    ppermute x1, starting transfers between devices, line_total(): lax.ppermute(jnp.where(odd, even_set, odd_set), 'seq', pairs)  6.91 us
    ppermute x1, waiting for transfers between devices, shards(): far_mid = lax.ppermute(activation, 'batch', SWAP)  6.28 us
    ppermute x1, waiting for transfers between devices, line_total(): far_set = lax.ppermute(own_set, 'seq', pairs)  5.9 us
    ppermute x2, starting transfers between devices, shift_from(): return lax.ppermute(block, axis, route)  4.78 us
    dot_general x3, matrix products, shards(): jnp.dot(far_taps[:, k].T, far_cot, preferred_element_type=jnp.float32)  4.04 us
  transfers between devices with their start and end apart: 14, of which 8 were waited for; matrix products, arithmetic and copies ran while one was open for 17% of the time, Pallas kernels for 0%

profile of v8, /device:TPU:2, one launch (start us, length us, event | category | flops | bytes accessed | tf_op | source)
XLA Modules:
  0.0 123.4 jit_solution(12218870629497360512)
XLA Ops:
  0.7 2.9 %multiply_convert_fusion = (bf16[512,384]{1,0:T(8,128)(2,1)S(1)}, f32[512,384]{1,0:T(8,128)}) fusion(bf16[1,1024,384]{2,1,0:T(8,128)(2,1)} %param.3, s32[1024]{0:T(1024)S(1)} %get-tuple-element.30, s32[1024]{0:T(1024)S(1)} %get-tuple-element.31, pred[1024]{0:T(1024)(128)(4,1)S(1)} %fusion.65), kind=kOutput, calls=%fused_computation.64 | convolution fusion | flops 406519808 | bytes 1975296 | tf_op jit(solution)/shard_map/dot_general | solution.py:101
  3.6 1.0 fusion.48
  4.6 3.5 %collective-permute-start = (bf16[2,256,384]{2,1,0:T(8,128)(2,1)}, bf16[2,256,384]{2,1,0:T(8,128)(2,1)S(1)}, u32[]{:S(2)}, u32[]{:S(2)}) collective-permute-start(bf16[2,256,384]{2,1,0:T(8,128)(2,1)} %get-tuple-element.24), channel_id=1, source_target_pairs={{0,4},{4,8},{8,12},{1,5},{5,9},{9,13},{2,6},{6,10},{10,14},{3,7},{... | collective-permute-start | bytes 1179656 | tf_op jit(solution)/shard_map/ppermute | solution.py:12
  8.1 1.3 %collective-permute-start.1 = (bf16[2,256,384]{2,1,0:T(8,128)(2,1)}, bf16[2,256,384]{2,1,0:T(8,128)(2,1)S(1)}, u32[]{:S(2)}, u32[]{:S(2)}) collective-permute-start(bf16[2,256,384]{2,1,0:T(8,128)(2,1)} %get-tuple-element.25), channel_id=1, source_target_pairs={{4,0},{8,4},{12,8},{5,1},{9,5},{13,9},{6,2},{10,6},{14,10},{7,3},{... | collective-permute-start | bytes 1179656 | tf_op jit(solution)/shard_map/ppermute | solution.py:12
  9.4 3.2 %collective-permute-start.7 = (bf16[512,384]{1,0:T(8,128)(2,1)S(1)}, bf16[512,384]{1,0:T(8,128)(2,1)}, u32[]{:S(2)}, u32[]{:S(2)}) collective-permute-start(bf16[512,384]{1,0:T(8,128)(2,1)S(1)} %bitcast.118), channel_id=1, source_target_pairs={{2,0},{1,3},{6,4},{5,7},{10,8},{9,11},{14,12},{13,15},{18,16},{17,... | collective-permute-start | bytes 1179656 | tf_op jit(solution)/shard_map/ppermute | solution.py:143
  12.6 2.3 %collective-permute-start.8 = (bf16[512,384]{1,0:T(8,128)(2,1)S(1)}, bf16[512,384]{1,0:T(8,128)(2,1)}, u32[]{:S(2)}, u32[]{:S(2)}) collective-permute-start(bf16[512,384]{1,0:T(8,128)(2,1)S(1)} %bitcast.119), channel_id=1, source_target_pairs={{2,1},{1,2},{6,5},{5,6},{10,9},{9,10},{14,13},{13,14},{18,17},{17,... | collective-permute-start | bytes 1179656 | tf_op jit(solution)/shard_map/ppermute | solution.py:144
  14.9 0.7 fusion.78
  15.6 1.0 pad_maximum_fusion.1
  16.6 0.1 collective-permute-done
  16.7 1.4 %collective-permute-start.3 = (bf16[2,512,384]{2,1,0:T(8,128)(2,1)}, bf16[2,512,384]{2,1,0:T(8,128)(2,1)S(1)}, u32[]{:S(2)}, u32[]{:S(2)}) collective-permute-start(bf16[2,512,384]{2,1,0:T(8,128)(2,1)} %pad_maximum_fusion.1), channel_id=1, source_target_pairs={{0,1},{1,0},{2,3},{3,2},{4,5},{5,4},{6,7},{7,6},{8,9},{9,8},{10,11... | collective-permute-start | bytes 2359304 | tf_op jit(solution)/shard_map/ppermute | solution.py:105
  18.1 2.7 %collective-permute-done.1 = bf16[2,256,384]{2,1,0:T(8,128)(2,1)S(1)} collective-permute-done((bf16[2,256,384]{2,1,0:T(8,128)(2,1)}, bf16[2,256,384]{2,1,0:T(8,128)(2,1)S(1)}, u32[]{:S(2)}, u32[]{:S(2)}) %collective-permute-start.1) | collective-permute-done | bytes 393248 | tf_op jit(solution)/shard_map/ppermute | solution.py:12
  20.8 3.4 %collective-permute-start.5 = (bf16[256,384]{1,0:T(8,128)(2,1)}, bf16[256,384]{1,0:T(8,128)(2,1)S(1)}, u32[]{:S(2)}, u32[]{:S(2)}) collective-permute-start(bf16[256,384]{1,0:T(8,128)(2,1)} %get-tuple-element.26), channel_id=1, source_target_pairs={{2,4},{0,6},{6,8},{4,10},{10,12},{8,14},{3,5},{1,7},{7,9},{5,11},{... | collective-permute-start | bytes 589832 | tf_op jit(solution)/shard_map/ppermute | solution.py:147
  24.2 0.1 pad_maximum_fusion.2
  24.3 1.3 %collective-permute-start.9 = (bf16[256,384]{1,0:T(8,128)(2,1)S(1)}, bf16[256,384]{1,0:T(8,128)(2,1)S(1)}, u32[]{:S(2)}, u32[]{:S(2)}) collective-permute-start(bf16[256,384]{1,0:T(8,128)(2,1)S(1)} %get-tuple-element.27), channel_id=1, source_target_pairs={{6,0},{4,2},{10,4},{8,6},{14,8},{12,10},{7,1},{5,3},{11,5},{9,7},{... | collective-permute-start | bytes 589832 | tf_op jit(solution)/shard_map/ppermute | solution.py:152
  25.7 1.1 broadcast_select_fusion
  26.8 0.9 collective-permute-done.5
  27.7 6.3 %collective-permute-done.6 = bf16[512,384]{1,0:T(8,128)(2,1)} collective-permute-done((bf16[512,384]{1,0:T(8,128)(2,1)S(1)}, bf16[512,384]{1,0:T(8,128)(2,1)}, u32[]{:S(2)}, u32[]{:S(2)}) %collective-permute-start.6) | collective-permute-done | bytes 393248 | tf_op jit(solution)/shard_map/ppermute | solution.py:146
  34.0 1.3 %fusion.52 = f32[384,384]{1,0:T(8,128)S(1)} fusion(bf16[512,384]{1,0:T(8,128)(2,1)S(1)} %broadcast_select_fusion, bf16[512,384]{1,0:T(8,128)(2,1)} %collective-permute-done.6, bf16[256,384]{1,0:T(8,128)(2,1)S(1)} %collective-permute-done.5), kind=kOutput, calls=%fused_computation.79 | convolution fusion | flops 151781376 | bytes 1572864 | tf_op jit(solution)/shard_map/dot_general | solution.py:163
  35.3 1.3 %fusion.50 = f32[384,384]{1,0:T(8,128)S(1)} fusion(bf16[512,384]{1,0:T(8,128)(2,1)S(1)} %broadcast_select_fusion, bf16[256,384]{1,0:T(8,128)(2,1)S(1)} %collective-permute-done.9, bf16[512,384]{1,0:T(8,128)(2,1)} %collective-permute-done.6), kind=kOutput, calls=%fused_computation.76 | convolution fusion | flops 151781376 | bytes 1572864 | tf_op jit(solution)/shard_map/dot_general | solution.py:163
  36.6 1.4 %fusion.79 = f32[384,384]{1,0:T(8,128)S(1)} fusion(bf16[512,384]{1,0:T(8,128)(2,1)} %collective-permute-done.6, bf16[512,384]{1,0:T(8,128)(2,1)S(1)} %broadcast_select_fusion), kind=kOutput, calls=%fused_computation.127 | convolution fusion | flops 150994944 | bytes 1376256 | tf_op jit(solution)/shard_map/dot_general | solution.py:163
  38.1 1.5 %broadcast_select_fusion.1 = (bf16[1,512,384]{2,1,0:T(8,128)(2,1)S(1)}, bf16[512,1,384]{2,0,1:T(8,128)(2,1)}, bf16[512,1,384]{2,0,1:T(8,128)(2,1)}, bf16[512,1,3...) fusion(bf16[1,512,384]{2,1,0:T(8,128)(2,1)S(1)} %copy-done.2, ...), kind=kLoop, calls=%fused_computation.104 | loop fusion | flops 3342336 | bytes 5505025 | tf_op jit(solution)/shard_map/jit(_where)/select_n | solution.py:142
  39.6 0.4 convolution_add_fusion.1
  40.1 0.4 convolution_add_fusion.2
  40.5 0.4 convolution_add_fusion
  40.9 0.1 pad_maximum_fusion
  41.0 1.2 copy-done.1
  42.2 0.1 select_bitcast_fusion
  42.3 6.9 %collective-permute-start.10 = (f32[2,288,384]{2,1,0:T(8,128)S(1)}, f32[2,288,384]{2,1,0:T(8,128)}, u32[]{:S(2)}, u32[]{:S(2)}) collective-permute-start(f32[2,288,384]{2,1,0:T(8,128)S(1)} %select_bitcast_fusion), channel_id=1, source_target_pairs={{0,4},{4,0},{8,12},{12,8},{1,5},{5,1},{9,13},{13,9},{2,6},{6,2},{1... | collective-permute-start | bytes 2654216 | tf_op jit(solution)/shard_map/ppermute | solution.py:76
  49.2 20.2 %collective-permute-done.10 = f32[2,288,384]{2,1,0:T(8,128)} collective-permute-done((f32[2,288,384]{2,1,0:T(8,128)S(1)}, f32[2,288,384]{2,1,0:T(8,128)}, u32[]{:S(2)}, u32[]{:S(2)}) %collective-permute-start.10) | collective-permute-done | bytes 884768 | tf_op jit(solution)/shard_map/ppermute | solution.py:76
  69.4 1.8 %fusion.32 = f32[2,288,384]{2,1,0:T(8,128)S(1)} fusion(f32[2,288,384]{2,1,0:T(8,128)} %collective-permute-done.10, f32[2,2,288,384]{3,2,1,0:T(8,128)} %bitcast.117, pred[]{:T(512)S(6)} %eq.13), kind=kLoop, calls=%fused_computation.51 | loop fusion | flops 442368 | bytes 3538945 | tf_op jit(solution)/shard_map/add | solution.py:76
  71.2 0.8 select_bitcast_fusion.3
  72.1 2.7 %collective-permute-start.11 = (f32[288,384]{1,0:T(8,128)}, f32[288,384]{1,0:T(8,128)}, u32[]{:S(2)}, u32[]{:S(2)}) collective-permute-start(f32[288,384]{1,0:T(8,128)} %select_bitcast_fusion.3), channel_id=1, source_target_pairs={{0,8},{8,0},{4,12},{12,4},{1,9},{9,1},{5,13},{13,5},{2,10},{10,2},... | collective-permute-start | bytes 1327112 | tf_op jit(solution)/shard_map/ppermute | solution.py:81
  74.8 1.0 constant_dynamic-slice_fusion
  75.8 1.4 %fusion.57 = (bf16[512,1,384]{2,0,1:T(8,128)(2,1)S(1)}, bf16[512,1,384]{2,0,1:T(8,128)(2,1)S(1)}, bf16[512,1,384]{2,0,1:T(8,128)(2,1)S(1)}, bf16[512,1,384]{2,0,1:T(8,128)(2,1)S(1)}) fusion(bf16[2,256,384]{2,1,0:T(8,128)(2,1)} %copy-done.4, bf16[1,512,384]{2,1,0:T(8,128)(2,1)S(1)} %copy-done.2, bf16[1,512,384]{2,1,0:T(8,128)(2,1)S(1)} %bitcast.114, ...), kind=kLoop, calls=%fused_computation.89 | loop fusion | flops 4718592 | bytes 3145728 | tf_op jit(solution)/shard_map/stack | solution.py:21
  77.2 1.7 %convolution_bitcast_fusion.3 = f32[512,384]{1,0:T(8,128)} fusion(bf16[512,1,384]{2,0,1:T(8,128)(2,1)S(1)} %get-tuple-element.4, bf16[512,1,384]{2,0,1:T(8,128)(2,1)S(1)} %bitcast.115, bf16[512,1,384]{2,0,1:T(8,128)(2,1)S(1)} %get-tuple-element.20, bf16[3,384,768]{2,1,0:T(8,128)(2,1)S(1)} %copy-done, s32[]{:T(128)S(6)} %select_n.97), kind=kOutput, calls=%fused_computation.6 | convolution fusion | flops 454164480 | bytes 2850820 | tf_op jit(solution)/shard_map/tki,kio->to/dot_general | solution.py:116
  78.9 15.7 %collective-permute-done.11 = f32[288,384]{1,0:T(8,128)} collective-permute-done((f32[288,384]{1,0:T(8,128)}, f32[288,384]{1,0:T(8,128)}, u32[]{:S(2)}, u32[]{:S(2)}) %collective-permute-start.11) | collective-permute-done | bytes 442400 | tf_op jit(solution)/shard_map/ppermute | solution.py:81
  94.5 1.1 fusion.47
  95.8 2.1 %convolution_bitcast_fusion = f32[512,384]{1,0:T(8,128)S(1)} fusion(bf16[3,384,384]{2,1,0:T(8,128)(2,1)} %constant_dynamic-slice_fusion, bf16[512,1,384]{2,0,1:T(8,128)(2,1)S(1)} %copy-done.9, bf16[512,1,384]{2,0,1:T(8,128)(2,1)S(1)} %copy-done.7, bf16[512,1,384]{2,0,1:T(8,128)(2,1)S(1)} %copy-done.8), kind=kOutput, calls=%fused_computation.3 | convolution fusion | flops 454164480 | bytes 2850816 | tf_op jit(solution)/shard_map/tko,kio->ti/dot_general | solution.py:128
  97.8 9.7 %collective-permute-done.12 = bf16[288,384]{1,0:T(8,128)(2,1)S(1)} collective-permute-done((bf16[288,384]{1,0:T(8,128)(2,1)S(1)}, bf16[288,384]{1,0:T(8,128)(2,1)S(1)}, u32[]{:S(2)}, u32[]{:S(2)}) %collective-permute-start.12) | collective-permute-done | bytes 221216 | tf_op jit(solution)/shard_map/ppermute | solution.py:82
  107.6 0.8 maximum_select_fusion
  108.4 1.3 %fusion.41 = bf16[512,384]{1,0:T(8,128)(2,1)S(1)} fusion(f32[512,384]{1,0:T(8,128)S(1)} %copy-done.10, f32[512,384]{1,0:T(8,128)S(1)} %convolution_bitcast_fusion, bf16[512,1,384]{2,0,1:T(8,128)(2,1)S(1)} %get-tuple-element.21, bf16[512,1,384]{2,0,1:T(8,128)(2,1)S(1)} %bitcast.120, bf16[512,1,384]{2,0,1:T(8,128)(2,1)S(1)} %get-tuple-element.3, ...), kind=kOutput, calls=%fused_computation.61 | convolution fusion | flops 458883072 | bytes 4423684 | tf_op jit(solution)/shard_map/tko,kio->ti/dot_general | solution.py:125
  109.7 0.4 broadcast_in_dim.18
  110.1 1.2 convert_element_type.41
  111.3 3.6 %fusion.4 = bf16[1,512,384]{2,1,0:T(8,128)(2,1)} fusion(f32[512,384]{1,0:T(8,128)} %get-tuple-element.29, f32[512,384]{1,0:T(8,128)} %convolution_bitcast_fusion.3, bf16[3,384,384]{2,1,0:T(8,128)(2,1)} %collective-permute-done.4, bf16[512,1,384]{2,0,1:T(8,128)(2,1)} %get-tuple-element.15, bf16[512,1,384]{2,0,1:T(8,128)(2,1)} %get-tuple-element.17, ...), kind=kOutput, calls=%fused_computation.14 | convolution fusion | flops 454754304 | bytes 4030464 | tf_op jit(solution)/shard_map/tki,kio->to/dot_general | solution.py:119
  114.9 5.9 %collective-permute-done.13 = bf16[2,288,384]{2,1,0:T(8,128)(2,1)} collective-permute-done((bf16[2,288,384]{2,1,0:T(8,128)(2,1)}, bf16[2,288,384]{2,1,0:T(8,128)(2,1)}, u32[]{:S(2)}, u32[]{:S(2)}) %collective-permute-start.13) | collective-permute-done | bytes 442400 | tf_op jit(solution)/shard_map/ppermute | solution.py:84
  120.8 1.1 select_bitcast_fusion.2
  122.0 0.1 maximum_convert_fusion
  122.1 1.3 %copy.10 = f32[2,2,288,384]{3,2,1,0:T(8,128)} copy(f32[2,2,288,384]{3,2,0,1:T(8,128)S(1)} %maximum_convert_fusion) | data formatting | bytes 3538944 | tf_op jit(solution)/shard_map/convert_element_type | solution.py:87
  (35 shorter events, 0.4 us)
Async XLA Ops:
  0.6 74.1 %copy-start = (bf16[3,384,768]{2,1,0:T(8,128)(2,1)S(1)}, bf16[3,384,768]{2,1,0:T(8,128)(2,1)}, u32[]{:S(2)}) copy-start(bf16[3,384,768]{2,1,0:T(8,128)(2,1)} %param.4) | copy-start | bytes 5308420
  0.7 2.9 %copy-start.2 = (bf16[1,512,384]{2,1,0:T(8,128)(2,1)S(1)}, bf16[1,512,384]{2,1,0:T(8,128)(2,1)}, u32[]{:S(2)}) copy-start(bf16[1,512,384]{2,1,0:T(8,128)(2,1)} %param.5) | copy-start | bytes 1179652
  4.6 12.1 %collective-permute-start = (bf16[2,256,384]{2,1,0:T(8,128)(2,1)}, bf16[2,256,384]{2,1,0:T(8,128)(2,1)S(1)}, u32[]{:S(2)}, u32[]{:S(2)}) collective-permute-start(bf16[2,256,384]{2,1,0:T(8,128)(2,1)} %get-tuple-element.24), channel_id=1, source_target_pairs={{0,4},{4,8},{8,12},{1,5},{5,9},{9,13},{2,6},{6,10},{10,14},{3,7},{... | collective-permute-start | bytes 1179656 | tf_op jit(solution)/shard_map/ppermute | solution.py:12
  8.1 12.7 %collective-permute-start.1 = (bf16[2,256,384]{2,1,0:T(8,128)(2,1)}, bf16[2,256,384]{2,1,0:T(8,128)(2,1)S(1)}, u32[]{:S(2)}, u32[]{:S(2)}) collective-permute-start(bf16[2,256,384]{2,1,0:T(8,128)(2,1)} %get-tuple-element.25), channel_id=1, source_target_pairs={{4,0},{8,4},{12,8},{5,1},{9,5},{13,9},{6,2},{10,6},{14,10},{7,3},{... | collective-permute-start | bytes 1179656 | tf_op jit(solution)/shard_map/ppermute | solution.py:12
  9.4 14.9 %collective-permute-start.7 = (bf16[512,384]{1,0:T(8,128)(2,1)S(1)}, bf16[512,384]{1,0:T(8,128)(2,1)}, u32[]{:S(2)}, u32[]{:S(2)}) collective-permute-start(bf16[512,384]{1,0:T(8,128)(2,1)S(1)} %bitcast.118), channel_id=1, source_target_pairs={{2,0},{1,3},{6,4},{5,7},{10,8},{9,11},{14,12},{13,15},{18,16},{17,... | collective-permute-start | bytes 1179656 | tf_op jit(solution)/shard_map/ppermute | solution.py:143
  12.6 13.0 %collective-permute-start.8 = (bf16[512,384]{1,0:T(8,128)(2,1)S(1)}, bf16[512,384]{1,0:T(8,128)(2,1)}, u32[]{:S(2)}, u32[]{:S(2)}) collective-permute-start(bf16[512,384]{1,0:T(8,128)(2,1)S(1)} %bitcast.119), channel_id=1, source_target_pairs={{2,1},{1,2},{6,5},{5,6},{10,9},{9,10},{14,13},{13,14},{18,17},{17,... | collective-permute-start | bytes 1179656 | tf_op jit(solution)/shard_map/ppermute | solution.py:144
  14.8 19.1 %collective-permute-start.6 = (bf16[512,384]{1,0:T(8,128)(2,1)S(1)}, bf16[512,384]{1,0:T(8,128)(2,1)}, u32[]{:S(2)}, u32[]{:S(2)}) collective-permute-start(bf16[512,384]{1,0:T(8,128)(2,1)S(1)} %get-tuple-element.28), channel_id=1, source_target_pairs={{0,2},{2,0},{1,3},{3,1},{4,6},{6,4},{5,7},{7,5},{8,10},{10,8},{9,1... | collective-permute-start | bytes 1179656 | tf_op jit(solution)/shard_map/ppermute | solution.py:146
  16.7 23.3 %copy-start.3 = (bf16[2,256,384]{2,1,0:T(8,128)(2,1)}, bf16[2,256,384]{2,1,0:T(8,128)(2,1)S(1)}, u32[]{:S(2)}) copy-start(bf16[2,256,384]{2,1,0:T(8,128)(2,1)S(1)} %collective-permute-done) | copy-start | bytes 1179652
  16.7 21.4 %collective-permute-start.3 = (bf16[2,512,384]{2,1,0:T(8,128)(2,1)}, bf16[2,512,384]{2,1,0:T(8,128)(2,1)S(1)}, u32[]{:S(2)}, u32[]{:S(2)}) collective-permute-start(bf16[2,512,384]{2,1,0:T(8,128)(2,1)} %pad_maximum_fusion.1), channel_id=1, source_target_pairs={{0,1},{1,0},{2,3},{3,2},{4,5},{5,4},{6,7},{7,6},{8,9},{9,8},{10,11... | collective-permute-start | bytes 2359304 | tf_op jit(solution)/shard_map/ppermute | solution.py:105
  20.8 19.7 %copy-start.4 = (bf16[2,256,384]{2,1,0:T(8,128)(2,1)}, bf16[2,256,384]{2,1,0:T(8,128)(2,1)S(1)}, u32[]{:S(2)}) copy-start(bf16[2,256,384]{2,1,0:T(8,128)(2,1)S(1)} %collective-permute-done.1) | copy-start | bytes 1179652
  20.8 6.9 %collective-permute-start.5 = (bf16[256,384]{1,0:T(8,128)(2,1)}, bf16[256,384]{1,0:T(8,128)(2,1)S(1)}, u32[]{:S(2)}, u32[]{:S(2)}) collective-permute-start(bf16[256,384]{1,0:T(8,128)(2,1)} %get-tuple-element.26), channel_id=1, source_target_pairs={{2,4},{0,6},{6,8},{4,10},{10,12},{8,14},{3,5},{1,7},{7,9},{5,11},{... | collective-permute-start | bytes 589832 | tf_op jit(solution)/shard_map/ppermute | solution.py:147
  24.3 11.0 %collective-permute-start.9 = (bf16[256,384]{1,0:T(8,128)(2,1)S(1)}, bf16[256,384]{1,0:T(8,128)(2,1)S(1)}, u32[]{:S(2)}, u32[]{:S(2)}) collective-permute-start(bf16[256,384]{1,0:T(8,128)(2,1)S(1)} %get-tuple-element.27), channel_id=1, source_target_pairs={{6,0},{4,2},{10,4},{8,6},{14,8},{12,10},{7,1},{5,3},{11,5},{9,7},{... | collective-permute-start | bytes 589832 | tf_op jit(solution)/shard_map/ppermute | solution.py:152
  25.6 12.4 %collective-permute-start.2 = (bf16[2,2,256,384]{3,2,1,0:T(8,128)(2,1)S(1)}, bf16[2,2,256,384]{3,2,1,0:T(8,128)(2,1)S(1)}, u32[]{:S(2)}, u32[]{:S(2)}) collective-permute-start(bf16[2,2,256,384]{3,2,1,0:T(8,128)(2,1)S(1)} %pad_maximum_fusion.2), channel_id=1, source_target_pairs={{0,1},{1,0},{2,3},{3,2},{4,5},{5,4},{6,7},{7,6},{8,9},{9,8},{10,11... | collective-permute-start | bytes 2359304 | tf_op jit(solution)/shard_map/ppermute | solution.py:108
  41.0 1.2 copy-start.1
  42.3 27.1 %collective-permute-start.10 = (f32[2,288,384]{2,1,0:T(8,128)S(1)}, f32[2,288,384]{2,1,0:T(8,128)}, u32[]{:S(2)}, u32[]{:S(2)}) collective-permute-start(f32[2,288,384]{2,1,0:T(8,128)S(1)} %select_bitcast_fusion), channel_id=1, source_target_pairs={{0,4},{4,0},{8,12},{12,8},{1,5},{5,1},{9,13},{13,9},{2,6},{6,2},{1... | collective-permute-start | bytes 2654216 | tf_op jit(solution)/shard_map/ppermute | solution.py:76
  72.1 22.5 %collective-permute-start.11 = (f32[288,384]{1,0:T(8,128)}, f32[288,384]{1,0:T(8,128)}, u32[]{:S(2)}, u32[]{:S(2)}) collective-permute-start(f32[288,384]{1,0:T(8,128)} %select_bitcast_fusion.3), channel_id=1, source_target_pairs={{0,8},{8,0},{4,12},{12,4},{1,9},{9,1},{5,13},{13,5},{2,10},{10,2},... | collective-permute-start | bytes 1327112 | tf_op jit(solution)/shard_map/ppermute | solution.py:81
  75.8 35.5 %collective-permute-start.4 = (bf16[3,384,384]{2,1,0:T(8,128)(2,1)}, bf16[3,384,384]{2,1,0:T(8,128)(2,1)}, u32[]{:S(2)}, u32[]{:S(2)}) collective-permute-start(bf16[3,384,384]{2,1,0:T(8,128)(2,1)} %constant_dynamic-slice_fusion), channel_id=1, source_target_pairs={{0,1},{1,0},{2,3},{3,2},{4,5},{5,4},{6,7},{7,6},{8,9},{9,8},{10,11... | collective-permute-start | bytes 2654216 | tf_op jit(solution)/shard_map/ppermute | solution.py:114
  77.2 18.6 %copy-start.7 = (bf16[512,1,384]{2,0,1:T(8,128)(2,1)S(1)}, bf16[512,1,384]{2,0,1:T(8,128)(2,1)}, u32[]{:S(2)}) copy-start(bf16[512,1,384]{2,0,1:T(8,128)(2,1)} %get-tuple-element.14) | copy-start | bytes 1179652
  77.2 18.6 %copy-start.8 = (bf16[512,1,384]{2,0,1:T(8,128)(2,1)S(1)}, bf16[512,1,384]{2,0,1:T(8,128)(2,1)}, u32[]{:S(2)}) copy-start(bf16[512,1,384]{2,0,1:T(8,128)(2,1)} %get-tuple-element.16) | copy-start | bytes 1179652
  77.2 18.6 %copy-start.9 = (bf16[512,1,384]{2,0,1:T(8,128)(2,1)S(1)}, bf16[512,1,384]{2,0,1:T(8,128)(2,1)}, u32[]{:S(2)}) copy-start(bf16[512,1,384]{2,0,1:T(8,128)(2,1)} %get-tuple-element.19) | copy-start | bytes 1179652
  95.6 11.9 %copy-start.5 = (bf16[288,384]{1,0:T(8,128)(2,1)}, bf16[288,384]{1,0:T(8,128)(2,1)S(1)}, u32[]{:S(2)}) copy-start(bf16[288,384]{1,0:T(8,128)(2,1)S(1)} %fusion.47) | copy-start | bytes 663556
  95.6 11.9 %collective-permute-start.12 = (bf16[288,384]{1,0:T(8,128)(2,1)S(1)}, bf16[288,384]{1,0:T(8,128)(2,1)S(1)}, u32[]{:S(2)}, u32[]{:S(2)}) collective-permute-start(bf16[288,384]{1,0:T(8,128)(2,1)S(1)} %fusion.47), channel_id=1, source_target_pairs={{0,8},{8,0},{4,12},{12,4},{1,9},{9,1},{5,13},{13,5},{2,10},{10,2},... | collective-permute-start | bytes 663560 | tf_op jit(solution)/shard_map/ppermute | solution.py:82
  95.7 12.7 %copy-start.10 = (f32[512,384]{1,0:T(8,128)S(1)}, f32[512,384]{1,0:T(8,128)}, u32[]{:S(2)}) copy-start(f32[512,384]{1,0:T(8,128)} %get-tuple-element.29) | copy-start | bytes 2359300
  108.4 12.4 %collective-permute-start.13 = (bf16[2,288,384]{2,1,0:T(8,128)(2,1)}, bf16[2,288,384]{2,1,0:T(8,128)(2,1)}, u32[]{:S(2)}, u32[]{:S(2)}) collective-permute-start(bf16[2,288,384]{2,1,0:T(8,128)(2,1)} %maximum_select_fusion), channel_id=1, source_target_pairs={{0,4},{4,0},{8,12},{12,8},{1,5},{5,1},{9,13},{13,9},{2,6},{6,2},{1... | collective-permute-start | bytes 1327112 | tf_op jit(solution)/shard_map/ppermute | solution.py:84
  111.3 9.5 %copy-start.6 = (bf16[288,384]{1,0:T(8,128)(2,1)S(1)}, bf16[288,384]{1,0:T(8,128)(2,1)}, u32[]{:S(2)}) copy-start(bf16[288,384]{1,0:T(8,128)(2,1)} %copy-done.5) | copy-start | bytes 663556

commit v9 on v7

--- a/solution.py
+++ b/solution.py
@@ -144,14 +144,18 @@
         cross_core = lax.ppermute(local_cot, ("batch", "chan"), [(2, 1), (1, 2)])
         far_cot = jnp.where(b == c, same_core, cross_core)
         far_mid = lax.ppermute(activation, "batch", SWAP)
-        far_halo = lax.ppermute(jnp.stack([from_prev[0], from_next[0]]), "batch", SWAP)
-        far_act = jnp.concatenate([far_halo[0], far_mid, far_halo[1]], 0)
-        far_taps = tap_stack(far_act, rows, spread, (0, 1, 2))
+        cot_next = shift_from(far_cot[:spread], "seq", -1)
+        cot_prev = shift_from(far_cot[rows - spread :], "seq", 1)
+        far_shifted = {
+            1: far_cot,
+            0: jnp.concatenate([far_cot[spread:], cot_next], 0),
+            2: jnp.concatenate([cot_prev, far_cot[: rows - spread]], 0),
+        }
         grads = {}
         for k in (1, 0, 2):
             grads[k] = jnp.dot(
                 own_taps[:, k].T, cot_mine, preferred_element_type=jnp.float32
-            ) + jnp.dot(far_taps[:, k].T, far_cot, preferred_element_type=jnp.float32)
+            ) + jnp.dot(far_mid.T, far_shifted[k], preferred_element_type=jnp.float32)
         if seq_count == 4:
             middle = line_total(grads[1])
             sides = line_total(jnp.concatenate([grads[0], grads[2]], 0))

time: 107 us -> 105 us (0.981)
    ppermute x2 -> x4, starting transfers between devices: 6.26 us -> 12.1 us  [shift_from(): return lax.ppermute(block, axis, route)]
    ppermute x1 -> x0, starting transfers between devices: 5.5 us -> none  [shards(): lax.ppermute(jnp.stack([from_prev[0], from_next[0]]), 'batch', SWAP)]
    ppermute x1 -> x0, waiting for transfers between devices: 4.42 us -> none  [shards(): lax.ppermute(jnp.stack([from_prev[0], from_next[0]]), 'batch', SWAP)]
    ppermute x1, waiting for transfers between devices: 5.24 us -> 7.95 us  [shards(): far_mid = lax.ppermute(activation, 'batch', SWAP)]
    ppermute x2 -> x4, waiting for transfers between devices: 2.2 us -> 4.13 us  [shift_from(): return lax.ppermute(block, axis, route)]
  transfers between devices with their start and end apart: 17 -> 18, of which waited for: 9 -> 9; matrix products, arithmetic and copies ran while one was open for 14% -> 14% of each run, Pallas kernels for 0% -> 0%
where the time goes in v9:
time: 105 us; the launch traced here: 104 us
  waiting for transfers between devices  55.5 us (53%)
  starting transfers between devices  27.8 us (26%)
  matrix products  12.8 us (12%)
  other arithmetic  4.77 us (5%)
  local copies, waits for them, and re-layouts  1.94 us (2%)
    ppermute x2, waiting for transfers between devices, line_total(): total = (keep + lax.ppermute(give, 'seq', across)).astype(jnp.bfloat16)  13.5 us
    ppermute x2, waiting for transfers between devices, line_total(): other = lax.ppermute(total, 'seq', across)  12.8 us
    ppermute x4, starting transfers between devices, shift_from(): return lax.ppermute(block, axis, route)  12.1 us
    ppermute x2, waiting for transfers between devices, line_total(): far_set = lax.ppermute(own_set, 'seq', pairs)  8.76 us
    ppermute x2, waiting for transfers between devices, line_total(): lax.ppermute(jnp.where(odd, even_set, odd_set), 'seq', pairs)  8.41 us
    ppermute x1, waiting for transfers between devices, shards(): far_mid = lax.ppermute(activation, 'batch', SWAP)  7.95 us
    ppermute x1, starting transfers between devices, shards(): far_mid = lax.ppermute(activation, 'batch', SWAP)  4.32 us
    dot_general x3, matrix products, shards(): jnp.dot(far_mid.T, far_shifted[k], preferred_element_type=jnp.float32)  4.18 us
  transfers between devices with their start and end apart: 18, of which 9 were waited for; matrix products, arithmetic and copies ran while one was open for 14% of the time, Pallas kernels for 0%

profile of v9, /device:TPU:0, one launch (start us, length us, event | category | flops | bytes accessed | tf_op | source)
XLA Modules:
  0.0 103.8 jit_solution(13700555674013922374)
XLA Ops:
  0.7 2.9 %multiply_convert_fusion = (bf16[512,384]{1,0:T(8,128)(2,1)S(1)}, f32[512,384]{1,0:T(8,128)}) fusion(bf16[1,1024,384]{2,1,0:T(8,128)(2,1)} %param.3, s32[1024]{0:T(1024)S(1)} %get-tuple-element.34, s32[1024]{0:T(1024)S(1)} %get-tuple-element.35, pred[1024]{0:T(1024)(128)(4,1)S(1)} %fusion.72), kind=kOutput, calls=%fused_computation.60 | convolution fusion | flops 406519808 | bytes 1975296 | tf_op jit(solution)/shard_map/dot_general | solution.py:101
  3.6 1.0 fusion.47
  4.6 5.0 %collective-permute-start = (bf16[2,256,384]{2,1,0:T(8,128)(2,1)}, bf16[2,256,384]{2,1,0:T(8,128)(2,1)S(1)}, u32[]{:S(2)}, u32[]{:S(2)}) collective-permute-start(bf16[2,256,384]{2,1,0:T(8,128)(2,1)} %get-tuple-element.24), channel_id=1, source_target_pairs={{0,4},{4,8},{8,12},{1,5},{5,9},{9,13},{2,6},{6,10},{10,14},{3,7},{... | collective-permute-start | bytes 1179656 | tf_op jit(solution)/shard_map/ppermute | solution.py:12
  9.5 1.3 %collective-permute-start.1 = (bf16[2,256,384]{2,1,0:T(8,128)(2,1)}, bf16[2,256,384]{2,1,0:T(8,128)(2,1)S(1)}, u32[]{:S(2)}, u32[]{:S(2)}) collective-permute-start(bf16[2,256,384]{2,1,0:T(8,128)(2,1)} %get-tuple-element.25), channel_id=1, source_target_pairs={{4,0},{8,4},{12,8},{5,1},{9,5},{13,9},{6,2},{10,6},{14,10},{7,3},{... | collective-permute-start | bytes 1179656 | tf_op jit(solution)/shard_map/ppermute | solution.py:12
  10.8 1.3 %collective-permute-start.6 = (bf16[512,384]{1,0:T(8,128)(2,1)S(1)}, bf16[512,384]{1,0:T(8,128)(2,1)}, u32[]{:S(2)}, u32[]{:S(2)}) collective-permute-start(bf16[512,384]{1,0:T(8,128)(2,1)S(1)} %bitcast.143), channel_id=1, source_target_pairs={{2,0},{1,3},{6,4},{5,7},{10,8},{9,11},{14,12},{13,15},{18,16},{17,... | collective-permute-start | bytes 1179656 | tf_op jit(solution)/shard_map/ppermute | solution.py:143
  12.1 1.4 %collective-permute-start.7 = (bf16[512,384]{1,0:T(8,128)(2,1)S(1)}, bf16[512,384]{1,0:T(8,128)(2,1)}, u32[]{:S(2)}, u32[]{:S(2)}) collective-permute-start(bf16[512,384]{1,0:T(8,128)(2,1)S(1)} %bitcast.144), channel_id=1, source_target_pairs={{2,1},{1,2},{6,5},{5,6},{10,9},{9,10},{14,13},{13,14},{18,17},{17,... | collective-permute-start | bytes 1179656 | tf_op jit(solution)/shard_map/ppermute | solution.py:144
  13.6 4.3 %collective-permute-start.5 = (bf16[512,384]{1,0:T(8,128)(2,1)S(1)}, bf16[512,384]{1,0:T(8,128)(2,1)}, u32[]{:S(2)}, u32[]{:S(2)}) collective-permute-start(bf16[512,384]{1,0:T(8,128)(2,1)S(1)} %get-tuple-element.32), channel_id=1, source_target_pairs={{0,2},{2,0},{1,3},{3,1},{4,6},{6,4},{5,7},{7,5},{8,10},{10,8},{9,1... | collective-permute-start | bytes 1179656 | tf_op jit(solution)/shard_map/ppermute | solution.py:146
  17.9 0.1 pad_maximum_fusion.2
  18.0 0.1 constant_dynamic-slice_fusion
  18.1 0.1 collective-permute-done
  18.2 4.0 %collective-permute-done.1 = bf16[2,256,384]{2,1,0:T(8,128)(2,1)S(1)} collective-permute-done((bf16[2,256,384]{2,1,0:T(8,128)(2,1)}, bf16[2,256,384]{2,1,0:T(8,128)(2,1)S(1)}, u32[]{:S(2)}, u32[]{:S(2)}) %collective-permute-start.1) | collective-permute-done | bytes 393248 | tf_op jit(solution)/shard_map/ppermute | solution.py:12
  22.2 0.1 pad_maximum_fusion.3
  22.3 0.6 collective-permute-start.2
  22.9 1.0 %broadcast_select_fusion = bf16[512,384]{1,0:T(8,128)(2,1)S(1)} fusion(bf16[512,384]{1,0:T(8,128)(2,1)} %collective-permute-done.6, bf16[512,384]{1,0:T(8,128)(2,1)} %collective-permute-done.7, pred[]{:T(512)S(6)} %eq.16), kind=kLoop, calls=%fused_computation.100 | loop fusion | flops 196608 | bytes 1179649 | tf_op jit(solution)/shard_map/jit(_where)/select_n | solution.py:145
  24.0 1.3 %collective-permute-start.8 = (bf16[256,384]{1,0:T(8,128)(2,1)S(1)}, bf16[256,384]{1,0:T(8,128)(2,1)S(1)}, u32[]{:S(2)}, u32[]{:S(2)}) collective-permute-start(bf16[256,384]{1,0:T(8,128)(2,1)S(1)} %get-tuple-element.29), channel_id=1, source_target_pairs={{4,0},{8,4},{12,8},{5,1},{9,5},{13,9},{6,2},{10,6},{14,10},{7,3},{... | collective-permute-start | bytes 589832 | tf_op jit(solution)/shard_map/ppermute | solution.py:12
  25.3 8.0 %collective-permute-done.5 = bf16[512,384]{1,0:T(8,128)(2,1)} collective-permute-done((bf16[512,384]{1,0:T(8,128)(2,1)S(1)}, bf16[512,384]{1,0:T(8,128)(2,1)}, u32[]{:S(2)}, u32[]{:S(2)}) %collective-permute-start.5) | collective-permute-done | bytes 393248 | tf_op jit(solution)/shard_map/ppermute | solution.py:146
  33.2 4.5 %collective-permute-start.9 = (bf16[256,384]{1,0:T(8,128)(2,1)S(1)}, bf16[256,384]{1,0:T(8,128)(2,1)S(1)}, u32[]{:S(2)}, u32[]{:S(2)}) collective-permute-start(bf16[256,384]{1,0:T(8,128)(2,1)S(1)} %get-tuple-element.28), channel_id=1, source_target_pairs={{0,4},{4,8},{8,12},{1,5},{5,9},{9,13},{2,6},{6,10},{10,14},{3,7},{... | collective-permute-start | bytes 589832 | tf_op jit(solution)/shard_map/ppermute | solution.py:12
  37.8 1.4 %fusion.87 = f32[384,384]{1,0:T(8,128)S(1)} fusion(bf16[512,384]{1,0:T(8,128)(2,1)} %collective-permute-done.5, bf16[512,384]{1,0:T(8,128)(2,1)S(1)} %broadcast_select_fusion), kind=kOutput, calls=%fused_computation.142 | convolution fusion | flops 150994944 | bytes 1376256 | tf_op jit(solution)/shard_map/dot_general | solution.py:158
  39.2 0.2 fusion.52
  39.4 0.8 convolution_bitcast_fusion.3
  40.2 1.4 %fusion.53 = f32[384,384]{1,0:T(8,128)S(1)} fusion(bf16[512,384]{1,0:T(8,128)(2,1)} %collective-permute-done.5, bf16[256,384]{1,0:T(8,128)(2,1)S(1)} %collective-permute-done.8, bf16[256,384]{1,0:T(8,128)(2,1)S(1)} %get-tuple-element.28), kind=kOutput, calls=%fused_computation.87 | convolution fusion | flops 151781376 | bytes 1376256 | tf_op jit(solution)/shard_map/dot_general | solution.py:158
  41.6 1.4 %fusion.57 = f32[384,384]{1,0:T(8,128)S(1)} fusion(bf16[512,384]{1,0:T(8,128)(2,1)} %collective-permute-done.5, bf16[256,384]{1,0:T(8,128)(2,1)S(1)} %get-tuple-element.29, bf16[256,384]{1,0:T(8,128)(2,1)S(1)} %collective-permute-done.9), kind=kOutput, calls=%fused_computation.91 | convolution fusion | flops 151781376 | bytes 1376256 | tf_op jit(solution)/shard_map/dot_general | solution.py:158
  43.0 0.1 slice_bitcast_fusion.2
  43.1 0.3 broadcast_select_fusion.1
  43.4 0.4 convolution_add_fusion
  43.9 1.9 %collective-permute-start.14 = (f32[2,96,384]{2,1,0:T(8,128)S(1)}, f32[2,96,384]{2,1,0:T(8,128)S(1)}, u32[]{:S(2)}, u32[]{:S(2)}) collective-permute-start(f32[2,96,384]{2,1,0:T(8,128)S(1)} %select_bitcast_fusion.1), channel_id=1, source_target_pairs={{0,4},{4,0},{8,12},{12,8},{1,5},{5,1},{9,13},{13,9},{2,6},{6,2},{1... | collective-permute-start | bytes 884744 | tf_op jit(solution)/shard_map/ppermute | solution.py:76
  45.8 0.4 convolution_add_fusion.2
  46.2 0.4 convolution_add_fusion.1
  46.6 0.1 pad_maximum_fusion.1
  46.8 0.2 collective-permute-start.10
  47.0 8.4 %collective-permute-done.14 = f32[2,96,384]{2,1,0:T(8,128)S(1)} collective-permute-done((f32[2,96,384]{2,1,0:T(8,128)S(1)}, f32[2,96,384]{2,1,0:T(8,128)S(1)}, u32[]{:S(2)}, u32[]{:S(2)}) %collective-permute-start.14) | collective-permute-done | bytes 294944 | tf_op jit(solution)/shard_map/ppermute | solution.py:76
  55.5 2.1 %collective-permute-start.15 = (f32[96,384]{1,0:T(8,128)S(1)}, f32[96,384]{1,0:T(8,128)S(1)}, u32[]{:S(2)}, u32[]{:S(2)}) collective-permute-start(f32[96,384]{1,0:T(8,128)S(1)} %select_bitcast_fusion.7), channel_id=1, source_target_pairs={{0,8},{8,0},{4,12},{12,4},{1,9},{9,1},{5,13},{13,5},{2,10},{10,2},... | collective-permute-start | bytes 442376 | tf_op jit(solution)/shard_map/ppermute | solution.py:81
  57.6 0.8 convolution_bitcast_fusion
  58.5 8.0 %collective-permute-done.15 = f32[96,384]{1,0:T(8,128)S(1)} collective-permute-done((f32[96,384]{1,0:T(8,128)S(1)}, f32[96,384]{1,0:T(8,128)S(1)}, u32[]{:S(2)}, u32[]{:S(2)}) %collective-permute-start.15) | collective-permute-done | bytes 147488 | tf_op jit(solution)/shard_map/ppermute | solution.py:81
  66.5 3.5 %collective-permute-start.16 = (bf16[96,384]{1,0:T(8,128)(2,1)S(1)}, bf16[96,384]{1,0:T(8,128)(2,1)S(1)}, u32[]{:S(2)}, u32[]{:S(2)}) collective-permute-start(bf16[96,384]{1,0:T(8,128)(2,1)S(1)} %fusion.69), channel_id=1, source_target_pairs={{0,8},{8,0},{4,12},{12,4},{1,9},{9,1},{5,13},{13,5},{2,10},{10,2},... | collective-permute-start | bytes 221192 | tf_op jit(solution)/shard_map/ppermute | solution.py:82
  70.0 0.1 fusion.46
  70.1 0.1 collective-permute-start.11
  70.2 1.3 %fusion.39 = bf16[512,384]{1,0:T(8,128)(2,1)S(1)} fusion(f32[512,384]{1,0:T(8,128)S(1)} %copy-done.2, f32[512,384]{1,0:T(8,128)S(1)} %convolution_bitcast_fusion, bf16[512,1,384]{2,0,1:T(8,128)(2,1)S(1)} %get-tuple-element.21, bf16[512,1,384]{2,0,1:T(8,128)(2,1)S(1)} %bitcast.145, bf16[512,1,384]{2,0,1:T(8,128)(2,1)S(1)} %get-tuple-element.5, ...), kind=kOutput, calls=%fused_computation.57 | convolution fusion | flops 458883072 | bytes 4423684 | tf_op jit(solution)/shard_map/tko,kio->ti/dot_general | solution.py:125
  71.5 8.2 %collective-permute-done.16 = bf16[96,384]{1,0:T(8,128)(2,1)S(1)} collective-permute-done((bf16[96,384]{1,0:T(8,128)(2,1)S(1)}, bf16[96,384]{1,0:T(8,128)(2,1)S(1)}, u32[]{:S(2)}, u32[]{:S(2)}) %collective-permute-start.16) | collective-permute-done | bytes 73760 | tf_op jit(solution)/shard_map/ppermute | solution.py:82
  79.8 5.5 %collective-permute-done.11 = f32[192,384]{1,0:T(8,128)S(1)} collective-permute-done((f32[192,384]{1,0:T(8,128)S(1)}, f32[192,384]{1,0:T(8,128)S(1)}, u32[]{:S(2)}, u32[]{:S(2)}) %collective-permute-start.11) | collective-permute-done | bytes 294944 | tf_op jit(solution)/shard_map/ppermute | solution.py:81
  85.4 1.6 %fusion.4 = bf16[1,512,384]{2,1,0:T(8,128)(2,1)} fusion(f32[512,384]{1,0:T(8,128)S(1)} %copy-done.2, f32[512,384]{1,0:T(8,128)S(1)} %convolution_bitcast_fusion.3, bf16[3,384,384]{2,1,0:T(8,128)(2,1)S(1)} %collective-permute-done.4, bf16[512,1,384]{2,0,1:T(8,128)(2,1)S(1)} %get-tuple-element.15, bf16[512,1,384]{2,0,1:T(8,128)(2,1)S(1)} %get-tuple-element.17, ...), kind=kOutput, calls=%fused_computation.14 | convolution fusion | flops 454754304 | bytes 4030464 | tf_op jit(solution)/shard_map/tki,kio->to/dot_general | solution.py:119
  87.0 0.4 broadcast_in_dim.18
  87.4 1.2 %convert_element_type.54 = bf16[1,1024,384]{2,1,0:T(8,128)(2,1)} reshape(bf16[512,2,384]{2,1,0:T(2,128)(2,1)S(1)} %broadcast_in_dim.18) | data formatting | bytes 1572864 | tf_op jit(solution)/shard_map/convert_element_type | solution.py:134
  88.6 4.6 %collective-permute-done.12 = bf16[192,384]{1,0:T(8,128)(2,1)S(1)} collective-permute-done((bf16[192,384]{1,0:T(8,128)(2,1)S(1)}, bf16[192,384]{1,0:T(8,128)(2,1)S(1)}, u32[]{:S(2)}, u32[]{:S(2)}) %collective-permute-start.12) | collective-permute-done | bytes 147488 | tf_op jit(solution)/shard_map/ppermute | solution.py:82
  93.5 8.8 %collective-permute-done.13 = bf16[2,192,384]{2,1,0:T(8,128)(2,1)S(1)} collective-permute-done((bf16[2,192,384]{2,1,0:T(8,128)(2,1)S(1)}, bf16[2,192,384]{2,1,0:T(8,128)(2,1)S(1)}, u32[]{:S(2)}, u32[]{:S(2)}) %collective-permute-start.13) | collective-permute-done | bytes 294944 | tf_op jit(solution)/shard_map/ppermute | solution.py:84
  102.2 0.1 select_bitcast_fusion.3
  102.3 0.1 maximum_convert_fusion
  102.5 1.3 %pad_maximum_fusion = f32[3,384,384]{2,1,0:T(8,128)} fusion(f32[1,384,384]{2,1,0:T(8,128)S(1)} %bitcast.160, f32[1,384,384]{2,1,0:T(8,128)S(1)} %bitcast.158, f32[1,384,384]{2,1,0:T(8,128)S(1)} %bitcast.159), kind=kLoop, calls=%fused_computation.2 | loop fusion | flops 884736 | bytes 3538944 | tf_op jit(solution)/shard_map/stack | solution.py:162
  (36 shorter events, 0.9 us)
Async XLA Ops:
  0.6 17.3 %copy-start = (bf16[3,384,768]{2,1,0:T(8,128)(2,1)S(1)}, bf16[3,384,768]{2,1,0:T(8,128)(2,1)}, u32[]{:S(2)}) copy-start(bf16[3,384,768]{2,1,0:T(8,128)(2,1)} %param.4) | copy-start | bytes 5308420
  0.7 2.9 %copy-start.1 = (bf16[1,512,384]{2,1,0:T(8,128)(2,1)S(1)}, bf16[1,512,384]{2,1,0:T(8,128)(2,1)}, u32[]{:S(2)}) copy-start(bf16[1,512,384]{2,1,0:T(8,128)(2,1)} %param.5) | copy-start | bytes 1179652
  4.6 13.6 %collective-permute-start = (bf16[2,256,384]{2,1,0:T(8,128)(2,1)}, bf16[2,256,384]{2,1,0:T(8,128)(2,1)S(1)}, u32[]{:S(2)}, u32[]{:S(2)}) collective-permute-start(bf16[2,256,384]{2,1,0:T(8,128)(2,1)} %get-tuple-element.24), channel_id=1, source_target_pairs={{0,4},{4,8},{8,12},{1,5},{5,9},{9,13},{2,6},{6,10},{10,14},{3,7},{... | collective-permute-start | bytes 1179656 | tf_op jit(solution)/shard_map/ppermute | solution.py:12
  9.5 12.7 %collective-permute-start.1 = (bf16[2,256,384]{2,1,0:T(8,128)(2,1)}, bf16[2,256,384]{2,1,0:T(8,128)(2,1)S(1)}, u32[]{:S(2)}, u32[]{:S(2)}) collective-permute-start(bf16[2,256,384]{2,1,0:T(8,128)(2,1)} %get-tuple-element.25), channel_id=1, source_target_pairs={{4,0},{8,4},{12,8},{5,1},{9,5},{13,9},{6,2},{10,6},{14,10},{7,3},{... | collective-permute-start | bytes 1179656 | tf_op jit(solution)/shard_map/ppermute | solution.py:12
  10.8 11.5 %collective-permute-start.6 = (bf16[512,384]{1,0:T(8,128)(2,1)S(1)}, bf16[512,384]{1,0:T(8,128)(2,1)}, u32[]{:S(2)}, u32[]{:S(2)}) collective-permute-start(bf16[512,384]{1,0:T(8,128)(2,1)S(1)} %bitcast.143), channel_id=1, source_target_pairs={{2,0},{1,3},{6,4},{5,7},{10,8},{9,11},{14,12},{13,15},{18,16},{17,... | collective-permute-start | bytes 1179656 | tf_op jit(solution)/shard_map/ppermute | solution.py:143
  12.1 10.8 %collective-permute-start.7 = (bf16[512,384]{1,0:T(8,128)(2,1)S(1)}, bf16[512,384]{1,0:T(8,128)(2,1)}, u32[]{:S(2)}, u32[]{:S(2)}) collective-permute-start(bf16[512,384]{1,0:T(8,128)(2,1)S(1)} %bitcast.144), channel_id=1, source_target_pairs={{2,1},{1,2},{6,5},{5,6},{10,9},{9,10},{14,13},{13,14},{18,17},{17,... | collective-permute-start | bytes 1179656 | tf_op jit(solution)/shard_map/ppermute | solution.py:144
  13.6 19.7 %collective-permute-start.5 = (bf16[512,384]{1,0:T(8,128)(2,1)S(1)}, bf16[512,384]{1,0:T(8,128)(2,1)}, u32[]{:S(2)}, u32[]{:S(2)}) collective-permute-start(bf16[512,384]{1,0:T(8,128)(2,1)S(1)} %get-tuple-element.32), channel_id=1, source_target_pairs={{0,2},{2,0},{1,3},{3,1},{4,6},{6,4},{5,7},{7,5},{8,10},{10,8},{9,1... | collective-permute-start | bytes 1179656 | tf_op jit(solution)/shard_map/ppermute | solution.py:146
  18.2 24.9 %collective-permute-start.3 = (bf16[2,512,384]{2,1,0:T(8,128)(2,1)S(1)}, bf16[2,512,384]{2,1,0:T(8,128)(2,1)S(1)}, u32[]{:S(2)}, u32[]{:S(2)}) collective-permute-start(bf16[2,512,384]{2,1,0:T(8,128)(2,1)S(1)} %pad_maximum_fusion.2), channel_id=1, source_target_pairs={{0,1},{1,0},{2,3},{3,2},{4,5},{5,4},{6,7},{7,6},{8,9},{9,8},{10,11... | collective-permute-start | bytes 2359304 | tf_op jit(solution)/shard_map/ppermute | solution.py:105
  22.2 63.2 %collective-permute-start.4 = (bf16[3,384,384]{2,1,0:T(8,128)(2,1)S(1)}, bf16[3,384,384]{2,1,0:T(8,128)(2,1)S(1)}, u32[]{:S(2)}, u32[]{:S(2)}) collective-permute-start(bf16[3,384,384]{2,1,0:T(8,128)(2,1)S(1)} %constant_dynamic-slice_fusion), channel_id=1, source_target_pairs={{0,1},{1,0},{2,3},{3,2},{4,5},{5,4},{6,7},{7,6},{8,9},{9,8},{10,11... | collective-permute-start | bytes 2654216 | tf_op jit(solution)/shard_map/ppermute | solution.py:114
  22.3 20.7 %collective-permute-start.2 = (bf16[2,2,256,384]{3,2,1,0:T(8,128)(2,1)S(1)}, bf16[2,2,256,384]{3,2,1,0:T(8,128)(2,1)S(1)}, u32[]{:S(2)}, u32[]{:S(2)}) collective-permute-start(bf16[2,2,256,384]{3,2,1,0:T(8,128)(2,1)S(1)} %pad_maximum_fusion.3), channel_id=1, source_target_pairs={{0,1},{1,0},{2,3},{3,2},{4,5},{5,4},{6,7},{7,6},{8,9},{9,8},{10,11... | collective-permute-start | bytes 2359304 | tf_op jit(solution)/shard_map/ppermute | solution.py:108
  24.0 16.2 %collective-permute-start.8 = (bf16[256,384]{1,0:T(8,128)(2,1)S(1)}, bf16[256,384]{1,0:T(8,128)(2,1)S(1)}, u32[]{:S(2)}, u32[]{:S(2)}) collective-permute-start(bf16[256,384]{1,0:T(8,128)(2,1)S(1)} %get-tuple-element.29), channel_id=1, source_target_pairs={{4,0},{8,4},{12,8},{5,1},{9,5},{13,9},{6,2},{10,6},{14,10},{7,3},{... | collective-permute-start | bytes 589832 | tf_op jit(solution)/shard_map/ppermute | solution.py:12
  33.2 8.3 %collective-permute-start.9 = (bf16[256,384]{1,0:T(8,128)(2,1)S(1)}, bf16[256,384]{1,0:T(8,128)(2,1)S(1)}, u32[]{:S(2)}, u32[]{:S(2)}) collective-permute-start(bf16[256,384]{1,0:T(8,128)(2,1)S(1)} %get-tuple-element.28), channel_id=1, source_target_pairs={{0,4},{4,8},{8,12},{1,5},{5,9},{9,13},{2,6},{6,10},{10,14},{3,7},{... | collective-permute-start | bytes 589832 | tf_op jit(solution)/shard_map/ppermute | solution.py:12
  43.9 11.5 %collective-permute-start.14 = (f32[2,96,384]{2,1,0:T(8,128)S(1)}, f32[2,96,384]{2,1,0:T(8,128)S(1)}, u32[]{:S(2)}, u32[]{:S(2)}) collective-permute-start(f32[2,96,384]{2,1,0:T(8,128)S(1)} %select_bitcast_fusion.1), channel_id=1, source_target_pairs={{0,4},{4,0},{8,12},{12,8},{1,5},{5,1},{9,13},{13,9},{2,6},{6,2},{1... | collective-permute-start | bytes 884744 | tf_op jit(solution)/shard_map/ppermute | solution.py:76
  46.8 23.2 %collective-permute-start.10 = (f32[2,192,384]{2,1,0:T(8,128)S(1)}, f32[2,192,384]{2,1,0:T(8,128)S(1)}, u32[]{:S(2)}, u32[]{:S(2)}) collective-permute-start(f32[2,192,384]{2,1,0:T(8,128)S(1)} %select_bitcast_fusion), channel_id=1, source_target_pairs={{0,4},{4,0},{8,12},{12,8},{1,5},{5,1},{9,13},{13,9},{2,6},{6,2},{1... | collective-permute-start | bytes 1769480 | tf_op jit(solution)/shard_map/ppermute | solution.py:76
  55.5 11.0 %collective-permute-start.15 = (f32[96,384]{1,0:T(8,128)S(1)}, f32[96,384]{1,0:T(8,128)S(1)}, u32[]{:S(2)}, u32[]{:S(2)}) collective-permute-start(f32[96,384]{1,0:T(8,128)S(1)} %select_bitcast_fusion.7), channel_id=1, source_target_pairs={{0,8},{8,0},{4,12},{12,4},{1,9},{9,1},{5,13},{13,5},{2,10},{10,2},... | collective-permute-start | bytes 442376 | tf_op jit(solution)/shard_map/ppermute | solution.py:81
  66.5 3.7 %copy-start.2 = (f32[512,384]{1,0:T(8,128)S(1)}, f32[512,384]{1,0:T(8,128)}, u32[]{:S(2)}) copy-start(f32[512,384]{1,0:T(8,128)} %get-tuple-element.33) | copy-start | bytes 2359300
  66.5 13.2 %collective-permute-start.16 = (bf16[96,384]{1,0:T(8,128)(2,1)S(1)}, bf16[96,384]{1,0:T(8,128)(2,1)S(1)}, u32[]{:S(2)}, u32[]{:S(2)}) collective-permute-start(bf16[96,384]{1,0:T(8,128)(2,1)S(1)} %fusion.69), channel_id=1, source_target_pairs={{0,8},{8,0},{4,12},{12,4},{1,9},{9,1},{5,13},{13,5},{2,10},{10,2},... | collective-permute-start | bytes 221192 | tf_op jit(solution)/shard_map/ppermute | solution.py:82
  70.1 15.2 %collective-permute-start.11 = (f32[192,384]{1,0:T(8,128)S(1)}, f32[192,384]{1,0:T(8,128)S(1)}, u32[]{:S(2)}, u32[]{:S(2)}) collective-permute-start(f32[192,384]{1,0:T(8,128)S(1)} %select_bitcast_fusion.4), channel_id=1, source_target_pairs={{0,8},{8,0},{4,12},{12,4},{1,9},{9,1},{5,13},{13,5},{2,10},{10,2},... | collective-permute-start | bytes 884744 | tf_op jit(solution)/shard_map/ppermute | solution.py:81
  79.7 13.6 %collective-permute-start.17 = (bf16[2,96,384]{2,1,0:T(8,128)(2,1)S(1)}, bf16[2,96,384]{2,1,0:T(8,128)(2,1)S(1)}, u32[]{:S(2)}, u32[]{:S(2)}) collective-permute-start(bf16[2,96,384]{2,1,0:T(8,128)(2,1)S(1)} %maximum_select_fusion.1), channel_id=1, source_target_pairs={{0,4},{4,0},{8,12},{12,8},{1,5},{5,1},{9,13},{13,9},{2,6},{6,2},{1... | collective-permute-start | bytes 442376 | tf_op jit(solution)/shard_map/ppermute | solution.py:84
  85.3 7.8 %collective-permute-start.12 = (bf16[192,384]{1,0:T(8,128)(2,1)S(1)}, bf16[192,384]{1,0:T(8,128)(2,1)S(1)}, u32[]{:S(2)}, u32[]{:S(2)}) collective-permute-start(bf16[192,384]{1,0:T(8,128)(2,1)S(1)} %fusion.68), channel_id=1, source_target_pairs={{0,8},{8,0},{4,12},{12,4},{1,9},{9,1},{5,13},{13,5},{2,10},{10,2},... | collective-permute-start | bytes 442376 | tf_op jit(solution)/shard_map/ppermute | solution.py:82
  93.2 9.0 %collective-permute-start.13 = (bf16[2,192,384]{2,1,0:T(8,128)(2,1)S(1)}, bf16[2,192,384]{2,1,0:T(8,128)(2,1)S(1)}, u32[]{:S(2)}, u32[]{:S(2)}) collective-permute-start(bf16[2,192,384]{2,1,0:T(8,128)(2,1)S(1)} %maximum_select_fusion), channel_id=1, source_target_pairs={{0,4},{4,0},{8,12},{12,8},{1,5},{5,1},{9,13},{13,9},{2,6},{6,2},{1... | collective-permute-start | bytes 884744 | tf_op jit(solution)/shard_map/ppermute | solution.py:84

commit v10 on v9

--- a/solution.py
+++ b/solution.py
@@ -102,16 +102,19 @@
     activation = jax.nn.gelu(pooled).astype(jnp.bfloat16)
 
     both = jnp.stack([activation, local_cot])
-    par_mid = lax.ppermute(both, "chan", SWAP)
+    w_own = half_of(conv_weight, c, 2)
+    w_other = half_of(conv_weight, 1 - c, 2)
+    swapped = lax.ppermute(
+        jnp.concatenate([both.reshape(-1, width), w_other.reshape(-1, width)], 0), "chan", SWAP
+    )
+    par_mid = swapped[: 2 * rows].reshape(both.shape)
+    w_par = swapped[2 * rows :].reshape(w_other.shape)
     from_prev = shift_from(both[:, rows - spread :], "seq", 1)
     from_next = shift_from(both[:, :spread], "seq", -1)
     par_halo = lax.ppermute(jnp.stack([from_prev, from_next]), "chan", SWAP)
     own_ext = jnp.concatenate([from_prev, both, from_next], 1)
     par_ext = jnp.concatenate([par_halo[0], par_mid, par_halo[1]], 1)
 
-    w_own = half_of(conv_weight, c, 2)
-    w_other = half_of(conv_weight, 1 - c, 2)
-    w_par = lax.ppermute(w_other, "chan", SWAP)
 
     conv_out = jnp.einsum(
         "tki,kio->to", tap_stack(own_ext[0], rows, spread, (0, 1, 2)), w_own,

time: 105 us -> 103 us (0.981)
  waiting for transfers between devices: 55.5 us -> 42.3 us
  local copies, waits for them, and re-layouts: 1.94 us -> 6.93 us
  other arithmetic: 4.77 us -> 9.42 us
  starting transfers between devices: 27.8 us -> 31.2 us
  matrix products: 12.8 us -> 11.5 us
    ppermute x2, waiting for transfers between devices: 13.5 us -> 0.01 us  [line_total(): total = (keep + lax.ppermute(give, 'seq', across)).astype(jnp.bfloat16)]
    ppermute x1, waiting for transfers between devices: 7.95 us -> 0.01 us  [shards(): far_mid = lax.ppermute(activation, 'batch', SWAP)]
    ppermute x4, waiting for transfers between devices: 4.13 us -> 8.39 us  [shift_from(): return lax.ppermute(block, axis, route)]
    ppermute x2, waiting for transfers between devices: 12.8 us -> 16.6 us  [line_total(): other = lax.ppermute(total, 'seq', across)]
    ppermute x2 -> x1, starting transfers between devices: 0.01 us -> 3.71 us  [shards(): lax.ppermute(jnp.concatenate([both.reshape(-1, width), w_other.reshape(-1...]
    ppermute x1, starting transfers between devices: 4.32 us -> 0.97 us  [shards(): far_mid = lax.ppermute(activation, 'batch', SWAP)]
    dot_general x3, matrix products: 4.18 us -> 1.16 us  [shards(): jnp.dot(far_mid.T, far_shifted[k], preferred_element_type=jnp.float32)]
    ppermute x2, waiting for transfers between devices: 8.41 us -> 10.9 us  [line_total(): lax.ppermute(jnp.where(odd, even_set, odd_set), 'seq', pairs)]
  transfers between devices with their start and end apart: 18 -> 17, of which waited for: 9 -> 7; matrix products, arithmetic and copies ran while one was open for 14% -> 22% of each run, Pallas kernels for 0% -> 0%
where the time goes in v10:
time: 103 us; the launch traced here: 102 us
  waiting for transfers between devices  42.3 us (41%)
  starting transfers between devices  31.2 us (30%)
  matrix products  11.5 us (11%)
  other arithmetic  9.42 us (9%)
  local copies, waits for them, and re-layouts  6.93 us (7%)
    ppermute x2, waiting for transfers between devices, line_total(): other = lax.ppermute(total, 'seq', across)  16.6 us
    ppermute x4, starting transfers between devices, shift_from(): return lax.ppermute(block, axis, route)  11 us
    ppermute x2, waiting for transfers between devices, line_total(): lax.ppermute(jnp.where(odd, even_set, odd_set), 'seq', pairs)  10.9 us
    ppermute x4, waiting for transfers between devices, shift_from(): return lax.ppermute(block, axis, route)  8.39 us
    ppermute x2, waiting for transfers between devices, line_total(): far_set = lax.ppermute(own_set, 'seq', pairs)  6.41 us
    ppermute x2, starting transfers between devices, line_total(): other = lax.ppermute(total, 'seq', across)  5.92 us
    ppermute x1, starting transfers between devices, shards(): lax.ppermute(jnp.concatenate([both.reshape(-1, width), w_other.reshape(-1...  3.71 us
    dot_general x3, matrix products, shards(): jnp.dot(own_taps[:, k].T, cot_mine, preferred_element_type=jnp.float32)  3.05 us
  transfers between devices with their start and end apart: 17, of which 7 were waited for; matrix products, arithmetic and copies ran while one was open for 22% of the time, Pallas kernels for 0%

profile of v10, /device:TPU:0, one launch (start us, length us, event | category | flops | bytes accessed | tf_op | source)
XLA Modules:
  0.0 102.4 jit_solution(12732497085712349625)
XLA Ops:
  0.6 1.4 %collective-permute-start.5 = (bf16[512,384]{1,0:T(8,128)(2,1)}, bf16[512,384]{1,0:T(8,128)(2,1)}, u32[]{:S(2)}, u32[]{:S(2)}) collective-permute-start(bf16[512,384]{1,0:T(8,128)(2,1)} %bitcast.157), channel_id=1, source_target_pairs={{2,0},{1,3},{6,4},{5,7},{10,8},{9,11},{14,12},{13,15},{18,16},{17,... | collective-permute-start | bytes 1179656 | tf_op jit(solution)/shard_map/ppermute | solution.py:146
  2.1 1.4 %collective-permute-start.6 = (bf16[512,384]{1,0:T(8,128)(2,1)}, bf16[512,384]{1,0:T(8,128)(2,1)}, u32[]{:S(2)}, u32[]{:S(2)}) collective-permute-start(bf16[512,384]{1,0:T(8,128)(2,1)} %bitcast.158), channel_id=1, source_target_pairs={{2,1},{1,2},{6,5},{5,6},{10,9},{9,10},{14,13},{13,14},{18,17},{17,... | collective-permute-start | bytes 1179656 | tf_op jit(solution)/shard_map/ppermute | solution.py:147
  3.5 2.8 %multiply_convert_fusion = (bf16[512,384]{1,0:T(8,128)(2,1)S(1)}, f32[512,384]{1,0:T(8,128)}) fusion(bf16[1,1024,384]{2,1,0:T(8,128)(2,1)} %param.3, s32[1024]{0:T(1024)S(1)} %get-tuple-element.32, s32[1024]{0:T(1024)S(1)} %get-tuple-element.33, pred[1024]{0:T(1024)(128)(4,1)S(1)} %fusion.72), kind=kOutput, calls=%fused_computation.61 | convolution fusion | flops 406519808 | bytes 1975296 | tf_op jit(solution)/shard_map/dot_general | solution.py:101
  6.3 1.0 fusion.47
  7.3 5.7 %collective-permute-start = (bf16[2,256,384]{2,1,0:T(8,128)(2,1)}, bf16[2,256,384]{2,1,0:T(8,128)(2,1)}, u32[]{:S(2)}, u32[]{:S(2)}) collective-permute-start(bf16[2,256,384]{2,1,0:T(8,128)(2,1)} %get-tuple-element.21), channel_id=1, source_target_pairs={{0,4},{4,8},{8,12},{1,5},{5,9},{9,13},{2,6},{6,10},{10,14},{3,7},{... | collective-permute-start | bytes 1179656 | tf_op jit(solution)/shard_map/ppermute | solution.py:12
  13.0 1.3 %collective-permute-start.1 = (bf16[2,256,384]{2,1,0:T(8,128)(2,1)}, bf16[2,256,384]{2,1,0:T(8,128)(2,1)}, u32[]{:S(2)}, u32[]{:S(2)}) collective-permute-start(bf16[2,256,384]{2,1,0:T(8,128)(2,1)} %get-tuple-element.22), channel_id=1, source_target_pairs={{4,0},{8,4},{12,8},{5,1},{9,5},{13,9},{6,2},{10,6},{14,10},{7,3},{... | collective-permute-start | bytes 1179656 | tf_op jit(solution)/shard_map/ppermute | solution.py:12
  14.3 1.0 pad_maximum_fusion.3
  15.4 1.0 %copy-done.2 = bf16[2,512,384]{2,1,0:T(8,128)(2,1)S(1)} copy-done((bf16[2,512,384]{2,1,0:T(8,128)(2,1)S(1)}, bf16[2,512,384]{2,1,0:T(8,128)(2,1)}, u32[]{:S(2)}) %copy-start.2) | copy-done | bytes 786456
  16.4 1.3 %pad_maximum_fusion.1 = bf16[2176,384]{1,0:T(8,128)(2,1)} fusion(bf16[1152,384]{1,0:T(8,128)(2,1)S(1)} %bitcast.162, bf16[1024,384]{1,0:T(8,128)(2,1)S(1)} %bitcast.163), kind=kLoop, calls=%fused_computation.3 | loop fusion | flops 3342336 | bytes 3342336 | tf_op jit(solution)/shard_map/concatenate | solution.py:108
  17.8 3.7 %collective-permute-start.3 = (bf16[2176,384]{1,0:T(8,128)(2,1)}, bf16[2176,384]{1,0:T(8,128)(2,1)}, u32[]{:S(2)}, u32[]{:S(2)}) collective-permute-start(bf16[2176,384]{1,0:T(8,128)(2,1)} %pad_maximum_fusion.1), channel_id=1, source_target_pairs={{0,1},{1,0},{2,3},{3,2},{4,5},{5,4},{6,7},{7,6},{8,9},{9,8},{10,11... | collective-permute-start | bytes 5013512 | tf_op jit(solution)/shard_map/ppermute | solution.py:107
  21.5 1.0 collective-permute-start.4
  22.4 2.0 %collective-permute-done.1 = bf16[2,256,384]{2,1,0:T(8,128)(2,1)} collective-permute-done((bf16[2,256,384]{2,1,0:T(8,128)(2,1)}, bf16[2,256,384]{2,1,0:T(8,128)(2,1)}, u32[]{:S(2)}, u32[]{:S(2)}) %collective-permute-start.1) | collective-permute-done | bytes 393248 | tf_op jit(solution)/shard_map/ppermute | solution.py:12
  24.5 1.2 %pad_maximum_fusion.4 = bf16[2,2,256,384]{3,2,1,0:T(8,128)(2,1)S(1)} fusion(bf16[1,2,256,384]{3,2,1,0:T(8,128)(2,1)} %bitcast.7, bf16[1,2,256,384]{3,2,1,0:T(8,128)(2,1)} %bitcast.6), kind=kLoop, calls=%fused_computation.59 | loop fusion | flops 393216 | bytes 1572864 | tf_op jit(solution)/shard_map/stack | solution.py:114
  25.7 2.8 %collective-permute-start.2 = (bf16[2,2,256,384]{3,2,1,0:T(8,128)(2,1)S(1)}, bf16[2,2,256,384]{3,2,1,0:T(8,128)(2,1)S(1)}, u32[]{:S(2)}, u32[]{:S(2)}) collective-permute-start(bf16[2,2,256,384]{3,2,1,0:T(8,128)(2,1)S(1)} %pad_maximum_fusion.4), channel_id=1, source_target_pairs={{0,1},{1,0},{2,3},{3,2},{4,5},{5,4},{6,7},{7,6},{8,9},{9,8},{10,11... | collective-permute-start | bytes 2359304 | tf_op jit(solution)/shard_map/ppermute | solution.py:114
  28.5 1.0 %broadcast_select_fusion = bf16[512,384]{1,0:T(8,128)(2,1)S(1)} fusion(bf16[512,384]{1,0:T(8,128)(2,1)} %collective-permute-done.5, bf16[512,384]{1,0:T(8,128)(2,1)} %collective-permute-done.6, pred[]{:T(512)S(6)} %eq.16), kind=kLoop, calls=%fused_computation.102 | loop fusion | flops 196608 | bytes 1179649 | tf_op jit(solution)/shard_map/jit(_where)/select_n | solution.py:148
  29.6 2.8 %collective-permute-start.8 = (bf16[256,384]{1,0:T(8,128)(2,1)S(1)}, bf16[256,384]{1,0:T(8,128)(2,1)S(1)}, u32[]{:S(2)}, u32[]{:S(2)}) collective-permute-start(bf16[256,384]{1,0:T(8,128)(2,1)S(1)} %get-tuple-element.26), channel_id=1, source_target_pairs={{0,4},{4,8},{8,12},{1,5},{5,9},{9,13},{2,6},{6,10},{10,14},{3,7},{... | collective-permute-start | bytes 589832 | tf_op jit(solution)/shard_map/ppermute | solution.py:12
  32.4 1.3 %collective-permute-start.7 = (bf16[256,384]{1,0:T(8,128)(2,1)S(1)}, bf16[256,384]{1,0:T(8,128)(2,1)S(1)}, u32[]{:S(2)}, u32[]{:S(2)}) collective-permute-start(bf16[256,384]{1,0:T(8,128)(2,1)S(1)} %get-tuple-element.27), channel_id=1, source_target_pairs={{4,0},{8,4},{12,8},{5,1},{9,5},{13,9},{6,2},{10,6},{14,10},{7,3},{... | collective-permute-start | bytes 589832 | tf_op jit(solution)/shard_map/ppermute | solution.py:12
  33.7 0.4 fusion.87
  34.1 2.6 %collective-permute-done.8 = bf16[256,384]{1,0:T(8,128)(2,1)S(1)} collective-permute-done((bf16[256,384]{1,0:T(8,128)(2,1)S(1)}, bf16[256,384]{1,0:T(8,128)(2,1)S(1)}, u32[]{:S(2)}, u32[]{:S(2)}) %collective-permute-start.8) | collective-permute-done | bytes 196640 | tf_op jit(solution)/shard_map/ppermute | solution.py:12
  36.7 0.4 fusion.57
  37.1 3.7 %collective-permute-done.7 = bf16[256,384]{1,0:T(8,128)(2,1)S(1)} collective-permute-done((bf16[256,384]{1,0:T(8,128)(2,1)S(1)}, bf16[256,384]{1,0:T(8,128)(2,1)S(1)}, u32[]{:S(2)}, u32[]{:S(2)}) %collective-permute-start.7) | collective-permute-done | bytes 196640 | tf_op jit(solution)/shard_map/ppermute | solution.py:12
  40.8 0.4 fusion.53
  41.3 1.6 %fusion.52 = (bf16[512,1,384]{2,0,1:T(8,128)(2,1)S(1)}, bf16[512,1,384]{2,0,1:T(8,128)(2,1)S(1)}, bf16[512,1,384]{2,0,1:T(8,128)(2,1)S(1)}, bf16[512,1,384]{2,0,1:T(8,128)(2,1)S(1)}, bf16[1,512,384]{2,1,0:T(8,128)(2,1)S(1)}) fusion(bf16[2,256,384]{2,1,0:T(8,128)(2,1)} %collective-permute-done.1, bf16[1,512,384]{2,1,0:T(8,128)(2,1)S(1)} %copy-done.1, ...), kind=kLoop, calls=%fused_computation.79 | loop fusion | flops 4915200 | bytes 3932161 | tf_op jit(solution)/shard_map/stack | solution.py:21
  42.9 0.4 convolution_add_fusion
  43.4 1.6 %collective-permute-start.13 = (f32[2,96,384]{2,1,0:T(8,128)S(1)}, f32[2,96,384]{2,1,0:T(8,128)S(1)}, u32[]{:S(2)}, u32[]{:S(2)}) collective-permute-start(f32[2,96,384]{2,1,0:T(8,128)S(1)} %select_bitcast_fusion.1), channel_id=1, source_target_pairs={{0,4},{4,0},{8,12},{12,8},{1,5},{5,1},{9,13},{13,9},{2,6},{6,2},{1... | collective-permute-start | bytes 884744 | tf_op jit(solution)/shard_map/ppermute | solution.py:76
  45.0 1.3 %convolution_add_fusion.1 = f32[384,384]{1,0:T(8,128)S(1)} fusion(f32[384,384]{1,0:T(8,128)S(1)} %fusion.57, bf16[1,512,384]{2,1,0:T(8,128)(2,1)S(1)} %get-tuple-element.25, bf16[2,256,384]{2,1,0:T(8,128)(2,1)} %collective-permute-done.1, bf16[1,512,384]{2,1,0:T(8,128)(2,1)S(1)} %copy-done.1, bf16[1,512,384]{2,1,0:T(8,128)(2,1)S(1)} %bitcast.152), kind=kOutput, calls=%fused_computation.13 | convolution fusion | flops 152322048 | bytes 2752512 | tf_op jit(solution)/shard_map/dot_general | solution.py:159
  46.3 1.3 %convolution_add_fusion.2 = f32[384,384]{1,0:T(8,128)S(1)} fusion(f32[384,384]{1,0:T(8,128)S(1)} %fusion.53, bf16[1,512,384]{2,1,0:T(8,128)(2,1)S(1)} %get-tuple-element.25, bf16[2,256,384]{2,1,0:T(8,128)(2,1)} %collective-permute-done, bf16[1,512,384]{2,1,0:T(8,128)(2,1)S(1)} %copy-done.1, bf16[1,512,384]{2,1,0:T(8,128)(2,1)S(1)} %bitcast.153), kind=kOutput, calls=%fused_computation.14 | convolution fusion | flops 152322048 | bytes 2752512 | tf_op jit(solution)/shard_map/dot_general | solution.py:159
  47.8 0.5 collective-permute-start.9
  48.3 1.2 %slice.184 = bf16[1024,384]{1,0:T(8,128)(2,1)S(1)} slice(bf16[2176,384]{1,0:T(8,128)(2,1)} %collective-permute-done.3), slice={[0:1024], [0:384]} | slice | bytes 1572864 | tf_op jit(solution)/shard_map/slice | solution.py:110
  49.6 0.2 fusion.50
  49.8 1.2 %slice_bitcast_fusion.3 = (bf16[512,1,384]{2,0,1:T(8,128)(2,1)S(1)}, bf16[512,1,384]{2,0,1:T(8,128)(2,1)S(1)}) fusion(bf16[2176,384]{1,0:T(8,128)(2,1)} %collective-permute-done.3), kind=kLoop, calls=%fused_computation.103 | loop fusion | bytes 1572864 | tf_op jit(solution)/shard_map/stack | solution.py:21
  51.0 0.8 convolution_bitcast_fusion
  51.8 0.3 copy-done.3
  52.1 1.3 %fusion.39 = bf16[512,384]{1,0:T(8,128)(2,1)S(1)} fusion(f32[512,384]{1,0:T(8,128)S(1)} %copy-done.3, f32[512,384]{1,0:T(8,128)S(1)} %convolution_bitcast_fusion, bf16[512,1,384]{2,0,1:T(8,128)(2,1)S(1)} %get-tuple-element.16, bf16[512,1,384]{2,0,1:T(8,128)(2,1)S(1)} %bitcast.159, bf16[512,1,384]{2,0,1:T(8,128)(2,1)S(1)} %get-tuple-element.7, ...), kind=kOutput, calls=%fused_computation.58 | convolution fusion | flops 458883072 | bytes 4423684 | tf_op jit(solution)/shard_map/tko,kio->ti/dot_general | solution.py:128
  53.4 1.3 %slice.187 = bf16[1152,384]{1,0:T(8,128)(2,1)S(1)} slice(bf16[2176,384]{1,0:T(8,128)(2,1)} %collective-permute-done.3), slice={[1024:2176], [0:384]} | slice | bytes 1769472 | tf_op jit(solution)/shard_map/slice | solution.py:111
  54.8 1.4 %collective-permute-start.14 = (f32[96,384]{1,0:T(8,128)S(1)}, f32[96,384]{1,0:T(8,128)S(1)}, u32[]{:S(2)}, u32[]{:S(2)}) collective-permute-start(f32[96,384]{1,0:T(8,128)S(1)} %select_bitcast_fusion.7), channel_id=1, source_target_pairs={{0,8},{8,0},{4,12},{12,4},{1,9},{9,1},{5,13},{13,5},{2,10},{10,2},... | collective-permute-start | bytes 442376 | tf_op jit(solution)/shard_map/ppermute | solution.py:81
  56.1 10.9 %collective-permute-done.9 = f32[2,192,384]{2,1,0:T(8,128)S(1)} collective-permute-done((f32[2,192,384]{2,1,0:T(8,128)S(1)}, f32[2,192,384]{2,1,0:T(8,128)S(1)}, u32[]{:S(2)}, u32[]{:S(2)}) %collective-permute-start.9) | collective-permute-done | bytes 589856 | tf_op jit(solution)/shard_map/ppermute | solution.py:76
  67.3 3.0 %collective-permute-start.15 = (bf16[96,384]{1,0:T(8,128)(2,1)S(1)}, bf16[96,384]{1,0:T(8,128)(2,1)S(1)}, u32[]{:S(2)}, u32[]{:S(2)}) collective-permute-start(bf16[96,384]{1,0:T(8,128)(2,1)S(1)} %fusion.69), channel_id=1, source_target_pairs={{0,8},{8,0},{4,12},{12,4},{1,9},{9,1},{5,13},{13,5},{2,10},{10,2},... | collective-permute-start | bytes 221192 | tf_op jit(solution)/shard_map/ppermute | solution.py:82
  70.3 0.8 convolution_bitcast_fusion.3
  71.1 12.8 %collective-permute-done.15 = bf16[96,384]{1,0:T(8,128)(2,1)S(1)} collective-permute-done((bf16[96,384]{1,0:T(8,128)(2,1)S(1)}, bf16[96,384]{1,0:T(8,128)(2,1)S(1)}, u32[]{:S(2)}, u32[]{:S(2)}) %collective-permute-start.15) | collective-permute-done | bytes 73760 | tf_op jit(solution)/shard_map/ppermute | solution.py:82
  84.0 3.0 %collective-permute-start.11 = (bf16[192,384]{1,0:T(8,128)(2,1)S(1)}, bf16[192,384]{1,0:T(8,128)(2,1)S(1)}, u32[]{:S(2)}, u32[]{:S(2)}) collective-permute-start(bf16[192,384]{1,0:T(8,128)(2,1)S(1)} %fusion.68), channel_id=1, source_target_pairs={{0,8},{8,0},{4,12},{12,4},{1,9},{9,1},{5,13},{13,5},{2,10},{10,2},... | collective-permute-start | bytes 442376 | tf_op jit(solution)/shard_map/ppermute | solution.py:82
  87.0 1.6 %fusion.4 = bf16[1,512,384]{2,1,0:T(8,128)(2,1)} fusion(f32[512,384]{1,0:T(8,128)S(1)} %copy-done.3, f32[512,384]{1,0:T(8,128)S(1)} %convolution_bitcast_fusion.3, bf16[3,384,384]{2,1,0:T(8,128)(2,1)S(1)} %bitcast.170, bf16[512,1,384]{2,0,1:T(8,128)(2,1)S(1)} %get-tuple-element.12, bf16[512,1,384]{2,0,1:T(8,128)(2,1)S(1)} %get-tuple-element.4, ...), kind=kOutput, calls=%fused_computation.15 | convolution fusion | flops 454754304 | bytes 4030464 | tf_op jit(solution)/shard_map/tki,kio->to/dot_general | solution.py:122
  88.6 0.4 broadcast_in_dim.18
  89.0 1.2 %convert_element_type.54 = bf16[1,1024,384]{2,1,0:T(8,128)(2,1)} reshape(bf16[512,2,384]{2,1,0:T(2,128)(2,1)S(1)} %broadcast_in_dim.18) | data formatting | bytes 1572864 | tf_op jit(solution)/shard_map/convert_element_type | solution.py:137
  90.2 3.8 %collective-permute-done.11 = bf16[192,384]{1,0:T(8,128)(2,1)S(1)} collective-permute-done((bf16[192,384]{1,0:T(8,128)(2,1)S(1)}, bf16[192,384]{1,0:T(8,128)(2,1)S(1)}, u32[]{:S(2)}, u32[]{:S(2)}) %collective-permute-start.11) | collective-permute-done | bytes 147488 | tf_op jit(solution)/shard_map/ppermute | solution.py:82
  94.0 0.3 collective-permute-start.12
  94.4 6.4 %collective-permute-done.12 = bf16[2,192,384]{2,1,0:T(8,128)(2,1)S(1)} collective-permute-done((bf16[2,192,384]{2,1,0:T(8,128)(2,1)S(1)}, bf16[2,192,384]{2,1,0:T(8,128)(2,1)S(1)}, u32[]{:S(2)}, u32[]{:S(2)}) %collective-permute-start.12) | collective-permute-done | bytes 294944 | tf_op jit(solution)/shard_map/ppermute | solution.py:84
  101.1 1.3 %pad_maximum_fusion = f32[3,384,384]{2,1,0:T(8,128)} fusion(f32[1,384,384]{2,1,0:T(8,128)S(1)} %bitcast.167, f32[1,384,384]{2,1,0:T(8,128)S(1)} %bitcast.165, f32[1,384,384]{2,1,0:T(8,128)S(1)} %bitcast.166), kind=kLoop, calls=%fused_computation.2 | loop fusion | flops 884736 | bytes 3538944 | tf_op jit(solution)/shard_map/stack | solution.py:165
  (40 shorter events, 1.3 us)
Async XLA Ops:
  0.6 14.7 %copy-start = (bf16[3,384,768]{2,1,0:T(8,128)(2,1)S(1)}, bf16[3,384,768]{2,1,0:T(8,128)(2,1)}, u32[]{:S(2)}) copy-start(bf16[3,384,768]{2,1,0:T(8,128)(2,1)} %param.4) | copy-start | bytes 5308420
  0.6 27.9 %collective-permute-start.5 = (bf16[512,384]{1,0:T(8,128)(2,1)}, bf16[512,384]{1,0:T(8,128)(2,1)}, u32[]{:S(2)}, u32[]{:S(2)}) collective-permute-start(bf16[512,384]{1,0:T(8,128)(2,1)} %bitcast.157), channel_id=1, source_target_pairs={{2,0},{1,3},{6,4},{5,7},{10,8},{9,11},{14,12},{13,15},{18,16},{17,... | collective-permute-start | bytes 1179656 | tf_op jit(solution)/shard_map/ppermute | solution.py:146
  2.1 26.4 %collective-permute-start.6 = (bf16[512,384]{1,0:T(8,128)(2,1)}, bf16[512,384]{1,0:T(8,128)(2,1)}, u32[]{:S(2)}, u32[]{:S(2)}) collective-permute-start(bf16[512,384]{1,0:T(8,128)(2,1)} %bitcast.158), channel_id=1, source_target_pairs={{2,1},{1,2},{6,5},{5,6},{10,9},{9,10},{14,13},{13,14},{18,17},{17,... | collective-permute-start | bytes 1179656 | tf_op jit(solution)/shard_map/ppermute | solution.py:147
  3.5 2.8 %copy-start.1 = (bf16[1,512,384]{2,1,0:T(8,128)(2,1)S(1)}, bf16[1,512,384]{2,1,0:T(8,128)(2,1)}, u32[]{:S(2)}) copy-start(bf16[1,512,384]{2,1,0:T(8,128)(2,1)} %param.5) | copy-start | bytes 1179652
  7.3 14.1 %collective-permute-start = (bf16[2,256,384]{2,1,0:T(8,128)(2,1)}, bf16[2,256,384]{2,1,0:T(8,128)(2,1)}, u32[]{:S(2)}, u32[]{:S(2)}) collective-permute-start(bf16[2,256,384]{2,1,0:T(8,128)(2,1)} %get-tuple-element.21), channel_id=1, source_target_pairs={{0,4},{4,8},{8,12},{1,5},{5,9},{9,13},{2,6},{6,10},{10,14},{3,7},{... | collective-permute-start | bytes 1179656 | tf_op jit(solution)/shard_map/ppermute | solution.py:12
  13.0 11.4 %collective-permute-start.1 = (bf16[2,256,384]{2,1,0:T(8,128)(2,1)}, bf16[2,256,384]{2,1,0:T(8,128)(2,1)}, u32[]{:S(2)}, u32[]{:S(2)}) collective-permute-start(bf16[2,256,384]{2,1,0:T(8,128)(2,1)} %get-tuple-element.22), channel_id=1, source_target_pairs={{4,0},{8,4},{12,8},{5,1},{9,5},{13,9},{6,2},{10,6},{14,10},{7,3},{... | collective-permute-start | bytes 1179656 | tf_op jit(solution)/shard_map/ppermute | solution.py:12
  15.3 1.1 %copy-start.2 = (bf16[2,512,384]{2,1,0:T(8,128)(2,1)S(1)}, bf16[2,512,384]{2,1,0:T(8,128)(2,1)}, u32[]{:S(2)}) copy-start(bf16[2,512,384]{2,1,0:T(8,128)(2,1)} %pad_maximum_fusion.3) | copy-start | bytes 2359300
  17.8 23.6 %collective-permute-start.3 = (bf16[2176,384]{1,0:T(8,128)(2,1)}, bf16[2176,384]{1,0:T(8,128)(2,1)}, u32[]{:S(2)}, u32[]{:S(2)}) collective-permute-start(bf16[2176,384]{1,0:T(8,128)(2,1)} %pad_maximum_fusion.1), channel_id=1, source_target_pairs={{0,1},{1,0},{2,3},{3,2},{4,5},{5,4},{6,7},{7,6},{8,9},{9,8},{10,11... | collective-permute-start | bytes 5013512 | tf_op jit(solution)/shard_map/ppermute | solution.py:107
  21.5 12.2 %collective-permute-start.4 = (bf16[512,384]{1,0:T(8,128)(2,1)S(1)}, bf16[512,384]{1,0:T(8,128)(2,1)S(1)}, u32[]{:S(2)}, u32[]{:S(2)}) collective-permute-start(bf16[512,384]{1,0:T(8,128)(2,1)S(1)} %get-tuple-element.30), channel_id=1, source_target_pairs={{0,2},{2,0},{1,3},{3,1},{4,6},{6,4},{5,7},{7,5},{8,10},{10,8},{9,1... | collective-permute-start | bytes 1179656 | tf_op jit(solution)/shard_map/ppermute | solution.py:149
  25.7 15.6 %collective-permute-start.2 = (bf16[2,2,256,384]{3,2,1,0:T(8,128)(2,1)S(1)}, bf16[2,2,256,384]{3,2,1,0:T(8,128)(2,1)S(1)}, u32[]{:S(2)}, u32[]{:S(2)}) collective-permute-start(bf16[2,2,256,384]{3,2,1,0:T(8,128)(2,1)S(1)} %pad_maximum_fusion.4), channel_id=1, source_target_pairs={{0,1},{1,0},{2,3},{3,2},{4,5},{5,4},{6,7},{7,6},{8,9},{9,8},{10,11... | collective-permute-start | bytes 2359304 | tf_op jit(solution)/shard_map/ppermute | solution.py:114
  29.6 7.1 %collective-permute-start.8 = (bf16[256,384]{1,0:T(8,128)(2,1)S(1)}, bf16[256,384]{1,0:T(8,128)(2,1)S(1)}, u32[]{:S(2)}, u32[]{:S(2)}) collective-permute-start(bf16[256,384]{1,0:T(8,128)(2,1)S(1)} %get-tuple-element.26), channel_id=1, source_target_pairs={{0,4},{4,8},{8,12},{1,5},{5,9},{9,13},{2,6},{6,10},{10,14},{3,7},{... | collective-permute-start | bytes 589832 | tf_op jit(solution)/shard_map/ppermute | solution.py:12
  32.4 8.5 %collective-permute-start.7 = (bf16[256,384]{1,0:T(8,128)(2,1)S(1)}, bf16[256,384]{1,0:T(8,128)(2,1)S(1)}, u32[]{:S(2)}, u32[]{:S(2)}) collective-permute-start(bf16[256,384]{1,0:T(8,128)(2,1)S(1)} %get-tuple-element.27), channel_id=1, source_target_pairs={{4,0},{8,4},{12,8},{5,1},{9,5},{13,9},{6,2},{10,6},{14,10},{7,3},{... | collective-permute-start | bytes 589832 | tf_op jit(solution)/shard_map/ppermute | solution.py:12
  43.4 11.3 %collective-permute-start.13 = (f32[2,96,384]{2,1,0:T(8,128)S(1)}, f32[2,96,384]{2,1,0:T(8,128)S(1)}, u32[]{:S(2)}, u32[]{:S(2)}) collective-permute-start(f32[2,96,384]{2,1,0:T(8,128)S(1)} %select_bitcast_fusion.1), channel_id=1, source_target_pairs={{0,4},{4,0},{8,12},{12,8},{1,5},{5,1},{9,13},{13,9},{2,6},{6,2},{1... | collective-permute-start | bytes 884744 | tf_op jit(solution)/shard_map/ppermute | solution.py:76
  47.8 19.2 %collective-permute-start.9 = (f32[2,192,384]{2,1,0:T(8,128)S(1)}, f32[2,192,384]{2,1,0:T(8,128)S(1)}, u32[]{:S(2)}, u32[]{:S(2)}) collective-permute-start(f32[2,192,384]{2,1,0:T(8,128)S(1)} %select_bitcast_fusion), channel_id=1, source_target_pairs={{0,4},{4,0},{8,12},{12,8},{1,5},{5,1},{9,13},{13,9},{2,6},{6,2},{1... | collective-permute-start | bytes 1769480 | tf_op jit(solution)/shard_map/ppermute | solution.py:76
  51.0 1.1 %copy-start.3 = (f32[512,384]{1,0:T(8,128)S(1)}, f32[512,384]{1,0:T(8,128)}, u32[]{:S(2)}) copy-start(f32[512,384]{1,0:T(8,128)} %get-tuple-element.31) | copy-start | bytes 2359300
  54.8 12.5 %collective-permute-start.14 = (f32[96,384]{1,0:T(8,128)S(1)}, f32[96,384]{1,0:T(8,128)S(1)}, u32[]{:S(2)}, u32[]{:S(2)}) collective-permute-start(f32[96,384]{1,0:T(8,128)S(1)} %select_bitcast_fusion.7), channel_id=1, source_target_pairs={{0,8},{8,0},{4,12},{12,4},{1,9},{9,1},{5,13},{13,5},{2,10},{10,2},... | collective-permute-start | bytes 442376 | tf_op jit(solution)/shard_map/ppermute | solution.py:81
  67.2 16.8 %collective-permute-start.10 = (f32[192,384]{1,0:T(8,128)S(1)}, f32[192,384]{1,0:T(8,128)S(1)}, u32[]{:S(2)}, u32[]{:S(2)}) collective-permute-start(f32[192,384]{1,0:T(8,128)S(1)} %select_bitcast_fusion.4), channel_id=1, source_target_pairs={{0,8},{8,0},{4,12},{12,4},{1,9},{9,1},{5,13},{13,5},{2,10},{10,2},... | collective-permute-start | bytes 884744 | tf_op jit(solution)/shard_map/ppermute | solution.py:81
  67.3 16.6 %collective-permute-start.15 = (bf16[96,384]{1,0:T(8,128)(2,1)S(1)}, bf16[96,384]{1,0:T(8,128)(2,1)S(1)}, u32[]{:S(2)}, u32[]{:S(2)}) collective-permute-start(bf16[96,384]{1,0:T(8,128)(2,1)S(1)} %fusion.69), channel_id=1, source_target_pairs={{0,8},{8,0},{4,12},{12,4},{1,9},{9,1},{5,13},{13,5},{2,10},{10,2},... | collective-permute-start | bytes 221192 | tf_op jit(solution)/shard_map/ppermute | solution.py:82
  83.9 10.4 %collective-permute-start.16 = (bf16[2,96,384]{2,1,0:T(8,128)(2,1)S(1)}, bf16[2,96,384]{2,1,0:T(8,128)(2,1)S(1)}, u32[]{:S(2)}, u32[]{:S(2)}) collective-permute-start(bf16[2,96,384]{2,1,0:T(8,128)(2,1)S(1)} %maximum_select_fusion.1), channel_id=1, source_target_pairs={{0,4},{4,0},{8,12},{12,8},{1,5},{5,1},{9,13},{13,9},{2,6},{6,2},{1... | collective-permute-start | bytes 442376 | tf_op jit(solution)/shard_map/ppermute | solution.py:84
  84.0 9.9 %collective-permute-start.11 = (bf16[192,384]{1,0:T(8,128)(2,1)S(1)}, bf16[192,384]{1,0:T(8,128)(2,1)S(1)}, u32[]{:S(2)}, u32[]{:S(2)}) collective-permute-start(bf16[192,384]{1,0:T(8,128)(2,1)S(1)} %fusion.68), channel_id=1, source_target_pairs={{0,8},{8,0},{4,12},{12,4},{1,9},{9,1},{5,13},{13,5},{2,10},{10,2},... | collective-permute-start | bytes 442376 | tf_op jit(solution)/shard_map/ppermute | solution.py:82
  94.0 6.8 %collective-permute-start.12 = (bf16[2,192,384]{2,1,0:T(8,128)(2,1)S(1)}, bf16[2,192,384]{2,1,0:T(8,128)(2,1)S(1)}, u32[]{:S(2)}, u32[]{:S(2)}) collective-permute-start(bf16[2,192,384]{2,1,0:T(8,128)(2,1)S(1)} %maximum_select_fusion), channel_id=1, source_target_pairs={{0,4},{4,0},{8,12},{12,8},{1,5},{5,1},{9,13},{13,9},{2,6},{6,2},{1... | collective-permute-start | bytes 884744 | tf_op jit(solution)/shard_map/ppermute | solution.py:84

commit v11 on v10

--- a/solution.py
+++ b/solution.py
@@ -47,24 +47,6 @@
     return [totals[n] for n in range(count)]
 
 
-def seq_total(block):
-    count = lax.axis_size("seq")
-    s = lax.axis_index("seq")
-    rows = block.shape[1] // count
-    quarters = block.reshape(block.shape[0], count, rows, block.shape[2])
-    mine = lax.dynamic_index_in_dim(quarters, s, 1, keepdims=False)
-    for d in range(1, count):
-        going = lax.dynamic_index_in_dim(quarters, (s + d) % count, 1, keepdims=False)
-        mine = mine + lax.ppermute(going, "seq", [(j, (j + d) % count) for j in range(count)])
-    mine = mine.astype(jnp.bfloat16)
-    gathered = [mine] + [
-        lax.ppermute(mine, "seq", [(j, (j + d) % count) for j in range(count)]) for d in range(1, count)
-    ]
-    stacked = jnp.stack(gathered, 1)
-    order = (s - jnp.arange(count)) % count
-    return jnp.take(stacked, order, axis=1).reshape(block.shape).astype(jnp.float32)
-
-
 def line_total(block):
     s = lax.axis_index("seq")
     odd = (s % 2) == 1
@@ -101,6 +83,13 @@
     pooled = jnp.dot(pairing, local_in, preferred_element_type=jnp.float32)
     activation = jax.nn.gelu(pooled).astype(jnp.bfloat16)
 
+    if lax.axis_size("batch") == 2:
+        b = lax.axis_index("batch")
+        same_core = lax.ppermute(local_cot, ("batch", "chan"), [(2, 0), (1, 3)])
+        cross_core = lax.ppermute(local_cot, ("batch", "chan"), [(2, 1), (1, 2)])
+        far_cot = jnp.where(b == c, same_core, cross_core)
+        far_mid = lax.ppermute(activation, "batch", SWAP)
+
     both = jnp.stack([activation, local_cot])
     w_own = half_of(conv_weight, c, 2)
     w_other = half_of(conv_weight, 1 - c, 2)
@@ -114,7 +103,6 @@
     par_halo = lax.ppermute(jnp.stack([from_prev, from_next]), "chan", SWAP)
     own_ext = jnp.concatenate([from_prev, both, from_next], 1)
     par_ext = jnp.concatenate([par_halo[0], par_mid, par_halo[1]], 1)
-
 
     conv_out = jnp.einsum(
         "tki,kio->to", tap_stack(own_ext[0], rows, spread, (0, 1, 2)), w_own,
@@ -141,12 +129,7 @@
     batch_count = lax.axis_size("batch")
     seq_count = lax.axis_size("seq")
     if batch_count == 2:
-        b = lax.axis_index("batch")
         cot_mine = jnp.where(b == c, local_cot, par_cot)
-        same_core = lax.ppermute(local_cot, ("batch", "chan"), [(2, 0), (1, 3)])
-        cross_core = lax.ppermute(local_cot, ("batch", "chan"), [(2, 1), (1, 2)])
-        far_cot = jnp.where(b == c, same_core, cross_core)
-        far_mid = lax.ppermute(activation, "batch", SWAP)
         cot_next = shift_from(far_cot[:spread], "seq", -1)
         cot_prev = shift_from(far_cot[rows - spread :], "seq", 1)
         far_shifted = {

time: 103 us -> 103 us (level)
  no operation moved by 1% of the time
where the time goes in v11:
time: 103 us; the launch traced here: 102 us
  waiting for transfers between devices  42.3 us (41%)
  starting transfers between devices  31.2 us (30%)
  matrix products  11.5 us (11%)
  other arithmetic  9.42 us (9%)
  local copies, waits for them, and re-layouts  6.93 us (7%)
    ppermute x2, waiting for transfers between devices, line_total(): other = lax.ppermute(total, 'seq', across)  16.6 us
    ppermute x4, starting transfers between devices, shift_from(): return lax.ppermute(block, axis, route)  11 us
    ppermute x2, waiting for transfers between devices, line_total(): lax.ppermute(jnp.where(odd, even_set, odd_set), 'seq', pairs)  10.9 us
    ppermute x4, waiting for transfers between devices, shift_from(): return lax.ppermute(block, axis, route)  8.39 us
    ppermute x2, waiting for transfers between devices, line_total(): far_set = lax.ppermute(own_set, 'seq', pairs)  6.41 us
    ppermute x2, starting transfers between devices, line_total(): other = lax.ppermute(total, 'seq', across)  5.92 us
    ppermute x1, starting transfers between devices, shards(): lax.ppermute(jnp.concatenate([both.reshape(-1, width), w_other.reshape(-1...  3.71 us
    dot_general x3, matrix products, shards(): jnp.dot(own_taps[:, k].T, cot_mine, preferred_element_type=jnp.float32)  3.05 us
  transfers between devices with their start and end apart: 17, of which 7 were waited for; matrix products, arithmetic and copies ran while one was open for 22% of the time, Pallas kernels for 0%

profile of v11, /device:TPU:0, one launch (start us, length us, event | category | flops | bytes accessed | tf_op | source)
XLA Modules:
  0.0 102.4 jit_solution(12732497085712349625)
XLA Ops:
  0.6 1.4 %collective-permute-start.5 = (bf16[512,384]{1,0:T(8,128)(2,1)}, bf16[512,384]{1,0:T(8,128)(2,1)}, u32[]{:S(2)}, u32[]{:S(2)}) collective-permute-start(bf16[512,384]{1,0:T(8,128)(2,1)} %bitcast.157), channel_id=1, source_target_pairs={{2,0},{1,3},{6,4},{5,7},{10,8},{9,11},{14,12},{13,15},{18,16},{17,... | collective-permute-start | bytes 1179656 | tf_op jit(solution)/shard_map/ppermute | solution.py:88
  2.1 1.4 %collective-permute-start.6 = (bf16[512,384]{1,0:T(8,128)(2,1)}, bf16[512,384]{1,0:T(8,128)(2,1)}, u32[]{:S(2)}, u32[]{:S(2)}) collective-permute-start(bf16[512,384]{1,0:T(8,128)(2,1)} %bitcast.158), channel_id=1, source_target_pairs={{2,1},{1,2},{6,5},{5,6},{10,9},{9,10},{14,13},{13,14},{18,17},{17,... | collective-permute-start | bytes 1179656 | tf_op jit(solution)/shard_map/ppermute | solution.py:89
  3.5 2.8 %multiply_convert_fusion = (bf16[512,384]{1,0:T(8,128)(2,1)S(1)}, f32[512,384]{1,0:T(8,128)}) fusion(bf16[1,1024,384]{2,1,0:T(8,128)(2,1)} %param.3, s32[1024]{0:T(1024)S(1)} %get-tuple-element.32, s32[1024]{0:T(1024)S(1)} %get-tuple-element.33, pred[1024]{0:T(1024)(128)(4,1)S(1)} %fusion.72), kind=kOutput, calls=%fused_computation.61 | convolution fusion | flops 406519808 | bytes 1975296 | tf_op jit(solution)/shard_map/dot_general | solution.py:83
  6.3 1.0 fusion.47
  7.3 5.7 %collective-permute-start = (bf16[2,256,384]{2,1,0:T(8,128)(2,1)}, bf16[2,256,384]{2,1,0:T(8,128)(2,1)}, u32[]{:S(2)}, u32[]{:S(2)}) collective-permute-start(bf16[2,256,384]{2,1,0:T(8,128)(2,1)} %get-tuple-element.21), channel_id=1, source_target_pairs={{0,4},{4,8},{8,12},{1,5},{5,9},{9,13},{2,6},{6,10},{10,14},{3,7},{... | collective-permute-start | bytes 1179656 | tf_op jit(solution)/shard_map/ppermute | solution.py:12
  13.0 1.3 %collective-permute-start.1 = (bf16[2,256,384]{2,1,0:T(8,128)(2,1)}, bf16[2,256,384]{2,1,0:T(8,128)(2,1)}, u32[]{:S(2)}, u32[]{:S(2)}) collective-permute-start(bf16[2,256,384]{2,1,0:T(8,128)(2,1)} %get-tuple-element.22), channel_id=1, source_target_pairs={{4,0},{8,4},{12,8},{5,1},{9,5},{13,9},{6,2},{10,6},{14,10},{7,3},{... | collective-permute-start | bytes 1179656 | tf_op jit(solution)/shard_map/ppermute | solution.py:12
  14.3 1.0 pad_maximum_fusion.3
  15.4 1.0 %copy-done.2 = bf16[2,512,384]{2,1,0:T(8,128)(2,1)S(1)} copy-done((bf16[2,512,384]{2,1,0:T(8,128)(2,1)S(1)}, bf16[2,512,384]{2,1,0:T(8,128)(2,1)}, u32[]{:S(2)}) %copy-start.2) | copy-done | bytes 786456
  16.4 1.3 %pad_maximum_fusion.1 = bf16[2176,384]{1,0:T(8,128)(2,1)} fusion(bf16[1152,384]{1,0:T(8,128)(2,1)S(1)} %bitcast.162, bf16[1024,384]{1,0:T(8,128)(2,1)S(1)} %bitcast.163), kind=kLoop, calls=%fused_computation.3 | loop fusion | flops 3342336 | bytes 3342336 | tf_op jit(solution)/shard_map/concatenate | solution.py:97
  17.8 3.7 %collective-permute-start.3 = (bf16[2176,384]{1,0:T(8,128)(2,1)}, bf16[2176,384]{1,0:T(8,128)(2,1)}, u32[]{:S(2)}, u32[]{:S(2)}) collective-permute-start(bf16[2176,384]{1,0:T(8,128)(2,1)} %pad_maximum_fusion.1), channel_id=1, source_target_pairs={{0,1},{1,0},{2,3},{3,2},{4,5},{5,4},{6,7},{7,6},{8,9},{9,8},{10,11... | collective-permute-start | bytes 5013512 | tf_op jit(solution)/shard_map/ppermute | solution.py:96
  21.5 1.0 collective-permute-start.4
  22.4 2.0 %collective-permute-done.1 = bf16[2,256,384]{2,1,0:T(8,128)(2,1)} collective-permute-done((bf16[2,256,384]{2,1,0:T(8,128)(2,1)}, bf16[2,256,384]{2,1,0:T(8,128)(2,1)}, u32[]{:S(2)}, u32[]{:S(2)}) %collective-permute-start.1) | collective-permute-done | bytes 393248 | tf_op jit(solution)/shard_map/ppermute | solution.py:12
  24.5 1.2 %pad_maximum_fusion.4 = bf16[2,2,256,384]{3,2,1,0:T(8,128)(2,1)S(1)} fusion(bf16[1,2,256,384]{3,2,1,0:T(8,128)(2,1)} %bitcast.7, bf16[1,2,256,384]{3,2,1,0:T(8,128)(2,1)} %bitcast.6), kind=kLoop, calls=%fused_computation.59 | loop fusion | flops 393216 | bytes 1572864 | tf_op jit(solution)/shard_map/stack | solution.py:103
  25.7 2.8 %collective-permute-start.2 = (bf16[2,2,256,384]{3,2,1,0:T(8,128)(2,1)S(1)}, bf16[2,2,256,384]{3,2,1,0:T(8,128)(2,1)S(1)}, u32[]{:S(2)}, u32[]{:S(2)}) collective-permute-start(bf16[2,2,256,384]{3,2,1,0:T(8,128)(2,1)S(1)} %pad_maximum_fusion.4), channel_id=1, source_target_pairs={{0,1},{1,0},{2,3},{3,2},{4,5},{5,4},{6,7},{7,6},{8,9},{9,8},{10,11... | collective-permute-start | bytes 2359304 | tf_op jit(solution)/shard_map/ppermute | solution.py:103
  28.5 1.0 %broadcast_select_fusion = bf16[512,384]{1,0:T(8,128)(2,1)S(1)} fusion(bf16[512,384]{1,0:T(8,128)(2,1)} %collective-permute-done.5, bf16[512,384]{1,0:T(8,128)(2,1)} %collective-permute-done.6, pred[]{:T(512)S(6)} %eq.16), kind=kLoop, calls=%fused_computation.102 | loop fusion | flops 196608 | bytes 1179649 | tf_op jit(solution)/shard_map/jit(_where)/select_n | solution.py:90
  29.6 2.8 %collective-permute-start.8 = (bf16[256,384]{1,0:T(8,128)(2,1)S(1)}, bf16[256,384]{1,0:T(8,128)(2,1)S(1)}, u32[]{:S(2)}, u32[]{:S(2)}) collective-permute-start(bf16[256,384]{1,0:T(8,128)(2,1)S(1)} %get-tuple-element.26), channel_id=1, source_target_pairs={{0,4},{4,8},{8,12},{1,5},{5,9},{9,13},{2,6},{6,10},{10,14},{3,7},{... | collective-permute-start | bytes 589832 | tf_op jit(solution)/shard_map/ppermute | solution.py:12
  32.4 1.3 %collective-permute-start.7 = (bf16[256,384]{1,0:T(8,128)(2,1)S(1)}, bf16[256,384]{1,0:T(8,128)(2,1)S(1)}, u32[]{:S(2)}, u32[]{:S(2)}) collective-permute-start(bf16[256,384]{1,0:T(8,128)(2,1)S(1)} %get-tuple-element.27), channel_id=1, source_target_pairs={{4,0},{8,4},{12,8},{5,1},{9,5},{13,9},{6,2},{10,6},{14,10},{7,3},{... | collective-permute-start | bytes 589832 | tf_op jit(solution)/shard_map/ppermute | solution.py:12
  33.7 0.4 fusion.87
  34.1 2.6 %collective-permute-done.8 = bf16[256,384]{1,0:T(8,128)(2,1)S(1)} collective-permute-done((bf16[256,384]{1,0:T(8,128)(2,1)S(1)}, bf16[256,384]{1,0:T(8,128)(2,1)S(1)}, u32[]{:S(2)}, u32[]{:S(2)}) %collective-permute-start.8) | collective-permute-done | bytes 196640 | tf_op jit(solution)/shard_map/ppermute | solution.py:12
  36.7 0.4 fusion.57
  37.1 3.7 %collective-permute-done.7 = bf16[256,384]{1,0:T(8,128)(2,1)S(1)} collective-permute-done((bf16[256,384]{1,0:T(8,128)(2,1)S(1)}, bf16[256,384]{1,0:T(8,128)(2,1)S(1)}, u32[]{:S(2)}, u32[]{:S(2)}) %collective-permute-start.7) | collective-permute-done | bytes 196640 | tf_op jit(solution)/shard_map/ppermute | solution.py:12
  40.8 0.4 fusion.53
  41.3 1.6 %fusion.52 = (bf16[512,1,384]{2,0,1:T(8,128)(2,1)S(1)}, bf16[512,1,384]{2,0,1:T(8,128)(2,1)S(1)}, bf16[512,1,384]{2,0,1:T(8,128)(2,1)S(1)}, bf16[512,1,384]{2,0,1:T(8,128)(2,1)S(1)}, bf16[1,512,384]{2,1,0:T(8,128)(2,1)S(1)}) fusion(bf16[2,256,384]{2,1,0:T(8,128)(2,1)} %collective-permute-done.1, bf16[1,512,384]{2,1,0:T(8,128)(2,1)S(1)} %copy-done.1, ...), kind=kLoop, calls=%fused_computation.79 | loop fusion | flops 4915200 | bytes 3932161 | tf_op jit(solution)/shard_map/stack | solution.py:21
  42.9 0.4 convolution_add_fusion
  43.4 1.6 %collective-permute-start.13 = (f32[2,96,384]{2,1,0:T(8,128)S(1)}, f32[2,96,384]{2,1,0:T(8,128)S(1)}, u32[]{:S(2)}, u32[]{:S(2)}) collective-permute-start(f32[2,96,384]{2,1,0:T(8,128)S(1)} %select_bitcast_fusion.1), channel_id=1, source_target_pairs={{0,4},{4,0},{8,12},{12,8},{1,5},{5,1},{9,13},{13,9},{2,6},{6,2},{1... | collective-permute-start | bytes 884744 | tf_op jit(solution)/shard_map/ppermute | solution.py:58
  45.0 1.3 %convolution_add_fusion.1 = f32[384,384]{1,0:T(8,128)S(1)} fusion(f32[384,384]{1,0:T(8,128)S(1)} %fusion.57, bf16[1,512,384]{2,1,0:T(8,128)(2,1)S(1)} %get-tuple-element.25, bf16[2,256,384]{2,1,0:T(8,128)(2,1)} %collective-permute-done.1, bf16[1,512,384]{2,1,0:T(8,128)(2,1)S(1)} %copy-done.1, bf16[1,512,384]{2,1,0:T(8,128)(2,1)S(1)} %bitcast.152), kind=kOutput, calls=%fused_computation.13 | convolution fusion | flops 152322048 | bytes 2752512 | tf_op jit(solution)/shard_map/dot_general | solution.py:142
  46.3 1.3 %convolution_add_fusion.2 = f32[384,384]{1,0:T(8,128)S(1)} fusion(f32[384,384]{1,0:T(8,128)S(1)} %fusion.53, bf16[1,512,384]{2,1,0:T(8,128)(2,1)S(1)} %get-tuple-element.25, bf16[2,256,384]{2,1,0:T(8,128)(2,1)} %collective-permute-done, bf16[1,512,384]{2,1,0:T(8,128)(2,1)S(1)} %copy-done.1, bf16[1,512,384]{2,1,0:T(8,128)(2,1)S(1)} %bitcast.153), kind=kOutput, calls=%fused_computation.14 | convolution fusion | flops 152322048 | bytes 2752512 | tf_op jit(solution)/shard_map/dot_general | solution.py:142
  47.8 0.5 collective-permute-start.9
  48.3 1.2 %slice.184 = bf16[1024,384]{1,0:T(8,128)(2,1)S(1)} slice(bf16[2176,384]{1,0:T(8,128)(2,1)} %collective-permute-done.3), slice={[0:1024], [0:384]} | slice | bytes 1572864 | tf_op jit(solution)/shard_map/slice | solution.py:99
  49.6 0.2 fusion.50
  49.8 1.2 %slice_bitcast_fusion.3 = (bf16[512,1,384]{2,0,1:T(8,128)(2,1)S(1)}, bf16[512,1,384]{2,0,1:T(8,128)(2,1)S(1)}) fusion(bf16[2176,384]{1,0:T(8,128)(2,1)} %collective-permute-done.3), kind=kLoop, calls=%fused_computation.103 | loop fusion | bytes 1572864 | tf_op jit(solution)/shard_map/stack | solution.py:21
  51.0 0.8 convolution_bitcast_fusion
  51.8 0.3 copy-done.3
  52.1 1.3 %fusion.39 = bf16[512,384]{1,0:T(8,128)(2,1)S(1)} fusion(f32[512,384]{1,0:T(8,128)S(1)} %copy-done.3, f32[512,384]{1,0:T(8,128)S(1)} %convolution_bitcast_fusion, bf16[512,1,384]{2,0,1:T(8,128)(2,1)S(1)} %get-tuple-element.16, bf16[512,1,384]{2,0,1:T(8,128)(2,1)S(1)} %bitcast.159, bf16[512,1,384]{2,0,1:T(8,128)(2,1)S(1)} %get-tuple-element.7, ...), kind=kOutput, calls=%fused_computation.58 | convolution fusion | flops 458883072 | bytes 4423684 | tf_op jit(solution)/shard_map/tko,kio->ti/dot_general | solution.py:116
  53.4 1.3 %slice.187 = bf16[1152,384]{1,0:T(8,128)(2,1)S(1)} slice(bf16[2176,384]{1,0:T(8,128)(2,1)} %collective-permute-done.3), slice={[1024:2176], [0:384]} | slice | bytes 1769472 | tf_op jit(solution)/shard_map/slice | solution.py:100
  54.8 1.4 %collective-permute-start.14 = (f32[96,384]{1,0:T(8,128)S(1)}, f32[96,384]{1,0:T(8,128)S(1)}, u32[]{:S(2)}, u32[]{:S(2)}) collective-permute-start(f32[96,384]{1,0:T(8,128)S(1)} %select_bitcast_fusion.7), channel_id=1, source_target_pairs={{0,8},{8,0},{4,12},{12,4},{1,9},{9,1},{5,13},{13,5},{2,10},{10,2},... | collective-permute-start | bytes 442376 | tf_op jit(solution)/shard_map/ppermute | solution.py:63
  56.1 10.9 %collective-permute-done.9 = f32[2,192,384]{2,1,0:T(8,128)S(1)} collective-permute-done((f32[2,192,384]{2,1,0:T(8,128)S(1)}, f32[2,192,384]{2,1,0:T(8,128)S(1)}, u32[]{:S(2)}, u32[]{:S(2)}) %collective-permute-start.9) | collective-permute-done | bytes 589856 | tf_op jit(solution)/shard_map/ppermute | solution.py:58
  67.3 3.0 %collective-permute-start.15 = (bf16[96,384]{1,0:T(8,128)(2,1)S(1)}, bf16[96,384]{1,0:T(8,128)(2,1)S(1)}, u32[]{:S(2)}, u32[]{:S(2)}) collective-permute-start(bf16[96,384]{1,0:T(8,128)(2,1)S(1)} %fusion.69), channel_id=1, source_target_pairs={{0,8},{8,0},{4,12},{12,4},{1,9},{9,1},{5,13},{13,5},{2,10},{10,2},... | collective-permute-start | bytes 221192 | tf_op jit(solution)/shard_map/ppermute | solution.py:64
  70.3 0.8 convolution_bitcast_fusion.3
  71.1 12.8 %collective-permute-done.15 = bf16[96,384]{1,0:T(8,128)(2,1)S(1)} collective-permute-done((bf16[96,384]{1,0:T(8,128)(2,1)S(1)}, bf16[96,384]{1,0:T(8,128)(2,1)S(1)}, u32[]{:S(2)}, u32[]{:S(2)}) %collective-permute-start.15) | collective-permute-done | bytes 73760 | tf_op jit(solution)/shard_map/ppermute | solution.py:64
  84.0 3.0 %collective-permute-start.11 = (bf16[192,384]{1,0:T(8,128)(2,1)S(1)}, bf16[192,384]{1,0:T(8,128)(2,1)S(1)}, u32[]{:S(2)}, u32[]{:S(2)}) collective-permute-start(bf16[192,384]{1,0:T(8,128)(2,1)S(1)} %fusion.68), channel_id=1, source_target_pairs={{0,8},{8,0},{4,12},{12,4},{1,9},{9,1},{5,13},{13,5},{2,10},{10,2},... | collective-permute-start | bytes 442376 | tf_op jit(solution)/shard_map/ppermute | solution.py:64
  87.0 1.6 %fusion.4 = bf16[1,512,384]{2,1,0:T(8,128)(2,1)} fusion(f32[512,384]{1,0:T(8,128)S(1)} %copy-done.3, f32[512,384]{1,0:T(8,128)S(1)} %convolution_bitcast_fusion.3, bf16[3,384,384]{2,1,0:T(8,128)(2,1)S(1)} %bitcast.170, bf16[512,1,384]{2,0,1:T(8,128)(2,1)S(1)} %get-tuple-element.12, bf16[512,1,384]{2,0,1:T(8,128)(2,1)S(1)} %get-tuple-element.4, ...), kind=kOutput, calls=%fused_computation.15 | convolution fusion | flops 454754304 | bytes 4030464 | tf_op jit(solution)/shard_map/tki,kio->to/dot_general | solution.py:110
  88.6 0.4 broadcast_in_dim.18
  89.0 1.2 %convert_element_type.54 = bf16[1,1024,384]{2,1,0:T(8,128)(2,1)} reshape(bf16[512,2,384]{2,1,0:T(2,128)(2,1)S(1)} %broadcast_in_dim.18) | data formatting | bytes 1572864 | tf_op jit(solution)/shard_map/convert_element_type | solution.py:125
  90.2 3.8 %collective-permute-done.11 = bf16[192,384]{1,0:T(8,128)(2,1)S(1)} collective-permute-done((bf16[192,384]{1,0:T(8,128)(2,1)S(1)}, bf16[192,384]{1,0:T(8,128)(2,1)S(1)}, u32[]{:S(2)}, u32[]{:S(2)}) %collective-permute-start.11) | collective-permute-done | bytes 147488 | tf_op jit(solution)/shard_map/ppermute | solution.py:64
  94.0 0.3 collective-permute-start.12
  94.4 6.4 %collective-permute-done.12 = bf16[2,192,384]{2,1,0:T(8,128)(2,1)S(1)} collective-permute-done((bf16[2,192,384]{2,1,0:T(8,128)(2,1)S(1)}, bf16[2,192,384]{2,1,0:T(8,128)(2,1)S(1)}, u32[]{:S(2)}, u32[]{:S(2)}) %collective-permute-start.12) | collective-permute-done | bytes 294944 | tf_op jit(solution)/shard_map/ppermute | solution.py:66
  101.1 1.3 %pad_maximum_fusion = f32[3,384,384]{2,1,0:T(8,128)} fusion(f32[1,384,384]{2,1,0:T(8,128)S(1)} %bitcast.167, f32[1,384,384]{2,1,0:T(8,128)S(1)} %bitcast.165, f32[1,384,384]{2,1,0:T(8,128)S(1)} %bitcast.166), kind=kLoop, calls=%fused_computation.2 | loop fusion | flops 884736 | bytes 3538944 | tf_op jit(solution)/shard_map/stack | solution.py:148
  (40 shorter events, 1.3 us)
Async XLA Ops:
  0.6 14.7 %copy-start = (bf16[3,384,768]{2,1,0:T(8,128)(2,1)S(1)}, bf16[3,384,768]{2,1,0:T(8,128)(2,1)}, u32[]{:S(2)}) copy-start(bf16[3,384,768]{2,1,0:T(8,128)(2,1)} %param.4) | copy-start | bytes 5308420
  0.6 27.9 %collective-permute-start.5 = (bf16[512,384]{1,0:T(8,128)(2,1)}, bf16[512,384]{1,0:T(8,128)(2,1)}, u32[]{:S(2)}, u32[]{:S(2)}) collective-permute-start(bf16[512,384]{1,0:T(8,128)(2,1)} %bitcast.157), channel_id=1, source_target_pairs={{2,0},{1,3},{6,4},{5,7},{10,8},{9,11},{14,12},{13,15},{18,16},{17,... | collective-permute-start | bytes 1179656 | tf_op jit(solution)/shard_map/ppermute | solution.py:88
  2.1 26.4 %collective-permute-start.6 = (bf16[512,384]{1,0:T(8,128)(2,1)}, bf16[512,384]{1,0:T(8,128)(2,1)}, u32[]{:S(2)}, u32[]{:S(2)}) collective-permute-start(bf16[512,384]{1,0:T(8,128)(2,1)} %bitcast.158), channel_id=1, source_target_pairs={{2,1},{1,2},{6,5},{5,6},{10,9},{9,10},{14,13},{13,14},{18,17},{17,... | collective-permute-start | bytes 1179656 | tf_op jit(solution)/shard_map/ppermute | solution.py:89
  3.5 2.8 %copy-start.1 = (bf16[1,512,384]{2,1,0:T(8,128)(2,1)S(1)}, bf16[1,512,384]{2,1,0:T(8,128)(2,1)}, u32[]{:S(2)}) copy-start(bf16[1,512,384]{2,1,0:T(8,128)(2,1)} %param.5) | copy-start | bytes 1179652
  7.3 14.1 %collective-permute-start = (bf16[2,256,384]{2,1,0:T(8,128)(2,1)}, bf16[2,256,384]{2,1,0:T(8,128)(2,1)}, u32[]{:S(2)}, u32[]{:S(2)}) collective-permute-start(bf16[2,256,384]{2,1,0:T(8,128)(2,1)} %get-tuple-element.21), channel_id=1, source_target_pairs={{0,4},{4,8},{8,12},{1,5},{5,9},{9,13},{2,6},{6,10},{10,14},{3,7},{... | collective-permute-start | bytes 1179656 | tf_op jit(solution)/shard_map/ppermute | solution.py:12
  13.0 11.4 %collective-permute-start.1 = (bf16[2,256,384]{2,1,0:T(8,128)(2,1)}, bf16[2,256,384]{2,1,0:T(8,128)(2,1)}, u32[]{:S(2)}, u32[]{:S(2)}) collective-permute-start(bf16[2,256,384]{2,1,0:T(8,128)(2,1)} %get-tuple-element.22), channel_id=1, source_target_pairs={{4,0},{8,4},{12,8},{5,1},{9,5},{13,9},{6,2},{10,6},{14,10},{7,3},{... | collective-permute-start | bytes 1179656 | tf_op jit(solution)/shard_map/ppermute | solution.py:12
  15.3 1.1 %copy-start.2 = (bf16[2,512,384]{2,1,0:T(8,128)(2,1)S(1)}, bf16[2,512,384]{2,1,0:T(8,128)(2,1)}, u32[]{:S(2)}) copy-start(bf16[2,512,384]{2,1,0:T(8,128)(2,1)} %pad_maximum_fusion.3) | copy-start | bytes 2359300
  17.8 23.6 %collective-permute-start.3 = (bf16[2176,384]{1,0:T(8,128)(2,1)}, bf16[2176,384]{1,0:T(8,128)(2,1)}, u32[]{:S(2)}, u32[]{:S(2)}) collective-permute-start(bf16[2176,384]{1,0:T(8,128)(2,1)} %pad_maximum_fusion.1), channel_id=1, source_target_pairs={{0,1},{1,0},{2,3},{3,2},{4,5},{5,4},{6,7},{7,6},{8,9},{9,8},{10,11... | collective-permute-start | bytes 5013512 | tf_op jit(solution)/shard_map/ppermute | solution.py:96
  21.5 12.2 %collective-permute-start.4 = (bf16[512,384]{1,0:T(8,128)(2,1)S(1)}, bf16[512,384]{1,0:T(8,128)(2,1)S(1)}, u32[]{:S(2)}, u32[]{:S(2)}) collective-permute-start(bf16[512,384]{1,0:T(8,128)(2,1)S(1)} %get-tuple-element.30), channel_id=1, source_target_pairs={{0,2},{2,0},{1,3},{3,1},{4,6},{6,4},{5,7},{7,5},{8,10},{10,8},{9,1... | collective-permute-start | bytes 1179656 | tf_op jit(solution)/shard_map/ppermute | solution.py:91
  25.7 15.6 %collective-permute-start.2 = (bf16[2,2,256,384]{3,2,1,0:T(8,128)(2,1)S(1)}, bf16[2,2,256,384]{3,2,1,0:T(8,128)(2,1)S(1)}, u32[]{:S(2)}, u32[]{:S(2)}) collective-permute-start(bf16[2,2,256,384]{3,2,1,0:T(8,128)(2,1)S(1)} %pad_maximum_fusion.4), channel_id=1, source_target_pairs={{0,1},{1,0},{2,3},{3,2},{4,5},{5,4},{6,7},{7,6},{8,9},{9,8},{10,11... | collective-permute-start | bytes 2359304 | tf_op jit(solution)/shard_map/ppermute | solution.py:103
  29.6 7.1 %collective-permute-start.8 = (bf16[256,384]{1,0:T(8,128)(2,1)S(1)}, bf16[256,384]{1,0:T(8,128)(2,1)S(1)}, u32[]{:S(2)}, u32[]{:S(2)}) collective-permute-start(bf16[256,384]{1,0:T(8,128)(2,1)S(1)} %get-tuple-element.26), channel_id=1, source_target_pairs={{0,4},{4,8},{8,12},{1,5},{5,9},{9,13},{2,6},{6,10},{10,14},{3,7},{... | collective-permute-start | bytes 589832 | tf_op jit(solution)/shard_map/ppermute | solution.py:12
  32.4 8.5 %collective-permute-start.7 = (bf16[256,384]{1,0:T(8,128)(2,1)S(1)}, bf16[256,384]{1,0:T(8,128)(2,1)S(1)}, u32[]{:S(2)}, u32[]{:S(2)}) collective-permute-start(bf16[256,384]{1,0:T(8,128)(2,1)S(1)} %get-tuple-element.27), channel_id=1, source_target_pairs={{4,0},{8,4},{12,8},{5,1},{9,5},{13,9},{6,2},{10,6},{14,10},{7,3},{... | collective-permute-start | bytes 589832 | tf_op jit(solution)/shard_map/ppermute | solution.py:12
  43.4 11.3 %collective-permute-start.13 = (f32[2,96,384]{2,1,0:T(8,128)S(1)}, f32[2,96,384]{2,1,0:T(8,128)S(1)}, u32[]{:S(2)}, u32[]{:S(2)}) collective-permute-start(f32[2,96,384]{2,1,0:T(8,128)S(1)} %select_bitcast_fusion.1), channel_id=1, source_target_pairs={{0,4},{4,0},{8,12},{12,8},{1,5},{5,1},{9,13},{13,9},{2,6},{6,2},{1... | collective-permute-start | bytes 884744 | tf_op jit(solution)/shard_map/ppermute | solution.py:58
  47.8 19.2 %collective-permute-start.9 = (f32[2,192,384]{2,1,0:T(8,128)S(1)}, f32[2,192,384]{2,1,0:T(8,128)S(1)}, u32[]{:S(2)}, u32[]{:S(2)}) collective-permute-start(f32[2,192,384]{2,1,0:T(8,128)S(1)} %select_bitcast_fusion), channel_id=1, source_target_pairs={{0,4},{4,0},{8,12},{12,8},{1,5},{5,1},{9,13},{13,9},{2,6},{6,2},{1... | collective-permute-start | bytes 1769480 | tf_op jit(solution)/shard_map/ppermute | solution.py:58
  51.0 1.1 %copy-start.3 = (f32[512,384]{1,0:T(8,128)S(1)}, f32[512,384]{1,0:T(8,128)}, u32[]{:S(2)}) copy-start(f32[512,384]{1,0:T(8,128)} %get-tuple-element.31) | copy-start | bytes 2359300
  54.8 12.5 %collective-permute-start.14 = (f32[96,384]{1,0:T(8,128)S(1)}, f32[96,384]{1,0:T(8,128)S(1)}, u32[]{:S(2)}, u32[]{:S(2)}) collective-permute-start(f32[96,384]{1,0:T(8,128)S(1)} %select_bitcast_fusion.7), channel_id=1, source_target_pairs={{0,8},{8,0},{4,12},{12,4},{1,9},{9,1},{5,13},{13,5},{2,10},{10,2},... | collective-permute-start | bytes 442376 | tf_op jit(solution)/shard_map/ppermute | solution.py:63
  67.2 16.8 %collective-permute-start.10 = (f32[192,384]{1,0:T(8,128)S(1)}, f32[192,384]{1,0:T(8,128)S(1)}, u32[]{:S(2)}, u32[]{:S(2)}) collective-permute-start(f32[192,384]{1,0:T(8,128)S(1)} %select_bitcast_fusion.4), channel_id=1, source_target_pairs={{0,8},{8,0},{4,12},{12,4},{1,9},{9,1},{5,13},{13,5},{2,10},{10,2},... | collective-permute-start | bytes 884744 | tf_op jit(solution)/shard_map/ppermute | solution.py:63
  67.3 16.6 %collective-permute-start.15 = (bf16[96,384]{1,0:T(8,128)(2,1)S(1)}, bf16[96,384]{1,0:T(8,128)(2,1)S(1)}, u32[]{:S(2)}, u32[]{:S(2)}) collective-permute-start(bf16[96,384]{1,0:T(8,128)(2,1)S(1)} %fusion.69), channel_id=1, source_target_pairs={{0,8},{8,0},{4,12},{12,4},{1,9},{9,1},{5,13},{13,5},{2,10},{10,2},... | collective-permute-start | bytes 221192 | tf_op jit(solution)/shard_map/ppermute | solution.py:64
  83.9 10.4 %collective-permute-start.16 = (bf16[2,96,384]{2,1,0:T(8,128)(2,1)S(1)}, bf16[2,96,384]{2,1,0:T(8,128)(2,1)S(1)}, u32[]{:S(2)}, u32[]{:S(2)}) collective-permute-start(bf16[2,96,384]{2,1,0:T(8,128)(2,1)S(1)} %maximum_select_fusion.1), channel_id=1, source_target_pairs={{0,4},{4,0},{8,12},{12,8},{1,5},{5,1},{9,13},{13,9},{2,6},{6,2},{1... | collective-permute-start | bytes 442376 | tf_op jit(solution)/shard_map/ppermute | solution.py:66
  84.0 9.9 %collective-permute-start.11 = (bf16[192,384]{1,0:T(8,128)(2,1)S(1)}, bf16[192,384]{1,0:T(8,128)(2,1)S(1)}, u32[]{:S(2)}, u32[]{:S(2)}) collective-permute-start(bf16[192,384]{1,0:T(8,128)(2,1)S(1)} %fusion.68), channel_id=1, source_target_pairs={{0,8},{8,0},{4,12},{12,4},{1,9},{9,1},{5,13},{13,5},{2,10},{10,2},... | collective-permute-start | bytes 442376 | tf_op jit(solution)/shard_map/ppermute | solution.py:64
  94.0 6.8 %collective-permute-start.12 = (bf16[2,192,384]{2,1,0:T(8,128)(2,1)S(1)}, bf16[2,192,384]{2,1,0:T(8,128)(2,1)S(1)}, u32[]{:S(2)}, u32[]{:S(2)}) collective-permute-start(bf16[2,192,384]{2,1,0:T(8,128)(2,1)S(1)} %maximum_select_fusion), channel_id=1, source_target_pairs={{0,4},{4,0},{8,12},{12,8},{1,5},{5,1},{9,13},{13,9},{2,6},{6,2},{1... | collective-permute-start | bytes 884744 | tf_op jit(solution)/shard_map/ppermute | solution.py:66

commit v12 on v11

--- a/solution.py
+++ b/solution.py
@@ -89,6 +89,7 @@
         cross_core = lax.ppermute(local_cot, ("batch", "chan"), [(2, 1), (1, 2)])
         far_cot = jnp.where(b == c, same_core, cross_core)
         far_mid = lax.ppermute(activation, "batch", SWAP)
+        activation, far_mid = lax.optimization_barrier((activation, far_mid))
 
     both = jnp.stack([activation, local_cot])
     w_own = half_of(conv_weight, c, 2)

time: 103 us -> 110 us (1.068)
  waiting for transfers between devices: 42.3 us -> 55 us
  starting transfers between devices: 31.2 us -> 24.5 us
  matrix products: 11.5 us -> 14.6 us
    ppermute x1, waiting for transfers between devices: 0.01 us -> 6.7 us  [shards(): far_mid = lax.ppermute(activation, 'batch', SWAP)]
    ppermute x4, waiting for transfers between devices: 8.39 us -> 13 us  [shift_from(): return lax.ppermute(block, axis, route)]
    ppermute x1, starting transfers between devices: 3.71 us -> 0.01 us  [shards(): lax.ppermute(jnp.concatenate([both.reshape(-1, width), w_other.reshape(-1...]
    dot_general x3, matrix products: 1.16 us -> 4.16 us  [shards(): jnp.dot(far_mid.T, far_shifted[k], preferred_element_type=jnp.float32)]
    ppermute x1, starting transfers between devices: 2.82 us -> 0.07 us  [shards(): par_halo = lax.ppermute(jnp.stack([from_prev, from_next]), 'chan', SWAP)]
    ppermute x1, starting transfers between devices: 0.97 us -> 2.97 us  [shards(): far_mid = lax.ppermute(activation, 'batch', SWAP)]
    ppermute x4, starting transfers between devices: 11 us -> 9.55 us  [shift_from(): return lax.ppermute(block, axis, route)]
  transfers between devices with their start and end apart: 17 -> 17, of which waited for: 7 -> 9; matrix products, arithmetic and copies ran while one was open for 22% -> 20% of each run, Pallas kernels for 0% -> 0%
where the time goes in v12:
time: 110 us
  waiting for transfers between devices  55 us (50%)
  starting transfers between devices  24.5 us (22%)
  matrix products  14.6 us (13%)
  other arithmetic  8.56 us (8%)
  local copies, waits for them, and re-layouts  5.89 us (5%)
    ppermute x2, waiting for transfers between devices, line_total(): other = lax.ppermute(total, 'seq', across)  17.4 us
    ppermute x4, waiting for transfers between devices, shift_from(): return lax.ppermute(block, axis, route)  13 us
    ppermute x2, waiting for transfers between devices, line_total(): lax.ppermute(jnp.where(odd, even_set, odd_set), 'seq', pairs)  11.4 us
    ppermute x4, starting transfers between devices, shift_from(): return lax.ppermute(block, axis, route)  9.55 us
    ppermute x1, waiting for transfers between devices, shards(): far_mid = lax.ppermute(activation, 'batch', SWAP)  6.7 us
    ppermute x2, waiting for transfers between devices, line_total(): far_set = lax.ppermute(own_set, 'seq', pairs)  6.55 us
    ppermute x2, starting transfers between devices, line_total(): other = lax.ppermute(total, 'seq', across)  5.52 us
    dot_general x3, matrix products, shards(): jnp.dot(far_mid.T, far_shifted[k], preferred_element_type=jnp.float32)  4.16 us
  transfers between devices with their start and end apart: 17, of which 9 were waited for; matrix products, arithmetic and copies ran while one was open for 20% of the time, Pallas kernels for 0%

profile of v12, /device:TPU:0, one launch (start us, length us, event | category | flops | bytes accessed | tf_op | source)
XLA Modules:
  0.0 109.7 jit_solution(2418785280848491951)
XLA Ops:
  0.7 2.9 %multiply_convert_fusion = (bf16[512,384]{1,0:T(8,128)(2,1)S(1)}, f32[512,384]{1,0:T(8,128)}) fusion(bf16[1,1024,384]{2,1,0:T(8,128)(2,1)} %param.3, s32[1024]{0:T(1024)S(1)} %get-tuple-element.36, s32[1024]{0:T(1024)S(1)} %get-tuple-element.37, pred[1024]{0:T(1024)(128)(4,1)S(1)} %fusion.72), kind=kOutput, calls=%fused_computation.61 | convolution fusion | flops 406519808 | bytes 1975296 | tf_op jit(solution)/shard_map/dot_general | solution.py:83
  3.6 3.0 %collective-permute-start = (bf16[512,384]{1,0:T(8,128)(2,1)S(1)}, bf16[512,384]{1,0:T(8,128)(2,1)}, u32[]{:S(2)}, u32[]{:S(2)}) collective-permute-start(bf16[512,384]{1,0:T(8,128)(2,1)S(1)} %get-tuple-element.5), channel_id=1, source_target_pairs={{0,2},{2,0},{1,3},{3,1},{4,6},{6,4},{5,7},{7,5},{8,10},{10,8},{9,1... | collective-permute-start | bytes 1179656 | tf_op jit(solution)/shard_map/ppermute | solution.py:91
  6.6 1.3 %collective-permute-start.5 = (bf16[512,384]{1,0:T(8,128)(2,1)S(1)}, bf16[512,384]{1,0:T(8,128)(2,1)}, u32[]{:S(2)}, u32[]{:S(2)}) collective-permute-start(bf16[512,384]{1,0:T(8,128)(2,1)S(1)} %bitcast.157), channel_id=1, source_target_pairs={{2,0},{1,3},{6,4},{5,7},{10,8},{9,11},{14,12},{13,15},{18,16},{17,... | collective-permute-start | bytes 1179656 | tf_op jit(solution)/shard_map/ppermute | solution.py:88
  7.8 1.4 %collective-permute-start.6 = (bf16[512,384]{1,0:T(8,128)(2,1)S(1)}, bf16[512,384]{1,0:T(8,128)(2,1)}, u32[]{:S(2)}, u32[]{:S(2)}) collective-permute-start(bf16[512,384]{1,0:T(8,128)(2,1)S(1)} %bitcast.158), channel_id=1, source_target_pairs={{2,1},{1,2},{6,5},{5,6},{10,9},{9,10},{14,13},{13,14},{18,17},{17,... | collective-permute-start | bytes 1179656 | tf_op jit(solution)/shard_map/ppermute | solution.py:89
  9.3 0.1 constant_dynamic-slice_fusion
  9.4 6.7 %collective-permute-done = bf16[512,384]{1,0:T(8,128)(2,1)} collective-permute-done((bf16[512,384]{1,0:T(8,128)(2,1)S(1)}, bf16[512,384]{1,0:T(8,128)(2,1)}, u32[]{:S(2)}, u32[]{:S(2)}) %collective-permute-start) | collective-permute-done | bytes 393248 | tf_op jit(solution)/shard_map/ppermute | solution.py:91
  16.1 0.1 pad_maximum_fusion.3
  16.2 1.0 fusion.47
  17.1 4.2 %collective-permute-start.1 = (bf16[2,256,384]{2,1,0:T(8,128)(2,1)}, bf16[2,256,384]{2,1,0:T(8,128)(2,1)}, u32[]{:S(2)}, u32[]{:S(2)}) collective-permute-start(bf16[2,256,384]{2,1,0:T(8,128)(2,1)} %get-tuple-element.25), channel_id=1, source_target_pairs={{0,4},{4,8},{8,12},{1,5},{5,9},{9,13},{2,6},{6,10},{10,14},{3,7},{... | collective-permute-start | bytes 1179656 | tf_op jit(solution)/shard_map/ppermute | solution.py:12
  21.4 1.3 %collective-permute-start.2 = (bf16[2,256,384]{2,1,0:T(8,128)(2,1)}, bf16[2,256,384]{2,1,0:T(8,128)(2,1)}, u32[]{:S(2)}, u32[]{:S(2)}) collective-permute-start(bf16[2,256,384]{2,1,0:T(8,128)(2,1)} %get-tuple-element.26), channel_id=1, source_target_pairs={{4,0},{8,4},{12,8},{5,1},{9,5},{13,9},{6,2},{10,6},{14,10},{7,3},{... | collective-permute-start | bytes 1179656 | tf_op jit(solution)/shard_map/ppermute | solution.py:12
  22.6 1.3 %pad_maximum_fusion.1 = bf16[2176,384]{1,0:T(8,128)(2,1)} fusion(bf16[1152,384]{1,0:T(8,128)(2,1)S(1)} %bitcast.162, bf16[1024,384]{1,0:T(8,128)(2,1)S(1)} %bitcast.163), kind=kLoop, calls=%fused_computation.3 | loop fusion | flops 3342336 | bytes 3342336 | tf_op jit(solution)/shard_map/concatenate | solution.py:98
  24.0 1.1 broadcast_select_fusion
  25.1 3.3 %collective-permute-done.1 = bf16[2,256,384]{2,1,0:T(8,128)(2,1)} collective-permute-done((bf16[2,256,384]{2,1,0:T(8,128)(2,1)}, bf16[2,256,384]{2,1,0:T(8,128)(2,1)}, u32[]{:S(2)}, u32[]{:S(2)}) %collective-permute-start.1) | collective-permute-done | bytes 393248 | tf_op jit(solution)/shard_map/ppermute | solution.py:12
  28.4 4.8 %collective-permute-done.2 = bf16[2,256,384]{2,1,0:T(8,128)(2,1)} collective-permute-done((bf16[2,256,384]{2,1,0:T(8,128)(2,1)}, bf16[2,256,384]{2,1,0:T(8,128)(2,1)}, u32[]{:S(2)}, u32[]{:S(2)}) %collective-permute-start.2) | collective-permute-done | bytes 393248 | tf_op jit(solution)/shard_map/ppermute | solution.py:12
  33.2 1.2 %pad_maximum_fusion.4 = bf16[2,2,256,384]{3,2,1,0:T(8,128)(2,1)S(1)} fusion(bf16[1,2,256,384]{3,2,1,0:T(8,128)(2,1)} %bitcast.7, bf16[1,2,256,384]{3,2,1,0:T(8,128)(2,1)} %bitcast.6), kind=kLoop, calls=%fused_computation.59 | loop fusion | flops 393216 | bytes 1572864 | tf_op jit(solution)/shard_map/stack | solution.py:104
  34.6 2.8 %collective-permute-start.8 = (bf16[256,384]{1,0:T(8,128)(2,1)S(1)}, bf16[256,384]{1,0:T(8,128)(2,1)S(1)}, u32[]{:S(2)}, u32[]{:S(2)}) collective-permute-start(bf16[256,384]{1,0:T(8,128)(2,1)S(1)} %get-tuple-element.30), channel_id=1, source_target_pairs={{0,4},{4,8},{8,12},{1,5},{5,9},{9,13},{2,6},{6,10},{10,14},{3,7},{... | collective-permute-start | bytes 589832 | tf_op jit(solution)/shard_map/ppermute | solution.py:12
  37.4 1.3 %collective-permute-start.7 = (bf16[256,384]{1,0:T(8,128)(2,1)S(1)}, bf16[256,384]{1,0:T(8,128)(2,1)S(1)}, u32[]{:S(2)}, u32[]{:S(2)}) collective-permute-start(bf16[256,384]{1,0:T(8,128)(2,1)S(1)} %get-tuple-element.31), channel_id=1, source_target_pairs={{4,0},{8,4},{12,8},{5,1},{9,5},{13,9},{6,2},{10,6},{14,10},{7,3},{... | collective-permute-start | bytes 589832 | tf_op jit(solution)/shard_map/ppermute | solution.py:12
  38.7 1.4 %fusion.87 = f32[384,384]{1,0:T(8,128)S(1)} fusion(bf16[512,384]{1,0:T(8,128)(2,1)} %collective-permute-done, bf16[512,384]{1,0:T(8,128)(2,1)S(1)} %broadcast_select_fusion), kind=kOutput, calls=%fused_computation.143 | convolution fusion | flops 150994944 | bytes 1376256 | tf_op jit(solution)/shard_map/dot_general | solution.py:145
  40.0 2.1 %collective-permute-done.8 = bf16[256,384]{1,0:T(8,128)(2,1)S(1)} collective-permute-done((bf16[256,384]{1,0:T(8,128)(2,1)S(1)}, bf16[256,384]{1,0:T(8,128)(2,1)S(1)}, u32[]{:S(2)}, u32[]{:S(2)}) %collective-permute-start.8) | collective-permute-done | bytes 196640 | tf_op jit(solution)/shard_map/ppermute | solution.py:12
  42.1 1.4 %fusion.57 = f32[384,384]{1,0:T(8,128)S(1)} fusion(bf16[512,384]{1,0:T(8,128)(2,1)} %collective-permute-done, bf16[256,384]{1,0:T(8,128)(2,1)S(1)} %get-tuple-element.31, bf16[256,384]{1,0:T(8,128)(2,1)S(1)} %collective-permute-done.8), kind=kOutput, calls=%fused_computation.92 | convolution fusion | flops 151781376 | bytes 1376256 | tf_op jit(solution)/shard_map/dot_general | solution.py:145
  43.5 2.7 %collective-permute-done.7 = bf16[256,384]{1,0:T(8,128)(2,1)S(1)} collective-permute-done((bf16[256,384]{1,0:T(8,128)(2,1)S(1)}, bf16[256,384]{1,0:T(8,128)(2,1)S(1)}, u32[]{:S(2)}, u32[]{:S(2)}) %collective-permute-start.7) | collective-permute-done | bytes 196640 | tf_op jit(solution)/shard_map/ppermute | solution.py:12
  46.3 1.4 %fusion.53 = f32[384,384]{1,0:T(8,128)S(1)} fusion(bf16[512,384]{1,0:T(8,128)(2,1)} %collective-permute-done, bf16[256,384]{1,0:T(8,128)(2,1)S(1)} %collective-permute-done.7, bf16[256,384]{1,0:T(8,128)(2,1)S(1)} %get-tuple-element.30), kind=kOutput, calls=%fused_computation.88 | convolution fusion | flops 151781376 | bytes 1376256 | tf_op jit(solution)/shard_map/dot_general | solution.py:145
  47.8 1.6 %fusion.52 = (bf16[512,1,384]{2,0,1:T(8,128)(2,1)S(1)}, bf16[512,1,384]{2,0,1:T(8,128)(2,1)S(1)}, bf16[512,1,384]{2,0,1:T(8,128)(2,1)S(1)}, bf16[512,1,384]{2,0,1:T(8,128)(2,1)S(1)}, bf16[1,512,384]{2,1,0:T(8,128)(2,1)S(1)}) fusion(bf16[2,256,384]{2,1,0:T(8,128)(2,1)} %collective-permute-done.2, bf16[1,512,384]{2,1,0:T(8,128)(2,1)S(1)} %copy-done.1, ...), kind=kLoop, calls=%fused_computation.79 | loop fusion | flops 4915200 | bytes 3932161 | tf_op jit(solution)/shard_map/stack | solution.py:21
  49.3 0.4 convolution_add_fusion
  49.8 1.6 %collective-permute-start.13 = (f32[2,96,384]{2,1,0:T(8,128)S(1)}, f32[2,96,384]{2,1,0:T(8,128)S(1)}, u32[]{:S(2)}, u32[]{:S(2)}) collective-permute-start(f32[2,96,384]{2,1,0:T(8,128)S(1)} %select_bitcast_fusion.1), channel_id=1, source_target_pairs={{0,4},{4,0},{8,12},{12,8},{1,5},{5,1},{9,13},{13,9},{2,6},{6,2},{1... | collective-permute-start | bytes 884744 | tf_op jit(solution)/shard_map/ppermute | solution.py:58
  51.4 1.3 %convolution_add_fusion.1 = f32[384,384]{1,0:T(8,128)S(1)} fusion(f32[384,384]{1,0:T(8,128)S(1)} %fusion.57, bf16[1,512,384]{2,1,0:T(8,128)(2,1)S(1)} %get-tuple-element.29, bf16[2,256,384]{2,1,0:T(8,128)(2,1)} %collective-permute-done.2, bf16[1,512,384]{2,1,0:T(8,128)(2,1)S(1)} %copy-done.1, bf16[1,512,384]{2,1,0:T(8,128)(2,1)S(1)} %bitcast.152), kind=kOutput, calls=%fused_computation.13 | convolution fusion | flops 152322048 | bytes 2752512 | tf_op jit(solution)/shard_map/dot_general | solution.py:143
  52.8 1.3 %convolution_add_fusion.2 = f32[384,384]{1,0:T(8,128)S(1)} fusion(f32[384,384]{1,0:T(8,128)S(1)} %fusion.53, bf16[1,512,384]{2,1,0:T(8,128)(2,1)S(1)} %get-tuple-element.29, bf16[2,256,384]{2,1,0:T(8,128)(2,1)} %collective-permute-done.1, bf16[1,512,384]{2,1,0:T(8,128)(2,1)S(1)} %copy-done.1, bf16[1,512,384]{2,1,0:T(8,128)(2,1)S(1)} %bitcast.153), kind=kOutput, calls=%fused_computation.14 | convolution fusion | flops 152322048 | bytes 2752512 | tf_op jit(solution)/shard_map/dot_general | solution.py:143
  54.2 0.5 collective-permute-start.9
  54.8 1.2 %slice.184 = bf16[1024,384]{1,0:T(8,128)(2,1)S(1)} slice(bf16[2176,384]{1,0:T(8,128)(2,1)} %collective-permute-done.4), slice={[0:1024], [0:384]} | slice | bytes 1572864 | tf_op jit(solution)/shard_map/slice | solution.py:100
  56.0 0.2 fusion.50
  56.2 1.2 %slice_bitcast_fusion.3 = (bf16[512,1,384]{2,0,1:T(8,128)(2,1)S(1)}, bf16[512,1,384]{2,0,1:T(8,128)(2,1)S(1)}) fusion(bf16[2176,384]{1,0:T(8,128)(2,1)} %collective-permute-done.4), kind=kLoop, calls=%fused_computation.103 | loop fusion | bytes 1572864 | tf_op jit(solution)/shard_map/stack | solution.py:21
  57.4 0.8 convolution_bitcast_fusion
  58.2 0.3 copy-done.2
  58.5 1.3 %fusion.39 = bf16[512,384]{1,0:T(8,128)(2,1)S(1)} fusion(f32[512,384]{1,0:T(8,128)S(1)} %copy-done.2, f32[512,384]{1,0:T(8,128)S(1)} %convolution_bitcast_fusion, bf16[512,1,384]{2,0,1:T(8,128)(2,1)S(1)} %get-tuple-element.20, bf16[512,1,384]{2,0,1:T(8,128)(2,1)S(1)} %bitcast.159, bf16[512,1,384]{2,0,1:T(8,128)(2,1)S(1)} %get-tuple-element.11, ...), kind=kOutput, calls=%fused_computation.58 | convolution fusion | flops 458883072 | bytes 4423684 | tf_op jit(solution)/shard_map/tko,kio->ti/dot_general | solution.py:117
  59.8 1.3 %slice.187 = bf16[1152,384]{1,0:T(8,128)(2,1)S(1)} slice(bf16[2176,384]{1,0:T(8,128)(2,1)} %collective-permute-done.4), slice={[1024:2176], [0:384]} | slice | bytes 1769472 | tf_op jit(solution)/shard_map/slice | solution.py:101
  61.2 1.4 %collective-permute-start.14 = (f32[96,384]{1,0:T(8,128)S(1)}, f32[96,384]{1,0:T(8,128)S(1)}, u32[]{:S(2)}, u32[]{:S(2)}) collective-permute-start(f32[96,384]{1,0:T(8,128)S(1)} %select_bitcast_fusion.7), channel_id=1, source_target_pairs={{0,8},{8,0},{4,12},{12,4},{1,9},{9,1},{5,13},{13,5},{2,10},{10,2},... | collective-permute-start | bytes 442376 | tf_op jit(solution)/shard_map/ppermute | solution.py:63
  62.6 11.4 %collective-permute-done.9 = f32[2,192,384]{2,1,0:T(8,128)S(1)} collective-permute-done((f32[2,192,384]{2,1,0:T(8,128)S(1)}, f32[2,192,384]{2,1,0:T(8,128)S(1)}, u32[]{:S(2)}, u32[]{:S(2)}) %collective-permute-start.9) | collective-permute-done | bytes 589856 | tf_op jit(solution)/shard_map/ppermute | solution.py:58
  74.2 3.0 %collective-permute-start.15 = (bf16[96,384]{1,0:T(8,128)(2,1)S(1)}, bf16[96,384]{1,0:T(8,128)(2,1)S(1)}, u32[]{:S(2)}, u32[]{:S(2)}) collective-permute-start(bf16[96,384]{1,0:T(8,128)(2,1)S(1)} %fusion.69), channel_id=1, source_target_pairs={{0,8},{8,0},{4,12},{12,4},{1,9},{9,1},{5,13},{13,5},{2,10},{10,2},... | collective-permute-start | bytes 221192 | tf_op jit(solution)/shard_map/ppermute | solution.py:64
  77.1 0.8 convolution_bitcast_fusion.3
  77.9 13.2 %collective-permute-done.15 = bf16[96,384]{1,0:T(8,128)(2,1)S(1)} collective-permute-done((bf16[96,384]{1,0:T(8,128)(2,1)S(1)}, bf16[96,384]{1,0:T(8,128)(2,1)S(1)}, u32[]{:S(2)}, u32[]{:S(2)}) %collective-permute-start.15) | collective-permute-done | bytes 73760 | tf_op jit(solution)/shard_map/ppermute | solution.py:64
  91.3 2.6 %collective-permute-start.11 = (bf16[192,384]{1,0:T(8,128)(2,1)S(1)}, bf16[192,384]{1,0:T(8,128)(2,1)S(1)}, u32[]{:S(2)}, u32[]{:S(2)}) collective-permute-start(bf16[192,384]{1,0:T(8,128)(2,1)S(1)} %fusion.68), channel_id=1, source_target_pairs={{0,8},{8,0},{4,12},{12,4},{1,9},{9,1},{5,13},{13,5},{2,10},{10,2},... | collective-permute-start | bytes 442376 | tf_op jit(solution)/shard_map/ppermute | solution.py:64
  93.9 1.6 %fusion.4 = bf16[1,512,384]{2,1,0:T(8,128)(2,1)} fusion(f32[512,384]{1,0:T(8,128)S(1)} %copy-done.2, f32[512,384]{1,0:T(8,128)S(1)} %convolution_bitcast_fusion.3, bf16[3,384,384]{2,1,0:T(8,128)(2,1)S(1)} %bitcast.170, bf16[512,1,384]{2,0,1:T(8,128)(2,1)S(1)} %get-tuple-element.16, bf16[512,1,384]{2,0,1:T(8,128)(2,1)S(1)} %get-tuple-element.8, ...), kind=kOutput, calls=%fused_computation.15 | convolution fusion | flops 454754304 | bytes 4030464 | tf_op jit(solution)/shard_map/tki,kio->to/dot_general | solution.py:111
  95.5 0.4 broadcast_in_dim.18
  95.9 1.2 %convert_element_type.54 = bf16[1,1024,384]{2,1,0:T(8,128)(2,1)} reshape(bf16[512,2,384]{2,1,0:T(2,128)(2,1)S(1)} %broadcast_in_dim.18) | data formatting | bytes 1572864 | tf_op jit(solution)/shard_map/convert_element_type | solution.py:126
  97.0 4.2 %collective-permute-done.11 = bf16[192,384]{1,0:T(8,128)(2,1)S(1)} collective-permute-done((bf16[192,384]{1,0:T(8,128)(2,1)S(1)}, bf16[192,384]{1,0:T(8,128)(2,1)S(1)}, u32[]{:S(2)}, u32[]{:S(2)}) %collective-permute-start.11) | collective-permute-done | bytes 147488 | tf_op jit(solution)/shard_map/ppermute | solution.py:64
  101.5 6.5 %collective-permute-done.12 = bf16[2,192,384]{2,1,0:T(8,128)(2,1)S(1)} collective-permute-done((bf16[2,192,384]{2,1,0:T(8,128)(2,1)S(1)}, bf16[2,192,384]{2,1,0:T(8,128)(2,1)S(1)}, u32[]{:S(2)}, u32[]{:S(2)}) %collective-permute-start.12) | collective-permute-done | bytes 294944 | tf_op jit(solution)/shard_map/ppermute | solution.py:66
  108.1 0.1 select_bitcast_fusion.3
  108.4 1.3 %pad_maximum_fusion = f32[3,384,384]{2,1,0:T(8,128)} fusion(f32[1,384,384]{2,1,0:T(8,128)S(1)} %bitcast.167, f32[1,384,384]{2,1,0:T(8,128)S(1)} %bitcast.165, f32[1,384,384]{2,1,0:T(8,128)S(1)} %bitcast.166), kind=kLoop, calls=%fused_computation.2 | loop fusion | flops 884736 | bytes 3538944 | tf_op jit(solution)/shard_map/stack | solution.py:149
  (38 shorter events, 1.3 us)
Async XLA Ops:
  0.6 8.6 %copy-start = (bf16[3,384,768]{2,1,0:T(8,128)(2,1)S(1)}, bf16[3,384,768]{2,1,0:T(8,128)(2,1)}, u32[]{:S(2)}) copy-start(bf16[3,384,768]{2,1,0:T(8,128)(2,1)} %param.4) | copy-start | bytes 5308420
  0.7 5.9 %copy-start.1 = (bf16[1,512,384]{2,1,0:T(8,128)(2,1)S(1)}, bf16[1,512,384]{2,1,0:T(8,128)(2,1)}, u32[]{:S(2)}) copy-start(bf16[1,512,384]{2,1,0:T(8,128)(2,1)} %param.5) | copy-start | bytes 1179652
  3.6 12.5 %collective-permute-start = (bf16[512,384]{1,0:T(8,128)(2,1)S(1)}, bf16[512,384]{1,0:T(8,128)(2,1)}, u32[]{:S(2)}, u32[]{:S(2)}) collective-permute-start(bf16[512,384]{1,0:T(8,128)(2,1)S(1)} %get-tuple-element.5), channel_id=1, source_target_pairs={{0,2},{2,0},{1,3},{3,1},{4,6},{6,4},{5,7},{7,5},{8,10},{10,8},{9,1... | collective-permute-start | bytes 1179656 | tf_op jit(solution)/shard_map/ppermute | solution.py:91
  6.6 17.4 %collective-permute-start.5 = (bf16[512,384]{1,0:T(8,128)(2,1)S(1)}, bf16[512,384]{1,0:T(8,128)(2,1)}, u32[]{:S(2)}, u32[]{:S(2)}) collective-permute-start(bf16[512,384]{1,0:T(8,128)(2,1)S(1)} %bitcast.157), channel_id=1, source_target_pairs={{2,0},{1,3},{6,4},{5,7},{10,8},{9,11},{14,12},{13,15},{18,16},{17,... | collective-permute-start | bytes 1179656 | tf_op jit(solution)/shard_map/ppermute | solution.py:88
  7.8 16.2 %collective-permute-start.6 = (bf16[512,384]{1,0:T(8,128)(2,1)S(1)}, bf16[512,384]{1,0:T(8,128)(2,1)}, u32[]{:S(2)}, u32[]{:S(2)}) collective-permute-start(bf16[512,384]{1,0:T(8,128)(2,1)S(1)} %bitcast.158), channel_id=1, source_target_pairs={{2,1},{1,2},{6,5},{5,6},{10,9},{9,10},{14,13},{13,14},{18,17},{17,... | collective-permute-start | bytes 1179656 | tf_op jit(solution)/shard_map/ppermute | solution.py:89
  17.1 11.3 %collective-permute-start.1 = (bf16[2,256,384]{2,1,0:T(8,128)(2,1)}, bf16[2,256,384]{2,1,0:T(8,128)(2,1)}, u32[]{:S(2)}, u32[]{:S(2)}) collective-permute-start(bf16[2,256,384]{2,1,0:T(8,128)(2,1)} %get-tuple-element.25), channel_id=1, source_target_pairs={{0,4},{4,8},{8,12},{1,5},{5,9},{9,13},{2,6},{6,10},{10,14},{3,7},{... | collective-permute-start | bytes 1179656 | tf_op jit(solution)/shard_map/ppermute | solution.py:12
  21.4 11.9 %collective-permute-start.2 = (bf16[2,256,384]{2,1,0:T(8,128)(2,1)}, bf16[2,256,384]{2,1,0:T(8,128)(2,1)}, u32[]{:S(2)}, u32[]{:S(2)}) collective-permute-start(bf16[2,256,384]{2,1,0:T(8,128)(2,1)} %get-tuple-element.26), channel_id=1, source_target_pairs={{4,0},{8,4},{12,8},{5,1},{9,5},{13,9},{6,2},{10,6},{14,10},{7,3},{... | collective-permute-start | bytes 1179656 | tf_op jit(solution)/shard_map/ppermute | solution.py:12
  24.0 23.8 %collective-permute-start.4 = (bf16[2176,384]{1,0:T(8,128)(2,1)}, bf16[2176,384]{1,0:T(8,128)(2,1)}, u32[]{:S(2)}, u32[]{:S(2)}) collective-permute-start(bf16[2176,384]{1,0:T(8,128)(2,1)} %pad_maximum_fusion.1), channel_id=1, source_target_pairs={{0,1},{1,0},{2,3},{3,2},{4,5},{5,4},{6,7},{7,6},{8,9},{9,8},{10,11... | collective-permute-start | bytes 5013512 | tf_op jit(solution)/shard_map/ppermute | solution.py:97
  34.5 13.2 %collective-permute-start.3 = (bf16[2,2,256,384]{3,2,1,0:T(8,128)(2,1)S(1)}, bf16[2,2,256,384]{3,2,1,0:T(8,128)(2,1)S(1)}, u32[]{:S(2)}, u32[]{:S(2)}) collective-permute-start(bf16[2,2,256,384]{3,2,1,0:T(8,128)(2,1)S(1)} %pad_maximum_fusion.4), channel_id=1, source_target_pairs={{0,1},{1,0},{2,3},{3,2},{4,5},{5,4},{6,7},{7,6},{8,9},{9,8},{10,11... | collective-permute-start | bytes 2359304 | tf_op jit(solution)/shard_map/ppermute | solution.py:104
  34.6 7.6 %collective-permute-start.8 = (bf16[256,384]{1,0:T(8,128)(2,1)S(1)}, bf16[256,384]{1,0:T(8,128)(2,1)S(1)}, u32[]{:S(2)}, u32[]{:S(2)}) collective-permute-start(bf16[256,384]{1,0:T(8,128)(2,1)S(1)} %get-tuple-element.30), channel_id=1, source_target_pairs={{0,4},{4,8},{8,12},{1,5},{5,9},{9,13},{2,6},{6,10},{10,14},{3,7},{... | collective-permute-start | bytes 589832 | tf_op jit(solution)/shard_map/ppermute | solution.py:12
  37.4 8.9 %collective-permute-start.7 = (bf16[256,384]{1,0:T(8,128)(2,1)S(1)}, bf16[256,384]{1,0:T(8,128)(2,1)S(1)}, u32[]{:S(2)}, u32[]{:S(2)}) collective-permute-start(bf16[256,384]{1,0:T(8,128)(2,1)S(1)} %get-tuple-element.31), channel_id=1, source_target_pairs={{4,0},{8,4},{12,8},{5,1},{9,5},{13,9},{6,2},{10,6},{14,10},{7,3},{... | collective-permute-start | bytes 589832 | tf_op jit(solution)/shard_map/ppermute | solution.py:12
  49.8 11.3 %collective-permute-start.13 = (f32[2,96,384]{2,1,0:T(8,128)S(1)}, f32[2,96,384]{2,1,0:T(8,128)S(1)}, u32[]{:S(2)}, u32[]{:S(2)}) collective-permute-start(f32[2,96,384]{2,1,0:T(8,128)S(1)} %select_bitcast_fusion.1), channel_id=1, source_target_pairs={{0,4},{4,0},{8,12},{12,8},{1,5},{5,1},{9,13},{13,9},{2,6},{6,2},{1... | collective-permute-start | bytes 884744 | tf_op jit(solution)/shard_map/ppermute | solution.py:58
  54.2 19.7 %collective-permute-start.9 = (f32[2,192,384]{2,1,0:T(8,128)S(1)}, f32[2,192,384]{2,1,0:T(8,128)S(1)}, u32[]{:S(2)}, u32[]{:S(2)}) collective-permute-start(f32[2,192,384]{2,1,0:T(8,128)S(1)} %select_bitcast_fusion), channel_id=1, source_target_pairs={{0,4},{4,0},{8,12},{12,8},{1,5},{5,1},{9,13},{13,9},{2,6},{6,2},{1... | collective-permute-start | bytes 1769480 | tf_op jit(solution)/shard_map/ppermute | solution.py:58
  57.4 1.1 %copy-start.2 = (f32[512,384]{1,0:T(8,128)S(1)}, f32[512,384]{1,0:T(8,128)}, u32[]{:S(2)}) copy-start(f32[512,384]{1,0:T(8,128)} %get-tuple-element.35) | copy-start | bytes 2359300
  61.2 12.9 %collective-permute-start.14 = (f32[96,384]{1,0:T(8,128)S(1)}, f32[96,384]{1,0:T(8,128)S(1)}, u32[]{:S(2)}, u32[]{:S(2)}) collective-permute-start(f32[96,384]{1,0:T(8,128)S(1)} %select_bitcast_fusion.7), channel_id=1, source_target_pairs={{0,8},{8,0},{4,12},{12,4},{1,9},{9,1},{5,13},{13,5},{2,10},{10,2},... | collective-permute-start | bytes 442376 | tf_op jit(solution)/shard_map/ppermute | solution.py:63
  74.0 17.2 %collective-permute-start.10 = (f32[192,384]{1,0:T(8,128)S(1)}, f32[192,384]{1,0:T(8,128)S(1)}, u32[]{:S(2)}, u32[]{:S(2)}) collective-permute-start(f32[192,384]{1,0:T(8,128)S(1)} %select_bitcast_fusion.4), channel_id=1, source_target_pairs={{0,8},{8,0},{4,12},{12,4},{1,9},{9,1},{5,13},{13,5},{2,10},{10,2},... | collective-permute-start | bytes 884744 | tf_op jit(solution)/shard_map/ppermute | solution.py:63
  74.2 17.0 %collective-permute-start.15 = (bf16[96,384]{1,0:T(8,128)(2,1)S(1)}, bf16[96,384]{1,0:T(8,128)(2,1)S(1)}, u32[]{:S(2)}, u32[]{:S(2)}) collective-permute-start(bf16[96,384]{1,0:T(8,128)(2,1)S(1)} %fusion.69), channel_id=1, source_target_pairs={{0,8},{8,0},{4,12},{12,4},{1,9},{9,1},{5,13},{13,5},{2,10},{10,2},... | collective-permute-start | bytes 221192 | tf_op jit(solution)/shard_map/ppermute | solution.py:64
  91.2 10.2 %collective-permute-start.16 = (bf16[2,96,384]{2,1,0:T(8,128)(2,1)S(1)}, bf16[2,96,384]{2,1,0:T(8,128)(2,1)S(1)}, u32[]{:S(2)}, u32[]{:S(2)}) collective-permute-start(bf16[2,96,384]{2,1,0:T(8,128)(2,1)S(1)} %maximum_select_fusion.1), channel_id=1, source_target_pairs={{0,4},{4,0},{8,12},{12,8},{1,5},{5,1},{9,13},{13,9},{2,6},{6,2},{1... | collective-permute-start | bytes 442376 | tf_op jit(solution)/shard_map/ppermute | solution.py:66
  91.3 9.9 %collective-permute-start.11 = (bf16[192,384]{1,0:T(8,128)(2,1)S(1)}, bf16[192,384]{1,0:T(8,128)(2,1)S(1)}, u32[]{:S(2)}, u32[]{:S(2)}) collective-permute-start(bf16[192,384]{1,0:T(8,128)(2,1)S(1)} %fusion.68), channel_id=1, source_target_pairs={{0,8},{8,0},{4,12},{12,4},{1,9},{9,1},{5,13},{13,5},{2,10},{10,2},... | collective-permute-start | bytes 442376 | tf_op jit(solution)/shard_map/ppermute | solution.py:64
  101.3 6.8 %collective-permute-start.12 = (bf16[2,192,384]{2,1,0:T(8,128)(2,1)S(1)}, bf16[2,192,384]{2,1,0:T(8,128)(2,1)S(1)}, u32[]{:S(2)}, u32[]{:S(2)}) collective-permute-start(bf16[2,192,384]{2,1,0:T(8,128)(2,1)S(1)} %maximum_select_fusion), channel_id=1, source_target_pairs={{0,4},{4,0},{8,12},{12,8},{1,5},{5,1},{9,13},{13,9},{2,6},{6,2},{1... | collective-permute-start | bytes 884744 | tf_op jit(solution)/shard_map/ppermute | solution.py:66

commit v13 on v11

--- a/solution.py
+++ b/solution.py
@@ -130,6 +130,10 @@
     seq_count = lax.axis_size("seq")
     if batch_count == 2:
         cot_mine = jnp.where(b == c, local_cot, par_cot)
+        centre = jnp.dot(own_taps[:, 1].T, cot_mine, preferred_element_type=jnp.float32) + jnp.dot(
+            far_mid.T, far_cot, preferred_element_type=jnp.float32
+        )
+        centre, far_cot = lax.optimization_barrier((centre, far_cot))
         cot_next = shift_from(far_cot[:spread], "seq", -1)
         cot_prev = shift_from(far_cot[rows - spread :], "seq", 1)
         far_shifted = {
@@ -137,8 +141,8 @@
             0: jnp.concatenate([far_cot[spread:], cot_next], 0),
             2: jnp.concatenate([cot_prev, far_cot[: rows - spread]], 0),
         }
-        grads = {}
-        for k in (1, 0, 2):
+        grads = {1: centre}
+        for k in (0, 2):
             grads[k] = jnp.dot(
                 own_taps[:, k].T, cot_mine, preferred_element_type=jnp.float32
             ) + jnp.dot(far_mid.T, far_shifted[k], preferred_element_type=jnp.float32)

time: 103 us -> 112 us (1.087)
  waiting for transfers between devices: 42.3 us -> 57 us
  starting transfers between devices: 31.2 us -> 24.7 us
  local copies, waits for them, and re-layouts: 6.93 us -> 10.2 us
  other arithmetic: 9.42 us -> 7.11 us
    ppermute x1, waiting for transfers between devices: 0.01 us -> 8.99 us  [shards(): far_mid = lax.ppermute(activation, 'batch', SWAP)]
    ppermute x1, starting transfers between devices: 3.71 us -> 0.49 us  [shards(): lax.ppermute(jnp.concatenate([both.reshape(-1, width), w_other.reshape(-1...]
    ppermute x4, waiting for transfers between devices: 8.39 us -> 11.3 us  [shift_from(): return lax.ppermute(block, axis, route)]
    ppermute x1, starting transfers between devices: 2.82 us -> 0.01 us  [shards(): par_halo = lax.ppermute(jnp.stack([from_prev, from_next]), 'chan', SWAP)]
    dot_general x3 -> x2, matrix products: 3.05 us -> 0.8 us  [shards(): jnp.dot(own_taps[:, k].T, cot_mine, preferred_element_type=jnp.float32)]
    unnamed x8 -> x16, local copies, waits for them, and re-layouts: 1.36 us -> 3.48 us
    dot_general x0 -> x2, matrix products: none -> 1.79 us  [the longest x1 1.39 us: shards(): jnp.dot(far_mid.T, far_cot, preferred_element_type=jnp.float32)]
    another operation x2, other arithmetic: 1.95 us -> 0.18 us  [shards(): both = jnp.stack([activation, local_cot])]
  transfers between devices with their start and end apart: 17 -> 17, of which waited for: 7 -> 8; matrix products, arithmetic and copies ran while one was open for 22% -> 17% of each run, Pallas kernels for 0% -> 0%
where the time goes in v13:
time: 112 us
  waiting for transfers between devices  57 us (51%)
  starting transfers between devices  24.7 us (22%)
  matrix products  11.5 us (10%)
  local copies, waits for them, and re-layouts  10.2 us (9%)
  other arithmetic  7.11 us (6%)
    ppermute x2, waiting for transfers between devices, line_total(): other = lax.ppermute(total, 'seq', across)  17.5 us
    ppermute x4, waiting for transfers between devices, shift_from(): return lax.ppermute(block, axis, route)  11.3 us
    ppermute x2, waiting for transfers between devices, line_total(): lax.ppermute(jnp.where(odd, even_set, odd_set), 'seq', pairs)  11.3 us
    ppermute x4, starting transfers between devices, shift_from(): return lax.ppermute(block, axis, route)  10.5 us
    ppermute x1, waiting for transfers between devices, shards(): far_mid = lax.ppermute(activation, 'batch', SWAP)  8.99 us
    ppermute x2, waiting for transfers between devices, line_total(): far_set = lax.ppermute(own_set, 'seq', pairs)  7.9 us
    ppermute x2, starting transfers between devices, line_total(): other = lax.ppermute(total, 'seq', across)  4.78 us
    unnamed x16, local copies, waits for them, and re-layouts  3.48 us
  transfers between devices with their start and end apart: 17, of which 8 were waited for; matrix products, arithmetic and copies ran while one was open for 17% of the time, Pallas kernels for 0%

profile of v13, /device:TPU:0, one launch (start us, length us, event | category | flops | bytes accessed | tf_op | source)
XLA Modules:
  0.0 111.6 jit_solution(1097254752455251484)
XLA Ops:
  0.7 1.4 %copy-done = bf16[3,384,768]{2,1,0:T(8,128)(2,1)S(1)} copy-done((bf16[3,384,768]{2,1,0:T(8,128)(2,1)S(1)}, bf16[3,384,768]{2,1,0:T(8,128)(2,1)}, u32[]{:S(2)}) %copy-start) | copy-done | bytes 1769496
  2.2 1.0 copy-done.6
  3.2 1.6 %multiply_convert_fusion = (bf16[512,384]{1,0:T(8,128)(2,1)S(1)}, f32[512,384]{1,0:T(8,128)}) fusion(bf16[1,1024,384]{2,1,0:T(8,128)(2,1)S(1)} %copy-done.6, s32[1024]{0:T(1024)S(1)} %get-tuple-element.36, s32[1024]{0:T(1024)S(1)} %get-tuple-element.37, pred[1024]{0:T(1024)(128)(4,1)S(1)} %fusion.72), kind=kOutput, calls=%fused_computation.61 | convolution fusion | flops 406519808 | bytes 1975296 | tf_op jit(solution)/shard_map/dot_general | solution.py:83
  5.0 1.3 %pad_maximum_fusion.1 = bf16[2176,384]{1,0:T(8,128)(2,1)} fusion(bf16[1152,384]{1,0:T(8,128)(2,1)S(1)} %bitcast.162, bf16[1024,384]{1,0:T(8,128)(2,1)S(1)} %bitcast.166), kind=kLoop, calls=%fused_computation.3 | loop fusion | flops 3342336 | bytes 3342336 | tf_op jit(solution)/shard_map/concatenate | solution.py:97
  6.3 0.5 collective-permute-start.3
  6.8 0.1 fusion.47
  6.9 4.5 %collective-permute-start = (bf16[2,256,384]{2,1,0:T(8,128)(2,1)S(1)}, bf16[2,256,384]{2,1,0:T(8,128)(2,1)S(1)}, u32[]{:S(2)}, u32[]{:S(2)}) collective-permute-start(bf16[2,256,384]{2,1,0:T(8,128)(2,1)S(1)} %get-tuple-element.25), channel_id=1, source_target_pairs={{0,4},{4,8},{8,12},{1,5},{5,9},{9,13},{2,6},{6,10},{10,14},{3,7},{... | collective-permute-start | bytes 1179656 | tf_op jit(solution)/shard_map/ppermute | solution.py:12
  11.4 1.3 %collective-permute-start.1 = (bf16[2,256,384]{2,1,0:T(8,128)(2,1)S(1)}, bf16[2,256,384]{2,1,0:T(8,128)(2,1)S(1)}, u32[]{:S(2)}, u32[]{:S(2)}) collective-permute-start(bf16[2,256,384]{2,1,0:T(8,128)(2,1)S(1)} %get-tuple-element.26), channel_id=1, source_target_pairs={{4,0},{8,4},{12,8},{5,1},{9,5},{13,9},{6,2},{10,6},{14,10},{7,3},{... | collective-permute-start | bytes 1179656 | tf_op jit(solution)/shard_map/ppermute | solution.py:12
  12.7 1.3 %collective-permute-start.5 = (bf16[512,384]{1,0:T(8,128)(2,1)S(1)}, bf16[512,384]{1,0:T(8,128)(2,1)}, u32[]{:S(2)}, u32[]{:S(2)}) collective-permute-start(bf16[512,384]{1,0:T(8,128)(2,1)S(1)} %bitcast.157), channel_id=1, source_target_pairs={{2,0},{1,3},{6,4},{5,7},{10,8},{9,11},{14,12},{13,15},{18,16},{17,... | collective-permute-start | bytes 1179656 | tf_op jit(solution)/shard_map/ppermute | solution.py:88
  14.0 1.4 %collective-permute-start.6 = (bf16[512,384]{1,0:T(8,128)(2,1)S(1)}, bf16[512,384]{1,0:T(8,128)(2,1)}, u32[]{:S(2)}, u32[]{:S(2)}) collective-permute-start(bf16[512,384]{1,0:T(8,128)(2,1)S(1)} %bitcast.158), channel_id=1, source_target_pairs={{2,1},{1,2},{6,5},{5,6},{10,9},{9,10},{14,13},{13,14},{18,17},{17,... | collective-permute-start | bytes 1179656 | tf_op jit(solution)/shard_map/ppermute | solution.py:89
  15.4 5.0 %collective-permute-done = bf16[2,256,384]{2,1,0:T(8,128)(2,1)S(1)} collective-permute-done((bf16[2,256,384]{2,1,0:T(8,128)(2,1)S(1)}, bf16[2,256,384]{2,1,0:T(8,128)(2,1)S(1)}, u32[]{:S(2)}, u32[]{:S(2)}) %collective-permute-start) | collective-permute-done | bytes 393248 | tf_op jit(solution)/shard_map/ppermute | solution.py:12
  20.4 4.1 %collective-permute-done.1 = bf16[2,256,384]{2,1,0:T(8,128)(2,1)S(1)} collective-permute-done((bf16[2,256,384]{2,1,0:T(8,128)(2,1)S(1)}, bf16[2,256,384]{2,1,0:T(8,128)(2,1)S(1)}, u32[]{:S(2)}, u32[]{:S(2)}) %collective-permute-start.1) | collective-permute-done | bytes 393248 | tf_op jit(solution)/shard_map/ppermute | solution.py:12
  24.5 1.0 pad_maximum_fusion.4
  25.6 1.6 %collective-permute-start.4 = (bf16[512,384]{1,0:T(8,128)(2,1)S(1)}, bf16[512,384]{1,0:T(8,128)(2,1)}, u32[]{:S(2)}, u32[]{:S(2)}) collective-permute-start(bf16[512,384]{1,0:T(8,128)(2,1)S(1)} %get-tuple-element.34), channel_id=1, source_target_pairs={{0,2},{2,0},{1,3},{3,1},{4,6},{6,4},{5,7},{7,5},{8,10},{10,8},{9,1... | collective-permute-start | bytes 1179656 | tf_op jit(solution)/shard_map/ppermute | solution.py:91
  27.1 1.0 broadcast_select_fusion
  28.2 9.0 %collective-permute-done.4 = bf16[512,384]{1,0:T(8,128)(2,1)} collective-permute-done((bf16[512,384]{1,0:T(8,128)(2,1)S(1)}, bf16[512,384]{1,0:T(8,128)(2,1)}, u32[]{:S(2)}, u32[]{:S(2)}) %collective-permute-start.4) | collective-permute-done | bytes 393248 | tf_op jit(solution)/shard_map/ppermute | solution.py:91
  37.2 1.4 %fusion.87 = f32[384,384]{1,0:T(8,128)S(1)} fusion(bf16[512,384]{1,0:T(8,128)(2,1)} %collective-permute-done.4, bf16[512,384]{1,0:T(8,128)(2,1)S(1)} %broadcast_select_fusion), kind=kOutput, calls=%fused_computation.143 | convolution fusion | flops 150994944 | bytes 1376256 | tf_op jit(solution)/shard_map/dot_general | solution.py:133
  38.6 1.2 %slice_bitcast_fusion.2 = (bf16[2,256,384]{2,1,0:T(8,128)(2,1)S(1)}, bf16[2,256,384]{2,1,0:T(8,128)(2,1)S(1)}) fusion(bf16[2,2,256,384]{3,2,1,0:T(8,128)(2,1)} %collective-permute-done.2), kind=kLoop, calls=%fused_computation.85 | loop fusion | bytes 1572864 | tf_op jit(solution)/shard_map/squeeze | solution.py:105
  39.8 1.2 %fusion.52 = (bf16[512,1,384]{2,0,1:T(8,128)(2,1)S(1)}, bf16[512,1,384]{2,0,1:T(8,128)(2,1)S(1)}, bf16[512,1,384]{2,0,1:T(8,128)(2,1)S(1)}, bf16[512,1,384]{2,0,1:T(8,128)(2,1)S(1)}, bf16[1,512,384]{2,1,0:T(8,128)(2,1)S(1)}) fusion(bf16[2,256,384]{2,1,0:T(8,128)(2,1)S(1)} %copy-done.3, bf16[1,512,384]{2,1,0:T(8,128)(2,1)S(1)} %copy-done.1, ...), kind=kLoop, calls=%fused_computation.79 | loop fusion | flops 4915200 | bytes 3932161 | tf_op jit(solution)/shard_map/stack | solution.py:21
  41.1 0.4 convolution_add_fusion.1
  41.5 3.5 %collective-permute-start.8 = (bf16[256,384]{1,0:T(8,128)(2,1)S(1)}, bf16[256,384]{1,0:T(8,128)(2,1)S(1)}, u32[]{:S(2)}, u32[]{:S(2)}) collective-permute-start(bf16[256,384]{1,0:T(8,128)(2,1)S(1)} %get-tuple-element.29), channel_id=1, source_target_pairs={{0,4},{4,8},{8,12},{1,5},{5,9},{9,13},{2,6},{6,10},{10,14},{3,7},{... | collective-permute-start | bytes 589832 | tf_op jit(solution)/shard_map/ppermute | solution.py:12
  45.0 1.3 %collective-permute-start.7 = (bf16[256,384]{1,0:T(8,128)(2,1)S(1)}, bf16[256,384]{1,0:T(8,128)(2,1)S(1)}, u32[]{:S(2)}, u32[]{:S(2)}) collective-permute-start(bf16[256,384]{1,0:T(8,128)(2,1)S(1)} %get-tuple-element.30), channel_id=1, source_target_pairs={{4,0},{8,4},{12,8},{5,1},{9,5},{13,9},{6,2},{10,6},{14,10},{7,3},{... | collective-permute-start | bytes 589832 | tf_op jit(solution)/shard_map/ppermute | solution.py:12
  46.3 2.7 %collective-permute-start.13 = (f32[2,96,384]{2,1,0:T(8,128)S(1)}, f32[2,96,384]{2,1,0:T(8,128)S(1)}, u32[]{:S(2)}, u32[]{:S(2)}) collective-permute-start(f32[2,96,384]{2,1,0:T(8,128)S(1)} %select_bitcast_fusion.1), channel_id=1, source_target_pairs={{0,4},{4,0},{8,12},{12,8},{1,5},{5,1},{9,13},{13,9},{2,6},{6,2},{1... | collective-permute-start | bytes 884744 | tf_op jit(solution)/shard_map/ppermute | solution.py:58
  49.1 1.2 %slice.184 = bf16[1024,384]{1,0:T(8,128)(2,1)S(1)} slice(bf16[2176,384]{1,0:T(8,128)(2,1)} %collective-permute-done.3), slice={[0:1024], [0:384]} | slice | bytes 1572864 | tf_op jit(solution)/shard_map/slice | solution.py:99
  50.3 0.2 fusion.50
  50.5 1.2 %slice_bitcast_fusion.3 = (bf16[512,1,384]{2,0,1:T(8,128)(2,1)S(1)}, bf16[512,1,384]{2,0,1:T(8,128)(2,1)S(1)}) fusion(bf16[2176,384]{1,0:T(8,128)(2,1)} %collective-permute-done.3), kind=kLoop, calls=%fused_computation.103 | loop fusion | bytes 1572864 | tf_op jit(solution)/shard_map/stack | solution.py:21
  51.7 0.8 convolution_bitcast_fusion
  52.5 2.2 %collective-permute-done.7 = bf16[256,384]{1,0:T(8,128)(2,1)S(1)} collective-permute-done((bf16[256,384]{1,0:T(8,128)(2,1)S(1)}, bf16[256,384]{1,0:T(8,128)(2,1)S(1)}, u32[]{:S(2)}, u32[]{:S(2)}) %collective-permute-start.7) | collective-permute-done | bytes 196640 | tf_op jit(solution)/shard_map/ppermute | solution.py:12
  54.7 1.4 %fusion.53 = f32[384,384]{1,0:T(8,128)S(1)} fusion(bf16[512,384]{1,0:T(8,128)(2,1)} %collective-permute-done.4, bf16[256,384]{1,0:T(8,128)(2,1)S(1)} %collective-permute-done.7, bf16[256,384]{1,0:T(8,128)(2,1)S(1)} %get-tuple-element.29), kind=kOutput, calls=%fused_computation.88 | convolution fusion | flops 151781376 | bytes 1376256 | tf_op jit(solution)/shard_map/dot_general | solution.py:148
  56.1 0.4 convolution_add_fusion.2
  56.5 1.4 %fusion.57 = f32[384,384]{1,0:T(8,128)S(1)} fusion(bf16[512,384]{1,0:T(8,128)(2,1)} %collective-permute-done.4, bf16[256,384]{1,0:T(8,128)(2,1)S(1)} %get-tuple-element.30, bf16[256,384]{1,0:T(8,128)(2,1)S(1)} %collective-permute-done.8), kind=kOutput, calls=%fused_computation.92 | convolution fusion | flops 151781376 | bytes 1376256 | tf_op jit(solution)/shard_map/dot_general | solution.py:148
  57.9 0.4 convolution_add_fusion
  58.5 1.0 copy-done.7
  59.5 1.3 %fusion.39 = bf16[512,384]{1,0:T(8,128)(2,1)S(1)} fusion(f32[512,384]{1,0:T(8,128)S(1)} %copy-done.7, f32[512,384]{1,0:T(8,128)S(1)} %convolution_bitcast_fusion, bf16[512,1,384]{2,0,1:T(8,128)(2,1)S(1)} %get-tuple-element.20, bf16[512,1,384]{2,0,1:T(8,128)(2,1)S(1)} %bitcast.159, bf16[512,1,384]{2,0,1:T(8,128)(2,1)S(1)} %get-tuple-element.11, ...), kind=kOutput, calls=%fused_computation.58 | convolution fusion | flops 458883072 | bytes 4423684 | tf_op jit(solution)/shard_map/tko,kio->ti/dot_general | solution.py:116
  60.8 1.3 %slice.187 = bf16[1152,384]{1,0:T(8,128)(2,1)S(1)} slice(bf16[2176,384]{1,0:T(8,128)(2,1)} %collective-permute-done.3), slice={[1024:2176], [0:384]} | slice | bytes 1769472 | tf_op jit(solution)/shard_map/slice | solution.py:100
  62.2 1.7 %collective-permute-start.14 = (f32[96,384]{1,0:T(8,128)S(1)}, f32[96,384]{1,0:T(8,128)S(1)}, u32[]{:S(2)}, u32[]{:S(2)}) collective-permute-start(f32[96,384]{1,0:T(8,128)S(1)} %select_bitcast_fusion.7), channel_id=1, source_target_pairs={{0,8},{8,0},{4,12},{12,4},{1,9},{9,1},{5,13},{13,5},{2,10},{10,2},... | collective-permute-start | bytes 442376 | tf_op jit(solution)/shard_map/ppermute | solution.py:63
  63.8 11.3 %collective-permute-done.9 = f32[2,192,384]{2,1,0:T(8,128)S(1)} collective-permute-done((f32[2,192,384]{2,1,0:T(8,128)S(1)}, f32[2,192,384]{2,1,0:T(8,128)S(1)}, u32[]{:S(2)}, u32[]{:S(2)}) %collective-permute-start.9) | collective-permute-done | bytes 589856 | tf_op jit(solution)/shard_map/ppermute | solution.py:58
  75.4 3.0 %collective-permute-start.15 = (bf16[96,384]{1,0:T(8,128)(2,1)S(1)}, bf16[96,384]{1,0:T(8,128)(2,1)S(1)}, u32[]{:S(2)}, u32[]{:S(2)}) collective-permute-start(bf16[96,384]{1,0:T(8,128)(2,1)S(1)} %fusion.69), channel_id=1, source_target_pairs={{0,8},{8,0},{4,12},{12,4},{1,9},{9,1},{5,13},{13,5},{2,10},{10,2},... | collective-permute-start | bytes 221192 | tf_op jit(solution)/shard_map/ppermute | solution.py:64
  78.3 0.8 convolution_bitcast_fusion.3
  79.1 12.5 %collective-permute-done.15 = bf16[96,384]{1,0:T(8,128)(2,1)S(1)} collective-permute-done((bf16[96,384]{1,0:T(8,128)(2,1)S(1)}, bf16[96,384]{1,0:T(8,128)(2,1)S(1)}, u32[]{:S(2)}, u32[]{:S(2)}) %collective-permute-start.15) | collective-permute-done | bytes 73760 | tf_op jit(solution)/shard_map/ppermute | solution.py:64
  91.8 1.8 %collective-permute-start.11 = (bf16[192,384]{1,0:T(8,128)(2,1)S(1)}, bf16[192,384]{1,0:T(8,128)(2,1)S(1)}, u32[]{:S(2)}, u32[]{:S(2)}) collective-permute-start(bf16[192,384]{1,0:T(8,128)(2,1)S(1)} %fusion.68), channel_id=1, source_target_pairs={{0,8},{8,0},{4,12},{12,4},{1,9},{9,1},{5,13},{13,5},{2,10},{10,2},... | collective-permute-start | bytes 442376 | tf_op jit(solution)/shard_map/ppermute | solution.py:64
  93.7 1.6 %fusion.4 = bf16[1,512,384]{2,1,0:T(8,128)(2,1)} fusion(f32[512,384]{1,0:T(8,128)S(1)} %copy-done.7, f32[512,384]{1,0:T(8,128)S(1)} %convolution_bitcast_fusion.3, bf16[3,384,384]{2,1,0:T(8,128)(2,1)S(1)} %bitcast.172, bf16[512,1,384]{2,0,1:T(8,128)(2,1)S(1)} %get-tuple-element.16, bf16[512,1,384]{2,0,1:T(8,128)(2,1)S(1)} %get-tuple-element.8, ...), kind=kOutput, calls=%fused_computation.15 | convolution fusion | flops 454754304 | bytes 4030464 | tf_op jit(solution)/shard_map/tki,kio->to/dot_general | solution.py:110
  95.2 0.4 broadcast_in_dim.18
  95.6 1.2 %convert_element_type.54 = bf16[1,1024,384]{2,1,0:T(8,128)(2,1)} reshape(bf16[512,2,384]{2,1,0:T(2,128)(2,1)S(1)} %broadcast_in_dim.18) | data formatting | bytes 1572864 | tf_op jit(solution)/shard_map/convert_element_type | solution.py:125
  96.8 5.0 %collective-permute-done.11 = bf16[192,384]{1,0:T(8,128)(2,1)S(1)} collective-permute-done((bf16[192,384]{1,0:T(8,128)(2,1)S(1)}, bf16[192,384]{1,0:T(8,128)(2,1)S(1)}, u32[]{:S(2)}, u32[]{:S(2)}) %collective-permute-start.11) | collective-permute-done | bytes 147488 | tf_op jit(solution)/shard_map/ppermute | solution.py:64
  102.1 7.9 %collective-permute-done.12 = bf16[2,192,384]{2,1,0:T(8,128)(2,1)S(1)} collective-permute-done((bf16[2,192,384]{2,1,0:T(8,128)(2,1)S(1)}, bf16[2,192,384]{2,1,0:T(8,128)(2,1)S(1)}, u32[]{:S(2)}, u32[]{:S(2)}) %collective-permute-start.12) | collective-permute-done | bytes 294944 | tf_op jit(solution)/shard_map/ppermute | solution.py:66
  110.0 0.1 select_bitcast_fusion.3
  110.2 1.3 %pad_maximum_fusion = f32[3,384,384]{2,1,0:T(8,128)} fusion(f32[1,384,384]{2,1,0:T(8,128)S(1)} %bitcast.169, f32[1,384,384]{2,1,0:T(8,128)S(1)} %bitcast.167, f32[1,384,384]{2,1,0:T(8,128)S(1)} %bitcast.168), kind=kLoop, calls=%fused_computation.2 | loop fusion | flops 884736 | bytes 3538944 | tf_op jit(solution)/shard_map/stack | solution.py:152
  (48 shorter events, 1.4 us)
Async XLA Ops:
  0.6 1.5 %copy-start = (bf16[3,384,768]{2,1,0:T(8,128)(2,1)S(1)}, bf16[3,384,768]{2,1,0:T(8,128)(2,1)}, u32[]{:S(2)}) copy-start(bf16[3,384,768]{2,1,0:T(8,128)(2,1)} %param.4) | copy-start | bytes 5308420
  2.1 1.1 %copy-start.6 = (bf16[1,1024,384]{2,1,0:T(8,128)(2,1)S(1)}, bf16[1,1024,384]{2,1,0:T(8,128)(2,1)}, u32[]{:S(2)}) copy-start(bf16[1,1024,384]{2,1,0:T(8,128)(2,1)} %param.3) | copy-start | bytes 2359300
  3.2 1.6 %copy-start.1 = (bf16[1,512,384]{2,1,0:T(8,128)(2,1)S(1)}, bf16[1,512,384]{2,1,0:T(8,128)(2,1)}, u32[]{:S(2)}) copy-start(bf16[1,512,384]{2,1,0:T(8,128)(2,1)} %param.5) | copy-start | bytes 1179652
  6.3 33.5 %collective-permute-start.3 = (bf16[2176,384]{1,0:T(8,128)(2,1)}, bf16[2176,384]{1,0:T(8,128)(2,1)}, u32[]{:S(2)}, u32[]{:S(2)}) collective-permute-start(bf16[2176,384]{1,0:T(8,128)(2,1)} %pad_maximum_fusion.1), channel_id=1, source_target_pairs={{0,1},{1,0},{2,3},{3,2},{4,5},{5,4},{6,7},{7,6},{8,9},{9,8},{10,11... | collective-permute-start | bytes 5013512 | tf_op jit(solution)/shard_map/ppermute | solution.py:96
  6.9 13.5 %collective-permute-start = (bf16[2,256,384]{2,1,0:T(8,128)(2,1)S(1)}, bf16[2,256,384]{2,1,0:T(8,128)(2,1)S(1)}, u32[]{:S(2)}, u32[]{:S(2)}) collective-permute-start(bf16[2,256,384]{2,1,0:T(8,128)(2,1)S(1)} %get-tuple-element.25), channel_id=1, source_target_pairs={{0,4},{4,8},{8,12},{1,5},{5,9},{9,13},{2,6},{6,10},{10,14},{3,7},{... | collective-permute-start | bytes 1179656 | tf_op jit(solution)/shard_map/ppermute | solution.py:12
  11.4 13.1 %collective-permute-start.1 = (bf16[2,256,384]{2,1,0:T(8,128)(2,1)S(1)}, bf16[2,256,384]{2,1,0:T(8,128)(2,1)S(1)}, u32[]{:S(2)}, u32[]{:S(2)}) collective-permute-start(bf16[2,256,384]{2,1,0:T(8,128)(2,1)S(1)} %get-tuple-element.26), channel_id=1, source_target_pairs={{4,0},{8,4},{12,8},{5,1},{9,5},{13,9},{6,2},{10,6},{14,10},{7,3},{... | collective-permute-start | bytes 1179656 | tf_op jit(solution)/shard_map/ppermute | solution.py:12
  12.7 14.4 %collective-permute-start.5 = (bf16[512,384]{1,0:T(8,128)(2,1)S(1)}, bf16[512,384]{1,0:T(8,128)(2,1)}, u32[]{:S(2)}, u32[]{:S(2)}) collective-permute-start(bf16[512,384]{1,0:T(8,128)(2,1)S(1)} %bitcast.157), channel_id=1, source_target_pairs={{2,0},{1,3},{6,4},{5,7},{10,8},{9,11},{14,12},{13,15},{18,16},{17,... | collective-permute-start | bytes 1179656 | tf_op jit(solution)/shard_map/ppermute | solution.py:88
  14.0 13.1 %collective-permute-start.6 = (bf16[512,384]{1,0:T(8,128)(2,1)S(1)}, bf16[512,384]{1,0:T(8,128)(2,1)}, u32[]{:S(2)}, u32[]{:S(2)}) collective-permute-start(bf16[512,384]{1,0:T(8,128)(2,1)S(1)} %bitcast.158), channel_id=1, source_target_pairs={{2,1},{1,2},{6,5},{5,6},{10,9},{9,10},{14,13},{13,14},{18,17},{17,... | collective-permute-start | bytes 1179656 | tf_op jit(solution)/shard_map/ppermute | solution.py:89
  20.4 5.2 %copy-start.4 = (bf16[2,256,384]{2,1,0:T(8,128)(2,1)}, bf16[2,256,384]{2,1,0:T(8,128)(2,1)S(1)}, u32[]{:S(2)}) copy-start(bf16[2,256,384]{2,1,0:T(8,128)(2,1)S(1)} %collective-permute-done) | copy-start | bytes 1179652
  24.5 1.0 copy-start.2
  25.6 13.0 %collective-permute-start.2 = (bf16[2,2,256,384]{3,2,1,0:T(8,128)(2,1)}, bf16[2,2,256,384]{3,2,1,0:T(8,128)(2,1)}, u32[]{:S(2)}, u32[]{:S(2)}) collective-permute-start(bf16[2,2,256,384]{3,2,1,0:T(8,128)(2,1)} %pad_maximum_fusion.4), channel_id=1, source_target_pairs={{0,1},{1,0},{2,3},{3,2},{4,5},{5,4},{6,7},{7,6},{8,9},{9,8},{10,11... | collective-permute-start | bytes 2359304 | tf_op jit(solution)/shard_map/ppermute | solution.py:103
  25.6 11.6 %collective-permute-start.4 = (bf16[512,384]{1,0:T(8,128)(2,1)S(1)}, bf16[512,384]{1,0:T(8,128)(2,1)}, u32[]{:S(2)}, u32[]{:S(2)}) collective-permute-start(bf16[512,384]{1,0:T(8,128)(2,1)S(1)} %get-tuple-element.34), channel_id=1, source_target_pairs={{0,2},{2,0},{1,3},{3,1},{4,6},{6,4},{5,7},{7,5},{8,10},{10,8},{9,1... | collective-permute-start | bytes 1179656 | tf_op jit(solution)/shard_map/ppermute | solution.py:91
  28.2 11.6 %copy-start.3 = (bf16[2,256,384]{2,1,0:T(8,128)(2,1)S(1)}, bf16[2,256,384]{2,1,0:T(8,128)(2,1)}, u32[]{:S(2)}) copy-start(bf16[2,256,384]{2,1,0:T(8,128)(2,1)} %copy-done.2) | copy-start | bytes 1179652
  28.2 11.6 %copy-start.5 = (bf16[2,256,384]{2,1,0:T(8,128)(2,1)S(1)}, bf16[2,256,384]{2,1,0:T(8,128)(2,1)}, u32[]{:S(2)}) copy-start(bf16[2,256,384]{2,1,0:T(8,128)(2,1)} %copy-done.4) | copy-start | bytes 1179652
  41.5 15.0 %collective-permute-start.8 = (bf16[256,384]{1,0:T(8,128)(2,1)S(1)}, bf16[256,384]{1,0:T(8,128)(2,1)S(1)}, u32[]{:S(2)}, u32[]{:S(2)}) collective-permute-start(bf16[256,384]{1,0:T(8,128)(2,1)S(1)} %get-tuple-element.29), channel_id=1, source_target_pairs={{0,4},{4,8},{8,12},{1,5},{5,9},{9,13},{2,6},{6,10},{10,14},{3,7},{... | collective-permute-start | bytes 589832 | tf_op jit(solution)/shard_map/ppermute | solution.py:12
  45.0 9.7 %collective-permute-start.7 = (bf16[256,384]{1,0:T(8,128)(2,1)S(1)}, bf16[256,384]{1,0:T(8,128)(2,1)S(1)}, u32[]{:S(2)}, u32[]{:S(2)}) collective-permute-start(bf16[256,384]{1,0:T(8,128)(2,1)S(1)} %get-tuple-element.30), channel_id=1, source_target_pairs={{4,0},{8,4},{12,8},{5,1},{9,5},{13,9},{6,2},{10,6},{14,10},{7,3},{... | collective-permute-start | bytes 589832 | tf_op jit(solution)/shard_map/ppermute | solution.py:12
  46.3 15.8 %collective-permute-start.13 = (f32[2,96,384]{2,1,0:T(8,128)S(1)}, f32[2,96,384]{2,1,0:T(8,128)S(1)}, u32[]{:S(2)}, u32[]{:S(2)}) collective-permute-start(f32[2,96,384]{2,1,0:T(8,128)S(1)} %select_bitcast_fusion.1), channel_id=1, source_target_pairs={{0,4},{4,0},{8,12},{12,8},{1,5},{5,1},{9,13},{13,9},{2,6},{6,2},{1... | collective-permute-start | bytes 884744 | tf_op jit(solution)/shard_map/ppermute | solution.py:58
  58.4 1.1 %copy-start.7 = (f32[512,384]{1,0:T(8,128)S(1)}, f32[512,384]{1,0:T(8,128)}, u32[]{:S(2)}) copy-start(f32[512,384]{1,0:T(8,128)} %get-tuple-element.35) | copy-start | bytes 2359300
  58.5 16.7 %collective-permute-start.9 = (f32[2,192,384]{2,1,0:T(8,128)S(1)}, f32[2,192,384]{2,1,0:T(8,128)S(1)}, u32[]{:S(2)}, u32[]{:S(2)}) collective-permute-start(f32[2,192,384]{2,1,0:T(8,128)S(1)} %select_bitcast_fusion), channel_id=1, source_target_pairs={{0,4},{4,0},{8,12},{12,8},{1,5},{5,1},{9,13},{13,9},{2,6},{6,2},{1... | collective-permute-start | bytes 1769480 | tf_op jit(solution)/shard_map/ppermute | solution.py:58
  62.2 13.1 %collective-permute-start.14 = (f32[96,384]{1,0:T(8,128)S(1)}, f32[96,384]{1,0:T(8,128)S(1)}, u32[]{:S(2)}, u32[]{:S(2)}) collective-permute-start(f32[96,384]{1,0:T(8,128)S(1)} %select_bitcast_fusion.7), channel_id=1, source_target_pairs={{0,8},{8,0},{4,12},{12,4},{1,9},{9,1},{5,13},{13,5},{2,10},{10,2},... | collective-permute-start | bytes 442376 | tf_op jit(solution)/shard_map/ppermute | solution.py:63
  75.3 16.5 %collective-permute-start.10 = (f32[192,384]{1,0:T(8,128)S(1)}, f32[192,384]{1,0:T(8,128)S(1)}, u32[]{:S(2)}, u32[]{:S(2)}) collective-permute-start(f32[192,384]{1,0:T(8,128)S(1)} %select_bitcast_fusion.4), channel_id=1, source_target_pairs={{0,8},{8,0},{4,12},{12,4},{1,9},{9,1},{5,13},{13,5},{2,10},{10,2},... | collective-permute-start | bytes 884744 | tf_op jit(solution)/shard_map/ppermute | solution.py:63
  75.4 16.3 %collective-permute-start.15 = (bf16[96,384]{1,0:T(8,128)(2,1)S(1)}, bf16[96,384]{1,0:T(8,128)(2,1)S(1)}, u32[]{:S(2)}, u32[]{:S(2)}) collective-permute-start(bf16[96,384]{1,0:T(8,128)(2,1)S(1)} %fusion.69), channel_id=1, source_target_pairs={{0,8},{8,0},{4,12},{12,4},{1,9},{9,1},{5,13},{13,5},{2,10},{10,2},... | collective-permute-start | bytes 221192 | tf_op jit(solution)/shard_map/ppermute | solution.py:64
  91.7 10.2 %collective-permute-start.16 = (bf16[2,96,384]{2,1,0:T(8,128)(2,1)S(1)}, bf16[2,96,384]{2,1,0:T(8,128)(2,1)S(1)}, u32[]{:S(2)}, u32[]{:S(2)}) collective-permute-start(bf16[2,96,384]{2,1,0:T(8,128)(2,1)S(1)} %maximum_select_fusion.1), channel_id=1, source_target_pairs={{0,4},{4,0},{8,12},{12,8},{1,5},{5,1},{9,13},{13,9},{2,6},{6,2},{1... | collective-permute-start | bytes 442376 | tf_op jit(solution)/shard_map/ppermute | solution.py:66
  91.8 9.9 %collective-permute-start.11 = (bf16[192,384]{1,0:T(8,128)(2,1)S(1)}, bf16[192,384]{1,0:T(8,128)(2,1)S(1)}, u32[]{:S(2)}, u32[]{:S(2)}) collective-permute-start(bf16[192,384]{1,0:T(8,128)(2,1)S(1)} %fusion.68), channel_id=1, source_target_pairs={{0,8},{8,0},{4,12},{12,4},{1,9},{9,1},{5,13},{13,5},{2,10},{10,2},... | collective-permute-start | bytes 442376 | tf_op jit(solution)/shard_map/ppermute | solution.py:64
  101.8 8.1 %collective-permute-start.12 = (bf16[2,192,384]{2,1,0:T(8,128)(2,1)S(1)}, bf16[2,192,384]{2,1,0:T(8,128)(2,1)S(1)}, u32[]{:S(2)}, u32[]{:S(2)}) collective-permute-start(bf16[2,192,384]{2,1,0:T(8,128)(2,1)S(1)} %maximum_select_fusion), channel_id=1, source_target_pairs={{0,4},{4,0},{8,12},{12,8},{1,5},{5,1},{9,13},{13,9},{2,6},{6,2},{1... | collective-permute-start | bytes 884744 | tf_op jit(solution)/shard_map/ppermute | solution.py:66

commit v14 on v13

--- a/solution.py
+++ b/solution.py
@@ -133,7 +133,6 @@
         centre = jnp.dot(own_taps[:, 1].T, cot_mine, preferred_element_type=jnp.float32) + jnp.dot(
             far_mid.T, far_cot, preferred_element_type=jnp.float32
         )
-        centre, far_cot = lax.optimization_barrier((centre, far_cot))
         cot_next = shift_from(far_cot[:spread], "seq", -1)
         cot_prev = shift_from(far_cot[rows - spread :], "seq", 1)
         far_shifted = {
@@ -147,7 +146,7 @@
                 own_taps[:, k].T, cot_mine, preferred_element_type=jnp.float32
             ) + jnp.dot(far_mid.T, far_shifted[k], preferred_element_type=jnp.float32)
         if seq_count == 4:
-            middle = line_total(grads[1])
+            middle = lax.psum(grads[1], "seq")
             sides = line_total(jnp.concatenate([grads[0], grads[2]], 0))
             weight_grad = jnp.stack([sides[: middle.shape[0]], middle, sides[middle.shape[0] :]])
         else:

time: 112 us -> 115 us (1.027)
  between operations: 1.07 us -> 14.4 us
  waiting for transfers between devices: 57 us -> 46.9 us
  other arithmetic: 7.11 us -> 11.7 us
  local copies, waits for them, and re-layouts: 10.2 us -> 7.72 us
  starting transfers between devices: 24.7 us -> 23.5 us
    ppermute x2 -> x1, waiting for transfers between devices: 17.5 us -> 3.36 us  [line_total(): other = lax.ppermute(total, 'seq', across)]
    ppermute x2 -> x1, waiting for transfers between devices: 0.01 us -> 11.5 us  [line_total(): total = (keep + lax.ppermute(give, 'seq', across)).astype(jnp.bfloat16)]
    ppermute x1, waiting for transfers between devices: 8.99 us -> 0.01 us  [shards(): far_mid = lax.ppermute(activation, 'batch', SWAP)]
    ppermute x2 -> x1, starting transfers between devices: 4.78 us -> 0.07 us  [line_total(): other = lax.ppermute(total, 'seq', across)]
    ppermute x1, starting transfers between devices: 0.49 us -> 4.4 us  [shards(): lax.ppermute(jnp.concatenate([both.reshape(-1, width), w_other.reshape(-1...]
    unnamed x16 -> x32, local copies, waits for them, and re-layouts: 3.48 us -> 0.45 us
    ppermute x2 -> x1, waiting for transfers between devices: 7.9 us -> 10.8 us  [line_total(): far_set = lax.ppermute(own_set, 'seq', pairs)]
    ppermute x4, waiting for transfers between devices: 11.3 us -> 8.46 us  [shift_from(): return lax.ppermute(block, axis, route)]
  transfers between devices with their start and end apart: 17 -> 14, of which waited for: 8 -> 7; matrix products, arithmetic and copies ran while one was open for 17% -> 24% of each run, Pallas kernels for 0% -> 0%
where the time goes in v14:
time: 115 us
  waiting for transfers between devices  46.9 us (41%)
  starting transfers between devices  23.5 us (20%)
  between operations  14.4 us (13%)
  other arithmetic  11.7 us (10%)
  matrix products  10.5 us (9%)
  local copies, waits for them, and re-layouts  7.72 us (7%)
    ppermute x1, waiting for transfers between devices, line_total(): lax.ppermute(jnp.where(odd, even_set, odd_set), 'seq', pairs)  12.8 us
    ppermute x1, waiting for transfers between devices, line_total(): total = (keep + lax.ppermute(give, 'seq', across)).astype(jnp.bfloat16)  11.5 us
    ppermute x1, waiting for transfers between devices, line_total(): far_set = lax.ppermute(own_set, 'seq', pairs)  10.8 us
    ppermute x4, starting transfers between devices, shift_from(): return lax.ppermute(block, axis, route)  10.6 us
    ppermute x4, waiting for transfers between devices, shift_from(): return lax.ppermute(block, axis, route)  8.46 us
    ppermute x1, starting transfers between devices, shards(): lax.ppermute(jnp.concatenate([both.reshape(-1, width), w_other.reshape(-1...  4.4 us
    ppermute x1, waiting for transfers between devices, line_total(): other = lax.ppermute(total, 'seq', across)  3.36 us
    another operation x2, other arithmetic, tap_stack(): return jnp.stack([ext[k * spread:k * spread + rows] for k in order], 1)  3.27 us
  transfers between devices with their start and end apart: 14, of which 7 were waited for; matrix products, arithmetic and copies ran while one was open for 24% of the time, Pallas kernels for 0%

profile of v14, /device:TPU:0, one launch (start us, length us, event | category | flops | bytes accessed | tf_op | source)
XLA Modules:
  0.0 114.8 jit_solution(11821152476815317329)
XLA Ops:
  7.2 1.4 %collective-permute-start.5 = (bf16[512,384]{1,0:T(8,128)(2,1)}, bf16[512,384]{1,0:T(8,128)(2,1)}, u32[]{:S(2)}, u32[]{:S(2)}) collective-permute-start(bf16[512,384]{1,0:T(8,128)(2,1)} %bitcast.127), channel_id=1, source_target_pairs={{2,0},{1,3},{6,4},{5,7},{10,8},{9,11},{14,12},{13,15},{18,16},{17,... | collective-permute-start | bytes 1179656 | tf_op jit(solution)/shard_map/ppermute | solution.py:88
  8.7 1.4 %collective-permute-start.6 = (bf16[512,384]{1,0:T(8,128)(2,1)}, bf16[512,384]{1,0:T(8,128)(2,1)}, u32[]{:S(2)}, u32[]{:S(2)}) collective-permute-start(bf16[512,384]{1,0:T(8,128)(2,1)} %bitcast.128), channel_id=1, source_target_pairs={{2,1},{1,2},{6,5},{5,6},{10,9},{9,10},{14,13},{13,14},{18,17},{17,... | collective-permute-start | bytes 1179656 | tf_op jit(solution)/shard_map/ppermute | solution.py:89
  10.1 2.8 %multiply_convert_fusion = (bf16[512,384]{1,0:T(8,128)(2,1)S(1)}, f32[512,384]{1,0:T(8,128)}) fusion(bf16[1,1024,384]{2,1,0:T(8,128)(2,1)} %param.3, s32[1024]{0:T(1024)S(1)} %get-tuple-element.30, s32[1024]{0:T(1024)S(1)} %get-tuple-element.31, pred[1024]{0:T(1024)(128)(4,1)S(1)} %fusion.70), kind=kOutput, calls=%fused_computation.62 | convolution fusion | flops 406519808 | bytes 1975296 | tf_op jit(solution)/shard_map/dot_general | solution.py:83
  12.9 0.1 pad_maximum_fusion.3
  13.0 0.1 constant_dynamic-slice_fusion
  13.1 1.5 %pad_maximum_fusion.1 = bf16[2176,384]{1,0:T(8,128)(2,1)} fusion(bf16[1152,384]{1,0:T(8,128)(2,1)S(1)} %bitcast.130, bf16[1024,384]{1,0:T(8,128)(2,1)S(1)} %bitcast.134), kind=kLoop, calls=%fused_computation.3 | loop fusion | flops 3342336 | bytes 3342336 | tf_op jit(solution)/shard_map/concatenate | solution.py:97
  14.6 4.4 %collective-permute-start.3 = (bf16[2176,384]{1,0:T(8,128)(2,1)}, bf16[2176,384]{1,0:T(8,128)(2,1)}, u32[]{:S(2)}, u32[]{:S(2)}) collective-permute-start(bf16[2176,384]{1,0:T(8,128)(2,1)} %pad_maximum_fusion.1), channel_id=1, source_target_pairs={{0,1},{1,0},{2,3},{3,2},{4,5},{5,4},{6,7},{7,6},{8,9},{9,8},{10,11... | collective-permute-start | bytes 5013512 | tf_op jit(solution)/shard_map/ppermute | solution.py:96
  19.0 1.6 %collective-permute-start.4 = (bf16[512,384]{1,0:T(8,128)(2,1)S(1)}, bf16[512,384]{1,0:T(8,128)(2,1)S(1)}, u32[]{:S(2)}, u32[]{:S(2)}) collective-permute-start(bf16[512,384]{1,0:T(8,128)(2,1)S(1)} %get-tuple-element.28), channel_id=1, source_target_pairs={{0,2},{2,0},{1,3},{3,1},{4,6},{6,4},{5,7},{7,5},{8,10},{10,8},{9,1... | collective-permute-start | bytes 1179656 | tf_op jit(solution)/shard_map/ppermute | solution.py:91
  20.6 1.0 fusion.48
  21.6 3.5 %collective-permute-start = (bf16[2,256,384]{2,1,0:T(8,128)(2,1)}, bf16[2,256,384]{2,1,0:T(8,128)(2,1)S(1)}, u32[]{:S(2)}, u32[]{:S(2)}) collective-permute-start(bf16[2,256,384]{2,1,0:T(8,128)(2,1)} %get-tuple-element.21), channel_id=1, source_target_pairs={{0,4},{4,8},{8,12},{1,5},{5,9},{9,13},{2,6},{6,10},{10,14},{3,7},{... | collective-permute-start | bytes 1179656 | tf_op jit(solution)/shard_map/ppermute | solution.py:12
  25.1 1.3 %collective-permute-start.1 = (bf16[2,256,384]{2,1,0:T(8,128)(2,1)}, bf16[2,256,384]{2,1,0:T(8,128)(2,1)S(1)}, u32[]{:S(2)}, u32[]{:S(2)}) collective-permute-start(bf16[2,256,384]{2,1,0:T(8,128)(2,1)} %get-tuple-element.22), channel_id=1, source_target_pairs={{4,0},{8,4},{12,8},{5,1},{9,5},{13,9},{6,2},{10,6},{14,10},{7,3},{... | collective-permute-start | bytes 1179656 | tf_op jit(solution)/shard_map/ppermute | solution.py:12
  26.4 1.1 broadcast_select_fusion
  27.5 4.6 %collective-permute-start.8 = (bf16[256,384]{1,0:T(8,128)(2,1)S(1)}, bf16[256,384]{1,0:T(8,128)(2,1)S(1)}, u32[]{:S(2)}, u32[]{:S(2)}) collective-permute-start(bf16[256,384]{1,0:T(8,128)(2,1)S(1)} %get-tuple-element.26), channel_id=1, source_target_pairs={{0,4},{4,8},{8,12},{1,5},{5,9},{9,13},{2,6},{6,10},{10,14},{3,7},{... | collective-permute-start | bytes 589832 | tf_op jit(solution)/shard_map/ppermute | solution.py:12
  32.1 2.8 %collective-permute-done = bf16[2,256,384]{2,1,0:T(8,128)(2,1)S(1)} collective-permute-done((bf16[2,256,384]{2,1,0:T(8,128)(2,1)}, bf16[2,256,384]{2,1,0:T(8,128)(2,1)S(1)}, u32[]{:S(2)}, u32[]{:S(2)}) %collective-permute-start) | collective-permute-done | bytes 393248 | tf_op jit(solution)/shard_map/ppermute | solution.py:12
  34.9 1.3 %collective-permute-start.7 = (bf16[256,384]{1,0:T(8,128)(2,1)S(1)}, bf16[256,384]{1,0:T(8,128)(2,1)S(1)}, u32[]{:S(2)}, u32[]{:S(2)}) collective-permute-start(bf16[256,384]{1,0:T(8,128)(2,1)S(1)} %get-tuple-element.27), channel_id=1, source_target_pairs={{4,0},{8,4},{12,8},{5,1},{9,5},{13,9},{6,2},{10,6},{14,10},{7,3},{... | collective-permute-start | bytes 589832 | tf_op jit(solution)/shard_map/ppermute | solution.py:12
  36.2 2.0 %collective-permute-done.1 = bf16[2,256,384]{2,1,0:T(8,128)(2,1)S(1)} collective-permute-done((bf16[2,256,384]{2,1,0:T(8,128)(2,1)}, bf16[2,256,384]{2,1,0:T(8,128)(2,1)S(1)}, u32[]{:S(2)}, u32[]{:S(2)}) %collective-permute-start.1) | collective-permute-done | bytes 393248 | tf_op jit(solution)/shard_map/ppermute | solution.py:12
  38.2 0.1 pad_maximum_fusion.4
  38.4 0.4 fusion.85
  38.8 0.4 fusion.58
  39.2 3.7 %collective-permute-done.7 = bf16[256,384]{1,0:T(8,128)(2,1)S(1)} collective-permute-done((bf16[256,384]{1,0:T(8,128)(2,1)S(1)}, bf16[256,384]{1,0:T(8,128)(2,1)S(1)}, u32[]{:S(2)}, u32[]{:S(2)}) %collective-permute-start.7) | collective-permute-done | bytes 196640 | tf_op jit(solution)/shard_map/ppermute | solution.py:12
  42.8 0.4 fusion.54
  43.2 2.2 %fusion.53 = (bf16[512,1,384]{2,0,1:T(8,128)(2,1)}, bf16[512,1,384]{2,0,1:T(8,128)(2,1)}, bf16[512,1,384]{2,0,1:T(8,128)(2,1)}, bf16[512,1,384]{2,0,1:T(8,128)(2,1)}, bf16[1,512,384]{2,1,0:T(8,128)(2,1)S(1)}) fusion(bf16[2,256,384]{2,1,0:T(8,128)(2,1)S(1)} %collective-permute-done.1, bf16[1,512,384]{2,1,0:T(8,128)(2,1)S(1)} %copy-done.1, ...), kind=kLoop, calls=%fused_computation.80 | loop fusion | flops 4915200 | bytes 3932161 | tf_op jit(solution)/shard_map/stack | solution.py:21
  45.5 0.4 convolution_add_fusion.1
  45.9 0.4 convolution_add_fusion.2
  46.4 0.9 select_bitcast_fusion
  47.3 2.0 %collective-permute-start.9 = (f32[2,192,384]{2,1,0:T(8,128)}, f32[2,192,384]{2,1,0:T(8,128)}, u32[]{:S(2)}, u32[]{:S(2)}) collective-permute-start(f32[2,192,384]{2,1,0:T(8,128)} %select_bitcast_fusion), channel_id=1, source_target_pairs={{0,4},{4,0},{8,12},{12,8},{1,5},{5,1},{9,13},{13,9},{2,6},{6,2},{1... | collective-permute-start | bytes 1769480 | tf_op jit(solution)/shard_map/ppermute | solution.py:58
  49.2 1.0 slice_bitcast_fusion.2
  50.2 1.2 %fusion.4 = f32[1,384,384]{2,1,0:T(8,128)} fusion(f32[384,384]{1,0:T(8,128)S(1)} %fusion.85, bf16[512,384]{1,0:T(8,128)(2,1)S(1)} %get-tuple-element.28, bf16[1,512,384]{2,1,0:T(8,128)(2,1)S(1)} %get-tuple-element.25), kind=kOutput, calls=%fused_computation.13 | convolution fusion | flops 151142400 | bytes 1966080 | tf_op jit(solution)/shard_map/dot_general | solution.py:133
  51.4 1.2 %slice.166 = bf16[1024,384]{1,0:T(8,128)(2,1)S(1)} slice(bf16[2176,384]{1,0:T(8,128)(2,1)} %collective-permute-done.3), slice={[0:1024], [0:384]} | slice | bytes 1572864 | tf_op jit(solution)/shard_map/slice | solution.py:99
  52.6 1.9 %slice_bitcast_fusion.3 = (bf16[512,1,384]{2,0,1:T(8,128)(2,1)S(1)}, bf16[512,1,384]{2,0,1:T(8,128)(2,1)}) fusion(bf16[2176,384]{1,0:T(8,128)(2,1)} %collective-permute-done.3), kind=kLoop, calls=%fused_computation.104 | loop fusion | bytes 1572864 | tf_op jit(solution)/shard_map/stack | solution.py:21
  54.6 12.8 %collective-permute-done.9 = f32[2,192,384]{2,1,0:T(8,128)} collective-permute-done((f32[2,192,384]{2,1,0:T(8,128)}, f32[2,192,384]{2,1,0:T(8,128)}, u32[]{:S(2)}, u32[]{:S(2)}) %collective-permute-start.9) | collective-permute-done | bytes 589856 | tf_op jit(solution)/shard_map/ppermute | solution.py:58
  67.3 1.1 fusion.47
  68.5 0.4 collective-permute-start.10
  68.9 1.0 fusion.51
  69.9 0.3 copy-done.4
  70.3 0.8 convolution_bitcast_fusion
  71.1 11.5 %collective-permute-done.10 = f32[192,384]{1,0:T(8,128)S(1)} collective-permute-done((f32[192,384]{1,0:T(8,128)S(1)}, f32[192,384]{1,0:T(8,128)S(1)}, u32[]{:S(2)}, u32[]{:S(2)}) %collective-permute-start.10) | collective-permute-done | bytes 294944 | tf_op jit(solution)/shard_map/ppermute | solution.py:63
  82.8 1.3 %fusion.40 = bf16[512,384]{1,0:T(8,128)(2,1)S(1)} fusion(f32[512,384]{1,0:T(8,128)S(1)} %copy-done.14, f32[512,384]{1,0:T(8,128)S(1)} %convolution_bitcast_fusion, bf16[512,1,384]{2,0,1:T(8,128)(2,1)S(1)} %copy-done.10, bf16[512,1,384]{2,0,1:T(8,128)(2,1)S(1)} %bitcast.129, bf16[512,1,384]{2,0,1:T(8,128)(2,1)S(1)} %copy-done.9, ...), kind=kOutput, calls=%fused_computation.59 | convolution fusion | flops 458883072 | bytes 4423684 | tf_op jit(solution)/shard_map/tko,kio->ti/dot_general | solution.py:116
  84.1 0.4 broadcast_in_dim.18
  84.5 1.2 %convert_element_type.38 = bf16[1,1024,384]{2,1,0:T(8,128)(2,1)} reshape(bf16[512,2,384]{2,1,0:T(2,128)(2,1)S(1)} %broadcast_in_dim.18) | data formatting | bytes 1572864 | tf_op jit(solution)/shard_map/convert_element_type | solution.py:125
  85.7 1.4 %slice.169 = bf16[1152,384]{1,0:T(8,128)(2,1)S(1)} slice(bf16[2176,384]{1,0:T(8,128)(2,1)} %collective-permute-done.3), slice={[1024:2176], [0:384]} | slice | bytes 1769472 | tf_op jit(solution)/shard_map/slice | solution.py:100
  87.1 0.8 convolution_bitcast_fusion.3
  87.9 3.4 %collective-permute-done.11 = bf16[192,384]{1,0:T(8,128)(2,1)S(1)} collective-permute-done((bf16[192,384]{1,0:T(8,128)(2,1)S(1)}, bf16[192,384]{1,0:T(8,128)(2,1)S(1)}, u32[]{:S(2)}, u32[]{:S(2)}) %collective-permute-start.11) | collective-permute-done | bytes 147488 | tf_op jit(solution)/shard_map/ppermute | solution.py:64
  91.3 1.5 %collective-permute-start.12 = (bf16[2,192,384]{2,1,0:T(8,128)(2,1)S(1)}, bf16[2,192,384]{2,1,0:T(8,128)(2,1)S(1)}, u32[]{:S(2)}, u32[]{:S(2)}) collective-permute-start(bf16[2,192,384]{2,1,0:T(8,128)(2,1)S(1)} %maximum_select_fusion), channel_id=1, source_target_pairs={{0,4},{4,0},{8,12},{12,8},{1,5},{5,1},{9,13},{13,9},{2,6},{6,2},{1... | collective-permute-start | bytes 884744 | tf_op jit(solution)/shard_map/ppermute | solution.py:66
  92.9 1.6 %fusion.5 = bf16[1,512,384]{2,1,0:T(8,128)(2,1)} fusion(f32[512,384]{1,0:T(8,128)S(1)} %copy-done.15, f32[512,384]{1,0:T(8,128)S(1)} %convolution_bitcast_fusion.3, bf16[3,384,384]{2,1,0:T(8,128)(2,1)S(1)} %bitcast.139, bf16[512,1,384]{2,0,1:T(8,128)(2,1)S(1)} %copy-done.11, bf16[512,1,384]{2,0,1:T(8,128)(2,1)S(1)} %copy-done.13, ...), kind=kOutput, calls=%fused_computation.16 | convolution fusion | flops 454754304 | bytes 4030464 | tf_op jit(solution)/shard_map/tki,kio->to/dot_general | solution.py:110
  94.4 10.8 %collective-permute-done.12 = bf16[2,192,384]{2,1,0:T(8,128)(2,1)S(1)} collective-permute-done((bf16[2,192,384]{2,1,0:T(8,128)(2,1)S(1)}, bf16[2,192,384]{2,1,0:T(8,128)(2,1)S(1)}, u32[]{:S(2)}, u32[]{:S(2)}) %collective-permute-start.12) | collective-permute-done | bytes 294944 | tf_op jit(solution)/shard_map/ppermute | solution.py:66
  105.3 0.1 select_bitcast_fusion.2
  105.6 2.4 %pad_maximum_fusion = f32[3,384,384]{2,1,0:T(8,128)} fusion(f32[1,384,384]{2,1,0:T(8,128)S(1)} %bitcast.136, f32[1,384,384]{2,1,0:T(8,128)} %all-reduce.2.cloned.1.call-done, f32[1,384,384]{2,1,0:T(8,128)S(1)} %bitcast.135), kind=kLoop, calls=%fused_computation.2 | loop fusion | flops 884736 | bytes 3538944 | tf_op jit(solution)/shard_map/stack | solution.py:151
  (51 shorter events, 0.8 us)
Async XLA Ops:
  7.2 5.9 %copy-start = (bf16[3,384,768]{2,1,0:T(8,128)(2,1)S(1)}, bf16[3,384,768]{2,1,0:T(8,128)(2,1)}, u32[]{:S(2)}) copy-start(bf16[3,384,768]{2,1,0:T(8,128)(2,1)} %param.4) | copy-start | bytes 5308420
  7.2 98.4 %all-reduce.2.cloned.1.call-start = ((), (), s32[]{:S(2)}) async-start(), calls=%async_computation | async-start | bytes 1179648 | tf_op jit(solution)/shard_map/psum | solution.py:149
  7.2 17.9 %collective-permute-start.5 = (bf16[512,384]{1,0:T(8,128)(2,1)}, bf16[512,384]{1,0:T(8,128)(2,1)}, u32[]{:S(2)}, u32[]{:S(2)}) collective-permute-start(bf16[512,384]{1,0:T(8,128)(2,1)} %bitcast.127), channel_id=1, source_target_pairs={{2,0},{1,3},{6,4},{5,7},{10,8},{9,11},{14,12},{13,15},{18,16},{17,... | collective-permute-start | bytes 1179656 | tf_op jit(solution)/shard_map/ppermute | solution.py:88
  8.7 17.8 %collective-permute-start.6 = (bf16[512,384]{1,0:T(8,128)(2,1)}, bf16[512,384]{1,0:T(8,128)(2,1)}, u32[]{:S(2)}, u32[]{:S(2)}) collective-permute-start(bf16[512,384]{1,0:T(8,128)(2,1)} %bitcast.128), channel_id=1, source_target_pairs={{2,1},{1,2},{6,5},{5,6},{10,9},{9,10},{14,13},{13,14},{18,17},{17,... | collective-permute-start | bytes 1179656 | tf_op jit(solution)/shard_map/ppermute | solution.py:89
  10.1 2.8 %copy-start.1 = (bf16[1,512,384]{2,1,0:T(8,128)(2,1)S(1)}, bf16[1,512,384]{2,1,0:T(8,128)(2,1)}, u32[]{:S(2)}) copy-start(bf16[1,512,384]{2,1,0:T(8,128)(2,1)} %param.5) | copy-start | bytes 1179652
  13.1 1.5 %copy-start.3 = (bf16[3,384,384]{2,1,0:T(8,128)(2,1)}, bf16[3,384,384]{2,1,0:T(8,128)(2,1)S(1)}, u32[]{:S(2)}) copy-start(bf16[3,384,384]{2,1,0:T(8,128)(2,1)S(1)} %constant_dynamic-slice_fusion) | copy-start | bytes 2654212
  14.6 28.6 %collective-permute-start.3 = (bf16[2176,384]{1,0:T(8,128)(2,1)}, bf16[2176,384]{1,0:T(8,128)(2,1)}, u32[]{:S(2)}, u32[]{:S(2)}) collective-permute-start(bf16[2176,384]{1,0:T(8,128)(2,1)} %pad_maximum_fusion.1), channel_id=1, source_target_pairs={{0,1},{1,0},{2,3},{3,2},{4,5},{5,4},{6,7},{7,6},{8,9},{9,8},{10,11... | collective-permute-start | bytes 5013512 | tf_op jit(solution)/shard_map/ppermute | solution.py:96
  19.0 19.4 %collective-permute-start.4 = (bf16[512,384]{1,0:T(8,128)(2,1)S(1)}, bf16[512,384]{1,0:T(8,128)(2,1)S(1)}, u32[]{:S(2)}, u32[]{:S(2)}) collective-permute-start(bf16[512,384]{1,0:T(8,128)(2,1)S(1)} %get-tuple-element.28), channel_id=1, source_target_pairs={{0,2},{2,0},{1,3},{3,1},{4,6},{6,4},{5,7},{7,5},{8,10},{10,8},{9,1... | collective-permute-start | bytes 1179656 | tf_op jit(solution)/shard_map/ppermute | solution.py:91
  21.6 13.3 %collective-permute-start = (bf16[2,256,384]{2,1,0:T(8,128)(2,1)}, bf16[2,256,384]{2,1,0:T(8,128)(2,1)S(1)}, u32[]{:S(2)}, u32[]{:S(2)}) collective-permute-start(bf16[2,256,384]{2,1,0:T(8,128)(2,1)} %get-tuple-element.21), channel_id=1, source_target_pairs={{0,4},{4,8},{8,12},{1,5},{5,9},{9,13},{2,6},{6,10},{10,14},{3,7},{... | collective-permute-start | bytes 1179656 | tf_op jit(solution)/shard_map/ppermute | solution.py:12
  25.1 13.1 %collective-permute-start.1 = (bf16[2,256,384]{2,1,0:T(8,128)(2,1)}, bf16[2,256,384]{2,1,0:T(8,128)(2,1)S(1)}, u32[]{:S(2)}, u32[]{:S(2)}) collective-permute-start(bf16[2,256,384]{2,1,0:T(8,128)(2,1)} %get-tuple-element.22), channel_id=1, source_target_pairs={{4,0},{8,4},{12,8},{5,1},{9,5},{13,9},{6,2},{10,6},{14,10},{7,3},{... | collective-permute-start | bytes 1179656 | tf_op jit(solution)/shard_map/ppermute | solution.py:12
  27.5 11.2 %collective-permute-start.8 = (bf16[256,384]{1,0:T(8,128)(2,1)S(1)}, bf16[256,384]{1,0:T(8,128)(2,1)S(1)}, u32[]{:S(2)}, u32[]{:S(2)}) collective-permute-start(bf16[256,384]{1,0:T(8,128)(2,1)S(1)} %get-tuple-element.26), channel_id=1, source_target_pairs={{0,4},{4,8},{8,12},{1,5},{5,9},{9,13},{2,6},{6,10},{10,14},{3,7},{... | collective-permute-start | bytes 589832 | tf_op jit(solution)/shard_map/ppermute | solution.py:12
  34.9 8.0 %collective-permute-start.7 = (bf16[256,384]{1,0:T(8,128)(2,1)S(1)}, bf16[256,384]{1,0:T(8,128)(2,1)S(1)}, u32[]{:S(2)}, u32[]{:S(2)}) collective-permute-start(bf16[256,384]{1,0:T(8,128)(2,1)S(1)} %get-tuple-element.27), channel_id=1, source_target_pairs={{4,0},{8,4},{12,8},{5,1},{9,5},{13,9},{6,2},{10,6},{14,10},{7,3},{... | collective-permute-start | bytes 589832 | tf_op jit(solution)/shard_map/ppermute | solution.py:12
  38.3 10.9 %collective-permute-start.2 = (bf16[2,2,256,384]{3,2,1,0:T(8,128)(2,1)S(1)}, bf16[2,2,256,384]{3,2,1,0:T(8,128)(2,1)S(1)}, u32[]{:S(2)}, u32[]{:S(2)}) collective-permute-start(bf16[2,2,256,384]{3,2,1,0:T(8,128)(2,1)S(1)} %pad_maximum_fusion.4), channel_id=1, source_target_pairs={{0,1},{1,0},{2,3},{3,2},{4,5},{5,4},{6,7},{7,6},{8,9},{9,8},{10,11... | collective-permute-start | bytes 2359304 | tf_op jit(solution)/shard_map/ppermute | solution.py:103
  47.3 20.1 %collective-permute-start.9 = (f32[2,192,384]{2,1,0:T(8,128)}, f32[2,192,384]{2,1,0:T(8,128)}, u32[]{:S(2)}, u32[]{:S(2)}) collective-permute-start(f32[2,192,384]{2,1,0:T(8,128)} %select_bitcast_fusion), channel_id=1, source_target_pairs={{0,4},{4,0},{8,12},{12,8},{1,5},{5,1},{9,13},{13,9},{2,6},{6,2},{1... | collective-permute-start | bytes 1769480 | tf_op jit(solution)/shard_map/ppermute | solution.py:58
  54.6 14.3 %copy-start.5 = (bf16[2,256,384]{2,1,0:T(8,128)(2,1)S(1)}, bf16[2,256,384]{2,1,0:T(8,128)(2,1)}, u32[]{:S(2)}) copy-start(bf16[2,256,384]{2,1,0:T(8,128)(2,1)} %get-tuple-element.19) | copy-start | bytes 1179652
  54.6 14.3 %copy-start.6 = (bf16[2,256,384]{2,1,0:T(8,128)(2,1)S(1)}, bf16[2,256,384]{2,1,0:T(8,128)(2,1)}, u32[]{:S(2)}) copy-start(bf16[2,256,384]{2,1,0:T(8,128)(2,1)} %get-tuple-element.20) | copy-start | bytes 1179652
  68.5 14.1 %collective-permute-start.10 = (f32[192,384]{1,0:T(8,128)S(1)}, f32[192,384]{1,0:T(8,128)S(1)}, u32[]{:S(2)}, u32[]{:S(2)}) collective-permute-start(f32[192,384]{1,0:T(8,128)S(1)} %select_bitcast_fusion.3), channel_id=1, source_target_pairs={{0,8},{8,0},{4,12},{12,4},{1,9},{9,1},{5,13},{13,5},{2,10},{10,2},... | collective-permute-start | bytes 884744 | tf_op jit(solution)/shard_map/ppermute | solution.py:63
  68.9 1.4 %copy-start.4 = (bf16[3,384,384]{2,1,0:T(8,128)(2,1)S(1)}, bf16[3,384,384]{2,1,0:T(8,128)(2,1)}, u32[]{:S(2)}) copy-start(bf16[3,384,384]{2,1,0:T(8,128)(2,1)} %copy-done.3) | copy-start | bytes 2654212
  70.3 12.4 %copy-start.2 = (bf16[1,512,384]{2,1,0:T(8,128)(2,1)S(1)}, bf16[1,512,384]{2,1,0:T(8,128)(2,1)}, u32[]{:S(2)}) copy-start(bf16[1,512,384]{2,1,0:T(8,128)(2,1)} %param.5) | copy-start | bytes 1179652
  70.3 12.4 %copy-start.9 = (bf16[512,1,384]{2,0,1:T(8,128)(2,1)S(1)}, bf16[512,1,384]{2,0,1:T(8,128)(2,1)}, u32[]{:S(2)}) copy-start(bf16[512,1,384]{2,0,1:T(8,128)(2,1)} %get-tuple-element.7) | copy-start | bytes 1179652
  70.3 12.4 %copy-start.10 = (bf16[512,1,384]{2,0,1:T(8,128)(2,1)S(1)}, bf16[512,1,384]{2,0,1:T(8,128)(2,1)}, u32[]{:S(2)}) copy-start(bf16[512,1,384]{2,0,1:T(8,128)(2,1)} %get-tuple-element.16) | copy-start | bytes 1179652
  70.3 12.5 %copy-start.14 = (f32[512,384]{1,0:T(8,128)S(1)}, f32[512,384]{1,0:T(8,128)}, u32[]{:S(2)}) copy-start(f32[512,384]{1,0:T(8,128)} %get-tuple-element.29) | copy-start | bytes 2359300
  82.6 8.6 %collective-permute-start.11 = (bf16[192,384]{1,0:T(8,128)(2,1)S(1)}, bf16[192,384]{1,0:T(8,128)(2,1)S(1)}, u32[]{:S(2)}, u32[]{:S(2)}) collective-permute-start(bf16[192,384]{1,0:T(8,128)(2,1)S(1)} %fusion.67), channel_id=1, source_target_pairs={{0,8},{8,0},{4,12},{12,4},{1,9},{9,1},{5,13},{13,5},{2,10},{10,2},... | collective-permute-start | bytes 442376 | tf_op jit(solution)/shard_map/ppermute | solution.py:64
  85.7 1.4 %copy-start.7 = (bf16[512,1,384]{2,0,1:T(8,128)(2,1)S(1)}, bf16[512,1,384]{2,0,1:T(8,128)(2,1)}, u32[]{:S(2)}) copy-start(bf16[512,1,384]{2,0,1:T(8,128)(2,1)} %get-tuple-element.8) | copy-start | bytes 1179652
  85.7 1.4 %copy-start.8 = (bf16[512,1,384]{2,0,1:T(8,128)(2,1)S(1)}, bf16[512,1,384]{2,0,1:T(8,128)(2,1)}, u32[]{:S(2)}) copy-start(bf16[512,1,384]{2,0,1:T(8,128)(2,1)} %get-tuple-element.15) | copy-start | bytes 1179652
  87.1 5.8 %copy-start.11 = (bf16[512,1,384]{2,0,1:T(8,128)(2,1)S(1)}, bf16[512,1,384]{2,0,1:T(8,128)(2,1)}, u32[]{:S(2)}) copy-start(bf16[512,1,384]{2,0,1:T(8,128)(2,1)} %get-tuple-element.12) | copy-start | bytes 1179652
  87.1 5.8 %copy-start.12 = (bf16[512,1,384]{2,0,1:T(8,128)(2,1)S(1)}, bf16[512,1,384]{2,0,1:T(8,128)(2,1)}, u32[]{:S(2)}) copy-start(bf16[512,1,384]{2,0,1:T(8,128)(2,1)} %get-tuple-element.17) | copy-start | bytes 1179652
  87.1 5.8 %copy-start.13 = (bf16[512,1,384]{2,0,1:T(8,128)(2,1)S(1)}, bf16[512,1,384]{2,0,1:T(8,128)(2,1)}, u32[]{:S(2)}) copy-start(bf16[512,1,384]{2,0,1:T(8,128)(2,1)} %get-tuple-element.4) | copy-start | bytes 1179652
  87.1 5.8 %copy-start.15 = (f32[512,384]{1,0:T(8,128)S(1)}, f32[512,384]{1,0:T(8,128)}, u32[]{:S(2)}) copy-start(f32[512,384]{1,0:T(8,128)} %get-tuple-element.29) | copy-start | bytes 2359300
  91.3 13.9 %collective-permute-start.12 = (bf16[2,192,384]{2,1,0:T(8,128)(2,1)S(1)}, bf16[2,192,384]{2,1,0:T(8,128)(2,1)S(1)}, u32[]{:S(2)}, u32[]{:S(2)}) collective-permute-start(bf16[2,192,384]{2,1,0:T(8,128)(2,1)S(1)} %maximum_select_fusion), channel_id=1, source_target_pairs={{0,4},{4,0},{8,12},{12,8},{1,5},{5,1},{9,13},{13,9},{2,6},{6,2},{1... | collective-permute-start | bytes 884744 | tf_op jit(solution)/shard_map/ppermute | solution.py:66
Sparse Core Ops, SparseCore 0:
  51.5 50.9 all-reduce.1

commit v15 on v13

--- a/solution.py
+++ b/solution.py
@@ -130,10 +130,9 @@
     seq_count = lax.axis_size("seq")
     if batch_count == 2:
         cot_mine = jnp.where(b == c, local_cot, par_cot)
-        centre = jnp.dot(own_taps[:, 1].T, cot_mine, preferred_element_type=jnp.float32) + jnp.dot(
+        centre = jnp.dot(activation.T, cot_mine, preferred_element_type=jnp.float32) + jnp.dot(
             far_mid.T, far_cot, preferred_element_type=jnp.float32
         )
-        centre, far_cot = lax.optimization_barrier((centre, far_cot))
         cot_next = shift_from(far_cot[:spread], "seq", -1)
         cot_prev = shift_from(far_cot[rows - spread :], "seq", 1)
         far_shifted = {

time: 112 us -> 108 us (0.964)
  waiting for transfers between devices: 57 us -> 38.3 us
  starting transfers between devices: 24.7 us -> 36.7 us
  matrix products: 11.5 us -> 15.8 us
  local copies, waits for them, and re-layouts: 10.2 us -> 6.64 us
  other arithmetic: 7.11 us -> 8.93 us
    ppermute x2, waiting for transfers between devices: 0.01 us -> 17.1 us  [line_total(): total = (keep + lax.ppermute(give, 'seq', across)).astype(jnp.bfloat16)]
    ppermute x2, waiting for transfers between devices: 17.5 us -> 6.01 us  [line_total(): other = lax.ppermute(total, 'seq', across)]
    ppermute x2, waiting for transfers between devices: 11.3 us -> 2.13 us  [line_total(): lax.ppermute(jnp.where(odd, even_set, odd_set), 'seq', pairs)]
    ppermute x1, waiting for transfers between devices: 8.99 us -> 0.01 us  [shards(): far_mid = lax.ppermute(activation, 'batch', SWAP)]
    ppermute x2, starting transfers between devices: 0.14 us -> 8.06 us  [line_total(): far_set = lax.ppermute(own_set, 'seq', pairs)]
    ppermute x4, waiting for transfers between devices: 11.3 us -> 4.29 us  [shift_from(): return lax.ppermute(block, axis, route)]
    ppermute x1, starting transfers between devices: 1.56 us -> 6 us  [shards(): far_mid = lax.ppermute(activation, 'batch', SWAP)]
    unnamed x16 -> x8, local copies, waits for them, and re-layouts: 3.48 us -> 1.06 us
  transfers between devices with their start and end apart: 17 -> 17, of which waited for: 8 -> 8; matrix products, arithmetic and copies ran while one was open for 17% -> 25% of each run, Pallas kernels for 0% -> 0%
where the time goes in v15:
time: 108 us; the launch traced here: 107 us
  waiting for transfers between devices  38.3 us (35%)
  starting transfers between devices  36.7 us (34%)
  matrix products  15.8 us (15%)
  other arithmetic  8.93 us (8%)
  local copies, waits for them, and re-layouts  6.64 us (6%)
    ppermute x2, waiting for transfers between devices, line_total(): total = (keep + lax.ppermute(give, 'seq', across)).astype(jnp.bfloat16)  17.1 us
    ppermute x4, starting transfers between devices, shift_from(): return lax.ppermute(block, axis, route)  10.6 us
    ppermute x2, waiting for transfers between devices, line_total(): far_set = lax.ppermute(own_set, 'seq', pairs)  8.76 us
    ppermute x2, starting transfers between devices, line_total(): far_set = lax.ppermute(own_set, 'seq', pairs)  8.06 us
    ppermute x2, waiting for transfers between devices, line_total(): other = lax.ppermute(total, 'seq', across)  6.01 us
    ppermute x1, starting transfers between devices, shards(): far_mid = lax.ppermute(activation, 'batch', SWAP)  6 us
    ppermute x4, waiting for transfers between devices, shift_from(): return lax.ppermute(block, axis, route)  4.29 us
    ppermute x2, starting transfers between devices, line_total(): other = lax.ppermute(total, 'seq', across)  3.52 us
  transfers between devices with their start and end apart: 17, of which 8 were waited for; matrix products, arithmetic and copies ran while one was open for 25% of the time, Pallas kernels for 0%

profile of v15, /device:TPU:0, one launch (start us, length us, event | category | flops | bytes accessed | tf_op | source)
XLA Modules:
  0.0 107.4 jit_solution(14305979381563138056)
XLA Ops:
  0.6 1.4 %collective-permute-start.5 = (bf16[512,384]{1,0:T(8,128)(2,1)}, bf16[512,384]{1,0:T(8,128)(2,1)}, u32[]{:S(2)}, u32[]{:S(2)}) collective-permute-start(bf16[512,384]{1,0:T(8,128)(2,1)} %bitcast.157), channel_id=1, source_target_pairs={{2,0},{1,3},{6,4},{5,7},{10,8},{9,11},{14,12},{13,15},{18,16},{17,... | collective-permute-start | bytes 1179656 | tf_op jit(solution)/shard_map/ppermute | solution.py:88
  2.1 1.4 %collective-permute-start.6 = (bf16[512,384]{1,0:T(8,128)(2,1)}, bf16[512,384]{1,0:T(8,128)(2,1)}, u32[]{:S(2)}, u32[]{:S(2)}) collective-permute-start(bf16[512,384]{1,0:T(8,128)(2,1)} %bitcast.158), channel_id=1, source_target_pairs={{2,1},{1,2},{6,5},{5,6},{10,9},{9,10},{14,13},{13,14},{18,17},{17,... | collective-permute-start | bytes 1179656 | tf_op jit(solution)/shard_map/ppermute | solution.py:89
  3.5 2.8 %multiply_convert_fusion = (bf16[512,384]{1,0:T(8,128)(2,1)S(1)}, f32[512,384]{1,0:T(8,128)}) fusion(bf16[1,1024,384]{2,1,0:T(8,128)(2,1)} %param.3, s32[1024]{0:T(1024)S(1)} %get-tuple-element.31, s32[1024]{0:T(1024)S(1)} %get-tuple-element.32, pred[1024]{0:T(1024)(128)(4,1)S(1)} %fusion.74), kind=kOutput, calls=%fused_computation.61 | convolution fusion | flops 406519808 | bytes 1975296 | tf_op jit(solution)/shard_map/dot_general | solution.py:83
  6.3 6.0 %collective-permute-start.4 = (bf16[512,384]{1,0:T(8,128)(2,1)S(1)}, bf16[512,384]{1,0:T(8,128)(2,1)}, u32[]{:S(2)}, u32[]{:S(2)}) collective-permute-start(bf16[512,384]{1,0:T(8,128)(2,1)S(1)} %get-tuple-element.29), channel_id=1, source_target_pairs={{0,2},{2,0},{1,3},{3,1},{4,6},{6,4},{5,7},{7,5},{8,10},{10,8},{9,1... | collective-permute-start | bytes 1179656 | tf_op jit(solution)/shard_map/ppermute | solution.py:91
  12.4 1.0 pad_maximum_fusion.3
  13.3 0.1 constant_dynamic-slice_fusion
  13.4 1.0 copy-done.2
  14.5 1.3 %pad_maximum_fusion.1 = bf16[2176,384]{1,0:T(8,128)(2,1)} fusion(bf16[1152,384]{1,0:T(8,128)(2,1)S(1)} %bitcast.170, bf16[1024,384]{1,0:T(8,128)(2,1)S(1)} %bitcast.173), kind=kLoop, calls=%fused_computation.3 | loop fusion | flops 3342336 | bytes 3342336 | tf_op jit(solution)/shard_map/concatenate | solution.py:97
  15.8 1.0 fusion.47
  16.8 1.3 %collective-permute-start.1 = (bf16[2,256,384]{2,1,0:T(8,128)(2,1)}, bf16[2,256,384]{2,1,0:T(8,128)(2,1)}, u32[]{:S(2)}, u32[]{:S(2)}) collective-permute-start(bf16[2,256,384]{2,1,0:T(8,128)(2,1)} %get-tuple-element.22), channel_id=1, source_target_pairs={{4,0},{8,4},{12,8},{5,1},{9,5},{13,9},{6,2},{10,6},{14,10},{7,3},{... | collective-permute-start | bytes 1179656 | tf_op jit(solution)/shard_map/ppermute | solution.py:12
  18.1 4.6 %collective-permute-start = (bf16[2,256,384]{2,1,0:T(8,128)(2,1)}, bf16[2,256,384]{2,1,0:T(8,128)(2,1)S(1)}, u32[]{:S(2)}, u32[]{:S(2)}) collective-permute-start(bf16[2,256,384]{2,1,0:T(8,128)(2,1)} %get-tuple-element.21), channel_id=1, source_target_pairs={{0,4},{4,8},{8,12},{1,5},{5,9},{9,13},{2,6},{6,10},{10,14},{3,7},{... | collective-permute-start | bytes 1179656 | tf_op jit(solution)/shard_map/ppermute | solution.py:12
  22.7 1.1 broadcast_select_fusion
  23.8 3.5 %collective-permute-start.8 = (bf16[256,384]{1,0:T(8,128)(2,1)S(1)}, bf16[256,384]{1,0:T(8,128)(2,1)S(1)}, u32[]{:S(2)}, u32[]{:S(2)}) collective-permute-start(bf16[256,384]{1,0:T(8,128)(2,1)S(1)} %get-tuple-element.25), channel_id=1, source_target_pairs={{0,4},{4,8},{8,12},{1,5},{5,9},{9,13},{2,6},{6,10},{10,14},{3,7},{... | collective-permute-start | bytes 589832 | tf_op jit(solution)/shard_map/ppermute | solution.py:12
  27.3 3.2 %collective-permute-done.1 = bf16[2,256,384]{2,1,0:T(8,128)(2,1)} collective-permute-done((bf16[2,256,384]{2,1,0:T(8,128)(2,1)}, bf16[2,256,384]{2,1,0:T(8,128)(2,1)}, u32[]{:S(2)}, u32[]{:S(2)}) %collective-permute-start.1) | collective-permute-done | bytes 393248 | tf_op jit(solution)/shard_map/ppermute | solution.py:12
  30.5 1.3 %collective-permute-start.7 = (bf16[256,384]{1,0:T(8,128)(2,1)S(1)}, bf16[256,384]{1,0:T(8,128)(2,1)S(1)}, u32[]{:S(2)}, u32[]{:S(2)}) collective-permute-start(bf16[256,384]{1,0:T(8,128)(2,1)S(1)} %get-tuple-element.26), channel_id=1, source_target_pairs={{4,0},{8,4},{12,8},{5,1},{9,5},{13,9},{6,2},{10,6},{14,10},{7,3},{... | collective-permute-start | bytes 589832 | tf_op jit(solution)/shard_map/ppermute | solution.py:12
  31.8 0.7 collective-permute-done
  32.5 1.1 %pad_maximum_fusion.4 = bf16[2,2,256,384]{3,2,1,0:T(8,128)(2,1)S(1)} fusion(bf16[1,2,256,384]{3,2,1,0:T(8,128)(2,1)} %bitcast.7, bf16[1,2,256,384]{3,2,1,0:T(8,128)(2,1)S(1)} %bitcast.171), kind=kLoop, calls=%fused_computation.59 | loop fusion | flops 393216 | bytes 1572864 | tf_op jit(solution)/shard_map/stack | solution.py:103
  33.6 1.2 %fusion.52 = (bf16[512,1,384]{2,0,1:T(8,128)(2,1)S(1)}, bf16[512,1,384]{2,0,1:T(8,128)(2,1)S(1)}, bf16[512,1,384]{2,0,1:T(8,128)(2,1)S(1)}, bf16[512,1,384]{2,0,1:T(8,128)(2,1)S(1)}) fusion(bf16[2,256,384]{2,1,0:T(8,128)(2,1)} %collective-permute-done.1, bf16[1,512,384]{2,1,0:T(8,128)(2,1)S(1)} %copy-done.1, bf16[1,512,384]{2,1,0:T(8,128)(2,1)S(1)} %bitcast.162, ...), kind=kLoop, calls=%fused_computation.79 | loop fusion | flops 4718592 | bytes 3145728 | tf_op jit(solution)/shard_map/stack | solution.py:21
  34.8 0.8 convolution_bitcast_fusion.3
  35.6 1.4 %fusion.90 = f32[384,384]{1,0:T(8,128)S(1)} fusion(bf16[512,384]{1,0:T(8,128)(2,1)} %collective-permute-done.4, bf16[512,384]{1,0:T(8,128)(2,1)S(1)} %broadcast_select_fusion), kind=kOutput, calls=%fused_computation.146 | convolution fusion | flops 150994944 | bytes 1376256 | tf_op jit(solution)/shard_map/dot_general | solution.py:133
  37.1 1.4 %fusion.57 = f32[384,384]{1,0:T(8,128)S(1)} fusion(bf16[512,384]{1,0:T(8,128)(2,1)} %collective-permute-done.4, bf16[256,384]{1,0:T(8,128)(2,1)S(1)} %get-tuple-element.26, bf16[256,384]{1,0:T(8,128)(2,1)S(1)} %collective-permute-done.8), kind=kOutput, calls=%fused_computation.92 | convolution fusion | flops 151781376 | bytes 1376256 | tf_op jit(solution)/shard_map/dot_general | solution.py:147
  38.5 0.4 collective-permute-done.7
  38.8 1.4 %fusion.53 = f32[384,384]{1,0:T(8,128)S(1)} fusion(bf16[512,384]{1,0:T(8,128)(2,1)} %collective-permute-done.4, bf16[256,384]{1,0:T(8,128)(2,1)S(1)} %collective-permute-done.7, bf16[256,384]{1,0:T(8,128)(2,1)S(1)} %get-tuple-element.25), kind=kOutput, calls=%fused_computation.88 | convolution fusion | flops 151781376 | bytes 1376256 | tf_op jit(solution)/shard_map/dot_general | solution.py:147
  40.4 1.4 %convolution_add_fusion = f32[384,384]{1,0:T(8,128)S(1)} fusion(f32[384,384]{1,0:T(8,128)S(1)} %fusion.90, bf16[512,384]{1,0:T(8,128)(2,1)S(1)} %get-tuple-element.29, pred[]{:T(512)S(6)} %eq.16, bf16[2176,384]{1,0:T(8,128)(2,1)} %collective-permute-done.3, bf16[1,512,384]{2,1,0:T(8,128)(2,1)S(1)} %copy-done.1), kind=kOutput, calls=%fused_computation.12 | convolution fusion | flops 151339008 | bytes 2359297 | tf_op jit(solution)/shard_map/dot_general | solution.py:133
  41.8 2.1 %collective-permute-start.13 = (f32[2,96,384]{2,1,0:T(8,128)S(1)}, f32[2,96,384]{2,1,0:T(8,128)S(1)}, u32[]{:S(2)}, u32[]{:S(2)}) collective-permute-start(f32[2,96,384]{2,1,0:T(8,128)S(1)} %select_bitcast_fusion.1), channel_id=1, source_target_pairs={{0,4},{4,0},{8,12},{12,8},{1,5},{5,1},{9,13},{13,9},{2,6},{6,2},{1... | collective-permute-start | bytes 884744 | tf_op jit(solution)/shard_map/ppermute | solution.py:58
  43.9 1.5 %convolution_add_fusion.1 = f32[384,384]{1,0:T(8,128)S(1)} fusion(f32[384,384]{1,0:T(8,128)S(1)} %fusion.57, bf16[1,512,384]{2,1,0:T(8,128)(2,1)S(1)} %copy-done.1, pred[]{:T(512)S(6)} %eq.16, bf16[2176,384]{1,0:T(8,128)(2,1)} %collective-permute-done.3, bf16[2,256,384]{2,1,0:T(8,128)(2,1)} %collective-permute-done.1, bf16[1,512,384]{2,1,0:T(8,128)(2,1)S(1)} %bitcast.164), kind=kOutput, calls=%fused_computation.13 | convolution fusion | flops 152518656 | bytes 3145729 | tf_op jit(solution)/shard_map/dot_general | solution.py:145
  45.4 1.4 %convolution_add_fusion.2 = f32[384,384]{1,0:T(8,128)S(1)} fusion(f32[384,384]{1,0:T(8,128)S(1)} %fusion.53, bf16[1,512,384]{2,1,0:T(8,128)(2,1)S(1)} %copy-done.1, pred[]{:T(512)S(6)} %eq.16, bf16[2176,384]{1,0:T(8,128)(2,1)} %collective-permute-done.3, bf16[2,256,384]{2,1,0:T(8,128)(2,1)S(1)} %collective-permute-done, bf16[1,512,384]{2,1,0:T(8,128)(2,1)S(1)} %bitcast.165), kind=kOutput, calls=%fused_computation.14 | convolution fusion | flops 152518656 | bytes 3145729 | tf_op jit(solution)/shard_map/dot_general | solution.py:145
  46.9 0.1 collective-permute-start.9
  47.0 1.2 %slice.183 = bf16[1024,384]{1,0:T(8,128)(2,1)S(1)} slice(bf16[2176,384]{1,0:T(8,128)(2,1)} %collective-permute-done.3), slice={[0:1024], [0:384]} | slice | bytes 1572864 | tf_op jit(solution)/shard_map/slice | solution.py:99
  48.3 0.2 fusion.50
  48.4 1.2 %slice_bitcast_fusion.3 = (bf16[512,1,384]{2,0,1:T(8,128)(2,1)S(1)}, bf16[512,1,384]{2,0,1:T(8,128)(2,1)S(1)}) fusion(bf16[2176,384]{1,0:T(8,128)(2,1)} %collective-permute-done.3), kind=kLoop, calls=%fused_computation.105 | loop fusion | bytes 1572864 | tf_op jit(solution)/shard_map/stack | solution.py:21
  49.6 2.1 %collective-permute-done.13 = f32[2,96,384]{2,1,0:T(8,128)S(1)} collective-permute-done((f32[2,96,384]{2,1,0:T(8,128)S(1)}, f32[2,96,384]{2,1,0:T(8,128)S(1)}, u32[]{:S(2)}, u32[]{:S(2)}) %collective-permute-start.13) | collective-permute-done | bytes 294944 | tf_op jit(solution)/shard_map/ppermute | solution.py:58
  51.8 3.3 %collective-permute-start.14 = (f32[96,384]{1,0:T(8,128)S(1)}, f32[96,384]{1,0:T(8,128)S(1)}, u32[]{:S(2)}, u32[]{:S(2)}) collective-permute-start(f32[96,384]{1,0:T(8,128)S(1)} %select_bitcast_fusion.7), channel_id=1, source_target_pairs={{0,8},{8,0},{4,12},{12,4},{1,9},{9,1},{5,13},{13,5},{2,10},{10,2},... | collective-permute-start | bytes 442376 | tf_op jit(solution)/shard_map/ppermute | solution.py:63
  55.2 0.8 convolution_bitcast_fusion
  56.0 10.6 %collective-permute-done.14 = f32[96,384]{1,0:T(8,128)S(1)} collective-permute-done((f32[96,384]{1,0:T(8,128)S(1)}, f32[96,384]{1,0:T(8,128)S(1)}, u32[]{:S(2)}, u32[]{:S(2)}) %collective-permute-start.14) | collective-permute-done | bytes 147488 | tf_op jit(solution)/shard_map/ppermute | solution.py:63
  66.6 3.4 %collective-permute-start.15 = (bf16[96,384]{1,0:T(8,128)(2,1)S(1)}, bf16[96,384]{1,0:T(8,128)(2,1)S(1)}, u32[]{:S(2)}, u32[]{:S(2)}) collective-permute-start(bf16[96,384]{1,0:T(8,128)(2,1)S(1)} %fusion.71), channel_id=1, source_target_pairs={{0,8},{8,0},{4,12},{12,4},{1,9},{9,1},{5,13},{13,5},{2,10},{10,2},... | collective-permute-start | bytes 221192 | tf_op jit(solution)/shard_map/ppermute | solution.py:64
  70.1 0.1 fusion.46
  70.3 1.3 %fusion.39 = bf16[512,384]{1,0:T(8,128)(2,1)S(1)} fusion(f32[512,384]{1,0:T(8,128)S(1)} %copy-done.3, f32[512,384]{1,0:T(8,128)S(1)} %convolution_bitcast_fusion, bf16[512,1,384]{2,0,1:T(8,128)(2,1)S(1)} %get-tuple-element.16, bf16[512,1,384]{2,0,1:T(8,128)(2,1)S(1)} %bitcast.159, bf16[512,1,384]{2,0,1:T(8,128)(2,1)S(1)} %get-tuple-element.7, ...), kind=kOutput, calls=%fused_computation.58 | convolution fusion | flops 458883072 | bytes 4423684 | tf_op jit(solution)/shard_map/tko,kio->ti/dot_general | solution.py:116
  71.7 1.3 %slice.186 = bf16[1152,384]{1,0:T(8,128)(2,1)S(1)} slice(bf16[2176,384]{1,0:T(8,128)(2,1)} %collective-permute-done.3), slice={[1024:2176], [0:384]} | slice | bytes 1769472 | tf_op jit(solution)/shard_map/slice | solution.py:100
  73.0 8.0 %collective-permute-start.16 = (bf16[2,96,384]{2,1,0:T(8,128)(2,1)S(1)}, bf16[2,96,384]{2,1,0:T(8,128)(2,1)S(1)}, u32[]{:S(2)}, u32[]{:S(2)}) collective-permute-start(bf16[2,96,384]{2,1,0:T(8,128)(2,1)S(1)} %maximum_select_fusion.1), channel_id=1, source_target_pairs={{0,4},{4,0},{8,12},{12,8},{1,5},{5,1},{9,13},{13,9},{2,6},{6,2},{1... | collective-permute-start | bytes 442376 | tf_op jit(solution)/shard_map/ppermute | solution.py:66
  81.0 6.5 %collective-permute-done.10 = f32[192,384]{1,0:T(8,128)S(1)} collective-permute-done((f32[192,384]{1,0:T(8,128)S(1)}, f32[192,384]{1,0:T(8,128)S(1)}, u32[]{:S(2)}, u32[]{:S(2)}) %collective-permute-start.10) | collective-permute-done | bytes 294944 | tf_op jit(solution)/shard_map/ppermute | solution.py:63
  87.6 1.6 %fusion.4 = bf16[1,512,384]{2,1,0:T(8,128)(2,1)} fusion(f32[512,384]{1,0:T(8,128)S(1)} %copy-done.3, f32[512,384]{1,0:T(8,128)S(1)} %convolution_bitcast_fusion.3, bf16[3,384,384]{2,1,0:T(8,128)(2,1)S(1)} %bitcast.179, bf16[512,1,384]{2,0,1:T(8,128)(2,1)S(1)} %get-tuple-element.12, bf16[512,1,384]{2,0,1:T(8,128)(2,1)S(1)} %get-tuple-element.4, ...), kind=kOutput, calls=%fused_computation.15 | convolution fusion | flops 454754304 | bytes 4030464 | tf_op jit(solution)/shard_map/tki,kio->to/dot_general | solution.py:110
  89.2 0.4 broadcast_in_dim.18
  89.6 1.2 %convert_element_type.54 = bf16[1,1024,384]{2,1,0:T(8,128)(2,1)} reshape(bf16[512,2,384]{2,1,0:T(2,128)(2,1)S(1)} %broadcast_in_dim.18) | data formatting | bytes 1572864 | tf_op jit(solution)/shard_map/convert_element_type | solution.py:125
  90.8 6.0 %collective-permute-done.11 = bf16[192,384]{1,0:T(8,128)(2,1)S(1)} collective-permute-done((bf16[192,384]{1,0:T(8,128)(2,1)S(1)}, bf16[192,384]{1,0:T(8,128)(2,1)S(1)}, u32[]{:S(2)}, u32[]{:S(2)}) %collective-permute-start.11) | collective-permute-done | bytes 147488 | tf_op jit(solution)/shard_map/ppermute | solution.py:64
  97.1 8.8 %collective-permute-done.12 = bf16[2,192,384]{2,1,0:T(8,128)(2,1)S(1)} collective-permute-done((bf16[2,192,384]{2,1,0:T(8,128)(2,1)S(1)}, bf16[2,192,384]{2,1,0:T(8,128)(2,1)S(1)}, u32[]{:S(2)}, u32[]{:S(2)}) %collective-permute-start.12) | collective-permute-done | bytes 294944 | tf_op jit(solution)/shard_map/ppermute | solution.py:66
  105.8 0.1 select_bitcast_fusion.3
  106.1 1.4 %pad_maximum_fusion = f32[3,384,384]{2,1,0:T(8,128)} fusion(f32[1,384,384]{2,1,0:T(8,128)S(1)} %bitcast.176, f32[1,384,384]{2,1,0:T(8,128)S(1)} %bitcast.174, f32[1,384,384]{2,1,0:T(8,128)S(1)} %bitcast.175), kind=kLoop, calls=%fused_computation.2 | loop fusion | flops 884736 | bytes 3538944 | tf_op jit(solution)/shard_map/stack | solution.py:151
  (40 shorter events, 1.2 us)
Async XLA Ops:
  0.6 12.7 %copy-start = (bf16[3,384,768]{2,1,0:T(8,128)(2,1)S(1)}, bf16[3,384,768]{2,1,0:T(8,128)(2,1)}, u32[]{:S(2)}) copy-start(bf16[3,384,768]{2,1,0:T(8,128)(2,1)} %param.4) | copy-start | bytes 5308420
  0.6 17.4 %collective-permute-start.5 = (bf16[512,384]{1,0:T(8,128)(2,1)}, bf16[512,384]{1,0:T(8,128)(2,1)}, u32[]{:S(2)}, u32[]{:S(2)}) collective-permute-start(bf16[512,384]{1,0:T(8,128)(2,1)} %bitcast.157), channel_id=1, source_target_pairs={{2,0},{1,3},{6,4},{5,7},{10,8},{9,11},{14,12},{13,15},{18,16},{17,... | collective-permute-start | bytes 1179656 | tf_op jit(solution)/shard_map/ppermute | solution.py:88
  2.1 20.6 %collective-permute-start.6 = (bf16[512,384]{1,0:T(8,128)(2,1)}, bf16[512,384]{1,0:T(8,128)(2,1)}, u32[]{:S(2)}, u32[]{:S(2)}) collective-permute-start(bf16[512,384]{1,0:T(8,128)(2,1)} %bitcast.158), channel_id=1, source_target_pairs={{2,1},{1,2},{6,5},{5,6},{10,9},{9,10},{14,13},{13,14},{18,17},{17,... | collective-permute-start | bytes 1179656 | tf_op jit(solution)/shard_map/ppermute | solution.py:89
  3.5 8.8 %copy-start.1 = (bf16[1,512,384]{2,1,0:T(8,128)(2,1)S(1)}, bf16[1,512,384]{2,1,0:T(8,128)(2,1)}, u32[]{:S(2)}) copy-start(bf16[1,512,384]{2,1,0:T(8,128)(2,1)} %param.5) | copy-start | bytes 1179652
  6.3 29.3 %collective-permute-start.4 = (bf16[512,384]{1,0:T(8,128)(2,1)S(1)}, bf16[512,384]{1,0:T(8,128)(2,1)}, u32[]{:S(2)}, u32[]{:S(2)}) collective-permute-start(bf16[512,384]{1,0:T(8,128)(2,1)S(1)} %get-tuple-element.29), channel_id=1, source_target_pairs={{0,2},{2,0},{1,3},{3,1},{4,6},{6,4},{5,7},{7,5},{8,10},{10,8},{9,1... | collective-permute-start | bytes 1179656 | tf_op jit(solution)/shard_map/ppermute | solution.py:91
  13.3 1.1 %copy-start.2 = (bf16[2,512,384]{2,1,0:T(8,128)(2,1)S(1)}, bf16[2,512,384]{2,1,0:T(8,128)(2,1)}, u32[]{:S(2)}) copy-start(bf16[2,512,384]{2,1,0:T(8,128)(2,1)} %pad_maximum_fusion.3) | copy-start | bytes 2359300
  15.8 24.6 %collective-permute-start.3 = (bf16[2176,384]{1,0:T(8,128)(2,1)}, bf16[2176,384]{1,0:T(8,128)(2,1)}, u32[]{:S(2)}, u32[]{:S(2)}) collective-permute-start(bf16[2176,384]{1,0:T(8,128)(2,1)} %pad_maximum_fusion.1), channel_id=1, source_target_pairs={{0,1},{1,0},{2,3},{3,2},{4,5},{5,4},{6,7},{7,6},{8,9},{9,8},{10,11... | collective-permute-start | bytes 5013512 | tf_op jit(solution)/shard_map/ppermute | solution.py:96
  16.8 13.7 %collective-permute-start.1 = (bf16[2,256,384]{2,1,0:T(8,128)(2,1)}, bf16[2,256,384]{2,1,0:T(8,128)(2,1)}, u32[]{:S(2)}, u32[]{:S(2)}) collective-permute-start(bf16[2,256,384]{2,1,0:T(8,128)(2,1)} %get-tuple-element.22), channel_id=1, source_target_pairs={{4,0},{8,4},{12,8},{5,1},{9,5},{13,9},{6,2},{10,6},{14,10},{7,3},{... | collective-permute-start | bytes 1179656 | tf_op jit(solution)/shard_map/ppermute | solution.py:12
  18.1 14.4 %collective-permute-start = (bf16[2,256,384]{2,1,0:T(8,128)(2,1)}, bf16[2,256,384]{2,1,0:T(8,128)(2,1)S(1)}, u32[]{:S(2)}, u32[]{:S(2)}) collective-permute-start(bf16[2,256,384]{2,1,0:T(8,128)(2,1)} %get-tuple-element.21), channel_id=1, source_target_pairs={{0,4},{4,8},{8,12},{1,5},{5,9},{9,13},{2,6},{6,10},{10,14},{3,7},{... | collective-permute-start | bytes 1179656 | tf_op jit(solution)/shard_map/ppermute | solution.py:12
  23.8 13.2 %collective-permute-start.8 = (bf16[256,384]{1,0:T(8,128)(2,1)S(1)}, bf16[256,384]{1,0:T(8,128)(2,1)S(1)}, u32[]{:S(2)}, u32[]{:S(2)}) collective-permute-start(bf16[256,384]{1,0:T(8,128)(2,1)S(1)} %get-tuple-element.25), channel_id=1, source_target_pairs={{0,4},{4,8},{8,12},{1,5},{5,9},{9,13},{2,6},{6,10},{10,14},{3,7},{... | collective-permute-start | bytes 589832 | tf_op jit(solution)/shard_map/ppermute | solution.py:12
  30.5 8.3 %collective-permute-start.7 = (bf16[256,384]{1,0:T(8,128)(2,1)S(1)}, bf16[256,384]{1,0:T(8,128)(2,1)S(1)}, u32[]{:S(2)}, u32[]{:S(2)}) collective-permute-start(bf16[256,384]{1,0:T(8,128)(2,1)S(1)} %get-tuple-element.26), channel_id=1, source_target_pairs={{4,0},{8,4},{12,8},{5,1},{9,5},{13,9},{6,2},{10,6},{14,10},{7,3},{... | collective-permute-start | bytes 589832 | tf_op jit(solution)/shard_map/ppermute | solution.py:12
  33.5 6.7 %collective-permute-start.2 = (bf16[2,2,256,384]{3,2,1,0:T(8,128)(2,1)S(1)}, bf16[2,2,256,384]{3,2,1,0:T(8,128)(2,1)S(1)}, u32[]{:S(2)}, u32[]{:S(2)}) collective-permute-start(bf16[2,2,256,384]{3,2,1,0:T(8,128)(2,1)S(1)} %pad_maximum_fusion.4), channel_id=1, source_target_pairs={{0,1},{1,0},{2,3},{3,2},{4,5},{5,4},{6,7},{7,6},{8,9},{9,8},{10,11... | collective-permute-start | bytes 2359304 | tf_op jit(solution)/shard_map/ppermute | solution.py:103
  41.8 9.9 %collective-permute-start.13 = (f32[2,96,384]{2,1,0:T(8,128)S(1)}, f32[2,96,384]{2,1,0:T(8,128)S(1)}, u32[]{:S(2)}, u32[]{:S(2)}) collective-permute-start(f32[2,96,384]{2,1,0:T(8,128)S(1)} %select_bitcast_fusion.1), channel_id=1, source_target_pairs={{0,4},{4,0},{8,12},{12,8},{1,5},{5,1},{9,13},{13,9},{2,6},{6,2},{1... | collective-permute-start | bytes 884744 | tf_op jit(solution)/shard_map/ppermute | solution.py:58
  46.9 23.1 %collective-permute-start.9 = (f32[2,192,384]{2,1,0:T(8,128)S(1)}, f32[2,192,384]{2,1,0:T(8,128)S(1)}, u32[]{:S(2)}, u32[]{:S(2)}) collective-permute-start(f32[2,192,384]{2,1,0:T(8,128)S(1)} %select_bitcast_fusion), channel_id=1, source_target_pairs={{0,4},{4,0},{8,12},{12,8},{1,5},{5,1},{9,13},{13,9},{2,6},{6,2},{1... | collective-permute-start | bytes 1769480 | tf_op jit(solution)/shard_map/ppermute | solution.py:58
  51.8 14.8 %collective-permute-start.14 = (f32[96,384]{1,0:T(8,128)S(1)}, f32[96,384]{1,0:T(8,128)S(1)}, u32[]{:S(2)}, u32[]{:S(2)}) collective-permute-start(f32[96,384]{1,0:T(8,128)S(1)} %select_bitcast_fusion.7), channel_id=1, source_target_pairs={{0,8},{8,0},{4,12},{12,4},{1,9},{9,1},{5,13},{13,5},{2,10},{10,2},... | collective-permute-start | bytes 442376 | tf_op jit(solution)/shard_map/ppermute | solution.py:63
  66.6 3.7 %copy-start.3 = (f32[512,384]{1,0:T(8,128)S(1)}, f32[512,384]{1,0:T(8,128)}, u32[]{:S(2)}) copy-start(f32[512,384]{1,0:T(8,128)} %get-tuple-element.30) | copy-start | bytes 2359300
  66.6 6.3 %collective-permute-start.15 = (bf16[96,384]{1,0:T(8,128)(2,1)S(1)}, bf16[96,384]{1,0:T(8,128)(2,1)S(1)}, u32[]{:S(2)}, u32[]{:S(2)}) collective-permute-start(bf16[96,384]{1,0:T(8,128)(2,1)S(1)} %fusion.71), channel_id=1, source_target_pairs={{0,8},{8,0},{4,12},{12,4},{1,9},{9,1},{5,13},{13,5},{2,10},{10,2},... | collective-permute-start | bytes 221192 | tf_op jit(solution)/shard_map/ppermute | solution.py:64
  70.2 17.2 %collective-permute-start.10 = (f32[192,384]{1,0:T(8,128)S(1)}, f32[192,384]{1,0:T(8,128)S(1)}, u32[]{:S(2)}, u32[]{:S(2)}) collective-permute-start(f32[192,384]{1,0:T(8,128)S(1)} %select_bitcast_fusion.4), channel_id=1, source_target_pairs={{0,8},{8,0},{4,12},{12,4},{1,9},{9,1},{5,13},{13,5},{2,10},{10,2},... | collective-permute-start | bytes 884744 | tf_op jit(solution)/shard_map/ppermute | solution.py:63
  73.0 23.9 %collective-permute-start.16 = (bf16[2,96,384]{2,1,0:T(8,128)(2,1)S(1)}, bf16[2,96,384]{2,1,0:T(8,128)(2,1)S(1)}, u32[]{:S(2)}, u32[]{:S(2)}) collective-permute-start(bf16[2,96,384]{2,1,0:T(8,128)(2,1)S(1)} %maximum_select_fusion.1), channel_id=1, source_target_pairs={{0,4},{4,0},{8,12},{12,8},{1,5},{5,1},{9,13},{13,9},{2,6},{6,2},{1... | collective-permute-start | bytes 442376 | tf_op jit(solution)/shard_map/ppermute | solution.py:66
  87.5 9.2 %collective-permute-start.11 = (bf16[192,384]{1,0:T(8,128)(2,1)S(1)}, bf16[192,384]{1,0:T(8,128)(2,1)S(1)}, u32[]{:S(2)}, u32[]{:S(2)}) collective-permute-start(bf16[192,384]{1,0:T(8,128)(2,1)S(1)} %fusion.70), channel_id=1, source_target_pairs={{0,8},{8,0},{4,12},{12,4},{1,9},{9,1},{5,13},{13,5},{2,10},{10,2},... | collective-permute-start | bytes 442376 | tf_op jit(solution)/shard_map/ppermute | solution.py:64
  96.8 9.0 %collective-permute-start.12 = (bf16[2,192,384]{2,1,0:T(8,128)(2,1)S(1)}, bf16[2,192,384]{2,1,0:T(8,128)(2,1)S(1)}, u32[]{:S(2)}, u32[]{:S(2)}) collective-permute-start(bf16[2,192,384]{2,1,0:T(8,128)(2,1)S(1)} %maximum_select_fusion), channel_id=1, source_target_pairs={{0,4},{4,0},{8,12},{12,8},{1,5},{5,1},{9,13},{13,9},{2,6},{6,2},{1... | collective-permute-start | bytes 884744 | tf_op jit(solution)/shard_map/ppermute | solution.py:66

commit v16 on v11

--- a/solution.py
+++ b/solution.py
@@ -143,9 +143,7 @@
                 own_taps[:, k].T, cot_mine, preferred_element_type=jnp.float32
             ) + jnp.dot(far_mid.T, far_shifted[k], preferred_element_type=jnp.float32)
         if seq_count == 4:
-            middle = line_total(grads[1])
-            sides = line_total(jnp.concatenate([grads[0], grads[2]], 0))
-            weight_grad = jnp.stack([sides[: middle.shape[0]], middle, sides[middle.shape[0] :]])
+            weight_grad = jnp.stack([line_total(grads[k]) for k in range(3)])
         else:
             weight_grad = lax.psum(jnp.stack([grads[0], grads[1], grads[2]]), "seq")
     else:

time: 103 us -> 105 us (1.019)
  waiting for transfers between devices: 42.3 us -> 29.1 us
  starting transfers between devices: 31.2 us -> 38.2 us
  other arithmetic: 9.42 us -> 14.9 us
  local copies, waits for them, and re-layouts: 6.93 us -> 11 us
  matrix products: 11.5 us -> 9.66 us
    ppermute x2 -> x3, waiting for transfers between devices: 0.01 us -> 15.9 us  [line_total(): total = (keep + lax.ppermute(give, 'seq', across)).astype(jnp.bfloat16)]
    ppermute x2 -> x3, waiting for transfers between devices: 16.6 us -> 3.03 us  [line_total(): other = lax.ppermute(total, 'seq', across)]
    ppermute x2 -> x3, waiting for transfers between devices: 10.9 us -> 0.01 us  [line_total(): lax.ppermute(jnp.where(odd, even_set, odd_set), 'seq', pairs)]
    ppermute x2 -> x3, starting transfers between devices: 5.92 us -> 0.21 us  [line_total(): other = lax.ppermute(total, 'seq', across)]
    ppermute x2 -> x3, starting transfers between devices: 0.33 us -> 4.84 us  [line_total(): far_set = lax.ppermute(own_set, 'seq', pairs)]
    ppermute x2 -> x3, starting transfers between devices: 1.43 us -> 5.71 us  [line_total(): total = (keep + lax.ppermute(give, 'seq', across)).astype(jnp.bfloat16)]
    ppermute x4, waiting for transfers between devices: 8.39 us -> 4.47 us  [shift_from(): return lax.ppermute(block, axis, route)]
    add x2 -> x3, other arithmetic: 0.14 us -> 3.07 us  [line_total(): jnp.where(odd, odd_set, even_set)]
  transfers between devices with their start and end apart: 17 -> 21, of which waited for: 7 -> 11; matrix products, arithmetic and copies ran while one was open for 22% -> 28% of each run, Pallas kernels for 0% -> 0%
where the time goes in v16:
time: 105 us; the launch traced here: 104 us
  starting transfers between devices  38.2 us (36%)
  waiting for transfers between devices  29.1 us (28%)
  other arithmetic  14.9 us (14%)
  local copies, waits for them, and re-layouts  11 us (10%)
  matrix products  9.66 us (9%)
  between operations  1.07 us (1%)
    ppermute x3, waiting for transfers between devices, line_total(): total = (keep + lax.ppermute(give, 'seq', across)).astype(jnp.bfloat16)  15.9 us
    ppermute x4, starting transfers between devices, shift_from(): return lax.ppermute(block, axis, route)  12.1 us
    ppermute x3, starting transfers between devices, line_total(): total = (keep + lax.ppermute(give, 'seq', across)).astype(jnp.bfloat16)  5.71 us
    ppermute x3, waiting for transfers between devices, line_total(): far_set = lax.ppermute(own_set, 'seq', pairs)  5.68 us
    ppermute x3, starting transfers between devices, line_total(): far_set = lax.ppermute(own_set, 'seq', pairs)  4.84 us
    ppermute x3, starting transfers between devices, line_total(): lax.ppermute(jnp.where(odd, even_set, odd_set), 'seq', pairs)  4.5 us
    ppermute x4, waiting for transfers between devices, shift_from(): return lax.ppermute(block, axis, route)  4.47 us
    ppermute x1, starting transfers between devices, shards(): lax.ppermute(jnp.concatenate([both.reshape(-1, width), w_other.reshape(-1...  3.71 us
  transfers between devices with their start and end apart: 21, of which 11 were waited for; matrix products, arithmetic and copies ran while one was open for 28% of the time, Pallas kernels for 0%

profile of v16, /device:TPU:0, one launch (start us, length us, event | category | flops | bytes accessed | tf_op | source)
XLA Modules:
  0.0 104.0 jit_solution(13272199607441002871)
XLA Ops:
  0.6 1.4 %collective-permute-start.5 = (bf16[512,384]{1,0:T(8,128)(2,1)}, bf16[512,384]{1,0:T(8,128)(2,1)}, u32[]{:S(2)}, u32[]{:S(2)}) collective-permute-start(bf16[512,384]{1,0:T(8,128)(2,1)} %bitcast.182), channel_id=1, source_target_pairs={{2,0},{1,3},{6,4},{5,7},{10,8},{9,11},{14,12},{13,15},{18,16},{17,... | collective-permute-start | bytes 1179656 | tf_op jit(solution)/shard_map/ppermute | solution.py:88
  2.1 1.4 %collective-permute-start.6 = (bf16[512,384]{1,0:T(8,128)(2,1)}, bf16[512,384]{1,0:T(8,128)(2,1)}, u32[]{:S(2)}, u32[]{:S(2)}) collective-permute-start(bf16[512,384]{1,0:T(8,128)(2,1)} %bitcast.183), channel_id=1, source_target_pairs={{2,1},{1,2},{6,5},{5,6},{10,9},{9,10},{14,13},{13,14},{18,17},{17,... | collective-permute-start | bytes 1179656 | tf_op jit(solution)/shard_map/ppermute | solution.py:89
  3.5 2.8 %multiply_convert_fusion = (bf16[512,384]{1,0:T(8,128)(2,1)S(1)}, f32[512,384]{1,0:T(8,128)}) fusion(bf16[1,1024,384]{2,1,0:T(8,128)(2,1)} %param.3, s32[1024]{0:T(1024)S(1)} %get-tuple-element.32, s32[1024]{0:T(1024)S(1)} %get-tuple-element.33, pred[1024]{0:T(1024)(128)(4,1)S(1)} %fusion.71), kind=kOutput, calls=%fused_computation.60 | convolution fusion | flops 406519808 | bytes 1975296 | tf_op jit(solution)/shard_map/dot_general | solution.py:83
  6.4 1.0 fusion.45
  7.3 5.0 %collective-permute-start = (bf16[2,256,384]{2,1,0:T(8,128)(2,1)}, bf16[2,256,384]{2,1,0:T(8,128)(2,1)S(1)}, u32[]{:S(2)}, u32[]{:S(2)}) collective-permute-start(bf16[2,256,384]{2,1,0:T(8,128)(2,1)} %get-tuple-element.19), channel_id=1, source_target_pairs={{0,4},{4,8},{8,12},{1,5},{5,9},{9,13},{2,6},{6,10},{10,14},{3,7},{... | collective-permute-start | bytes 1179656 | tf_op jit(solution)/shard_map/ppermute | solution.py:12
  12.3 1.3 %collective-permute-start.1 = (bf16[2,256,384]{2,1,0:T(8,128)(2,1)}, bf16[2,256,384]{2,1,0:T(8,128)(2,1)S(1)}, u32[]{:S(2)}, u32[]{:S(2)}) collective-permute-start(bf16[2,256,384]{2,1,0:T(8,128)(2,1)} %get-tuple-element.20), channel_id=1, source_target_pairs={{4,0},{8,4},{12,8},{5,1},{9,5},{13,9},{6,2},{10,6},{14,10},{7,3},{... | collective-permute-start | bytes 1179656 | tf_op jit(solution)/shard_map/ppermute | solution.py:12
  13.6 1.0 pad_maximum_fusion.1
  14.7 1.3 %copy-done.8 = bf16[2,512,384]{2,1,0:T(8,128)(2,1)S(1)} copy-done((bf16[2,512,384]{2,1,0:T(8,128)(2,1)S(1)}, bf16[2,512,384]{2,1,0:T(8,128)(2,1)}, u32[]{:S(2)}) %copy-start.8) | copy-done | bytes 786456
  16.0 1.3 %pad_maximum_fusion = bf16[2176,384]{1,0:T(8,128)(2,1)} fusion(bf16[1152,384]{1,0:T(8,128)(2,1)S(1)} %bitcast.191, bf16[1024,384]{1,0:T(8,128)(2,1)S(1)} %bitcast.194), kind=kLoop, calls=%fused_computation.2 | loop fusion | flops 3342336 | bytes 3342336 | tf_op jit(solution)/shard_map/concatenate | solution.py:97
  17.4 3.7 %collective-permute-start.3 = (bf16[2176,384]{1,0:T(8,128)(2,1)}, bf16[2176,384]{1,0:T(8,128)(2,1)}, u32[]{:S(2)}, u32[]{:S(2)}) collective-permute-start(bf16[2176,384]{1,0:T(8,128)(2,1)} %pad_maximum_fusion), channel_id=1, source_target_pairs={{0,1},{1,0},{2,3},{3,2},{4,5},{5,4},{6,7},{7,6},{8,9},{9,8},{10,11... | collective-permute-start | bytes 5013512 | tf_op jit(solution)/shard_map/ppermute | solution.py:96
  21.1 1.4 %collective-permute-start.4 = (bf16[512,384]{1,0:T(8,128)(2,1)S(1)}, bf16[512,384]{1,0:T(8,128)(2,1)S(1)}, u32[]{:S(2)}, u32[]{:S(2)}) collective-permute-start(bf16[512,384]{1,0:T(8,128)(2,1)S(1)} %get-tuple-element.30), channel_id=1, source_target_pairs={{0,2},{2,0},{1,3},{3,1},{4,6},{6,4},{5,7},{7,5},{8,10},{10,8},{9,1... | collective-permute-start | bytes 1179656 | tf_op jit(solution)/shard_map/ppermute | solution.py:91
  22.4 1.2 %collective-permute-done.1 = bf16[2,256,384]{2,1,0:T(8,128)(2,1)S(1)} collective-permute-done((bf16[2,256,384]{2,1,0:T(8,128)(2,1)}, bf16[2,256,384]{2,1,0:T(8,128)(2,1)S(1)}, u32[]{:S(2)}, u32[]{:S(2)}) %collective-permute-start.1) | collective-permute-done | bytes 393248 | tf_op jit(solution)/shard_map/ppermute | solution.py:12
  23.7 2.9 %collective-permute-start.2 = (bf16[2,2,256,384]{3,2,1,0:T(8,128)(2,1)S(1)}, bf16[2,2,256,384]{3,2,1,0:T(8,128)(2,1)S(1)}, u32[]{:S(2)}, u32[]{:S(2)}) collective-permute-start(bf16[2,2,256,384]{3,2,1,0:T(8,128)(2,1)S(1)} %pad_maximum_fusion.2), channel_id=1, source_target_pairs={{0,1},{1,0},{2,3},{3,2},{4,5},{5,4},{6,7},{7,6},{8,9},{9,8},{10,11... | collective-permute-start | bytes 2359304 | tf_op jit(solution)/shard_map/ppermute | solution.py:103
  26.7 1.0 %broadcast_select_fusion = bf16[512,384]{1,0:T(8,128)(2,1)S(1)} fusion(bf16[512,384]{1,0:T(8,128)(2,1)} %collective-permute-done.5, bf16[512,384]{1,0:T(8,128)(2,1)} %collective-permute-done.6, pred[]{:T(512)S(6)} %eq.18), kind=kLoop, calls=%fused_computation.96 | loop fusion | flops 196608 | bytes 1179649 | tf_op jit(solution)/shard_map/jit(_where)/select_n | solution.py:90
  27.8 1.3 %collective-permute-start.7 = (bf16[256,384]{1,0:T(8,128)(2,1)S(1)}, bf16[256,384]{1,0:T(8,128)(2,1)S(1)}, u32[]{:S(2)}, u32[]{:S(2)}) collective-permute-start(bf16[256,384]{1,0:T(8,128)(2,1)S(1)} %get-tuple-element.23), channel_id=1, source_target_pairs={{4,0},{8,4},{12,8},{5,1},{9,5},{13,9},{6,2},{10,6},{14,10},{7,3},{... | collective-permute-start | bytes 589832 | tf_op jit(solution)/shard_map/ppermute | solution.py:12
  29.1 4.6 %collective-permute-start.16 = (bf16[256,384]{1,0:T(8,128)(2,1)S(1)}, bf16[256,384]{1,0:T(8,128)(2,1)S(1)}, u32[]{:S(2)}, u32[]{:S(2)}) collective-permute-start(bf16[256,384]{1,0:T(8,128)(2,1)S(1)} %get-tuple-element.22), channel_id=1, source_target_pairs={{0,4},{4,8},{8,12},{1,5},{5,9},{9,13},{2,6},{6,10},{10,14},{3,7},{... | collective-permute-start | bytes 589832 | tf_op jit(solution)/shard_map/ppermute | solution.py:12
  34.0 2.5 %collective-permute-done.7 = bf16[256,384]{1,0:T(8,128)(2,1)S(1)} collective-permute-done((bf16[256,384]{1,0:T(8,128)(2,1)S(1)}, bf16[256,384]{1,0:T(8,128)(2,1)S(1)}, u32[]{:S(2)}, u32[]{:S(2)}) %collective-permute-start.7) | collective-permute-done | bytes 196640 | tf_op jit(solution)/shard_map/ppermute | solution.py:12
  36.9 0.8 collective-permute-done.16
  38.2 2.1 %fusion.50 = (bf16[512,1,384]{2,0,1:T(8,128)(2,1)S(1)}, bf16[512,1,384]{2,0,1:T(8,128)(2,1)}, bf16[512,1,384]{2,0,1:T(8,128)(2,1)}, bf16[512,1,384]{2,0,1:T(8,128)(2,1)S(1)}, bf16[1,512,384]{2,1,0:T(8,128)(2,1)S(1)}) fusion(bf16[2,256,384]{2,1,0:T(8,128)(2,1)S(1)} %collective-permute-done.1, bf16[1,512,384]{2,1,0:T(8,128)(2,1)S(1)} %copy-done.1, ...), kind=kLoop, calls=%fused_computation.73 | loop fusion | flops 4915200 | bytes 3932161 | tf_op jit(solution)/shard_map/stack | solution.py:21
  40.7 0.8 select_bitcast_fusion.2
  41.7 2.5 %collective-permute-start.8 = (f32[2,96,384]{2,1,0:T(8,128)}, f32[2,96,384]{2,1,0:T(8,128)}, u32[]{:S(2)}, u32[]{:S(2)}) collective-permute-start(f32[2,96,384]{2,1,0:T(8,128)} %select_bitcast_fusion.2), channel_id=1, source_target_pairs={{0,4},{4,0},{8,12},{12,8},{1,5},{5,1},{9,13},{13,9},{2,6},{6,2},{1... | collective-permute-start | bytes 884744 | tf_op jit(solution)/shard_map/ppermute | solution.py:58
  44.6 0.8 select_bitcast_fusion.1
  46.6 2.0 %collective-permute-start.17 = (f32[2,96,384]{2,1,0:T(8,128)}, f32[2,96,384]{2,1,0:T(8,128)}, u32[]{:S(2)}, u32[]{:S(2)}) collective-permute-start(f32[2,96,384]{2,1,0:T(8,128)} %select_bitcast_fusion), channel_id=1, source_target_pairs={{0,4},{4,0},{8,12},{12,8},{1,5},{5,1},{9,13},{13,9},{2,6},{6,2},{1... | collective-permute-start | bytes 884744 | tf_op jit(solution)/shard_map/ppermute | solution.py:58
  48.6 1.2 %slice.192 = bf16[1024,384]{1,0:T(8,128)(2,1)S(1)} slice(bf16[2176,384]{1,0:T(8,128)(2,1)} %collective-permute-done.3), slice={[0:1024], [0:384]} | slice | bytes 1572864 | tf_op jit(solution)/shard_map/slice | solution.py:99
  49.8 1.0 %fusion.48 = (bf16[512,1,384]{2,0,1:T(8,128)(2,1)S(1)}, bf16[512,1,384]{2,0,1:T(8,128)(2,1)}, bf16[512,1,384]{2,0,1:T(8,128)(2,1)}, bf16[512,1,384]{2,0,1:T(8,128)(2,1)S(1)}) fusion(bf16[2,256,384]{2,1,0:T(8,128)(2,1)S(1)} %get-tuple-element.18, bf16[2,512,384]{2,1,0:T(8,128)(2,1)S(1)} %bitcast.195, bf16[2,256,384]{2,1,0:T(8,128)(2,1)S(1)} %get-tuple-element.17), kind=kLoop, calls=%fused_computation.68 | loop fusion | flops 3145728 | bytes 3145728 | tf_op jit(solution)/shard_map/stack | solution.py:21
  50.9 2.0 %slice_bitcast_fusion.3 = (bf16[512,1,384]{2,0,1:T(8,128)(2,1)S(1)}, bf16[512,1,384]{2,0,1:T(8,128)(2,1)}) fusion(bf16[2176,384]{1,0:T(8,128)(2,1)} %collective-permute-done.3), kind=kLoop, calls=%fused_computation.97 | loop fusion | bytes 1572864 | tf_op jit(solution)/shard_map/stack | solution.py:21
  52.8 0.8 convolution_bitcast_fusion
  54.0 1.3 %fusion.39 = bf16[512,384]{1,0:T(8,128)(2,1)S(1)} fusion(f32[512,384]{1,0:T(8,128)S(1)} %copy-done.14, f32[512,384]{1,0:T(8,128)S(1)} %convolution_bitcast_fusion, bf16[512,1,384]{2,0,1:T(8,128)(2,1)S(1)} %get-tuple-element.14, bf16[512,1,384]{2,0,1:T(8,128)(2,1)S(1)} %bitcast.184, bf16[512,1,384]{2,0,1:T(8,128)(2,1)S(1)} %get-tuple-element.5, ...), kind=kOutput, calls=%fused_computation.57 | convolution fusion | flops 458883072 | bytes 4423684 | tf_op jit(solution)/shard_map/tko,kio->ti/dot_general | solution.py:116
  55.3 1.3 %broadcast_in_dim.18 = bf16[512,2,384]{2,1,0:T(2,128)(2,1)} broadcast(bf16[512,384]{1,0:T(8,128)(2,1)S(1)} %fusion.39), dimensions={0,2} | broadcast | bytes 1179648 | tf_op jit(solution)/shard_map/broadcast_in_dim | solution.py:125
  56.6 3.0 %convert_element_type.73 = bf16[1,1024,384]{2,1,0:T(8,128)(2,1)} reshape(bf16[512,2,384]{2,1,0:T(2,128)(2,1)} %broadcast_in_dim.18) | data formatting | bytes 1572864 | tf_op jit(solution)/shard_map/convert_element_type | solution.py:125
  59.6 0.8 convolution_bitcast_fusion.3
  60.4 1.3 %slice.195 = bf16[1152,384]{1,0:T(8,128)(2,1)S(1)} slice(bf16[2176,384]{1,0:T(8,128)(2,1)} %collective-permute-done.3), slice={[1024:2176], [0:384]} | slice | bytes 1769472 | tf_op jit(solution)/shard_map/slice | solution.py:100
  61.9 1.6 %fusion.4 = bf16[1,512,384]{2,1,0:T(8,128)(2,1)} fusion(f32[512,384]{1,0:T(8,128)S(1)} %copy-done.15, f32[512,384]{1,0:T(8,128)S(1)} %convolution_bitcast_fusion.3, bf16[3,384,384]{2,1,0:T(8,128)(2,1)S(1)} %bitcast.199, bf16[512,1,384]{2,0,1:T(8,128)(2,1)S(1)} %copy-done.11, bf16[512,1,384]{2,0,1:T(8,128)(2,1)S(1)} %copy-done.13, ...), kind=kOutput, calls=%fused_computation.14 | convolution fusion | flops 454754304 | bytes 4030464 | tf_op jit(solution)/shard_map/tki,kio->to/dot_general | solution.py:110
  63.5 1.1 %fusion.65 = f32[2,96,384]{2,1,0:T(8,128)S(1)} fusion(f32[2,96,384]{2,1,0:T(8,128)} %collective-permute-done.8, f32[2,2,96,384]{3,2,1,0:T(8,128)S(1)} %bitcast.190, pred[]{:T(512)S(6)} %eq.17), kind=kLoop, calls=%fused_computation.107 | loop fusion | flops 147456 | bytes 1179649 | tf_op jit(solution)/shard_map/add | solution.py:58
  64.6 2.7 %collective-permute-start.9 = (f32[96,384]{1,0:T(8,128)S(1)}, f32[96,384]{1,0:T(8,128)S(1)}, u32[]{:S(2)}, u32[]{:S(2)}) collective-permute-start(f32[96,384]{1,0:T(8,128)S(1)} %select_bitcast_fusion.11), channel_id=1, source_target_pairs={{0,8},{8,0},{4,12},{12,4},{1,9},{9,1},{5,13},{13,5},{2,10},{10,2},... | collective-permute-start | bytes 442376 | tf_op jit(solution)/shard_map/ppermute | solution.py:63
  67.2 1.0 bitcast_add_fusion.1
  68.7 1.0 bitcast_add_fusion
  69.7 2.7 %collective-permute-start.18 = (f32[96,384]{1,0:T(8,128)S(1)}, f32[96,384]{1,0:T(8,128)S(1)}, u32[]{:S(2)}, u32[]{:S(2)}) collective-permute-start(f32[96,384]{1,0:T(8,128)S(1)} %select_bitcast_fusion.5), channel_id=1, source_target_pairs={{0,8},{8,0},{4,12},{12,4},{1,9},{9,1},{5,13},{13,5},{2,10},{10,2},... | collective-permute-start | bytes 442376 | tf_op jit(solution)/shard_map/ppermute | solution.py:63
  72.4 7.4 %collective-permute-done.9 = f32[96,384]{1,0:T(8,128)S(1)} collective-permute-done((f32[96,384]{1,0:T(8,128)S(1)}, f32[96,384]{1,0:T(8,128)S(1)}, u32[]{:S(2)}, u32[]{:S(2)}) %collective-permute-start.9) | collective-permute-done | bytes 147488 | tf_op jit(solution)/shard_map/ppermute | solution.py:63
  79.9 3.8 %collective-permute-done.13 = f32[96,384]{1,0:T(8,128)S(1)} collective-permute-done((f32[96,384]{1,0:T(8,128)S(1)}, f32[96,384]{1,0:T(8,128)S(1)}, u32[]{:S(2)}, u32[]{:S(2)}) %collective-permute-start.13) | collective-permute-done | bytes 147488 | tf_op jit(solution)/shard_map/ppermute | solution.py:63
  83.9 4.6 %collective-permute-done.18 = f32[96,384]{1,0:T(8,128)S(1)} collective-permute-done((f32[96,384]{1,0:T(8,128)S(1)}, f32[96,384]{1,0:T(8,128)S(1)}, u32[]{:S(2)}, u32[]{:S(2)}) %collective-permute-start.18) | collective-permute-done | bytes 147488 | tf_op jit(solution)/shard_map/ppermute | solution.py:63
  88.6 2.9 %collective-permute-done.10 = bf16[96,384]{1,0:T(8,128)(2,1)S(1)} collective-permute-done((bf16[96,384]{1,0:T(8,128)(2,1)S(1)}, bf16[96,384]{1,0:T(8,128)(2,1)S(1)}, u32[]{:S(2)}, u32[]{:S(2)}) %collective-permute-start.10) | collective-permute-done | bytes 73760 | tf_op jit(solution)/shard_map/ppermute | solution.py:64
  91.5 1.9 %collective-permute-start.11 = (bf16[2,96,384]{2,1,0:T(8,128)(2,1)S(1)}, bf16[2,96,384]{2,1,0:T(8,128)(2,1)S(1)}, u32[]{:S(2)}, u32[]{:S(2)}) collective-permute-start(bf16[2,96,384]{2,1,0:T(8,128)(2,1)S(1)} %maximum_select_fusion), channel_id=1, source_target_pairs={{0,4},{4,0},{8,12},{12,8},{1,5},{5,1},{9,13},{13,9},{2,6},{6,2},{1... | collective-permute-start | bytes 442376 | tf_op jit(solution)/shard_map/ppermute | solution.py:66
  93.9 2.7 %collective-permute-start.20 = (bf16[2,96,384]{2,1,0:T(8,128)(2,1)S(1)}, bf16[2,96,384]{2,1,0:T(8,128)(2,1)S(1)}, u32[]{:S(2)}, u32[]{:S(2)}) collective-permute-start(bf16[2,96,384]{2,1,0:T(8,128)(2,1)S(1)} %maximum_select_fusion.2), channel_id=1, source_target_pairs={{0,4},{4,0},{8,12},{12,8},{1,5},{5,1},{9,13},{13,9},{2,6},{6,2},{1... | collective-permute-start | bytes 442376 | tf_op jit(solution)/shard_map/ppermute | solution.py:66
  96.6 1.7 %collective-permute-done.11 = bf16[2,96,384]{2,1,0:T(8,128)(2,1)S(1)} collective-permute-done((bf16[2,96,384]{2,1,0:T(8,128)(2,1)S(1)}, bf16[2,96,384]{2,1,0:T(8,128)(2,1)S(1)}, u32[]{:S(2)}, u32[]{:S(2)}) %collective-permute-start.11) | collective-permute-done | bytes 147488 | tf_op jit(solution)/shard_map/ppermute | solution.py:66
  98.3 2.6 %collective-permute-done.15 = bf16[2,96,384]{2,1,0:T(8,128)(2,1)S(1)} collective-permute-done((bf16[2,96,384]{2,1,0:T(8,128)(2,1)S(1)}, bf16[2,96,384]{2,1,0:T(8,128)(2,1)S(1)}, u32[]{:S(2)}, u32[]{:S(2)}) %collective-permute-start.15) | collective-permute-done | bytes 147488 | tf_op jit(solution)/shard_map/ppermute | solution.py:66
  101.1 1.4 %collective-permute-done.20 = bf16[2,96,384]{2,1,0:T(8,128)(2,1)S(1)} collective-permute-done((bf16[2,96,384]{2,1,0:T(8,128)(2,1)S(1)}, bf16[2,96,384]{2,1,0:T(8,128)(2,1)S(1)}, u32[]{:S(2)}, u32[]{:S(2)}) %collective-permute-start.20) | collective-permute-done | bytes 147488 | tf_op jit(solution)/shard_map/ppermute | solution.py:66
  102.6 1.3 %maximum_convert_fusion = f32[3,384,384]{2,1,0:T(8,128)} fusion(bf16[1,384,384]{2,1,0:T(8,128)(2,1)S(1)} %bitcast.198, bf16[1,384,384]{2,1,0:T(8,128)(2,1)S(1)} %bitcast.197, bf16[1,384,384]{2,1,0:T(8,128)(2,1)S(1)} %bitcast.196), kind=kLoop, calls=%fused_computation.48 | loop fusion | flops 1327104 | bytes 2654208 | tf_op jit(solution)/shard_map/stack | solution.py:146
  (79 shorter events, 5.6 us)
Async XLA Ops:
  0.6 14.0 %copy-start = (bf16[3,384,768]{2,1,0:T(8,128)(2,1)S(1)}, bf16[3,384,768]{2,1,0:T(8,128)(2,1)}, u32[]{:S(2)}) copy-start(bf16[3,384,768]{2,1,0:T(8,128)(2,1)} %param.4) | copy-start | bytes 5308420
  0.6 26.0 %collective-permute-start.5 = (bf16[512,384]{1,0:T(8,128)(2,1)}, bf16[512,384]{1,0:T(8,128)(2,1)}, u32[]{:S(2)}, u32[]{:S(2)}) collective-permute-start(bf16[512,384]{1,0:T(8,128)(2,1)} %bitcast.182), channel_id=1, source_target_pairs={{2,0},{1,3},{6,4},{5,7},{10,8},{9,11},{14,12},{13,15},{18,16},{17,... | collective-permute-start | bytes 1179656 | tf_op jit(solution)/shard_map/ppermute | solution.py:88
  2.1 24.6 %collective-permute-start.6 = (bf16[512,384]{1,0:T(8,128)(2,1)}, bf16[512,384]{1,0:T(8,128)(2,1)}, u32[]{:S(2)}, u32[]{:S(2)}) collective-permute-start(bf16[512,384]{1,0:T(8,128)(2,1)} %bitcast.183), channel_id=1, source_target_pairs={{2,1},{1,2},{6,5},{5,6},{10,9},{9,10},{14,13},{13,14},{18,17},{17,... | collective-permute-start | bytes 1179656 | tf_op jit(solution)/shard_map/ppermute | solution.py:89
  3.5 2.8 %copy-start.1 = (bf16[1,512,384]{2,1,0:T(8,128)(2,1)S(1)}, bf16[1,512,384]{2,1,0:T(8,128)(2,1)}, u32[]{:S(2)}) copy-start(bf16[1,512,384]{2,1,0:T(8,128)(2,1)} %param.5) | copy-start | bytes 1179652
  7.3 13.8 %collective-permute-start = (bf16[2,256,384]{2,1,0:T(8,128)(2,1)}, bf16[2,256,384]{2,1,0:T(8,128)(2,1)S(1)}, u32[]{:S(2)}, u32[]{:S(2)}) collective-permute-start(bf16[2,256,384]{2,1,0:T(8,128)(2,1)} %get-tuple-element.19), channel_id=1, source_target_pairs={{0,4},{4,8},{8,12},{1,5},{5,9},{9,13},{2,6},{6,10},{10,14},{3,7},{... | collective-permute-start | bytes 1179656 | tf_op jit(solution)/shard_map/ppermute | solution.py:12
  12.3 11.3 %collective-permute-start.1 = (bf16[2,256,384]{2,1,0:T(8,128)(2,1)}, bf16[2,256,384]{2,1,0:T(8,128)(2,1)S(1)}, u32[]{:S(2)}, u32[]{:S(2)}) collective-permute-start(bf16[2,256,384]{2,1,0:T(8,128)(2,1)} %get-tuple-element.20), channel_id=1, source_target_pairs={{4,0},{8,4},{12,8},{5,1},{9,5},{13,9},{6,2},{10,6},{14,10},{7,3},{... | collective-permute-start | bytes 1179656 | tf_op jit(solution)/shard_map/ppermute | solution.py:12
  14.6 1.4 %copy-start.8 = (bf16[2,512,384]{2,1,0:T(8,128)(2,1)S(1)}, bf16[2,512,384]{2,1,0:T(8,128)(2,1)}, u32[]{:S(2)}) copy-start(bf16[2,512,384]{2,1,0:T(8,128)(2,1)} %pad_maximum_fusion.1) | copy-start | bytes 2359300
  14.7 2.7 %copy-start.6 = (bf16[3,384,384]{2,1,0:T(8,128)(2,1)}, bf16[3,384,384]{2,1,0:T(8,128)(2,1)S(1)}, u32[]{:S(2)}) copy-start(bf16[3,384,384]{2,1,0:T(8,128)(2,1)S(1)} %constant_dynamic-slice_fusion) | copy-start | bytes 2654212
  17.4 20.8 %collective-permute-start.3 = (bf16[2176,384]{1,0:T(8,128)(2,1)}, bf16[2176,384]{1,0:T(8,128)(2,1)}, u32[]{:S(2)}, u32[]{:S(2)}) collective-permute-start(bf16[2176,384]{1,0:T(8,128)(2,1)} %pad_maximum_fusion), channel_id=1, source_target_pairs={{0,1},{1,0},{2,3},{3,2},{4,5},{5,4},{6,7},{7,6},{8,9},{9,8},{10,11... | collective-permute-start | bytes 5013512 | tf_op jit(solution)/shard_map/ppermute | solution.py:96
  21.1 12.6 %collective-permute-start.4 = (bf16[512,384]{1,0:T(8,128)(2,1)S(1)}, bf16[512,384]{1,0:T(8,128)(2,1)S(1)}, u32[]{:S(2)}, u32[]{:S(2)}) collective-permute-start(bf16[512,384]{1,0:T(8,128)(2,1)S(1)} %get-tuple-element.30), channel_id=1, source_target_pairs={{0,2},{2,0},{1,3},{3,1},{4,6},{6,4},{5,7},{7,5},{8,10},{10,8},{9,1... | collective-permute-start | bytes 1179656 | tf_op jit(solution)/shard_map/ppermute | solution.py:91
  23.7 14.4 %collective-permute-start.2 = (bf16[2,2,256,384]{3,2,1,0:T(8,128)(2,1)S(1)}, bf16[2,2,256,384]{3,2,1,0:T(8,128)(2,1)S(1)}, u32[]{:S(2)}, u32[]{:S(2)}) collective-permute-start(bf16[2,2,256,384]{3,2,1,0:T(8,128)(2,1)S(1)} %pad_maximum_fusion.2), channel_id=1, source_target_pairs={{0,1},{1,0},{2,3},{3,2},{4,5},{5,4},{6,7},{7,6},{8,9},{9,8},{10,11... | collective-permute-start | bytes 2359304 | tf_op jit(solution)/shard_map/ppermute | solution.py:103
  27.8 8.7 %collective-permute-start.7 = (bf16[256,384]{1,0:T(8,128)(2,1)S(1)}, bf16[256,384]{1,0:T(8,128)(2,1)S(1)}, u32[]{:S(2)}, u32[]{:S(2)}) collective-permute-start(bf16[256,384]{1,0:T(8,128)(2,1)S(1)} %get-tuple-element.23), channel_id=1, source_target_pairs={{4,0},{8,4},{12,8},{5,1},{9,5},{13,9},{6,2},{10,6},{14,10},{7,3},{... | collective-permute-start | bytes 589832 | tf_op jit(solution)/shard_map/ppermute | solution.py:12
  29.1 8.6 %collective-permute-start.16 = (bf16[256,384]{1,0:T(8,128)(2,1)S(1)}, bf16[256,384]{1,0:T(8,128)(2,1)S(1)}, u32[]{:S(2)}, u32[]{:S(2)}) collective-permute-start(bf16[256,384]{1,0:T(8,128)(2,1)S(1)} %get-tuple-element.22), channel_id=1, source_target_pairs={{0,4},{4,8},{8,12},{1,5},{5,9},{9,13},{2,6},{6,10},{10,14},{3,7},{... | collective-permute-start | bytes 589832 | tf_op jit(solution)/shard_map/ppermute | solution.py:12
  40.7 1.0 copy-start.4
  41.7 21.8 %collective-permute-start.8 = (f32[2,96,384]{2,1,0:T(8,128)}, f32[2,96,384]{2,1,0:T(8,128)}, u32[]{:S(2)}, u32[]{:S(2)}) collective-permute-start(f32[2,96,384]{2,1,0:T(8,128)} %select_bitcast_fusion.2), channel_id=1, source_target_pairs={{0,4},{4,0},{8,12},{12,8},{1,5},{5,1},{9,13},{13,9},{2,6},{6,2},{1... | collective-permute-start | bytes 884744 | tf_op jit(solution)/shard_map/ppermute | solution.py:58
  44.6 1.2 %copy-start.2 = (f32[384,384]{1,0:T(8,128)}, f32[384,384]{1,0:T(8,128)S(1)}, u32[]{:S(2)}) copy-start(f32[384,384]{1,0:T(8,128)S(1)} %convolution_add_fusion.1) | copy-start | bytes 1769476
  45.4 21.8 %collective-permute-start.12 = (f32[2,96,384]{2,1,0:T(8,128)}, f32[2,96,384]{2,1,0:T(8,128)}, u32[]{:S(2)}, u32[]{:S(2)}) collective-permute-start(f32[2,96,384]{2,1,0:T(8,128)} %select_bitcast_fusion.1), channel_id=1, source_target_pairs={{0,4},{4,0},{8,12},{12,8},{1,5},{5,1},{9,13},{13,9},{2,6},{6,2},{1... | collective-permute-start | bytes 884744 | tf_op jit(solution)/shard_map/ppermute | solution.py:58
  46.6 22.1 %collective-permute-start.17 = (f32[2,96,384]{2,1,0:T(8,128)}, f32[2,96,384]{2,1,0:T(8,128)}, u32[]{:S(2)}, u32[]{:S(2)}) collective-permute-start(f32[2,96,384]{2,1,0:T(8,128)} %select_bitcast_fusion), channel_id=1, source_target_pairs={{0,4},{4,0},{8,12},{12,8},{1,5},{5,1},{9,13},{13,9},{2,6},{6,2},{1... | collective-permute-start | bytes 884744 | tf_op jit(solution)/shard_map/ppermute | solution.py:58
  49.8 3.0 %copy-start.7 = (bf16[3,384,384]{2,1,0:T(8,128)(2,1)S(1)}, bf16[3,384,384]{2,1,0:T(8,128)(2,1)}, u32[]{:S(2)}) copy-start(bf16[3,384,384]{2,1,0:T(8,128)(2,1)} %copy-done.6) | copy-start | bytes 2654212
  52.8 1.1 %copy-start.14 = (f32[512,384]{1,0:T(8,128)S(1)}, f32[512,384]{1,0:T(8,128)}, u32[]{:S(2)}) copy-start(f32[512,384]{1,0:T(8,128)} %get-tuple-element.31) | copy-start | bytes 2359300
  55.3 4.3 %copy-start.9 = (bf16[512,1,384]{2,0,1:T(8,128)(2,1)S(1)}, bf16[512,1,384]{2,0,1:T(8,128)(2,1)}, u32[]{:S(2)}) copy-start(bf16[512,1,384]{2,0,1:T(8,128)(2,1)} %get-tuple-element.6) | copy-start | bytes 1179652
  55.3 4.3 %copy-start.10 = (bf16[512,1,384]{2,0,1:T(8,128)(2,1)S(1)}, bf16[512,1,384]{2,0,1:T(8,128)(2,1)}, u32[]{:S(2)}) copy-start(bf16[512,1,384]{2,0,1:T(8,128)(2,1)} %get-tuple-element.13) | copy-start | bytes 1179652
  59.5 2.2 %copy-start.15 = (f32[512,384]{1,0:T(8,128)S(1)}, f32[512,384]{1,0:T(8,128)}, u32[]{:S(2)}) copy-start(f32[512,384]{1,0:T(8,128)} %get-tuple-element.31) | copy-start | bytes 2359300
  60.4 1.4 %copy-start.11 = (bf16[512,1,384]{2,0,1:T(8,128)(2,1)S(1)}, bf16[512,1,384]{2,0,1:T(8,128)(2,1)}, u32[]{:S(2)}) copy-start(bf16[512,1,384]{2,0,1:T(8,128)(2,1)} %get-tuple-element.10) | copy-start | bytes 1179652
  60.4 1.4 %copy-start.12 = (bf16[512,1,384]{2,0,1:T(8,128)(2,1)S(1)}, bf16[512,1,384]{2,0,1:T(8,128)(2,1)}, u32[]{:S(2)}) copy-start(bf16[512,1,384]{2,0,1:T(8,128)(2,1)} %get-tuple-element.15) | copy-start | bytes 1179652
  60.4 1.5 %copy-start.13 = (bf16[512,1,384]{2,0,1:T(8,128)(2,1)S(1)}, bf16[512,1,384]{2,0,1:T(8,128)(2,1)}, u32[]{:S(2)}) copy-start(bf16[512,1,384]{2,0,1:T(8,128)(2,1)} %get-tuple-element.4) | copy-start | bytes 1179652
  61.9 1.6 %copy-start.5 = (f32[384,384]{1,0:T(8,128)S(1)}, f32[384,384]{1,0:T(8,128)}, u32[]{:S(2)}) copy-start(f32[384,384]{1,0:T(8,128)} %copy-done.4) | copy-start | bytes 1769476
  63.5 3.8 %copy-start.3 = (f32[384,384]{1,0:T(8,128)S(1)}, f32[384,384]{1,0:T(8,128)}, u32[]{:S(2)}) copy-start(f32[384,384]{1,0:T(8,128)} %copy-done.2) | copy-start | bytes 1769476
  64.6 15.2 %collective-permute-start.9 = (f32[96,384]{1,0:T(8,128)S(1)}, f32[96,384]{1,0:T(8,128)S(1)}, u32[]{:S(2)}, u32[]{:S(2)}) collective-permute-start(f32[96,384]{1,0:T(8,128)S(1)} %select_bitcast_fusion.11), channel_id=1, source_target_pairs={{0,8},{8,0},{4,12},{12,4},{1,9},{9,1},{5,13},{13,5},{2,10},{10,2},... | collective-permute-start | bytes 442376 | tf_op jit(solution)/shard_map/ppermute | solution.py:63
  68.3 15.5 %collective-permute-start.13 = (f32[96,384]{1,0:T(8,128)S(1)}, f32[96,384]{1,0:T(8,128)S(1)}, u32[]{:S(2)}, u32[]{:S(2)}) collective-permute-start(f32[96,384]{1,0:T(8,128)S(1)} %select_bitcast_fusion.8), channel_id=1, source_target_pairs={{0,8},{8,0},{4,12},{12,4},{1,9},{9,1},{5,13},{13,5},{2,10},{10,2},... | collective-permute-start | bytes 442376 | tf_op jit(solution)/shard_map/ppermute | solution.py:63
  69.7 18.8 %collective-permute-start.18 = (f32[96,384]{1,0:T(8,128)S(1)}, f32[96,384]{1,0:T(8,128)S(1)}, u32[]{:S(2)}, u32[]{:S(2)}) collective-permute-start(f32[96,384]{1,0:T(8,128)S(1)} %select_bitcast_fusion.5), channel_id=1, source_target_pairs={{0,8},{8,0},{4,12},{12,4},{1,9},{9,1},{5,13},{13,5},{2,10},{10,2},... | collective-permute-start | bytes 442376 | tf_op jit(solution)/shard_map/ppermute | solution.py:63
  79.8 11.6 %collective-permute-start.10 = (bf16[96,384]{1,0:T(8,128)(2,1)S(1)}, bf16[96,384]{1,0:T(8,128)(2,1)S(1)}, u32[]{:S(2)}, u32[]{:S(2)}) collective-permute-start(bf16[96,384]{1,0:T(8,128)(2,1)S(1)} %fusion.68), channel_id=1, source_target_pairs={{0,8},{8,0},{4,12},{12,4},{1,9},{9,1},{5,13},{13,5},{2,10},{10,2},... | collective-permute-start | bytes 221192 | tf_op jit(solution)/shard_map/ppermute | solution.py:64
  83.8 9.7 %collective-permute-start.14 = (bf16[96,384]{1,0:T(8,128)(2,1)S(1)}, bf16[96,384]{1,0:T(8,128)(2,1)S(1)}, u32[]{:S(2)}, u32[]{:S(2)}) collective-permute-start(bf16[96,384]{1,0:T(8,128)(2,1)S(1)} %fusion.67), channel_id=1, source_target_pairs={{0,8},{8,0},{4,12},{12,4},{1,9},{9,1},{5,13},{13,5},{2,10},{10,2},... | collective-permute-start | bytes 221192 | tf_op jit(solution)/shard_map/ppermute | solution.py:64
  88.5 5.3 %collective-permute-start.19 = (bf16[96,384]{1,0:T(8,128)(2,1)S(1)}, bf16[96,384]{1,0:T(8,128)(2,1)S(1)}, u32[]{:S(2)}, u32[]{:S(2)}) collective-permute-start(bf16[96,384]{1,0:T(8,128)(2,1)S(1)} %fusion.66), channel_id=1, source_target_pairs={{0,8},{8,0},{4,12},{12,4},{1,9},{9,1},{5,13},{13,5},{2,10},{10,2},... | collective-permute-start | bytes 221192 | tf_op jit(solution)/shard_map/ppermute | solution.py:64
  91.5 6.8 %collective-permute-start.11 = (bf16[2,96,384]{2,1,0:T(8,128)(2,1)S(1)}, bf16[2,96,384]{2,1,0:T(8,128)(2,1)S(1)}, u32[]{:S(2)}, u32[]{:S(2)}) collective-permute-start(bf16[2,96,384]{2,1,0:T(8,128)(2,1)S(1)} %maximum_select_fusion), channel_id=1, source_target_pairs={{0,4},{4,0},{8,12},{12,8},{1,5},{5,1},{9,13},{13,9},{2,6},{6,2},{1... | collective-permute-start | bytes 442376 | tf_op jit(solution)/shard_map/ppermute | solution.py:66
  93.5 7.5 %collective-permute-start.15 = (bf16[2,96,384]{2,1,0:T(8,128)(2,1)S(1)}, bf16[2,96,384]{2,1,0:T(8,128)(2,1)S(1)}, u32[]{:S(2)}, u32[]{:S(2)}) collective-permute-start(bf16[2,96,384]{2,1,0:T(8,128)(2,1)S(1)} %maximum_select_fusion.1), channel_id=1, source_target_pairs={{0,4},{4,0},{8,12},{12,8},{1,5},{5,1},{9,13},{13,9},{2,6},{6,2},{1... | collective-permute-start | bytes 442376 | tf_op jit(solution)/shard_map/ppermute | solution.py:66
  93.9 8.6 %collective-permute-start.20 = (bf16[2,96,384]{2,1,0:T(8,128)(2,1)S(1)}, bf16[2,96,384]{2,1,0:T(8,128)(2,1)S(1)}, u32[]{:S(2)}, u32[]{:S(2)}) collective-permute-start(bf16[2,96,384]{2,1,0:T(8,128)(2,1)S(1)} %maximum_select_fusion.2), channel_id=1, source_target_pairs={{0,4},{4,0},{8,12},{12,8},{1,5},{5,1},{9,13},{13,9},{2,6},{6,2},{1... | collective-permute-start | bytes 442376 | tf_op jit(solution)/shard_map/ppermute | solution.py:66

commit v17 on v11

--- a/solution.py
+++ b/solution.py
@@ -98,8 +98,15 @@
     )
     par_mid = swapped[: 2 * rows].reshape(both.shape)
     w_par = swapped[2 * rows :].reshape(w_other.shape)
-    from_prev = shift_from(both[:, rows - spread :], "seq", 1)
-    from_next = shift_from(both[:, :spread], "seq", -1)
+    if lax.axis_size("batch") == 2:
+        going_up = jnp.concatenate([both, far_cot[None]], 0)
+        up = shift_from(going_up[:, rows - spread :], "seq", 1)
+        down = shift_from(going_up[:, :spread], "seq", -1)
+        from_prev, cot_prev = up[:2], up[2]
+        from_next, cot_next = down[:2], down[2]
+    else:
+        from_prev = shift_from(both[:, rows - spread :], "seq", 1)
+        from_next = shift_from(both[:, :spread], "seq", -1)
     par_halo = lax.ppermute(jnp.stack([from_prev, from_next]), "chan", SWAP)
     own_ext = jnp.concatenate([from_prev, both, from_next], 1)
     par_ext = jnp.concatenate([par_halo[0], par_mid, par_halo[1]], 1)
@@ -130,8 +137,6 @@
     seq_count = lax.axis_size("seq")
     if batch_count == 2:
         cot_mine = jnp.where(b == c, local_cot, par_cot)
-        cot_next = shift_from(far_cot[:spread], "seq", -1)
-        cot_prev = shift_from(far_cot[rows - spread :], "seq", 1)
         far_shifted = {
             1: far_cot,
             0: jnp.concatenate([far_cot[spread:], cot_next], 0),

time: 103 us -> 114 us (1.11)
  waiting for transfers between devices: 42.3 us -> 58.4 us
  starting transfers between devices: 31.2 us -> 28 us
  other arithmetic: 9.42 us -> 6.32 us
  matrix products: 11.5 us -> 12.7 us
    ppermute x2, waiting for transfers between devices: 0.01 us -> 17.5 us  [line_total(): total = (keep + lax.ppermute(give, 'seq', across)).astype(jnp.bfloat16)]
    ppermute x2, waiting for transfers between devices: 16.6 us -> 6.54 us  [line_total(): other = lax.ppermute(total, 'seq', across)]
    ppermute x2, waiting for transfers between devices: 10.9 us -> 2.86 us  [line_total(): lax.ppermute(jnp.where(odd, even_set, odd_set), 'seq', pairs)]
    ppermute x1, waiting for transfers between devices: 0.01 us -> 7.72 us  [shards(): same_core = lax.ppermute(local_cot, ('batch', 'chan'), [(2, 0), (1, 3)])]
    ppermute x2, starting transfers between devices: 0.33 us -> 7.68 us  [line_total(): far_set = lax.ppermute(own_set, 'seq', pairs)]
    ppermute x4 -> x2, waiting for transfers between devices: 8.39 us -> 15 us  [shift_from(): return lax.ppermute(block, axis, route)]
    ppermute x4 -> x2, starting transfers between devices: 11 us -> 4.79 us  [shift_from(): return lax.ppermute(block, axis, route)]
    ppermute x1, starting transfers between devices: 0.97 us -> 4.94 us  [shards(): far_mid = lax.ppermute(activation, 'batch', SWAP)]
  transfers between devices with their start and end apart: 17 -> 15, of which waited for: 7 -> 9; matrix products, arithmetic and copies ran while one was open for 22% -> 21% of each run, Pallas kernels for 0% -> 0%
where the time goes in v17:
time: 114 us; the launch traced here: 113 us
  waiting for transfers between devices  58.4 us (51%)
  starting transfers between devices  28 us (25%)
  matrix products  12.7 us (11%)
  local copies, waits for them, and re-layouts  6.96 us (6%)
  other arithmetic  6.32 us (6%)
    ppermute x2, waiting for transfers between devices, line_total(): total = (keep + lax.ppermute(give, 'seq', across)).astype(jnp.bfloat16)  17.5 us
    ppermute x2, waiting for transfers between devices, shift_from(): return lax.ppermute(block, axis, route)  15 us
    ppermute x2, waiting for transfers between devices, line_total(): far_set = lax.ppermute(own_set, 'seq', pairs)  8.75 us
    ppermute x1, waiting for transfers between devices, shards(): same_core = lax.ppermute(local_cot, ('batch', 'chan'), [(2, 0), (1, 3)])  7.72 us
    ppermute x2, starting transfers between devices, line_total(): far_set = lax.ppermute(own_set, 'seq', pairs)  7.68 us
    ppermute x2, waiting for transfers between devices, line_total(): other = lax.ppermute(total, 'seq', across)  6.54 us
    ppermute x1, starting transfers between devices, shards(): far_mid = lax.ppermute(activation, 'batch', SWAP)  4.94 us
    ppermute x2, starting transfers between devices, shift_from(): return lax.ppermute(block, axis, route)  4.79 us
  transfers between devices with their start and end apart: 15, of which 9 were waited for; matrix products, arithmetic and copies ran while one was open for 21% of the time, Pallas kernels for 0%

profile of v17, /device:TPU:0, one launch (start us, length us, event | category | flops | bytes accessed | tf_op | source)
XLA Modules:
  0.0 113.4 jit_solution(1650486849085600055)
XLA Ops:
  0.6 0.8 collective-permute-start.1
  1.5 1.3 %collective-permute-start = (bf16[512,384]{1,0:T(8,128)(2,1)}, bf16[512,384]{1,0:T(8,128)(2,1)}, u32[]{:S(2)}, u32[]{:S(2)}) collective-permute-start(bf16[512,384]{1,0:T(8,128)(2,1)} %bitcast.165), channel_id=1, source_target_pairs={{2,0},{1,3},{6,4},{5,7},{10,8},{9,11},{14,12},{13,15},{18,16},{17,... | collective-permute-start | bytes 1179656 | tf_op jit(solution)/shard_map/ppermute | solution.py:88
  2.8 2.8 %multiply_convert_fusion = (bf16[512,384]{1,0:T(8,128)(2,1)S(1)}, f32[512,384]{1,0:T(8,128)}) fusion(bf16[1,1024,384]{2,1,0:T(8,128)(2,1)} %param.3, s32[1024]{0:T(1024)S(1)} %get-tuple-element.36, s32[1024]{0:T(1024)S(1)} %get-tuple-element.37, pred[1024]{0:T(1024)(128)(4,1)S(1)} %fusion.70), kind=kOutput, calls=%fused_computation.58 | convolution fusion | flops 406519808 | bytes 1975296 | tf_op jit(solution)/shard_map/dot_general | solution.py:83
  5.6 4.9 %collective-permute-start.6 = (bf16[512,384]{1,0:T(8,128)(2,1)S(1)}, bf16[512,384]{1,0:T(8,128)(2,1)}, u32[]{:S(2)}, u32[]{:S(2)}) collective-permute-start(bf16[512,384]{1,0:T(8,128)(2,1)S(1)} %get-tuple-element.34), channel_id=1, source_target_pairs={{0,2},{2,0},{1,3},{3,1},{4,6},{6,4},{5,7},{7,5},{8,10},{10,8},{9,1... | collective-permute-start | bytes 1179656 | tf_op jit(solution)/shard_map/ppermute | solution.py:91
  10.6 0.1 pad_maximum_fusion.4
  10.7 0.1 constant_dynamic-slice_fusion
  10.8 7.7 %collective-permute-done = bf16[512,384]{1,0:T(8,128)(2,1)} collective-permute-done((bf16[512,384]{1,0:T(8,128)(2,1)}, bf16[512,384]{1,0:T(8,128)(2,1)}, u32[]{:S(2)}, u32[]{:S(2)}) %collective-permute-start) | collective-permute-done | bytes 393248 | tf_op jit(solution)/shard_map/ppermute | solution.py:88
  18.5 1.0 broadcast_select_fusion
  19.6 0.2 pad_maximum_fusion.2
  19.7 1.1 %fusion.84 = (bf16[3,256,384]{2,1,0:T(8,128)(2,1)}, bf16[3,256,384]{2,1,0:T(8,128)(2,1)}) fusion(bf16[3,512,384]{2,1,0:T(8,128)(2,1)S(1)} %pad_maximum_fusion.2), kind=kLoop, calls=%fused_computation.141 | loop fusion | bytes 2359296 | tf_op jit(solution)/shard_map/slice | solution.py:103
  20.9 3.5 %collective-permute-start.2 = (bf16[3,256,384]{2,1,0:T(8,128)(2,1)}, bf16[3,256,384]{2,1,0:T(8,128)(2,1)S(1)}, u32[]{:S(2)}, u32[]{:S(2)}) collective-permute-start(bf16[3,256,384]{2,1,0:T(8,128)(2,1)} %get-tuple-element.15), channel_id=1, source_target_pairs={{0,4},{4,8},{8,12},{1,5},{5,9},{9,13},{2,6},{6,10},{10,14},{3,7},{... | collective-permute-start | bytes 1769480 | tf_op jit(solution)/shard_map/ppermute | solution.py:12
  24.4 1.3 %pad_maximum_fusion.1 = bf16[2176,384]{1,0:T(8,128)(2,1)} fusion(bf16[1152,384]{1,0:T(8,128)(2,1)S(1)} %bitcast.170, bf16[1024,384]{1,0:T(8,128)(2,1)S(1)} %bitcast.172), kind=kLoop, calls=%fused_computation.3 | loop fusion | flops 3342336 | bytes 3342336 | tf_op jit(solution)/shard_map/concatenate | solution.py:97
  25.7 1.3 %collective-permute-start.3 = (bf16[3,256,384]{2,1,0:T(8,128)(2,1)}, bf16[3,256,384]{2,1,0:T(8,128)(2,1)S(1)}, u32[]{:S(2)}, u32[]{:S(2)}) collective-permute-start(bf16[3,256,384]{2,1,0:T(8,128)(2,1)} %get-tuple-element.16), channel_id=1, source_target_pairs={{4,0},{8,4},{12,8},{5,1},{9,5},{13,9},{6,2},{10,6},{14,10},{7,3},{... | collective-permute-start | bytes 1769480 | tf_op jit(solution)/shard_map/ppermute | solution.py:12
  27.0 1.4 %fusion.86 = f32[384,384]{1,0:T(8,128)S(1)} fusion(bf16[512,384]{1,0:T(8,128)(2,1)} %collective-permute-done.6, bf16[512,384]{1,0:T(8,128)(2,1)S(1)} %broadcast_select_fusion), kind=kOutput, calls=%fused_computation.143 | convolution fusion | flops 150994944 | bytes 1376256 | tf_op jit(solution)/shard_map/dot_general | solution.py:149
  28.5 7.6 %collective-permute-done.2 = bf16[3,256,384]{2,1,0:T(8,128)(2,1)S(1)} collective-permute-done((bf16[3,256,384]{2,1,0:T(8,128)(2,1)}, bf16[3,256,384]{2,1,0:T(8,128)(2,1)S(1)}, u32[]{:S(2)}, u32[]{:S(2)}) %collective-permute-start.2) | collective-permute-done | bytes 589856 | tf_op jit(solution)/shard_map/ppermute | solution.py:12
  36.1 7.5 %collective-permute-done.3 = bf16[3,256,384]{2,1,0:T(8,128)(2,1)S(1)} collective-permute-done((bf16[3,256,384]{2,1,0:T(8,128)(2,1)}, bf16[3,256,384]{2,1,0:T(8,128)(2,1)S(1)}, u32[]{:S(2)}, u32[]{:S(2)}) %collective-permute-start.3) | collective-permute-done | bytes 589856 | tf_op jit(solution)/shard_map/ppermute | solution.py:12
  43.6 0.1 pad_maximum_fusion.5
  43.9 1.4 %fusion.55 = f32[384,384]{1,0:T(8,128)S(1)} fusion(bf16[512,384]{1,0:T(8,128)(2,1)} %collective-permute-done.6, bf16[256,384]{1,0:T(8,128)(2,1)S(1)} %get-tuple-element.30, bf16[256,384]{1,0:T(8,128)(2,1)S(1)} %slice_bitcast_fusion.4), kind=kOutput, calls=%fused_computation.87 | convolution fusion | flops 151781376 | bytes 1376256 | tf_op jit(solution)/shard_map/dot_general | solution.py:149
  45.3 1.4 %fusion.51 = f32[384,384]{1,0:T(8,128)S(1)} fusion(bf16[512,384]{1,0:T(8,128)(2,1)} %collective-permute-done.6, bf16[256,384]{1,0:T(8,128)(2,1)S(1)} %slice_bitcast_fusion.5, bf16[256,384]{1,0:T(8,128)(2,1)S(1)} %get-tuple-element.29), kind=kOutput, calls=%fused_computation.83 | convolution fusion | flops 151781376 | bytes 1376256 | tf_op jit(solution)/shard_map/dot_general | solution.py:149
  46.7 1.2 %fusion.50 = (bf16[512,1,384]{2,0,1:T(8,128)(2,1)S(1)}, bf16[512,1,384]{2,0,1:T(8,128)(2,1)S(1)}, bf16[512,1,384]{2,0,1:T(8,128)(2,1)S(1)}, bf16[512,1,384]{2,0,1:T(8,128)(2,1)S(1)}, bf16[1,512,384]{2,1,0:T(8,128)(2,1)S(1)}) fusion(bf16[2,256,384]{2,1,0:T(8,128)(2,1)S(1)} %get-tuple-element.28, bf16[1,512,384]{2,1,0:T(8,128)(2,1)S(1)} %copy-done.1, ...), kind=kLoop, calls=%fused_computation.74 | loop fusion | flops 4915200 | bytes 3932161 | tf_op jit(solution)/shard_map/stack | solution.py:21
  47.9 0.4 convolution_add_fusion.1
  48.3 0.4 convolution_add_fusion.2
  48.7 0.4 convolution_add_fusion
  49.2 1.6 %collective-permute-start.11 = (f32[2,96,384]{2,1,0:T(8,128)S(1)}, f32[2,96,384]{2,1,0:T(8,128)S(1)}, u32[]{:S(2)}, u32[]{:S(2)}) collective-permute-start(f32[2,96,384]{2,1,0:T(8,128)S(1)} %select_bitcast_fusion.1), channel_id=1, source_target_pairs={{0,4},{4,0},{8,12},{12,8},{1,5},{5,1},{9,13},{13,9},{2,6},{6,2},{1... | collective-permute-start | bytes 884744 | tf_op jit(solution)/shard_map/ppermute | solution.py:58
  50.9 0.5 collective-permute-start.7
  51.5 1.2 %slice.198 = bf16[1024,384]{1,0:T(8,128)(2,1)S(1)} slice(bf16[2176,384]{1,0:T(8,128)(2,1)} %collective-permute-done.5), slice={[0:1024], [0:384]} | slice | bytes 1572864 | tf_op jit(solution)/shard_map/slice | solution.py:99
  52.7 1.3 %slice.201 = bf16[1152,384]{1,0:T(8,128)(2,1)S(1)} slice(bf16[2176,384]{1,0:T(8,128)(2,1)} %collective-permute-done.5), slice={[1024:2176], [0:384]} | slice | bytes 1769472 | tf_op jit(solution)/shard_map/slice | solution.py:100
  54.0 0.8 convolution_bitcast_fusion.3
  54.8 1.2 %slice_bitcast_fusion.3 = (bf16[512,1,384]{2,0,1:T(8,128)(2,1)S(1)}, bf16[512,1,384]{2,0,1:T(8,128)(2,1)S(1)}) fusion(bf16[2176,384]{1,0:T(8,128)(2,1)} %collective-permute-done.5), kind=kLoop, calls=%fused_computation.98 | loop fusion | bytes 1572864 | tf_op jit(solution)/shard_map/stack | solution.py:21
  56.0 0.1 slice_bitcast_fusion.2
  56.1 0.2 fusion.48
  56.3 2.9 %collective-permute-done.11 = f32[2,96,384]{2,1,0:T(8,128)S(1)} collective-permute-done((f32[2,96,384]{2,1,0:T(8,128)S(1)}, f32[2,96,384]{2,1,0:T(8,128)S(1)}, u32[]{:S(2)}, u32[]{:S(2)}) %collective-permute-start.11) | collective-permute-done | bytes 294944 | tf_op jit(solution)/shard_map/ppermute | solution.py:58
  59.2 2.6 %collective-permute-start.12 = (f32[96,384]{1,0:T(8,128)S(1)}, f32[96,384]{1,0:T(8,128)S(1)}, u32[]{:S(2)}, u32[]{:S(2)}) collective-permute-start(f32[96,384]{1,0:T(8,128)S(1)} %select_bitcast_fusion.7), channel_id=1, source_target_pairs={{0,8},{8,0},{4,12},{12,4},{1,9},{9,1},{5,13},{13,5},{2,10},{10,2},... | collective-permute-start | bytes 442376 | tf_op jit(solution)/shard_map/ppermute | solution.py:63
  61.8 0.8 convolution_bitcast_fusion
  62.7 10.8 %collective-permute-done.12 = f32[96,384]{1,0:T(8,128)S(1)} collective-permute-done((f32[96,384]{1,0:T(8,128)S(1)}, f32[96,384]{1,0:T(8,128)S(1)}, u32[]{:S(2)}, u32[]{:S(2)}) %collective-permute-start.12) | collective-permute-done | bytes 147488 | tf_op jit(solution)/shard_map/ppermute | solution.py:63
  73.5 3.4 %collective-permute-start.13 = (bf16[96,384]{1,0:T(8,128)(2,1)S(1)}, bf16[96,384]{1,0:T(8,128)(2,1)S(1)}, u32[]{:S(2)}, u32[]{:S(2)}) collective-permute-start(bf16[96,384]{1,0:T(8,128)(2,1)S(1)} %fusion.67), channel_id=1, source_target_pairs={{0,8},{8,0},{4,12},{12,4},{1,9},{9,1},{5,13},{13,5},{2,10},{10,2},... | collective-permute-start | bytes 221192 | tf_op jit(solution)/shard_map/ppermute | solution.py:64
  77.1 0.1 collective-permute-start.8
  77.2 1.3 %fusion.39 = bf16[512,384]{1,0:T(8,128)(2,1)S(1)} fusion(f32[512,384]{1,0:T(8,128)S(1)} %copy-done.6, f32[512,384]{1,0:T(8,128)S(1)} %convolution_bitcast_fusion, bf16[512,1,384]{2,0,1:T(8,128)(2,1)S(1)} %get-tuple-element.18, bf16[512,1,384]{2,0,1:T(8,128)(2,1)S(1)} %bitcast.166, bf16[512,1,384]{2,0,1:T(8,128)(2,1)S(1)} %get-tuple-element.7, ...), kind=kOutput, calls=%fused_computation.54 | convolution fusion | flops 458883072 | bytes 4423684 | tf_op jit(solution)/shard_map/tko,kio->ti/dot_general | solution.py:123
  78.5 1.1 collective-permute-done.13
  79.7 7.6 %collective-permute-start.14 = (bf16[2,96,384]{2,1,0:T(8,128)(2,1)S(1)}, bf16[2,96,384]{2,1,0:T(8,128)(2,1)S(1)}, u32[]{:S(2)}, u32[]{:S(2)}) collective-permute-start(bf16[2,96,384]{2,1,0:T(8,128)(2,1)S(1)} %maximum_select_fusion.1), channel_id=1, source_target_pairs={{0,4},{4,0},{8,12},{12,8},{1,5},{5,1},{9,13},{13,9},{2,6},{6,2},{1... | collective-permute-start | bytes 442376 | tf_op jit(solution)/shard_map/ppermute | solution.py:66
  87.3 6.7 %collective-permute-done.8 = f32[192,384]{1,0:T(8,128)S(1)} collective-permute-done((f32[192,384]{1,0:T(8,128)S(1)}, f32[192,384]{1,0:T(8,128)S(1)}, u32[]{:S(2)}, u32[]{:S(2)}) %collective-permute-start.8) | collective-permute-done | bytes 294944 | tf_op jit(solution)/shard_map/ppermute | solution.py:63
  94.1 1.6 %fusion.4 = bf16[1,512,384]{2,1,0:T(8,128)(2,1)} fusion(f32[512,384]{1,0:T(8,128)S(1)} %copy-done.6, f32[512,384]{1,0:T(8,128)S(1)} %convolution_bitcast_fusion.3, bf16[3,384,384]{2,1,0:T(8,128)(2,1)S(1)} %bitcast.178, bf16[512,1,384]{2,0,1:T(8,128)(2,1)S(1)} %get-tuple-element.12, bf16[512,1,384]{2,0,1:T(8,128)(2,1)S(1)} %get-tuple-element.4, ...), kind=kOutput, calls=%fused_computation.15 | convolution fusion | flops 454754304 | bytes 4030464 | tf_op jit(solution)/shard_map/tki,kio->to/dot_general | solution.py:117
  95.7 0.4 broadcast_in_dim.22
  96.1 1.2 %convert_element_type.54 = bf16[1,1024,384]{2,1,0:T(8,128)(2,1)} reshape(bf16[512,2,384]{2,1,0:T(2,128)(2,1)S(1)} %broadcast_in_dim.22) | data formatting | bytes 1572864 | tf_op jit(solution)/shard_map/convert_element_type | solution.py:132
  97.3 5.4 %collective-permute-done.9 = bf16[192,384]{1,0:T(8,128)(2,1)S(1)} collective-permute-done((bf16[192,384]{1,0:T(8,128)(2,1)S(1)}, bf16[192,384]{1,0:T(8,128)(2,1)S(1)}, u32[]{:S(2)}, u32[]{:S(2)}) %collective-permute-start.9) | collective-permute-done | bytes 147488 | tf_op jit(solution)/shard_map/ppermute | solution.py:64
  103.0 8.7 %collective-permute-done.10 = bf16[2,192,384]{2,1,0:T(8,128)(2,1)S(1)} collective-permute-done((bf16[2,192,384]{2,1,0:T(8,128)(2,1)S(1)}, bf16[2,192,384]{2,1,0:T(8,128)(2,1)S(1)}, u32[]{:S(2)}, u32[]{:S(2)}) %collective-permute-start.10) | collective-permute-done | bytes 294944 | tf_op jit(solution)/shard_map/ppermute | solution.py:66
  111.8 0.1 select_bitcast_fusion.3
  112.1 1.4 %pad_maximum_fusion = f32[3,384,384]{2,1,0:T(8,128)} fusion(f32[1,384,384]{2,1,0:T(8,128)S(1)} %bitcast.175, f32[1,384,384]{2,1,0:T(8,128)S(1)} %bitcast.173, f32[1,384,384]{2,1,0:T(8,128)S(1)} %bitcast.174), kind=kLoop, calls=%fused_computation.2 | loop fusion | flops 884736 | bytes 3538944 | tf_op jit(solution)/shard_map/stack | solution.py:153
  (47 shorter events, 1.3 us)
Async XLA Ops:
  0.6 10.0 %copy-start = (bf16[3,384,768]{2,1,0:T(8,128)(2,1)S(1)}, bf16[3,384,768]{2,1,0:T(8,128)(2,1)}, u32[]{:S(2)}) copy-start(bf16[3,384,768]{2,1,0:T(8,128)(2,1)} %param.4) | copy-start | bytes 5308420
  0.6 10.1 %collective-permute-start.1 = (bf16[512,384]{1,0:T(8,128)(2,1)}, bf16[512,384]{1,0:T(8,128)(2,1)S(1)}, u32[]{:S(2)}, u32[]{:S(2)}) collective-permute-start(bf16[512,384]{1,0:T(8,128)(2,1)} %bitcast.164), channel_id=1, source_target_pairs={{2,1},{1,2},{6,5},{5,6},{10,9},{9,10},{14,13},{13,14},{18,17},{17,... | collective-permute-start | bytes 1179656 | tf_op jit(solution)/shard_map/ppermute | solution.py:89
  1.5 17.0 %collective-permute-start = (bf16[512,384]{1,0:T(8,128)(2,1)}, bf16[512,384]{1,0:T(8,128)(2,1)}, u32[]{:S(2)}, u32[]{:S(2)}) collective-permute-start(bf16[512,384]{1,0:T(8,128)(2,1)} %bitcast.165), channel_id=1, source_target_pairs={{2,0},{1,3},{6,4},{5,7},{10,8},{9,11},{14,12},{13,15},{18,16},{17,... | collective-permute-start | bytes 1179656 | tf_op jit(solution)/shard_map/ppermute | solution.py:88
  2.8 7.8 %copy-start.1 = (bf16[1,512,384]{2,1,0:T(8,128)(2,1)S(1)}, bf16[1,512,384]{2,1,0:T(8,128)(2,1)}, u32[]{:S(2)}) copy-start(bf16[1,512,384]{2,1,0:T(8,128)(2,1)} %param.5) | copy-start | bytes 1179652
  5.6 21.4 %collective-permute-start.6 = (bf16[512,384]{1,0:T(8,128)(2,1)S(1)}, bf16[512,384]{1,0:T(8,128)(2,1)}, u32[]{:S(2)}, u32[]{:S(2)}) collective-permute-start(bf16[512,384]{1,0:T(8,128)(2,1)S(1)} %get-tuple-element.34), channel_id=1, source_target_pairs={{0,2},{2,0},{1,3},{3,1},{4,6},{6,4},{5,7},{7,5},{8,10},{10,8},{9,1... | collective-permute-start | bytes 1179656 | tf_op jit(solution)/shard_map/ppermute | solution.py:91
  10.8 13.6 %copy-start.2 = (bf16[3,384,384]{2,1,0:T(8,128)(2,1)}, bf16[3,384,384]{2,1,0:T(8,128)(2,1)S(1)}, u32[]{:S(2)}) copy-start(bf16[3,384,384]{2,1,0:T(8,128)(2,1)S(1)} %constant_dynamic-slice_fusion) | copy-start | bytes 2654212
  20.9 15.2 %collective-permute-start.2 = (bf16[3,256,384]{2,1,0:T(8,128)(2,1)}, bf16[3,256,384]{2,1,0:T(8,128)(2,1)S(1)}, u32[]{:S(2)}, u32[]{:S(2)}) collective-permute-start(bf16[3,256,384]{2,1,0:T(8,128)(2,1)} %get-tuple-element.15), channel_id=1, source_target_pairs={{0,4},{4,8},{8,12},{1,5},{5,9},{9,13},{2,6},{6,10},{10,14},{3,7},{... | collective-permute-start | bytes 1769480 | tf_op jit(solution)/shard_map/ppermute | solution.py:12
  25.7 20.9 %collective-permute-start.5 = (bf16[2176,384]{1,0:T(8,128)(2,1)}, bf16[2176,384]{1,0:T(8,128)(2,1)}, u32[]{:S(2)}, u32[]{:S(2)}) collective-permute-start(bf16[2176,384]{1,0:T(8,128)(2,1)} %pad_maximum_fusion.1), channel_id=1, source_target_pairs={{0,1},{1,0},{2,3},{3,2},{4,5},{5,4},{6,7},{7,6},{8,9},{9,8},{10,11... | collective-permute-start | bytes 5013512 | tf_op jit(solution)/shard_map/ppermute | solution.py:96
  25.7 17.8 %collective-permute-start.3 = (bf16[3,256,384]{2,1,0:T(8,128)(2,1)}, bf16[3,256,384]{2,1,0:T(8,128)(2,1)S(1)}, u32[]{:S(2)}, u32[]{:S(2)}) collective-permute-start(bf16[3,256,384]{2,1,0:T(8,128)(2,1)} %get-tuple-element.16), channel_id=1, source_target_pairs={{4,0},{8,4},{12,8},{5,1},{9,5},{13,9},{6,2},{10,6},{14,10},{7,3},{... | collective-permute-start | bytes 1769480 | tf_op jit(solution)/shard_map/ppermute | solution.py:12
  43.7 12.2 %collective-permute-start.4 = (bf16[2,2,256,384]{3,2,1,0:T(8,128)(2,1)S(1)}, bf16[2,2,256,384]{3,2,1,0:T(8,128)(2,1)S(1)}, u32[]{:S(2)}, u32[]{:S(2)}) collective-permute-start(bf16[2,2,256,384]{3,2,1,0:T(8,128)(2,1)S(1)} %pad_maximum_fusion.5), channel_id=1, source_target_pairs={{0,1},{1,0},{2,3},{3,2},{4,5},{5,4},{6,7},{7,6},{8,9},{9,8},{10,11... | collective-permute-start | bytes 2359304 | tf_op jit(solution)/shard_map/ppermute | solution.py:110
  49.2 9.9 %collective-permute-start.11 = (f32[2,96,384]{2,1,0:T(8,128)S(1)}, f32[2,96,384]{2,1,0:T(8,128)S(1)}, u32[]{:S(2)}, u32[]{:S(2)}) collective-permute-start(f32[2,96,384]{2,1,0:T(8,128)S(1)} %select_bitcast_fusion.1), channel_id=1, source_target_pairs={{0,4},{4,0},{8,12},{12,8},{1,5},{5,1},{9,13},{13,9},{2,6},{6,2},{1... | collective-permute-start | bytes 884744 | tf_op jit(solution)/shard_map/ppermute | solution.py:58
  50.9 26.1 %collective-permute-start.7 = (f32[2,192,384]{2,1,0:T(8,128)S(1)}, f32[2,192,384]{2,1,0:T(8,128)S(1)}, u32[]{:S(2)}, u32[]{:S(2)}) collective-permute-start(f32[2,192,384]{2,1,0:T(8,128)S(1)} %select_bitcast_fusion), channel_id=1, source_target_pairs={{0,4},{4,0},{8,12},{12,8},{1,5},{5,1},{9,13},{13,9},{2,6},{6,2},{1... | collective-permute-start | bytes 1769480 | tf_op jit(solution)/shard_map/ppermute | solution.py:58
  56.3 5.6 %copy-start.3 = (bf16[3,384,384]{2,1,0:T(8,128)(2,1)S(1)}, bf16[3,384,384]{2,1,0:T(8,128)(2,1)}, u32[]{:S(2)}) copy-start(bf16[3,384,384]{2,1,0:T(8,128)(2,1)} %copy-done.2) | copy-start | bytes 2654212
  59.2 14.3 %collective-permute-start.12 = (f32[96,384]{1,0:T(8,128)S(1)}, f32[96,384]{1,0:T(8,128)S(1)}, u32[]{:S(2)}, u32[]{:S(2)}) collective-permute-start(f32[96,384]{1,0:T(8,128)S(1)} %select_bitcast_fusion.7), channel_id=1, source_target_pairs={{0,8},{8,0},{4,12},{12,4},{1,9},{9,1},{5,13},{13,5},{2,10},{10,2},... | collective-permute-start | bytes 442376 | tf_op jit(solution)/shard_map/ppermute | solution.py:63
  73.5 3.7 %copy-start.6 = (f32[512,384]{1,0:T(8,128)S(1)}, f32[512,384]{1,0:T(8,128)}, u32[]{:S(2)}) copy-start(f32[512,384]{1,0:T(8,128)} %get-tuple-element.35) | copy-start | bytes 2359300
  73.5 6.1 %collective-permute-start.13 = (bf16[96,384]{1,0:T(8,128)(2,1)S(1)}, bf16[96,384]{1,0:T(8,128)(2,1)S(1)}, u32[]{:S(2)}, u32[]{:S(2)}) collective-permute-start(bf16[96,384]{1,0:T(8,128)(2,1)S(1)} %fusion.67), channel_id=1, source_target_pairs={{0,8},{8,0},{4,12},{12,4},{1,9},{9,1},{5,13},{13,5},{2,10},{10,2},... | collective-permute-start | bytes 221192 | tf_op jit(solution)/shard_map/ppermute | solution.py:64
  77.1 16.9 %collective-permute-start.8 = (f32[192,384]{1,0:T(8,128)S(1)}, f32[192,384]{1,0:T(8,128)S(1)}, u32[]{:S(2)}, u32[]{:S(2)}) collective-permute-start(f32[192,384]{1,0:T(8,128)S(1)} %select_bitcast_fusion.4), channel_id=1, source_target_pairs={{0,8},{8,0},{4,12},{12,4},{1,9},{9,1},{5,13},{13,5},{2,10},{10,2},... | collective-permute-start | bytes 884744 | tf_op jit(solution)/shard_map/ppermute | solution.py:63
  79.7 14.5 %copy-start.4 = (bf16[96,384]{1,0:T(8,128)(2,1)}, bf16[96,384]{1,0:T(8,128)(2,1)S(1)}, u32[]{:S(2)}) copy-start(bf16[96,384]{1,0:T(8,128)(2,1)S(1)} %collective-permute-done.13) | copy-start | bytes 221188
  79.7 23.2 %collective-permute-start.14 = (bf16[2,96,384]{2,1,0:T(8,128)(2,1)S(1)}, bf16[2,96,384]{2,1,0:T(8,128)(2,1)S(1)}, u32[]{:S(2)}, u32[]{:S(2)}) collective-permute-start(bf16[2,96,384]{2,1,0:T(8,128)(2,1)S(1)} %maximum_select_fusion.1), channel_id=1, source_target_pairs={{0,4},{4,0},{8,12},{12,8},{1,5},{5,1},{9,13},{13,9},{2,6},{6,2},{1... | collective-permute-start | bytes 442376 | tf_op jit(solution)/shard_map/ppermute | solution.py:66
  94.0 8.7 %collective-permute-start.9 = (bf16[192,384]{1,0:T(8,128)(2,1)S(1)}, bf16[192,384]{1,0:T(8,128)(2,1)S(1)}, u32[]{:S(2)}, u32[]{:S(2)}) collective-permute-start(bf16[192,384]{1,0:T(8,128)(2,1)S(1)} %fusion.66), channel_id=1, source_target_pairs={{0,8},{8,0},{4,12},{12,4},{1,9},{9,1},{5,13},{13,5},{2,10},{10,2},... | collective-permute-start | bytes 442376 | tf_op jit(solution)/shard_map/ppermute | solution.py:64
  96.1 6.8 %copy-start.5 = (bf16[96,384]{1,0:T(8,128)(2,1)S(1)}, bf16[96,384]{1,0:T(8,128)(2,1)}, u32[]{:S(2)}) copy-start(bf16[96,384]{1,0:T(8,128)(2,1)} %copy-done.4) | copy-start | bytes 221188
  102.8 9.0 %collective-permute-start.10 = (bf16[2,192,384]{2,1,0:T(8,128)(2,1)S(1)}, bf16[2,192,384]{2,1,0:T(8,128)(2,1)S(1)}, u32[]{:S(2)}, u32[]{:S(2)}) collective-permute-start(bf16[2,192,384]{2,1,0:T(8,128)(2,1)S(1)} %maximum_select_fusion), channel_id=1, source_target_pairs={{0,4},{4,0},{8,12},{12,8},{1,5},{5,1},{9,13},{13,9},{2,6},{6,2},{1... | collective-permute-start | bytes 884744 | tf_op jit(solution)/shard_map/ppermute | solution.py:66

commit v18 on v11

--- a/solution.py
+++ b/solution.py
@@ -86,18 +86,19 @@
     if lax.axis_size("batch") == 2:
         b = lax.axis_index("batch")
         same_core = lax.ppermute(local_cot, ("batch", "chan"), [(2, 0), (1, 3)])
-        cross_core = lax.ppermute(local_cot, ("batch", "chan"), [(2, 1), (1, 2)])
-        far_cot = jnp.where(b == c, same_core, cross_core)
         far_mid = lax.ppermute(activation, "batch", SWAP)
 
     both = jnp.stack([activation, local_cot])
     w_own = half_of(conv_weight, c, 2)
     w_other = half_of(conv_weight, 1 - c, 2)
-    swapped = lax.ppermute(
-        jnp.concatenate([both.reshape(-1, width), w_other.reshape(-1, width)], 0), "chan", SWAP
-    )
+    sending = [both.reshape(-1, width), w_other.reshape(-1, width)]
+    if lax.axis_size("batch") == 2:
+        sending.append(same_core)
+    swapped = lax.ppermute(jnp.concatenate(sending, 0), "chan", SWAP)
     par_mid = swapped[: 2 * rows].reshape(both.shape)
-    w_par = swapped[2 * rows :].reshape(w_other.shape)
+    w_par = swapped[2 * rows : 2 * rows + w_other.shape[0] * w_other.shape[1]].reshape(w_other.shape)
+    if lax.axis_size("batch") == 2:
+        far_cot = jnp.where(b == c, same_core, swapped[-rows:])
     from_prev = shift_from(both[:, rows - spread :], "seq", 1)
     from_next = shift_from(both[:, :spread], "seq", -1)
     par_halo = lax.ppermute(jnp.stack([from_prev, from_next]), "chan", SWAP)

time: 103 us -> 110 us (1.068)
  waiting for transfers between devices: 42.3 us -> 58.8 us
  starting transfers between devices: 31.2 us -> 22.1 us
  other arithmetic: 9.42 us -> 7.52 us
  matrix products: 11.5 us -> 12.7 us
    ppermute x1, waiting for transfers between devices: 0.01 us -> 5.84 us  [shards(): same_core = lax.ppermute(local_cot, ('batch', 'chan'), [(2, 0), (1, 3)])]
    ppermute x2 -> x1, starting transfers between devices: 5.14 us -> 0.01 us  [shards(): swapped = lax.ppermute(jnp.concatenate(sending, 0), 'chan', SWAP)]
    ppermute x4, waiting for transfers between devices: 8.39 us -> 11.8 us  [shift_from(): return lax.ppermute(block, axis, route)]
    dot_general x3, matrix products: 1.16 us -> 4.17 us  [shards(): jnp.dot(far_mid.T, far_shifted[k], preferred_element_type=jnp.float32)]
    ppermute x1, starting transfers between devices: 2.82 us -> 0.01 us  [shards(): par_halo = lax.ppermute(jnp.stack([from_prev, from_next]), 'chan', SWAP)]
    ppermute x1, waiting for transfers between devices: 0.01 us -> 2.62 us  [shards(): par_halo = lax.ppermute(jnp.stack([from_prev, from_next]), 'chan', SWAP)]
    dot_general x3, matrix products: 3.05 us -> 1.2 us  [shards(): jnp.dot(own_taps[:, k].T, cot_mine, preferred_element_type=jnp.float32)]
    another operation x2, other arithmetic: 1.95 us -> 0.18 us  [shards(): both = jnp.stack([activation, local_cot])]
  transfers between devices with their start and end apart: 17 -> 16, of which waited for: 7 -> 9; matrix products, arithmetic and copies ran while one was open for 22% -> 21% of each run, Pallas kernels for 0% -> 0%
where the time goes in v18:
time: 110 us
  waiting for transfers between devices  58.8 us (53%)
  starting transfers between devices  22.1 us (20%)
  matrix products  12.7 us (12%)
  other arithmetic  7.52 us (7%)
  local copies, waits for them, and re-layouts  7.48 us (7%)
    ppermute x2, waiting for transfers between devices, line_total(): other = lax.ppermute(total, 'seq', across)  18.3 us
    ppermute x2, waiting for transfers between devices, line_total(): lax.ppermute(jnp.where(odd, even_set, odd_set), 'seq', pairs)  11.9 us
    ppermute x4, waiting for transfers between devices, shift_from(): return lax.ppermute(block, axis, route)  11.8 us
    ppermute x4, starting transfers between devices, shift_from(): return lax.ppermute(block, axis, route)  10.7 us
    ppermute x2, waiting for transfers between devices, line_total(): far_set = lax.ppermute(own_set, 'seq', pairs)  7.9 us
    ppermute x1, waiting for transfers between devices, shards(): same_core = lax.ppermute(local_cot, ('batch', 'chan'), [(2, 0), (1, 3)])  5.84 us
    ppermute x2, starting transfers between devices, line_total(): other = lax.ppermute(total, 'seq', across)  4.66 us
    dot_general x3, matrix products, shards(): jnp.dot(far_mid.T, far_shifted[k], preferred_element_type=jnp.float32)  4.17 us
  transfers between devices with their start and end apart: 16, of which 9 were waited for; matrix products, arithmetic and copies ran while one was open for 21% of the time, Pallas kernels for 0%

profile of v18, /device:TPU:0, one launch (start us, length us, event | category | flops | bytes accessed | tf_op | source)
XLA Modules:
  0.0 109.6 jit_solution(11343140569369493921)
XLA Ops:
  0.6 1.4 %collective-permute-start.3 = (bf16[512,384]{1,0:T(8,128)(2,1)}, bf16[512,384]{1,0:T(8,128)(2,1)S(1)}, u32[]{:S(2)}, u32[]{:S(2)}) collective-permute-start(bf16[512,384]{1,0:T(8,128)(2,1)} %bitcast.157), channel_id=1, source_target_pairs={{2,0},{1,3},{6,4},{5,7},{10,8},{9,11},{14,12},{13,15},{18,16},{17,... | collective-permute-start | bytes 1179656 | tf_op jit(solution)/shard_map/ppermute | solution.py:88
  2.1 2.8 %multiply_convert_fusion = (bf16[512,384]{1,0:T(8,128)(2,1)S(1)}, f32[512,384]{1,0:T(8,128)}) fusion(bf16[1,1024,384]{2,1,0:T(8,128)(2,1)} %param.3, s32[1024]{0:T(1024)S(1)} %get-tuple-element.33, s32[1024]{0:T(1024)S(1)} %get-tuple-element.34, pred[1024]{0:T(1024)(128)(4,1)S(1)} %fusion.72), kind=kOutput, calls=%fused_computation.61 | convolution fusion | flops 406519808 | bytes 1975296 | tf_op jit(solution)/shard_map/dot_general | solution.py:83
  4.9 0.1 pad_maximum_fusion.3
  5.0 0.1 constant_dynamic-slice_fusion
  5.1 5.8 %collective-permute-done.3 = bf16[512,384]{1,0:T(8,128)(2,1)S(1)} collective-permute-done((bf16[512,384]{1,0:T(8,128)(2,1)}, bf16[512,384]{1,0:T(8,128)(2,1)S(1)}, u32[]{:S(2)}, u32[]{:S(2)}) %collective-permute-start.3) | collective-permute-done | bytes 393248 | tf_op jit(solution)/shard_map/ppermute | solution.py:88
  11.0 1.5 %pad_maximum_fusion = bf16[2688,384]{1,0:T(8,128)(2,1)} fusion(bf16[512,384]{1,0:T(8,128)(2,1)S(1)} %collective-permute-done.3, bf16[1152,384]{1,0:T(8,128)(2,1)S(1)} %bitcast.163, bf16[1024,384]{1,0:T(8,128)(2,1)S(1)} %bitcast.165), kind=kLoop, calls=%fused_computation.2 | loop fusion | flops 6193152 | bytes 4128768 | tf_op jit(solution)/shard_map/concatenate | solution.py:97
  12.5 0.1 fusion.47
  12.6 4.7 %collective-permute-start = (bf16[2,256,384]{2,1,0:T(8,128)(2,1)S(1)}, bf16[2,256,384]{2,1,0:T(8,128)(2,1)S(1)}, u32[]{:S(2)}, u32[]{:S(2)}) collective-permute-start(bf16[2,256,384]{2,1,0:T(8,128)(2,1)S(1)} %get-tuple-element.22), channel_id=1, source_target_pairs={{0,4},{4,8},{8,12},{1,5},{5,9},{9,13},{2,6},{6,10},{10,14},{3,7},{... | collective-permute-start | bytes 1179656 | tf_op jit(solution)/shard_map/ppermute | solution.py:12
  17.3 1.3 %collective-permute-start.1 = (bf16[2,256,384]{2,1,0:T(8,128)(2,1)S(1)}, bf16[2,256,384]{2,1,0:T(8,128)(2,1)S(1)}, u32[]{:S(2)}, u32[]{:S(2)}) collective-permute-start(bf16[2,256,384]{2,1,0:T(8,128)(2,1)S(1)} %get-tuple-element.23), channel_id=1, source_target_pairs={{4,0},{8,4},{12,8},{5,1},{9,5},{13,9},{6,2},{10,6},{14,10},{7,3},{... | collective-permute-start | bytes 1179656 | tf_op jit(solution)/shard_map/ppermute | solution.py:12
  18.6 7.7 %collective-permute-done = bf16[2,256,384]{2,1,0:T(8,128)(2,1)S(1)} collective-permute-done((bf16[2,256,384]{2,1,0:T(8,128)(2,1)S(1)}, bf16[2,256,384]{2,1,0:T(8,128)(2,1)S(1)}, u32[]{:S(2)}, u32[]{:S(2)}) %collective-permute-start) | collective-permute-done | bytes 393248 | tf_op jit(solution)/shard_map/ppermute | solution.py:12
  26.3 4.1 %collective-permute-done.1 = bf16[2,256,384]{2,1,0:T(8,128)(2,1)S(1)} collective-permute-done((bf16[2,256,384]{2,1,0:T(8,128)(2,1)S(1)}, bf16[2,256,384]{2,1,0:T(8,128)(2,1)S(1)}, u32[]{:S(2)}, u32[]{:S(2)}) %collective-permute-start.1) | collective-permute-done | bytes 393248 | tf_op jit(solution)/shard_map/ppermute | solution.py:12
  30.4 1.0 pad_maximum_fusion.4
  31.4 2.6 %collective-permute-done.2 = bf16[2,2,256,384]{3,2,1,0:T(8,128)(2,1)} collective-permute-done((bf16[2,2,256,384]{3,2,1,0:T(8,128)(2,1)}, bf16[2,2,256,384]{3,2,1,0:T(8,128)(2,1)}, u32[]{:S(2)}, u32[]{:S(2)}) %collective-permute-start.2) | collective-permute-done | bytes 786464 | tf_op jit(solution)/shard_map/ppermute | solution.py:104
  34.0 1.2 %slice_bitcast_fusion.2 = (bf16[2,256,384]{2,1,0:T(8,128)(2,1)S(1)}, bf16[2,256,384]{2,1,0:T(8,128)(2,1)S(1)}) fusion(bf16[2,2,256,384]{3,2,1,0:T(8,128)(2,1)} %collective-permute-done.2), kind=kLoop, calls=%fused_computation.86 | loop fusion | bytes 1572864 | tf_op jit(solution)/shard_map/squeeze | solution.py:106
  35.2 1.3 %slice_select_fusion = (bf16[512,384]{1,0:T(8,128)(2,1)S(1)}, bf16[512,1,384]{2,0,1:T(8,128)(2,1)S(1)}, bf16[512,1,384]{2,0,1:T(8,128)(2,1)S(1)}) fusion(bf16[512,384]{1,0:T(8,128)(2,1)S(1)} %copy-done.5, bf16[2688,384]{1,0:T(8,128)(2,1)} %collective-permute-done.4, pred[]{:T(512)S(6)} %eq.16), kind=kLoop, calls=%fused_computation.71 | loop fusion | flops 196608 | bytes 2752513 | tf_op jit(solution)/shard_map/jit(_where)/select_n | solution.py:101
  36.6 3.5 %collective-permute-start.7 = (bf16[256,384]{1,0:T(8,128)(2,1)S(1)}, bf16[256,384]{1,0:T(8,128)(2,1)S(1)}, u32[]{:S(2)}, u32[]{:S(2)}) collective-permute-start(bf16[256,384]{1,0:T(8,128)(2,1)S(1)} %get-tuple-element.27), channel_id=1, source_target_pairs={{0,4},{4,8},{8,12},{1,5},{5,9},{9,13},{2,6},{6,10},{10,14},{3,7},{... | collective-permute-start | bytes 589832 | tf_op jit(solution)/shard_map/ppermute | solution.py:12
  40.1 1.3 %collective-permute-start.6 = (bf16[256,384]{1,0:T(8,128)(2,1)S(1)}, bf16[256,384]{1,0:T(8,128)(2,1)S(1)}, u32[]{:S(2)}, u32[]{:S(2)}) collective-permute-start(bf16[256,384]{1,0:T(8,128)(2,1)S(1)} %get-tuple-element.28), channel_id=1, source_target_pairs={{4,0},{8,4},{12,8},{5,1},{9,5},{13,9},{6,2},{10,6},{14,10},{7,3},{... | collective-permute-start | bytes 589832 | tf_op jit(solution)/shard_map/ppermute | solution.py:12
  41.4 1.2 %fusion.52 = (bf16[512,1,384]{2,0,1:T(8,128)(2,1)S(1)}, bf16[512,1,384]{2,0,1:T(8,128)(2,1)S(1)}, bf16[512,1,384]{2,0,1:T(8,128)(2,1)S(1)}, bf16[512,1,384]{2,0,1:T(8,128)(2,1)S(1)}, bf16[1,512,384]{2,1,0:T(8,128)(2,1)S(1)}) fusion(bf16[2,256,384]{2,1,0:T(8,128)(2,1)S(1)} %collective-permute-done.1, bf16[1,512,384]{2,1,0:T(8,128)(2,1)S(1)} %copy-done.1, ...), kind=kLoop, calls=%fused_computation.80 | loop fusion | flops 4915200 | bytes 3932161 | tf_op jit(solution)/shard_map/stack | solution.py:21
  42.6 0.4 collective-permute-done.5
  43.0 1.4 %fusion.87 = f32[384,384]{1,0:T(8,128)S(1)} fusion(bf16[512,384]{1,0:T(8,128)(2,1)} %collective-permute-done.5, bf16[512,384]{1,0:T(8,128)(2,1)S(1)} %get-tuple-element.3), kind=kOutput, calls=%fused_computation.143 | convolution fusion | flops 150994944 | bytes 1376256 | tf_op jit(solution)/shard_map/dot_general | solution.py:145
  44.4 0.4 convolution_add_fusion
  44.9 2.3 %collective-permute-start.12 = (f32[2,96,384]{2,1,0:T(8,128)S(1)}, f32[2,96,384]{2,1,0:T(8,128)S(1)}, u32[]{:S(2)}, u32[]{:S(2)}) collective-permute-start(f32[2,96,384]{2,1,0:T(8,128)S(1)} %select_bitcast_fusion.1), channel_id=1, source_target_pairs={{0,4},{4,0},{8,12},{12,8},{1,5},{5,1},{9,13},{13,9},{2,6},{6,2},{1... | collective-permute-start | bytes 884744 | tf_op jit(solution)/shard_map/ppermute | solution.py:58
  47.2 1.2 %slice.188 = bf16[1024,384]{1,0:T(8,128)(2,1)S(1)} slice(bf16[2688,384]{1,0:T(8,128)(2,1)} %collective-permute-done.4), slice={[0:1024], [0:384]} | slice | bytes 1572864 | tf_op jit(solution)/shard_map/slice | solution.py:98
  48.4 0.2 fusion.50
  48.6 1.0 copy-done.3
  49.6 0.8 convolution_bitcast_fusion
  50.4 1.4 %fusion.53 = f32[384,384]{1,0:T(8,128)S(1)} fusion(bf16[512,384]{1,0:T(8,128)(2,1)} %collective-permute-done.5, bf16[256,384]{1,0:T(8,128)(2,1)S(1)} %collective-permute-done.6, bf16[256,384]{1,0:T(8,128)(2,1)S(1)} %get-tuple-element.27), kind=kOutput, calls=%fused_computation.89 | convolution fusion | flops 151781376 | bytes 1376256 | tf_op jit(solution)/shard_map/dot_general | solution.py:145
  51.8 1.4 %fusion.57 = f32[384,384]{1,0:T(8,128)S(1)} fusion(bf16[512,384]{1,0:T(8,128)(2,1)} %collective-permute-done.5, bf16[256,384]{1,0:T(8,128)(2,1)S(1)} %get-tuple-element.28, bf16[256,384]{1,0:T(8,128)(2,1)S(1)} %collective-permute-done.7), kind=kOutput, calls=%fused_computation.93 | convolution fusion | flops 151781376 | bytes 1376256 | tf_op jit(solution)/shard_map/dot_general | solution.py:145
  53.2 0.4 convolution_add_fusion.1
  53.6 0.4 convolution_add_fusion.2
  54.3 1.0 copy-done.6
  55.3 1.3 %fusion.39 = bf16[512,384]{1,0:T(8,128)(2,1)S(1)} fusion(f32[512,384]{1,0:T(8,128)S(1)} %copy-done.6, f32[512,384]{1,0:T(8,128)S(1)} %convolution_bitcast_fusion, bf16[512,1,384]{2,0,1:T(8,128)(2,1)S(1)} %get-tuple-element.17, bf16[512,1,384]{2,0,1:T(8,128)(2,1)S(1)} %bitcast.158, bf16[512,1,384]{2,0,1:T(8,128)(2,1)S(1)} %get-tuple-element.8, ...), kind=kOutput, calls=%fused_computation.58 | convolution fusion | flops 458883072 | bytes 4423684 | tf_op jit(solution)/shard_map/tko,kio->ti/dot_general | solution.py:117
  56.6 1.3 %slice.191 = bf16[1152,384]{1,0:T(8,128)(2,1)S(1)} slice(bf16[2688,384]{1,0:T(8,128)(2,1)} %collective-permute-done.4), slice={[1024:2176], [0:384]} | slice | bytes 1769472 | tf_op jit(solution)/shard_map/slice | solution.py:99
  57.9 2.1 %collective-permute-start.13 = (f32[96,384]{1,0:T(8,128)S(1)}, f32[96,384]{1,0:T(8,128)S(1)}, u32[]{:S(2)}, u32[]{:S(2)}) collective-permute-start(f32[96,384]{1,0:T(8,128)S(1)} %select_bitcast_fusion.7), channel_id=1, source_target_pairs={{0,8},{8,0},{4,12},{12,4},{1,9},{9,1},{5,13},{13,5},{2,10},{10,2},... | collective-permute-start | bytes 442376 | tf_op jit(solution)/shard_map/ppermute | solution.py:63
  60.0 11.9 %collective-permute-done.8 = f32[2,192,384]{2,1,0:T(8,128)S(1)} collective-permute-done((f32[2,192,384]{2,1,0:T(8,128)S(1)}, f32[2,192,384]{2,1,0:T(8,128)S(1)}, u32[]{:S(2)}, u32[]{:S(2)}) %collective-permute-start.8) | collective-permute-done | bytes 589856 | tf_op jit(solution)/shard_map/ppermute | solution.py:58
  72.1 0.6 collective-permute-start.9
  72.7 2.4 %collective-permute-start.14 = (bf16[96,384]{1,0:T(8,128)(2,1)S(1)}, bf16[96,384]{1,0:T(8,128)(2,1)S(1)}, u32[]{:S(2)}, u32[]{:S(2)}) collective-permute-start(bf16[96,384]{1,0:T(8,128)(2,1)S(1)} %fusion.69), channel_id=1, source_target_pairs={{0,8},{8,0},{4,12},{12,4},{1,9},{9,1},{5,13},{13,5},{2,10},{10,2},... | collective-permute-start | bytes 221192 | tf_op jit(solution)/shard_map/ppermute | solution.py:64
  75.2 0.8 convolution_bitcast_fusion.3
  76.0 13.7 %collective-permute-done.14 = bf16[96,384]{1,0:T(8,128)(2,1)S(1)} collective-permute-done((bf16[96,384]{1,0:T(8,128)(2,1)S(1)}, bf16[96,384]{1,0:T(8,128)(2,1)S(1)}, u32[]{:S(2)}, u32[]{:S(2)}) %collective-permute-start.14) | collective-permute-done | bytes 73760 | tf_op jit(solution)/shard_map/ppermute | solution.py:64
  89.9 2.2 %collective-permute-start.10 = (bf16[192,384]{1,0:T(8,128)(2,1)S(1)}, bf16[192,384]{1,0:T(8,128)(2,1)S(1)}, u32[]{:S(2)}, u32[]{:S(2)}) collective-permute-start(bf16[192,384]{1,0:T(8,128)(2,1)S(1)} %fusion.68), channel_id=1, source_target_pairs={{0,8},{8,0},{4,12},{12,4},{1,9},{9,1},{5,13},{13,5},{2,10},{10,2},... | collective-permute-start | bytes 442376 | tf_op jit(solution)/shard_map/ppermute | solution.py:64
  92.1 1.6 %fusion.4 = bf16[1,512,384]{2,1,0:T(8,128)(2,1)} fusion(f32[512,384]{1,0:T(8,128)S(1)} %copy-done.6, f32[512,384]{1,0:T(8,128)S(1)} %convolution_bitcast_fusion.3, bf16[3,384,384]{2,1,0:T(8,128)(2,1)S(1)} %bitcast.171, bf16[512,1,384]{2,0,1:T(8,128)(2,1)S(1)} %get-tuple-element.13, bf16[512,1,384]{2,0,1:T(8,128)(2,1)S(1)} %get-tuple-element.5, ...), kind=kOutput, calls=%fused_computation.15 | convolution fusion | flops 454754304 | bytes 4030464 | tf_op jit(solution)/shard_map/tki,kio->to/dot_general | solution.py:111
  93.7 0.4 broadcast_in_dim.18
  94.1 1.2 %convert_element_type.54 = bf16[1,1024,384]{2,1,0:T(8,128)(2,1)} reshape(bf16[512,2,384]{2,1,0:T(2,128)(2,1)S(1)} %broadcast_in_dim.18) | data formatting | bytes 1572864 | tf_op jit(solution)/shard_map/convert_element_type | solution.py:126
  95.3 4.5 %collective-permute-done.10 = bf16[192,384]{1,0:T(8,128)(2,1)S(1)} collective-permute-done((bf16[192,384]{1,0:T(8,128)(2,1)S(1)}, bf16[192,384]{1,0:T(8,128)(2,1)S(1)}, u32[]{:S(2)}, u32[]{:S(2)}) %collective-permute-start.10) | collective-permute-done | bytes 147488 | tf_op jit(solution)/shard_map/ppermute | solution.py:64
  100.1 7.9 %collective-permute-done.11 = bf16[2,192,384]{2,1,0:T(8,128)(2,1)S(1)} collective-permute-done((bf16[2,192,384]{2,1,0:T(8,128)(2,1)S(1)}, bf16[2,192,384]{2,1,0:T(8,128)(2,1)S(1)}, u32[]{:S(2)}, u32[]{:S(2)}) %collective-permute-start.11) | collective-permute-done | bytes 294944 | tf_op jit(solution)/shard_map/ppermute | solution.py:66
  108.0 0.1 select_bitcast_fusion.3
  108.1 0.1 maximum_convert_fusion
  108.3 1.3 %pad_maximum_fusion.1 = f32[3,384,384]{2,1,0:T(8,128)} fusion(f32[1,384,384]{2,1,0:T(8,128)S(1)} %bitcast.168, f32[1,384,384]{2,1,0:T(8,128)S(1)} %bitcast.166, f32[1,384,384]{2,1,0:T(8,128)S(1)} %bitcast.167), kind=kLoop, calls=%fused_computation.3 | loop fusion | flops 884736 | bytes 3538944 | tf_op jit(solution)/shard_map/stack | solution.py:149
  (43 shorter events, 1.0 us)
Async XLA Ops:
  0.6 4.4 %copy-start = (bf16[3,384,768]{2,1,0:T(8,128)(2,1)S(1)}, bf16[3,384,768]{2,1,0:T(8,128)(2,1)}, u32[]{:S(2)}) copy-start(bf16[3,384,768]{2,1,0:T(8,128)(2,1)} %param.4) | copy-start | bytes 5308420
  0.6 10.3 %collective-permute-start.3 = (bf16[512,384]{1,0:T(8,128)(2,1)}, bf16[512,384]{1,0:T(8,128)(2,1)S(1)}, u32[]{:S(2)}, u32[]{:S(2)}) collective-permute-start(bf16[512,384]{1,0:T(8,128)(2,1)} %bitcast.157), channel_id=1, source_target_pairs={{2,0},{1,3},{6,4},{5,7},{10,8},{9,11},{14,12},{13,15},{18,16},{17,... | collective-permute-start | bytes 1179656 | tf_op jit(solution)/shard_map/ppermute | solution.py:88
  2.1 2.8 %copy-start.1 = (bf16[1,512,384]{2,1,0:T(8,128)(2,1)S(1)}, bf16[1,512,384]{2,1,0:T(8,128)(2,1)}, u32[]{:S(2)}) copy-start(bf16[1,512,384]{2,1,0:T(8,128)(2,1)} %param.5) | copy-start | bytes 1179652
  5.1 7.4 %copy-start.2 = (bf16[3,384,384]{2,1,0:T(8,128)(2,1)}, bf16[3,384,384]{2,1,0:T(8,128)(2,1)S(1)}, u32[]{:S(2)}) copy-start(bf16[3,384,384]{2,1,0:T(8,128)(2,1)S(1)} %constant_dynamic-slice_fusion) | copy-start | bytes 2654212
  11.0 1.5 %copy-start.4 = (bf16[512,384]{1,0:T(8,128)(2,1)}, bf16[512,384]{1,0:T(8,128)(2,1)S(1)}, u32[]{:S(2)}) copy-start(bf16[512,384]{1,0:T(8,128)(2,1)S(1)} %collective-permute-done.3) | copy-start | bytes 1179652
  12.5 22.7 %collective-permute-start.4 = (bf16[2688,384]{1,0:T(8,128)(2,1)}, bf16[2688,384]{1,0:T(8,128)(2,1)}, u32[]{:S(2)}, u32[]{:S(2)}) collective-permute-start(bf16[2688,384]{1,0:T(8,128)(2,1)} %pad_maximum_fusion), channel_id=1, source_target_pairs={{0,1},{1,0},{2,3},{3,2},{4,5},{5,4},{6,7},{7,6},{8,9},{9,8},{10,11... | collective-permute-start | bytes 6193160 | tf_op jit(solution)/shard_map/ppermute | solution.py:97
  12.6 13.7 %collective-permute-start = (bf16[2,256,384]{2,1,0:T(8,128)(2,1)S(1)}, bf16[2,256,384]{2,1,0:T(8,128)(2,1)S(1)}, u32[]{:S(2)}, u32[]{:S(2)}) collective-permute-start(bf16[2,256,384]{2,1,0:T(8,128)(2,1)S(1)} %get-tuple-element.22), channel_id=1, source_target_pairs={{0,4},{4,8},{8,12},{1,5},{5,9},{9,13},{2,6},{6,10},{10,14},{3,7},{... | collective-permute-start | bytes 1179656 | tf_op jit(solution)/shard_map/ppermute | solution.py:12
  17.3 13.1 %collective-permute-start.1 = (bf16[2,256,384]{2,1,0:T(8,128)(2,1)S(1)}, bf16[2,256,384]{2,1,0:T(8,128)(2,1)S(1)}, u32[]{:S(2)}, u32[]{:S(2)}) collective-permute-start(bf16[2,256,384]{2,1,0:T(8,128)(2,1)S(1)} %get-tuple-element.23), channel_id=1, source_target_pairs={{4,0},{8,4},{12,8},{5,1},{9,5},{13,9},{6,2},{10,6},{14,10},{7,3},{... | collective-permute-start | bytes 1179656 | tf_op jit(solution)/shard_map/ppermute | solution.py:12
  31.4 2.6 %collective-permute-start.2 = (bf16[2,2,256,384]{3,2,1,0:T(8,128)(2,1)}, bf16[2,2,256,384]{3,2,1,0:T(8,128)(2,1)}, u32[]{:S(2)}, u32[]{:S(2)}) collective-permute-start(bf16[2,2,256,384]{3,2,1,0:T(8,128)(2,1)} %pad_maximum_fusion.4), channel_id=1, source_target_pairs={{0,1},{1,0},{2,3},{3,2},{4,5},{5,4},{6,7},{7,6},{8,9},{9,8},{10,11... | collective-permute-start | bytes 2359304 | tf_op jit(solution)/shard_map/ppermute | solution.py:104
  31.4 11.6 %collective-permute-start.5 = (bf16[512,384]{1,0:T(8,128)(2,1)S(1)}, bf16[512,384]{1,0:T(8,128)(2,1)}, u32[]{:S(2)}, u32[]{:S(2)}) collective-permute-start(bf16[512,384]{1,0:T(8,128)(2,1)S(1)} %get-tuple-element.31), channel_id=1, source_target_pairs={{0,2},{2,0},{1,3},{3,1},{4,6},{6,4},{5,7},{7,5},{8,10},{10,8},{9,1... | collective-permute-start | bytes 1179656 | tf_op jit(solution)/shard_map/ppermute | solution.py:89
  31.4 3.8 %copy-start.5 = (bf16[512,384]{1,0:T(8,128)(2,1)S(1)}, bf16[512,384]{1,0:T(8,128)(2,1)}, u32[]{:S(2)}) copy-start(bf16[512,384]{1,0:T(8,128)(2,1)} %copy-done.4) | copy-start | bytes 1179652
  36.6 15.2 %collective-permute-start.7 = (bf16[256,384]{1,0:T(8,128)(2,1)S(1)}, bf16[256,384]{1,0:T(8,128)(2,1)S(1)}, u32[]{:S(2)}, u32[]{:S(2)}) collective-permute-start(bf16[256,384]{1,0:T(8,128)(2,1)S(1)} %get-tuple-element.27), channel_id=1, source_target_pairs={{0,4},{4,8},{8,12},{1,5},{5,9},{9,13},{2,6},{6,10},{10,14},{3,7},{... | collective-permute-start | bytes 589832 | tf_op jit(solution)/shard_map/ppermute | solution.py:12
  40.1 10.3 %collective-permute-start.6 = (bf16[256,384]{1,0:T(8,128)(2,1)S(1)}, bf16[256,384]{1,0:T(8,128)(2,1)S(1)}, u32[]{:S(2)}, u32[]{:S(2)}) collective-permute-start(bf16[256,384]{1,0:T(8,128)(2,1)S(1)} %get-tuple-element.28), channel_id=1, source_target_pairs={{4,0},{8,4},{12,8},{5,1},{9,5},{13,9},{6,2},{10,6},{14,10},{7,3},{... | collective-permute-start | bytes 589832 | tf_op jit(solution)/shard_map/ppermute | solution.py:12
  44.9 13.0 %collective-permute-start.12 = (f32[2,96,384]{2,1,0:T(8,128)S(1)}, f32[2,96,384]{2,1,0:T(8,128)S(1)}, u32[]{:S(2)}, u32[]{:S(2)}) collective-permute-start(f32[2,96,384]{2,1,0:T(8,128)S(1)} %select_bitcast_fusion.1), channel_id=1, source_target_pairs={{0,4},{4,0},{8,12},{12,8},{1,5},{5,1},{9,13},{13,9},{2,6},{6,2},{1... | collective-permute-start | bytes 884744 | tf_op jit(solution)/shard_map/ppermute | solution.py:58
  48.4 1.2 %copy-start.3 = (bf16[3,384,384]{2,1,0:T(8,128)(2,1)S(1)}, bf16[3,384,384]{2,1,0:T(8,128)(2,1)}, u32[]{:S(2)}) copy-start(bf16[3,384,384]{2,1,0:T(8,128)(2,1)} %copy-done.2) | copy-start | bytes 2654212
  54.1 1.1 %copy-start.6 = (f32[512,384]{1,0:T(8,128)S(1)}, f32[512,384]{1,0:T(8,128)}, u32[]{:S(2)}) copy-start(f32[512,384]{1,0:T(8,128)} %get-tuple-element.32) | copy-start | bytes 2359300
  54.2 17.8 %collective-permute-start.8 = (f32[2,192,384]{2,1,0:T(8,128)S(1)}, f32[2,192,384]{2,1,0:T(8,128)S(1)}, u32[]{:S(2)}, u32[]{:S(2)}) collective-permute-start(f32[2,192,384]{2,1,0:T(8,128)S(1)} %select_bitcast_fusion), channel_id=1, source_target_pairs={{0,4},{4,0},{8,12},{12,8},{1,5},{5,1},{9,13},{13,9},{2,6},{6,2},{1... | collective-permute-start | bytes 1769480 | tf_op jit(solution)/shard_map/ppermute | solution.py:58
  57.9 14.8 %collective-permute-start.13 = (f32[96,384]{1,0:T(8,128)S(1)}, f32[96,384]{1,0:T(8,128)S(1)}, u32[]{:S(2)}, u32[]{:S(2)}) collective-permute-start(f32[96,384]{1,0:T(8,128)S(1)} %select_bitcast_fusion.7), channel_id=1, source_target_pairs={{0,8},{8,0},{4,12},{12,4},{1,9},{9,1},{5,13},{13,5},{2,10},{10,2},... | collective-permute-start | bytes 442376 | tf_op jit(solution)/shard_map/ppermute | solution.py:63
  72.1 17.7 %collective-permute-start.9 = (f32[192,384]{1,0:T(8,128)S(1)}, f32[192,384]{1,0:T(8,128)S(1)}, u32[]{:S(2)}, u32[]{:S(2)}) collective-permute-start(f32[192,384]{1,0:T(8,128)S(1)} %select_bitcast_fusion.4), channel_id=1, source_target_pairs={{0,8},{8,0},{4,12},{12,4},{1,9},{9,1},{5,13},{13,5},{2,10},{10,2},... | collective-permute-start | bytes 884744 | tf_op jit(solution)/shard_map/ppermute | solution.py:63
  72.7 17.0 %collective-permute-start.14 = (bf16[96,384]{1,0:T(8,128)(2,1)S(1)}, bf16[96,384]{1,0:T(8,128)(2,1)S(1)}, u32[]{:S(2)}, u32[]{:S(2)}) collective-permute-start(bf16[96,384]{1,0:T(8,128)(2,1)S(1)} %fusion.69), channel_id=1, source_target_pairs={{0,8},{8,0},{4,12},{12,4},{1,9},{9,1},{5,13},{13,5},{2,10},{10,2},... | collective-permute-start | bytes 221192 | tf_op jit(solution)/shard_map/ppermute | solution.py:64
  89.7 10.2 %collective-permute-start.15 = (bf16[2,96,384]{2,1,0:T(8,128)(2,1)S(1)}, bf16[2,96,384]{2,1,0:T(8,128)(2,1)S(1)}, u32[]{:S(2)}, u32[]{:S(2)}) collective-permute-start(bf16[2,96,384]{2,1,0:T(8,128)(2,1)S(1)} %maximum_select_fusion.1), channel_id=1, source_target_pairs={{0,4},{4,0},{8,12},{12,8},{1,5},{5,1},{9,13},{13,9},{2,6},{6,2},{1... | collective-permute-start | bytes 442376 | tf_op jit(solution)/shard_map/ppermute | solution.py:66
  89.9 9.9 %collective-permute-start.10 = (bf16[192,384]{1,0:T(8,128)(2,1)S(1)}, bf16[192,384]{1,0:T(8,128)(2,1)S(1)}, u32[]{:S(2)}, u32[]{:S(2)}) collective-permute-start(bf16[192,384]{1,0:T(8,128)(2,1)S(1)} %fusion.68), channel_id=1, source_target_pairs={{0,8},{8,0},{4,12},{12,4},{1,9},{9,1},{5,13},{13,5},{2,10},{10,2},... | collective-permute-start | bytes 442376 | tf_op jit(solution)/shard_map/ppermute | solution.py:64
  99.9 8.1 %collective-permute-start.11 = (bf16[2,192,384]{2,1,0:T(8,128)(2,1)S(1)}, bf16[2,192,384]{2,1,0:T(8,128)(2,1)S(1)}, u32[]{:S(2)}, u32[]{:S(2)}) collective-permute-start(bf16[2,192,384]{2,1,0:T(8,128)(2,1)S(1)} %maximum_select_fusion), channel_id=1, source_target_pairs={{0,4},{4,0},{8,12},{12,8},{1,5},{5,1},{9,13},{13,9},{2,6},{6,2},{1... | collective-permute-start | bytes 884744 | tf_op jit(solution)/shard_map/ppermute | solution.py:66

commit v19 on v11

--- a/solution.py
+++ b/solution.py
@@ -61,12 +61,11 @@
     keep = jnp.where(low, pair[0], pair[1])
     give = jnp.where(low, pair[1], pair[0])
     total = (keep + lax.ppermute(give, "seq", across)).astype(jnp.bfloat16)
-    other = lax.ppermute(total, "seq", across)
-    own_set = jnp.where(low, jnp.stack([total, other]), jnp.stack([other, total]))
-    far_set = lax.ppermute(own_set, "seq", pairs)
-    evens = jnp.where(odd, far_set, own_set)
-    odds = jnp.where(odd, own_set, far_set)
-    return jnp.stack([evens, odds], 1).reshape(block.shape).astype(jnp.float32)
+    gathered = [total] + [
+        lax.ppermute(total, "seq", [(j, (j + d) % 4) for j in range(4)]) for d in range(1, 4)
+    ]
+    order = (s - jnp.arange(4)) % 4
+    return jnp.take(jnp.stack(gathered), order, axis=0).reshape(block.shape).astype(jnp.float32)
 
 
 def shards(seq_in, conv_weight, cotangent):

time: 103 us -> 105 us (1.019); the launches traced: 102 us -> 103 us
  waiting for transfers between devices: 42.3 us -> 36.4 us
  starting transfers between devices: 31.2 us -> 35 us
  other arithmetic: 9.42 us -> 11.3 us
  local copies, waits for them, and re-layouts: 6.93 us -> 8.21 us
    ppermute x2, waiting for transfers between devices: 0.01 us -> 12.7 us  [line_total(): total = (keep + lax.ppermute(give, 'seq', across)).astype(jnp.bfloat16)]
    ppermute x2, waiting for transfers between devices: 10.9 us -> 1.52 us  [line_total(): lax.ppermute(jnp.where(odd, even_set, odd_set), 'seq', pairs)]
    ppermute x4 -> x6, waiting for transfers between devices: 23 us -> 14 us  [line_total(): lax.ppermute(total, 'seq', [(j, (j + d) % 4) for j in range(4)])]
    ppermute x4 -> x6, starting transfers between devices: 6.24 us -> 10.2 us  [line_total(): lax.ppermute(total, 'seq', [(j, (j + d) % 4) for j in range(4)])]
    gather x0 -> x2, local copies, waits for them, and re-layouts: none -> 1.29 us  [line_total(): jnp.take(jnp.stack(gathered), order, axis=0).reshape(block.shape)]
  transfers between devices with their start and end apart: 17 -> 19, of which waited for: 7 -> 9; matrix products, arithmetic and copies ran while one was open for 22% -> 25% of each run, Pallas kernels for 0% -> 0%
where the time goes in v19:
time: 105 us; the launch traced here: 103 us
  waiting for transfers between devices  36.4 us (35%)
  starting transfers between devices  35 us (33%)
  matrix products  11.5 us (11%)
  other arithmetic  11.3 us (11%)
  local copies, waits for them, and re-layouts  8.21 us (8%)
    ppermute x6, waiting for transfers between devices, line_total(): lax.ppermute(total, 'seq', [(j, (j + d) % 4) for j in range(4)])  14 us
    ppermute x2, waiting for transfers between devices, line_total(): total = (keep + lax.ppermute(give, 'seq', across)).astype(jnp.bfloat16)  12.7 us
    ppermute x4, starting transfers between devices, shift_from(): return lax.ppermute(block, axis, route)  11 us
    ppermute x6, starting transfers between devices, line_total(): lax.ppermute(total, 'seq', [(j, (j + d) % 4) for j in range(4)])  10.2 us
    ppermute x4, waiting for transfers between devices, shift_from(): return lax.ppermute(block, axis, route)  8.15 us
    ppermute x1, starting transfers between devices, shards(): lax.ppermute(jnp.concatenate([both.reshape(-1, width), w_other.reshape(-1...  3.71 us
    dot_general x3, matrix products, shards(): jnp.dot(own_taps[:, k].T, cot_mine, preferred_element_type=jnp.float32)  3.05 us
    ppermute x1, starting transfers between devices, shards(): par_halo = lax.ppermute(jnp.stack([from_prev, from_next]), 'chan', SWAP)  2.82 us
  transfers between devices with their start and end apart: 19, of which 9 were waited for; matrix products, arithmetic and copies ran while one was open for 25% of the time, Pallas kernels for 0%

profile of v19, /device:TPU:0, one launch (start us, length us, event | category | flops | bytes accessed | tf_op | source)
XLA Modules:
  0.0 103.4 jit_solution(7085171074580550502)
XLA Ops:
  0.6 1.4 %collective-permute-start.5 = (bf16[512,384]{1,0:T(8,128)(2,1)}, bf16[512,384]{1,0:T(8,128)(2,1)}, u32[]{:S(2)}, u32[]{:S(2)}) collective-permute-start(bf16[512,384]{1,0:T(8,128)(2,1)} %bitcast.165), channel_id=1, source_target_pairs={{2,0},{1,3},{6,4},{5,7},{10,8},{9,11},{14,12},{13,15},{18,16},{17,... | collective-permute-start | bytes 1179656 | tf_op jit(solution)/shard_map/ppermute | solution.py:87
  2.1 1.4 %collective-permute-start.6 = (bf16[512,384]{1,0:T(8,128)(2,1)}, bf16[512,384]{1,0:T(8,128)(2,1)}, u32[]{:S(2)}, u32[]{:S(2)}) collective-permute-start(bf16[512,384]{1,0:T(8,128)(2,1)} %bitcast.166), channel_id=1, source_target_pairs={{2,1},{1,2},{6,5},{5,6},{10,9},{9,10},{14,13},{13,14},{18,17},{17,... | collective-permute-start | bytes 1179656 | tf_op jit(solution)/shard_map/ppermute | solution.py:88
  3.5 2.8 %multiply_convert_fusion = (bf16[512,384]{1,0:T(8,128)(2,1)S(1)}, f32[512,384]{1,0:T(8,128)}) fusion(bf16[1,1024,384]{2,1,0:T(8,128)(2,1)} %param.3, s32[1024]{0:T(1024)S(1)} %get-tuple-element.28, s32[1024]{0:T(1024)S(1)} %get-tuple-element.29, pred[1024]{0:T(1024)(128)(4,1)S(1)} %fusion.74), kind=kOutput, calls=%fused_computation.63 | convolution fusion | flops 406519808 | bytes 1975296 | tf_op jit(solution)/shard_map/dot_general | solution.py:82
  6.3 1.0 fusion.48
  7.3 5.7 %collective-permute-start = (bf16[2,256,384]{2,1,0:T(8,128)(2,1)}, bf16[2,256,384]{2,1,0:T(8,128)(2,1)}, u32[]{:S(2)}, u32[]{:S(2)}) collective-permute-start(bf16[2,256,384]{2,1,0:T(8,128)(2,1)} %get-tuple-element.21), channel_id=1, source_target_pairs={{0,4},{4,8},{8,12},{1,5},{5,9},{9,13},{2,6},{6,10},{10,14},{3,7},{... | collective-permute-start | bytes 1179656 | tf_op jit(solution)/shard_map/ppermute | solution.py:12
  13.0 1.3 %collective-permute-start.1 = (bf16[2,256,384]{2,1,0:T(8,128)(2,1)}, bf16[2,256,384]{2,1,0:T(8,128)(2,1)}, u32[]{:S(2)}, u32[]{:S(2)}) collective-permute-start(bf16[2,256,384]{2,1,0:T(8,128)(2,1)} %get-tuple-element.22), channel_id=1, source_target_pairs={{4,0},{8,4},{12,8},{5,1},{9,5},{13,9},{6,2},{10,6},{14,10},{7,3},{... | collective-permute-start | bytes 1179656 | tf_op jit(solution)/shard_map/ppermute | solution.py:12
  14.3 1.0 pad_maximum_fusion.3
  15.4 1.0 %copy-done.2 = bf16[2,512,384]{2,1,0:T(8,128)(2,1)S(1)} copy-done((bf16[2,512,384]{2,1,0:T(8,128)(2,1)S(1)}, bf16[2,512,384]{2,1,0:T(8,128)(2,1)}, u32[]{:S(2)}) %copy-start.2) | copy-done | bytes 786456
  16.4 1.3 %pad_maximum_fusion.1 = bf16[2176,384]{1,0:T(8,128)(2,1)} fusion(bf16[1152,384]{1,0:T(8,128)(2,1)S(1)} %bitcast.170, bf16[1024,384]{1,0:T(8,128)(2,1)S(1)} %bitcast.171), kind=kLoop, calls=%fused_computation.5 | loop fusion | flops 3342336 | bytes 3342336 | tf_op jit(solution)/shard_map/concatenate | solution.py:96
  17.8 3.7 %collective-permute-start.3 = (bf16[2176,384]{1,0:T(8,128)(2,1)}, bf16[2176,384]{1,0:T(8,128)(2,1)}, u32[]{:S(2)}, u32[]{:S(2)}) collective-permute-start(bf16[2176,384]{1,0:T(8,128)(2,1)} %pad_maximum_fusion.1), channel_id=1, source_target_pairs={{0,1},{1,0},{2,3},{3,2},{4,5},{5,4},{6,7},{7,6},{8,9},{9,8},{10,11... | collective-permute-start | bytes 5013512 | tf_op jit(solution)/shard_map/ppermute | solution.py:95
  21.9 0.8 collective-permute-start.4
  22.7 1.8 %collective-permute-done.1 = bf16[2,256,384]{2,1,0:T(8,128)(2,1)} collective-permute-done((bf16[2,256,384]{2,1,0:T(8,128)(2,1)}, bf16[2,256,384]{2,1,0:T(8,128)(2,1)}, u32[]{:S(2)}, u32[]{:S(2)}) %collective-permute-start.1) | collective-permute-done | bytes 393248 | tf_op jit(solution)/shard_map/ppermute | solution.py:12
  24.5 1.2 %pad_maximum_fusion.4 = bf16[2,2,256,384]{3,2,1,0:T(8,128)(2,1)S(1)} fusion(bf16[1,2,256,384]{3,2,1,0:T(8,128)(2,1)} %bitcast.7, bf16[1,2,256,384]{3,2,1,0:T(8,128)(2,1)} %bitcast.6), kind=kLoop, calls=%fused_computation.61 | loop fusion | flops 393216 | bytes 1572864 | tf_op jit(solution)/shard_map/stack | solution.py:102
  25.7 2.8 %collective-permute-start.2 = (bf16[2,2,256,384]{3,2,1,0:T(8,128)(2,1)S(1)}, bf16[2,2,256,384]{3,2,1,0:T(8,128)(2,1)S(1)}, u32[]{:S(2)}, u32[]{:S(2)}) collective-permute-start(bf16[2,2,256,384]{3,2,1,0:T(8,128)(2,1)S(1)} %pad_maximum_fusion.4), channel_id=1, source_target_pairs={{0,1},{1,0},{2,3},{3,2},{4,5},{5,4},{6,7},{7,6},{8,9},{9,8},{10,11... | collective-permute-start | bytes 2359304 | tf_op jit(solution)/shard_map/ppermute | solution.py:102
  28.5 1.0 %broadcast_select_fusion = bf16[512,384]{1,0:T(8,128)(2,1)S(1)} fusion(bf16[512,384]{1,0:T(8,128)(2,1)} %collective-permute-done.5, bf16[512,384]{1,0:T(8,128)(2,1)} %collective-permute-done.6, pred[]{:T(512)S(6)} %eq.19), kind=kLoop, calls=%fused_computation.108 | loop fusion | flops 196608 | bytes 1179649 | tf_op jit(solution)/shard_map/jit(_where)/select_n | solution.py:89
  29.6 2.8 %collective-permute-start.8 = (bf16[256,384]{1,0:T(8,128)(2,1)S(1)}, bf16[256,384]{1,0:T(8,128)(2,1)S(1)}, u32[]{:S(2)}, u32[]{:S(2)}) collective-permute-start(bf16[256,384]{1,0:T(8,128)(2,1)S(1)} %get-tuple-element.24), channel_id=1, source_target_pairs={{0,4},{4,8},{8,12},{1,5},{5,9},{9,13},{2,6},{6,10},{10,14},{3,7},{... | collective-permute-start | bytes 589832 | tf_op jit(solution)/shard_map/ppermute | solution.py:12
  32.4 1.3 %collective-permute-start.7 = (bf16[256,384]{1,0:T(8,128)(2,1)S(1)}, bf16[256,384]{1,0:T(8,128)(2,1)S(1)}, u32[]{:S(2)}, u32[]{:S(2)}) collective-permute-start(bf16[256,384]{1,0:T(8,128)(2,1)S(1)} %get-tuple-element.25), channel_id=1, source_target_pairs={{4,0},{8,4},{12,8},{5,1},{9,5},{13,9},{6,2},{10,6},{14,10},{7,3},{... | collective-permute-start | bytes 589832 | tf_op jit(solution)/shard_map/ppermute | solution.py:12
  34.1 2.6 %collective-permute-done.8 = bf16[256,384]{1,0:T(8,128)(2,1)S(1)} collective-permute-done((bf16[256,384]{1,0:T(8,128)(2,1)S(1)}, bf16[256,384]{1,0:T(8,128)(2,1)S(1)}, u32[]{:S(2)}, u32[]{:S(2)}) %collective-permute-start.8) | collective-permute-done | bytes 196640 | tf_op jit(solution)/shard_map/ppermute | solution.py:12
  37.1 3.7 %collective-permute-done.7 = bf16[256,384]{1,0:T(8,128)(2,1)S(1)} collective-permute-done((bf16[256,384]{1,0:T(8,128)(2,1)S(1)}, bf16[256,384]{1,0:T(8,128)(2,1)S(1)}, u32[]{:S(2)}, u32[]{:S(2)}) %collective-permute-start.7) | collective-permute-done | bytes 196640 | tf_op jit(solution)/shard_map/ppermute | solution.py:12
  41.3 1.6 %fusion.53 = (bf16[512,1,384]{2,0,1:T(8,128)(2,1)S(1)}, bf16[512,1,384]{2,0,1:T(8,128)(2,1)S(1)}, bf16[512,1,384]{2,0,1:T(8,128)(2,1)S(1)}, bf16[512,1,384]{2,0,1:T(8,128)(2,1)S(1)}, bf16[1,512,384]{2,1,0:T(8,128)(2,1)S(1)}) fusion(bf16[2,256,384]{2,1,0:T(8,128)(2,1)} %collective-permute-done.1, bf16[1,512,384]{2,1,0:T(8,128)(2,1)S(1)} %copy-done.1, ...), kind=kLoop, calls=%fused_computation.85 | loop fusion | flops 4915200 | bytes 3932161 | tf_op jit(solution)/shard_map/stack | solution.py:21
  43.4 1.6 %collective-permute-start.14 = (f32[2,96,384]{2,1,0:T(8,128)S(1)}, f32[2,96,384]{2,1,0:T(8,128)S(1)}, u32[]{:S(2)}, u32[]{:S(2)}) collective-permute-start(f32[2,96,384]{2,1,0:T(8,128)S(1)} %select_bitcast_fusion.1), channel_id=1, source_target_pairs={{0,4},{4,0},{8,12},{12,8},{1,5},{5,1},{9,13},{13,9},{2,6},{6,2},{1... | collective-permute-start | bytes 884744 | tf_op jit(solution)/shard_map/ppermute | solution.py:58
  45.0 1.3 %convolution_add_fusion.1 = f32[384,384]{1,0:T(8,128)S(1)} fusion(f32[384,384]{1,0:T(8,128)S(1)} %fusion.58, bf16[1,512,384]{2,1,0:T(8,128)(2,1)S(1)} %get-tuple-element.23, bf16[2,256,384]{2,1,0:T(8,128)(2,1)} %collective-permute-done.1, bf16[1,512,384]{2,1,0:T(8,128)(2,1)S(1)} %copy-done.1, bf16[1,512,384]{2,1,0:T(8,128)(2,1)S(1)} %bitcast.160), kind=kOutput, calls=%fused_computation.15 | convolution fusion | flops 152322048 | bytes 2752512 | tf_op jit(solution)/shard_map/dot_general | solution.py:141
  46.3 1.3 %convolution_add_fusion.2 = f32[384,384]{1,0:T(8,128)S(1)} fusion(f32[384,384]{1,0:T(8,128)S(1)} %fusion.54, bf16[1,512,384]{2,1,0:T(8,128)(2,1)S(1)} %get-tuple-element.23, bf16[2,256,384]{2,1,0:T(8,128)(2,1)} %collective-permute-done, bf16[1,512,384]{2,1,0:T(8,128)(2,1)S(1)} %copy-done.1, bf16[1,512,384]{2,1,0:T(8,128)(2,1)S(1)} %bitcast.161), kind=kOutput, calls=%fused_computation.16 | convolution fusion | flops 152322048 | bytes 2752512 | tf_op jit(solution)/shard_map/dot_general | solution.py:141
  47.8 0.5 collective-permute-start.9
  48.3 1.2 %slice.186 = bf16[1024,384]{1,0:T(8,128)(2,1)S(1)} slice(bf16[2176,384]{1,0:T(8,128)(2,1)} %collective-permute-done.3), slice={[0:1024], [0:384]} | slice | bytes 1572864 | tf_op jit(solution)/shard_map/slice | solution.py:98
  49.6 1.2 %slice_bitcast_fusion.5 = (bf16[512,1,384]{2,0,1:T(8,128)(2,1)S(1)}, bf16[512,1,384]{2,0,1:T(8,128)(2,1)S(1)}) fusion(bf16[2176,384]{1,0:T(8,128)(2,1)} %collective-permute-done.3), kind=kLoop, calls=%fused_computation.109 | loop fusion | bytes 1572864 | tf_op jit(solution)/shard_map/stack | solution.py:21
  51.0 0.8 convolution_bitcast_fusion
  51.8 1.5 %collective-permute-done.14 = f32[2,96,384]{2,1,0:T(8,128)S(1)} collective-permute-done((f32[2,96,384]{2,1,0:T(8,128)S(1)}, f32[2,96,384]{2,1,0:T(8,128)S(1)}, u32[]{:S(2)}, u32[]{:S(2)}) %collective-permute-start.14) | collective-permute-done | bytes 294944 | tf_op jit(solution)/shard_map/ppermute | solution.py:58
  53.4 1.4 %collective-permute-start.15 = (f32[96,384]{1,0:T(8,128)S(1)}, f32[96,384]{1,0:T(8,128)S(1)}, u32[]{:S(2)}, u32[]{:S(2)}) collective-permute-start(f32[96,384]{1,0:T(8,128)S(1)} %select_bitcast_fusion.3), channel_id=1, source_target_pairs={{0,8},{8,0},{4,12},{12,4},{1,9},{9,1},{5,13},{13,5},{2,10},{10,2},... | collective-permute-start | bytes 442376 | tf_op jit(solution)/shard_map/ppermute | solution.py:63
  54.8 1.3 %fusion.39 = bf16[512,384]{1,0:T(8,128)(2,1)S(1)} fusion(f32[512,384]{1,0:T(8,128)S(1)} %copy-done.3, f32[512,384]{1,0:T(8,128)S(1)} %convolution_bitcast_fusion, bf16[512,1,384]{2,0,1:T(8,128)(2,1)S(1)} %get-tuple-element.16, bf16[512,1,384]{2,0,1:T(8,128)(2,1)S(1)} %bitcast.167, bf16[512,1,384]{2,0,1:T(8,128)(2,1)S(1)} %get-tuple-element.7, ...), kind=kOutput, calls=%fused_computation.60 | convolution fusion | flops 458883072 | bytes 4423684 | tf_op jit(solution)/shard_map/tko,kio->ti/dot_general | solution.py:115
  56.1 1.3 %slice.189 = bf16[1152,384]{1,0:T(8,128)(2,1)S(1)} slice(bf16[2176,384]{1,0:T(8,128)(2,1)} %collective-permute-done.3), slice={[1024:2176], [0:384]} | slice | bytes 1769472 | tf_op jit(solution)/shard_map/slice | solution.py:99
  57.3 0.8 convolution_bitcast_fusion.3
  58.2 8.0 %collective-permute-done.15 = f32[96,384]{1,0:T(8,128)S(1)} collective-permute-done((f32[96,384]{1,0:T(8,128)S(1)}, f32[96,384]{1,0:T(8,128)S(1)}, u32[]{:S(2)}, u32[]{:S(2)}) %collective-permute-start.15) | collective-permute-done | bytes 147488 | tf_op jit(solution)/shard_map/ppermute | solution.py:63
  66.2 2.5 %collective-permute-start.16 = (bf16[96,384]{1,0:T(8,128)(2,1)S(1)}, bf16[96,384]{1,0:T(8,128)(2,1)}, u32[]{:S(2)}, u32[]{:S(2)}) collective-permute-start(bf16[96,384]{1,0:T(8,128)(2,1)S(1)} %fusion.71), channel_id=1, source_target_pairs={{0,4},{4,8},{8,12},{12,0},{1,5},{5,9},{9,13},{13,1},{2,6},{6,10},{... | collective-permute-start | bytes 221192 | tf_op jit(solution)/shard_map/ppermute | solution.py:65
  68.7 1.0 collective-permute-start.17
  69.7 2.8 %collective-permute-start.18 = (bf16[96,384]{1,0:T(8,128)(2,1)S(1)}, bf16[96,384]{1,0:T(8,128)(2,1)}, u32[]{:S(2)}, u32[]{:S(2)}) collective-permute-start(bf16[96,384]{1,0:T(8,128)(2,1)S(1)} %fusion.71), channel_id=1, source_target_pairs={{0,12},{4,0},{8,4},{12,8},{1,13},{5,1},{9,5},{13,9},{2,14},{6,2},{... | collective-permute-start | bytes 221192 | tf_op jit(solution)/shard_map/ppermute | solution.py:65
  72.6 0.7 select_bitcast_fusion.2
  73.4 1.6 %fusion.4 = bf16[1,512,384]{2,1,0:T(8,128)(2,1)} fusion(f32[512,384]{1,0:T(8,128)S(1)} %copy-done.3, f32[512,384]{1,0:T(8,128)S(1)} %convolution_bitcast_fusion.3, bf16[3,384,384]{2,1,0:T(8,128)(2,1)S(1)} %bitcast.174, bf16[512,1,384]{2,0,1:T(8,128)(2,1)S(1)} %get-tuple-element.12, bf16[512,1,384]{2,0,1:T(8,128)(2,1)S(1)} %get-tuple-element.4, ...), kind=kOutput, calls=%fused_computation.17 | convolution fusion | flops 454754304 | bytes 4030464 | tf_op jit(solution)/shard_map/tki,kio->to/dot_general | solution.py:109
  75.3 1.2 %convert_element_type.50 = bf16[1,1024,384]{2,1,0:T(8,128)(2,1)} reshape(bf16[512,2,384]{2,1,0:T(2,128)(2,1)S(1)} %broadcast_in_dim.46) | data formatting | bytes 1572864 | tf_op jit(solution)/shard_map/convert_element_type | solution.py:124
  76.5 5.2 %collective-permute-done.17 = bf16[96,384]{1,0:T(8,128)(2,1)} collective-permute-done((bf16[96,384]{1,0:T(8,128)(2,1)S(1)}, bf16[96,384]{1,0:T(8,128)(2,1)}, u32[]{:S(2)}, u32[]{:S(2)}) %collective-permute-start.17) | collective-permute-done | bytes 73760 | tf_op jit(solution)/shard_map/ppermute | solution.py:65
  81.7 1.0 pad_maximum_fusion.14
  82.7 0.6 gather_fusion.1
  83.3 4.8 %collective-permute-done.10 = f32[192,384]{1,0:T(8,128)S(1)} collective-permute-done((f32[192,384]{1,0:T(8,128)}, f32[192,384]{1,0:T(8,128)S(1)}, u32[]{:S(2)}, u32[]{:S(2)}) %collective-permute-start.10) | collective-permute-done | bytes 294944 | tf_op jit(solution)/shard_map/ppermute | solution.py:63
  88.5 3.3 %collective-permute-start.12 = (bf16[192,384]{1,0:T(8,128)(2,1)S(1)}, bf16[192,384]{1,0:T(8,128)(2,1)S(1)}, u32[]{:S(2)}, u32[]{:S(2)}) collective-permute-start(bf16[192,384]{1,0:T(8,128)(2,1)S(1)} %fusion.70), channel_id=1, source_target_pairs={{0,8},{4,12},{8,0},{12,4},{1,9},{5,13},{9,1},{13,5},{2,10},{6,14},... | collective-permute-start | bytes 442376 | tf_op jit(solution)/shard_map/ppermute | solution.py:65
  92.2 4.6 %collective-permute-done.11 = bf16[192,384]{1,0:T(8,128)(2,1)S(1)} collective-permute-done((bf16[192,384]{1,0:T(8,128)(2,1)S(1)}, bf16[192,384]{1,0:T(8,128)(2,1)S(1)}, u32[]{:S(2)}, u32[]{:S(2)}) %collective-permute-start.11) | collective-permute-done | bytes 147488 | tf_op jit(solution)/shard_map/ppermute | solution.py:65
  96.8 4.2 %collective-permute-done.12 = bf16[192,384]{1,0:T(8,128)(2,1)S(1)} collective-permute-done((bf16[192,384]{1,0:T(8,128)(2,1)S(1)}, bf16[192,384]{1,0:T(8,128)(2,1)S(1)}, u32[]{:S(2)}, u32[]{:S(2)}) %collective-permute-start.12) | collective-permute-done | bytes 147488 | tf_op jit(solution)/shard_map/ppermute | solution.py:65
  101.1 0.7 gather_fusion
  102.0 1.4 %pad_maximum_fusion = f32[3,384,384]{2,1,0:T(8,128)} fusion(f32[1,384,384]{2,1,0:T(8,128)S(1)} %get-tuple-element.6, f32[1,384,384]{2,1,0:T(8,128)S(1)} %fusion.69, f32[1,384,384]{2,1,0:T(8,128)S(1)} %get-tuple-element.5), kind=kLoop, calls=%fused_computation.4 | loop fusion | flops 884736 | bytes 3538944 | tf_op jit(solution)/shard_map/stack | solution.py:147
  (50 shorter events, 4.3 us)
Async XLA Ops:
  0.6 14.7 %copy-start = (bf16[3,384,768]{2,1,0:T(8,128)(2,1)S(1)}, bf16[3,384,768]{2,1,0:T(8,128)(2,1)}, u32[]{:S(2)}) copy-start(bf16[3,384,768]{2,1,0:T(8,128)(2,1)} %param.4) | copy-start | bytes 5308420
  0.6 27.9 %collective-permute-start.5 = (bf16[512,384]{1,0:T(8,128)(2,1)}, bf16[512,384]{1,0:T(8,128)(2,1)}, u32[]{:S(2)}, u32[]{:S(2)}) collective-permute-start(bf16[512,384]{1,0:T(8,128)(2,1)} %bitcast.165), channel_id=1, source_target_pairs={{2,0},{1,3},{6,4},{5,7},{10,8},{9,11},{14,12},{13,15},{18,16},{17,... | collective-permute-start | bytes 1179656 | tf_op jit(solution)/shard_map/ppermute | solution.py:87
  2.1 26.4 %collective-permute-start.6 = (bf16[512,384]{1,0:T(8,128)(2,1)}, bf16[512,384]{1,0:T(8,128)(2,1)}, u32[]{:S(2)}, u32[]{:S(2)}) collective-permute-start(bf16[512,384]{1,0:T(8,128)(2,1)} %bitcast.166), channel_id=1, source_target_pairs={{2,1},{1,2},{6,5},{5,6},{10,9},{9,10},{14,13},{13,14},{18,17},{17,... | collective-permute-start | bytes 1179656 | tf_op jit(solution)/shard_map/ppermute | solution.py:88
  3.5 2.8 %copy-start.1 = (bf16[1,512,384]{2,1,0:T(8,128)(2,1)S(1)}, bf16[1,512,384]{2,1,0:T(8,128)(2,1)}, u32[]{:S(2)}) copy-start(bf16[1,512,384]{2,1,0:T(8,128)(2,1)} %param.5) | copy-start | bytes 1179652
  7.3 14.5 %collective-permute-start = (bf16[2,256,384]{2,1,0:T(8,128)(2,1)}, bf16[2,256,384]{2,1,0:T(8,128)(2,1)}, u32[]{:S(2)}, u32[]{:S(2)}) collective-permute-start(bf16[2,256,384]{2,1,0:T(8,128)(2,1)} %get-tuple-element.21), channel_id=1, source_target_pairs={{0,4},{4,8},{8,12},{1,5},{5,9},{9,13},{2,6},{6,10},{10,14},{3,7},{... | collective-permute-start | bytes 1179656 | tf_op jit(solution)/shard_map/ppermute | solution.py:12
  13.0 11.4 %collective-permute-start.1 = (bf16[2,256,384]{2,1,0:T(8,128)(2,1)}, bf16[2,256,384]{2,1,0:T(8,128)(2,1)}, u32[]{:S(2)}, u32[]{:S(2)}) collective-permute-start(bf16[2,256,384]{2,1,0:T(8,128)(2,1)} %get-tuple-element.22), channel_id=1, source_target_pairs={{4,0},{8,4},{12,8},{5,1},{9,5},{13,9},{6,2},{10,6},{14,10},{7,3},{... | collective-permute-start | bytes 1179656 | tf_op jit(solution)/shard_map/ppermute | solution.py:12
  15.3 1.1 %copy-start.2 = (bf16[2,512,384]{2,1,0:T(8,128)(2,1)S(1)}, bf16[2,512,384]{2,1,0:T(8,128)(2,1)}, u32[]{:S(2)}) copy-start(bf16[2,512,384]{2,1,0:T(8,128)(2,1)} %pad_maximum_fusion.3) | copy-start | bytes 2359300
  17.8 23.6 %collective-permute-start.3 = (bf16[2176,384]{1,0:T(8,128)(2,1)}, bf16[2176,384]{1,0:T(8,128)(2,1)}, u32[]{:S(2)}, u32[]{:S(2)}) collective-permute-start(bf16[2176,384]{1,0:T(8,128)(2,1)} %pad_maximum_fusion.1), channel_id=1, source_target_pairs={{0,1},{1,0},{2,3},{3,2},{4,5},{5,4},{6,7},{7,6},{8,9},{9,8},{10,11... | collective-permute-start | bytes 5013512 | tf_op jit(solution)/shard_map/ppermute | solution.py:95
  21.9 11.8 %collective-permute-start.4 = (bf16[512,384]{1,0:T(8,128)(2,1)S(1)}, bf16[512,384]{1,0:T(8,128)(2,1)S(1)}, u32[]{:S(2)}, u32[]{:S(2)}) collective-permute-start(bf16[512,384]{1,0:T(8,128)(2,1)S(1)} %get-tuple-element.26), channel_id=1, source_target_pairs={{0,2},{2,0},{1,3},{3,1},{4,6},{6,4},{5,7},{7,5},{8,10},{10,8},{9,1... | collective-permute-start | bytes 1179656 | tf_op jit(solution)/shard_map/ppermute | solution.py:90
  25.7 15.6 %collective-permute-start.2 = (bf16[2,2,256,384]{3,2,1,0:T(8,128)(2,1)S(1)}, bf16[2,2,256,384]{3,2,1,0:T(8,128)(2,1)S(1)}, u32[]{:S(2)}, u32[]{:S(2)}) collective-permute-start(bf16[2,2,256,384]{3,2,1,0:T(8,128)(2,1)S(1)} %pad_maximum_fusion.4), channel_id=1, source_target_pairs={{0,1},{1,0},{2,3},{3,2},{4,5},{5,4},{6,7},{7,6},{8,9},{9,8},{10,11... | collective-permute-start | bytes 2359304 | tf_op jit(solution)/shard_map/ppermute | solution.py:102
  29.6 7.1 %collective-permute-start.8 = (bf16[256,384]{1,0:T(8,128)(2,1)S(1)}, bf16[256,384]{1,0:T(8,128)(2,1)S(1)}, u32[]{:S(2)}, u32[]{:S(2)}) collective-permute-start(bf16[256,384]{1,0:T(8,128)(2,1)S(1)} %get-tuple-element.24), channel_id=1, source_target_pairs={{0,4},{4,8},{8,12},{1,5},{5,9},{9,13},{2,6},{6,10},{10,14},{3,7},{... | collective-permute-start | bytes 589832 | tf_op jit(solution)/shard_map/ppermute | solution.py:12
  32.4 8.5 %collective-permute-start.7 = (bf16[256,384]{1,0:T(8,128)(2,1)S(1)}, bf16[256,384]{1,0:T(8,128)(2,1)S(1)}, u32[]{:S(2)}, u32[]{:S(2)}) collective-permute-start(bf16[256,384]{1,0:T(8,128)(2,1)S(1)} %get-tuple-element.25), channel_id=1, source_target_pairs={{4,0},{8,4},{12,8},{5,1},{9,5},{13,9},{6,2},{10,6},{14,10},{7,3},{... | collective-permute-start | bytes 589832 | tf_op jit(solution)/shard_map/ppermute | solution.py:12
  43.4 9.9 %collective-permute-start.14 = (f32[2,96,384]{2,1,0:T(8,128)S(1)}, f32[2,96,384]{2,1,0:T(8,128)S(1)}, u32[]{:S(2)}, u32[]{:S(2)}) collective-permute-start(f32[2,96,384]{2,1,0:T(8,128)S(1)} %select_bitcast_fusion.1), channel_id=1, source_target_pairs={{0,4},{4,0},{8,12},{12,8},{1,5},{5,1},{9,13},{13,9},{2,6},{6,2},{1... | collective-permute-start | bytes 884744 | tf_op jit(solution)/shard_map/ppermute | solution.py:58
  47.8 24.7 %collective-permute-start.9 = (f32[2,192,384]{2,1,0:T(8,128)S(1)}, f32[2,192,384]{2,1,0:T(8,128)S(1)}, u32[]{:S(2)}, u32[]{:S(2)}) collective-permute-start(f32[2,192,384]{2,1,0:T(8,128)S(1)} %select_bitcast_fusion), channel_id=1, source_target_pairs={{0,4},{4,0},{8,12},{12,8},{1,5},{5,1},{9,13},{13,9},{2,6},{6,2},{1... | collective-permute-start | bytes 1769480 | tf_op jit(solution)/shard_map/ppermute | solution.py:58
  51.8 3.0 %copy-start.3 = (f32[512,384]{1,0:T(8,128)S(1)}, f32[512,384]{1,0:T(8,128)}, u32[]{:S(2)}) copy-start(f32[512,384]{1,0:T(8,128)} %get-tuple-element.27) | copy-start | bytes 2359300
  53.4 12.7 %collective-permute-start.15 = (f32[96,384]{1,0:T(8,128)S(1)}, f32[96,384]{1,0:T(8,128)S(1)}, u32[]{:S(2)}, u32[]{:S(2)}) collective-permute-start(f32[96,384]{1,0:T(8,128)S(1)} %select_bitcast_fusion.3), channel_id=1, source_target_pairs={{0,8},{8,0},{4,12},{12,4},{1,9},{9,1},{5,13},{13,5},{2,10},{10,2},... | collective-permute-start | bytes 442376 | tf_op jit(solution)/shard_map/ppermute | solution.py:63
  66.2 10.4 %collective-permute-start.16 = (bf16[96,384]{1,0:T(8,128)(2,1)S(1)}, bf16[96,384]{1,0:T(8,128)(2,1)}, u32[]{:S(2)}, u32[]{:S(2)}) collective-permute-start(bf16[96,384]{1,0:T(8,128)(2,1)S(1)} %fusion.71), channel_id=1, source_target_pairs={{0,4},{4,8},{8,12},{12,0},{1,5},{5,9},{9,13},{13,1},{2,6},{6,10},{... | collective-permute-start | bytes 221192 | tf_op jit(solution)/shard_map/ppermute | solution.py:65
  68.7 13.0 %collective-permute-start.17 = (bf16[96,384]{1,0:T(8,128)(2,1)S(1)}, bf16[96,384]{1,0:T(8,128)(2,1)}, u32[]{:S(2)}, u32[]{:S(2)}) collective-permute-start(bf16[96,384]{1,0:T(8,128)(2,1)S(1)} %fusion.71), channel_id=1, source_target_pairs={{0,8},{4,12},{8,0},{12,4},{1,9},{5,13},{9,1},{13,5},{2,10},{6,14},... | collective-permute-start | bytes 221192 | tf_op jit(solution)/shard_map/ppermute | solution.py:65
  69.7 12.0 %collective-permute-start.18 = (bf16[96,384]{1,0:T(8,128)(2,1)S(1)}, bf16[96,384]{1,0:T(8,128)(2,1)}, u32[]{:S(2)}, u32[]{:S(2)}) collective-permute-start(bf16[96,384]{1,0:T(8,128)(2,1)S(1)} %fusion.71), channel_id=1, source_target_pairs={{0,12},{4,0},{8,4},{12,8},{1,13},{5,1},{9,5},{13,9},{2,14},{6,2},{... | collective-permute-start | bytes 221192 | tf_op jit(solution)/shard_map/ppermute | solution.py:65
  73.3 14.8 %collective-permute-start.10 = (f32[192,384]{1,0:T(8,128)}, f32[192,384]{1,0:T(8,128)S(1)}, u32[]{:S(2)}, u32[]{:S(2)}) collective-permute-start(f32[192,384]{1,0:T(8,128)} %select_bitcast_fusion.2), channel_id=1, source_target_pairs={{0,8},{8,0},{4,12},{12,4},{1,9},{9,1},{5,13},{13,5},{2,10},{10,2},... | collective-permute-start | bytes 884744 | tf_op jit(solution)/shard_map/ppermute | solution.py:63
  88.2 8.6 %collective-permute-start.11 = (bf16[192,384]{1,0:T(8,128)(2,1)S(1)}, bf16[192,384]{1,0:T(8,128)(2,1)S(1)}, u32[]{:S(2)}, u32[]{:S(2)}) collective-permute-start(bf16[192,384]{1,0:T(8,128)(2,1)S(1)} %fusion.70), channel_id=1, source_target_pairs={{0,4},{4,8},{8,12},{12,0},{1,5},{5,9},{9,13},{13,1},{2,6},{6,10},{... | collective-permute-start | bytes 442376 | tf_op jit(solution)/shard_map/ppermute | solution.py:65
  88.5 12.5 %collective-permute-start.12 = (bf16[192,384]{1,0:T(8,128)(2,1)S(1)}, bf16[192,384]{1,0:T(8,128)(2,1)S(1)}, u32[]{:S(2)}, u32[]{:S(2)}) collective-permute-start(bf16[192,384]{1,0:T(8,128)(2,1)S(1)} %fusion.70), channel_id=1, source_target_pairs={{0,8},{4,12},{8,0},{12,4},{1,9},{5,13},{9,1},{13,5},{2,10},{6,14},... | collective-permute-start | bytes 442376 | tf_op jit(solution)/shard_map/ppermute | solution.py:65
  91.8 9.2 %collective-permute-start.13 = (bf16[192,384]{1,0:T(8,128)(2,1)S(1)}, bf16[192,384]{1,0:T(8,128)(2,1)S(1)}, u32[]{:S(2)}, u32[]{:S(2)}) collective-permute-start(bf16[192,384]{1,0:T(8,128)(2,1)S(1)} %fusion.70), channel_id=1, source_target_pairs={{0,12},{4,0},{8,4},{12,8},{1,13},{5,1},{9,5},{13,9},{2,14},{6,2},{... | collective-permute-start | bytes 442376 | tf_op jit(solution)/shard_map/ppermute | solution.py:65

commit v20 on v11

--- a/solution.py
+++ b/solution.py
@@ -76,6 +76,7 @@
     width = local_in.shape[1]
     spread = rows // 2
     c = lax.axis_index("chan")
+    par_cot_early = lax.ppermute(local_cot, "chan", SWAP)
     pairing = lax.broadcasted_iota(jnp.int32, (rows, 2 * rows), 1) // 2 == lax.broadcasted_iota(
         jnp.int32, (rows, 2 * rows), 0
     )
@@ -94,10 +95,10 @@
     w_own = half_of(conv_weight, c, 2)
     w_other = half_of(conv_weight, 1 - c, 2)
     swapped = lax.ppermute(
-        jnp.concatenate([both.reshape(-1, width), w_other.reshape(-1, width)], 0), "chan", SWAP
+        jnp.concatenate([activation, w_other.reshape(-1, width)], 0), "chan", SWAP
     )
-    par_mid = swapped[: 2 * rows].reshape(both.shape)
-    w_par = swapped[2 * rows :].reshape(w_other.shape)
+    par_mid = jnp.stack([swapped[:rows], par_cot_early])
+    w_par = swapped[rows:].reshape(w_other.shape)
     from_prev = shift_from(both[:, rows - spread :], "seq", 1)
     from_next = shift_from(both[:, :spread], "seq", -1)
     par_halo = lax.ppermute(jnp.stack([from_prev, from_next]), "chan", SWAP)

time: 103 us -> 116 us (1.13)
  waiting for transfers between devices: 42.3 us -> 58.4 us
  local copies, waits for them, and re-layouts: 6.93 us -> 2.88 us
  matrix products: 11.5 us -> 12.9 us
    ppermute x2, waiting for transfers between devices: 0.01 us -> 16.7 us  [line_total(): total = (keep + lax.ppermute(give, 'seq', across)).astype(jnp.bfloat16)]
    ppermute x2, waiting for transfers between devices: 6.41 us -> 17.5 us  [line_total(): far_set = lax.ppermute(own_set, 'seq', pairs)]
    ppermute x2, waiting for transfers between devices: 16.6 us -> 9.35 us  [line_total(): other = lax.ppermute(total, 'seq', across)]
    ppermute x2, waiting for transfers between devices: 10.9 us -> 4.02 us  [line_total(): lax.ppermute(jnp.where(odd, even_set, odd_set), 'seq', pairs)]
    ppermute x2, starting transfers between devices: 5.92 us -> 0.07 us  [line_total(): other = lax.ppermute(total, 'seq', across)]
    ppermute x2, starting transfers between devices: 2.16 us -> 5.88 us  [line_total(): lax.ppermute(jnp.where(odd, even_set, odd_set), 'seq', pairs)]
    ppermute x1, starting transfers between devices: 0.97 us -> 4.65 us  [shards(): far_mid = lax.ppermute(activation, 'batch', SWAP)]
    ppermute x1, waiting for transfers between devices: 0.01 us -> 2.96 us  [shards(): far_mid = lax.ppermute(activation, 'batch', SWAP)]
  transfers between devices with their start and end apart: 17 -> 18, of which waited for: 7 -> 10; matrix products, arithmetic and copies ran while one was open for 22% -> 19% of each run, Pallas kernels for 0% -> 0%
where the time goes in v20:
time: 116 us
  waiting for transfers between devices  58.4 us (50%)
  starting transfers between devices  30.2 us (26%)
  matrix products  12.9 us (11%)
  other arithmetic  10.2 us (9%)
  local copies, waits for them, and re-layouts  2.88 us (2%)
    ppermute x2, waiting for transfers between devices, line_total(): far_set = lax.ppermute(own_set, 'seq', pairs)  17.5 us
    ppermute x2, waiting for transfers between devices, line_total(): total = (keep + lax.ppermute(give, 'seq', across)).astype(jnp.bfloat16)  16.7 us
    ppermute x4, starting transfers between devices, shift_from(): return lax.ppermute(block, axis, route)  11.6 us
    ppermute x2, waiting for transfers between devices, line_total(): other = lax.ppermute(total, 'seq', across)  9.35 us
    ppermute x4, waiting for transfers between devices, shift_from(): return lax.ppermute(block, axis, route)  7.93 us
    ppermute x2, starting transfers between devices, line_total(): lax.ppermute(jnp.where(odd, even_set, odd_set), 'seq', pairs)  5.88 us
    ppermute x1, starting transfers between devices, shards(): far_mid = lax.ppermute(activation, 'batch', SWAP)  4.65 us
    ppermute x2, starting transfers between devices, line_total(): total = (keep + lax.ppermute(give, 'seq', across)).astype(jnp.bfloat16)  4.03 us
  transfers between devices with their start and end apart: 18, of which 10 were waited for; matrix products, arithmetic and copies ran while one was open for 19% of the time, Pallas kernels for 0%

profile of v20, /device:TPU:0, one launch (start us, length us, event | category | flops | bytes accessed | tf_op | source)
XLA Modules:
  0.0 115.6 jit_solution(15049111587135688438)
XLA Ops:
  0.6 0.6 collective-permute-start.4
  1.2 1.3 %collective-permute-start.6 = (bf16[512,384]{1,0:T(8,128)(2,1)}, bf16[512,384]{1,0:T(8,128)(2,1)}, u32[]{:S(2)}, u32[]{:S(2)}) collective-permute-start(bf16[512,384]{1,0:T(8,128)(2,1)} %bitcast.152), channel_id=1, source_target_pairs={{2,0},{1,3},{6,4},{5,7},{10,8},{9,11},{14,12},{13,15},{18,16},{17,... | collective-permute-start | bytes 1179656 | tf_op jit(solution)/shard_map/ppermute | solution.py:89
  2.5 1.4 %collective-permute-start.7 = (bf16[512,384]{1,0:T(8,128)(2,1)}, bf16[512,384]{1,0:T(8,128)(2,1)}, u32[]{:S(2)}, u32[]{:S(2)}) collective-permute-start(bf16[512,384]{1,0:T(8,128)(2,1)} %bitcast.153), channel_id=1, source_target_pairs={{2,1},{1,2},{6,5},{5,6},{10,9},{9,10},{14,13},{13,14},{18,17},{17,... | collective-permute-start | bytes 1179656 | tf_op jit(solution)/shard_map/ppermute | solution.py:90
  3.9 2.8 %multiply_convert_fusion = (bf16[512,384]{1,0:T(8,128)(2,1)S(1)}, f32[512,384]{1,0:T(8,128)}) fusion(bf16[1,1024,384]{2,1,0:T(8,128)(2,1)} %param.3, s32[1024]{0:T(1024)S(1)} %get-tuple-element.31, s32[1024]{0:T(1024)S(1)} %get-tuple-element.32, pred[1024]{0:T(1024)(128)(4,1)S(1)} %fusion.68), kind=kOutput, calls=%fused_computation.58 | convolution fusion | flops 406519808 | bytes 1975296 | tf_op jit(solution)/shard_map/dot_general | solution.py:84
  6.7 1.0 fusion.47
  7.7 1.3 %collective-permute-start.1 = (bf16[2,256,384]{2,1,0:T(8,128)(2,1)}, bf16[2,256,384]{2,1,0:T(8,128)(2,1)}, u32[]{:S(2)}, u32[]{:S(2)}) collective-permute-start(bf16[2,256,384]{2,1,0:T(8,128)(2,1)} %get-tuple-element.22), channel_id=1, source_target_pairs={{4,0},{8,4},{12,8},{5,1},{9,5},{13,9},{6,2},{10,6},{14,10},{7,3},{... | collective-permute-start | bytes 1179656 | tf_op jit(solution)/shard_map/ppermute | solution.py:12
  9.0 5.3 %collective-permute-start = (bf16[2,256,384]{2,1,0:T(8,128)(2,1)}, bf16[2,256,384]{2,1,0:T(8,128)(2,1)S(1)}, u32[]{:S(2)}, u32[]{:S(2)}) collective-permute-start(bf16[2,256,384]{2,1,0:T(8,128)(2,1)} %get-tuple-element.21), channel_id=1, source_target_pairs={{0,4},{4,8},{8,12},{1,5},{5,9},{9,13},{2,6},{6,10},{10,14},{3,7},{... | collective-permute-start | bytes 1179656 | tf_op jit(solution)/shard_map/ppermute | solution.py:12
  14.4 0.1 pad_maximum_fusion.1
  14.5 4.7 %collective-permute-done.1 = bf16[2,256,384]{2,1,0:T(8,128)(2,1)} collective-permute-done((bf16[2,256,384]{2,1,0:T(8,128)(2,1)}, bf16[2,256,384]{2,1,0:T(8,128)(2,1)}, u32[]{:S(2)}, u32[]{:S(2)}) %collective-permute-start.1) | collective-permute-done | bytes 393248 | tf_op jit(solution)/shard_map/ppermute | solution.py:12
  19.2 4.7 %collective-permute-start.5 = (bf16[512,384]{1,0:T(8,128)(2,1)S(1)}, bf16[512,384]{1,0:T(8,128)(2,1)S(1)}, u32[]{:S(2)}, u32[]{:S(2)}) collective-permute-start(bf16[512,384]{1,0:T(8,128)(2,1)S(1)} %get-tuple-element.29), channel_id=1, source_target_pairs={{0,2},{2,0},{1,3},{3,1},{4,6},{6,4},{5,7},{7,5},{8,10},{10,8},{9,1... | collective-permute-start | bytes 1179656 | tf_op jit(solution)/shard_map/ppermute | solution.py:92
  23.9 0.3 collective-permute-start.3
  24.2 1.1 pad_maximum_fusion.3
  25.3 0.3 collective-permute-start.2
  25.6 1.0 broadcast_select_fusion
  26.7 3.8 %collective-permute-start.9 = (bf16[256,384]{1,0:T(8,128)(2,1)S(1)}, bf16[256,384]{1,0:T(8,128)(2,1)S(1)}, u32[]{:S(2)}, u32[]{:S(2)}) collective-permute-start(bf16[256,384]{1,0:T(8,128)(2,1)S(1)} %get-tuple-element.25), channel_id=1, source_target_pairs={{0,4},{4,8},{8,12},{1,5},{5,9},{9,13},{2,6},{6,10},{10,14},{3,7},{... | collective-permute-start | bytes 589832 | tf_op jit(solution)/shard_map/ppermute | solution.py:12
  30.5 3.0 %collective-permute-done.5 = bf16[512,384]{1,0:T(8,128)(2,1)S(1)} collective-permute-done((bf16[512,384]{1,0:T(8,128)(2,1)S(1)}, bf16[512,384]{1,0:T(8,128)(2,1)S(1)}, u32[]{:S(2)}, u32[]{:S(2)}) %collective-permute-start.5) | collective-permute-done | bytes 393248 | tf_op jit(solution)/shard_map/ppermute | solution.py:92
  33.4 1.3 %collective-permute-start.8 = (bf16[256,384]{1,0:T(8,128)(2,1)S(1)}, bf16[256,384]{1,0:T(8,128)(2,1)S(1)}, u32[]{:S(2)}, u32[]{:S(2)}) collective-permute-start(bf16[256,384]{1,0:T(8,128)(2,1)S(1)} %get-tuple-element.26), channel_id=1, source_target_pairs={{4,0},{8,4},{12,8},{5,1},{9,5},{13,9},{6,2},{10,6},{14,10},{7,3},{... | collective-permute-start | bytes 589832 | tf_op jit(solution)/shard_map/ppermute | solution.py:12
  34.7 0.4 fusion.83
  35.1 0.4 convolution_add_fusion
  35.6 2.7 %collective-permute-start.14 = (f32[2,96,384]{2,1,0:T(8,128)S(1)}, f32[2,96,384]{2,1,0:T(8,128)S(1)}, u32[]{:S(2)}, u32[]{:S(2)}) collective-permute-start(f32[2,96,384]{2,1,0:T(8,128)S(1)} %select_bitcast_fusion.1), channel_id=1, source_target_pairs={{0,4},{4,0},{8,12},{12,8},{1,5},{5,1},{9,13},{13,9},{2,6},{6,2},{1... | collective-permute-start | bytes 884744 | tf_op jit(solution)/shard_map/ppermute | solution.py:58
  38.3 1.2 %fusion.51 = (bf16[512,1,384]{2,0,1:T(8,128)(2,1)S(1)}, bf16[512,1,384]{2,0,1:T(8,128)(2,1)S(1)}, bf16[512,1,384]{2,0,1:T(8,128)(2,1)S(1)}, bf16[512,1,384]{2,0,1:T(8,128)(2,1)S(1)}) fusion(bf16[2,256,384]{2,1,0:T(8,128)(2,1)} %collective-permute-done.1, bf16[1,512,384]{2,1,0:T(8,128)(2,1)S(1)} %copy-done.1, bf16[1,512,384]{2,1,0:T(8,128)(2,1)S(1)} %bitcast.145, ...), kind=kLoop, calls=%fused_computation.77 | loop fusion | flops 4718592 | bytes 3145728 | tf_op jit(solution)/shard_map/stack | solution.py:21
  39.5 0.4 fusion.56
  39.9 3.2 %collective-permute-done.8 = bf16[256,384]{1,0:T(8,128)(2,1)S(1)} collective-permute-done((bf16[256,384]{1,0:T(8,128)(2,1)S(1)}, bf16[256,384]{1,0:T(8,128)(2,1)S(1)}, u32[]{:S(2)}, u32[]{:S(2)}) %collective-permute-start.8) | collective-permute-done | bytes 196640 | tf_op jit(solution)/shard_map/ppermute | solution.py:12
  43.1 0.4 fusion.52
  43.5 1.3 %convolution_add_fusion.1 = f32[384,384]{1,0:T(8,128)S(1)} fusion(f32[384,384]{1,0:T(8,128)S(1)} %fusion.56, bf16[2,256,384]{2,1,0:T(8,128)(2,1)} %collective-permute-done.1, bf16[1,512,384]{2,1,0:T(8,128)(2,1)S(1)} %copy-done.1, bf16[1,512,384]{2,1,0:T(8,128)(2,1)S(1)} %bitcast.146, bf16[512,384]{1,0:T(8,128)(2,1)S(1)} %collective-permute-done.4, pred[]{:T(512)S(6)} %eq.16), kind=kOutput, calls=%fused_computation.13 | convolution fusion | flops 152518656 | bytes 2752513 | tf_op jit(solution)/shard_map/dot_general | solution.py:143
  44.8 4.0 %collective-permute-done.14 = f32[2,96,384]{2,1,0:T(8,128)S(1)} collective-permute-done((f32[2,96,384]{2,1,0:T(8,128)S(1)}, f32[2,96,384]{2,1,0:T(8,128)S(1)}, u32[]{:S(2)}, u32[]{:S(2)}) %collective-permute-start.14) | collective-permute-done | bytes 294944 | tf_op jit(solution)/shard_map/ppermute | solution.py:58
  48.9 2.8 %collective-permute-start.15 = (f32[96,384]{1,0:T(8,128)S(1)}, f32[96,384]{1,0:T(8,128)S(1)}, u32[]{:S(2)}, u32[]{:S(2)}) collective-permute-start(f32[96,384]{1,0:T(8,128)S(1)} %select_bitcast_fusion.7), channel_id=1, source_target_pairs={{0,8},{8,0},{4,12},{12,4},{1,9},{9,1},{5,13},{13,5},{2,10},{10,2},... | collective-permute-start | bytes 442376 | tf_op jit(solution)/shard_map/ppermute | solution.py:63
  51.7 0.4 convolution_add_fusion.2
  52.2 5.9 %collective-permute-done.15 = f32[96,384]{1,0:T(8,128)S(1)} collective-permute-done((f32[96,384]{1,0:T(8,128)S(1)}, f32[96,384]{1,0:T(8,128)S(1)}, u32[]{:S(2)}, u32[]{:S(2)}) %collective-permute-start.15) | collective-permute-done | bytes 147488 | tf_op jit(solution)/shard_map/ppermute | solution.py:63
  58.3 3.2 %collective-permute-start.10 = (f32[2,192,384]{2,1,0:T(8,128)S(1)}, f32[2,192,384]{2,1,0:T(8,128)S(1)}, u32[]{:S(2)}, u32[]{:S(2)}) collective-permute-start(f32[2,192,384]{2,1,0:T(8,128)S(1)} %select_bitcast_fusion), channel_id=1, source_target_pairs={{0,4},{4,0},{8,12},{12,8},{1,5},{5,1},{9,13},{13,9},{2,6},{6,2},{1... | collective-permute-start | bytes 1769480 | tf_op jit(solution)/shard_map/ppermute | solution.py:58
  61.5 2.7 %collective-permute-done.16 = bf16[96,384]{1,0:T(8,128)(2,1)S(1)} collective-permute-done((bf16[96,384]{1,0:T(8,128)(2,1)S(1)}, bf16[96,384]{1,0:T(8,128)(2,1)S(1)}, u32[]{:S(2)}, u32[]{:S(2)}) %collective-permute-start.16) | collective-permute-done | bytes 73760 | tf_op jit(solution)/shard_map/ppermute | solution.py:64
  64.3 1.7 %convolution_bitcast_fusion.3 = f32[512,384]{1,0:T(8,128)} fusion(bf16[512,1,384]{2,0,1:T(8,128)(2,1)S(1)} %get-tuple-element.12, bf16[512,1,384]{2,0,1:T(8,128)(2,1)S(1)} %bitcast.148, bf16[512,1,384]{2,0,1:T(8,128)(2,1)S(1)} %get-tuple-element.17, bf16[3,384,768]{2,1,0:T(8,128)(2,1)S(1)} %copy-done, s32[]{:T(128)S(6)} %select_n.146), kind=kOutput, calls=%fused_computation.6 | convolution fusion | flops 454164480 | bytes 2850820 | tf_op jit(solution)/shard_map/tki,kio->to/dot_general | solution.py:108
  66.0 0.8 convolution_bitcast_fusion.1
  66.9 11.5 %collective-permute-done.17 = bf16[2,96,384]{2,1,0:T(8,128)(2,1)S(1)} collective-permute-done((bf16[2,96,384]{2,1,0:T(8,128)(2,1)S(1)}, bf16[2,96,384]{2,1,0:T(8,128)(2,1)S(1)}, u32[]{:S(2)}, u32[]{:S(2)}) %collective-permute-start.17) | collective-permute-done | bytes 147488 | tf_op jit(solution)/shard_map/ppermute | solution.py:66
  78.7 1.2 %collective-permute-start.11 = (f32[192,384]{1,0:T(8,128)S(1)}, f32[192,384]{1,0:T(8,128)S(1)}, u32[]{:S(2)}, u32[]{:S(2)}) collective-permute-start(f32[192,384]{1,0:T(8,128)S(1)} %select_bitcast_fusion.4), channel_id=1, source_target_pairs={{0,8},{8,0},{4,12},{12,4},{1,9},{9,1},{5,13},{13,5},{2,10},{10,2},... | collective-permute-start | bytes 884744 | tf_op jit(solution)/shard_map/ppermute | solution.py:63
  80.0 0.9 slice_bitcast_fusion.2
  80.9 1.0 fusion.49
  81.9 10.8 %collective-permute-done.11 = f32[192,384]{1,0:T(8,128)S(1)} collective-permute-done((f32[192,384]{1,0:T(8,128)S(1)}, f32[192,384]{1,0:T(8,128)S(1)}, u32[]{:S(2)}, u32[]{:S(2)}) %collective-permute-start.11) | collective-permute-done | bytes 294944 | tf_op jit(solution)/shard_map/ppermute | solution.py:63
  92.7 0.7 fusion.64
  93.4 1.3 %fusion.39 = bf16[512,384]{1,0:T(8,128)(2,1)S(1)} fusion(f32[512,384]{1,0:T(8,128)S(1)} %copy-done.6, f32[512,384]{1,0:T(8,128)S(1)} %convolution_bitcast_fusion.1, bf16[3,384,384]{2,1,0:T(8,128)(2,1)S(1)} %constant_dynamic-slice_fusion, bf16[512,1,384]{2,0,1:T(8,128)(2,1)S(1)} %get-tuple-element.16, bf16[512,1,384]{2,0,1:T(8,128)(2,1)S(1)} %bitcast.156, ...), kind=kOutput, calls=%fused_computation.53 | convolution fusion | flops 458883072 | bytes 4423680 | tf_op jit(solution)/shard_map/tko,kio->ti/dot_general | solution.py:120
  94.8 0.4 broadcast_in_dim.18
  95.2 1.2 %convert_element_type.54 = bf16[1,1024,384]{2,1,0:T(8,128)(2,1)} reshape(bf16[512,2,384]{2,1,0:T(2,128)(2,1)S(1)} %broadcast_in_dim.18) | data formatting | bytes 1572864 | tf_op jit(solution)/shard_map/convert_element_type | solution.py:126
  96.4 6.6 %collective-permute-done.12 = bf16[192,384]{1,0:T(8,128)(2,1)S(1)} collective-permute-done((bf16[192,384]{1,0:T(8,128)(2,1)}, bf16[192,384]{1,0:T(8,128)(2,1)S(1)}, u32[]{:S(2)}, u32[]{:S(2)}) %collective-permute-start.12) | collective-permute-done | bytes 147488 | tf_op jit(solution)/shard_map/ppermute | solution.py:64
  103.0 1.0 maximum_select_fusion
  104.1 2.9 %fusion.4 = bf16[1,512,384]{2,1,0:T(8,128)(2,1)} fusion(f32[512,384]{1,0:T(8,128)} %get-tuple-element.30, f32[512,384]{1,0:T(8,128)} %convolution_bitcast_fusion.3, bf16[3,384,384]{2,1,0:T(8,128)(2,1)S(1)} %bitcast.164, bf16[512,1,384]{2,0,1:T(8,128)(2,1)S(1)} %copy-done.3, bf16[512,1,384]{2,0,1:T(8,128)(2,1)S(1)} %copy-done.5, ...), kind=kOutput, calls=%fused_computation.15 | convolution fusion | flops 454754304 | bytes 4030464 | tf_op jit(solution)/shard_map/tki,kio->to/dot_general | solution.py:111
  107.1 6.0 %collective-permute-done.13 = bf16[2,192,384]{2,1,0:T(8,128)(2,1)S(1)} collective-permute-done((bf16[2,192,384]{2,1,0:T(8,128)(2,1)S(1)}, bf16[2,192,384]{2,1,0:T(8,128)(2,1)S(1)}, u32[]{:S(2)}, u32[]{:S(2)}) %collective-permute-start.13) | collective-permute-done | bytes 294944 | tf_op jit(solution)/shard_map/ppermute | solution.py:66
  113.0 1.1 select_bitcast_fusion.3
  114.3 1.3 %pad_maximum_fusion = f32[3,384,384]{2,1,0:T(8,128)} fusion(f32[1,384,384]{2,1,0:T(8,128)S(1)} %bitcast.163, f32[1,384,384]{2,1,0:T(8,128)S(1)} %bitcast.161, f32[1,384,384]{2,1,0:T(8,128)S(1)} %bitcast.162), kind=kLoop, calls=%fused_computation.2 | loop fusion | flops 884736 | bytes 3538944 | tf_op jit(solution)/shard_map/stack | solution.py:149
  (47 shorter events, 1.2 us)
Async XLA Ops:
  0.6 13.7 %copy-start = (bf16[3,384,768]{2,1,0:T(8,128)(2,1)S(1)}, bf16[3,384,768]{2,1,0:T(8,128)(2,1)}, u32[]{:S(2)}) copy-start(bf16[3,384,768]{2,1,0:T(8,128)(2,1)} %param.4) | copy-start | bytes 5308420
  0.6 34.5 %collective-permute-start.4 = (bf16[512,384]{1,0:T(8,128)(2,1)}, bf16[512,384]{1,0:T(8,128)(2,1)S(1)}, u32[]{:S(2)}, u32[]{:S(2)}) collective-permute-start(bf16[512,384]{1,0:T(8,128)(2,1)} %bitcast.151), channel_id=1, source_target_pairs={{0,1},{1,0},{2,3},{3,2},{4,5},{5,4},{6,7},{7,6},{8,9},{9,8},{10,11... | collective-permute-start | bytes 1179656 | tf_op jit(solution)/shard_map/ppermute | solution.py:79
  1.2 24.1 %collective-permute-start.6 = (bf16[512,384]{1,0:T(8,128)(2,1)}, bf16[512,384]{1,0:T(8,128)(2,1)}, u32[]{:S(2)}, u32[]{:S(2)}) collective-permute-start(bf16[512,384]{1,0:T(8,128)(2,1)} %bitcast.152), channel_id=1, source_target_pairs={{2,0},{1,3},{6,4},{5,7},{10,8},{9,11},{14,12},{13,15},{18,16},{17,... | collective-permute-start | bytes 1179656 | tf_op jit(solution)/shard_map/ppermute | solution.py:89
  2.5 23.1 %collective-permute-start.7 = (bf16[512,384]{1,0:T(8,128)(2,1)}, bf16[512,384]{1,0:T(8,128)(2,1)}, u32[]{:S(2)}, u32[]{:S(2)}) collective-permute-start(bf16[512,384]{1,0:T(8,128)(2,1)} %bitcast.153), channel_id=1, source_target_pairs={{2,1},{1,2},{6,5},{5,6},{10,9},{9,10},{14,13},{13,14},{18,17},{17,... | collective-permute-start | bytes 1179656 | tf_op jit(solution)/shard_map/ppermute | solution.py:90
  3.9 2.8 %copy-start.1 = (bf16[1,512,384]{2,1,0:T(8,128)(2,1)S(1)}, bf16[1,512,384]{2,1,0:T(8,128)(2,1)}, u32[]{:S(2)}) copy-start(bf16[1,512,384]{2,1,0:T(8,128)(2,1)} %param.5) | copy-start | bytes 1179652
  7.7 11.6 %collective-permute-start.1 = (bf16[2,256,384]{2,1,0:T(8,128)(2,1)}, bf16[2,256,384]{2,1,0:T(8,128)(2,1)}, u32[]{:S(2)}, u32[]{:S(2)}) collective-permute-start(bf16[2,256,384]{2,1,0:T(8,128)(2,1)} %get-tuple-element.22), channel_id=1, source_target_pairs={{4,0},{8,4},{12,8},{5,1},{9,5},{13,9},{6,2},{10,6},{14,10},{7,3},{... | collective-permute-start | bytes 1179656 | tf_op jit(solution)/shard_map/ppermute | solution.py:12
  9.0 14.9 %collective-permute-start = (bf16[2,256,384]{2,1,0:T(8,128)(2,1)}, bf16[2,256,384]{2,1,0:T(8,128)(2,1)S(1)}, u32[]{:S(2)}, u32[]{:S(2)}) collective-permute-start(bf16[2,256,384]{2,1,0:T(8,128)(2,1)} %get-tuple-element.21), channel_id=1, source_target_pairs={{0,4},{4,8},{8,12},{1,5},{5,9},{9,13},{2,6},{6,10},{10,14},{3,7},{... | collective-permute-start | bytes 1179656 | tf_op jit(solution)/shard_map/ppermute | solution.py:12
  19.2 14.2 %collective-permute-start.5 = (bf16[512,384]{1,0:T(8,128)(2,1)S(1)}, bf16[512,384]{1,0:T(8,128)(2,1)S(1)}, u32[]{:S(2)}, u32[]{:S(2)}) collective-permute-start(bf16[512,384]{1,0:T(8,128)(2,1)S(1)} %get-tuple-element.29), channel_id=1, source_target_pairs={{0,2},{2,0},{1,3},{3,1},{4,6},{6,4},{5,7},{7,5},{8,10},{10,8},{9,1... | collective-permute-start | bytes 1179656 | tf_op jit(solution)/shard_map/ppermute | solution.py:92
  23.9 56.0 %collective-permute-start.3 = (bf16[1664,384]{1,0:T(8,128)(2,1)S(1)}, bf16[1664,384]{1,0:T(8,128)(2,1)S(1)}, u32[]{:S(2)}, u32[]{:S(2)}) collective-permute-start(bf16[1664,384]{1,0:T(8,128)(2,1)S(1)} %pad_maximum_fusion.1), channel_id=1, source_target_pairs={{0,1},{1,0},{2,3},{3,2},{4,5},{5,4},{6,7},{7,6},{8,9},{9,8},{10,11... | collective-permute-start | bytes 3833864 | tf_op jit(solution)/shard_map/ppermute | solution.py:97
  25.3 54.6 %collective-permute-start.2 = (bf16[2,2,256,384]{3,2,1,0:T(8,128)(2,1)S(1)}, bf16[2,2,256,384]{3,2,1,0:T(8,128)(2,1)S(1)}, u32[]{:S(2)}, u32[]{:S(2)}) collective-permute-start(bf16[2,2,256,384]{3,2,1,0:T(8,128)(2,1)S(1)} %pad_maximum_fusion.3), channel_id=1, source_target_pairs={{0,1},{1,0},{2,3},{3,2},{4,5},{5,4},{6,7},{7,6},{8,9},{9,8},{10,11... | collective-permute-start | bytes 2359304 | tf_op jit(solution)/shard_map/ppermute | solution.py:104
  26.7 12.8 %collective-permute-start.9 = (bf16[256,384]{1,0:T(8,128)(2,1)S(1)}, bf16[256,384]{1,0:T(8,128)(2,1)S(1)}, u32[]{:S(2)}, u32[]{:S(2)}) collective-permute-start(bf16[256,384]{1,0:T(8,128)(2,1)S(1)} %get-tuple-element.25), channel_id=1, source_target_pairs={{0,4},{4,8},{8,12},{1,5},{5,9},{9,13},{2,6},{6,10},{10,14},{3,7},{... | collective-permute-start | bytes 589832 | tf_op jit(solution)/shard_map/ppermute | solution.py:12
  33.4 9.7 %collective-permute-start.8 = (bf16[256,384]{1,0:T(8,128)(2,1)S(1)}, bf16[256,384]{1,0:T(8,128)(2,1)S(1)}, u32[]{:S(2)}, u32[]{:S(2)}) collective-permute-start(bf16[256,384]{1,0:T(8,128)(2,1)S(1)} %get-tuple-element.26), channel_id=1, source_target_pairs={{4,0},{8,4},{12,8},{5,1},{9,5},{13,9},{6,2},{10,6},{14,10},{7,3},{... | collective-permute-start | bytes 589832 | tf_op jit(solution)/shard_map/ppermute | solution.py:12
  35.6 13.3 %collective-permute-start.14 = (f32[2,96,384]{2,1,0:T(8,128)S(1)}, f32[2,96,384]{2,1,0:T(8,128)S(1)}, u32[]{:S(2)}, u32[]{:S(2)}) collective-permute-start(f32[2,96,384]{2,1,0:T(8,128)S(1)} %select_bitcast_fusion.1), channel_id=1, source_target_pairs={{0,4},{4,0},{8,12},{12,8},{1,5},{5,1},{9,13},{13,9},{2,6},{6,2},{1... | collective-permute-start | bytes 884744 | tf_op jit(solution)/shard_map/ppermute | solution.py:58
  48.9 9.2 %collective-permute-start.15 = (f32[96,384]{1,0:T(8,128)S(1)}, f32[96,384]{1,0:T(8,128)S(1)}, u32[]{:S(2)}, u32[]{:S(2)}) collective-permute-start(f32[96,384]{1,0:T(8,128)S(1)} %select_bitcast_fusion.7), channel_id=1, source_target_pairs={{0,8},{8,0},{4,12},{12,4},{1,9},{9,1},{5,13},{13,5},{2,10},{10,2},... | collective-permute-start | bytes 442376 | tf_op jit(solution)/shard_map/ppermute | solution.py:63
  58.2 6.0 %collective-permute-start.16 = (bf16[96,384]{1,0:T(8,128)(2,1)S(1)}, bf16[96,384]{1,0:T(8,128)(2,1)S(1)}, u32[]{:S(2)}, u32[]{:S(2)}) collective-permute-start(bf16[96,384]{1,0:T(8,128)(2,1)S(1)} %fusion.65), channel_id=1, source_target_pairs={{0,8},{8,0},{4,12},{12,4},{1,9},{9,1},{5,13},{13,5},{2,10},{10,2},... | collective-permute-start | bytes 221192 | tf_op jit(solution)/shard_map/ppermute | solution.py:64
  58.3 20.2 %collective-permute-start.10 = (f32[2,192,384]{2,1,0:T(8,128)S(1)}, f32[2,192,384]{2,1,0:T(8,128)S(1)}, u32[]{:S(2)}, u32[]{:S(2)}) collective-permute-start(f32[2,192,384]{2,1,0:T(8,128)S(1)} %select_bitcast_fusion), channel_id=1, source_target_pairs={{0,4},{4,0},{8,12},{12,8},{1,5},{5,1},{9,13},{13,9},{2,6},{6,2},{1... | collective-permute-start | bytes 1769480 | tf_op jit(solution)/shard_map/ppermute | solution.py:58
  64.2 14.1 %collective-permute-start.17 = (bf16[2,96,384]{2,1,0:T(8,128)(2,1)S(1)}, bf16[2,96,384]{2,1,0:T(8,128)(2,1)S(1)}, u32[]{:S(2)}, u32[]{:S(2)}) collective-permute-start(bf16[2,96,384]{2,1,0:T(8,128)(2,1)S(1)} %maximum_select_fusion.1), channel_id=1, source_target_pairs={{0,4},{4,0},{8,12},{12,8},{1,5},{5,1},{9,13},{13,9},{2,6},{6,2},{1... | collective-permute-start | bytes 442376 | tf_op jit(solution)/shard_map/ppermute | solution.py:66
  78.7 14.1 %collective-permute-start.11 = (f32[192,384]{1,0:T(8,128)S(1)}, f32[192,384]{1,0:T(8,128)S(1)}, u32[]{:S(2)}, u32[]{:S(2)}) collective-permute-start(f32[192,384]{1,0:T(8,128)S(1)} %select_bitcast_fusion.4), channel_id=1, source_target_pairs={{0,8},{8,0},{4,12},{12,4},{1,9},{9,1},{5,13},{13,5},{2,10},{10,2},... | collective-permute-start | bytes 884744 | tf_op jit(solution)/shard_map/ppermute | solution.py:63
  80.0 2.0 %copy-start.2 = (bf16[1664,384]{1,0:T(8,128)(2,1)}, bf16[1664,384]{1,0:T(8,128)(2,1)S(1)}, u32[]{:S(2)}) copy-start(bf16[1664,384]{1,0:T(8,128)(2,1)S(1)} %collective-permute-done.3) | copy-start | bytes 3833860
  80.9 12.5 %copy-start.6 = (f32[512,384]{1,0:T(8,128)S(1)}, f32[512,384]{1,0:T(8,128)}, u32[]{:S(2)}) copy-start(f32[512,384]{1,0:T(8,128)} %get-tuple-element.30) | copy-start | bytes 2359300
  93.4 9.6 %collective-permute-start.12 = (bf16[192,384]{1,0:T(8,128)(2,1)}, bf16[192,384]{1,0:T(8,128)(2,1)S(1)}, u32[]{:S(2)}, u32[]{:S(2)}) collective-permute-start(bf16[192,384]{1,0:T(8,128)(2,1)} %fusion.64), channel_id=1, source_target_pairs={{0,8},{8,0},{4,12},{12,4},{1,9},{9,1},{5,13},{13,5},{2,10},{10,2},... | collective-permute-start | bytes 442376 | tf_op jit(solution)/shard_map/ppermute | solution.py:64
  96.3 7.8 %slice-start = ((bf16[1664,384]{1,0:T(8,128)(2,1)}), bf16[1152,384]{1,0:T(8,128)(2,1)S(1)}, s32[]{:S(2)}) async-start(bf16[1664,384]{1,0:T(8,128)(2,1)} %copy-done.2), calls=%async_computation | async-start | bytes 1769472 | tf_op jit(solution)/shard_map/slice | solution.py:101
  96.4 7.8 %copy-start.3 = (bf16[512,1,384]{2,0,1:T(8,128)(2,1)S(1)}, bf16[512,1,384]{2,0,1:T(8,128)(2,1)}, u32[]{:S(2)}) copy-start(bf16[512,1,384]{2,0,1:T(8,128)(2,1)} %get-tuple-element.8) | copy-start | bytes 1179652
  96.4 7.8 %copy-start.4 = (bf16[512,1,384]{2,0,1:T(8,128)(2,1)S(1)}, bf16[512,1,384]{2,0,1:T(8,128)(2,1)}, u32[]{:S(2)}) copy-start(bf16[512,1,384]{2,0,1:T(8,128)(2,1)} %get-tuple-element.15) | copy-start | bytes 1179652
  96.4 7.8 %copy-start.5 = (bf16[512,1,384]{2,0,1:T(8,128)(2,1)S(1)}, bf16[512,1,384]{2,0,1:T(8,128)(2,1)}, u32[]{:S(2)}) copy-start(bf16[512,1,384]{2,0,1:T(8,128)(2,1)} %get-tuple-element.3) | copy-start | bytes 1179652
  104.0 9.0 %collective-permute-start.13 = (bf16[2,192,384]{2,1,0:T(8,128)(2,1)S(1)}, bf16[2,192,384]{2,1,0:T(8,128)(2,1)S(1)}, u32[]{:S(2)}, u32[]{:S(2)}) collective-permute-start(bf16[2,192,384]{2,1,0:T(8,128)(2,1)S(1)} %maximum_select_fusion), channel_id=1, source_target_pairs={{0,4},{4,0},{8,12},{12,8},{1,5},{5,1},{9,13},{13,9},{2,6},{6,2},{1... | collective-permute-start | bytes 884744 | tf_op jit(solution)/shard_map/ppermute | solution.py:66

commit v21 on v11

--- a/solution.py
+++ b/solution.py
@@ -45,6 +45,22 @@
             ready = pairs[step - 1]
             wholes[step - 1] = ready + lax.ppermute(ready, "seq", middle)
     return [totals[n] for n in range(count)]
+
+
+def direct_total(block):
+    s = lax.axis_index("seq")
+    rows = block.shape[0] // 4
+    quarters = block.reshape(4, rows, block.shape[1])
+    mine = lax.dynamic_index_in_dim(quarters, s, 0, keepdims=False)
+    for d in range(1, 4):
+        going = lax.dynamic_index_in_dim(quarters, (s + d) % 4, 0, keepdims=False)
+        mine = mine + lax.ppermute(going, "seq", [(j, (j + d) % 4) for j in range(4)])
+    mine = mine.astype(jnp.bfloat16)
+    gathered = [mine] + [
+        lax.ppermute(mine, "seq", [(j, (j + d) % 4) for j in range(4)]) for d in range(1, 4)
+    ]
+    order = (s - jnp.arange(4)) % 4
+    return jnp.take(jnp.stack(gathered), order, axis=0).reshape(block.shape).astype(jnp.float32)
 
 
 def line_total(block):
@@ -143,7 +159,7 @@
                 own_taps[:, k].T, cot_mine, preferred_element_type=jnp.float32
             ) + jnp.dot(far_mid.T, far_shifted[k], preferred_element_type=jnp.float32)
         if seq_count == 4:
-            middle = line_total(grads[1])
+            middle = direct_total(grads[1])
             sides = line_total(jnp.concatenate([grads[0], grads[2]], 0))
             weight_grad = jnp.stack([sides[: middle.shape[0]], middle, sides[middle.shape[0] :]])
         else:

time: 103 us -> 109 us (1.058)
  local copies, waits for them, and re-layouts: 6.93 us -> 12.6 us
  other arithmetic: 9.42 us -> 13.6 us
  waiting for transfers between devices: 42.3 us -> 38.9 us
  matrix products: 11.5 us -> 9.63 us
  starting transfers between devices: 31.2 us -> 32.7 us
    ppermute x2 -> x1, waiting for transfers between devices: 0.01 us -> 12.3 us  [line_total(): total = (keep + lax.ppermute(give, 'seq', across)).astype(jnp.bfloat16)]
    ppermute x2 -> x1, waiting for transfers between devices: 16.6 us -> 4.62 us  [line_total(): other = lax.ppermute(total, 'seq', across)]
    ppermute x0 -> x6, starting transfers between devices: none -> 10.1 us  [the longest x3 5.87 us: direct_total(): lax.ppermute(mine, 'seq', [(j, (j + d) % 4) for j in range(4)])]
    ppermute x2 -> x1, starting transfers between devices: 5.92 us -> 0.07 us  [line_total(): other = lax.ppermute(total, 'seq', across)]
    ppermute x2 -> x1, waiting for transfers between devices: 10.9 us -> 6.17 us  [line_total(): lax.ppermute(jnp.where(odd, even_set, odd_set), 'seq', pairs)]
    ppermute x2 -> x1, starting transfers between devices: 2.16 us -> 0.16 us  [line_total(): lax.ppermute(jnp.where(odd, even_set, odd_set), 'seq', pairs)]
    dot_general x3, matrix products: 3.05 us -> 1.19 us  [shards(): jnp.dot(own_taps[:, k].T, cot_mine, preferred_element_type=jnp.float32)]
    convert_element_type x1, local copies, waits for them, and re-layouts: 1.17 us -> 2.95 us  [shards(): input_grad = jnp.repeat(0.5 * pooled_grad, 2, axis=0).astype(jnp.bfloat16)]
  transfers between devices with their start and end apart: 17 -> 19, of which waited for: 7 -> 9; matrix products, arithmetic and copies ran while one was open for 22% -> 26% of each run, Pallas kernels for 0% -> 0%
where the time goes in v21:
time: 109 us; the launch traced here: 108 us
  waiting for transfers between devices  38.9 us (36%)
  starting transfers between devices  32.7 us (30%)
  other arithmetic  13.6 us (12%)
  local copies, waits for them, and re-layouts  12.6 us (12%)
  matrix products  9.63 us (9%)
    ppermute x1, waiting for transfers between devices, line_total(): total = (keep + lax.ppermute(give, 'seq', across)).astype(jnp.bfloat16)  12.3 us
    ppermute x4, starting transfers between devices, shift_from(): return lax.ppermute(block, axis, route)  11 us
    ppermute x4, waiting for transfers between devices, shift_from(): return lax.ppermute(block, axis, route)  6.93 us
    ppermute x1, waiting for transfers between devices, line_total(): far_set = lax.ppermute(own_set, 'seq', pairs)  6.68 us
    ppermute x1, waiting for transfers between devices, line_total(): lax.ppermute(jnp.where(odd, even_set, odd_set), 'seq', pairs)  6.17 us
    ppermute x3, starting transfers between devices, direct_total(): lax.ppermute(mine, 'seq', [(j, (j + d) % 4) for j in range(4)])  5.87 us
    ppermute x1, waiting for transfers between devices, line_total(): other = lax.ppermute(total, 'seq', across)  4.62 us
    ppermute x3, starting transfers between devices, direct_total(): lax.ppermute(going, 'seq', [(j, (j + d) % 4) for j in range(4)])  4.23 us
  transfers between devices with their start and end apart: 19, of which 9 were waited for; matrix products, arithmetic and copies ran while one was open for 26% of the time, Pallas kernels for 0%

profile of v21, /device:TPU:0, one launch (start us, length us, event | category | flops | bytes accessed | tf_op | source)
XLA Modules:
  0.0 108.4 jit_solution(11498344355102485261)
XLA Ops:
  0.6 1.4 %collective-permute-start.5 = (bf16[512,384]{1,0:T(8,128)(2,1)}, bf16[512,384]{1,0:T(8,128)(2,1)}, u32[]{:S(2)}, u32[]{:S(2)}) collective-permute-start(bf16[512,384]{1,0:T(8,128)(2,1)} %bitcast.151), channel_id=1, source_target_pairs={{2,0},{1,3},{6,4},{5,7},{10,8},{9,11},{14,12},{13,15},{18,16},{17,... | collective-permute-start | bytes 1179656 | tf_op jit(solution)/shard_map/ppermute | solution.py:104
  2.1 1.4 %collective-permute-start.6 = (bf16[512,384]{1,0:T(8,128)(2,1)}, bf16[512,384]{1,0:T(8,128)(2,1)}, u32[]{:S(2)}, u32[]{:S(2)}) collective-permute-start(bf16[512,384]{1,0:T(8,128)(2,1)} %bitcast.152), channel_id=1, source_target_pairs={{2,1},{1,2},{6,5},{5,6},{10,9},{9,10},{14,13},{13,14},{18,17},{17,... | collective-permute-start | bytes 1179656 | tf_op jit(solution)/shard_map/ppermute | solution.py:105
  3.5 2.8 %multiply_convert_fusion = (bf16[512,384]{1,0:T(8,128)(2,1)S(1)}, f32[512,384]{1,0:T(8,128)}) fusion(bf16[1,1024,384]{2,1,0:T(8,128)(2,1)} %param.3, s32[1024]{0:T(1024)S(1)} %get-tuple-element.33, s32[1024]{0:T(1024)S(1)} %get-tuple-element.34, pred[1024]{0:T(1024)(128)(4,1)S(1)} %fusion.73), kind=kOutput, calls=%fused_computation.62 | convolution fusion | flops 406519808 | bytes 1975296 | tf_op jit(solution)/shard_map/dot_general | solution.py:99
  6.3 1.0 fusion.47
  7.3 5.0 %collective-permute-start = (bf16[2,256,384]{2,1,0:T(8,128)(2,1)}, bf16[2,256,384]{2,1,0:T(8,128)(2,1)S(1)}, u32[]{:S(2)}, u32[]{:S(2)}) collective-permute-start(bf16[2,256,384]{2,1,0:T(8,128)(2,1)} %get-tuple-element.21), channel_id=1, source_target_pairs={{0,4},{4,8},{8,12},{1,5},{5,9},{9,13},{2,6},{6,10},{10,14},{3,7},{... | collective-permute-start | bytes 1179656 | tf_op jit(solution)/shard_map/ppermute | solution.py:12
  12.3 1.3 %collective-permute-start.1 = (bf16[2,256,384]{2,1,0:T(8,128)(2,1)}, bf16[2,256,384]{2,1,0:T(8,128)(2,1)S(1)}, u32[]{:S(2)}, u32[]{:S(2)}) collective-permute-start(bf16[2,256,384]{2,1,0:T(8,128)(2,1)} %get-tuple-element.22), channel_id=1, source_target_pairs={{4,0},{8,4},{12,8},{5,1},{9,5},{13,9},{6,2},{10,6},{14,10},{7,3},{... | collective-permute-start | bytes 1179656 | tf_op jit(solution)/shard_map/ppermute | solution.py:12
  13.6 1.0 pad_maximum_fusion.3
  14.7 1.3 %copy-done.5 = bf16[2,512,384]{2,1,0:T(8,128)(2,1)S(1)} copy-done((bf16[2,512,384]{2,1,0:T(8,128)(2,1)S(1)}, bf16[2,512,384]{2,1,0:T(8,128)(2,1)}, u32[]{:S(2)}) %copy-start.5) | copy-done | bytes 786456
  16.0 1.3 %pad_maximum_fusion.1 = bf16[2176,384]{1,0:T(8,128)(2,1)} fusion(bf16[1152,384]{1,0:T(8,128)(2,1)S(1)} %bitcast.154, bf16[1024,384]{1,0:T(8,128)(2,1)S(1)} %bitcast.157), kind=kLoop, calls=%fused_computation.4 | loop fusion | flops 3342336 | bytes 3342336 | tf_op jit(solution)/shard_map/concatenate | solution.py:113
  17.4 3.7 %collective-permute-start.3 = (bf16[2176,384]{1,0:T(8,128)(2,1)}, bf16[2176,384]{1,0:T(8,128)(2,1)}, u32[]{:S(2)}, u32[]{:S(2)}) collective-permute-start(bf16[2176,384]{1,0:T(8,128)(2,1)} %pad_maximum_fusion.1), channel_id=1, source_target_pairs={{0,1},{1,0},{2,3},{3,2},{4,5},{5,4},{6,7},{7,6},{8,9},{9,8},{10,11... | collective-permute-start | bytes 5013512 | tf_op jit(solution)/shard_map/ppermute | solution.py:112
  21.3 1.1 %collective-permute-start.4 = (bf16[512,384]{1,0:T(8,128)(2,1)S(1)}, bf16[512,384]{1,0:T(8,128)(2,1)S(1)}, u32[]{:S(2)}, u32[]{:S(2)}) collective-permute-start(bf16[512,384]{1,0:T(8,128)(2,1)S(1)} %get-tuple-element.31), channel_id=1, source_target_pairs={{0,2},{2,0},{1,3},{3,1},{4,6},{6,4},{5,7},{7,5},{8,10},{10,8},{9,1... | collective-permute-start | bytes 1179656 | tf_op jit(solution)/shard_map/ppermute | solution.py:107
  22.4 1.2 %collective-permute-done.1 = bf16[2,256,384]{2,1,0:T(8,128)(2,1)S(1)} collective-permute-done((bf16[2,256,384]{2,1,0:T(8,128)(2,1)}, bf16[2,256,384]{2,1,0:T(8,128)(2,1)S(1)}, u32[]{:S(2)}, u32[]{:S(2)}) %collective-permute-start.1) | collective-permute-done | bytes 393248 | tf_op jit(solution)/shard_map/ppermute | solution.py:12
  23.8 2.9 %collective-permute-start.2 = (bf16[2,2,256,384]{3,2,1,0:T(8,128)(2,1)S(1)}, bf16[2,2,256,384]{3,2,1,0:T(8,128)(2,1)S(1)}, u32[]{:S(2)}, u32[]{:S(2)}) collective-permute-start(bf16[2,2,256,384]{3,2,1,0:T(8,128)(2,1)S(1)} %pad_maximum_fusion.4), channel_id=1, source_target_pairs={{0,1},{1,0},{2,3},{3,2},{4,5},{5,4},{6,7},{7,6},{8,9},{9,8},{10,11... | collective-permute-start | bytes 2359304 | tf_op jit(solution)/shard_map/ppermute | solution.py:119
  26.7 1.0 broadcast_select_fusion
  27.8 3.5 %collective-permute-start.8 = (bf16[256,384]{1,0:T(8,128)(2,1)S(1)}, bf16[256,384]{1,0:T(8,128)(2,1)S(1)}, u32[]{:S(2)}, u32[]{:S(2)}) collective-permute-start(bf16[256,384]{1,0:T(8,128)(2,1)S(1)} %get-tuple-element.29), channel_id=1, source_target_pairs={{0,4},{4,8},{8,12},{1,5},{5,9},{9,13},{2,6},{6,10},{10,14},{3,7},{... | collective-permute-start | bytes 589832 | tf_op jit(solution)/shard_map/ppermute | solution.py:12
  31.3 1.3 %collective-permute-start.7 = (bf16[256,384]{1,0:T(8,128)(2,1)S(1)}, bf16[256,384]{1,0:T(8,128)(2,1)S(1)}, u32[]{:S(2)}, u32[]{:S(2)}) collective-permute-start(bf16[256,384]{1,0:T(8,128)(2,1)S(1)} %get-tuple-element.30), channel_id=1, source_target_pairs={{4,0},{8,4},{12,8},{5,1},{9,5},{13,9},{6,2},{10,6},{14,10},{7,3},{... | collective-permute-start | bytes 589832 | tf_op jit(solution)/shard_map/ppermute | solution.py:12
  32.6 0.7 collective-permute-done.4
  33.6 2.0 %collective-permute-done.8 = bf16[256,384]{1,0:T(8,128)(2,1)S(1)} collective-permute-done((bf16[256,384]{1,0:T(8,128)(2,1)S(1)}, bf16[256,384]{1,0:T(8,128)(2,1)S(1)}, u32[]{:S(2)}, u32[]{:S(2)}) %collective-permute-start.8) | collective-permute-done | bytes 196640 | tf_op jit(solution)/shard_map/ppermute | solution.py:12
  36.0 3.7 %collective-permute-done.7 = bf16[256,384]{1,0:T(8,128)(2,1)S(1)} collective-permute-done((bf16[256,384]{1,0:T(8,128)(2,1)S(1)}, bf16[256,384]{1,0:T(8,128)(2,1)S(1)}, u32[]{:S(2)}, u32[]{:S(2)}) %collective-permute-start.7) | collective-permute-done | bytes 196640 | tf_op jit(solution)/shard_map/ppermute | solution.py:12
  40.2 2.1 %fusion.52 = (bf16[512,1,384]{2,0,1:T(8,128)(2,1)S(1)}, bf16[512,1,384]{2,0,1:T(8,128)(2,1)}, bf16[512,1,384]{2,0,1:T(8,128)(2,1)}, bf16[512,1,384]{2,0,1:T(8,128)(2,1)S(1)}, bf16[1,512,384]{2,1,0:T(8,128)(2,1)S(1)}) fusion(bf16[2,256,384]{2,1,0:T(8,128)(2,1)S(1)} %collective-permute-done.1, bf16[1,512,384]{2,1,0:T(8,128)(2,1)S(1)} %copy-done.1, ...), kind=kLoop, calls=%fused_computation.80 | loop fusion | flops 4915200 | bytes 3932161 | tf_op jit(solution)/shard_map/stack | solution.py:21
  42.7 0.8 dynamic-slice_bitcast_fusion.2
  43.6 1.6 %collective-permute-start.13 = (f32[96,384]{1,0:T(8,128)}, f32[96,384]{1,0:T(8,128)S(1)}, u32[]{:S(2)}, u32[]{:S(2)}) collective-permute-start(f32[96,384]{1,0:T(8,128)} %get-tuple-element.23), channel_id=1, source_target_pairs={{0,4},{4,8},{8,12},{12,0},{1,5},{5,9},{9,13},{13,1},{2,6},{6,10},{... | collective-permute-start | bytes 442376 | tf_op jit(solution)/shard_map/ppermute | solution.py:57
  45.2 2.7 %collective-permute-start.15 = (f32[96,384]{1,0:T(8,128)}, f32[96,384]{1,0:T(8,128)}, u32[]{:S(2)}, u32[]{:S(2)}) collective-permute-start(f32[96,384]{1,0:T(8,128)} %get-tuple-element.24), channel_id=1, source_target_pairs={{0,12},{4,0},{8,4},{12,8},{1,13},{5,1},{9,5},{13,9},{2,14},{6,2},{... | collective-permute-start | bytes 442376 | tf_op jit(solution)/shard_map/ppermute | solution.py:57
  48.7 0.9 select_bitcast_fusion
  49.8 1.2 %slice.168 = bf16[1024,384]{1,0:T(8,128)(2,1)S(1)} slice(bf16[2176,384]{1,0:T(8,128)(2,1)} %collective-permute-done.3), slice={[0:1024], [0:384]} | slice | bytes 1572864 | tf_op jit(solution)/shard_map/slice | solution.py:115
  51.0 1.1 fusion.50
  52.0 2.0 %slice_bitcast_fusion.3 = (bf16[512,1,384]{2,0,1:T(8,128)(2,1)S(1)}, bf16[512,1,384]{2,0,1:T(8,128)(2,1)}) fusion(bf16[2176,384]{1,0:T(8,128)(2,1)} %collective-permute-done.3), kind=kLoop, calls=%fused_computation.104 | loop fusion | bytes 1572864 | tf_op jit(solution)/shard_map/stack | solution.py:21
  54.1 0.8 convolution_bitcast_fusion
  55.4 1.3 %fusion.39 = bf16[512,384]{1,0:T(8,128)(2,1)S(1)} fusion(f32[512,384]{1,0:T(8,128)S(1)} %copy-done.12, f32[512,384]{1,0:T(8,128)S(1)} %convolution_bitcast_fusion, bf16[512,1,384]{2,0,1:T(8,128)(2,1)S(1)} %get-tuple-element.16, bf16[512,1,384]{2,0,1:T(8,128)(2,1)S(1)} %bitcast.153, bf16[512,1,384]{2,0,1:T(8,128)(2,1)S(1)} %get-tuple-element.7, ...), kind=kOutput, calls=%fused_computation.59 | convolution fusion | flops 458883072 | bytes 4423684 | tf_op jit(solution)/shard_map/tko,kio->ti/dot_general | solution.py:132
  56.7 1.3 %broadcast_in_dim.32 = bf16[512,2,384]{2,1,0:T(2,128)(2,1)} broadcast(bf16[512,384]{1,0:T(8,128)(2,1)S(1)} %fusion.39), dimensions={0,2} | broadcast | bytes 1179648 | tf_op jit(solution)/shard_map/broadcast_in_dim | solution.py:141
  58.0 3.0 %convert_element_type.51 = bf16[1,1024,384]{2,1,0:T(8,128)(2,1)} reshape(bf16[512,2,384]{2,1,0:T(2,128)(2,1)} %broadcast_in_dim.32) | data formatting | bytes 1572864 | tf_op jit(solution)/shard_map/convert_element_type | solution.py:141
  60.9 1.3 %slice.171 = bf16[1152,384]{1,0:T(8,128)(2,1)S(1)} slice(bf16[2176,384]{1,0:T(8,128)(2,1)} %collective-permute-done.3), slice={[1024:2176], [0:384]} | slice | bytes 1769472 | tf_op jit(solution)/shard_map/slice | solution.py:116
  62.3 0.8 convolution_bitcast_fusion.3
  63.1 6.2 %collective-permute-done.9 = f32[2,192,384]{2,1,0:T(8,128)} collective-permute-done((f32[2,192,384]{2,1,0:T(8,128)}, f32[2,192,384]{2,1,0:T(8,128)}, u32[]{:S(2)}, u32[]{:S(2)}) %collective-permute-start.9) | collective-permute-done | bytes 589856 | tf_op jit(solution)/shard_map/ppermute | solution.py:74
  69.3 1.1 %fusion.46 = f32[2,192,384]{2,1,0:T(8,128)S(1)} fusion(f32[2,192,384]{2,1,0:T(8,128)} %collective-permute-done.9, f32[2,2,192,384]{3,2,1,0:T(8,128)S(1)} %bitcast.150, pred[]{:T(512)S(6)} %eq.18), kind=kLoop, calls=%fused_computation.68 | loop fusion | flops 294912 | bytes 2359297 | tf_op jit(solution)/shard_map/add | solution.py:74
  70.5 0.7 collective-permute-start.10
  71.2 1.6 %fusion.4 = bf16[1,512,384]{2,1,0:T(8,128)(2,1)} fusion(f32[512,384]{1,0:T(8,128)S(1)} %copy-done.13, f32[512,384]{1,0:T(8,128)S(1)} %convolution_bitcast_fusion.3, bf16[3,384,384]{2,1,0:T(8,128)(2,1)S(1)} %bitcast.166, bf16[512,1,384]{2,0,1:T(8,128)(2,1)S(1)} %copy-done.9, bf16[512,1,384]{2,0,1:T(8,128)(2,1)S(1)} %copy-done.11, ...), kind=kOutput, calls=%fused_computation.16 | convolution fusion | flops 454754304 | bytes 4030464 | tf_op jit(solution)/shard_map/tki,kio->to/dot_general | solution.py:126
  72.7 12.3 %collective-permute-done.10 = f32[192,384]{1,0:T(8,128)S(1)} collective-permute-done((f32[192,384]{1,0:T(8,128)S(1)}, f32[192,384]{1,0:T(8,128)S(1)}, u32[]{:S(2)}, u32[]{:S(2)}) %collective-permute-start.10) | collective-permute-done | bytes 294944 | tf_op jit(solution)/shard_map/ppermute | solution.py:79
  85.2 1.1 %fusion.70 = bf16[96,384]{1,0:T(8,128)(2,1)S(1)} fusion(f32[96,384]{1,0:T(8,128)} %collective-permute-done.15, f32[96,384]{1,0:T(8,128)} %collective-permute-done.14, f32[96,384]{1,0:T(8,128)S(1)} %collective-permute-done.13, f32[4,96,384]{2,1,0:T(8,128)} %bitcast.162, s32[]{:T(128)S(6)} %select_n.192), kind=kLoop, calls=%fused_computation.117 | loop fusion | flops 147456 | bytes 663556 | tf_op jit(solution)/shard_map/convert_element_type | solution.py:58
  86.3 2.3 %collective-permute-start.16 = (bf16[96,384]{1,0:T(8,128)(2,1)S(1)}, bf16[96,384]{1,0:T(8,128)(2,1)S(1)}, u32[]{:S(2)}, u32[]{:S(2)}) collective-permute-start(bf16[96,384]{1,0:T(8,128)(2,1)S(1)} %fusion.70), channel_id=1, source_target_pairs={{0,4},{4,8},{8,12},{12,0},{1,5},{5,9},{9,13},{13,1},{2,6},{6,10},{... | collective-permute-start | bytes 221192 | tf_op jit(solution)/shard_map/ppermute | solution.py:60
  88.6 0.7 collective-permute-start.17
  89.4 2.8 %collective-permute-start.18 = (bf16[96,384]{1,0:T(8,128)(2,1)S(1)}, bf16[96,384]{1,0:T(8,128)(2,1)S(1)}, u32[]{:S(2)}, u32[]{:S(2)}) collective-permute-start(bf16[96,384]{1,0:T(8,128)(2,1)S(1)} %fusion.70), channel_id=1, source_target_pairs={{0,12},{4,0},{8,4},{12,8},{1,13},{5,1},{9,5},{13,9},{2,14},{6,2},{... | collective-permute-start | bytes 221192 | tf_op jit(solution)/shard_map/ppermute | solution.py:60
  92.2 4.6 %collective-permute-done.11 = bf16[192,384]{1,0:T(8,128)(2,1)S(1)} collective-permute-done((bf16[192,384]{1,0:T(8,128)(2,1)S(1)}, bf16[192,384]{1,0:T(8,128)(2,1)S(1)}, u32[]{:S(2)}, u32[]{:S(2)}) %collective-permute-start.11) | collective-permute-done | bytes 147488 | tf_op jit(solution)/shard_map/ppermute | solution.py:80
  97.0 1.4 %collective-permute-done.17 = bf16[96,384]{1,0:T(8,128)(2,1)S(1)} collective-permute-done((bf16[96,384]{1,0:T(8,128)(2,1)S(1)}, bf16[96,384]{1,0:T(8,128)(2,1)S(1)}, u32[]{:S(2)}, u32[]{:S(2)}) %collective-permute-start.17) | collective-permute-done | bytes 73760 | tf_op jit(solution)/shard_map/ppermute | solution.py:60
  98.5 0.6 gather_fusion
  99.2 6.7 %collective-permute-done.12 = bf16[2,192,384]{2,1,0:T(8,128)(2,1)} collective-permute-done((bf16[2,192,384]{2,1,0:T(8,128)(2,1)S(1)}, bf16[2,192,384]{2,1,0:T(8,128)(2,1)}, u32[]{:S(2)}, u32[]{:S(2)}) %collective-permute-start.12) | collective-permute-done | bytes 294944 | tf_op jit(solution)/shard_map/ppermute | solution.py:82
  105.9 1.1 select_bitcast_fusion.2
  107.1 1.3 %pad_maximum_fusion = f32[3,384,384]{2,1,0:T(8,128)} fusion(f32[1,384,384]{2,1,0:T(8,128)S(1)} %bitcast.160, f32[1,384,384]{2,1,0:T(8,128)S(1)} %fusion.66, f32[1,384,384]{2,1,0:T(8,128)S(1)} %bitcast.159), kind=kLoop, calls=%fused_computation.3 | loop fusion | flops 884736 | bytes 3538944 | tf_op jit(solution)/shard_map/stack | solution.py:164
  (66 shorter events, 4.2 us)
Async XLA Ops:
  0.6 14.0 %copy-start = (bf16[3,384,768]{2,1,0:T(8,128)(2,1)S(1)}, bf16[3,384,768]{2,1,0:T(8,128)(2,1)}, u32[]{:S(2)}) copy-start(bf16[3,384,768]{2,1,0:T(8,128)(2,1)} %param.4) | copy-start | bytes 5308420
  0.6 26.0 %collective-permute-start.5 = (bf16[512,384]{1,0:T(8,128)(2,1)}, bf16[512,384]{1,0:T(8,128)(2,1)}, u32[]{:S(2)}, u32[]{:S(2)}) collective-permute-start(bf16[512,384]{1,0:T(8,128)(2,1)} %bitcast.151), channel_id=1, source_target_pairs={{2,0},{1,3},{6,4},{5,7},{10,8},{9,11},{14,12},{13,15},{18,16},{17,... | collective-permute-start | bytes 1179656 | tf_op jit(solution)/shard_map/ppermute | solution.py:104
  2.1 24.6 %collective-permute-start.6 = (bf16[512,384]{1,0:T(8,128)(2,1)}, bf16[512,384]{1,0:T(8,128)(2,1)}, u32[]{:S(2)}, u32[]{:S(2)}) collective-permute-start(bf16[512,384]{1,0:T(8,128)(2,1)} %bitcast.152), channel_id=1, source_target_pairs={{2,1},{1,2},{6,5},{5,6},{10,9},{9,10},{14,13},{13,14},{18,17},{17,... | collective-permute-start | bytes 1179656 | tf_op jit(solution)/shard_map/ppermute | solution.py:105
  3.5 2.8 %copy-start.1 = (bf16[1,512,384]{2,1,0:T(8,128)(2,1)S(1)}, bf16[1,512,384]{2,1,0:T(8,128)(2,1)}, u32[]{:S(2)}) copy-start(bf16[1,512,384]{2,1,0:T(8,128)(2,1)} %param.5) | copy-start | bytes 1179652
  7.3 14.0 %collective-permute-start = (bf16[2,256,384]{2,1,0:T(8,128)(2,1)}, bf16[2,256,384]{2,1,0:T(8,128)(2,1)S(1)}, u32[]{:S(2)}, u32[]{:S(2)}) collective-permute-start(bf16[2,256,384]{2,1,0:T(8,128)(2,1)} %get-tuple-element.21), channel_id=1, source_target_pairs={{0,4},{4,8},{8,12},{1,5},{5,9},{9,13},{2,6},{6,10},{10,14},{3,7},{... | collective-permute-start | bytes 1179656 | tf_op jit(solution)/shard_map/ppermute | solution.py:12
  12.3 11.4 %collective-permute-start.1 = (bf16[2,256,384]{2,1,0:T(8,128)(2,1)}, bf16[2,256,384]{2,1,0:T(8,128)(2,1)S(1)}, u32[]{:S(2)}, u32[]{:S(2)}) collective-permute-start(bf16[2,256,384]{2,1,0:T(8,128)(2,1)} %get-tuple-element.22), channel_id=1, source_target_pairs={{4,0},{8,4},{12,8},{5,1},{9,5},{13,9},{6,2},{10,6},{14,10},{7,3},{... | collective-permute-start | bytes 1179656 | tf_op jit(solution)/shard_map/ppermute | solution.py:12
  14.6 1.4 %copy-start.5 = (bf16[2,512,384]{2,1,0:T(8,128)(2,1)S(1)}, bf16[2,512,384]{2,1,0:T(8,128)(2,1)}, u32[]{:S(2)}) copy-start(bf16[2,512,384]{2,1,0:T(8,128)(2,1)} %pad_maximum_fusion.3) | copy-start | bytes 2359300
  14.7 2.7 %copy-start.3 = (bf16[3,384,384]{2,1,0:T(8,128)(2,1)}, bf16[3,384,384]{2,1,0:T(8,128)(2,1)S(1)}, u32[]{:S(2)}) copy-start(bf16[3,384,384]{2,1,0:T(8,128)(2,1)S(1)} %constant_dynamic-slice_fusion) | copy-start | bytes 2654212
  17.4 22.8 %collective-permute-start.3 = (bf16[2176,384]{1,0:T(8,128)(2,1)}, bf16[2176,384]{1,0:T(8,128)(2,1)}, u32[]{:S(2)}, u32[]{:S(2)}) collective-permute-start(bf16[2176,384]{1,0:T(8,128)(2,1)} %pad_maximum_fusion.1), channel_id=1, source_target_pairs={{0,1},{1,0},{2,3},{3,2},{4,5},{5,4},{6,7},{7,6},{8,9},{9,8},{10,11... | collective-permute-start | bytes 5013512 | tf_op jit(solution)/shard_map/ppermute | solution.py:112
  21.3 11.9 %collective-permute-start.4 = (bf16[512,384]{1,0:T(8,128)(2,1)S(1)}, bf16[512,384]{1,0:T(8,128)(2,1)S(1)}, u32[]{:S(2)}, u32[]{:S(2)}) collective-permute-start(bf16[512,384]{1,0:T(8,128)(2,1)S(1)} %get-tuple-element.31), channel_id=1, source_target_pairs={{0,2},{2,0},{1,3},{3,1},{4,6},{6,4},{5,7},{7,5},{8,10},{10,8},{9,1... | collective-permute-start | bytes 1179656 | tf_op jit(solution)/shard_map/ppermute | solution.py:107
  23.8 16.4 %collective-permute-start.2 = (bf16[2,2,256,384]{3,2,1,0:T(8,128)(2,1)S(1)}, bf16[2,2,256,384]{3,2,1,0:T(8,128)(2,1)S(1)}, u32[]{:S(2)}, u32[]{:S(2)}) collective-permute-start(bf16[2,2,256,384]{3,2,1,0:T(8,128)(2,1)S(1)} %pad_maximum_fusion.4), channel_id=1, source_target_pairs={{0,1},{1,0},{2,3},{3,2},{4,5},{5,4},{6,7},{7,6},{8,9},{9,8},{10,11... | collective-permute-start | bytes 2359304 | tf_op jit(solution)/shard_map/ppermute | solution.py:119
  27.8 7.8 %collective-permute-start.8 = (bf16[256,384]{1,0:T(8,128)(2,1)S(1)}, bf16[256,384]{1,0:T(8,128)(2,1)S(1)}, u32[]{:S(2)}, u32[]{:S(2)}) collective-permute-start(bf16[256,384]{1,0:T(8,128)(2,1)S(1)} %get-tuple-element.29), channel_id=1, source_target_pairs={{0,4},{4,8},{8,12},{1,5},{5,9},{9,13},{2,6},{6,10},{10,14},{3,7},{... | collective-permute-start | bytes 589832 | tf_op jit(solution)/shard_map/ppermute | solution.py:12
  31.3 8.5 %collective-permute-start.7 = (bf16[256,384]{1,0:T(8,128)(2,1)S(1)}, bf16[256,384]{1,0:T(8,128)(2,1)S(1)}, u32[]{:S(2)}, u32[]{:S(2)}) collective-permute-start(bf16[256,384]{1,0:T(8,128)(2,1)S(1)} %get-tuple-element.30), channel_id=1, source_target_pairs={{4,0},{8,4},{12,8},{5,1},{9,5},{13,9},{6,2},{10,6},{14,10},{7,3},{... | collective-permute-start | bytes 589832 | tf_op jit(solution)/shard_map/ppermute | solution.py:12
  42.7 5.5 %copy-start.6 = (f32[384,384]{1,0:T(8,128)}, f32[384,384]{1,0:T(8,128)S(1)}, u32[]{:S(2)}) copy-start(f32[384,384]{1,0:T(8,128)S(1)} %convolution_add_fusion) | copy-start | bytes 1769476
  43.6 41.6 %collective-permute-start.13 = (f32[96,384]{1,0:T(8,128)}, f32[96,384]{1,0:T(8,128)S(1)}, u32[]{:S(2)}, u32[]{:S(2)}) collective-permute-start(f32[96,384]{1,0:T(8,128)} %get-tuple-element.23), channel_id=1, source_target_pairs={{0,4},{4,8},{8,12},{12,0},{1,5},{5,9},{9,13},{13,1},{2,6},{6,10},{... | collective-permute-start | bytes 442376 | tf_op jit(solution)/shard_map/ppermute | solution.py:57
  45.1 40.1 %collective-permute-start.14 = (f32[96,384]{1,0:T(8,128)}, f32[96,384]{1,0:T(8,128)}, u32[]{:S(2)}, u32[]{:S(2)}) collective-permute-start(f32[96,384]{1,0:T(8,128)} %get-tuple-element.25), channel_id=1, source_target_pairs={{0,8},{4,12},{8,0},{12,4},{1,9},{5,13},{9,1},{13,5},{2,10},{6,14},... | collective-permute-start | bytes 442376 | tf_op jit(solution)/shard_map/ppermute | solution.py:57
  45.2 40.1 %collective-permute-start.15 = (f32[96,384]{1,0:T(8,128)}, f32[96,384]{1,0:T(8,128)}, u32[]{:S(2)}, u32[]{:S(2)}) collective-permute-start(f32[96,384]{1,0:T(8,128)} %get-tuple-element.24), channel_id=1, source_target_pairs={{0,12},{4,0},{8,4},{12,8},{1,13},{5,1},{9,5},{13,9},{2,14},{6,2},{... | collective-permute-start | bytes 442376 | tf_op jit(solution)/shard_map/ppermute | solution.py:57
  49.6 19.7 %collective-permute-start.9 = (f32[2,192,384]{2,1,0:T(8,128)}, f32[2,192,384]{2,1,0:T(8,128)}, u32[]{:S(2)}, u32[]{:S(2)}) collective-permute-start(f32[2,192,384]{2,1,0:T(8,128)} %select_bitcast_fusion), channel_id=1, source_target_pairs={{0,4},{4,0},{8,12},{12,8},{1,5},{5,1},{9,13},{13,9},{2,6},{6,2},{1... | collective-permute-start | bytes 1769480 | tf_op jit(solution)/shard_map/ppermute | solution.py:74
  52.0 2.0 %copy-start.4 = (bf16[3,384,384]{2,1,0:T(8,128)(2,1)S(1)}, bf16[3,384,384]{2,1,0:T(8,128)(2,1)}, u32[]{:S(2)}) copy-start(bf16[3,384,384]{2,1,0:T(8,128)(2,1)} %copy-done.3) | copy-start | bytes 2654212
  54.1 1.0 copy-start.2
  54.1 1.3 %copy-start.12 = (f32[512,384]{1,0:T(8,128)S(1)}, f32[512,384]{1,0:T(8,128)}, u32[]{:S(2)}) copy-start(f32[512,384]{1,0:T(8,128)} %get-tuple-element.32) | copy-start | bytes 2359300
  60.9 1.3 %copy-start.7 = (bf16[512,1,384]{2,0,1:T(8,128)(2,1)S(1)}, bf16[512,1,384]{2,0,1:T(8,128)(2,1)}, u32[]{:S(2)}) copy-start(bf16[512,1,384]{2,0,1:T(8,128)(2,1)} %get-tuple-element.8) | copy-start | bytes 1179652
  60.9 1.4 %copy-start.8 = (bf16[512,1,384]{2,0,1:T(8,128)(2,1)S(1)}, bf16[512,1,384]{2,0,1:T(8,128)(2,1)}, u32[]{:S(2)}) copy-start(bf16[512,1,384]{2,0,1:T(8,128)(2,1)} %get-tuple-element.15) | copy-start | bytes 1179652
  63.1 8.1 %copy-start.9 = (bf16[512,1,384]{2,0,1:T(8,128)(2,1)S(1)}, bf16[512,1,384]{2,0,1:T(8,128)(2,1)}, u32[]{:S(2)}) copy-start(bf16[512,1,384]{2,0,1:T(8,128)(2,1)} %get-tuple-element.12) | copy-start | bytes 1179652
  63.1 8.1 %copy-start.10 = (bf16[512,1,384]{2,0,1:T(8,128)(2,1)S(1)}, bf16[512,1,384]{2,0,1:T(8,128)(2,1)}, u32[]{:S(2)}) copy-start(bf16[512,1,384]{2,0,1:T(8,128)(2,1)} %get-tuple-element.17) | copy-start | bytes 1179652
  63.1 8.1 %copy-start.11 = (bf16[512,1,384]{2,0,1:T(8,128)(2,1)S(1)}, bf16[512,1,384]{2,0,1:T(8,128)(2,1)}, u32[]{:S(2)}) copy-start(bf16[512,1,384]{2,0,1:T(8,128)(2,1)} %get-tuple-element.4) | copy-start | bytes 1179652
  63.1 8.1 %copy-start.13 = (f32[512,384]{1,0:T(8,128)S(1)}, f32[512,384]{1,0:T(8,128)}, u32[]{:S(2)}) copy-start(f32[512,384]{1,0:T(8,128)} %get-tuple-element.32) | copy-start | bytes 2359300
  70.5 14.6 %collective-permute-start.10 = (f32[192,384]{1,0:T(8,128)S(1)}, f32[192,384]{1,0:T(8,128)S(1)}, u32[]{:S(2)}, u32[]{:S(2)}) collective-permute-start(f32[192,384]{1,0:T(8,128)S(1)} %select_bitcast_fusion.3), channel_id=1, source_target_pairs={{0,8},{8,0},{4,12},{12,4},{1,9},{9,1},{5,13},{13,5},{2,10},{10,2},... | collective-permute-start | bytes 884744 | tf_op jit(solution)/shard_map/ppermute | solution.py:79
  85.1 11.7 %collective-permute-start.11 = (bf16[192,384]{1,0:T(8,128)(2,1)S(1)}, bf16[192,384]{1,0:T(8,128)(2,1)S(1)}, u32[]{:S(2)}, u32[]{:S(2)}) collective-permute-start(bf16[192,384]{1,0:T(8,128)(2,1)S(1)} %fusion.67), channel_id=1, source_target_pairs={{0,8},{8,0},{4,12},{12,4},{1,9},{9,1},{5,13},{13,5},{2,10},{10,2},... | collective-permute-start | bytes 442376 | tf_op jit(solution)/shard_map/ppermute | solution.py:80
  86.3 10.6 %collective-permute-start.16 = (bf16[96,384]{1,0:T(8,128)(2,1)S(1)}, bf16[96,384]{1,0:T(8,128)(2,1)S(1)}, u32[]{:S(2)}, u32[]{:S(2)}) collective-permute-start(bf16[96,384]{1,0:T(8,128)(2,1)S(1)} %fusion.70), channel_id=1, source_target_pairs={{0,4},{4,8},{8,12},{12,0},{1,5},{5,9},{9,13},{13,1},{2,6},{6,10},{... | collective-permute-start | bytes 221192 | tf_op jit(solution)/shard_map/ppermute | solution.py:60
  88.6 9.8 %collective-permute-start.17 = (bf16[96,384]{1,0:T(8,128)(2,1)S(1)}, bf16[96,384]{1,0:T(8,128)(2,1)S(1)}, u32[]{:S(2)}, u32[]{:S(2)}) collective-permute-start(bf16[96,384]{1,0:T(8,128)(2,1)S(1)} %fusion.70), channel_id=1, source_target_pairs={{0,8},{4,12},{8,0},{12,4},{1,9},{5,13},{9,1},{13,5},{2,10},{6,14},... | collective-permute-start | bytes 221192 | tf_op jit(solution)/shard_map/ppermute | solution.py:60
  89.4 9.1 %collective-permute-start.18 = (bf16[96,384]{1,0:T(8,128)(2,1)S(1)}, bf16[96,384]{1,0:T(8,128)(2,1)S(1)}, u32[]{:S(2)}, u32[]{:S(2)}) collective-permute-start(bf16[96,384]{1,0:T(8,128)(2,1)S(1)} %fusion.70), channel_id=1, source_target_pairs={{0,12},{4,0},{8,4},{12,8},{1,13},{5,1},{9,5},{13,9},{2,14},{6,2},{... | collective-permute-start | bytes 221192 | tf_op jit(solution)/shard_map/ppermute | solution.py:60
  96.9 9.0 %collective-permute-start.12 = (bf16[2,192,384]{2,1,0:T(8,128)(2,1)S(1)}, bf16[2,192,384]{2,1,0:T(8,128)(2,1)}, u32[]{:S(2)}, u32[]{:S(2)}) collective-permute-start(bf16[2,192,384]{2,1,0:T(8,128)(2,1)S(1)} %maximum_select_fusion), channel_id=1, source_target_pairs={{0,4},{4,0},{8,12},{12,8},{1,5},{5,1},{9,13},{13,9},{2,6},{6,2},{1... | collective-permute-start | bytes 884744 | tf_op jit(solution)/shard_map/ppermute | solution.py:82

commit v22 on v11

--- a/solution.py
+++ b/solution.py
@@ -85,10 +85,10 @@
 
     if lax.axis_size("batch") == 2:
         b = lax.axis_index("batch")
-        same_core = lax.ppermute(local_cot, ("batch", "chan"), [(2, 0), (1, 3)])
+        far_both = lax.ppermute(jnp.stack([activation, local_cot]), "batch", SWAP)
         cross_core = lax.ppermute(local_cot, ("batch", "chan"), [(2, 1), (1, 2)])
-        far_cot = jnp.where(b == c, same_core, cross_core)
-        far_mid = lax.ppermute(activation, "batch", SWAP)
+        far_cot = jnp.where(b == c, far_both[1], cross_core)
+        far_mid = far_both[0]
 
     both = jnp.stack([activation, local_cot])
     w_own = half_of(conv_weight, c, 2)

time: 103 us -> 105 us (1.019)
  starting transfers between devices: 31.2 us -> 27.5 us
  matrix products: 11.5 us -> 14.6 us
  waiting for transfers between devices: 42.3 us -> 44.7 us
  other arithmetic: 9.42 us -> 10.6 us
    ppermute x2, waiting for transfers between devices: 16.6 us -> 20.3 us  [line_total(): other = lax.ppermute(total, 'seq', across)]
    dot_general x3, matrix products: 1.16 us -> 4.17 us  [shards(): jnp.dot(far_mid.T, far_shifted[k], preferred_element_type=jnp.float32)]
    ppermute x1, starting transfers between devices: 2.82 us -> 0.07 us  [shards(): par_halo = lax.ppermute(jnp.stack([from_prev, from_next]), 'chan', SWAP)]
    ppermute x1, starting transfers between devices: 3.71 us -> 1.16 us  [shards(): lax.ppermute(jnp.concatenate([both.reshape(-1, width), w_other.reshape(-1...]
    ppermute x4, waiting for transfers between devices: 8.39 us -> 6.66 us  [shift_from(): return lax.ppermute(block, axis, route)]
    ppermute x2, starting transfers between devices: 1.43 us -> 2.75 us  [line_total(): total = (keep + lax.ppermute(give, 'seq', across)).astype(jnp.bfloat16)]
    concatenate x1, other arithmetic: 1.34 us -> 2.48 us  [shards(): jnp.concatenate([both.reshape(-1, width), w_other.reshape(-1, width)], 0)]
    ppermute x2 -> x1, starting transfers between devices: 2.4 us -> 2.97 us  [shards(): far_both = lax.ppermute(jnp.stack([activation, local_cot]), 'batch', SWAP)]
  transfers between devices with their start and end apart: 17 -> 16, of which waited for: 7 -> 8; matrix products, arithmetic and copies ran while one was open for 22% -> 22% of each run, Pallas kernels for 0% -> 0%
where the time goes in v22:
time: 105 us; the launch traced here: 104 us
  waiting for transfers between devices  44.7 us (43%)
  starting transfers between devices  27.5 us (26%)
  matrix products  14.6 us (14%)
  other arithmetic  10.6 us (10%)
  local copies, waits for them, and re-layouts  5.9 us (6%)
    ppermute x2, waiting for transfers between devices, line_total(): other = lax.ppermute(total, 'seq', across)  20.3 us
    ppermute x4, starting transfers between devices, shift_from(): return lax.ppermute(block, axis, route)  11.3 us
    ppermute x2, waiting for transfers between devices, line_total(): lax.ppermute(jnp.where(odd, even_set, odd_set), 'seq', pairs)  11.2 us
    ppermute x4, waiting for transfers between devices, shift_from(): return lax.ppermute(block, axis, route)  6.66 us
    ppermute x2, waiting for transfers between devices, line_total(): far_set = lax.ppermute(own_set, 'seq', pairs)  6.55 us
    ppermute x2, starting transfers between devices, line_total(): other = lax.ppermute(total, 'seq', across)  4.97 us
    dot_general x3, matrix products, shards(): jnp.dot(far_mid.T, far_shifted[k], preferred_element_type=jnp.float32)  4.17 us
    dot_general x3, matrix products, shards(): jnp.dot(own_taps[:, k].T, cot_mine, preferred_element_type=jnp.float32)  3.04 us
  transfers between devices with their start and end apart: 16, of which 8 were waited for; matrix products, arithmetic and copies ran while one was open for 22% of the time, Pallas kernels for 0%

profile of v22, /device:TPU:0, one launch (start us, length us, event | category | flops | bytes accessed | tf_op | source)
XLA Modules:
  0.0 104.3 jit_solution(6571013498417848003)
XLA Ops:
  0.7 2.9 %multiply_convert_fusion = (bf16[512,384]{1,0:T(8,128)(2,1)S(1)}, f32[512,384]{1,0:T(8,128)}) fusion(bf16[1,1024,384]{2,1,0:T(8,128)(2,1)} %param.3, s32[1024]{0:T(1024)S(1)} %get-tuple-element.32, s32[1024]{0:T(1024)S(1)} %get-tuple-element.33, pred[1024]{0:T(1024)(128)(4,1)S(1)} %fusion.74), kind=kOutput, calls=%fused_computation.61 | convolution fusion | flops 406519808 | bytes 1975296 | tf_op jit(solution)/shard_map/dot_general | solution.py:83
  3.6 1.0 pad_maximum_fusion.3
  4.6 3.0 %collective-permute-start.4 = (bf16[2,512,384]{2,1,0:T(8,128)(2,1)}, bf16[2,512,384]{2,1,0:T(8,128)(2,1)}, u32[]{:S(2)}, u32[]{:S(2)}) collective-permute-start(bf16[2,512,384]{2,1,0:T(8,128)(2,1)} %pad_maximum_fusion.3), channel_id=1, source_target_pairs={{0,2},{2,0},{1,3},{3,1},{4,6},{6,4},{5,7},{7,5},{8,10},{10,8},{9,1... | collective-permute-start | bytes 2359304 | tf_op jit(solution)/shard_map/ppermute | solution.py:88
  7.5 1.0 fusion.47
  8.5 4.2 %collective-permute-start = (bf16[2,256,384]{2,1,0:T(8,128)(2,1)}, bf16[2,256,384]{2,1,0:T(8,128)(2,1)}, u32[]{:S(2)}, u32[]{:S(2)}) collective-permute-start(bf16[2,256,384]{2,1,0:T(8,128)(2,1)} %get-tuple-element.21), channel_id=1, source_target_pairs={{0,4},{4,8},{8,12},{1,5},{5,9},{9,13},{2,6},{6,10},{10,14},{3,7},{... | collective-permute-start | bytes 1179656 | tf_op jit(solution)/shard_map/ppermute | solution.py:12
  12.7 1.3 %collective-permute-start.1 = (bf16[2,256,384]{2,1,0:T(8,128)(2,1)}, bf16[2,256,384]{2,1,0:T(8,128)(2,1)}, u32[]{:S(2)}, u32[]{:S(2)}) collective-permute-start(bf16[2,256,384]{2,1,0:T(8,128)(2,1)} %get-tuple-element.22), channel_id=1, source_target_pairs={{4,0},{8,4},{12,8},{5,1},{9,5},{13,9},{6,2},{10,6},{14,10},{7,3},{... | collective-permute-start | bytes 1179656 | tf_op jit(solution)/shard_map/ppermute | solution.py:12
  14.0 1.4 %collective-permute-start.5 = (bf16[512,384]{1,0:T(8,128)(2,1)S(1)}, bf16[512,384]{1,0:T(8,128)(2,1)}, u32[]{:S(2)}, u32[]{:S(2)}) collective-permute-start(bf16[512,384]{1,0:T(8,128)(2,1)S(1)} %bitcast.163), channel_id=1, source_target_pairs={{2,1},{1,2},{6,5},{5,6},{10,9},{9,10},{14,13},{13,14},{18,17},{17,... | collective-permute-start | bytes 1179656 | tf_op jit(solution)/shard_map/ppermute | solution.py:89
  15.4 0.1 constant_dynamic-slice_fusion
  15.5 2.5 %pad_maximum_fusion.1 = bf16[2176,384]{1,0:T(8,128)(2,1)} fusion(bf16[1152,384]{1,0:T(8,128)(2,1)S(1)} %bitcast.167, bf16[1024,384]{1,0:T(8,128)(2,1)} %bitcast.9), kind=kLoop, calls=%fused_computation.3 | loop fusion | flops 3342336 | bytes 3342336 | tf_op jit(solution)/shard_map/concatenate | solution.py:97
  18.0 1.2 %collective-permute-start.3 = (bf16[2176,384]{1,0:T(8,128)(2,1)}, bf16[2176,384]{1,0:T(8,128)(2,1)}, u32[]{:S(2)}, u32[]{:S(2)}) collective-permute-start(bf16[2176,384]{1,0:T(8,128)(2,1)} %pad_maximum_fusion.1), channel_id=1, source_target_pairs={{0,1},{1,0},{2,3},{3,2},{4,5},{5,4},{6,7},{7,6},{8,9},{9,8},{10,11... | collective-permute-start | bytes 5013512 | tf_op jit(solution)/shard_map/ppermute | solution.py:96
  19.2 1.2 %collective-permute-done = bf16[2,256,384]{2,1,0:T(8,128)(2,1)} collective-permute-done((bf16[2,256,384]{2,1,0:T(8,128)(2,1)}, bf16[2,256,384]{2,1,0:T(8,128)(2,1)}, u32[]{:S(2)}, u32[]{:S(2)}) %collective-permute-start) | collective-permute-done | bytes 393248 | tf_op jit(solution)/shard_map/ppermute | solution.py:12
  20.4 4.8 %collective-permute-done.1 = bf16[2,256,384]{2,1,0:T(8,128)(2,1)} collective-permute-done((bf16[2,256,384]{2,1,0:T(8,128)(2,1)}, bf16[2,256,384]{2,1,0:T(8,128)(2,1)}, u32[]{:S(2)}, u32[]{:S(2)}) %collective-permute-start.1) | collective-permute-done | bytes 393248 | tf_op jit(solution)/shard_map/ppermute | solution.py:12
  25.2 1.2 %pad_maximum_fusion.4 = bf16[2,2,256,384]{3,2,1,0:T(8,128)(2,1)S(1)} fusion(bf16[1,2,256,384]{3,2,1,0:T(8,128)(2,1)} %bitcast.7, bf16[1,2,256,384]{3,2,1,0:T(8,128)(2,1)} %bitcast.6), kind=kLoop, calls=%fused_computation.59 | loop fusion | flops 393216 | bytes 1572864 | tf_op jit(solution)/shard_map/stack | solution.py:103
  26.5 1.1 %fusion.49 = bf16[512,384]{1,0:T(8,128)(2,1)S(1)} fusion(bf16[512,384]{1,0:T(8,128)(2,1)} %collective-permute-done.5, bf16[2,512,384]{2,1,0:T(8,128)(2,1)} %collective-permute-done.4, pred[]{:T(512)S(6)} %eq.16), kind=kLoop, calls=%fused_computation.72 | loop fusion | flops 196608 | bytes 1179649 | tf_op jit(solution)/shard_map/jit(_where)/select_n | solution.py:90
  27.6 1.3 %collective-permute-start.6 = (bf16[256,384]{1,0:T(8,128)(2,1)S(1)}, bf16[256,384]{1,0:T(8,128)(2,1)S(1)}, u32[]{:S(2)}, u32[]{:S(2)}) collective-permute-start(bf16[256,384]{1,0:T(8,128)(2,1)S(1)} %get-tuple-element.27), channel_id=1, source_target_pairs={{4,0},{8,4},{12,8},{5,1},{9,5},{13,9},{6,2},{10,6},{14,10},{7,3},{... | collective-permute-start | bytes 589832 | tf_op jit(solution)/shard_map/ppermute | solution.py:12
  28.9 4.6 %collective-permute-start.7 = (bf16[256,384]{1,0:T(8,128)(2,1)S(1)}, bf16[256,384]{1,0:T(8,128)(2,1)S(1)}, u32[]{:S(2)}, u32[]{:S(2)}) collective-permute-start(bf16[256,384]{1,0:T(8,128)(2,1)S(1)} %get-tuple-element.26), channel_id=1, source_target_pairs={{0,4},{4,8},{8,12},{1,5},{5,9},{9,13},{2,6},{6,10},{10,14},{3,7},{... | collective-permute-start | bytes 589832 | tf_op jit(solution)/shard_map/ppermute | solution.py:12
  33.5 1.4 %fusion.67 = f32[384,384]{1,0:T(8,128)S(1)} fusion(bf16[512,384]{1,0:T(8,128)(2,1)S(1)} %fusion.49, bf16[2,512,384]{2,1,0:T(8,128)(2,1)} %collective-permute-done.4), kind=kOutput, calls=%fused_computation.106 | convolution fusion | flops 150994944 | bytes 1376256 | tf_op jit(solution)/shard_map/dot_general | solution.py:144
  34.9 0.3 collective-permute-done.6
  35.2 1.4 %fusion.54 = f32[384,384]{1,0:T(8,128)S(1)} fusion(bf16[256,384]{1,0:T(8,128)(2,1)S(1)} %collective-permute-done.6, bf16[256,384]{1,0:T(8,128)(2,1)S(1)} %get-tuple-element.26, bf16[2,512,384]{2,1,0:T(8,128)(2,1)} %collective-permute-done.4), kind=kOutput, calls=%fused_computation.91 | convolution fusion | flops 151781376 | bytes 1376256 | tf_op jit(solution)/shard_map/dot_general | solution.py:144
  36.6 0.3 collective-permute-done.7
  36.9 1.4 %fusion.58 = f32[384,384]{1,0:T(8,128)S(1)} fusion(bf16[256,384]{1,0:T(8,128)(2,1)S(1)} %get-tuple-element.27, bf16[256,384]{1,0:T(8,128)(2,1)S(1)} %collective-permute-done.7, bf16[2,512,384]{2,1,0:T(8,128)(2,1)} %collective-permute-done.4), kind=kOutput, calls=%fused_computation.95 | convolution fusion | flops 151781376 | bytes 1376256 | tf_op jit(solution)/shard_map/dot_general | solution.py:144
  38.3 0.1 slice_bitcast_fusion.4
  38.4 1.6 %fusion.53 = (bf16[512,1,384]{2,0,1:T(8,128)(2,1)S(1)}, bf16[512,1,384]{2,0,1:T(8,128)(2,1)S(1)}, bf16[512,1,384]{2,0,1:T(8,128)(2,1)S(1)}, bf16[512,1,384]{2,0,1:T(8,128)(2,1)S(1)}, bf16[1,512,384]{2,1,0:T(8,128)(2,1)S(1)}) fusion(bf16[2,256,384]{2,1,0:T(8,128)(2,1)} %collective-permute-done.1, bf16[1,512,384]{2,1,0:T(8,128)(2,1)S(1)} %copy-done.1, ...), kind=kLoop, calls=%fused_computation.82 | loop fusion | flops 4915200 | bytes 3932161 | tf_op jit(solution)/shard_map/stack | solution.py:21
  40.0 0.4 convolution_add_fusion
  40.4 2.5 %collective-permute-start.12 = (f32[2,96,384]{2,1,0:T(8,128)S(1)}, f32[2,96,384]{2,1,0:T(8,128)S(1)}, u32[]{:S(2)}, u32[]{:S(2)}) collective-permute-start(f32[2,96,384]{2,1,0:T(8,128)S(1)} %select_bitcast_fusion.1), channel_id=1, source_target_pairs={{0,4},{4,0},{8,12},{12,8},{1,5},{5,1},{9,13},{13,9},{2,6},{6,2},{1... | collective-permute-start | bytes 884744 | tf_op jit(solution)/shard_map/ppermute | solution.py:58
  43.0 1.3 %convolution_add_fusion.2 = f32[384,384]{1,0:T(8,128)S(1)} fusion(f32[384,384]{1,0:T(8,128)S(1)} %fusion.54, bf16[1,512,384]{2,1,0:T(8,128)(2,1)S(1)} %get-tuple-element.25, bf16[2,256,384]{2,1,0:T(8,128)(2,1)} %collective-permute-done, bf16[1,512,384]{2,1,0:T(8,128)(2,1)S(1)} %copy-done.1, bf16[1,512,384]{2,1,0:T(8,128)(2,1)S(1)} %bitcast.158), kind=kOutput, calls=%fused_computation.14 | convolution fusion | flops 152322048 | bytes 2752512 | tf_op jit(solution)/shard_map/dot_general | solution.py:142
  44.3 1.3 %convolution_add_fusion.1 = f32[384,384]{1,0:T(8,128)S(1)} fusion(f32[384,384]{1,0:T(8,128)S(1)} %fusion.58, bf16[1,512,384]{2,1,0:T(8,128)(2,1)S(1)} %get-tuple-element.25, bf16[2,256,384]{2,1,0:T(8,128)(2,1)} %collective-permute-done.1, bf16[1,512,384]{2,1,0:T(8,128)(2,1)S(1)} %copy-done.1, bf16[1,512,384]{2,1,0:T(8,128)(2,1)S(1)} %bitcast.159), kind=kOutput, calls=%fused_computation.13 | convolution fusion | flops 152322048 | bytes 2752512 | tf_op jit(solution)/shard_map/dot_general | solution.py:142
  45.9 1.2 %slice.192 = bf16[1024,384]{1,0:T(8,128)(2,1)S(1)} slice(bf16[2176,384]{1,0:T(8,128)(2,1)} %collective-permute-done.3), slice={[0:1024], [0:384]} | slice | bytes 1572864 | tf_op jit(solution)/shard_map/slice | solution.py:99
  47.1 0.2 fusion.51
  47.3 1.2 %slice_bitcast_fusion.5 = (bf16[512,1,384]{2,0,1:T(8,128)(2,1)S(1)}, bf16[512,1,384]{2,0,1:T(8,128)(2,1)S(1)}) fusion(bf16[2176,384]{1,0:T(8,128)(2,1)} %collective-permute-done.3), kind=kLoop, calls=%fused_computation.105 | loop fusion | bytes 1572864 | tf_op jit(solution)/shard_map/stack | solution.py:21
  48.5 0.8 convolution_bitcast_fusion
  49.3 0.3 copy-done.2
  49.6 1.3 %fusion.39 = bf16[512,384]{1,0:T(8,128)(2,1)S(1)} fusion(f32[512,384]{1,0:T(8,128)S(1)} %copy-done.2, f32[512,384]{1,0:T(8,128)S(1)} %convolution_bitcast_fusion, bf16[512,1,384]{2,0,1:T(8,128)(2,1)S(1)} %get-tuple-element.16, bf16[512,1,384]{2,0,1:T(8,128)(2,1)S(1)} %bitcast.164, bf16[512,1,384]{2,0,1:T(8,128)(2,1)S(1)} %get-tuple-element.7, ...), kind=kOutput, calls=%fused_computation.58 | convolution fusion | flops 458883072 | bytes 4423684 | tf_op jit(solution)/shard_map/tko,kio->ti/dot_general | solution.py:116
  51.0 1.3 %slice.195 = bf16[1152,384]{1,0:T(8,128)(2,1)S(1)} slice(bf16[2176,384]{1,0:T(8,128)(2,1)} %collective-permute-done.3), slice={[1024:2176], [0:384]} | slice | bytes 1769472 | tf_op jit(solution)/shard_map/slice | solution.py:100
  52.3 2.1 %collective-permute-start.13 = (f32[96,384]{1,0:T(8,128)S(1)}, f32[96,384]{1,0:T(8,128)S(1)}, u32[]{:S(2)}, u32[]{:S(2)}) collective-permute-start(f32[96,384]{1,0:T(8,128)S(1)} %select_bitcast_fusion.7), channel_id=1, source_target_pairs={{0,8},{8,0},{4,12},{12,4},{1,9},{9,1},{5,13},{13,5},{2,10},{10,2},... | collective-permute-start | bytes 442376 | tf_op jit(solution)/shard_map/ppermute | solution.py:63
  54.4 11.2 %collective-permute-done.8 = f32[2,192,384]{2,1,0:T(8,128)S(1)} collective-permute-done((f32[2,192,384]{2,1,0:T(8,128)S(1)}, f32[2,192,384]{2,1,0:T(8,128)S(1)}, u32[]{:S(2)}, u32[]{:S(2)}) %collective-permute-start.8) | collective-permute-done | bytes 589856 | tf_op jit(solution)/shard_map/ppermute | solution.py:58
  65.8 0.6 collective-permute-start.9
  66.4 2.5 %collective-permute-start.14 = (bf16[96,384]{1,0:T(8,128)(2,1)S(1)}, bf16[96,384]{1,0:T(8,128)(2,1)S(1)}, u32[]{:S(2)}, u32[]{:S(2)}) collective-permute-start(bf16[96,384]{1,0:T(8,128)(2,1)S(1)} %fusion.71), channel_id=1, source_target_pairs={{0,8},{8,0},{4,12},{12,4},{1,9},{9,1},{5,13},{13,5},{2,10},{10,2},... | collective-permute-start | bytes 221192 | tf_op jit(solution)/shard_map/ppermute | solution.py:64
  68.9 0.8 convolution_bitcast_fusion.3
  69.7 15.9 %collective-permute-done.14 = bf16[96,384]{1,0:T(8,128)(2,1)S(1)} collective-permute-done((bf16[96,384]{1,0:T(8,128)(2,1)S(1)}, bf16[96,384]{1,0:T(8,128)(2,1)S(1)}, u32[]{:S(2)}, u32[]{:S(2)}) %collective-permute-start.14) | collective-permute-done | bytes 73760 | tf_op jit(solution)/shard_map/ppermute | solution.py:64
  85.8 2.5 %collective-permute-start.10 = (bf16[192,384]{1,0:T(8,128)(2,1)S(1)}, bf16[192,384]{1,0:T(8,128)(2,1)S(1)}, u32[]{:S(2)}, u32[]{:S(2)}) collective-permute-start(bf16[192,384]{1,0:T(8,128)(2,1)S(1)} %fusion.70), channel_id=1, source_target_pairs={{0,8},{8,0},{4,12},{12,4},{1,9},{9,1},{5,13},{13,5},{2,10},{10,2},... | collective-permute-start | bytes 442376 | tf_op jit(solution)/shard_map/ppermute | solution.py:64
  88.3 1.6 %fusion.4 = bf16[1,512,384]{2,1,0:T(8,128)(2,1)} fusion(f32[512,384]{1,0:T(8,128)S(1)} %copy-done.2, f32[512,384]{1,0:T(8,128)S(1)} %convolution_bitcast_fusion.3, bf16[3,384,384]{2,1,0:T(8,128)(2,1)S(1)} %bitcast.174, bf16[512,1,384]{2,0,1:T(8,128)(2,1)S(1)} %get-tuple-element.12, bf16[512,1,384]{2,0,1:T(8,128)(2,1)S(1)} %get-tuple-element.4, ...), kind=kOutput, calls=%fused_computation.15 | convolution fusion | flops 454754304 | bytes 4030464 | tf_op jit(solution)/shard_map/tki,kio->to/dot_general | solution.py:110
  89.9 0.4 broadcast_in_dim.18
  90.3 1.2 %convert_element_type.54 = bf16[1,1024,384]{2,1,0:T(8,128)(2,1)} reshape(bf16[512,2,384]{2,1,0:T(2,128)(2,1)S(1)} %broadcast_in_dim.18) | data formatting | bytes 1572864 | tf_op jit(solution)/shard_map/convert_element_type | solution.py:125
  91.5 4.4 %collective-permute-done.10 = bf16[192,384]{1,0:T(8,128)(2,1)S(1)} collective-permute-done((bf16[192,384]{1,0:T(8,128)(2,1)S(1)}, bf16[192,384]{1,0:T(8,128)(2,1)S(1)}, u32[]{:S(2)}, u32[]{:S(2)}) %collective-permute-start.10) | collective-permute-done | bytes 147488 | tf_op jit(solution)/shard_map/ppermute | solution.py:64
  96.1 6.5 %collective-permute-done.11 = bf16[2,192,384]{2,1,0:T(8,128)(2,1)S(1)} collective-permute-done((bf16[2,192,384]{2,1,0:T(8,128)(2,1)S(1)}, bf16[2,192,384]{2,1,0:T(8,128)(2,1)S(1)}, u32[]{:S(2)}, u32[]{:S(2)}) %collective-permute-start.11) | collective-permute-done | bytes 294944 | tf_op jit(solution)/shard_map/ppermute | solution.py:66
  102.7 0.1 select_bitcast_fusion.3
  103.0 1.3 %pad_maximum_fusion = f32[3,384,384]{2,1,0:T(8,128)} fusion(f32[1,384,384]{2,1,0:T(8,128)S(1)} %bitcast.171, f32[1,384,384]{2,1,0:T(8,128)S(1)} %bitcast.169, f32[1,384,384]{2,1,0:T(8,128)S(1)} %bitcast.170), kind=kLoop, calls=%fused_computation.2 | loop fusion | flops 884736 | bytes 3538944 | tf_op jit(solution)/shard_map/stack | solution.py:148
  (36 shorter events, 1.2 us)
Async XLA Ops:
  0.6 14.8 %copy-start = (bf16[3,384,768]{2,1,0:T(8,128)(2,1)S(1)}, bf16[3,384,768]{2,1,0:T(8,128)(2,1)}, u32[]{:S(2)}) copy-start(bf16[3,384,768]{2,1,0:T(8,128)(2,1)} %param.4) | copy-start | bytes 5308420
  0.7 2.9 %copy-start.1 = (bf16[1,512,384]{2,1,0:T(8,128)(2,1)S(1)}, bf16[1,512,384]{2,1,0:T(8,128)(2,1)}, u32[]{:S(2)}) copy-start(bf16[1,512,384]{2,1,0:T(8,128)(2,1)} %param.5) | copy-start | bytes 1179652
  4.6 22.0 %collective-permute-start.4 = (bf16[2,512,384]{2,1,0:T(8,128)(2,1)}, bf16[2,512,384]{2,1,0:T(8,128)(2,1)}, u32[]{:S(2)}, u32[]{:S(2)}) collective-permute-start(bf16[2,512,384]{2,1,0:T(8,128)(2,1)} %pad_maximum_fusion.3), channel_id=1, source_target_pairs={{0,2},{2,0},{1,3},{3,1},{4,6},{6,4},{5,7},{7,5},{8,10},{10,8},{9,1... | collective-permute-start | bytes 2359304 | tf_op jit(solution)/shard_map/ppermute | solution.py:88
  8.5 11.9 %collective-permute-start = (bf16[2,256,384]{2,1,0:T(8,128)(2,1)}, bf16[2,256,384]{2,1,0:T(8,128)(2,1)}, u32[]{:S(2)}, u32[]{:S(2)}) collective-permute-start(bf16[2,256,384]{2,1,0:T(8,128)(2,1)} %get-tuple-element.21), channel_id=1, source_target_pairs={{0,4},{4,8},{8,12},{1,5},{5,9},{9,13},{2,6},{6,10},{10,14},{3,7},{... | collective-permute-start | bytes 1179656 | tf_op jit(solution)/shard_map/ppermute | solution.py:12
  12.7 12.5 %collective-permute-start.1 = (bf16[2,256,384]{2,1,0:T(8,128)(2,1)}, bf16[2,256,384]{2,1,0:T(8,128)(2,1)}, u32[]{:S(2)}, u32[]{:S(2)}) collective-permute-start(bf16[2,256,384]{2,1,0:T(8,128)(2,1)} %get-tuple-element.22), channel_id=1, source_target_pairs={{4,0},{8,4},{12,8},{5,1},{9,5},{13,9},{6,2},{10,6},{14,10},{7,3},{... | collective-permute-start | bytes 1179656 | tf_op jit(solution)/shard_map/ppermute | solution.py:12
  14.0 12.5 %collective-permute-start.5 = (bf16[512,384]{1,0:T(8,128)(2,1)S(1)}, bf16[512,384]{1,0:T(8,128)(2,1)}, u32[]{:S(2)}, u32[]{:S(2)}) collective-permute-start(bf16[512,384]{1,0:T(8,128)(2,1)S(1)} %bitcast.163), channel_id=1, source_target_pairs={{2,1},{1,2},{6,5},{5,6},{10,9},{9,10},{14,13},{13,14},{18,17},{17,... | collective-permute-start | bytes 1179656 | tf_op jit(solution)/shard_map/ppermute | solution.py:89
  18.0 20.4 %collective-permute-start.3 = (bf16[2176,384]{1,0:T(8,128)(2,1)}, bf16[2176,384]{1,0:T(8,128)(2,1)}, u32[]{:S(2)}, u32[]{:S(2)}) collective-permute-start(bf16[2176,384]{1,0:T(8,128)(2,1)} %pad_maximum_fusion.1), channel_id=1, source_target_pairs={{0,1},{1,0},{2,3},{3,2},{4,5},{5,4},{6,7},{7,6},{8,9},{9,8},{10,11... | collective-permute-start | bytes 5013512 | tf_op jit(solution)/shard_map/ppermute | solution.py:96
  26.4 11.9 %collective-permute-start.2 = (bf16[2,2,256,384]{3,2,1,0:T(8,128)(2,1)S(1)}, bf16[2,2,256,384]{3,2,1,0:T(8,128)(2,1)S(1)}, u32[]{:S(2)}, u32[]{:S(2)}) collective-permute-start(bf16[2,2,256,384]{3,2,1,0:T(8,128)(2,1)S(1)} %pad_maximum_fusion.4), channel_id=1, source_target_pairs={{0,1},{1,0},{2,3},{3,2},{4,5},{5,4},{6,7},{7,6},{8,9},{9,8},{10,11... | collective-permute-start | bytes 2359304 | tf_op jit(solution)/shard_map/ppermute | solution.py:103
  27.6 7.6 %collective-permute-start.6 = (bf16[256,384]{1,0:T(8,128)(2,1)S(1)}, bf16[256,384]{1,0:T(8,128)(2,1)S(1)}, u32[]{:S(2)}, u32[]{:S(2)}) collective-permute-start(bf16[256,384]{1,0:T(8,128)(2,1)S(1)} %get-tuple-element.27), channel_id=1, source_target_pairs={{4,0},{8,4},{12,8},{5,1},{9,5},{13,9},{6,2},{10,6},{14,10},{7,3},{... | collective-permute-start | bytes 589832 | tf_op jit(solution)/shard_map/ppermute | solution.py:12
  28.9 8.0 %collective-permute-start.7 = (bf16[256,384]{1,0:T(8,128)(2,1)S(1)}, bf16[256,384]{1,0:T(8,128)(2,1)S(1)}, u32[]{:S(2)}, u32[]{:S(2)}) collective-permute-start(bf16[256,384]{1,0:T(8,128)(2,1)S(1)} %get-tuple-element.26), channel_id=1, source_target_pairs={{0,4},{4,8},{8,12},{1,5},{5,9},{9,13},{2,6},{6,10},{10,14},{3,7},{... | collective-permute-start | bytes 589832 | tf_op jit(solution)/shard_map/ppermute | solution.py:12
  40.4 11.8 %collective-permute-start.12 = (f32[2,96,384]{2,1,0:T(8,128)S(1)}, f32[2,96,384]{2,1,0:T(8,128)S(1)}, u32[]{:S(2)}, u32[]{:S(2)}) collective-permute-start(f32[2,96,384]{2,1,0:T(8,128)S(1)} %select_bitcast_fusion.1), channel_id=1, source_target_pairs={{0,4},{4,0},{8,12},{12,8},{1,5},{5,1},{9,13},{13,9},{2,6},{6,2},{1... | collective-permute-start | bytes 884744 | tf_op jit(solution)/shard_map/ppermute | solution.py:58
  45.8 19.8 %collective-permute-start.8 = (f32[2,192,384]{2,1,0:T(8,128)S(1)}, f32[2,192,384]{2,1,0:T(8,128)S(1)}, u32[]{:S(2)}, u32[]{:S(2)}) collective-permute-start(f32[2,192,384]{2,1,0:T(8,128)S(1)} %select_bitcast_fusion), channel_id=1, source_target_pairs={{0,4},{4,0},{8,12},{12,8},{1,5},{5,1},{9,13},{13,9},{2,6},{6,2},{1... | collective-permute-start | bytes 1769480 | tf_op jit(solution)/shard_map/ppermute | solution.py:58
  48.5 1.1 %copy-start.2 = (f32[512,384]{1,0:T(8,128)S(1)}, f32[512,384]{1,0:T(8,128)}, u32[]{:S(2)}) copy-start(f32[512,384]{1,0:T(8,128)} %get-tuple-element.31) | copy-start | bytes 2359300
  52.3 14.1 %collective-permute-start.13 = (f32[96,384]{1,0:T(8,128)S(1)}, f32[96,384]{1,0:T(8,128)S(1)}, u32[]{:S(2)}, u32[]{:S(2)}) collective-permute-start(f32[96,384]{1,0:T(8,128)S(1)} %select_bitcast_fusion.7), channel_id=1, source_target_pairs={{0,8},{8,0},{4,12},{12,4},{1,9},{9,1},{5,13},{13,5},{2,10},{10,2},... | collective-permute-start | bytes 442376 | tf_op jit(solution)/shard_map/ppermute | solution.py:63
  65.8 20.0 %collective-permute-start.9 = (f32[192,384]{1,0:T(8,128)S(1)}, f32[192,384]{1,0:T(8,128)S(1)}, u32[]{:S(2)}, u32[]{:S(2)}) collective-permute-start(f32[192,384]{1,0:T(8,128)S(1)} %select_bitcast_fusion.4), channel_id=1, source_target_pairs={{0,8},{8,0},{4,12},{12,4},{1,9},{9,1},{5,13},{13,5},{2,10},{10,2},... | collective-permute-start | bytes 884744 | tf_op jit(solution)/shard_map/ppermute | solution.py:63
  66.4 19.2 %collective-permute-start.14 = (bf16[96,384]{1,0:T(8,128)(2,1)S(1)}, bf16[96,384]{1,0:T(8,128)(2,1)S(1)}, u32[]{:S(2)}, u32[]{:S(2)}) collective-permute-start(bf16[96,384]{1,0:T(8,128)(2,1)S(1)} %fusion.71), channel_id=1, source_target_pairs={{0,8},{8,0},{4,12},{12,4},{1,9},{9,1},{5,13},{13,5},{2,10},{10,2},... | collective-permute-start | bytes 221192 | tf_op jit(solution)/shard_map/ppermute | solution.py:64
  85.7 10.3 %collective-permute-start.15 = (bf16[2,96,384]{2,1,0:T(8,128)(2,1)S(1)}, bf16[2,96,384]{2,1,0:T(8,128)(2,1)S(1)}, u32[]{:S(2)}, u32[]{:S(2)}) collective-permute-start(bf16[2,96,384]{2,1,0:T(8,128)(2,1)S(1)} %maximum_select_fusion.1), channel_id=1, source_target_pairs={{0,4},{4,0},{8,12},{12,8},{1,5},{5,1},{9,13},{13,9},{2,6},{6,2},{1... | collective-permute-start | bytes 442376 | tf_op jit(solution)/shard_map/ppermute | solution.py:66
  85.8 10.0 %collective-permute-start.10 = (bf16[192,384]{1,0:T(8,128)(2,1)S(1)}, bf16[192,384]{1,0:T(8,128)(2,1)S(1)}, u32[]{:S(2)}, u32[]{:S(2)}) collective-permute-start(bf16[192,384]{1,0:T(8,128)(2,1)S(1)} %fusion.70), channel_id=1, source_target_pairs={{0,8},{8,0},{4,12},{12,4},{1,9},{9,1},{5,13},{13,5},{2,10},{10,2},... | collective-permute-start | bytes 442376 | tf_op jit(solution)/shard_map/ppermute | solution.py:64
  95.9 6.8 %collective-permute-start.11 = (bf16[2,192,384]{2,1,0:T(8,128)(2,1)S(1)}, bf16[2,192,384]{2,1,0:T(8,128)(2,1)S(1)}, u32[]{:S(2)}, u32[]{:S(2)}) collective-permute-start(bf16[2,192,384]{2,1,0:T(8,128)(2,1)S(1)} %maximum_select_fusion), channel_id=1, source_target_pairs={{0,4},{4,0},{8,12},{12,8},{1,5},{5,1},{9,13},{13,9},{2,6},{6,2},{1... | collective-permute-start | bytes 884744 | tf_op jit(solution)/shard_map/ppermute | solution.py:66

commit v23 on v11

--- a/solution.py
+++ b/solution.py
@@ -1,4 +1,5 @@
 import jax
+import numpy as np
 import jax.numpy as jnp
 from jax import lax
 from jax.sharding import PartitionSpec as P
@@ -76,10 +77,9 @@
     width = local_in.shape[1]
     spread = rows // 2
     c = lax.axis_index("chan")
-    pairing = lax.broadcasted_iota(jnp.int32, (rows, 2 * rows), 1) // 2 == lax.broadcasted_iota(
-        jnp.int32, (rows, 2 * rows), 0
+    pairing = jnp.asarray(
+        np.kron(np.eye(rows, dtype=np.float32), np.full((1, 2), 0.5, np.float32)), jnp.bfloat16
     )
-    pairing = jnp.where(pairing, 0.5, 0.0).astype(jnp.bfloat16)
     pooled = jnp.dot(pairing, local_in, preferred_element_type=jnp.float32)
     activation = jax.nn.gelu(pooled).astype(jnp.bfloat16)
 

time: 103 us -> 103 us (level)
  transfers between devices with their start and end apart: 17 -> 17, of which waited for: 7 -> 7; matrix products, arithmetic and copies ran while one was open for 22% -> 23% of each run, Pallas kernels for 0% -> 0%
where the time goes in v23:
time: 103 us
  waiting for transfers between devices  42.3 us (41%)
  starting transfers between devices  31.2 us (30%)
  matrix products  11.8 us (11%)
  other arithmetic  9.41 us (9%)
  local copies, waits for them, and re-layouts  6.93 us (7%)
    ppermute x2, waiting for transfers between devices, line_total(): other = lax.ppermute(total, 'seq', across)  16.6 us
    ppermute x4, starting transfers between devices, shift_from(): return lax.ppermute(block, axis, route)  11 us
    ppermute x2, waiting for transfers between devices, line_total(): lax.ppermute(jnp.where(odd, even_set, odd_set), 'seq', pairs)  10.9 us
    ppermute x4, waiting for transfers between devices, shift_from(): return lax.ppermute(block, axis, route)  8.41 us
    ppermute x2, waiting for transfers between devices, line_total(): far_set = lax.ppermute(own_set, 'seq', pairs)  6.41 us
    ppermute x2, starting transfers between devices, line_total(): other = lax.ppermute(total, 'seq', across)  5.92 us
    ppermute x1, starting transfers between devices, shards(): lax.ppermute(jnp.concatenate([both.reshape(-1, width), w_other.reshape(-1...  3.68 us
    dot_general x1, matrix products, shards(): pooled = jnp.dot(pairing, local_in, preferred_element_type=jnp.float32)  3.07 us
  transfers between devices with their start and end apart: 17, of which 7 were waited for; matrix products, arithmetic and copies ran while one was open for 23% of the time, Pallas kernels for 0%

profile of v23, /device:TPU:0, one launch (start us, length us, event | category | flops | bytes accessed | tf_op | source)
XLA Modules:
  0.0 102.7 jit_solution(2273747213203871177)
XLA Ops:
  0.7 1.4 %collective-permute-start.5 = (bf16[512,384]{1,0:T(8,128)(2,1)}, bf16[512,384]{1,0:T(8,128)(2,1)}, u32[]{:S(2)}, u32[]{:S(2)}) collective-permute-start(bf16[512,384]{1,0:T(8,128)(2,1)} %bitcast.158), channel_id=1, source_target_pairs={{2,0},{1,3},{6,4},{5,7},{10,8},{9,11},{14,12},{13,15},{18,16},{17,... | collective-permute-start | bytes 1179656 | tf_op jit(solution)/shard_map/ppermute | solution.py:88
  2.1 1.4 %collective-permute-start.6 = (bf16[512,384]{1,0:T(8,128)(2,1)}, bf16[512,384]{1,0:T(8,128)(2,1)}, u32[]{:S(2)}, u32[]{:S(2)}) collective-permute-start(bf16[512,384]{1,0:T(8,128)(2,1)} %bitcast.159), channel_id=1, source_target_pairs={{2,1},{1,2},{6,5},{5,6},{10,9},{9,10},{14,13},{13,14},{18,17},{17,... | collective-permute-start | bytes 1179656 | tf_op jit(solution)/shard_map/ppermute | solution.py:89
  3.5 3.1 %multiply_convert_fusion = (bf16[512,384]{1,0:T(8,128)(2,1)S(1)}, f32[512,384]{1,0:T(8,128)}) fusion(bf16[512,1024]{1,0:T(8,128)(2,1)} %constant.46.clone, bf16[1,1024,384]{2,1,0:T(8,128)(2,1)} %param.4), kind=kOutput, calls=%fused_computation.54 | convolution fusion | flops 404422656 | bytes 3014656 | tf_op jit(solution)/shard_map/dot_general | solution.py:83
  6.6 1.0 fusion.42
  7.6 5.7 %collective-permute-start = (bf16[2,256,384]{2,1,0:T(8,128)(2,1)}, bf16[2,256,384]{2,1,0:T(8,128)(2,1)}, u32[]{:S(2)}, u32[]{:S(2)}) collective-permute-start(bf16[2,256,384]{2,1,0:T(8,128)(2,1)} %get-tuple-element.21), channel_id=1, source_target_pairs={{0,4},{4,8},{8,12},{1,5},{5,9},{9,13},{2,6},{6,10},{10,14},{3,7},{... | collective-permute-start | bytes 1179656 | tf_op jit(solution)/shard_map/ppermute | solution.py:13
  13.3 1.3 %collective-permute-start.1 = (bf16[2,256,384]{2,1,0:T(8,128)(2,1)}, bf16[2,256,384]{2,1,0:T(8,128)(2,1)}, u32[]{:S(2)}, u32[]{:S(2)}) collective-permute-start(bf16[2,256,384]{2,1,0:T(8,128)(2,1)} %get-tuple-element.22), channel_id=1, source_target_pairs={{4,0},{8,4},{12,8},{5,1},{9,5},{13,9},{6,2},{10,6},{14,10},{7,3},{... | collective-permute-start | bytes 1179656 | tf_op jit(solution)/shard_map/ppermute | solution.py:13
  14.6 1.0 pad_maximum_fusion.3
  15.6 1.0 %copy-done.2 = bf16[2,512,384]{2,1,0:T(8,128)(2,1)S(1)} copy-done((bf16[2,512,384]{2,1,0:T(8,128)(2,1)S(1)}, bf16[2,512,384]{2,1,0:T(8,128)(2,1)}, u32[]{:S(2)}) %copy-start.2) | copy-done | bytes 786456
  16.7 1.3 %pad_maximum_fusion.1 = bf16[2176,384]{1,0:T(8,128)(2,1)} fusion(bf16[1152,384]{1,0:T(8,128)(2,1)S(1)} %bitcast.163, bf16[1024,384]{1,0:T(8,128)(2,1)S(1)} %bitcast.164), kind=kLoop, calls=%fused_computation.1 | loop fusion | flops 3342336 | bytes 3342336 | tf_op jit(solution)/shard_map/concatenate | solution.py:97
  18.0 3.7 %collective-permute-start.3 = (bf16[2176,384]{1,0:T(8,128)(2,1)}, bf16[2176,384]{1,0:T(8,128)(2,1)}, u32[]{:S(2)}, u32[]{:S(2)}) collective-permute-start(bf16[2176,384]{1,0:T(8,128)(2,1)} %pad_maximum_fusion.1), channel_id=1, source_target_pairs={{0,1},{1,0},{2,3},{3,2},{4,5},{5,4},{6,7},{7,6},{8,9},{9,8},{10,11... | collective-permute-start | bytes 5013512 | tf_op jit(solution)/shard_map/ppermute | solution.py:96
  21.7 1.0 collective-permute-start.4
  22.7 2.0 %collective-permute-done.1 = bf16[2,256,384]{2,1,0:T(8,128)(2,1)} collective-permute-done((bf16[2,256,384]{2,1,0:T(8,128)(2,1)}, bf16[2,256,384]{2,1,0:T(8,128)(2,1)}, u32[]{:S(2)}, u32[]{:S(2)}) %collective-permute-start.1) | collective-permute-done | bytes 393248 | tf_op jit(solution)/shard_map/ppermute | solution.py:13
  24.8 1.2 %pad_maximum_fusion.4 = bf16[2,2,256,384]{3,2,1,0:T(8,128)(2,1)S(1)} fusion(bf16[1,2,256,384]{3,2,1,0:T(8,128)(2,1)} %bitcast.7, bf16[1,2,256,384]{3,2,1,0:T(8,128)(2,1)} %bitcast.6), kind=kLoop, calls=%fused_computation.51 | loop fusion | flops 393216 | bytes 1572864 | tf_op jit(solution)/shard_map/stack | solution.py:103
  26.0 2.8 %collective-permute-start.2 = (bf16[2,2,256,384]{3,2,1,0:T(8,128)(2,1)S(1)}, bf16[2,2,256,384]{3,2,1,0:T(8,128)(2,1)S(1)}, u32[]{:S(2)}, u32[]{:S(2)}) collective-permute-start(bf16[2,2,256,384]{3,2,1,0:T(8,128)(2,1)S(1)} %pad_maximum_fusion.4), channel_id=1, source_target_pairs={{0,1},{1,0},{2,3},{3,2},{4,5},{5,4},{6,7},{7,6},{8,9},{9,8},{10,11... | collective-permute-start | bytes 2359304 | tf_op jit(solution)/shard_map/ppermute | solution.py:103
  28.8 1.0 %broadcast_select_fusion = bf16[512,384]{1,0:T(8,128)(2,1)S(1)} fusion(bf16[512,384]{1,0:T(8,128)(2,1)} %collective-permute-done.5, bf16[512,384]{1,0:T(8,128)(2,1)} %collective-permute-done.6, pred[]{:T(512)S(6)} %eq.12), kind=kLoop, calls=%fused_computation.95 | loop fusion | flops 196608 | bytes 1179649 | tf_op jit(solution)/shard_map/jit(_where)/select_n | solution.py:90
  29.9 2.8 %collective-permute-start.8 = (bf16[256,384]{1,0:T(8,128)(2,1)S(1)}, bf16[256,384]{1,0:T(8,128)(2,1)S(1)}, u32[]{:S(2)}, u32[]{:S(2)}) collective-permute-start(bf16[256,384]{1,0:T(8,128)(2,1)S(1)} %get-tuple-element.26), channel_id=1, source_target_pairs={{0,4},{4,8},{8,12},{1,5},{5,9},{9,13},{2,6},{6,10},{10,14},{3,7},{... | collective-permute-start | bytes 589832 | tf_op jit(solution)/shard_map/ppermute | solution.py:13
  32.6 1.3 %collective-permute-start.7 = (bf16[256,384]{1,0:T(8,128)(2,1)S(1)}, bf16[256,384]{1,0:T(8,128)(2,1)S(1)}, u32[]{:S(2)}, u32[]{:S(2)}) collective-permute-start(bf16[256,384]{1,0:T(8,128)(2,1)S(1)} %get-tuple-element.27), channel_id=1, source_target_pairs={{4,0},{8,4},{12,8},{5,1},{9,5},{13,9},{6,2},{10,6},{14,10},{7,3},{... | collective-permute-start | bytes 589832 | tf_op jit(solution)/shard_map/ppermute | solution.py:13
  33.9 0.4 fusion.77
  34.3 2.6 %collective-permute-done.8 = bf16[256,384]{1,0:T(8,128)(2,1)S(1)} collective-permute-done((bf16[256,384]{1,0:T(8,128)(2,1)S(1)}, bf16[256,384]{1,0:T(8,128)(2,1)S(1)}, u32[]{:S(2)}, u32[]{:S(2)}) %collective-permute-start.8) | collective-permute-done | bytes 196640 | tf_op jit(solution)/shard_map/ppermute | solution.py:13
  37.0 0.4 fusion.52
  37.4 3.7 %collective-permute-done.7 = bf16[256,384]{1,0:T(8,128)(2,1)S(1)} collective-permute-done((bf16[256,384]{1,0:T(8,128)(2,1)S(1)}, bf16[256,384]{1,0:T(8,128)(2,1)S(1)}, u32[]{:S(2)}, u32[]{:S(2)}) %collective-permute-start.7) | collective-permute-done | bytes 196640 | tf_op jit(solution)/shard_map/ppermute | solution.py:13
  41.1 0.4 fusion.48
  41.6 1.6 %fusion.47 = (bf16[512,1,384]{2,0,1:T(8,128)(2,1)S(1)}, bf16[512,1,384]{2,0,1:T(8,128)(2,1)S(1)}, bf16[512,1,384]{2,0,1:T(8,128)(2,1)S(1)}, bf16[512,1,384]{2,0,1:T(8,128)(2,1)S(1)}, bf16[1,512,384]{2,1,0:T(8,128)(2,1)S(1)}) fusion(bf16[2,256,384]{2,1,0:T(8,128)(2,1)} %collective-permute-done.1, bf16[1,512,384]{2,1,0:T(8,128)(2,1)S(1)} %copy-done.1, ...), kind=kLoop, calls=%fused_computation.72 | loop fusion | flops 4915200 | bytes 3932161 | tf_op jit(solution)/shard_map/stack | solution.py:22
  43.2 0.4 convolution_add_fusion
  43.6 1.6 %collective-permute-start.13 = (f32[2,96,384]{2,1,0:T(8,128)S(1)}, f32[2,96,384]{2,1,0:T(8,128)S(1)}, u32[]{:S(2)}, u32[]{:S(2)}) collective-permute-start(f32[2,96,384]{2,1,0:T(8,128)S(1)} %select_bitcast_fusion.1), channel_id=1, source_target_pairs={{0,4},{4,0},{8,12},{12,8},{1,5},{5,1},{9,13},{13,9},{2,6},{6,2},{1... | collective-permute-start | bytes 884744 | tf_op jit(solution)/shard_map/ppermute | solution.py:59
  45.3 1.3 %convolution_add_fusion.1 = f32[384,384]{1,0:T(8,128)S(1)} fusion(f32[384,384]{1,0:T(8,128)S(1)} %fusion.52, bf16[1,512,384]{2,1,0:T(8,128)(2,1)S(1)} %get-tuple-element.25, bf16[2,256,384]{2,1,0:T(8,128)(2,1)} %collective-permute-done.1, bf16[1,512,384]{2,1,0:T(8,128)(2,1)S(1)} %copy-done.1, bf16[1,512,384]{2,1,0:T(8,128)(2,1)S(1)} %bitcast.153), kind=kOutput, calls=%fused_computation.11 | convolution fusion | flops 152322048 | bytes 2752512 | tf_op jit(solution)/shard_map/dot_general | solution.py:142
  46.6 1.3 %convolution_add_fusion.2 = f32[384,384]{1,0:T(8,128)S(1)} fusion(f32[384,384]{1,0:T(8,128)S(1)} %fusion.48, bf16[1,512,384]{2,1,0:T(8,128)(2,1)S(1)} %get-tuple-element.25, bf16[2,256,384]{2,1,0:T(8,128)(2,1)} %collective-permute-done, bf16[1,512,384]{2,1,0:T(8,128)(2,1)S(1)} %copy-done.1, bf16[1,512,384]{2,1,0:T(8,128)(2,1)S(1)} %bitcast.154), kind=kOutput, calls=%fused_computation.12 | convolution fusion | flops 152322048 | bytes 2752512 | tf_op jit(solution)/shard_map/dot_general | solution.py:142
  48.1 0.5 collective-permute-start.9
  48.6 1.2 %slice.184 = bf16[1024,384]{1,0:T(8,128)(2,1)S(1)} slice(bf16[2176,384]{1,0:T(8,128)(2,1)} %collective-permute-done.3), slice={[0:1024], [0:384]} | slice | bytes 1572864 | tf_op jit(solution)/shard_map/slice | solution.py:99
  49.8 0.2 fusion.45
  50.0 1.2 %slice_bitcast_fusion.3 = (bf16[512,1,384]{2,0,1:T(8,128)(2,1)S(1)}, bf16[512,1,384]{2,0,1:T(8,128)(2,1)S(1)}) fusion(bf16[2176,384]{1,0:T(8,128)(2,1)} %collective-permute-done.3), kind=kLoop, calls=%fused_computation.96 | loop fusion | bytes 1572864 | tf_op jit(solution)/shard_map/stack | solution.py:22
  51.2 0.8 convolution_bitcast_fusion
  52.1 0.3 copy-done.3
  52.3 1.3 %fusion.33 = bf16[512,384]{1,0:T(8,128)(2,1)S(1)} fusion(f32[512,384]{1,0:T(8,128)S(1)} %copy-done.3, f32[512,384]{1,0:T(8,128)S(1)} %convolution_bitcast_fusion, bf16[512,1,384]{2,0,1:T(8,128)(2,1)S(1)} %get-tuple-element.16, bf16[512,1,384]{2,0,1:T(8,128)(2,1)S(1)} %bitcast.160, bf16[512,1,384]{2,0,1:T(8,128)(2,1)S(1)} %get-tuple-element.7, ...), kind=kOutput, calls=%fused_computation.50 | convolution fusion | flops 458883072 | bytes 4423684 | tf_op jit(solution)/shard_map/tko,kio->ti/dot_general | solution.py:116
  53.7 1.3 %slice.187 = bf16[1152,384]{1,0:T(8,128)(2,1)S(1)} slice(bf16[2176,384]{1,0:T(8,128)(2,1)} %collective-permute-done.3), slice={[1024:2176], [0:384]} | slice | bytes 1769472 | tf_op jit(solution)/shard_map/slice | solution.py:100
  55.0 1.4 %collective-permute-start.14 = (f32[96,384]{1,0:T(8,128)S(1)}, f32[96,384]{1,0:T(8,128)S(1)}, u32[]{:S(2)}, u32[]{:S(2)}) collective-permute-start(f32[96,384]{1,0:T(8,128)S(1)} %select_bitcast_fusion.7), channel_id=1, source_target_pairs={{0,8},{8,0},{4,12},{12,4},{1,9},{9,1},{5,13},{13,5},{2,10},{10,2},... | collective-permute-start | bytes 442376 | tf_op jit(solution)/shard_map/ppermute | solution.py:64
  56.4 10.9 %collective-permute-done.9 = f32[2,192,384]{2,1,0:T(8,128)S(1)} collective-permute-done((f32[2,192,384]{2,1,0:T(8,128)S(1)}, f32[2,192,384]{2,1,0:T(8,128)S(1)}, u32[]{:S(2)}, u32[]{:S(2)}) %collective-permute-start.9) | collective-permute-done | bytes 589856 | tf_op jit(solution)/shard_map/ppermute | solution.py:59
  67.6 3.0 %collective-permute-start.15 = (bf16[96,384]{1,0:T(8,128)(2,1)S(1)}, bf16[96,384]{1,0:T(8,128)(2,1)S(1)}, u32[]{:S(2)}, u32[]{:S(2)}) collective-permute-start(bf16[96,384]{1,0:T(8,128)(2,1)S(1)} %fusion.64), channel_id=1, source_target_pairs={{0,8},{8,0},{4,12},{12,4},{1,9},{9,1},{5,13},{13,5},{2,10},{10,2},... | collective-permute-start | bytes 221192 | tf_op jit(solution)/shard_map/ppermute | solution.py:65
  70.5 0.8 convolution_bitcast_fusion.3
  71.3 12.8 %collective-permute-done.15 = bf16[96,384]{1,0:T(8,128)(2,1)S(1)} collective-permute-done((bf16[96,384]{1,0:T(8,128)(2,1)S(1)}, bf16[96,384]{1,0:T(8,128)(2,1)S(1)}, u32[]{:S(2)}, u32[]{:S(2)}) %collective-permute-start.15) | collective-permute-done | bytes 73760 | tf_op jit(solution)/shard_map/ppermute | solution.py:65
  84.3 3.0 %collective-permute-start.11 = (bf16[192,384]{1,0:T(8,128)(2,1)S(1)}, bf16[192,384]{1,0:T(8,128)(2,1)S(1)}, u32[]{:S(2)}, u32[]{:S(2)}) collective-permute-start(bf16[192,384]{1,0:T(8,128)(2,1)S(1)} %fusion.63), channel_id=1, source_target_pairs={{0,8},{8,0},{4,12},{12,4},{1,9},{9,1},{5,13},{13,5},{2,10},{10,2},... | collective-permute-start | bytes 442376 | tf_op jit(solution)/shard_map/ppermute | solution.py:65
  87.2 1.6 %fusion.4 = bf16[1,512,384]{2,1,0:T(8,128)(2,1)} fusion(f32[512,384]{1,0:T(8,128)S(1)} %copy-done.3, f32[512,384]{1,0:T(8,128)S(1)} %convolution_bitcast_fusion.3, bf16[3,384,384]{2,1,0:T(8,128)(2,1)S(1)} %bitcast.171, bf16[512,1,384]{2,0,1:T(8,128)(2,1)S(1)} %get-tuple-element.12, bf16[512,1,384]{2,0,1:T(8,128)(2,1)S(1)} %get-tuple-element.4, ...), kind=kOutput, calls=%fused_computation.13 | convolution fusion | flops 454754304 | bytes 4030464 | tf_op jit(solution)/shard_map/tki,kio->to/dot_general | solution.py:110
  88.8 0.4 broadcast_in_dim.8
  89.2 1.2 %convert_element_type.50 = bf16[1,1024,384]{2,1,0:T(8,128)(2,1)} reshape(bf16[512,2,384]{2,1,0:T(2,128)(2,1)S(1)} %broadcast_in_dim.8) | data formatting | bytes 1572864 | tf_op jit(solution)/shard_map/convert_element_type | solution.py:125
  90.4 3.8 %collective-permute-done.11 = bf16[192,384]{1,0:T(8,128)(2,1)S(1)} collective-permute-done((bf16[192,384]{1,0:T(8,128)(2,1)S(1)}, bf16[192,384]{1,0:T(8,128)(2,1)S(1)}, u32[]{:S(2)}, u32[]{:S(2)}) %collective-permute-start.11) | collective-permute-done | bytes 147488 | tf_op jit(solution)/shard_map/ppermute | solution.py:65
  94.3 0.3 collective-permute-start.12
  94.7 6.4 %collective-permute-done.12 = bf16[2,192,384]{2,1,0:T(8,128)(2,1)S(1)} collective-permute-done((bf16[2,192,384]{2,1,0:T(8,128)(2,1)S(1)}, bf16[2,192,384]{2,1,0:T(8,128)(2,1)S(1)}, u32[]{:S(2)}, u32[]{:S(2)}) %collective-permute-start.12) | collective-permute-done | bytes 294944 | tf_op jit(solution)/shard_map/ppermute | solution.py:67
  101.4 1.3 %pad_maximum_fusion = f32[3,384,384]{2,1,0:T(8,128)} fusion(f32[1,384,384]{2,1,0:T(8,128)S(1)} %bitcast.168, f32[1,384,384]{2,1,0:T(8,128)S(1)} %bitcast.166, f32[1,384,384]{2,1,0:T(8,128)S(1)} %bitcast.167), kind=kLoop, calls=%fused_computation | loop fusion | flops 884736 | bytes 3538944 | tf_op jit(solution)/shard_map/stack | solution.py:148
  (38 shorter events, 1.3 us)
Async XLA Ops:
  0.6 14.9 %copy-start = (bf16[3,384,768]{2,1,0:T(8,128)(2,1)S(1)}, bf16[3,384,768]{2,1,0:T(8,128)(2,1)}, u32[]{:S(2)}) copy-start(bf16[3,384,768]{2,1,0:T(8,128)(2,1)} %param.5) | copy-start | bytes 5308420
  0.6 6.0 %copy-start.1 = (bf16[1,512,384]{2,1,0:T(8,128)(2,1)S(1)}, bf16[1,512,384]{2,1,0:T(8,128)(2,1)}, u32[]{:S(2)}) copy-start(bf16[1,512,384]{2,1,0:T(8,128)(2,1)} %param.6) | copy-start | bytes 1179652
  0.7 28.1 %collective-permute-start.5 = (bf16[512,384]{1,0:T(8,128)(2,1)}, bf16[512,384]{1,0:T(8,128)(2,1)}, u32[]{:S(2)}, u32[]{:S(2)}) collective-permute-start(bf16[512,384]{1,0:T(8,128)(2,1)} %bitcast.158), channel_id=1, source_target_pairs={{2,0},{1,3},{6,4},{5,7},{10,8},{9,11},{14,12},{13,15},{18,16},{17,... | collective-permute-start | bytes 1179656 | tf_op jit(solution)/shard_map/ppermute | solution.py:88
  2.1 26.7 %collective-permute-start.6 = (bf16[512,384]{1,0:T(8,128)(2,1)}, bf16[512,384]{1,0:T(8,128)(2,1)}, u32[]{:S(2)}, u32[]{:S(2)}) collective-permute-start(bf16[512,384]{1,0:T(8,128)(2,1)} %bitcast.159), channel_id=1, source_target_pairs={{2,1},{1,2},{6,5},{5,6},{10,9},{9,10},{14,13},{13,14},{18,17},{17,... | collective-permute-start | bytes 1179656 | tf_op jit(solution)/shard_map/ppermute | solution.py:89
  7.6 14.1 %collective-permute-start = (bf16[2,256,384]{2,1,0:T(8,128)(2,1)}, bf16[2,256,384]{2,1,0:T(8,128)(2,1)}, u32[]{:S(2)}, u32[]{:S(2)}) collective-permute-start(bf16[2,256,384]{2,1,0:T(8,128)(2,1)} %get-tuple-element.21), channel_id=1, source_target_pairs={{0,4},{4,8},{8,12},{1,5},{5,9},{9,13},{2,6},{6,10},{10,14},{3,7},{... | collective-permute-start | bytes 1179656 | tf_op jit(solution)/shard_map/ppermute | solution.py:13
  13.3 11.5 %collective-permute-start.1 = (bf16[2,256,384]{2,1,0:T(8,128)(2,1)}, bf16[2,256,384]{2,1,0:T(8,128)(2,1)}, u32[]{:S(2)}, u32[]{:S(2)}) collective-permute-start(bf16[2,256,384]{2,1,0:T(8,128)(2,1)} %get-tuple-element.22), channel_id=1, source_target_pairs={{4,0},{8,4},{12,8},{5,1},{9,5},{13,9},{6,2},{10,6},{14,10},{7,3},{... | collective-permute-start | bytes 1179656 | tf_op jit(solution)/shard_map/ppermute | solution.py:13
  15.5 1.1 %copy-start.2 = (bf16[2,512,384]{2,1,0:T(8,128)(2,1)S(1)}, bf16[2,512,384]{2,1,0:T(8,128)(2,1)}, u32[]{:S(2)}) copy-start(bf16[2,512,384]{2,1,0:T(8,128)(2,1)} %pad_maximum_fusion.3) | copy-start | bytes 2359300
  18.0 23.6 %collective-permute-start.3 = (bf16[2176,384]{1,0:T(8,128)(2,1)}, bf16[2176,384]{1,0:T(8,128)(2,1)}, u32[]{:S(2)}, u32[]{:S(2)}) collective-permute-start(bf16[2176,384]{1,0:T(8,128)(2,1)} %pad_maximum_fusion.1), channel_id=1, source_target_pairs={{0,1},{1,0},{2,3},{3,2},{4,5},{5,4},{6,7},{7,6},{8,9},{9,8},{10,11... | collective-permute-start | bytes 5013512 | tf_op jit(solution)/shard_map/ppermute | solution.py:96
  21.7 12.2 %collective-permute-start.4 = (bf16[512,384]{1,0:T(8,128)(2,1)S(1)}, bf16[512,384]{1,0:T(8,128)(2,1)S(1)}, u32[]{:S(2)}, u32[]{:S(2)}) collective-permute-start(bf16[512,384]{1,0:T(8,128)(2,1)S(1)} %get-tuple-element.30), channel_id=1, source_target_pairs={{0,2},{2,0},{1,3},{3,1},{4,6},{6,4},{5,7},{7,5},{8,10},{10,8},{9,1... | collective-permute-start | bytes 1179656 | tf_op jit(solution)/shard_map/ppermute | solution.py:91
  26.0 15.5 %collective-permute-start.2 = (bf16[2,2,256,384]{3,2,1,0:T(8,128)(2,1)S(1)}, bf16[2,2,256,384]{3,2,1,0:T(8,128)(2,1)S(1)}, u32[]{:S(2)}, u32[]{:S(2)}) collective-permute-start(bf16[2,2,256,384]{3,2,1,0:T(8,128)(2,1)S(1)} %pad_maximum_fusion.4), channel_id=1, source_target_pairs={{0,1},{1,0},{2,3},{3,2},{4,5},{5,4},{6,7},{7,6},{8,9},{9,8},{10,11... | collective-permute-start | bytes 2359304 | tf_op jit(solution)/shard_map/ppermute | solution.py:103
  29.9 7.1 %collective-permute-start.8 = (bf16[256,384]{1,0:T(8,128)(2,1)S(1)}, bf16[256,384]{1,0:T(8,128)(2,1)S(1)}, u32[]{:S(2)}, u32[]{:S(2)}) collective-permute-start(bf16[256,384]{1,0:T(8,128)(2,1)S(1)} %get-tuple-element.26), channel_id=1, source_target_pairs={{0,4},{4,8},{8,12},{1,5},{5,9},{9,13},{2,6},{6,10},{10,14},{3,7},{... | collective-permute-start | bytes 589832 | tf_op jit(solution)/shard_map/ppermute | solution.py:13
  32.6 8.5 %collective-permute-start.7 = (bf16[256,384]{1,0:T(8,128)(2,1)S(1)}, bf16[256,384]{1,0:T(8,128)(2,1)S(1)}, u32[]{:S(2)}, u32[]{:S(2)}) collective-permute-start(bf16[256,384]{1,0:T(8,128)(2,1)S(1)} %get-tuple-element.27), channel_id=1, source_target_pairs={{4,0},{8,4},{12,8},{5,1},{9,5},{13,9},{6,2},{10,6},{14,10},{7,3},{... | collective-permute-start | bytes 589832 | tf_op jit(solution)/shard_map/ppermute | solution.py:13
  43.6 11.3 %collective-permute-start.13 = (f32[2,96,384]{2,1,0:T(8,128)S(1)}, f32[2,96,384]{2,1,0:T(8,128)S(1)}, u32[]{:S(2)}, u32[]{:S(2)}) collective-permute-start(f32[2,96,384]{2,1,0:T(8,128)S(1)} %select_bitcast_fusion.1), channel_id=1, source_target_pairs={{0,4},{4,0},{8,12},{12,8},{1,5},{5,1},{9,13},{13,9},{2,6},{6,2},{1... | collective-permute-start | bytes 884744 | tf_op jit(solution)/shard_map/ppermute | solution.py:59
  48.1 19.2 %collective-permute-start.9 = (f32[2,192,384]{2,1,0:T(8,128)S(1)}, f32[2,192,384]{2,1,0:T(8,128)S(1)}, u32[]{:S(2)}, u32[]{:S(2)}) collective-permute-start(f32[2,192,384]{2,1,0:T(8,128)S(1)} %select_bitcast_fusion), channel_id=1, source_target_pairs={{0,4},{4,0},{8,12},{12,8},{1,5},{5,1},{9,13},{13,9},{2,6},{6,2},{1... | collective-permute-start | bytes 1769480 | tf_op jit(solution)/shard_map/ppermute | solution.py:59
  51.2 1.1 %copy-start.3 = (f32[512,384]{1,0:T(8,128)S(1)}, f32[512,384]{1,0:T(8,128)}, u32[]{:S(2)}) copy-start(f32[512,384]{1,0:T(8,128)} %get-tuple-element.31) | copy-start | bytes 2359300
  55.0 12.5 %collective-permute-start.14 = (f32[96,384]{1,0:T(8,128)S(1)}, f32[96,384]{1,0:T(8,128)S(1)}, u32[]{:S(2)}, u32[]{:S(2)}) collective-permute-start(f32[96,384]{1,0:T(8,128)S(1)} %select_bitcast_fusion.7), channel_id=1, source_target_pairs={{0,8},{8,0},{4,12},{12,4},{1,9},{9,1},{5,13},{13,5},{2,10},{10,2},... | collective-permute-start | bytes 442376 | tf_op jit(solution)/shard_map/ppermute | solution.py:64
  67.4 16.8 %collective-permute-start.10 = (f32[192,384]{1,0:T(8,128)S(1)}, f32[192,384]{1,0:T(8,128)S(1)}, u32[]{:S(2)}, u32[]{:S(2)}) collective-permute-start(f32[192,384]{1,0:T(8,128)S(1)} %select_bitcast_fusion.4), channel_id=1, source_target_pairs={{0,8},{8,0},{4,12},{12,4},{1,9},{9,1},{5,13},{13,5},{2,10},{10,2},... | collective-permute-start | bytes 884744 | tf_op jit(solution)/shard_map/ppermute | solution.py:64
  67.6 16.6 %collective-permute-start.15 = (bf16[96,384]{1,0:T(8,128)(2,1)S(1)}, bf16[96,384]{1,0:T(8,128)(2,1)S(1)}, u32[]{:S(2)}, u32[]{:S(2)}) collective-permute-start(bf16[96,384]{1,0:T(8,128)(2,1)S(1)} %fusion.64), channel_id=1, source_target_pairs={{0,8},{8,0},{4,12},{12,4},{1,9},{9,1},{5,13},{13,5},{2,10},{10,2},... | collective-permute-start | bytes 221192 | tf_op jit(solution)/shard_map/ppermute | solution.py:65
  84.1 10.4 %collective-permute-start.16 = (bf16[2,96,384]{2,1,0:T(8,128)(2,1)S(1)}, bf16[2,96,384]{2,1,0:T(8,128)(2,1)S(1)}, u32[]{:S(2)}, u32[]{:S(2)}) collective-permute-start(bf16[2,96,384]{2,1,0:T(8,128)(2,1)S(1)} %maximum_select_fusion.1), channel_id=1, source_target_pairs={{0,4},{4,0},{8,12},{12,8},{1,5},{5,1},{9,13},{13,9},{2,6},{6,2},{1... | collective-permute-start | bytes 442376 | tf_op jit(solution)/shard_map/ppermute | solution.py:67
  84.3 9.9 %collective-permute-start.11 = (bf16[192,384]{1,0:T(8,128)(2,1)S(1)}, bf16[192,384]{1,0:T(8,128)(2,1)S(1)}, u32[]{:S(2)}, u32[]{:S(2)}) collective-permute-start(bf16[192,384]{1,0:T(8,128)(2,1)S(1)} %fusion.63), channel_id=1, source_target_pairs={{0,8},{8,0},{4,12},{12,4},{1,9},{9,1},{5,13},{13,5},{2,10},{10,2},... | collective-permute-start | bytes 442376 | tf_op jit(solution)/shard_map/ppermute | solution.py:65
  94.3 6.8 %collective-permute-start.12 = (bf16[2,192,384]{2,1,0:T(8,128)(2,1)S(1)}, bf16[2,192,384]{2,1,0:T(8,128)(2,1)S(1)}, u32[]{:S(2)}, u32[]{:S(2)}) collective-permute-start(bf16[2,192,384]{2,1,0:T(8,128)(2,1)S(1)} %maximum_select_fusion), channel_id=1, source_target_pairs={{0,4},{4,0},{8,12},{12,8},{1,5},{5,1},{9,13},{13,9},{2,6},{6,2},{1... | collective-permute-start | bytes 884744 | tf_op jit(solution)/shard_map/ppermute | solution.py:67

commit v24 on v11

--- a/solution.py
+++ b/solution.py
@@ -67,6 +67,27 @@
     evens = jnp.where(odd, far_set, own_set)
     odds = jnp.where(odd, own_set, far_set)
     return jnp.stack([evens, odds], 1).reshape(block.shape).astype(jnp.float32)
+
+
+def line_total_across(block):
+    s = lax.axis_index("seq")
+    odd = (s % 2) == 1
+    low = s < 2
+    rows = block.shape[0] // 4
+    quarters = block.reshape(2, 2, rows, block.shape[1])
+    pairs, across = [(0, 1), (1, 0), (2, 3), (3, 2)], [(0, 2), (2, 0), (1, 3), (3, 1)]
+    row = jnp.where(low, quarters[0], quarters[1]) + lax.ppermute(
+        jnp.where(low, quarters[1], quarters[0]), "seq", across
+    )
+    keep = jnp.where(odd, row[1], row[0])
+    give = jnp.where(odd, row[0], row[1])
+    total = (keep + lax.ppermute(give, "seq", pairs)).astype(jnp.bfloat16)
+    other = lax.ppermute(total, "seq", pairs)
+    own_row = jnp.where(odd, jnp.stack([other, total]), jnp.stack([total, other]))
+    far_row = lax.ppermute(own_row, "seq", across)
+    lows = jnp.where(low, own_row, far_row)
+    highs = jnp.where(low, far_row, own_row)
+    return jnp.stack([lows, highs]).reshape(block.shape).astype(jnp.float32)
 
 
 def shards(seq_in, conv_weight, cotangent):
@@ -144,7 +165,7 @@
             ) + jnp.dot(far_mid.T, far_shifted[k], preferred_element_type=jnp.float32)
         if seq_count == 4:
             middle = line_total(grads[1])
-            sides = line_total(jnp.concatenate([grads[0], grads[2]], 0))
+            sides = line_total_across(jnp.concatenate([grads[0], grads[2]], 0))
             weight_grad = jnp.stack([sides[: middle.shape[0]], middle, sides[middle.shape[0] :]])
         else:
             weight_grad = lax.psum(jnp.stack([grads[0], grads[1], grads[2]]), "seq")

time: 103 us -> 108 us (1.049)
  waiting for transfers between devices: 42.3 us -> 47.2 us
  starting transfers between devices: 31.2 us -> 34.2 us
  matrix products: 11.5 us -> 9.72 us
  other arithmetic: 9.42 us -> 7.76 us
    ppermute x0 -> x4, waiting for transfers between devices: none -> 36.9 us  [the longest x1 21 us: line_total_across(): lax.ppermute(jnp.where(low, quarters[1], quarters[0]), 'seq', across)]
    ppermute x2 -> x1, waiting for transfers between devices: 16.6 us -> 2.93 us  [line_total(): other = lax.ppermute(total, 'seq', across)]
    ppermute x2 -> x1, waiting for transfers between devices: 10.9 us -> 1.45 us  [line_total(): lax.ppermute(jnp.where(odd, even_set, odd_set), 'seq', pairs)]
    ppermute x2 -> x1, waiting for transfers between devices: 6.41 us -> 0.01 us  [line_total(): far_set = lax.ppermute(own_set, 'seq', pairs)]
    ppermute x2 -> x1, starting transfers between devices: 5.92 us -> 1.68 us  [line_total(): other = lax.ppermute(total, 'seq', across)]
    ppermute x4, waiting for transfers between devices: 8.39 us -> 4.46 us  [shift_from(): return lax.ppermute(block, axis, route)]
    ppermute x0 -> x4, starting transfers between devices: none -> 3.47 us  [the longest x1 2.63 us: line_total_across(): lax.ppermute(jnp.where(low, quarters[1], quarters[0]), 'seq', across)]
    ppermute x2 -> x1, starting transfers between devices: 0.33 us -> 2.69 us  [line_total(): far_set = lax.ppermute(own_set, 'seq', pairs)]
  transfers between devices with their start and end apart: 17 -> 17, of which waited for: 7 -> 10; matrix products, arithmetic and copies ran while one was open for 22% -> 19% of each run, Pallas kernels for 0% -> 0%
where the time goes in v24:
time: 108 us; the launch traced here: 107 us
  waiting for transfers between devices  47.2 us (44%)
  starting transfers between devices  34.2 us (32%)
  matrix products  9.72 us (9%)
  other arithmetic  7.76 us (7%)
  local copies, waits for them, and re-layouts  7.3 us (7%)
    ppermute x1, waiting for transfers between devices, line_total_across(): lax.ppermute(jnp.where(low, quarters[1], quarters[0]), 'seq', across)  21 us
    ppermute x1, waiting for transfers between devices, line_total_across(): far_row = lax.ppermute(own_row, 'seq', across)  12.3 us
    ppermute x4, starting transfers between devices, shift_from(): return lax.ppermute(block, axis, route)  12.1 us
    ppermute x4, waiting for transfers between devices, shift_from(): return lax.ppermute(block, axis, route)  4.46 us
    ppermute x1, starting transfers between devices, shards(): lax.ppermute(jnp.concatenate([both.reshape(-1, width), w_other.reshape(-1...  3.72 us
    ppermute x1, starting transfers between devices, shards(): par_halo = lax.ppermute(jnp.stack([from_prev, from_next]), 'chan', SWAP)  2.93 us
    ppermute x1, waiting for transfers between devices, line_total(): other = lax.ppermute(total, 'seq', across)  2.93 us
    dot_general x1, matrix products, shards(): pooled = jnp.dot(pairing, local_in, preferred_element_type=jnp.float32)  2.81 us
  transfers between devices with their start and end apart: 17, of which 10 were waited for; matrix products, arithmetic and copies ran while one was open for 19% of the time, Pallas kernels for 0%

profile of v24, /device:TPU:0, one launch (start us, length us, event | category | flops | bytes accessed | tf_op | source)
XLA Modules:
  0.0 107.1 jit_solution(17579055242989067348)
XLA Ops:
  0.6 1.4 %collective-permute-start.5 = (bf16[512,384]{1,0:T(8,128)(2,1)}, bf16[512,384]{1,0:T(8,128)(2,1)}, u32[]{:S(2)}, u32[]{:S(2)}) collective-permute-start(bf16[512,384]{1,0:T(8,128)(2,1)} %bitcast.142), channel_id=1, source_target_pairs={{2,0},{1,3},{6,4},{5,7},{10,8},{9,11},{14,12},{13,15},{18,16},{17,... | collective-permute-start | bytes 1179656 | tf_op jit(solution)/shard_map/ppermute | solution.py:109
  2.1 1.4 %collective-permute-start.6 = (bf16[512,384]{1,0:T(8,128)(2,1)}, bf16[512,384]{1,0:T(8,128)(2,1)}, u32[]{:S(2)}, u32[]{:S(2)}) collective-permute-start(bf16[512,384]{1,0:T(8,128)(2,1)} %bitcast.143), channel_id=1, source_target_pairs={{2,1},{1,2},{6,5},{5,6},{10,9},{9,10},{14,13},{13,14},{18,17},{17,... | collective-permute-start | bytes 1179656 | tf_op jit(solution)/shard_map/ppermute | solution.py:110
  3.5 2.8 %multiply_convert_fusion = (bf16[512,384]{1,0:T(8,128)(2,1)S(1)}, f32[512,384]{1,0:T(8,128)}) fusion(bf16[1,1024,384]{2,1,0:T(8,128)(2,1)} %param.3, s32[1024]{0:T(1024)S(1)} %get-tuple-element.34, s32[1024]{0:T(1024)S(1)} %get-tuple-element.35, pred[1024]{0:T(1024)(128)(4,1)S(1)} %fusion.70), kind=kOutput, calls=%fused_computation.60 | convolution fusion | flops 406519808 | bytes 1975296 | tf_op jit(solution)/shard_map/dot_general | solution.py:104
  6.3 1.0 fusion.45
  7.3 5.0 %collective-permute-start = (bf16[2,256,384]{2,1,0:T(8,128)(2,1)}, bf16[2,256,384]{2,1,0:T(8,128)(2,1)S(1)}, u32[]{:S(2)}, u32[]{:S(2)}) collective-permute-start(bf16[2,256,384]{2,1,0:T(8,128)(2,1)} %get-tuple-element.23), channel_id=1, source_target_pairs={{0,4},{4,8},{8,12},{1,5},{5,9},{9,13},{2,6},{6,10},{10,14},{3,7},{... | collective-permute-start | bytes 1179656 | tf_op jit(solution)/shard_map/ppermute | solution.py:12
  12.3 1.3 %collective-permute-start.1 = (bf16[2,256,384]{2,1,0:T(8,128)(2,1)}, bf16[2,256,384]{2,1,0:T(8,128)(2,1)S(1)}, u32[]{:S(2)}, u32[]{:S(2)}) collective-permute-start(bf16[2,256,384]{2,1,0:T(8,128)(2,1)} %get-tuple-element.24), channel_id=1, source_target_pairs={{4,0},{8,4},{12,8},{5,1},{9,5},{13,9},{6,2},{10,6},{14,10},{7,3},{... | collective-permute-start | bytes 1179656 | tf_op jit(solution)/shard_map/ppermute | solution.py:12
  13.6 1.0 pad_maximum_fusion.2
  14.7 1.3 %copy-done.4 = bf16[2,512,384]{2,1,0:T(8,128)(2,1)S(1)} copy-done((bf16[2,512,384]{2,1,0:T(8,128)(2,1)S(1)}, bf16[2,512,384]{2,1,0:T(8,128)(2,1)}, u32[]{:S(2)}) %copy-start.4) | copy-done | bytes 786456
  16.0 1.3 %pad_maximum_fusion.1 = bf16[2176,384]{1,0:T(8,128)(2,1)} fusion(bf16[1152,384]{1,0:T(8,128)(2,1)S(1)} %bitcast.148, bf16[1024,384]{1,0:T(8,128)(2,1)S(1)} %bitcast.150), kind=kLoop, calls=%fused_computation.3 | loop fusion | flops 3342336 | bytes 3342336 | tf_op jit(solution)/shard_map/concatenate | solution.py:118
  17.3 3.7 %collective-permute-start.3 = (bf16[2176,384]{1,0:T(8,128)(2,1)}, bf16[2176,384]{1,0:T(8,128)(2,1)}, u32[]{:S(2)}, u32[]{:S(2)}) collective-permute-start(bf16[2176,384]{1,0:T(8,128)(2,1)} %pad_maximum_fusion.1), channel_id=1, source_target_pairs={{0,1},{1,0},{2,3},{3,2},{4,5},{5,4},{6,7},{7,6},{8,9},{9,8},{10,11... | collective-permute-start | bytes 5013512 | tf_op jit(solution)/shard_map/ppermute | solution.py:117
  21.1 1.4 %collective-permute-start.4 = (bf16[512,384]{1,0:T(8,128)(2,1)S(1)}, bf16[512,384]{1,0:T(8,128)(2,1)S(1)}, u32[]{:S(2)}, u32[]{:S(2)}) collective-permute-start(bf16[512,384]{1,0:T(8,128)(2,1)S(1)} %get-tuple-element.32), channel_id=1, source_target_pairs={{0,2},{2,0},{1,3},{3,1},{4,6},{6,4},{5,7},{7,5},{8,10},{10,8},{9,1... | collective-permute-start | bytes 1179656 | tf_op jit(solution)/shard_map/ppermute | solution.py:112
  22.4 1.2 %collective-permute-done.1 = bf16[2,256,384]{2,1,0:T(8,128)(2,1)S(1)} collective-permute-done((bf16[2,256,384]{2,1,0:T(8,128)(2,1)}, bf16[2,256,384]{2,1,0:T(8,128)(2,1)S(1)}, u32[]{:S(2)}, u32[]{:S(2)}) %collective-permute-start.1) | collective-permute-done | bytes 393248 | tf_op jit(solution)/shard_map/ppermute | solution.py:12
  23.7 2.9 %collective-permute-start.2 = (bf16[2,2,256,384]{3,2,1,0:T(8,128)(2,1)S(1)}, bf16[2,2,256,384]{3,2,1,0:T(8,128)(2,1)S(1)}, u32[]{:S(2)}, u32[]{:S(2)}) collective-permute-start(bf16[2,2,256,384]{3,2,1,0:T(8,128)(2,1)S(1)} %pad_maximum_fusion.3), channel_id=1, source_target_pairs={{0,1},{1,0},{2,3},{3,2},{4,5},{5,4},{6,7},{7,6},{8,9},{9,8},{10,11... | collective-permute-start | bytes 2359304 | tf_op jit(solution)/shard_map/ppermute | solution.py:124
  26.7 1.0 broadcast_select_fusion
  27.8 1.3 %collective-permute-start.7 = (bf16[256,384]{1,0:T(8,128)(2,1)S(1)}, bf16[256,384]{1,0:T(8,128)(2,1)S(1)}, u32[]{:S(2)}, u32[]{:S(2)}) collective-permute-start(bf16[256,384]{1,0:T(8,128)(2,1)S(1)} %get-tuple-element.29), channel_id=1, source_target_pairs={{4,0},{8,4},{12,8},{5,1},{9,5},{13,9},{6,2},{10,6},{14,10},{7,3},{... | collective-permute-start | bytes 589832 | tf_op jit(solution)/shard_map/ppermute | solution.py:12
  29.1 4.6 %collective-permute-start.8 = (bf16[256,384]{1,0:T(8,128)(2,1)S(1)}, bf16[256,384]{1,0:T(8,128)(2,1)S(1)}, u32[]{:S(2)}, u32[]{:S(2)}) collective-permute-start(bf16[256,384]{1,0:T(8,128)(2,1)S(1)} %get-tuple-element.28), channel_id=1, source_target_pairs={{0,4},{4,8},{8,12},{1,5},{5,9},{9,13},{2,6},{6,10},{10,14},{3,7},{... | collective-permute-start | bytes 589832 | tf_op jit(solution)/shard_map/ppermute | solution.py:12
  33.6 0.4 fusion.85
  34.0 2.5 %collective-permute-done.7 = bf16[256,384]{1,0:T(8,128)(2,1)S(1)} collective-permute-done((bf16[256,384]{1,0:T(8,128)(2,1)S(1)}, bf16[256,384]{1,0:T(8,128)(2,1)S(1)}, u32[]{:S(2)}, u32[]{:S(2)}) %collective-permute-start.7) | collective-permute-done | bytes 196640 | tf_op jit(solution)/shard_map/ppermute | solution.py:12
  36.5 0.4 fusion.51
  36.9 0.8 collective-permute-done.8
  37.7 0.4 fusion.55
  38.2 1.2 %fusion.50 = (bf16[512,1,384]{2,0,1:T(8,128)(2,1)S(1)}, bf16[512,1,384]{2,0,1:T(8,128)(2,1)S(1)}, bf16[512,1,384]{2,0,1:T(8,128)(2,1)S(1)}, bf16[512,1,384]{2,0,1:T(8,128)(2,1)S(1)}, bf16[1,512,384]{2,1,0:T(8,128)(2,1)S(1)}) fusion(bf16[2,256,384]{2,1,0:T(8,128)(2,1)S(1)} %collective-permute-done.1, bf16[1,512,384]{2,1,0:T(8,128)(2,1)S(1)} %copy-done.1, ...), kind=kLoop, calls=%fused_computation.74 | loop fusion | flops 4915200 | bytes 3932161 | tf_op jit(solution)/shard_map/stack | solution.py:21
  39.4 0.4 convolution_add_fusion
  39.9 2.6 %collective-permute-start.13 = (f32[2,96,384]{2,1,0:T(8,128)S(1)}, f32[2,96,384]{2,1,0:T(8,128)S(1)}, u32[]{:S(2)}, u32[]{:S(2)}) collective-permute-start(f32[2,96,384]{2,1,0:T(8,128)S(1)} %select_bitcast_fusion), channel_id=1, source_target_pairs={{0,4},{4,0},{8,12},{12,8},{1,5},{5,1},{9,13},{13,9},{2,6},{6,2},{1... | collective-permute-start | bytes 884744 | tf_op jit(solution)/shard_map/ppermute | solution.py:58
  42.4 0.4 convolution_add_fusion.2
  42.8 0.4 broadcast_select_fusion.1
  43.3 2.6 %collective-permute-start.9 = (f32[2,192,384]{2,1,0:T(8,128)S(1)}, f32[2,192,384]{2,1,0:T(8,128)S(1)}, u32[]{:S(2)}, u32[]{:S(2)}) collective-permute-start(f32[2,192,384]{2,1,0:T(8,128)S(1)} %bitcast.161), channel_id=1, source_target_pairs={{0,8},{8,0},{4,12},{12,4},{1,9},{9,1},{5,13},{13,5},{2,10},{10,2},... | collective-permute-start | bytes 1769480 | tf_op jit(solution)/shard_map/ppermute | solution.py:79
  45.9 1.2 %slice.182 = bf16[1024,384]{1,0:T(8,128)(2,1)S(1)} slice(bf16[2176,384]{1,0:T(8,128)(2,1)} %collective-permute-done.3), slice={[0:1024], [0:384]} | slice | bytes 1572864 | tf_op jit(solution)/shard_map/slice | solution.py:120
  47.3 1.3 %slice_bitcast_fusion.3 = (bf16[512,1,384]{2,0,1:T(8,128)(2,1)S(1)}, bf16[512,1,384]{2,0,1:T(8,128)(2,1)S(1)}) fusion(bf16[2176,384]{1,0:T(8,128)(2,1)} %collective-permute-done.3), kind=kLoop, calls=%fused_computation.98 | loop fusion | bytes 1572864 | tf_op jit(solution)/shard_map/stack | solution.py:21
  48.6 0.8 convolution_bitcast_fusion
  49.7 1.3 %fusion.39 = bf16[512,384]{1,0:T(8,128)(2,1)S(1)} fusion(f32[512,384]{1,0:T(8,128)S(1)} %copy-done.5, f32[512,384]{1,0:T(8,128)S(1)} %convolution_bitcast_fusion, bf16[512,1,384]{2,0,1:T(8,128)(2,1)S(1)} %get-tuple-element.18, bf16[512,1,384]{2,0,1:T(8,128)(2,1)S(1)} %bitcast.144, bf16[512,1,384]{2,0,1:T(8,128)(2,1)S(1)} %get-tuple-element.9, ...), kind=kOutput, calls=%fused_computation.57 | convolution fusion | flops 458883072 | bytes 4423684 | tf_op jit(solution)/shard_map/tko,kio->ti/dot_general | solution.py:137
  51.0 1.3 %slice.185 = bf16[1152,384]{1,0:T(8,128)(2,1)S(1)} slice(bf16[2176,384]{1,0:T(8,128)(2,1)} %collective-permute-done.3), slice={[1024:2176], [0:384]} | slice | bytes 1769472 | tf_op jit(solution)/shard_map/slice | solution.py:121
  52.3 1.5 %collective-permute-done.13 = f32[2,96,384]{2,1,0:T(8,128)S(1)} collective-permute-done((f32[2,96,384]{2,1,0:T(8,128)S(1)}, f32[2,96,384]{2,1,0:T(8,128)S(1)}, u32[]{:S(2)}, u32[]{:S(2)}) %collective-permute-start.13) | collective-permute-done | bytes 294944 | tf_op jit(solution)/shard_map/ppermute | solution.py:58
  53.8 0.8 collective-permute-start.14
  54.6 21.0 %collective-permute-done.9 = f32[2,192,384]{2,1,0:T(8,128)S(1)} collective-permute-done((f32[2,192,384]{2,1,0:T(8,128)S(1)}, f32[2,192,384]{2,1,0:T(8,128)S(1)}, u32[]{:S(2)}, u32[]{:S(2)}) %collective-permute-start.9) | collective-permute-done | bytes 589856 | tf_op jit(solution)/shard_map/ppermute | solution.py:79
  75.8 1.4 %collective-permute-done.14 = f32[96,384]{1,0:T(8,128)S(1)} collective-permute-done((f32[96,384]{1,0:T(8,128)S(1)}, f32[96,384]{1,0:T(8,128)S(1)}, u32[]{:S(2)}, u32[]{:S(2)}) %collective-permute-start.14) | collective-permute-done | bytes 147488 | tf_op jit(solution)/shard_map/ppermute | solution.py:63
  77.2 1.7 %collective-permute-start.15 = (bf16[96,384]{1,0:T(8,128)(2,1)S(1)}, bf16[96,384]{1,0:T(8,128)(2,1)S(1)}, u32[]{:S(2)}, u32[]{:S(2)}) collective-permute-start(bf16[96,384]{1,0:T(8,128)(2,1)S(1)} %fusion.67), channel_id=1, source_target_pairs={{0,8},{8,0},{4,12},{12,4},{1,9},{9,1},{5,13},{13,5},{2,10},{10,2},... | collective-permute-start | bytes 221192 | tf_op jit(solution)/shard_map/ppermute | solution.py:64
  78.9 0.8 convolution_bitcast_fusion.3
  79.7 2.9 %collective-permute-done.15 = bf16[96,384]{1,0:T(8,128)(2,1)S(1)} collective-permute-done((bf16[96,384]{1,0:T(8,128)(2,1)S(1)}, bf16[96,384]{1,0:T(8,128)(2,1)S(1)}, u32[]{:S(2)}, u32[]{:S(2)}) %collective-permute-start.15) | collective-permute-done | bytes 73760 | tf_op jit(solution)/shard_map/ppermute | solution.py:64
  82.6 2.7 %collective-permute-start.16 = (bf16[2,96,384]{2,1,0:T(8,128)(2,1)S(1)}, bf16[2,96,384]{2,1,0:T(8,128)(2,1)S(1)}, u32[]{:S(2)}, u32[]{:S(2)}) collective-permute-start(bf16[2,96,384]{2,1,0:T(8,128)(2,1)S(1)} %maximum_select_fusion.1), channel_id=1, source_target_pairs={{0,4},{4,0},{8,12},{12,8},{1,5},{5,1},{9,13},{13,9},{2,6},{6,2},{1... | collective-permute-start | bytes 442376 | tf_op jit(solution)/shard_map/ppermute | solution.py:66
  85.3 1.7 %collective-permute-done.10 = f32[192,384]{1,0:T(8,128)S(1)} collective-permute-done((f32[192,384]{1,0:T(8,128)S(1)}, f32[192,384]{1,0:T(8,128)S(1)}, u32[]{:S(2)}, u32[]{:S(2)}) %collective-permute-start.10) | collective-permute-done | bytes 294944 | tf_op jit(solution)/shard_map/ppermute | solution.py:84
  87.2 1.6 %fusion.4 = bf16[1,512,384]{2,1,0:T(8,128)(2,1)} fusion(f32[512,384]{1,0:T(8,128)S(1)} %copy-done.5, f32[512,384]{1,0:T(8,128)S(1)} %convolution_bitcast_fusion.3, bf16[3,384,384]{2,1,0:T(8,128)(2,1)S(1)} %bitcast.158, bf16[512,1,384]{2,0,1:T(8,128)(2,1)S(1)} %get-tuple-element.14, bf16[512,1,384]{2,0,1:T(8,128)(2,1)S(1)} %get-tuple-element.4, ...), kind=kOutput, calls=%fused_computation.15 | convolution fusion | flops 454754304 | bytes 4030464 | tf_op jit(solution)/shard_map/tki,kio->to/dot_general | solution.py:131
  88.8 0.4 broadcast_in_dim.18
  89.2 1.2 %convert_element_type.54 = bf16[1,1024,384]{2,1,0:T(8,128)(2,1)} reshape(bf16[512,2,384]{2,1,0:T(2,128)(2,1)S(1)} %broadcast_in_dim.18) | data formatting | bytes 1572864 | tf_op jit(solution)/shard_map/convert_element_type | solution.py:146
  90.3 2.0 %collective-permute-done.11 = bf16[192,384]{1,0:T(8,128)(2,1)S(1)} collective-permute-done((bf16[192,384]{1,0:T(8,128)(2,1)S(1)}, bf16[192,384]{1,0:T(8,128)(2,1)S(1)}, u32[]{:S(2)}, u32[]{:S(2)}) %collective-permute-start.11) | collective-permute-done | bytes 147488 | tf_op jit(solution)/shard_map/ppermute | solution.py:85
  92.4 0.7 collective-permute-start.12
  93.2 12.3 %collective-permute-done.12 = bf16[2,192,384]{2,1,0:T(8,128)(2,1)S(1)} collective-permute-done((bf16[2,192,384]{2,1,0:T(8,128)(2,1)S(1)}, bf16[2,192,384]{2,1,0:T(8,128)(2,1)S(1)}, u32[]{:S(2)}, u32[]{:S(2)}) %collective-permute-start.12) | collective-permute-done | bytes 294944 | tf_op jit(solution)/shard_map/ppermute | solution.py:87
  105.8 1.3 %pad_maximum_fusion = f32[3,384,384]{2,1,0:T(8,128)} fusion(f32[1,384,384]{2,1,0:T(8,128)S(1)} %bitcast.155, f32[1,384,384]{2,1,0:T(8,128)S(1)} %bitcast.152, f32[1,384,384]{2,1,0:T(8,128)S(1)} %bitcast.154), kind=kLoop, calls=%fused_computation.2 | loop fusion | flops 884736 | bytes 3538944 | tf_op jit(solution)/shard_map/stack | solution.py:169
  (42 shorter events, 1.7 us)
Async XLA Ops:
  0.6 13.9 %copy-start = (bf16[3,384,768]{2,1,0:T(8,128)(2,1)S(1)}, bf16[3,384,768]{2,1,0:T(8,128)(2,1)}, u32[]{:S(2)}) copy-start(bf16[3,384,768]{2,1,0:T(8,128)(2,1)} %param.4) | copy-start | bytes 5308420
  0.6 26.0 %collective-permute-start.5 = (bf16[512,384]{1,0:T(8,128)(2,1)}, bf16[512,384]{1,0:T(8,128)(2,1)}, u32[]{:S(2)}, u32[]{:S(2)}) collective-permute-start(bf16[512,384]{1,0:T(8,128)(2,1)} %bitcast.142), channel_id=1, source_target_pairs={{2,0},{1,3},{6,4},{5,7},{10,8},{9,11},{14,12},{13,15},{18,16},{17,... | collective-permute-start | bytes 1179656 | tf_op jit(solution)/shard_map/ppermute | solution.py:109
  2.1 24.6 %collective-permute-start.6 = (bf16[512,384]{1,0:T(8,128)(2,1)}, bf16[512,384]{1,0:T(8,128)(2,1)}, u32[]{:S(2)}, u32[]{:S(2)}) collective-permute-start(bf16[512,384]{1,0:T(8,128)(2,1)} %bitcast.143), channel_id=1, source_target_pairs={{2,1},{1,2},{6,5},{5,6},{10,9},{9,10},{14,13},{13,14},{18,17},{17,... | collective-permute-start | bytes 1179656 | tf_op jit(solution)/shard_map/ppermute | solution.py:110
  3.5 2.8 %copy-start.1 = (bf16[1,512,384]{2,1,0:T(8,128)(2,1)S(1)}, bf16[1,512,384]{2,1,0:T(8,128)(2,1)}, u32[]{:S(2)}) copy-start(bf16[1,512,384]{2,1,0:T(8,128)(2,1)} %param.5) | copy-start | bytes 1179652
  7.3 13.8 %collective-permute-start = (bf16[2,256,384]{2,1,0:T(8,128)(2,1)}, bf16[2,256,384]{2,1,0:T(8,128)(2,1)S(1)}, u32[]{:S(2)}, u32[]{:S(2)}) collective-permute-start(bf16[2,256,384]{2,1,0:T(8,128)(2,1)} %get-tuple-element.23), channel_id=1, source_target_pairs={{0,4},{4,8},{8,12},{1,5},{5,9},{9,13},{2,6},{6,10},{10,14},{3,7},{... | collective-permute-start | bytes 1179656 | tf_op jit(solution)/shard_map/ppermute | solution.py:12
  12.3 11.3 %collective-permute-start.1 = (bf16[2,256,384]{2,1,0:T(8,128)(2,1)}, bf16[2,256,384]{2,1,0:T(8,128)(2,1)S(1)}, u32[]{:S(2)}, u32[]{:S(2)}) collective-permute-start(bf16[2,256,384]{2,1,0:T(8,128)(2,1)} %get-tuple-element.24), channel_id=1, source_target_pairs={{4,0},{8,4},{12,8},{5,1},{9,5},{13,9},{6,2},{10,6},{14,10},{7,3},{... | collective-permute-start | bytes 1179656 | tf_op jit(solution)/shard_map/ppermute | solution.py:12
  14.6 1.4 %copy-start.4 = (bf16[2,512,384]{2,1,0:T(8,128)(2,1)S(1)}, bf16[2,512,384]{2,1,0:T(8,128)(2,1)}, u32[]{:S(2)}) copy-start(bf16[2,512,384]{2,1,0:T(8,128)(2,1)} %pad_maximum_fusion.2) | copy-start | bytes 2359300
  14.7 2.7 %copy-start.2 = (bf16[3,384,384]{2,1,0:T(8,128)(2,1)}, bf16[3,384,384]{2,1,0:T(8,128)(2,1)S(1)}, u32[]{:S(2)}) copy-start(bf16[3,384,384]{2,1,0:T(8,128)(2,1)S(1)} %constant_dynamic-slice_fusion) | copy-start | bytes 2654212
  17.3 20.8 %collective-permute-start.3 = (bf16[2176,384]{1,0:T(8,128)(2,1)}, bf16[2176,384]{1,0:T(8,128)(2,1)}, u32[]{:S(2)}, u32[]{:S(2)}) collective-permute-start(bf16[2176,384]{1,0:T(8,128)(2,1)} %pad_maximum_fusion.1), channel_id=1, source_target_pairs={{0,1},{1,0},{2,3},{3,2},{4,5},{5,4},{6,7},{7,6},{8,9},{9,8},{10,11... | collective-permute-start | bytes 5013512 | tf_op jit(solution)/shard_map/ppermute | solution.py:117
  21.1 12.6 %collective-permute-start.4 = (bf16[512,384]{1,0:T(8,128)(2,1)S(1)}, bf16[512,384]{1,0:T(8,128)(2,1)S(1)}, u32[]{:S(2)}, u32[]{:S(2)}) collective-permute-start(bf16[512,384]{1,0:T(8,128)(2,1)S(1)} %get-tuple-element.32), channel_id=1, source_target_pairs={{0,2},{2,0},{1,3},{3,1},{4,6},{6,4},{5,7},{7,5},{8,10},{10,8},{9,1... | collective-permute-start | bytes 1179656 | tf_op jit(solution)/shard_map/ppermute | solution.py:112
  23.7 14.4 %collective-permute-start.2 = (bf16[2,2,256,384]{3,2,1,0:T(8,128)(2,1)S(1)}, bf16[2,2,256,384]{3,2,1,0:T(8,128)(2,1)S(1)}, u32[]{:S(2)}, u32[]{:S(2)}) collective-permute-start(bf16[2,2,256,384]{3,2,1,0:T(8,128)(2,1)S(1)} %pad_maximum_fusion.3), channel_id=1, source_target_pairs={{0,1},{1,0},{2,3},{3,2},{4,5},{5,4},{6,7},{7,6},{8,9},{9,8},{10,11... | collective-permute-start | bytes 2359304 | tf_op jit(solution)/shard_map/ppermute | solution.py:124
  27.8 8.7 %collective-permute-start.7 = (bf16[256,384]{1,0:T(8,128)(2,1)S(1)}, bf16[256,384]{1,0:T(8,128)(2,1)S(1)}, u32[]{:S(2)}, u32[]{:S(2)}) collective-permute-start(bf16[256,384]{1,0:T(8,128)(2,1)S(1)} %get-tuple-element.29), channel_id=1, source_target_pairs={{4,0},{8,4},{12,8},{5,1},{9,5},{13,9},{6,2},{10,6},{14,10},{7,3},{... | collective-permute-start | bytes 589832 | tf_op jit(solution)/shard_map/ppermute | solution.py:12
  29.1 8.6 %collective-permute-start.8 = (bf16[256,384]{1,0:T(8,128)(2,1)S(1)}, bf16[256,384]{1,0:T(8,128)(2,1)S(1)}, u32[]{:S(2)}, u32[]{:S(2)}) collective-permute-start(bf16[256,384]{1,0:T(8,128)(2,1)S(1)} %get-tuple-element.28), channel_id=1, source_target_pairs={{0,4},{4,8},{8,12},{1,5},{5,9},{9,13},{2,6},{6,10},{10,14},{3,7},{... | collective-permute-start | bytes 589832 | tf_op jit(solution)/shard_map/ppermute | solution.py:12
  39.9 13.9 %collective-permute-start.13 = (f32[2,96,384]{2,1,0:T(8,128)S(1)}, f32[2,96,384]{2,1,0:T(8,128)S(1)}, u32[]{:S(2)}, u32[]{:S(2)}) collective-permute-start(f32[2,96,384]{2,1,0:T(8,128)S(1)} %select_bitcast_fusion), channel_id=1, source_target_pairs={{0,4},{4,0},{8,12},{12,8},{1,5},{5,1},{9,13},{13,9},{2,6},{6,2},{1... | collective-permute-start | bytes 884744 | tf_op jit(solution)/shard_map/ppermute | solution.py:58
  43.3 32.3 %collective-permute-start.9 = (f32[2,192,384]{2,1,0:T(8,128)S(1)}, f32[2,192,384]{2,1,0:T(8,128)S(1)}, u32[]{:S(2)}, u32[]{:S(2)}) collective-permute-start(f32[2,192,384]{2,1,0:T(8,128)S(1)} %bitcast.161), channel_id=1, source_target_pairs={{0,8},{8,0},{4,12},{12,4},{1,9},{9,1},{5,13},{13,5},{2,10},{10,2},... | collective-permute-start | bytes 1769480 | tf_op jit(solution)/shard_map/ppermute | solution.py:79
  47.1 1.5 %copy-start.3 = (bf16[3,384,384]{2,1,0:T(8,128)(2,1)S(1)}, bf16[3,384,384]{2,1,0:T(8,128)(2,1)}, u32[]{:S(2)}) copy-start(bf16[3,384,384]{2,1,0:T(8,128)(2,1)} %copy-done.2) | copy-start | bytes 2654212
  48.6 1.1 %copy-start.5 = (f32[512,384]{1,0:T(8,128)S(1)}, f32[512,384]{1,0:T(8,128)}, u32[]{:S(2)}) copy-start(f32[512,384]{1,0:T(8,128)} %get-tuple-element.33) | copy-start | bytes 2359300
  53.8 23.3 %collective-permute-start.14 = (f32[96,384]{1,0:T(8,128)S(1)}, f32[96,384]{1,0:T(8,128)S(1)}, u32[]{:S(2)}, u32[]{:S(2)}) collective-permute-start(f32[96,384]{1,0:T(8,128)S(1)} %select_bitcast_fusion.6), channel_id=1, source_target_pairs={{0,8},{8,0},{4,12},{12,4},{1,9},{9,1},{5,13},{13,5},{2,10},{10,2},... | collective-permute-start | bytes 442376 | tf_op jit(solution)/shard_map/ppermute | solution.py:63
  75.7 11.3 %collective-permute-start.10 = (f32[192,384]{1,0:T(8,128)S(1)}, f32[192,384]{1,0:T(8,128)S(1)}, u32[]{:S(2)}, u32[]{:S(2)}) collective-permute-start(f32[192,384]{1,0:T(8,128)S(1)} %select_bitcast_fusion.3), channel_id=1, source_target_pairs={{0,4},{4,0},{8,12},{12,8},{1,5},{5,1},{9,13},{13,9},{2,6},{6,2},{1... | collective-permute-start | bytes 884744 | tf_op jit(solution)/shard_map/ppermute | solution.py:84
  77.2 5.4 %collective-permute-start.15 = (bf16[96,384]{1,0:T(8,128)(2,1)S(1)}, bf16[96,384]{1,0:T(8,128)(2,1)S(1)}, u32[]{:S(2)}, u32[]{:S(2)}) collective-permute-start(bf16[96,384]{1,0:T(8,128)(2,1)S(1)} %fusion.67), channel_id=1, source_target_pairs={{0,8},{8,0},{4,12},{12,4},{1,9},{9,1},{5,13},{13,5},{2,10},{10,2},... | collective-permute-start | bytes 221192 | tf_op jit(solution)/shard_map/ppermute | solution.py:64
  82.6 10.4 %collective-permute-start.16 = (bf16[2,96,384]{2,1,0:T(8,128)(2,1)S(1)}, bf16[2,96,384]{2,1,0:T(8,128)(2,1)S(1)}, u32[]{:S(2)}, u32[]{:S(2)}) collective-permute-start(bf16[2,96,384]{2,1,0:T(8,128)(2,1)S(1)} %maximum_select_fusion.1), channel_id=1, source_target_pairs={{0,4},{4,0},{8,12},{12,8},{1,5},{5,1},{9,13},{13,9},{2,6},{6,2},{1... | collective-permute-start | bytes 442376 | tf_op jit(solution)/shard_map/ppermute | solution.py:66
  87.1 5.2 %collective-permute-start.11 = (bf16[192,384]{1,0:T(8,128)(2,1)S(1)}, bf16[192,384]{1,0:T(8,128)(2,1)S(1)}, u32[]{:S(2)}, u32[]{:S(2)}) collective-permute-start(bf16[192,384]{1,0:T(8,128)(2,1)S(1)} %fusion.66), channel_id=1, source_target_pairs={{0,4},{4,0},{8,12},{12,8},{1,5},{5,1},{9,13},{13,9},{2,6},{6,2},{1... | collective-permute-start | bytes 442376 | tf_op jit(solution)/shard_map/ppermute | solution.py:85
  92.4 13.1 %collective-permute-start.12 = (bf16[2,192,384]{2,1,0:T(8,128)(2,1)S(1)}, bf16[2,192,384]{2,1,0:T(8,128)(2,1)S(1)}, u32[]{:S(2)}, u32[]{:S(2)}) collective-permute-start(bf16[2,192,384]{2,1,0:T(8,128)(2,1)S(1)} %maximum_select_fusion), channel_id=1, source_target_pairs={{0,8},{8,0},{4,12},{12,4},{1,9},{9,1},{5,13},{13,5},{2,10},{10,2},... | collective-permute-start | bytes 884744 | tf_op jit(solution)/shard_map/ppermute | solution.py:87

commit v25 on v16

--- a/solution.py
+++ b/solution.py
@@ -143,7 +143,10 @@
                 own_taps[:, k].T, cot_mine, preferred_element_type=jnp.float32
             ) + jnp.dot(far_mid.T, far_shifted[k], preferred_element_type=jnp.float32)
         if seq_count == 4:
-            weight_grad = jnp.stack([line_total(grads[k]) for k in range(3)])
+            first = line_total(jnp.concatenate([grads[1], grads[0]], 0))
+            last = line_total(grads[2])
+            size = last.shape[0]
+            weight_grad = jnp.stack([first[size:], first[:size], last])
         else:
             weight_grad = lax.psum(jnp.stack([grads[0], grads[1], grads[2]]), "seq")
     else:

time: 105 us -> 108 us (1.029)
  waiting for transfers between devices: 29.1 us -> 46.3 us
  starting transfers between devices: 38.2 us -> 32.5 us
  other arithmetic: 14.9 us -> 9.43 us
  local copies, waits for them, and re-layouts: 11 us -> 6.93 us
  matrix products: 9.66 us -> 11.5 us
    ppermute x3 -> x2, waiting for transfers between devices: 0.01 us -> 10.9 us  [line_total(): lax.ppermute(jnp.where(odd, even_set, odd_set), 'seq', pairs)]
    ppermute x3 -> x2, waiting for transfers between devices: 3.03 us -> 11.3 us  [line_total(): other = lax.ppermute(total, 'seq', across)]
    ppermute x3 -> x2, starting transfers between devices: 4.84 us -> 0.35 us  [line_total(): far_set = lax.ppermute(own_set, 'seq', pairs)]
    ppermute x3 -> x2, waiting for transfers between devices: 15.9 us -> 12.4 us  [line_total(): total = (keep + lax.ppermute(give, 'seq', across)).astype(jnp.bfloat16)]
    ppermute x3 -> x2, starting transfers between devices: 0.21 us -> 3.34 us  [line_total(): other = lax.ppermute(total, 'seq', across)]
    add x3 -> x2, other arithmetic: 3.07 us -> 0.16 us  [line_total(): jnp.where(odd, odd_set, even_set)]
    ppermute x3 -> x2, starting transfers between devices: 5.71 us -> 3.06 us  [line_total(): total = (keep + lax.ppermute(give, 'seq', across)).astype(jnp.bfloat16)]
    select_n x3 -> x2, other arithmetic: 2.42 us -> 0.09 us  [line_total(): jnp.where(odd, even_set, odd_set)]
  transfers between devices with their start and end apart: 21 -> 17, of which waited for: 11 -> 8; matrix products, arithmetic and copies ran while one was open for 28% -> 20% of each run, Pallas kernels for 0% -> 0%
where the time goes in v25:
time: 108 us
  waiting for transfers between devices  46.3 us (43%)
  starting transfers between devices  32.5 us (30%)
  matrix products  11.5 us (11%)
  other arithmetic  9.43 us (9%)
  local copies, waits for them, and re-layouts  6.93 us (6%)
    ppermute x4, starting transfers between devices, shift_from(): return lax.ppermute(block, axis, route)  12.8 us
    ppermute x2, waiting for transfers between devices, line_total(): total = (keep + lax.ppermute(give, 'seq', across)).astype(jnp.bfloat16)  12.4 us
    ppermute x2, waiting for transfers between devices, line_total(): other = lax.ppermute(total, 'seq', across)  11.3 us
    ppermute x2, waiting for transfers between devices, line_total(): lax.ppermute(jnp.where(odd, even_set, odd_set), 'seq', pairs)  10.9 us
    ppermute x2, waiting for transfers between devices, line_total(): far_set = lax.ppermute(own_set, 'seq', pairs)  6.41 us
    ppermute x4, waiting for transfers between devices, shift_from(): return lax.ppermute(block, axis, route)  5.3 us
    ppermute x1, starting transfers between devices, shards(): lax.ppermute(jnp.concatenate([both.reshape(-1, width), w_other.reshape(-1...  3.71 us
    ppermute x2, starting transfers between devices, line_total(): other = lax.ppermute(total, 'seq', across)  3.34 us
  transfers between devices with their start and end apart: 17, of which 8 were waited for; matrix products, arithmetic and copies ran while one was open for 20% of the time, Pallas kernels for 0%

profile of v25, /device:TPU:0, one launch (start us, length us, event | category | flops | bytes accessed | tf_op | source)
XLA Modules:
  0.0 107.7 jit_solution(6366477396839912788)
XLA Ops:
  0.6 1.4 %collective-permute-start.5 = (bf16[512,384]{1,0:T(8,128)(2,1)}, bf16[512,384]{1,0:T(8,128)(2,1)}, u32[]{:S(2)}, u32[]{:S(2)}) collective-permute-start(bf16[512,384]{1,0:T(8,128)(2,1)} %bitcast.157), channel_id=1, source_target_pairs={{2,0},{1,3},{6,4},{5,7},{10,8},{9,11},{14,12},{13,15},{18,16},{17,... | collective-permute-start | bytes 1179656 | tf_op jit(solution)/shard_map/ppermute | solution.py:88
  2.1 1.4 %collective-permute-start.6 = (bf16[512,384]{1,0:T(8,128)(2,1)}, bf16[512,384]{1,0:T(8,128)(2,1)}, u32[]{:S(2)}, u32[]{:S(2)}) collective-permute-start(bf16[512,384]{1,0:T(8,128)(2,1)} %bitcast.158), channel_id=1, source_target_pairs={{2,1},{1,2},{6,5},{5,6},{10,9},{9,10},{14,13},{13,14},{18,17},{17,... | collective-permute-start | bytes 1179656 | tf_op jit(solution)/shard_map/ppermute | solution.py:89
  3.5 2.8 %multiply_convert_fusion = (bf16[512,384]{1,0:T(8,128)(2,1)S(1)}, f32[512,384]{1,0:T(8,128)}) fusion(bf16[1,1024,384]{2,1,0:T(8,128)(2,1)} %param.3, s32[1024]{0:T(1024)S(1)} %get-tuple-element.32, s32[1024]{0:T(1024)S(1)} %get-tuple-element.33, pred[1024]{0:T(1024)(128)(4,1)S(1)} %fusion.72), kind=kOutput, calls=%fused_computation.61 | convolution fusion | flops 406519808 | bytes 1975296 | tf_op jit(solution)/shard_map/dot_general | solution.py:83
  6.3 1.0 fusion.47
  7.3 5.7 %collective-permute-start = (bf16[2,256,384]{2,1,0:T(8,128)(2,1)}, bf16[2,256,384]{2,1,0:T(8,128)(2,1)}, u32[]{:S(2)}, u32[]{:S(2)}) collective-permute-start(bf16[2,256,384]{2,1,0:T(8,128)(2,1)} %get-tuple-element.21), channel_id=1, source_target_pairs={{0,4},{4,8},{8,12},{1,5},{5,9},{9,13},{2,6},{6,10},{10,14},{3,7},{... | collective-permute-start | bytes 1179656 | tf_op jit(solution)/shard_map/ppermute | solution.py:12
  13.0 1.3 %collective-permute-start.1 = (bf16[2,256,384]{2,1,0:T(8,128)(2,1)}, bf16[2,256,384]{2,1,0:T(8,128)(2,1)}, u32[]{:S(2)}, u32[]{:S(2)}) collective-permute-start(bf16[2,256,384]{2,1,0:T(8,128)(2,1)} %get-tuple-element.22), channel_id=1, source_target_pairs={{4,0},{8,4},{12,8},{5,1},{9,5},{13,9},{6,2},{10,6},{14,10},{7,3},{... | collective-permute-start | bytes 1179656 | tf_op jit(solution)/shard_map/ppermute | solution.py:12
  14.3 1.0 pad_maximum_fusion.3
  15.4 1.0 copy-done.2
  16.4 1.3 %pad_maximum_fusion.1 = bf16[2176,384]{1,0:T(8,128)(2,1)} fusion(bf16[1152,384]{1,0:T(8,128)(2,1)S(1)} %bitcast.162, bf16[1024,384]{1,0:T(8,128)(2,1)S(1)} %bitcast.163), kind=kLoop, calls=%fused_computation.3 | loop fusion | flops 3342336 | bytes 3342336 | tf_op jit(solution)/shard_map/concatenate | solution.py:97
  17.8 3.7 %collective-permute-start.3 = (bf16[2176,384]{1,0:T(8,128)(2,1)}, bf16[2176,384]{1,0:T(8,128)(2,1)}, u32[]{:S(2)}, u32[]{:S(2)}) collective-permute-start(bf16[2176,384]{1,0:T(8,128)(2,1)} %pad_maximum_fusion.1), channel_id=1, source_target_pairs={{0,1},{1,0},{2,3},{3,2},{4,5},{5,4},{6,7},{7,6},{8,9},{9,8},{10,11... | collective-permute-start | bytes 5013512 | tf_op jit(solution)/shard_map/ppermute | solution.py:96
  21.5 0.9 collective-permute-start.4
  22.4 2.0 %collective-permute-done.1 = bf16[2,256,384]{2,1,0:T(8,128)(2,1)} collective-permute-done((bf16[2,256,384]{2,1,0:T(8,128)(2,1)}, bf16[2,256,384]{2,1,0:T(8,128)(2,1)}, u32[]{:S(2)}, u32[]{:S(2)}) %collective-permute-start.1) | collective-permute-done | bytes 393248 | tf_op jit(solution)/shard_map/ppermute | solution.py:12
  24.5 1.2 %pad_maximum_fusion.4 = bf16[2,2,256,384]{3,2,1,0:T(8,128)(2,1)S(1)} fusion(bf16[1,2,256,384]{3,2,1,0:T(8,128)(2,1)} %bitcast.7, bf16[1,2,256,384]{3,2,1,0:T(8,128)(2,1)} %bitcast.6), kind=kLoop, calls=%fused_computation.59 | loop fusion | flops 393216 | bytes 1572864 | tf_op jit(solution)/shard_map/stack | solution.py:103
  25.7 2.8 %collective-permute-start.2 = (bf16[2,2,256,384]{3,2,1,0:T(8,128)(2,1)S(1)}, bf16[2,2,256,384]{3,2,1,0:T(8,128)(2,1)S(1)}, u32[]{:S(2)}, u32[]{:S(2)}) collective-permute-start(bf16[2,2,256,384]{3,2,1,0:T(8,128)(2,1)S(1)} %pad_maximum_fusion.4), channel_id=1, source_target_pairs={{0,1},{1,0},{2,3},{3,2},{4,5},{5,4},{6,7},{7,6},{8,9},{9,8},{10,11... | collective-permute-start | bytes 2359304 | tf_op jit(solution)/shard_map/ppermute | solution.py:103
  28.5 1.0 broadcast_select_fusion
  29.6 1.3 %collective-permute-start.7 = (bf16[256,384]{1,0:T(8,128)(2,1)S(1)}, bf16[256,384]{1,0:T(8,128)(2,1)S(1)}, u32[]{:S(2)}, u32[]{:S(2)}) collective-permute-start(bf16[256,384]{1,0:T(8,128)(2,1)S(1)} %get-tuple-element.27), channel_id=1, source_target_pairs={{4,0},{8,4},{12,8},{5,1},{9,5},{13,9},{6,2},{10,6},{14,10},{7,3},{... | collective-permute-start | bytes 589832 | tf_op jit(solution)/shard_map/ppermute | solution.py:12
  30.9 4.6 %collective-permute-start.12 = (bf16[256,384]{1,0:T(8,128)(2,1)S(1)}, bf16[256,384]{1,0:T(8,128)(2,1)S(1)}, u32[]{:S(2)}, u32[]{:S(2)}) collective-permute-start(bf16[256,384]{1,0:T(8,128)(2,1)S(1)} %get-tuple-element.26), channel_id=1, source_target_pairs={{0,4},{4,8},{8,12},{1,5},{5,9},{9,13},{2,6},{6,10},{10,14},{3,7},{... | collective-permute-start | bytes 589832 | tf_op jit(solution)/shard_map/ppermute | solution.py:12
  35.5 0.4 fusion.87
  35.9 2.5 %collective-permute-done.7 = bf16[256,384]{1,0:T(8,128)(2,1)S(1)} collective-permute-done((bf16[256,384]{1,0:T(8,128)(2,1)S(1)}, bf16[256,384]{1,0:T(8,128)(2,1)S(1)}, u32[]{:S(2)}, u32[]{:S(2)}) %collective-permute-start.7) | collective-permute-done | bytes 196640 | tf_op jit(solution)/shard_map/ppermute | solution.py:12
  38.3 0.4 fusion.53
  38.7 0.8 collective-permute-done.12
  39.5 0.4 fusion.57
  40.0 1.6 %fusion.52 = (bf16[512,1,384]{2,0,1:T(8,128)(2,1)S(1)}, bf16[512,1,384]{2,0,1:T(8,128)(2,1)S(1)}, bf16[512,1,384]{2,0,1:T(8,128)(2,1)S(1)}, bf16[512,1,384]{2,0,1:T(8,128)(2,1)S(1)}, bf16[1,512,384]{2,1,0:T(8,128)(2,1)S(1)}) fusion(bf16[2,256,384]{2,1,0:T(8,128)(2,1)} %collective-permute-done.1, bf16[1,512,384]{2,1,0:T(8,128)(2,1)S(1)} %copy-done.1, ...), kind=kLoop, calls=%fused_computation.79 | loop fusion | flops 4915200 | bytes 3932161 | tf_op jit(solution)/shard_map/stack | solution.py:21
  41.6 0.4 convolution_add_fusion.2
  42.0 1.3 %convolution_add_fusion.1 = f32[384,384]{1,0:T(8,128)S(1)} fusion(f32[384,384]{1,0:T(8,128)S(1)} %fusion.53, bf16[1,512,384]{2,1,0:T(8,128)(2,1)S(1)} %get-tuple-element.25, bf16[2,256,384]{2,1,0:T(8,128)(2,1)} %collective-permute-done, bf16[1,512,384]{2,1,0:T(8,128)(2,1)S(1)} %copy-done.1, bf16[1,512,384]{2,1,0:T(8,128)(2,1)S(1)} %bitcast.152), kind=kOutput, calls=%fused_computation.13 | convolution fusion | flops 152322048 | bytes 2752512 | tf_op jit(solution)/shard_map/dot_general | solution.py:142
  43.5 2.6 %collective-permute-start.8 = (f32[2,192,384]{2,1,0:T(8,128)S(1)}, f32[2,192,384]{2,1,0:T(8,128)S(1)}, u32[]{:S(2)}, u32[]{:S(2)}) collective-permute-start(f32[2,192,384]{2,1,0:T(8,128)S(1)} %select_bitcast_fusion), channel_id=1, source_target_pairs={{0,4},{4,0},{8,12},{12,8},{1,5},{5,1},{9,13},{13,9},{2,6},{6,2},{1... | collective-permute-start | bytes 1769480 | tf_op jit(solution)/shard_map/ppermute | solution.py:58
  46.0 1.3 %convolution_add_fusion = f32[384,384]{1,0:T(8,128)S(1)} fusion(f32[384,384]{1,0:T(8,128)S(1)} %fusion.57, bf16[1,512,384]{2,1,0:T(8,128)(2,1)S(1)} %get-tuple-element.25, bf16[2,256,384]{2,1,0:T(8,128)(2,1)} %collective-permute-done.1, bf16[1,512,384]{2,1,0:T(8,128)(2,1)S(1)} %copy-done.1, bf16[1,512,384]{2,1,0:T(8,128)(2,1)S(1)} %bitcast.153), kind=kOutput, calls=%fused_computation.12 | convolution fusion | flops 152322048 | bytes 2752512 | tf_op jit(solution)/shard_map/dot_general | solution.py:142
  47.5 1.2 %slice.184 = bf16[1024,384]{1,0:T(8,128)(2,1)S(1)} slice(bf16[2176,384]{1,0:T(8,128)(2,1)} %collective-permute-done.3), slice={[0:1024], [0:384]} | slice | bytes 1572864 | tf_op jit(solution)/shard_map/slice | solution.py:99
  48.7 0.2 fusion.50
  48.9 1.2 %slice_bitcast_fusion.3 = (bf16[512,1,384]{2,0,1:T(8,128)(2,1)S(1)}, bf16[512,1,384]{2,0,1:T(8,128)(2,1)S(1)}) fusion(bf16[2176,384]{1,0:T(8,128)(2,1)} %collective-permute-done.3), kind=kLoop, calls=%fused_computation.103 | loop fusion | bytes 1572864 | tf_op jit(solution)/shard_map/stack | solution.py:21
  50.1 0.8 convolution_bitcast_fusion
  51.0 0.3 copy-done.3
  51.3 1.3 %fusion.39 = bf16[512,384]{1,0:T(8,128)(2,1)S(1)} fusion(f32[512,384]{1,0:T(8,128)S(1)} %copy-done.3, f32[512,384]{1,0:T(8,128)S(1)} %convolution_bitcast_fusion, bf16[512,1,384]{2,0,1:T(8,128)(2,1)S(1)} %get-tuple-element.16, bf16[512,1,384]{2,0,1:T(8,128)(2,1)S(1)} %bitcast.159, bf16[512,1,384]{2,0,1:T(8,128)(2,1)S(1)} %get-tuple-element.7, ...), kind=kOutput, calls=%fused_computation.58 | convolution fusion | flops 458883072 | bytes 4423684 | tf_op jit(solution)/shard_map/tko,kio->ti/dot_general | solution.py:116
  52.6 1.3 %slice.187 = bf16[1152,384]{1,0:T(8,128)(2,1)S(1)} slice(bf16[2176,384]{1,0:T(8,128)(2,1)} %collective-permute-done.3), slice={[1024:2176], [0:384]} | slice | bytes 1769472 | tf_op jit(solution)/shard_map/slice | solution.py:100
  53.8 10.9 %collective-permute-done.13 = f32[2,96,384]{2,1,0:T(8,128)S(1)} collective-permute-done((f32[2,96,384]{2,1,0:T(8,128)S(1)}, f32[2,96,384]{2,1,0:T(8,128)S(1)}, u32[]{:S(2)}, u32[]{:S(2)}) %collective-permute-start.13) | collective-permute-done | bytes 294944 | tf_op jit(solution)/shard_map/ppermute | solution.py:58
  64.8 2.1 %collective-permute-start.14 = (f32[96,384]{1,0:T(8,128)S(1)}, f32[96,384]{1,0:T(8,128)S(1)}, u32[]{:S(2)}, u32[]{:S(2)}) collective-permute-start(f32[96,384]{1,0:T(8,128)S(1)} %select_bitcast_fusion.7), channel_id=1, source_target_pairs={{0,8},{8,0},{4,12},{12,4},{1,9},{9,1},{5,13},{13,5},{2,10},{10,2},... | collective-permute-start | bytes 442376 | tf_op jit(solution)/shard_map/ppermute | solution.py:63
  67.1 1.0 collective-permute-start.9
  68.0 12.4 %collective-permute-done.14 = f32[96,384]{1,0:T(8,128)S(1)} collective-permute-done((f32[96,384]{1,0:T(8,128)S(1)}, f32[96,384]{1,0:T(8,128)S(1)}, u32[]{:S(2)}, u32[]{:S(2)}) %collective-permute-start.14) | collective-permute-done | bytes 147488 | tf_op jit(solution)/shard_map/ppermute | solution.py:63
  80.5 0.8 convolution_bitcast_fusion.3
  81.3 7.5 %collective-permute-done.15 = bf16[96,384]{1,0:T(8,128)(2,1)S(1)} collective-permute-done((bf16[96,384]{1,0:T(8,128)(2,1)S(1)}, bf16[96,384]{1,0:T(8,128)(2,1)S(1)}, u32[]{:S(2)}, u32[]{:S(2)}) %collective-permute-start.15) | collective-permute-done | bytes 73760 | tf_op jit(solution)/shard_map/ppermute | solution.py:64
  89.0 3.3 %collective-permute-start.10 = (bf16[192,384]{1,0:T(8,128)(2,1)S(1)}, bf16[192,384]{1,0:T(8,128)(2,1)S(1)}, u32[]{:S(2)}, u32[]{:S(2)}) collective-permute-start(bf16[192,384]{1,0:T(8,128)(2,1)S(1)} %fusion.68), channel_id=1, source_target_pairs={{0,8},{8,0},{4,12},{12,4},{1,9},{9,1},{5,13},{13,5},{2,10},{10,2},... | collective-permute-start | bytes 442376 | tf_op jit(solution)/shard_map/ppermute | solution.py:64
  92.2 1.6 %fusion.4 = bf16[1,512,384]{2,1,0:T(8,128)(2,1)} fusion(f32[512,384]{1,0:T(8,128)S(1)} %copy-done.3, f32[512,384]{1,0:T(8,128)S(1)} %convolution_bitcast_fusion.3, bf16[3,384,384]{2,1,0:T(8,128)(2,1)S(1)} %bitcast.170, bf16[512,1,384]{2,0,1:T(8,128)(2,1)S(1)} %get-tuple-element.12, bf16[512,1,384]{2,0,1:T(8,128)(2,1)S(1)} %get-tuple-element.4, ...), kind=kOutput, calls=%fused_computation.15 | convolution fusion | flops 454754304 | bytes 4030464 | tf_op jit(solution)/shard_map/tki,kio->to/dot_general | solution.py:110
  93.8 0.4 broadcast_in_dim.18
  94.3 1.2 %convert_element_type.54 = bf16[1,1024,384]{2,1,0:T(8,128)(2,1)} reshape(bf16[512,2,384]{2,1,0:T(2,128)(2,1)S(1)} %broadcast_in_dim.18) | data formatting | bytes 1572864 | tf_op jit(solution)/shard_map/convert_element_type | solution.py:125
  95.4 3.8 %collective-permute-done.10 = bf16[192,384]{1,0:T(8,128)(2,1)S(1)} collective-permute-done((bf16[192,384]{1,0:T(8,128)(2,1)S(1)}, bf16[192,384]{1,0:T(8,128)(2,1)S(1)}, u32[]{:S(2)}, u32[]{:S(2)}) %collective-permute-start.10) | collective-permute-done | bytes 147488 | tf_op jit(solution)/shard_map/ppermute | solution.py:64
  99.3 0.3 collective-permute-start.11
  99.7 6.4 %collective-permute-done.11 = bf16[2,192,384]{2,1,0:T(8,128)(2,1)S(1)} collective-permute-done((bf16[2,192,384]{2,1,0:T(8,128)(2,1)S(1)}, bf16[2,192,384]{2,1,0:T(8,128)(2,1)S(1)}, u32[]{:S(2)}, u32[]{:S(2)}) %collective-permute-start.11) | collective-permute-done | bytes 294944 | tf_op jit(solution)/shard_map/ppermute | solution.py:66
  106.4 1.3 %pad_maximum_fusion = f32[3,384,384]{2,1,0:T(8,128)} fusion(f32[1,384,384]{2,1,0:T(8,128)S(1)} %bitcast.165, f32[1,384,384]{2,1,0:T(8,128)S(1)} %bitcast.167, f32[1,384,384]{2,1,0:T(8,128)S(1)} %bitcast.166), kind=kLoop, calls=%fused_computation.2 | loop fusion | flops 884736 | bytes 3538944 | tf_op jit(solution)/shard_map/stack | solution.py:149
  (40 shorter events, 1.4 us)
Async XLA Ops:
  0.6 14.7 %copy-start = (bf16[3,384,768]{2,1,0:T(8,128)(2,1)S(1)}, bf16[3,384,768]{2,1,0:T(8,128)(2,1)}, u32[]{:S(2)}) copy-start(bf16[3,384,768]{2,1,0:T(8,128)(2,1)} %param.4) | copy-start | bytes 5308420
  0.6 27.9 %collective-permute-start.5 = (bf16[512,384]{1,0:T(8,128)(2,1)}, bf16[512,384]{1,0:T(8,128)(2,1)}, u32[]{:S(2)}, u32[]{:S(2)}) collective-permute-start(bf16[512,384]{1,0:T(8,128)(2,1)} %bitcast.157), channel_id=1, source_target_pairs={{2,0},{1,3},{6,4},{5,7},{10,8},{9,11},{14,12},{13,15},{18,16},{17,... | collective-permute-start | bytes 1179656 | tf_op jit(solution)/shard_map/ppermute | solution.py:88
  2.1 26.4 %collective-permute-start.6 = (bf16[512,384]{1,0:T(8,128)(2,1)}, bf16[512,384]{1,0:T(8,128)(2,1)}, u32[]{:S(2)}, u32[]{:S(2)}) collective-permute-start(bf16[512,384]{1,0:T(8,128)(2,1)} %bitcast.158), channel_id=1, source_target_pairs={{2,1},{1,2},{6,5},{5,6},{10,9},{9,10},{14,13},{13,14},{18,17},{17,... | collective-permute-start | bytes 1179656 | tf_op jit(solution)/shard_map/ppermute | solution.py:89
  3.5 2.8 %copy-start.1 = (bf16[1,512,384]{2,1,0:T(8,128)(2,1)S(1)}, bf16[1,512,384]{2,1,0:T(8,128)(2,1)}, u32[]{:S(2)}) copy-start(bf16[1,512,384]{2,1,0:T(8,128)(2,1)} %param.5) | copy-start | bytes 1179652
  7.3 14.2 %collective-permute-start = (bf16[2,256,384]{2,1,0:T(8,128)(2,1)}, bf16[2,256,384]{2,1,0:T(8,128)(2,1)}, u32[]{:S(2)}, u32[]{:S(2)}) collective-permute-start(bf16[2,256,384]{2,1,0:T(8,128)(2,1)} %get-tuple-element.21), channel_id=1, source_target_pairs={{0,4},{4,8},{8,12},{1,5},{5,9},{9,13},{2,6},{6,10},{10,14},{3,7},{... | collective-permute-start | bytes 1179656 | tf_op jit(solution)/shard_map/ppermute | solution.py:12
  13.0 11.4 %collective-permute-start.1 = (bf16[2,256,384]{2,1,0:T(8,128)(2,1)}, bf16[2,256,384]{2,1,0:T(8,128)(2,1)}, u32[]{:S(2)}, u32[]{:S(2)}) collective-permute-start(bf16[2,256,384]{2,1,0:T(8,128)(2,1)} %get-tuple-element.22), channel_id=1, source_target_pairs={{4,0},{8,4},{12,8},{5,1},{9,5},{13,9},{6,2},{10,6},{14,10},{7,3},{... | collective-permute-start | bytes 1179656 | tf_op jit(solution)/shard_map/ppermute | solution.py:12
  15.3 1.1 %copy-start.2 = (bf16[2,512,384]{2,1,0:T(8,128)(2,1)S(1)}, bf16[2,512,384]{2,1,0:T(8,128)(2,1)}, u32[]{:S(2)}) copy-start(bf16[2,512,384]{2,1,0:T(8,128)(2,1)} %pad_maximum_fusion.3) | copy-start | bytes 2359300
  17.8 22.3 %collective-permute-start.3 = (bf16[2176,384]{1,0:T(8,128)(2,1)}, bf16[2176,384]{1,0:T(8,128)(2,1)}, u32[]{:S(2)}, u32[]{:S(2)}) collective-permute-start(bf16[2176,384]{1,0:T(8,128)(2,1)} %pad_maximum_fusion.1), channel_id=1, source_target_pairs={{0,1},{1,0},{2,3},{3,2},{4,5},{5,4},{6,7},{7,6},{8,9},{9,8},{10,11... | collective-permute-start | bytes 5013512 | tf_op jit(solution)/shard_map/ppermute | solution.py:96
  21.5 14.0 %collective-permute-start.4 = (bf16[512,384]{1,0:T(8,128)(2,1)S(1)}, bf16[512,384]{1,0:T(8,128)(2,1)S(1)}, u32[]{:S(2)}, u32[]{:S(2)}) collective-permute-start(bf16[512,384]{1,0:T(8,128)(2,1)S(1)} %get-tuple-element.30), channel_id=1, source_target_pairs={{0,2},{2,0},{1,3},{3,1},{4,6},{6,4},{5,7},{7,5},{8,10},{10,8},{9,1... | collective-permute-start | bytes 1179656 | tf_op jit(solution)/shard_map/ppermute | solution.py:91
  25.7 14.2 %collective-permute-start.2 = (bf16[2,2,256,384]{3,2,1,0:T(8,128)(2,1)S(1)}, bf16[2,2,256,384]{3,2,1,0:T(8,128)(2,1)S(1)}, u32[]{:S(2)}, u32[]{:S(2)}) collective-permute-start(bf16[2,2,256,384]{3,2,1,0:T(8,128)(2,1)S(1)} %pad_maximum_fusion.4), channel_id=1, source_target_pairs={{0,1},{1,0},{2,3},{3,2},{4,5},{5,4},{6,7},{7,6},{8,9},{9,8},{10,11... | collective-permute-start | bytes 2359304 | tf_op jit(solution)/shard_map/ppermute | solution.py:103
  29.6 8.7 %collective-permute-start.7 = (bf16[256,384]{1,0:T(8,128)(2,1)S(1)}, bf16[256,384]{1,0:T(8,128)(2,1)S(1)}, u32[]{:S(2)}, u32[]{:S(2)}) collective-permute-start(bf16[256,384]{1,0:T(8,128)(2,1)S(1)} %get-tuple-element.27), channel_id=1, source_target_pairs={{4,0},{8,4},{12,8},{5,1},{9,5},{13,9},{6,2},{10,6},{14,10},{7,3},{... | collective-permute-start | bytes 589832 | tf_op jit(solution)/shard_map/ppermute | solution.py:12
  30.9 8.6 %collective-permute-start.12 = (bf16[256,384]{1,0:T(8,128)(2,1)S(1)}, bf16[256,384]{1,0:T(8,128)(2,1)S(1)}, u32[]{:S(2)}, u32[]{:S(2)}) collective-permute-start(bf16[256,384]{1,0:T(8,128)(2,1)S(1)} %get-tuple-element.26), channel_id=1, source_target_pairs={{0,4},{4,8},{8,12},{1,5},{5,9},{9,13},{2,6},{6,10},{10,14},{3,7},{... | collective-permute-start | bytes 589832 | tf_op jit(solution)/shard_map/ppermute | solution.py:12
  43.5 23.4 %collective-permute-start.8 = (f32[2,192,384]{2,1,0:T(8,128)S(1)}, f32[2,192,384]{2,1,0:T(8,128)S(1)}, u32[]{:S(2)}, u32[]{:S(2)}) collective-permute-start(f32[2,192,384]{2,1,0:T(8,128)S(1)} %select_bitcast_fusion), channel_id=1, source_target_pairs={{0,4},{4,0},{8,12},{12,8},{1,5},{5,1},{9,13},{13,9},{2,6},{6,2},{1... | collective-permute-start | bytes 1769480 | tf_op jit(solution)/shard_map/ppermute | solution.py:58
  47.4 17.3 %collective-permute-start.13 = (f32[2,96,384]{2,1,0:T(8,128)S(1)}, f32[2,96,384]{2,1,0:T(8,128)S(1)}, u32[]{:S(2)}, u32[]{:S(2)}) collective-permute-start(f32[2,96,384]{2,1,0:T(8,128)S(1)} %select_bitcast_fusion.1), channel_id=1, source_target_pairs={{0,4},{4,0},{8,12},{12,8},{1,5},{5,1},{9,13},{13,9},{2,6},{6,2},{1... | collective-permute-start | bytes 884744 | tf_op jit(solution)/shard_map/ppermute | solution.py:58
  50.1 1.1 %copy-start.3 = (f32[512,384]{1,0:T(8,128)S(1)}, f32[512,384]{1,0:T(8,128)}, u32[]{:S(2)}) copy-start(f32[512,384]{1,0:T(8,128)} %get-tuple-element.31) | copy-start | bytes 2359300
  64.8 15.6 %collective-permute-start.14 = (f32[96,384]{1,0:T(8,128)S(1)}, f32[96,384]{1,0:T(8,128)S(1)}, u32[]{:S(2)}, u32[]{:S(2)}) collective-permute-start(f32[96,384]{1,0:T(8,128)S(1)} %select_bitcast_fusion.7), channel_id=1, source_target_pairs={{0,8},{8,0},{4,12},{12,4},{1,9},{9,1},{5,13},{13,5},{2,10},{10,2},... | collective-permute-start | bytes 442376 | tf_op jit(solution)/shard_map/ppermute | solution.py:63
  67.1 21.8 %collective-permute-start.9 = (f32[192,384]{1,0:T(8,128)S(1)}, f32[192,384]{1,0:T(8,128)S(1)}, u32[]{:S(2)}, u32[]{:S(2)}) collective-permute-start(f32[192,384]{1,0:T(8,128)S(1)} %select_bitcast_fusion.4), channel_id=1, source_target_pairs={{0,8},{8,0},{4,12},{12,4},{1,9},{9,1},{5,13},{13,5},{2,10},{10,2},... | collective-permute-start | bytes 884744 | tf_op jit(solution)/shard_map/ppermute | solution.py:63
  80.4 8.4 %collective-permute-start.15 = (bf16[96,384]{1,0:T(8,128)(2,1)S(1)}, bf16[96,384]{1,0:T(8,128)(2,1)S(1)}, u32[]{:S(2)}, u32[]{:S(2)}) collective-permute-start(bf16[96,384]{1,0:T(8,128)(2,1)S(1)} %fusion.69), channel_id=1, source_target_pairs={{0,8},{8,0},{4,12},{12,4},{1,9},{9,1},{5,13},{13,5},{2,10},{10,2},... | collective-permute-start | bytes 221192 | tf_op jit(solution)/shard_map/ppermute | solution.py:64
  88.8 10.7 %collective-permute-start.16 = (bf16[2,96,384]{2,1,0:T(8,128)(2,1)S(1)}, bf16[2,96,384]{2,1,0:T(8,128)(2,1)S(1)}, u32[]{:S(2)}, u32[]{:S(2)}) collective-permute-start(bf16[2,96,384]{2,1,0:T(8,128)(2,1)S(1)} %maximum_select_fusion.1), channel_id=1, source_target_pairs={{0,4},{4,0},{8,12},{12,8},{1,5},{5,1},{9,13},{13,9},{2,6},{6,2},{1... | collective-permute-start | bytes 442376 | tf_op jit(solution)/shard_map/ppermute | solution.py:66
  89.0 10.2 %collective-permute-start.10 = (bf16[192,384]{1,0:T(8,128)(2,1)S(1)}, bf16[192,384]{1,0:T(8,128)(2,1)S(1)}, u32[]{:S(2)}, u32[]{:S(2)}) collective-permute-start(bf16[192,384]{1,0:T(8,128)(2,1)S(1)} %fusion.68), channel_id=1, source_target_pairs={{0,8},{8,0},{4,12},{12,4},{1,9},{9,1},{5,13},{13,5},{2,10},{10,2},... | collective-permute-start | bytes 442376 | tf_op jit(solution)/shard_map/ppermute | solution.py:64
  99.3 6.8 %collective-permute-start.11 = (bf16[2,192,384]{2,1,0:T(8,128)(2,1)S(1)}, bf16[2,192,384]{2,1,0:T(8,128)(2,1)S(1)}, u32[]{:S(2)}, u32[]{:S(2)}) collective-permute-start(bf16[2,192,384]{2,1,0:T(8,128)(2,1)S(1)} %maximum_select_fusion), channel_id=1, source_target_pairs={{0,4},{4,0},{8,12},{12,8},{1,5},{5,1},{9,13},{13,9},{2,6},{6,2},{1... | collective-permute-start | bytes 884744 | tf_op jit(solution)/shard_map/ppermute | solution.py:66

commit v26 on v11

--- a/solution.py
+++ b/solution.py
@@ -66,7 +66,7 @@
     far_set = lax.ppermute(own_set, "seq", pairs)
     evens = jnp.where(odd, far_set, own_set)
     odds = jnp.where(odd, own_set, far_set)
-    return jnp.stack([evens, odds], 1).reshape(block.shape).astype(jnp.float32)
+    return jnp.stack([evens, odds], 1).reshape(block.shape)
 
 
 def shards(seq_in, conv_weight, cotangent):
@@ -145,7 +145,9 @@
         if seq_count == 4:
             middle = line_total(grads[1])
             sides = line_total(jnp.concatenate([grads[0], grads[2]], 0))
-            weight_grad = jnp.stack([sides[: middle.shape[0]], middle, sides[middle.shape[0] :]])
+            weight_grad = jnp.stack(
+                [sides[: middle.shape[0]], middle, sides[middle.shape[0] :]]
+            ).astype(jnp.float32)
         else:
             weight_grad = lax.psum(jnp.stack([grads[0], grads[1], grads[2]]), "seq")
     else:

time: 103 us -> 103 us (level)
    convert_element_type x2 -> x1, other arithmetic: 0.12 us -> 1.35 us  [shards(): weight_grad = jnp.stack([sides[:middle.shape[0]], middle, sides[middle.sh...]
    another operation x3 -> x4, other arithmetic: 1.47 us -> 0.25 us  [line_total(): return jnp.stack([evens, odds], 1).reshape(block.shape)]
where the time goes in v26:
time: 103 us; the launch traced here: 102 us
  waiting for transfers between devices  42.3 us (41%)
  starting transfers between devices  31.2 us (30%)
  matrix products  11.5 us (11%)
  other arithmetic  9.43 us (9%)
  local copies, waits for them, and re-layouts  6.85 us (7%)
    ppermute x2, waiting for transfers between devices, line_total(): other = lax.ppermute(total, 'seq', across)  16.6 us
    ppermute x4, starting transfers between devices, shift_from(): return lax.ppermute(block, axis, route)  11 us
    ppermute x2, waiting for transfers between devices, line_total(): lax.ppermute(jnp.where(odd, even_set, odd_set), 'seq', pairs)  10.9 us
    ppermute x4, waiting for transfers between devices, shift_from(): return lax.ppermute(block, axis, route)  8.39 us
    ppermute x2, waiting for transfers between devices, line_total(): far_set = lax.ppermute(own_set, 'seq', pairs)  6.42 us
    ppermute x2, starting transfers between devices, line_total(): other = lax.ppermute(total, 'seq', across)  5.92 us
    ppermute x1, starting transfers between devices, shards(): lax.ppermute(jnp.concatenate([both.reshape(-1, width), w_other.reshape(-1...  3.71 us
    dot_general x3, matrix products, shards(): jnp.dot(own_taps[:, k].T, cot_mine, preferred_element_type=jnp.float32)  3.05 us
  transfers between devices with their start and end apart: 17, of which 7 were waited for; matrix products, arithmetic and copies ran while one was open for 22% of the time, Pallas kernels for 0%

profile of v26, /device:TPU:0, one launch (start us, length us, event | category | flops | bytes accessed | tf_op | source)
XLA Modules:
  0.0 102.4 jit_solution(6810948528900752832)
XLA Ops:
  0.6 1.4 %collective-permute-start.5 = (bf16[512,384]{1,0:T(8,128)(2,1)}, bf16[512,384]{1,0:T(8,128)(2,1)}, u32[]{:S(2)}, u32[]{:S(2)}) collective-permute-start(bf16[512,384]{1,0:T(8,128)(2,1)} %bitcast.157), channel_id=1, source_target_pairs={{2,0},{1,3},{6,4},{5,7},{10,8},{9,11},{14,12},{13,15},{18,16},{17,... | collective-permute-start | bytes 1179656 | tf_op jit(solution)/shard_map/ppermute | solution.py:88
  2.1 1.4 %collective-permute-start.6 = (bf16[512,384]{1,0:T(8,128)(2,1)}, bf16[512,384]{1,0:T(8,128)(2,1)}, u32[]{:S(2)}, u32[]{:S(2)}) collective-permute-start(bf16[512,384]{1,0:T(8,128)(2,1)} %bitcast.158), channel_id=1, source_target_pairs={{2,1},{1,2},{6,5},{5,6},{10,9},{9,10},{14,13},{13,14},{18,17},{17,... | collective-permute-start | bytes 1179656 | tf_op jit(solution)/shard_map/ppermute | solution.py:89
  3.5 2.8 %multiply_convert_fusion = (bf16[512,384]{1,0:T(8,128)(2,1)S(1)}, f32[512,384]{1,0:T(8,128)}) fusion(bf16[1,1024,384]{2,1,0:T(8,128)(2,1)} %param.3, s32[1024]{0:T(1024)S(1)} %get-tuple-element.32, s32[1024]{0:T(1024)S(1)} %get-tuple-element.33, pred[1024]{0:T(1024)(128)(4,1)S(1)} %fusion.73), kind=kOutput, calls=%fused_computation.61 | convolution fusion | flops 406519808 | bytes 1975296 | tf_op jit(solution)/shard_map/dot_general | solution.py:83
  6.3 1.0 fusion.47
  7.3 5.7 %collective-permute-start = (bf16[2,256,384]{2,1,0:T(8,128)(2,1)}, bf16[2,256,384]{2,1,0:T(8,128)(2,1)}, u32[]{:S(2)}, u32[]{:S(2)}) collective-permute-start(bf16[2,256,384]{2,1,0:T(8,128)(2,1)} %get-tuple-element.19), channel_id=1, source_target_pairs={{0,4},{4,8},{8,12},{1,5},{5,9},{9,13},{2,6},{6,10},{10,14},{3,7},{... | collective-permute-start | bytes 1179656 | tf_op jit(solution)/shard_map/ppermute | solution.py:12
  13.0 1.3 %collective-permute-start.1 = (bf16[2,256,384]{2,1,0:T(8,128)(2,1)}, bf16[2,256,384]{2,1,0:T(8,128)(2,1)}, u32[]{:S(2)}, u32[]{:S(2)}) collective-permute-start(bf16[2,256,384]{2,1,0:T(8,128)(2,1)} %get-tuple-element.20), channel_id=1, source_target_pairs={{4,0},{8,4},{12,8},{5,1},{9,5},{13,9},{6,2},{10,6},{14,10},{7,3},{... | collective-permute-start | bytes 1179656 | tf_op jit(solution)/shard_map/ppermute | solution.py:12
  14.3 1.0 pad_maximum_fusion.2
  15.4 1.0 %copy-done.2 = bf16[2,512,384]{2,1,0:T(8,128)(2,1)S(1)} copy-done((bf16[2,512,384]{2,1,0:T(8,128)(2,1)S(1)}, bf16[2,512,384]{2,1,0:T(8,128)(2,1)}, u32[]{:S(2)}) %copy-start.2) | copy-done | bytes 786456
  16.4 1.3 %pad_maximum_fusion = bf16[2176,384]{1,0:T(8,128)(2,1)} fusion(bf16[1152,384]{1,0:T(8,128)(2,1)S(1)} %bitcast.162, bf16[1024,384]{1,0:T(8,128)(2,1)S(1)} %bitcast.163), kind=kLoop, calls=%fused_computation.2 | loop fusion | flops 3342336 | bytes 3342336 | tf_op jit(solution)/shard_map/concatenate | solution.py:97
  17.8 3.7 %collective-permute-start.3 = (bf16[2176,384]{1,0:T(8,128)(2,1)}, bf16[2176,384]{1,0:T(8,128)(2,1)}, u32[]{:S(2)}, u32[]{:S(2)}) collective-permute-start(bf16[2176,384]{1,0:T(8,128)(2,1)} %pad_maximum_fusion), channel_id=1, source_target_pairs={{0,1},{1,0},{2,3},{3,2},{4,5},{5,4},{6,7},{7,6},{8,9},{9,8},{10,11... | collective-permute-start | bytes 5013512 | tf_op jit(solution)/shard_map/ppermute | solution.py:96
  21.5 1.0 collective-permute-start.4
  22.4 2.0 %collective-permute-done.1 = bf16[2,256,384]{2,1,0:T(8,128)(2,1)} collective-permute-done((bf16[2,256,384]{2,1,0:T(8,128)(2,1)}, bf16[2,256,384]{2,1,0:T(8,128)(2,1)}, u32[]{:S(2)}, u32[]{:S(2)}) %collective-permute-start.1) | collective-permute-done | bytes 393248 | tf_op jit(solution)/shard_map/ppermute | solution.py:12
  24.5 1.2 %pad_maximum_fusion.3 = bf16[2,2,256,384]{3,2,1,0:T(8,128)(2,1)S(1)} fusion(bf16[1,2,256,384]{3,2,1,0:T(8,128)(2,1)} %bitcast.7, bf16[1,2,256,384]{3,2,1,0:T(8,128)(2,1)} %bitcast.6), kind=kLoop, calls=%fused_computation.59 | loop fusion | flops 393216 | bytes 1572864 | tf_op jit(solution)/shard_map/stack | solution.py:103
  25.7 2.8 %collective-permute-start.2 = (bf16[2,2,256,384]{3,2,1,0:T(8,128)(2,1)S(1)}, bf16[2,2,256,384]{3,2,1,0:T(8,128)(2,1)S(1)}, u32[]{:S(2)}, u32[]{:S(2)}) collective-permute-start(bf16[2,2,256,384]{3,2,1,0:T(8,128)(2,1)S(1)} %pad_maximum_fusion.3), channel_id=1, source_target_pairs={{0,1},{1,0},{2,3},{3,2},{4,5},{5,4},{6,7},{7,6},{8,9},{9,8},{10,11... | collective-permute-start | bytes 2359304 | tf_op jit(solution)/shard_map/ppermute | solution.py:103
  28.5 1.0 %broadcast_select_fusion = bf16[512,384]{1,0:T(8,128)(2,1)S(1)} fusion(bf16[512,384]{1,0:T(8,128)(2,1)} %collective-permute-done.5, bf16[512,384]{1,0:T(8,128)(2,1)} %collective-permute-done.6, pred[]{:T(512)S(6)} %eq.16), kind=kLoop, calls=%fused_computation.103 | loop fusion | flops 196608 | bytes 1179649 | tf_op jit(solution)/shard_map/jit(_where)/select_n | solution.py:90
  29.6 2.8 %collective-permute-start.8 = (bf16[256,384]{1,0:T(8,128)(2,1)S(1)}, bf16[256,384]{1,0:T(8,128)(2,1)S(1)}, u32[]{:S(2)}, u32[]{:S(2)}) collective-permute-start(bf16[256,384]{1,0:T(8,128)(2,1)S(1)} %get-tuple-element.26), channel_id=1, source_target_pairs={{0,4},{4,8},{8,12},{1,5},{5,9},{9,13},{2,6},{6,10},{10,14},{3,7},{... | collective-permute-start | bytes 589832 | tf_op jit(solution)/shard_map/ppermute | solution.py:12
  32.4 1.3 %collective-permute-start.7 = (bf16[256,384]{1,0:T(8,128)(2,1)S(1)}, bf16[256,384]{1,0:T(8,128)(2,1)S(1)}, u32[]{:S(2)}, u32[]{:S(2)}) collective-permute-start(bf16[256,384]{1,0:T(8,128)(2,1)S(1)} %get-tuple-element.27), channel_id=1, source_target_pairs={{4,0},{8,4},{12,8},{5,1},{9,5},{13,9},{6,2},{10,6},{14,10},{7,3},{... | collective-permute-start | bytes 589832 | tf_op jit(solution)/shard_map/ppermute | solution.py:12
  33.7 0.4 fusion.87
  34.1 2.6 %collective-permute-done.8 = bf16[256,384]{1,0:T(8,128)(2,1)S(1)} collective-permute-done((bf16[256,384]{1,0:T(8,128)(2,1)S(1)}, bf16[256,384]{1,0:T(8,128)(2,1)S(1)}, u32[]{:S(2)}, u32[]{:S(2)}) %collective-permute-start.8) | collective-permute-done | bytes 196640 | tf_op jit(solution)/shard_map/ppermute | solution.py:12
  36.7 0.4 fusion.57
  37.1 3.7 %collective-permute-done.7 = bf16[256,384]{1,0:T(8,128)(2,1)S(1)} collective-permute-done((bf16[256,384]{1,0:T(8,128)(2,1)S(1)}, bf16[256,384]{1,0:T(8,128)(2,1)S(1)}, u32[]{:S(2)}, u32[]{:S(2)}) %collective-permute-start.7) | collective-permute-done | bytes 196640 | tf_op jit(solution)/shard_map/ppermute | solution.py:12
  40.8 0.4 fusion.53
  41.3 1.6 %fusion.52 = (bf16[512,1,384]{2,0,1:T(8,128)(2,1)S(1)}, bf16[512,1,384]{2,0,1:T(8,128)(2,1)S(1)}, bf16[512,1,384]{2,0,1:T(8,128)(2,1)S(1)}, bf16[512,1,384]{2,0,1:T(8,128)(2,1)S(1)}, bf16[1,512,384]{2,1,0:T(8,128)(2,1)S(1)}) fusion(bf16[2,256,384]{2,1,0:T(8,128)(2,1)} %collective-permute-done.1, bf16[1,512,384]{2,1,0:T(8,128)(2,1)S(1)} %copy-done.1, ...), kind=kLoop, calls=%fused_computation.80 | loop fusion | flops 4915200 | bytes 3932161 | tf_op jit(solution)/shard_map/stack | solution.py:21
  42.9 0.4 convolution_add_fusion
  43.4 1.6 %collective-permute-start.13 = (f32[2,96,384]{2,1,0:T(8,128)S(1)}, f32[2,96,384]{2,1,0:T(8,128)S(1)}, u32[]{:S(2)}, u32[]{:S(2)}) collective-permute-start(f32[2,96,384]{2,1,0:T(8,128)S(1)} %select_bitcast_fusion.1), channel_id=1, source_target_pairs={{0,4},{4,0},{8,12},{12,8},{1,5},{5,1},{9,13},{13,9},{2,6},{6,2},{1... | collective-permute-start | bytes 884744 | tf_op jit(solution)/shard_map/ppermute | solution.py:58
  45.0 1.3 %convolution_add_fusion.1 = f32[384,384]{1,0:T(8,128)S(1)} fusion(f32[384,384]{1,0:T(8,128)S(1)} %fusion.57, bf16[1,512,384]{2,1,0:T(8,128)(2,1)S(1)} %get-tuple-element.25, bf16[2,256,384]{2,1,0:T(8,128)(2,1)} %collective-permute-done.1, bf16[1,512,384]{2,1,0:T(8,128)(2,1)S(1)} %copy-done.1, bf16[1,512,384]{2,1,0:T(8,128)(2,1)S(1)} %bitcast.152), kind=kOutput, calls=%fused_computation.12 | convolution fusion | flops 152322048 | bytes 2752512 | tf_op jit(solution)/shard_map/dot_general | solution.py:142
  46.3 1.3 %convolution_add_fusion.2 = f32[384,384]{1,0:T(8,128)S(1)} fusion(f32[384,384]{1,0:T(8,128)S(1)} %fusion.53, bf16[1,512,384]{2,1,0:T(8,128)(2,1)S(1)} %get-tuple-element.25, bf16[2,256,384]{2,1,0:T(8,128)(2,1)} %collective-permute-done, bf16[1,512,384]{2,1,0:T(8,128)(2,1)S(1)} %copy-done.1, bf16[1,512,384]{2,1,0:T(8,128)(2,1)S(1)} %bitcast.153), kind=kOutput, calls=%fused_computation.13 | convolution fusion | flops 152322048 | bytes 2752512 | tf_op jit(solution)/shard_map/dot_general | solution.py:142
  47.8 0.5 collective-permute-start.9
  48.3 1.2 %slice.184 = bf16[1024,384]{1,0:T(8,128)(2,1)S(1)} slice(bf16[2176,384]{1,0:T(8,128)(2,1)} %collective-permute-done.3), slice={[0:1024], [0:384]} | slice | bytes 1572864 | tf_op jit(solution)/shard_map/slice | solution.py:99
  49.6 0.2 fusion.50
  49.8 1.2 %slice_bitcast_fusion.3 = (bf16[512,1,384]{2,0,1:T(8,128)(2,1)S(1)}, bf16[512,1,384]{2,0,1:T(8,128)(2,1)S(1)}) fusion(bf16[2176,384]{1,0:T(8,128)(2,1)} %collective-permute-done.3), kind=kLoop, calls=%fused_computation.104 | loop fusion | bytes 1572864 | tf_op jit(solution)/shard_map/stack | solution.py:21
  51.0 0.8 convolution_bitcast_fusion
  51.8 0.3 copy-done.3
  52.1 1.3 %fusion.39 = bf16[512,384]{1,0:T(8,128)(2,1)S(1)} fusion(f32[512,384]{1,0:T(8,128)S(1)} %copy-done.3, f32[512,384]{1,0:T(8,128)S(1)} %convolution_bitcast_fusion, bf16[512,1,384]{2,0,1:T(8,128)(2,1)S(1)} %get-tuple-element.14, bf16[512,1,384]{2,0,1:T(8,128)(2,1)S(1)} %bitcast.159, bf16[512,1,384]{2,0,1:T(8,128)(2,1)S(1)} %get-tuple-element.5, ...), kind=kOutput, calls=%fused_computation.58 | convolution fusion | flops 458883072 | bytes 4423684 | tf_op jit(solution)/shard_map/tko,kio->ti/dot_general | solution.py:116
  53.4 1.3 %slice.187 = bf16[1152,384]{1,0:T(8,128)(2,1)S(1)} slice(bf16[2176,384]{1,0:T(8,128)(2,1)} %collective-permute-done.3), slice={[1024:2176], [0:384]} | slice | bytes 1769472 | tf_op jit(solution)/shard_map/slice | solution.py:100
  54.8 1.4 %collective-permute-start.14 = (f32[96,384]{1,0:T(8,128)S(1)}, f32[96,384]{1,0:T(8,128)S(1)}, u32[]{:S(2)}, u32[]{:S(2)}) collective-permute-start(f32[96,384]{1,0:T(8,128)S(1)} %select_bitcast_fusion.7), channel_id=1, source_target_pairs={{0,8},{8,0},{4,12},{12,4},{1,9},{9,1},{5,13},{13,5},{2,10},{10,2},... | collective-permute-start | bytes 442376 | tf_op jit(solution)/shard_map/ppermute | solution.py:63
  56.1 10.9 %collective-permute-done.9 = f32[2,192,384]{2,1,0:T(8,128)S(1)} collective-permute-done((f32[2,192,384]{2,1,0:T(8,128)S(1)}, f32[2,192,384]{2,1,0:T(8,128)S(1)}, u32[]{:S(2)}, u32[]{:S(2)}) %collective-permute-start.9) | collective-permute-done | bytes 589856 | tf_op jit(solution)/shard_map/ppermute | solution.py:58
  67.3 3.0 %collective-permute-start.15 = (bf16[96,384]{1,0:T(8,128)(2,1)S(1)}, bf16[96,384]{1,0:T(8,128)(2,1)S(1)}, u32[]{:S(2)}, u32[]{:S(2)}) collective-permute-start(bf16[96,384]{1,0:T(8,128)(2,1)S(1)} %fusion.70), channel_id=1, source_target_pairs={{0,8},{8,0},{4,12},{12,4},{1,9},{9,1},{5,13},{13,5},{2,10},{10,2},... | collective-permute-start | bytes 221192 | tf_op jit(solution)/shard_map/ppermute | solution.py:64
  70.3 0.8 convolution_bitcast_fusion.3
  71.1 12.8 %collective-permute-done.15 = bf16[96,384]{1,0:T(8,128)(2,1)S(1)} collective-permute-done((bf16[96,384]{1,0:T(8,128)(2,1)S(1)}, bf16[96,384]{1,0:T(8,128)(2,1)S(1)}, u32[]{:S(2)}, u32[]{:S(2)}) %collective-permute-start.15) | collective-permute-done | bytes 73760 | tf_op jit(solution)/shard_map/ppermute | solution.py:64
  84.0 3.0 %collective-permute-start.11 = (bf16[192,384]{1,0:T(8,128)(2,1)S(1)}, bf16[192,384]{1,0:T(8,128)(2,1)S(1)}, u32[]{:S(2)}, u32[]{:S(2)}) collective-permute-start(bf16[192,384]{1,0:T(8,128)(2,1)S(1)} %fusion.69), channel_id=1, source_target_pairs={{0,8},{8,0},{4,12},{12,4},{1,9},{9,1},{5,13},{13,5},{2,10},{10,2},... | collective-permute-start | bytes 442376 | tf_op jit(solution)/shard_map/ppermute | solution.py:64
  87.0 1.6 %fusion.4 = bf16[1,512,384]{2,1,0:T(8,128)(2,1)} fusion(f32[512,384]{1,0:T(8,128)S(1)} %copy-done.3, f32[512,384]{1,0:T(8,128)S(1)} %convolution_bitcast_fusion.3, bf16[3,384,384]{2,1,0:T(8,128)(2,1)S(1)} %bitcast.170, bf16[512,1,384]{2,0,1:T(8,128)(2,1)S(1)} %get-tuple-element.10, bf16[512,1,384]{2,0,1:T(8,128)(2,1)S(1)} %get-tuple-element.4, ...), kind=kOutput, calls=%fused_computation.14 | convolution fusion | flops 454754304 | bytes 4030464 | tf_op jit(solution)/shard_map/tki,kio->to/dot_general | solution.py:110
  88.6 0.4 broadcast_in_dim.18
  89.0 1.2 %convert_element_type.40 = bf16[1,1024,384]{2,1,0:T(8,128)(2,1)} reshape(bf16[512,2,384]{2,1,0:T(2,128)(2,1)S(1)} %broadcast_in_dim.18) | data formatting | bytes 1572864 | tf_op jit(solution)/shard_map/convert_element_type | solution.py:125
  90.2 3.8 %collective-permute-done.11 = bf16[192,384]{1,0:T(8,128)(2,1)S(1)} collective-permute-done((bf16[192,384]{1,0:T(8,128)(2,1)S(1)}, bf16[192,384]{1,0:T(8,128)(2,1)S(1)}, u32[]{:S(2)}, u32[]{:S(2)}) %collective-permute-start.11) | collective-permute-done | bytes 147488 | tf_op jit(solution)/shard_map/ppermute | solution.py:64
  94.0 0.3 collective-permute-start.12
  94.4 6.4 %collective-permute-done.12 = bf16[2,192,384]{2,1,0:T(8,128)(2,1)S(1)} collective-permute-done((bf16[2,192,384]{2,1,0:T(8,128)(2,1)S(1)}, bf16[2,192,384]{2,1,0:T(8,128)(2,1)S(1)}, u32[]{:S(2)}, u32[]{:S(2)}) %collective-permute-start.12) | collective-permute-done | bytes 294944 | tf_op jit(solution)/shard_map/ppermute | solution.py:66
  101.0 1.3 %maximum_convert_fusion = f32[3,384,384]{2,1,0:T(8,128)} fusion(bf16[1,384,384]{2,1,0:T(8,128)(2,1)S(1)} %bitcast.169, bf16[1,384,384]{2,1,0:T(8,128)(2,1)S(1)} %bitcast.167, bf16[1,384,384]{2,1,0:T(8,128)(2,1)S(1)} %bitcast.168), kind=kLoop, calls=%fused_computation.49 | loop fusion | flops 1327104 | bytes 2654208 | tf_op jit(solution)/shard_map/convert_element_type | solution.py:150
  (39 shorter events, 1.2 us)
Async XLA Ops:
  0.6 14.7 %copy-start = (bf16[3,384,768]{2,1,0:T(8,128)(2,1)S(1)}, bf16[3,384,768]{2,1,0:T(8,128)(2,1)}, u32[]{:S(2)}) copy-start(bf16[3,384,768]{2,1,0:T(8,128)(2,1)} %param.4) | copy-start | bytes 5308420
  0.6 27.9 %collective-permute-start.5 = (bf16[512,384]{1,0:T(8,128)(2,1)}, bf16[512,384]{1,0:T(8,128)(2,1)}, u32[]{:S(2)}, u32[]{:S(2)}) collective-permute-start(bf16[512,384]{1,0:T(8,128)(2,1)} %bitcast.157), channel_id=1, source_target_pairs={{2,0},{1,3},{6,4},{5,7},{10,8},{9,11},{14,12},{13,15},{18,16},{17,... | collective-permute-start | bytes 1179656 | tf_op jit(solution)/shard_map/ppermute | solution.py:88
  2.1 26.4 %collective-permute-start.6 = (bf16[512,384]{1,0:T(8,128)(2,1)}, bf16[512,384]{1,0:T(8,128)(2,1)}, u32[]{:S(2)}, u32[]{:S(2)}) collective-permute-start(bf16[512,384]{1,0:T(8,128)(2,1)} %bitcast.158), channel_id=1, source_target_pairs={{2,1},{1,2},{6,5},{5,6},{10,9},{9,10},{14,13},{13,14},{18,17},{17,... | collective-permute-start | bytes 1179656 | tf_op jit(solution)/shard_map/ppermute | solution.py:89
  3.5 2.8 %copy-start.1 = (bf16[1,512,384]{2,1,0:T(8,128)(2,1)S(1)}, bf16[1,512,384]{2,1,0:T(8,128)(2,1)}, u32[]{:S(2)}) copy-start(bf16[1,512,384]{2,1,0:T(8,128)(2,1)} %param.5) | copy-start | bytes 1179652
  7.3 14.1 %collective-permute-start = (bf16[2,256,384]{2,1,0:T(8,128)(2,1)}, bf16[2,256,384]{2,1,0:T(8,128)(2,1)}, u32[]{:S(2)}, u32[]{:S(2)}) collective-permute-start(bf16[2,256,384]{2,1,0:T(8,128)(2,1)} %get-tuple-element.19), channel_id=1, source_target_pairs={{0,4},{4,8},{8,12},{1,5},{5,9},{9,13},{2,6},{6,10},{10,14},{3,7},{... | collective-permute-start | bytes 1179656 | tf_op jit(solution)/shard_map/ppermute | solution.py:12
  13.0 11.4 %collective-permute-start.1 = (bf16[2,256,384]{2,1,0:T(8,128)(2,1)}, bf16[2,256,384]{2,1,0:T(8,128)(2,1)}, u32[]{:S(2)}, u32[]{:S(2)}) collective-permute-start(bf16[2,256,384]{2,1,0:T(8,128)(2,1)} %get-tuple-element.20), channel_id=1, source_target_pairs={{4,0},{8,4},{12,8},{5,1},{9,5},{13,9},{6,2},{10,6},{14,10},{7,3},{... | collective-permute-start | bytes 1179656 | tf_op jit(solution)/shard_map/ppermute | solution.py:12
  15.3 1.1 %copy-start.2 = (bf16[2,512,384]{2,1,0:T(8,128)(2,1)S(1)}, bf16[2,512,384]{2,1,0:T(8,128)(2,1)}, u32[]{:S(2)}) copy-start(bf16[2,512,384]{2,1,0:T(8,128)(2,1)} %pad_maximum_fusion.2) | copy-start | bytes 2359300
  17.8 23.6 %collective-permute-start.3 = (bf16[2176,384]{1,0:T(8,128)(2,1)}, bf16[2176,384]{1,0:T(8,128)(2,1)}, u32[]{:S(2)}, u32[]{:S(2)}) collective-permute-start(bf16[2176,384]{1,0:T(8,128)(2,1)} %pad_maximum_fusion), channel_id=1, source_target_pairs={{0,1},{1,0},{2,3},{3,2},{4,5},{5,4},{6,7},{7,6},{8,9},{9,8},{10,11... | collective-permute-start | bytes 5013512 | tf_op jit(solution)/shard_map/ppermute | solution.py:96
  21.5 12.2 %collective-permute-start.4 = (bf16[512,384]{1,0:T(8,128)(2,1)S(1)}, bf16[512,384]{1,0:T(8,128)(2,1)S(1)}, u32[]{:S(2)}, u32[]{:S(2)}) collective-permute-start(bf16[512,384]{1,0:T(8,128)(2,1)S(1)} %get-tuple-element.30), channel_id=1, source_target_pairs={{0,2},{2,0},{1,3},{3,1},{4,6},{6,4},{5,7},{7,5},{8,10},{10,8},{9,1... | collective-permute-start | bytes 1179656 | tf_op jit(solution)/shard_map/ppermute | solution.py:91
  25.7 15.6 %collective-permute-start.2 = (bf16[2,2,256,384]{3,2,1,0:T(8,128)(2,1)S(1)}, bf16[2,2,256,384]{3,2,1,0:T(8,128)(2,1)S(1)}, u32[]{:S(2)}, u32[]{:S(2)}) collective-permute-start(bf16[2,2,256,384]{3,2,1,0:T(8,128)(2,1)S(1)} %pad_maximum_fusion.3), channel_id=1, source_target_pairs={{0,1},{1,0},{2,3},{3,2},{4,5},{5,4},{6,7},{7,6},{8,9},{9,8},{10,11... | collective-permute-start | bytes 2359304 | tf_op jit(solution)/shard_map/ppermute | solution.py:103
  29.6 7.1 %collective-permute-start.8 = (bf16[256,384]{1,0:T(8,128)(2,1)S(1)}, bf16[256,384]{1,0:T(8,128)(2,1)S(1)}, u32[]{:S(2)}, u32[]{:S(2)}) collective-permute-start(bf16[256,384]{1,0:T(8,128)(2,1)S(1)} %get-tuple-element.26), channel_id=1, source_target_pairs={{0,4},{4,8},{8,12},{1,5},{5,9},{9,13},{2,6},{6,10},{10,14},{3,7},{... | collective-permute-start | bytes 589832 | tf_op jit(solution)/shard_map/ppermute | solution.py:12
  32.4 8.5 %collective-permute-start.7 = (bf16[256,384]{1,0:T(8,128)(2,1)S(1)}, bf16[256,384]{1,0:T(8,128)(2,1)S(1)}, u32[]{:S(2)}, u32[]{:S(2)}) collective-permute-start(bf16[256,384]{1,0:T(8,128)(2,1)S(1)} %get-tuple-element.27), channel_id=1, source_target_pairs={{4,0},{8,4},{12,8},{5,1},{9,5},{13,9},{6,2},{10,6},{14,10},{7,3},{... | collective-permute-start | bytes 589832 | tf_op jit(solution)/shard_map/ppermute | solution.py:12
  43.4 11.3 %collective-permute-start.13 = (f32[2,96,384]{2,1,0:T(8,128)S(1)}, f32[2,96,384]{2,1,0:T(8,128)S(1)}, u32[]{:S(2)}, u32[]{:S(2)}) collective-permute-start(f32[2,96,384]{2,1,0:T(8,128)S(1)} %select_bitcast_fusion.1), channel_id=1, source_target_pairs={{0,4},{4,0},{8,12},{12,8},{1,5},{5,1},{9,13},{13,9},{2,6},{6,2},{1... | collective-permute-start | bytes 884744 | tf_op jit(solution)/shard_map/ppermute | solution.py:58
  47.8 19.2 %collective-permute-start.9 = (f32[2,192,384]{2,1,0:T(8,128)S(1)}, f32[2,192,384]{2,1,0:T(8,128)S(1)}, u32[]{:S(2)}, u32[]{:S(2)}) collective-permute-start(f32[2,192,384]{2,1,0:T(8,128)S(1)} %select_bitcast_fusion), channel_id=1, source_target_pairs={{0,4},{4,0},{8,12},{12,8},{1,5},{5,1},{9,13},{13,9},{2,6},{6,2},{1... | collective-permute-start | bytes 1769480 | tf_op jit(solution)/shard_map/ppermute | solution.py:58
  51.0 1.1 %copy-start.3 = (f32[512,384]{1,0:T(8,128)S(1)}, f32[512,384]{1,0:T(8,128)}, u32[]{:S(2)}) copy-start(f32[512,384]{1,0:T(8,128)} %get-tuple-element.31) | copy-start | bytes 2359300
  54.8 12.5 %collective-permute-start.14 = (f32[96,384]{1,0:T(8,128)S(1)}, f32[96,384]{1,0:T(8,128)S(1)}, u32[]{:S(2)}, u32[]{:S(2)}) collective-permute-start(f32[96,384]{1,0:T(8,128)S(1)} %select_bitcast_fusion.7), channel_id=1, source_target_pairs={{0,8},{8,0},{4,12},{12,4},{1,9},{9,1},{5,13},{13,5},{2,10},{10,2},... | collective-permute-start | bytes 442376 | tf_op jit(solution)/shard_map/ppermute | solution.py:63
  67.2 16.8 %collective-permute-start.10 = (f32[192,384]{1,0:T(8,128)S(1)}, f32[192,384]{1,0:T(8,128)S(1)}, u32[]{:S(2)}, u32[]{:S(2)}) collective-permute-start(f32[192,384]{1,0:T(8,128)S(1)} %select_bitcast_fusion.4), channel_id=1, source_target_pairs={{0,8},{8,0},{4,12},{12,4},{1,9},{9,1},{5,13},{13,5},{2,10},{10,2},... | collective-permute-start | bytes 884744 | tf_op jit(solution)/shard_map/ppermute | solution.py:63
  67.3 16.6 %collective-permute-start.15 = (bf16[96,384]{1,0:T(8,128)(2,1)S(1)}, bf16[96,384]{1,0:T(8,128)(2,1)S(1)}, u32[]{:S(2)}, u32[]{:S(2)}) collective-permute-start(bf16[96,384]{1,0:T(8,128)(2,1)S(1)} %fusion.70), channel_id=1, source_target_pairs={{0,8},{8,0},{4,12},{12,4},{1,9},{9,1},{5,13},{13,5},{2,10},{10,2},... | collective-permute-start | bytes 221192 | tf_op jit(solution)/shard_map/ppermute | solution.py:64
  83.9 10.4 %collective-permute-start.16 = (bf16[2,96,384]{2,1,0:T(8,128)(2,1)S(1)}, bf16[2,96,384]{2,1,0:T(8,128)(2,1)S(1)}, u32[]{:S(2)}, u32[]{:S(2)}) collective-permute-start(bf16[2,96,384]{2,1,0:T(8,128)(2,1)S(1)} %maximum_select_fusion.1), channel_id=1, source_target_pairs={{0,4},{4,0},{8,12},{12,8},{1,5},{5,1},{9,13},{13,9},{2,6},{6,2},{1... | collective-permute-start | bytes 442376 | tf_op jit(solution)/shard_map/ppermute | solution.py:66
  84.0 9.9 %collective-permute-start.11 = (bf16[192,384]{1,0:T(8,128)(2,1)S(1)}, bf16[192,384]{1,0:T(8,128)(2,1)S(1)}, u32[]{:S(2)}, u32[]{:S(2)}) collective-permute-start(bf16[192,384]{1,0:T(8,128)(2,1)S(1)} %fusion.69), channel_id=1, source_target_pairs={{0,8},{8,0},{4,12},{12,4},{1,9},{9,1},{5,13},{13,5},{2,10},{10,2},... | collective-permute-start | bytes 442376 | tf_op jit(solution)/shard_map/ppermute | solution.py:64
  94.0 6.8 %collective-permute-start.12 = (bf16[2,192,384]{2,1,0:T(8,128)(2,1)S(1)}, bf16[2,192,384]{2,1,0:T(8,128)(2,1)S(1)}, u32[]{:S(2)}, u32[]{:S(2)}) collective-permute-start(bf16[2,192,384]{2,1,0:T(8,128)(2,1)S(1)} %maximum_select_fusion), channel_id=1, source_target_pairs={{0,4},{4,0},{8,12},{12,8},{1,5},{5,1},{9,13},{13,9},{2,6},{6,2},{1... | collective-permute-start | bytes 884744 | tf_op jit(solution)/shard_map/ppermute | solution.py:66

commit v27 on v26

--- a/solution.py
+++ b/solution.py
@@ -1,4 +1,5 @@
 import jax
+import numpy as np
 import jax.numpy as jnp
 from jax import lax
 from jax.sharding import PartitionSpec as P
@@ -76,10 +77,9 @@
     width = local_in.shape[1]
     spread = rows // 2
     c = lax.axis_index("chan")
-    pairing = lax.broadcasted_iota(jnp.int32, (rows, 2 * rows), 1) // 2 == lax.broadcasted_iota(
-        jnp.int32, (rows, 2 * rows), 0
+    pairing = jnp.asarray(
+        np.kron(np.eye(rows, dtype=np.float32), np.full((1, 2), 0.5, np.float32)), jnp.bfloat16
     )
-    pairing = jnp.where(pairing, 0.5, 0.0).astype(jnp.bfloat16)
     pooled = jnp.dot(pairing, local_in, preferred_element_type=jnp.float32)
     activation = jax.nn.gelu(pooled).astype(jnp.bfloat16)
 

time: 103 us -> 103 us (level)
  transfers between devices with their start and end apart: 17 -> 17, of which waited for: 7 -> 7; matrix products, arithmetic and copies ran while one was open for 22% -> 23% of each run, Pallas kernels for 0% -> 0%
where the time goes in v27:
time: 103 us
  waiting for transfers between devices  42.4 us (41%)
  starting transfers between devices  31.2 us (30%)
  matrix products  11.8 us (11%)
  other arithmetic  9.42 us (9%)
  local copies, waits for them, and re-layouts  6.84 us (7%)
    ppermute x2, waiting for transfers between devices, line_total(): other = lax.ppermute(total, 'seq', across)  16.6 us
    ppermute x4, starting transfers between devices, shift_from(): return lax.ppermute(block, axis, route)  11 us
    ppermute x2, waiting for transfers between devices, line_total(): lax.ppermute(jnp.where(odd, even_set, odd_set), 'seq', pairs)  10.9 us
    ppermute x4, waiting for transfers between devices, shift_from(): return lax.ppermute(block, axis, route)  8.41 us
    ppermute x2, waiting for transfers between devices, line_total(): far_set = lax.ppermute(own_set, 'seq', pairs)  6.42 us
    ppermute x2, starting transfers between devices, line_total(): other = lax.ppermute(total, 'seq', across)  5.92 us
    ppermute x1, starting transfers between devices, shards(): lax.ppermute(jnp.concatenate([both.reshape(-1, width), w_other.reshape(-1...  3.68 us
    dot_general x1, matrix products, shards(): pooled = jnp.dot(pairing, local_in, preferred_element_type=jnp.float32)  3.07 us
  transfers between devices with their start and end apart: 17, of which 7 were waited for; matrix products, arithmetic and copies ran while one was open for 23% of the time, Pallas kernels for 0%

profile of v27, /device:TPU:0, one launch (start us, length us, event | category | flops | bytes accessed | tf_op | source)
XLA Modules:
  0.0 102.6 jit_solution(748084952485190523)
XLA Ops:
  0.7 1.4 %collective-permute-start.5 = (bf16[512,384]{1,0:T(8,128)(2,1)}, bf16[512,384]{1,0:T(8,128)(2,1)}, u32[]{:S(2)}, u32[]{:S(2)}) collective-permute-start(bf16[512,384]{1,0:T(8,128)(2,1)} %bitcast.158), channel_id=1, source_target_pairs={{2,0},{1,3},{6,4},{5,7},{10,8},{9,11},{14,12},{13,15},{18,16},{17,... | collective-permute-start | bytes 1179656 | tf_op jit(solution)/shard_map/ppermute | solution.py:88
  2.1 1.4 %collective-permute-start.6 = (bf16[512,384]{1,0:T(8,128)(2,1)}, bf16[512,384]{1,0:T(8,128)(2,1)}, u32[]{:S(2)}, u32[]{:S(2)}) collective-permute-start(bf16[512,384]{1,0:T(8,128)(2,1)} %bitcast.159), channel_id=1, source_target_pairs={{2,1},{1,2},{6,5},{5,6},{10,9},{9,10},{14,13},{13,14},{18,17},{17,... | collective-permute-start | bytes 1179656 | tf_op jit(solution)/shard_map/ppermute | solution.py:89
  3.5 3.1 %multiply_convert_fusion = (bf16[512,384]{1,0:T(8,128)(2,1)S(1)}, f32[512,384]{1,0:T(8,128)}) fusion(bf16[512,1024]{1,0:T(8,128)(2,1)} %constant.46.clone, bf16[1,1024,384]{2,1,0:T(8,128)(2,1)} %param.4), kind=kOutput, calls=%fused_computation.54 | convolution fusion | flops 404422656 | bytes 3014656 | tf_op jit(solution)/shard_map/dot_general | solution.py:83
  6.6 1.0 fusion.42
  7.6 5.7 %collective-permute-start = (bf16[2,256,384]{2,1,0:T(8,128)(2,1)}, bf16[2,256,384]{2,1,0:T(8,128)(2,1)}, u32[]{:S(2)}, u32[]{:S(2)}) collective-permute-start(bf16[2,256,384]{2,1,0:T(8,128)(2,1)} %get-tuple-element.19), channel_id=1, source_target_pairs={{0,4},{4,8},{8,12},{1,5},{5,9},{9,13},{2,6},{6,10},{10,14},{3,7},{... | collective-permute-start | bytes 1179656 | tf_op jit(solution)/shard_map/ppermute | solution.py:13
  13.3 1.3 %collective-permute-start.1 = (bf16[2,256,384]{2,1,0:T(8,128)(2,1)}, bf16[2,256,384]{2,1,0:T(8,128)(2,1)}, u32[]{:S(2)}, u32[]{:S(2)}) collective-permute-start(bf16[2,256,384]{2,1,0:T(8,128)(2,1)} %get-tuple-element.20), channel_id=1, source_target_pairs={{4,0},{8,4},{12,8},{5,1},{9,5},{13,9},{6,2},{10,6},{14,10},{7,3},{... | collective-permute-start | bytes 1179656 | tf_op jit(solution)/shard_map/ppermute | solution.py:13
  14.6 1.0 pad_maximum_fusion.2
  15.6 1.0 %copy-done.2 = bf16[2,512,384]{2,1,0:T(8,128)(2,1)S(1)} copy-done((bf16[2,512,384]{2,1,0:T(8,128)(2,1)S(1)}, bf16[2,512,384]{2,1,0:T(8,128)(2,1)}, u32[]{:S(2)}) %copy-start.2) | copy-done | bytes 786456
  16.7 1.3 %pad_maximum_fusion = bf16[2176,384]{1,0:T(8,128)(2,1)} fusion(bf16[1152,384]{1,0:T(8,128)(2,1)S(1)} %bitcast.163, bf16[1024,384]{1,0:T(8,128)(2,1)S(1)} %bitcast.164), kind=kLoop, calls=%fused_computation | loop fusion | flops 3342336 | bytes 3342336 | tf_op jit(solution)/shard_map/concatenate | solution.py:97
  18.0 3.7 %collective-permute-start.3 = (bf16[2176,384]{1,0:T(8,128)(2,1)}, bf16[2176,384]{1,0:T(8,128)(2,1)}, u32[]{:S(2)}, u32[]{:S(2)}) collective-permute-start(bf16[2176,384]{1,0:T(8,128)(2,1)} %pad_maximum_fusion), channel_id=1, source_target_pairs={{0,1},{1,0},{2,3},{3,2},{4,5},{5,4},{6,7},{7,6},{8,9},{9,8},{10,11... | collective-permute-start | bytes 5013512 | tf_op jit(solution)/shard_map/ppermute | solution.py:96
  21.7 1.0 collective-permute-start.4
  22.7 2.0 %collective-permute-done.1 = bf16[2,256,384]{2,1,0:T(8,128)(2,1)} collective-permute-done((bf16[2,256,384]{2,1,0:T(8,128)(2,1)}, bf16[2,256,384]{2,1,0:T(8,128)(2,1)}, u32[]{:S(2)}, u32[]{:S(2)}) %collective-permute-start.1) | collective-permute-done | bytes 393248 | tf_op jit(solution)/shard_map/ppermute | solution.py:13
  24.8 1.2 %pad_maximum_fusion.3 = bf16[2,2,256,384]{3,2,1,0:T(8,128)(2,1)S(1)} fusion(bf16[1,2,256,384]{3,2,1,0:T(8,128)(2,1)} %bitcast.7, bf16[1,2,256,384]{3,2,1,0:T(8,128)(2,1)} %bitcast.6), kind=kLoop, calls=%fused_computation.51 | loop fusion | flops 393216 | bytes 1572864 | tf_op jit(solution)/shard_map/stack | solution.py:103
  26.0 2.8 %collective-permute-start.2 = (bf16[2,2,256,384]{3,2,1,0:T(8,128)(2,1)S(1)}, bf16[2,2,256,384]{3,2,1,0:T(8,128)(2,1)S(1)}, u32[]{:S(2)}, u32[]{:S(2)}) collective-permute-start(bf16[2,2,256,384]{3,2,1,0:T(8,128)(2,1)S(1)} %pad_maximum_fusion.3), channel_id=1, source_target_pairs={{0,1},{1,0},{2,3},{3,2},{4,5},{5,4},{6,7},{7,6},{8,9},{9,8},{10,11... | collective-permute-start | bytes 2359304 | tf_op jit(solution)/shard_map/ppermute | solution.py:103
  28.8 1.0 %broadcast_select_fusion = bf16[512,384]{1,0:T(8,128)(2,1)S(1)} fusion(bf16[512,384]{1,0:T(8,128)(2,1)} %collective-permute-done.5, bf16[512,384]{1,0:T(8,128)(2,1)} %collective-permute-done.6, pred[]{:T(512)S(6)} %eq.12), kind=kLoop, calls=%fused_computation.96 | loop fusion | flops 196608 | bytes 1179649 | tf_op jit(solution)/shard_map/jit(_where)/select_n | solution.py:90
  29.9 2.8 %collective-permute-start.8 = (bf16[256,384]{1,0:T(8,128)(2,1)S(1)}, bf16[256,384]{1,0:T(8,128)(2,1)S(1)}, u32[]{:S(2)}, u32[]{:S(2)}) collective-permute-start(bf16[256,384]{1,0:T(8,128)(2,1)S(1)} %get-tuple-element.26), channel_id=1, source_target_pairs={{0,4},{4,8},{8,12},{1,5},{5,9},{9,13},{2,6},{6,10},{10,14},{3,7},{... | collective-permute-start | bytes 589832 | tf_op jit(solution)/shard_map/ppermute | solution.py:13
  32.6 1.3 %collective-permute-start.7 = (bf16[256,384]{1,0:T(8,128)(2,1)S(1)}, bf16[256,384]{1,0:T(8,128)(2,1)S(1)}, u32[]{:S(2)}, u32[]{:S(2)}) collective-permute-start(bf16[256,384]{1,0:T(8,128)(2,1)S(1)} %get-tuple-element.27), channel_id=1, source_target_pairs={{4,0},{8,4},{12,8},{5,1},{9,5},{13,9},{6,2},{10,6},{14,10},{7,3},{... | collective-permute-start | bytes 589832 | tf_op jit(solution)/shard_map/ppermute | solution.py:13
  33.9 0.4 fusion.77
  34.3 2.6 %collective-permute-done.8 = bf16[256,384]{1,0:T(8,128)(2,1)S(1)} collective-permute-done((bf16[256,384]{1,0:T(8,128)(2,1)S(1)}, bf16[256,384]{1,0:T(8,128)(2,1)S(1)}, u32[]{:S(2)}, u32[]{:S(2)}) %collective-permute-start.8) | collective-permute-done | bytes 196640 | tf_op jit(solution)/shard_map/ppermute | solution.py:13
  37.0 0.4 fusion.52
  37.4 3.7 %collective-permute-done.7 = bf16[256,384]{1,0:T(8,128)(2,1)S(1)} collective-permute-done((bf16[256,384]{1,0:T(8,128)(2,1)S(1)}, bf16[256,384]{1,0:T(8,128)(2,1)S(1)}, u32[]{:S(2)}, u32[]{:S(2)}) %collective-permute-start.7) | collective-permute-done | bytes 196640 | tf_op jit(solution)/shard_map/ppermute | solution.py:13
  41.1 0.4 fusion.48
  41.6 1.6 %fusion.47 = (bf16[512,1,384]{2,0,1:T(8,128)(2,1)S(1)}, bf16[512,1,384]{2,0,1:T(8,128)(2,1)S(1)}, bf16[512,1,384]{2,0,1:T(8,128)(2,1)S(1)}, bf16[512,1,384]{2,0,1:T(8,128)(2,1)S(1)}, bf16[1,512,384]{2,1,0:T(8,128)(2,1)S(1)}) fusion(bf16[2,256,384]{2,1,0:T(8,128)(2,1)} %collective-permute-done.1, bf16[1,512,384]{2,1,0:T(8,128)(2,1)S(1)} %copy-done.1, ...), kind=kLoop, calls=%fused_computation.73 | loop fusion | flops 4915200 | bytes 3932161 | tf_op jit(solution)/shard_map/stack | solution.py:22
  43.2 0.4 convolution_add_fusion
  43.6 1.6 %collective-permute-start.13 = (f32[2,96,384]{2,1,0:T(8,128)S(1)}, f32[2,96,384]{2,1,0:T(8,128)S(1)}, u32[]{:S(2)}, u32[]{:S(2)}) collective-permute-start(f32[2,96,384]{2,1,0:T(8,128)S(1)} %select_bitcast_fusion.1), channel_id=1, source_target_pairs={{0,4},{4,0},{8,12},{12,8},{1,5},{5,1},{9,13},{13,9},{2,6},{6,2},{1... | collective-permute-start | bytes 884744 | tf_op jit(solution)/shard_map/ppermute | solution.py:59
  45.3 1.3 %convolution_add_fusion.1 = f32[384,384]{1,0:T(8,128)S(1)} fusion(f32[384,384]{1,0:T(8,128)S(1)} %fusion.52, bf16[1,512,384]{2,1,0:T(8,128)(2,1)S(1)} %get-tuple-element.25, bf16[2,256,384]{2,1,0:T(8,128)(2,1)} %collective-permute-done.1, bf16[1,512,384]{2,1,0:T(8,128)(2,1)S(1)} %copy-done.1, bf16[1,512,384]{2,1,0:T(8,128)(2,1)S(1)} %bitcast.153), kind=kOutput, calls=%fused_computation.10 | convolution fusion | flops 152322048 | bytes 2752512 | tf_op jit(solution)/shard_map/dot_general | solution.py:142
  46.6 1.3 %convolution_add_fusion.2 = f32[384,384]{1,0:T(8,128)S(1)} fusion(f32[384,384]{1,0:T(8,128)S(1)} %fusion.48, bf16[1,512,384]{2,1,0:T(8,128)(2,1)S(1)} %get-tuple-element.25, bf16[2,256,384]{2,1,0:T(8,128)(2,1)} %collective-permute-done, bf16[1,512,384]{2,1,0:T(8,128)(2,1)S(1)} %copy-done.1, bf16[1,512,384]{2,1,0:T(8,128)(2,1)S(1)} %bitcast.154), kind=kOutput, calls=%fused_computation.11 | convolution fusion | flops 152322048 | bytes 2752512 | tf_op jit(solution)/shard_map/dot_general | solution.py:142
  48.1 0.5 collective-permute-start.9
  48.6 1.2 %slice.184 = bf16[1024,384]{1,0:T(8,128)(2,1)S(1)} slice(bf16[2176,384]{1,0:T(8,128)(2,1)} %collective-permute-done.3), slice={[0:1024], [0:384]} | slice | bytes 1572864 | tf_op jit(solution)/shard_map/slice | solution.py:99
  49.8 0.2 fusion.45
  50.0 1.2 %slice_bitcast_fusion.3 = (bf16[512,1,384]{2,0,1:T(8,128)(2,1)S(1)}, bf16[512,1,384]{2,0,1:T(8,128)(2,1)S(1)}) fusion(bf16[2176,384]{1,0:T(8,128)(2,1)} %collective-permute-done.3), kind=kLoop, calls=%fused_computation.97 | loop fusion | bytes 1572864 | tf_op jit(solution)/shard_map/stack | solution.py:22
  51.2 0.8 convolution_bitcast_fusion
  52.1 0.3 copy-done.3
  52.3 1.3 %fusion.33 = bf16[512,384]{1,0:T(8,128)(2,1)S(1)} fusion(f32[512,384]{1,0:T(8,128)S(1)} %copy-done.3, f32[512,384]{1,0:T(8,128)S(1)} %convolution_bitcast_fusion, bf16[512,1,384]{2,0,1:T(8,128)(2,1)S(1)} %get-tuple-element.14, bf16[512,1,384]{2,0,1:T(8,128)(2,1)S(1)} %bitcast.160, bf16[512,1,384]{2,0,1:T(8,128)(2,1)S(1)} %get-tuple-element.5, ...), kind=kOutput, calls=%fused_computation.50 | convolution fusion | flops 458883072 | bytes 4423684 | tf_op jit(solution)/shard_map/tko,kio->ti/dot_general | solution.py:116
  53.7 1.3 %slice.187 = bf16[1152,384]{1,0:T(8,128)(2,1)S(1)} slice(bf16[2176,384]{1,0:T(8,128)(2,1)} %collective-permute-done.3), slice={[1024:2176], [0:384]} | slice | bytes 1769472 | tf_op jit(solution)/shard_map/slice | solution.py:100
  55.0 1.4 %collective-permute-start.14 = (f32[96,384]{1,0:T(8,128)S(1)}, f32[96,384]{1,0:T(8,128)S(1)}, u32[]{:S(2)}, u32[]{:S(2)}) collective-permute-start(f32[96,384]{1,0:T(8,128)S(1)} %select_bitcast_fusion.7), channel_id=1, source_target_pairs={{0,8},{8,0},{4,12},{12,4},{1,9},{9,1},{5,13},{13,5},{2,10},{10,2},... | collective-permute-start | bytes 442376 | tf_op jit(solution)/shard_map/ppermute | solution.py:64
  56.4 10.9 %collective-permute-done.9 = f32[2,192,384]{2,1,0:T(8,128)S(1)} collective-permute-done((f32[2,192,384]{2,1,0:T(8,128)S(1)}, f32[2,192,384]{2,1,0:T(8,128)S(1)}, u32[]{:S(2)}, u32[]{:S(2)}) %collective-permute-start.9) | collective-permute-done | bytes 589856 | tf_op jit(solution)/shard_map/ppermute | solution.py:59
  67.6 3.0 %collective-permute-start.15 = (bf16[96,384]{1,0:T(8,128)(2,1)S(1)}, bf16[96,384]{1,0:T(8,128)(2,1)S(1)}, u32[]{:S(2)}, u32[]{:S(2)}) collective-permute-start(bf16[96,384]{1,0:T(8,128)(2,1)S(1)} %fusion.65), channel_id=1, source_target_pairs={{0,8},{8,0},{4,12},{12,4},{1,9},{9,1},{5,13},{13,5},{2,10},{10,2},... | collective-permute-start | bytes 221192 | tf_op jit(solution)/shard_map/ppermute | solution.py:65
  70.5 0.8 convolution_bitcast_fusion.3
  71.3 12.8 %collective-permute-done.15 = bf16[96,384]{1,0:T(8,128)(2,1)S(1)} collective-permute-done((bf16[96,384]{1,0:T(8,128)(2,1)S(1)}, bf16[96,384]{1,0:T(8,128)(2,1)S(1)}, u32[]{:S(2)}, u32[]{:S(2)}) %collective-permute-start.15) | collective-permute-done | bytes 73760 | tf_op jit(solution)/shard_map/ppermute | solution.py:65
  84.3 3.0 %collective-permute-start.11 = (bf16[192,384]{1,0:T(8,128)(2,1)S(1)}, bf16[192,384]{1,0:T(8,128)(2,1)S(1)}, u32[]{:S(2)}, u32[]{:S(2)}) collective-permute-start(bf16[192,384]{1,0:T(8,128)(2,1)S(1)} %fusion.64), channel_id=1, source_target_pairs={{0,8},{8,0},{4,12},{12,4},{1,9},{9,1},{5,13},{13,5},{2,10},{10,2},... | collective-permute-start | bytes 442376 | tf_op jit(solution)/shard_map/ppermute | solution.py:65
  87.2 1.6 %fusion.4 = bf16[1,512,384]{2,1,0:T(8,128)(2,1)} fusion(f32[512,384]{1,0:T(8,128)S(1)} %copy-done.3, f32[512,384]{1,0:T(8,128)S(1)} %convolution_bitcast_fusion.3, bf16[3,384,384]{2,1,0:T(8,128)(2,1)S(1)} %bitcast.171, bf16[512,1,384]{2,0,1:T(8,128)(2,1)S(1)} %get-tuple-element.10, bf16[512,1,384]{2,0,1:T(8,128)(2,1)S(1)} %get-tuple-element.4, ...), kind=kOutput, calls=%fused_computation.12 | convolution fusion | flops 454754304 | bytes 4030464 | tf_op jit(solution)/shard_map/tki,kio->to/dot_general | solution.py:110
  88.8 0.4 broadcast_in_dim.8
  89.2 1.2 %convert_element_type.36 = bf16[1,1024,384]{2,1,0:T(8,128)(2,1)} reshape(bf16[512,2,384]{2,1,0:T(2,128)(2,1)S(1)} %broadcast_in_dim.8) | data formatting | bytes 1572864 | tf_op jit(solution)/shard_map/convert_element_type | solution.py:125
  90.4 3.8 %collective-permute-done.11 = bf16[192,384]{1,0:T(8,128)(2,1)S(1)} collective-permute-done((bf16[192,384]{1,0:T(8,128)(2,1)S(1)}, bf16[192,384]{1,0:T(8,128)(2,1)S(1)}, u32[]{:S(2)}, u32[]{:S(2)}) %collective-permute-start.11) | collective-permute-done | bytes 147488 | tf_op jit(solution)/shard_map/ppermute | solution.py:65
  94.3 0.3 collective-permute-start.12
  94.7 6.4 %collective-permute-done.12 = bf16[2,192,384]{2,1,0:T(8,128)(2,1)S(1)} collective-permute-done((bf16[2,192,384]{2,1,0:T(8,128)(2,1)S(1)}, bf16[2,192,384]{2,1,0:T(8,128)(2,1)S(1)}, u32[]{:S(2)}, u32[]{:S(2)}) %collective-permute-start.12) | collective-permute-done | bytes 294944 | tf_op jit(solution)/shard_map/ppermute | solution.py:67
  101.3 1.3 %maximum_convert_fusion = f32[3,384,384]{2,1,0:T(8,128)} fusion(bf16[1,384,384]{2,1,0:T(8,128)(2,1)S(1)} %bitcast.170, bf16[1,384,384]{2,1,0:T(8,128)(2,1)S(1)} %bitcast.168, bf16[1,384,384]{2,1,0:T(8,128)(2,1)S(1)} %bitcast.169), kind=kLoop, calls=%fused_computation.41 | loop fusion | flops 1327104 | bytes 2654208 | tf_op jit(solution)/shard_map/convert_element_type | solution.py:150
  (37 shorter events, 1.2 us)
Async XLA Ops:
  0.6 14.9 %copy-start = (bf16[3,384,768]{2,1,0:T(8,128)(2,1)S(1)}, bf16[3,384,768]{2,1,0:T(8,128)(2,1)}, u32[]{:S(2)}) copy-start(bf16[3,384,768]{2,1,0:T(8,128)(2,1)} %param.5) | copy-start | bytes 5308420
  0.6 6.0 %copy-start.1 = (bf16[1,512,384]{2,1,0:T(8,128)(2,1)S(1)}, bf16[1,512,384]{2,1,0:T(8,128)(2,1)}, u32[]{:S(2)}) copy-start(bf16[1,512,384]{2,1,0:T(8,128)(2,1)} %param.6) | copy-start | bytes 1179652
  0.7 28.1 %collective-permute-start.5 = (bf16[512,384]{1,0:T(8,128)(2,1)}, bf16[512,384]{1,0:T(8,128)(2,1)}, u32[]{:S(2)}, u32[]{:S(2)}) collective-permute-start(bf16[512,384]{1,0:T(8,128)(2,1)} %bitcast.158), channel_id=1, source_target_pairs={{2,0},{1,3},{6,4},{5,7},{10,8},{9,11},{14,12},{13,15},{18,16},{17,... | collective-permute-start | bytes 1179656 | tf_op jit(solution)/shard_map/ppermute | solution.py:88
  2.1 26.7 %collective-permute-start.6 = (bf16[512,384]{1,0:T(8,128)(2,1)}, bf16[512,384]{1,0:T(8,128)(2,1)}, u32[]{:S(2)}, u32[]{:S(2)}) collective-permute-start(bf16[512,384]{1,0:T(8,128)(2,1)} %bitcast.159), channel_id=1, source_target_pairs={{2,1},{1,2},{6,5},{5,6},{10,9},{9,10},{14,13},{13,14},{18,17},{17,... | collective-permute-start | bytes 1179656 | tf_op jit(solution)/shard_map/ppermute | solution.py:89
  7.6 14.1 %collective-permute-start = (bf16[2,256,384]{2,1,0:T(8,128)(2,1)}, bf16[2,256,384]{2,1,0:T(8,128)(2,1)}, u32[]{:S(2)}, u32[]{:S(2)}) collective-permute-start(bf16[2,256,384]{2,1,0:T(8,128)(2,1)} %get-tuple-element.19), channel_id=1, source_target_pairs={{0,4},{4,8},{8,12},{1,5},{5,9},{9,13},{2,6},{6,10},{10,14},{3,7},{... | collective-permute-start | bytes 1179656 | tf_op jit(solution)/shard_map/ppermute | solution.py:13
  13.3 11.5 %collective-permute-start.1 = (bf16[2,256,384]{2,1,0:T(8,128)(2,1)}, bf16[2,256,384]{2,1,0:T(8,128)(2,1)}, u32[]{:S(2)}, u32[]{:S(2)}) collective-permute-start(bf16[2,256,384]{2,1,0:T(8,128)(2,1)} %get-tuple-element.20), channel_id=1, source_target_pairs={{4,0},{8,4},{12,8},{5,1},{9,5},{13,9},{6,2},{10,6},{14,10},{7,3},{... | collective-permute-start | bytes 1179656 | tf_op jit(solution)/shard_map/ppermute | solution.py:13
  15.5 1.1 %copy-start.2 = (bf16[2,512,384]{2,1,0:T(8,128)(2,1)S(1)}, bf16[2,512,384]{2,1,0:T(8,128)(2,1)}, u32[]{:S(2)}) copy-start(bf16[2,512,384]{2,1,0:T(8,128)(2,1)} %pad_maximum_fusion.2) | copy-start | bytes 2359300
  18.0 23.6 %collective-permute-start.3 = (bf16[2176,384]{1,0:T(8,128)(2,1)}, bf16[2176,384]{1,0:T(8,128)(2,1)}, u32[]{:S(2)}, u32[]{:S(2)}) collective-permute-start(bf16[2176,384]{1,0:T(8,128)(2,1)} %pad_maximum_fusion), channel_id=1, source_target_pairs={{0,1},{1,0},{2,3},{3,2},{4,5},{5,4},{6,7},{7,6},{8,9},{9,8},{10,11... | collective-permute-start | bytes 5013512 | tf_op jit(solution)/shard_map/ppermute | solution.py:96
  21.7 12.2 %collective-permute-start.4 = (bf16[512,384]{1,0:T(8,128)(2,1)S(1)}, bf16[512,384]{1,0:T(8,128)(2,1)S(1)}, u32[]{:S(2)}, u32[]{:S(2)}) collective-permute-start(bf16[512,384]{1,0:T(8,128)(2,1)S(1)} %get-tuple-element.30), channel_id=1, source_target_pairs={{0,2},{2,0},{1,3},{3,1},{4,6},{6,4},{5,7},{7,5},{8,10},{10,8},{9,1... | collective-permute-start | bytes 1179656 | tf_op jit(solution)/shard_map/ppermute | solution.py:91
  26.0 15.5 %collective-permute-start.2 = (bf16[2,2,256,384]{3,2,1,0:T(8,128)(2,1)S(1)}, bf16[2,2,256,384]{3,2,1,0:T(8,128)(2,1)S(1)}, u32[]{:S(2)}, u32[]{:S(2)}) collective-permute-start(bf16[2,2,256,384]{3,2,1,0:T(8,128)(2,1)S(1)} %pad_maximum_fusion.3), channel_id=1, source_target_pairs={{0,1},{1,0},{2,3},{3,2},{4,5},{5,4},{6,7},{7,6},{8,9},{9,8},{10,11... | collective-permute-start | bytes 2359304 | tf_op jit(solution)/shard_map/ppermute | solution.py:103
  29.9 7.1 %collective-permute-start.8 = (bf16[256,384]{1,0:T(8,128)(2,1)S(1)}, bf16[256,384]{1,0:T(8,128)(2,1)S(1)}, u32[]{:S(2)}, u32[]{:S(2)}) collective-permute-start(bf16[256,384]{1,0:T(8,128)(2,1)S(1)} %get-tuple-element.26), channel_id=1, source_target_pairs={{0,4},{4,8},{8,12},{1,5},{5,9},{9,13},{2,6},{6,10},{10,14},{3,7},{... | collective-permute-start | bytes 589832 | tf_op jit(solution)/shard_map/ppermute | solution.py:13
  32.6 8.5 %collective-permute-start.7 = (bf16[256,384]{1,0:T(8,128)(2,1)S(1)}, bf16[256,384]{1,0:T(8,128)(2,1)S(1)}, u32[]{:S(2)}, u32[]{:S(2)}) collective-permute-start(bf16[256,384]{1,0:T(8,128)(2,1)S(1)} %get-tuple-element.27), channel_id=1, source_target_pairs={{4,0},{8,4},{12,8},{5,1},{9,5},{13,9},{6,2},{10,6},{14,10},{7,3},{... | collective-permute-start | bytes 589832 | tf_op jit(solution)/shard_map/ppermute | solution.py:13
  43.6 11.3 %collective-permute-start.13 = (f32[2,96,384]{2,1,0:T(8,128)S(1)}, f32[2,96,384]{2,1,0:T(8,128)S(1)}, u32[]{:S(2)}, u32[]{:S(2)}) collective-permute-start(f32[2,96,384]{2,1,0:T(8,128)S(1)} %select_bitcast_fusion.1), channel_id=1, source_target_pairs={{0,4},{4,0},{8,12},{12,8},{1,5},{5,1},{9,13},{13,9},{2,6},{6,2},{1... | collective-permute-start | bytes 884744 | tf_op jit(solution)/shard_map/ppermute | solution.py:59
  48.1 19.2 %collective-permute-start.9 = (f32[2,192,384]{2,1,0:T(8,128)S(1)}, f32[2,192,384]{2,1,0:T(8,128)S(1)}, u32[]{:S(2)}, u32[]{:S(2)}) collective-permute-start(f32[2,192,384]{2,1,0:T(8,128)S(1)} %select_bitcast_fusion), channel_id=1, source_target_pairs={{0,4},{4,0},{8,12},{12,8},{1,5},{5,1},{9,13},{13,9},{2,6},{6,2},{1... | collective-permute-start | bytes 1769480 | tf_op jit(solution)/shard_map/ppermute | solution.py:59
  51.2 1.1 %copy-start.3 = (f32[512,384]{1,0:T(8,128)S(1)}, f32[512,384]{1,0:T(8,128)}, u32[]{:S(2)}) copy-start(f32[512,384]{1,0:T(8,128)} %get-tuple-element.31) | copy-start | bytes 2359300
  55.0 12.5 %collective-permute-start.14 = (f32[96,384]{1,0:T(8,128)S(1)}, f32[96,384]{1,0:T(8,128)S(1)}, u32[]{:S(2)}, u32[]{:S(2)}) collective-permute-start(f32[96,384]{1,0:T(8,128)S(1)} %select_bitcast_fusion.7), channel_id=1, source_target_pairs={{0,8},{8,0},{4,12},{12,4},{1,9},{9,1},{5,13},{13,5},{2,10},{10,2},... | collective-permute-start | bytes 442376 | tf_op jit(solution)/shard_map/ppermute | solution.py:64
  67.4 16.8 %collective-permute-start.10 = (f32[192,384]{1,0:T(8,128)S(1)}, f32[192,384]{1,0:T(8,128)S(1)}, u32[]{:S(2)}, u32[]{:S(2)}) collective-permute-start(f32[192,384]{1,0:T(8,128)S(1)} %select_bitcast_fusion.4), channel_id=1, source_target_pairs={{0,8},{8,0},{4,12},{12,4},{1,9},{9,1},{5,13},{13,5},{2,10},{10,2},... | collective-permute-start | bytes 884744 | tf_op jit(solution)/shard_map/ppermute | solution.py:64
  67.6 16.6 %collective-permute-start.15 = (bf16[96,384]{1,0:T(8,128)(2,1)S(1)}, bf16[96,384]{1,0:T(8,128)(2,1)S(1)}, u32[]{:S(2)}, u32[]{:S(2)}) collective-permute-start(bf16[96,384]{1,0:T(8,128)(2,1)S(1)} %fusion.65), channel_id=1, source_target_pairs={{0,8},{8,0},{4,12},{12,4},{1,9},{9,1},{5,13},{13,5},{2,10},{10,2},... | collective-permute-start | bytes 221192 | tf_op jit(solution)/shard_map/ppermute | solution.py:65
  84.1 10.4 %collective-permute-start.16 = (bf16[2,96,384]{2,1,0:T(8,128)(2,1)S(1)}, bf16[2,96,384]{2,1,0:T(8,128)(2,1)S(1)}, u32[]{:S(2)}, u32[]{:S(2)}) collective-permute-start(bf16[2,96,384]{2,1,0:T(8,128)(2,1)S(1)} %maximum_select_fusion.1), channel_id=1, source_target_pairs={{0,4},{4,0},{8,12},{12,8},{1,5},{5,1},{9,13},{13,9},{2,6},{6,2},{1... | collective-permute-start | bytes 442376 | tf_op jit(solution)/shard_map/ppermute | solution.py:67
  84.3 9.9 %collective-permute-start.11 = (bf16[192,384]{1,0:T(8,128)(2,1)S(1)}, bf16[192,384]{1,0:T(8,128)(2,1)S(1)}, u32[]{:S(2)}, u32[]{:S(2)}) collective-permute-start(bf16[192,384]{1,0:T(8,128)(2,1)S(1)} %fusion.64), channel_id=1, source_target_pairs={{0,8},{8,0},{4,12},{12,4},{1,9},{9,1},{5,13},{13,5},{2,10},{10,2},... | collective-permute-start | bytes 442376 | tf_op jit(solution)/shard_map/ppermute | solution.py:65
  94.3 6.8 %collective-permute-start.12 = (bf16[2,192,384]{2,1,0:T(8,128)(2,1)S(1)}, bf16[2,192,384]{2,1,0:T(8,128)(2,1)S(1)}, u32[]{:S(2)}, u32[]{:S(2)}) collective-permute-start(bf16[2,192,384]{2,1,0:T(8,128)(2,1)S(1)} %maximum_select_fusion), channel_id=1, source_target_pairs={{0,4},{4,0},{8,12},{12,8},{1,5},{5,1},{9,13},{13,9},{2,6},{6,2},{1... | collective-permute-start | bytes 884744 | tf_op jit(solution)/shard_map/ppermute | solution.py:67
